TPU v7x, 32 devices: a whole 2x2x4 slice. The times are simulated.
32 devices in a mesh: blk: 16 (over z, y, core), rhs: 2 (over x).
Axes of the slice: x: 2, y: 2, z: 4, core: 2. Of those that a mesh axis runs over, the one named last changes fastest.
Arguments:
- factor_panel: float32 [2, 1024, 16384], P(None, None, 'blk'), may hold values from -0.0625 to 0.0625
- solved_before: float32 [16384, 512], P('blk', 'rhs'), may hold values from -6 to 6
- right_side: float32 [2, 1024, 512], P(None, None, 'rhs'), may hold values from -6 to 6
- diag_inverse: float32 [2, 1024, 1024], P(None, 'blk', 'rhs'), may hold values from -0.2 to 1.5, as said below
- coupling: float32 [1024, 1024], P(None, 'blk'), may hold values from -0.25 to 0.25
Outputs:
- solved: float32 [2, 1024, 512], P(None, 'blk', 'rhs')
Inputs may be any that keep to these rules, and one draw needn't show every extreme that they name: `diag_inverse`: each of the two blocks is lower triangular with a positive diagonal.
All inputs are finite; a program needn't handle non-finite values.
Results may differ from a plain program's by a relative error of at most 0.00009.
Values sent between devices are 32-bit elements; how exact they have to be, the bound alone decides.
No kernel may reach another device: no remote copies, remote signals or barrier semaphores. Data moves between devices by JAX's collectives and lax.ppermute only.
A program may use at most 64 MiB of HBM per device.

v0:
```python
import jax
import jax.numpy as jnp
from jax import lax
from jax.sharding import PartitionSpec as P


def product(left, right):
    return jnp.dot(left, right, precision=lax.Precision.HIGHEST, preferred_element_type=jnp.float32)


def shards(factor_panel, solved_before, right_side, diag_inverse, coupling):
    inverse_full = lax.all_gather(diag_inverse, "rhs", axis=2, tiled=True)
    own_count = diag_inverse.shape[1]
    my_index = lax.axis_index("blk")

    def own_slice(matrix):
        return lax.dynamic_slice_in_dim(matrix, my_index * own_count, own_count, 0)

    first_part = lax.psum_scatter(
        product(factor_panel[0], solved_before), "blk", scatter_dimension=0, tiled=True
    )
    first_remains = lax.all_gather(own_slice(right_side[0]) - first_part, "blk", axis=0, tiled=True)
    first_block = product(inverse_full[0], first_remains)
    panel_rows = factor_panel[1]
    second_part = lax.psum_scatter(
        product(panel_rows, solved_before) + product(coupling, first_block),
        "blk",
        scatter_dimension=0,
        tiled=True,
    )
    second_remains = lax.all_gather(
        own_slice(right_side[1]) - second_part, "blk", axis=0, tiled=True
    )
    second_block = product(inverse_full[1], second_remains)
    return jnp.stack([first_block, second_block])


def solution(mesh):
    placed = (
        P(None, None, "blk"),
        P("blk", "rhs"),
        P(None, None, "rhs"),
        P(None, "blk", "rhs"),
        P(None, "blk"),
    )
    return jax.shard_map(
        shards, mesh=mesh, in_specs=placed, out_specs=P(None, "blk", "rhs"), check_vma=False
    )
```

profile of v0, /device:TPU:0, one launch (start us, length us, event | category | flops | bytes accessed | tf_op | source)
XLA Modules:
  0.0 229.3 jit_solution(9284285652021798626)
XLA Ops:
  6.5 0.0 copy-start
  6.5 0.0 copy-start.1
  6.5 0.0 reduce-scatter.3.cloned.1.call-start
  6.5 1.2 copy-done
  7.8 6.6 %fusion.2 = f32[1024,256]{1,0:T(8,128)} fusion(f32[1024,256]{1,0:T(8,128)S(1)} %copy-done, f32[2,1024,1024]{2,1,0:T(8,128)} %param.5), kind=kOutput, calls=%fused_computation.2 | convolution fusion | flops 3221225472 | bytes 6291456 | tf_op jit(solution)/shard_map/dot_general | solution.py:8
  14.4 0.0 copy-start.2
  14.4 0.0 reduce-scatter.3.cloned.1.call-update
  14.4 0.0 all-gather.3.cloned.1.call-start
  14.5 0.0 copy-done.1
  14.5 1.5 fusion.10
  16.0 58.7 %reduce-scatter.3.cloned.1.call-done = f32[64,256]{1,0:T(8,128)} async-done(((f32[1024,256]{1,0:T(8,128)}), f32[64,256]{1,0:T(8,128)}) %reduce-scatter.3.cloned.1.call-update) | async-done | bytes 65552 | tf_op jit(solution)/shard_map/reduce_scatter | solution.py:19
  74.7 1.5 bitcast_subtract_fusion.1
  76.2 0.0 all-gather.3.cloned.1.call-update
  76.2 0.0 reduce-scatter.5.cloned.1.call-start
  76.3 0.0 copy-done.2
  76.3 7.0 %all_gather.10 = f32[2,64,1024]{2,1,0:T(8,128)S(1)} all-gather(f32[2,64,512]{2,1,0:T(8,128)S(1)} %copy-done.2), channel_id=1, replica_groups=mesh['blk'=16,'rhs'=2] {'rhs'}, dimensions={2}, use_global_device_ids=true | all-gather | bytes 786432 | tf_op jit(solution)/shard_map/all_gather | solution.py:12
  83.3 30.7 %all-gather.3.cloned.1.call-done = f32[1024,256]{1,0:T(8,128)} async-done(((f32[64,256]{1,0:T(8,128)}), f32[1024,256]{1,0:T(8,128)}) %all-gather.3.cloned.1.call-update) | async-done | bytes 1048592 | tf_op jit(solution)/shard_map/all_gather | solution.py:22
  114.0 2.0 fusion.9
  116.0 2.0 convolution_bitcast_fusion
  118.0 6.6 %fusion.6 = f32[1024,256]{1,0:T(8,128)} fusion(f32[1024,256]{1,0:T(8,128)S(1)} %convolution_bitcast_fusion, f32[1024,256]{1,0:T(8,128)S(1)} %copy-done, f32[2,1024,1024]{2,1,0:T(8,128)} %param.5), kind=kOutput, calls=%fused_computation.6 | convolution fusion | flops 3221487616 | bytes 7340032 | tf_op jit(solution)/shard_map/dot_general | solution.py:8
  124.6 0.0 reduce-scatter.5.cloned.1.call-update
  124.6 0.0 all-gather.5.cloned.1.call-start
  124.7 56.4 %reduce-scatter.5.cloned.1.call-done = f32[64,256]{1,0:T(8,128)} async-done(((f32[1024,256]{1,0:T(8,128)}), f32[64,256]{1,0:T(8,128)}) %reduce-scatter.5.cloned.1.call-update) | async-done | bytes 65552 | tf_op jit(solution)/shard_map/reduce_scatter | solution.py:25
  181.1 1.5 bitcast_subtract_fusion
  182.6 0.0 all-gather.5.cloned.1.call-update
  182.6 37.5 %all-gather.5.cloned.1.call-done = f32[1024,256]{1,0:T(8,128)} async-done(((f32[64,256]{1,0:T(8,128)}), f32[1024,256]{1,0:T(8,128)}) %all-gather.5.cloned.1.call-update) | async-done | bytes 1048592 | tf_op jit(solution)/shard_map/all_gather | solution.py:31
  220.1 2.0 convolution_bitcast_fusion.1
  222.1 0.7 pad_maximum_fusion
Async XLA Ops:
  6.5 1.2 copy-start
  6.5 7.9 %copy-start.1 = (f32[2,1024,256]{2,1,0:T(8,128)S(1)}, f32[2,1024,256]{2,1,0:T(8,128)}, u32[]{:S(2)}) copy-start(f32[2,1024,256]{2,1,0:T(8,128)} %param.7) | copy-start | bytes 6291460
  6.5 68.2 %reduce-scatter.3.cloned.1.call-start = ((), (), s32[]{:S(2)}) async-start(), calls=%async_computation.2 | async-start | bytes 1114112 | tf_op jit(solution)/shard_map/reduce_scatter | solution.py:19
  14.4 61.9 %copy-start.2 = (f32[2,64,512]{2,1,0:T(8,128)S(1)}, f32[2,64,512]{2,1,0:T(8,128)}, u32[]{:S(2)}) copy-start(f32[2,64,512]{2,1,0:T(8,128)} %param.8) | copy-start | bytes 786436
  14.4 99.6 %all-gather.3.cloned.1.call-start = ((), (), s32[]{:S(2)}) async-start(), calls=%async_computation.3 | async-start | bytes 1114112 | tf_op jit(solution)/shard_map/all_gather | solution.py:22
  76.2 104.9 %reduce-scatter.5.cloned.1.call-start = ((), (), s32[]{:S(2)}) async-start(), calls=%async_computation.4 | async-start | bytes 1114112 | tf_op jit(solution)/shard_map/reduce_scatter | solution.py:25
  124.6 95.5 %all-gather.5.cloned.1.call-start = ((), (), s32[]{:S(2)}) async-start(), calls=%async_computation.5 | async-start | bytes 1114112 | tf_op jit(solution)/shard_map/all_gather | solution.py:31
Sparse Core Ops, SparseCore 0:
  14.5 60.1 reduce-scatter.2
  77.1 36.8 all-gather.2
  124.7 56.3 reduce-scatter.4
  183.1 36.9 all-gather.4
where the time goes:
time: 230 us; the launch traced here: 229 us
  waiting for transfers between devices  183 us (80%)
  matrix products  19.1 us (8%)
  between operations  13.2 us (6%)
  blocking collectives  7.05 us (3%)
  other arithmetic  3.69 us (2%)
  local copies, waits for them, and re-layouts  2.72 us (1%)
    reduce_scatter x1, waiting for transfers between devices, shards(): lax.psum_scatter(product(factor_panel[0], solved_before), 'blk', scatter_...  58.7 us
    reduce_scatter x1, waiting for transfers between devices, shards(): lax.psum_scatter(product(panel_rows, solved_before) + product(coupling, f...  56.4 us
    all_gather x1, waiting for transfers between devices, shards(): lax.all_gather(own_slice(right_side[1]) - second_part, 'blk', axis=0, til...  37.5 us
    all_gather x1, waiting for transfers between devices, shards(): lax.all_gather(own_slice(right_side[0]) - first_part, 'blk', axis=0, tile...  30.7 us
    dot_general x5, matrix products, product(): jnp.dot(left, right, precision=lax.Precision.HIGHEST, preferred_element_t...  19.1 us
    all_gather x1, blocking collectives, shards(): inverse_full = lax.all_gather(diag_inverse, 'rhs', axis=2, tiled=True)  7.05 us
  transfers between devices with their start and end apart: 4, of which 4 were waited for; matrix products, arithmetic and copies ran while one was open for 1% of the time, Pallas kernels for 0%

commit v1 on v0

v1 whole, which is shorter than its diff:
```python
import jax
import jax.numpy as jnp
from jax import lax
from jax.sharding import PartitionSpec as P


def product(left, right):
    return jnp.dot(left, right, precision=lax.Precision.HIGHEST, preferred_element_type=jnp.float32)


def halving_sum_scatter(x, axis, n):
    k = n.bit_length() - 1
    me = lax.axis_index(axis)
    rows = x.shape[0] // n
    y = x.reshape((2,) * k + (rows,) + x.shape[1:])
    for j in range(k):
        bit_axis = k - 1 - j
        mine = (me >> j) & 1
        keep = lax.dynamic_index_in_dim(y, mine, bit_axis, keepdims=False)
        send = lax.dynamic_index_in_dim(y, 1 - mine, bit_axis, keepdims=False)
        got = lax.ppermute(send, axis, [(i, i ^ (1 << j)) for i in range(n)])
        y = keep + got
    return y.reshape((rows,) + x.shape[1:])


def doubling_gather(x, axis, n):
    k = n.bit_length() - 1
    me = lax.axis_index(axis)
    y = x[None]
    for j in reversed(range(k)):
        mine = (me >> j) & 1
        got = lax.ppermute(y, axis, [(i, i ^ (1 << j)) for i in range(n)])
        low = jnp.where(mine == 0, y, got)
        high = jnp.where(mine == 0, got, y)
        y = jnp.stack([low, high], 1).reshape((-1,) + x.shape)
    return y.reshape((-1,) + x.shape[1:])


def make_shards(n):
    power_of_two = n > 1 and (n & (n - 1)) == 0

    def sum_scatter(x):
        if power_of_two:
            return halving_sum_scatter(x, "blk", n)
        return lax.psum_scatter(x, "blk", scatter_dimension=0, tiled=True)

    def gather(x):
        if power_of_two:
            return doubling_gather(x, "blk", n)
        return lax.all_gather(x, "blk", axis=0, tiled=True)

    def shards(factor_panel, solved_before, right_side, diag_inverse, coupling):
        inverse_full = lax.all_gather(diag_inverse, "rhs", axis=2, tiled=True)
        own_count = diag_inverse.shape[1]
        my_index = lax.axis_index("blk")

        def own_slice(matrix):
            return lax.dynamic_slice_in_dim(matrix, my_index * own_count, own_count, 0)

        first_part = sum_scatter(product(factor_panel[0], solved_before))
        first_remains = gather(own_slice(right_side[0]) - first_part)
        first_block = product(inverse_full[0], first_remains)
        second_part = sum_scatter(
            product(factor_panel[1], solved_before) + product(coupling, first_block)
        )
        second_remains = gather(own_slice(right_side[1]) - second_part)
        second_block = product(inverse_full[1], second_remains)
        return jnp.stack([first_block, second_block])

    return shards


def solution(mesh):
    placed = (
        P(None, None, "blk"),
        P("blk", "rhs"),
        P(None, None, "rhs"),
        P(None, "blk", "rhs"),
        P(None, "blk"),
    )
    return jax.shard_map(
        make_shards(mesh.shape["blk"]), mesh=mesh, in_specs=placed, out_specs=P(None, "blk", "rhs"), check_vma=False
    )
```

time: 230 us -> 112 us (0.49)
  waiting for transfers between devices: 183 us -> 48.8 us
  starting transfers between devices: 0.13 us -> 28.5 us
  between operations: 13.2 us -> 0.33 us
  matrix products: 19.1 us -> 13.2 us
  local copies, waits for them, and re-layouts: 2.72 us -> 7.7 us
  blocking collectives: 7.05 us -> 9.48 us
    reduce_scatter x2 -> x0, waiting for transfers between devices: 115 us -> none  [the longest x1 58.7 us: shards(): lax.psum_scatter(product(factor_panel[0], solved_before), 'blk', scatter_...]
    all_gather x2 -> x0, waiting for transfers between devices: 68.2 us -> none  [the longest x1 37.5 us: shards(): lax.all_gather(own_slice(right_side[1]) - second_part, 'blk', axis=0, til...]
    ppermute x0 -> x16, waiting for transfers between devices: none -> 48.8 us  [the longest x8 26.2 us: halving_sum_scatter(): got = lax.ppermute(send, axis, [(i, i ^ 1 << j) for i in range(n)])]
    ppermute x0 -> x16, starting transfers between devices: none -> 28.5 us  [the longest x8 15.2 us: halving_sum_scatter(): got = lax.ppermute(send, axis, [(i, i ^ 1 << j) for i in range(n)])]
    dot_general x5, matrix products: 19.1 us -> 13.2 us  [product(): jnp.dot(left, right, precision=lax.Precision.HIGHEST, preferred_element_t...]
    slice x1 -> x2, local copies, waits for them, and re-layouts: 1.49 us -> 6.48 us  [the longest x1 4.81 us: shards(): first_part = sum_scatter(product(factor_panel[0], solved_before))]
    sub x2 -> x0, other arithmetic: 3.02 us -> none  [the longest x1 1.51 us: shards(): own_slice(right_side[0]) - first_part]
    all_gather x1, blocking collectives: 7.05 us -> 9.48 us  [shards(): inverse_full = lax.all_gather(diag_inverse, 'rhs', axis=2, tiled=True)]
  transfers between devices with their start and end apart: 4 -> 16, of which waited for: 4 -> 15; matrix products, arithmetic and copies ran while one was open for 1% -> 1% of each run, Pallas kernels for 0% -> 0%
where the time goes in v1:
time: 112 us
  waiting for transfers between devices  48.8 us (44%)
  starting transfers between devices  28.5 us (25%)
  matrix products  13.2 us (12%)
  blocking collectives  9.48 us (8%)
  local copies, waits for them, and re-layouts  7.7 us (7%)
  other arithmetic  3.95 us (4%)
    ppermute x8, waiting for transfers between devices, halving_sum_scatter(): got = lax.ppermute(send, axis, [(i, i ^ 1 << j) for i in range(n)])  26.2 us
    ppermute x8, waiting for transfers between devices, doubling_gather(): got = lax.ppermute(y, axis, [(i, i ^ 1 << j) for i in range(n)])  22.5 us
    ppermute x8, starting transfers between devices, halving_sum_scatter(): got = lax.ppermute(send, axis, [(i, i ^ 1 << j) for i in range(n)])  15.2 us
    ppermute x8, starting transfers between devices, doubling_gather(): got = lax.ppermute(y, axis, [(i, i ^ 1 << j) for i in range(n)])  13.3 us
    dot_general x5, matrix products, product(): jnp.dot(left, right, precision=lax.Precision.HIGHEST, preferred_element_t...  13.2 us
    all_gather x1, blocking collectives, shards(): inverse_full = lax.all_gather(diag_inverse, 'rhs', axis=2, tiled=True)  9.48 us
    slice x1, local copies, waits for them, and re-layouts, shards(): first_part = sum_scatter(product(factor_panel[0], solved_before))  4.81 us
  transfers between devices with their start and end apart: 16, of which 15 were waited for; matrix products, arithmetic and copies ran while one was open for 1% of the time, Pallas kernels for 0%

profile of v1, /device:TPU:0, one launch (start us, length us, event | category | flops | bytes accessed | tf_op | source)
XLA Modules:
  0.0 111.9 jit_solution(16886120217605874357)
XLA Ops:
  0.0 4.8 %slice.19 = f32[1,1024,1024]{2,1,0:T(8,128)} slice(f32[2,1024,1024]{2,1,0:T(8,128)} %param.5), slice={[0:1], [0:1024], [0:1024]} | slice | bytes 8388608 | tf_op jit(solution)/shard_map/slice | solution.py:60
  4.8 5.4 %fusion.6 = f32[2,2,2,2,64,256]{5,4,3,2,1,0:T(8,128)S(1)} fusion(f32[2,2,2,2,64,1024]{5,4,3,2,1,0:T(8,128)} %bitcast.142, f32[1024,256]{1,0:T(8,128)S(1)} %copy-done), kind=kOutput, calls=%fused_computation.8 | convolution fusion | flops 3221225472 | bytes 6291456 | tf_op jit(solution)/shard_map/dot_general | solution.py:8
  10.8 1.5 %collective-permute-done = f32[2,2,2,64,256]{4,3,2,1,0:T(8,128)S(1)} collective-permute-done((f32[2,2,2,64,256]{4,3,2,1,0:T(8,128)S(1)}, f32[2,2,2,64,256]{4,3,2,1,0:T(8,128)S(1)}, u32[]{:S(2)}, u32[]{:S(2)}) %collective-permute-start) | collective-permute-done | bytes 524320 | tf_op jit(solution)/shard_map/ppermute | solution.py:21
  12.5 3.0 %collective-permute-start.1 = (f32[2,2,64,256]{3,2,1,0:T(8,128)S(1)}, f32[2,2,64,256]{3,2,1,0:T(8,128)S(1)}, u32[]{:S(2)}, u32[]{:S(2)}) collective-permute-start(f32[2,2,64,256]{3,2,1,0:T(8,128)S(1)} %dynamic-slice_bitcast_fusion.2), channel_id=1, source_target_pairs={{0,4},{2,6},{4,0},{6,2},{8,12},{10,14},{12,8},{14,10},{16,20},{18,... | collective-permute-start | bytes 786440 | tf_op jit(solution)/shard_map/ppermute | solution.py:21
  15.4 6.6 %collective-permute-done.1 = f32[2,2,64,256]{3,2,1,0:T(8,128)S(1)} collective-permute-done((f32[2,2,64,256]{3,2,1,0:T(8,128)S(1)}, f32[2,2,64,256]{3,2,1,0:T(8,128)S(1)}, u32[]{:S(2)}, u32[]{:S(2)}) %collective-permute-start.1) | collective-permute-done | bytes 262176 | tf_op jit(solution)/shard_map/ppermute | solution.py:21
  22.1 1.9 %collective-permute-start.2 = (f32[2,64,256]{2,1,0:T(8,128)S(1)}, f32[2,64,256]{2,1,0:T(8,128)S(1)}, u32[]{:S(2)}, u32[]{:S(2)}) collective-permute-start(f32[2,64,256]{2,1,0:T(8,128)S(1)} %dynamic-slice_bitcast_fusion.4), channel_id=1, source_target_pairs={{0,8},{2,10},{4,12},{6,14},{8,0},{10,2},{12,4},{14,6},{16,24},{18,... | collective-permute-start | bytes 393224 | tf_op jit(solution)/shard_map/ppermute | solution.py:21
  24.0 3.2 %collective-permute-done.2 = f32[2,64,256]{2,1,0:T(8,128)S(1)} collective-permute-done((f32[2,64,256]{2,1,0:T(8,128)S(1)}, f32[2,64,256]{2,1,0:T(8,128)S(1)}, u32[]{:S(2)}, u32[]{:S(2)}) %collective-permute-start.2) | collective-permute-done | bytes 131104 | tf_op jit(solution)/shard_map/ppermute | solution.py:21
  27.9 2.7 %collective-permute-start.3 = (f32[64,256]{1,0:T(8,128)}, f32[64,256]{1,0:T(8,128)}, u32[]{:S(2)}, u32[]{:S(2)}) collective-permute-start(f32[64,256]{1,0:T(8,128)} %dynamic-slice_bitcast_fusion.6), channel_id=1, source_target_pairs={{0,16},{2,18},{4,20},{6,22},{8,24},{10,26},{12,28},{14,30},{16,0},... | collective-permute-start | bytes 196616 | tf_op jit(solution)/shard_map/ppermute | solution.py:21
  30.6 1.7 %fusion.13 = (f32[1,1024,256]{2,1,0:T(8,128)S(1)}, f32[1,1024,256]{2,1,0:T(8,128)S(1)}) fusion(f32[2,1024,256]{2,1,0:T(8,128)} %param.7), kind=kLoop, calls=%fused_computation.58 | loop fusion | bytes 4194304 | tf_op jit(solution)/shard_map/slice | solution.py:66
  33.3 1.5 %fusion.12 = f32[1,64,256]{2,1,0:T(8,128)} fusion(f32[64,256]{1,0:T(8,128)} %collective-permute-done.3, f32[2,64,256]{2,1,0:T(8,128)S(1)} %bitcast_add_fusion.5, s32[]{:T(128)S(6)} %select_n.131, f32[1,1024,256]{2,1,0:T(8,128)S(1)} %get-tuple-element.6, s32[]{:T(128)S(6)} %select_n.124), kind=kLoop, calls=%fused_computation.49 | loop fusion | flops 32768 | bytes 262152 | tf_op jit(solution)/shard_map/broadcast_in_dim | solution.py:29
  34.8 2.8 %collective-permute-start.4 = (f32[1,64,256]{2,1,0:T(8,128)}, f32[1,64,256]{2,1,0:T(8,128)S(1)}, u32[]{:S(2)}, u32[]{:S(2)}) collective-permute-start(f32[1,64,256]{2,1,0:T(8,128)} %fusion.12), channel_id=1, source_target_pairs={{0,16},{2,18},{4,20},{6,22},{8,24},{10,26},{12,28},{14,30},{16,0},... | collective-permute-start | bytes 196616 | tf_op jit(solution)/shard_map/ppermute | solution.py:32
  37.6 2.6 %collective-permute-done.4 = f32[1,64,256]{2,1,0:T(8,128)S(1)} collective-permute-done((f32[1,64,256]{2,1,0:T(8,128)}, f32[1,64,256]{2,1,0:T(8,128)S(1)}, u32[]{:S(2)}, u32[]{:S(2)}) %collective-permute-start.4) | collective-permute-done | bytes 65568 | tf_op jit(solution)/shard_map/ppermute | solution.py:32
  41.1 2.1 %collective-permute-start.5 = (f32[2,64,256]{2,1,0:T(8,128)S(1)}, f32[2,64,256]{2,1,0:T(8,128)S(1)}, u32[]{:S(2)}, u32[]{:S(2)}) collective-permute-start(f32[2,64,256]{2,1,0:T(8,128)S(1)} %maximum_bitcast_fusion), channel_id=1, source_target_pairs={{0,8},{2,10},{4,12},{6,14},{8,0},{10,2},{12,4},{14,6},{16,24},{18,... | collective-permute-start | bytes 393224 | tf_op jit(solution)/shard_map/ppermute | solution.py:32
  43.1 3.0 %collective-permute-done.5 = f32[2,64,256]{2,1,0:T(8,128)S(1)} collective-permute-done((f32[2,64,256]{2,1,0:T(8,128)S(1)}, f32[2,64,256]{2,1,0:T(8,128)S(1)}, u32[]{:S(2)}, u32[]{:S(2)}) %collective-permute-start.5) | collective-permute-done | bytes 131104 | tf_op jit(solution)/shard_map/ppermute | solution.py:32
  46.2 1.8 %collective-permute-start.6 = (f32[4,64,256]{2,1,0:T(8,128)S(1)}, f32[4,64,256]{2,1,0:T(8,128)S(1)}, u32[]{:S(2)}, u32[]{:S(2)}) collective-permute-start(f32[4,64,256]{2,1,0:T(8,128)S(1)} %bitcast.148), channel_id=1, source_target_pairs={{0,4},{2,6},{4,0},{6,2},{8,12},{10,14},{12,8},{14,10},{16,20},{18,... | collective-permute-start | bytes 786440 | tf_op jit(solution)/shard_map/ppermute | solution.py:32
  47.9 4.7 %collective-permute-done.6 = f32[4,64,256]{2,1,0:T(8,128)S(1)} collective-permute-done((f32[4,64,256]{2,1,0:T(8,128)S(1)}, f32[4,64,256]{2,1,0:T(8,128)S(1)}, u32[]{:S(2)}, u32[]{:S(2)}) %collective-permute-start.6) | collective-permute-done | bytes 262176 | tf_op jit(solution)/shard_map/ppermute | solution.py:32
  52.8 9.5 %all_gather.3 = f32[2,64,1024]{2,1,0:T(8,128)S(1)} all-gather(f32[2,64,512]{2,1,0:T(8,128)S(1)} %copy-done.1), channel_id=1, replica_groups=mesh['blk'=16,'rhs'=2] {'rhs'}, dimensions={2}, use_global_device_ids=true | all-gather | bytes 786432 | tf_op jit(solution)/shard_map/all_gather | solution.py:53
  64.4 5.2 %fusion.3 = f32[1024,256]{1,0:T(8,128)S(1)} fusion(f32[1024,256]{1,0:T(8,128)S(1)} %convolution_bitcast_fusion, f32[1024,256]{1,0:T(8,128)S(1)} %copy-done, f32[2,1024,1024]{2,1,0:T(8,128)} %param.5), kind=kOutput, calls=%fused_computation.3 | convolution fusion | flops 3221487616 | bytes 7340032 | tf_op jit(solution)/shard_map/dot_general | solution.py:8
  69.9 1.9 %collective-permute-done.8 = f32[2,2,2,64,256]{4,3,1,0,2:T(8,128)S(1)} collective-permute-done((f32[2,2,2,64,256]{4,3,1,0,2:T(8,128)S(1)}, f32[2,2,2,64,256]{4,3,1,0,2:T(8,128)S(1)}, u32[]{:S(2)}, u32[]{:S(2)}) %collective-permute-start.8) | collective-permute-done | bytes 524320 | tf_op jit(solution)/shard_map/ppermute | solution.py:21
  71.9 1.8 %collective-permute-start.9 = (f32[2,2,64,256]{3,2,1,0:T(8,128)S(1)}, f32[2,2,64,256]{3,2,1,0:T(8,128)S(1)}, u32[]{:S(2)}, u32[]{:S(2)}) collective-permute-start(f32[2,2,64,256]{3,2,1,0:T(8,128)S(1)} %dynamic-slice_bitcast_fusion.1), channel_id=1, source_target_pairs={{0,4},{2,6},{4,0},{6,2},{8,12},{10,14},{12,8},{14,10},{16,20},{18,... | collective-permute-start | bytes 786440 | tf_op jit(solution)/shard_map/ppermute | solution.py:21
  73.7 6.7 %collective-permute-done.9 = f32[2,2,64,256]{3,2,1,0:T(8,128)S(1)} collective-permute-done((f32[2,2,64,256]{3,2,1,0:T(8,128)S(1)}, f32[2,2,64,256]{3,2,1,0:T(8,128)S(1)}, u32[]{:S(2)}, u32[]{:S(2)}) %collective-permute-start.9) | collective-permute-done | bytes 262176 | tf_op jit(solution)/shard_map/ppermute | solution.py:21
  80.4 2.0 %collective-permute-start.10 = (f32[2,64,256]{2,1,0:T(8,128)S(1)}, f32[2,64,256]{2,1,0:T(8,128)S(1)}, u32[]{:S(2)}, u32[]{:S(2)}) collective-permute-start(f32[2,64,256]{2,1,0:T(8,128)S(1)} %dynamic-slice_bitcast_fusion.3), channel_id=1, source_target_pairs={{0,8},{2,10},{4,12},{6,14},{8,0},{10,2},{12,4},{14,6},{16,24},{18,... | collective-permute-start | bytes 393224 | tf_op jit(solution)/shard_map/ppermute | solution.py:21
  82.5 3.0 %collective-permute-done.10 = f32[2,64,256]{2,1,0:T(8,128)S(1)} collective-permute-done((f32[2,64,256]{2,1,0:T(8,128)S(1)}, f32[2,64,256]{2,1,0:T(8,128)S(1)}, u32[]{:S(2)}, u32[]{:S(2)}) %collective-permute-start.10) | collective-permute-done | bytes 131104 | tf_op jit(solution)/shard_map/ppermute | solution.py:21
  85.5 3.3 %collective-permute-start.11 = (f32[64,256]{1,0:T(8,128)S(1)}, f32[64,256]{1,0:T(8,128)S(1)}, u32[]{:S(2)}, u32[]{:S(2)}) collective-permute-start(f32[64,256]{1,0:T(8,128)S(1)} %dynamic-slice_bitcast_fusion.5), channel_id=1, source_target_pairs={{0,16},{2,18},{4,20},{6,22},{8,24},{10,26},{12,28},{14,30},{16,0},... | collective-permute-start | bytes 196616 | tf_op jit(solution)/shard_map/ppermute | solution.py:21
  88.8 2.2 %collective-permute-done.11 = f32[64,256]{1,0:T(8,128)S(1)} collective-permute-done((f32[64,256]{1,0:T(8,128)S(1)}, f32[64,256]{1,0:T(8,128)S(1)}, u32[]{:S(2)}, u32[]{:S(2)}) %collective-permute-start.11) | collective-permute-done | bytes 65568 | tf_op jit(solution)/shard_map/ppermute | solution.py:21
  91.0 3.0 %collective-permute-start.12 = (f32[1,64,256]{2,1,0:T(8,128)S(1)}, f32[1,64,256]{2,1,0:T(8,128)S(1)}, u32[]{:S(2)}, u32[]{:S(2)}) collective-permute-start(f32[1,64,256]{2,1,0:T(8,128)S(1)} %fusion.10), channel_id=1, source_target_pairs={{0,16},{2,18},{4,20},{6,22},{8,24},{10,26},{12,28},{14,30},{16,0},... | collective-permute-start | bytes 196616 | tf_op jit(solution)/shard_map/ppermute | solution.py:32
  94.0 2.5 %collective-permute-done.12 = f32[1,64,256]{2,1,0:T(8,128)S(1)} collective-permute-done((f32[1,64,256]{2,1,0:T(8,128)S(1)}, f32[1,64,256]{2,1,0:T(8,128)S(1)}, u32[]{:S(2)}, u32[]{:S(2)}) %collective-permute-start.12) | collective-permute-done | bytes 65568 | tf_op jit(solution)/shard_map/ppermute | solution.py:32
  96.5 2.0 %collective-permute-start.13 = (f32[2,64,256]{2,1,0:T(8,128)S(1)}, f32[2,64,256]{2,1,0:T(8,128)S(1)}, u32[]{:S(2)}, u32[]{:S(2)}) collective-permute-start(f32[2,64,256]{2,1,0:T(8,128)S(1)} %maximum_bitcast_fusion.1), channel_id=1, source_target_pairs={{0,8},{2,10},{4,12},{6,14},{8,0},{10,2},{12,4},{14,6},{16,24},{18,... | collective-permute-start | bytes 393224 | tf_op jit(solution)/shard_map/ppermute | solution.py:32
  98.5 3.1 %collective-permute-done.13 = f32[2,64,256]{2,1,0:T(8,128)S(1)} collective-permute-done((f32[2,64,256]{2,1,0:T(8,128)S(1)}, f32[2,64,256]{2,1,0:T(8,128)S(1)}, u32[]{:S(2)}, u32[]{:S(2)}) %collective-permute-start.13) | collective-permute-done | bytes 131104 | tf_op jit(solution)/shard_map/ppermute | solution.py:32
  101.7 1.6 %collective-permute-start.14 = (f32[4,64,256]{2,1,0:T(8,128)S(1)}, f32[4,64,256]{2,1,0:T(8,128)S(1)}, u32[]{:S(2)}, u32[]{:S(2)}) collective-permute-start(f32[4,64,256]{2,1,0:T(8,128)S(1)} %bitcast.149), channel_id=1, source_target_pairs={{0,4},{2,6},{4,0},{6,2},{8,12},{10,14},{12,8},{14,10},{16,20},{18,... | collective-permute-start | bytes 786440 | tf_op jit(solution)/shard_map/ppermute | solution.py:32
  103.2 4.9 %collective-permute-done.14 = f32[4,64,256]{2,1,0:T(8,128)S(1)} collective-permute-done((f32[4,64,256]{2,1,0:T(8,128)S(1)}, f32[4,64,256]{2,1,0:T(8,128)S(1)}, u32[]{:S(2)}, u32[]{:S(2)}) %collective-permute-start.14) | collective-permute-done | bytes 262176 | tf_op jit(solution)/shard_map/ppermute | solution.py:32
  108.3 1.9 %collective-permute-done.15 = f32[8,64,256]{2,1,0:T(8,128)S(1)} collective-permute-done((f32[8,64,256]{2,1,0:T(8,128)S(1)}, f32[8,64,256]{2,1,0:T(8,128)S(1)}, u32[]{:S(2)}, u32[]{:S(2)}) %collective-permute-start.15) | collective-permute-done | bytes 524320 | tf_op jit(solution)/shard_map/ppermute | solution.py:32
  (53 shorter events, 8.0 us)
Async XLA Ops:
  0.0 4.8 %copy-start = (f32[1024,256]{1,0:T(8,128)S(1)}, f32[1024,256]{1,0:T(8,128)}, u32[]{:S(2)}) copy-start(f32[1024,256]{1,0:T(8,128)} %param.6) | copy-start | bytes 3145732
  10.3 2.1 %collective-permute-start = (f32[2,2,2,64,256]{4,3,2,1,0:T(8,128)S(1)}, f32[2,2,2,64,256]{4,3,2,1,0:T(8,128)S(1)}, u32[]{:S(2)}, u32[]{:S(2)}) collective-permute-start(f32[2,2,2,64,256]{4,3,2,1,0:T(8,128)S(1)} %dynamic-slice_bitcast_fusion), channel_id=1, source_target_pairs={{0,2},{2,0},{4,6},{6,4},{8,10},{10,8},{12,14},{14,12},{16,18},{18,... | collective-permute-start | bytes 1572872 | tf_op jit(solution)/shard_map/ppermute | solution.py:21
  12.5 9.6 %collective-permute-start.1 = (f32[2,2,64,256]{3,2,1,0:T(8,128)S(1)}, f32[2,2,64,256]{3,2,1,0:T(8,128)S(1)}, u32[]{:S(2)}, u32[]{:S(2)}) collective-permute-start(f32[2,2,64,256]{3,2,1,0:T(8,128)S(1)} %dynamic-slice_bitcast_fusion.2), channel_id=1, source_target_pairs={{0,4},{2,6},{4,0},{6,2},{8,12},{10,14},{12,8},{14,10},{16,20},{18,... | collective-permute-start | bytes 786440 | tf_op jit(solution)/shard_map/ppermute | solution.py:21
  22.1 5.1 %collective-permute-start.2 = (f32[2,64,256]{2,1,0:T(8,128)S(1)}, f32[2,64,256]{2,1,0:T(8,128)S(1)}, u32[]{:S(2)}, u32[]{:S(2)}) collective-permute-start(f32[2,64,256]{2,1,0:T(8,128)S(1)} %dynamic-slice_bitcast_fusion.4), channel_id=1, source_target_pairs={{0,8},{2,10},{4,12},{6,14},{8,0},{10,2},{12,4},{14,6},{16,24},{18,... | collective-permute-start | bytes 393224 | tf_op jit(solution)/shard_map/ppermute | solution.py:21
  27.9 25.0 %copy-start.1 = (f32[2,64,512]{2,1,0:T(8,128)S(1)}, f32[2,64,512]{2,1,0:T(8,128)}, u32[]{:S(2)}) copy-start(f32[2,64,512]{2,1,0:T(8,128)} %param.8) | copy-start | bytes 786436
  27.9 5.5 %collective-permute-start.3 = (f32[64,256]{1,0:T(8,128)}, f32[64,256]{1,0:T(8,128)}, u32[]{:S(2)}, u32[]{:S(2)}) collective-permute-start(f32[64,256]{1,0:T(8,128)} %dynamic-slice_bitcast_fusion.6), channel_id=1, source_target_pairs={{0,16},{2,18},{4,20},{6,22},{8,24},{10,26},{12,28},{14,30},{16,0},... | collective-permute-start | bytes 196616 | tf_op jit(solution)/shard_map/ppermute | solution.py:21
  34.8 5.4 %collective-permute-start.4 = (f32[1,64,256]{2,1,0:T(8,128)}, f32[1,64,256]{2,1,0:T(8,128)S(1)}, u32[]{:S(2)}, u32[]{:S(2)}) collective-permute-start(f32[1,64,256]{2,1,0:T(8,128)} %fusion.12), channel_id=1, source_target_pairs={{0,16},{2,18},{4,20},{6,22},{8,24},{10,26},{12,28},{14,30},{16,0},... | collective-permute-start | bytes 196616 | tf_op jit(solution)/shard_map/ppermute | solution.py:32
  41.1 5.0 %collective-permute-start.5 = (f32[2,64,256]{2,1,0:T(8,128)S(1)}, f32[2,64,256]{2,1,0:T(8,128)S(1)}, u32[]{:S(2)}, u32[]{:S(2)}) collective-permute-start(f32[2,64,256]{2,1,0:T(8,128)S(1)} %maximum_bitcast_fusion), channel_id=1, source_target_pairs={{0,8},{2,10},{4,12},{6,14},{8,0},{10,2},{12,4},{14,6},{16,24},{18,... | collective-permute-start | bytes 393224 | tf_op jit(solution)/shard_map/ppermute | solution.py:32
  46.2 6.4 %collective-permute-start.6 = (f32[4,64,256]{2,1,0:T(8,128)S(1)}, f32[4,64,256]{2,1,0:T(8,128)S(1)}, u32[]{:S(2)}, u32[]{:S(2)}) collective-permute-start(f32[4,64,256]{2,1,0:T(8,128)S(1)} %bitcast.148), channel_id=1, source_target_pairs={{0,4},{2,6},{4,0},{6,2},{8,12},{10,14},{12,8},{14,10},{16,20},{18,... | collective-permute-start | bytes 786440 | tf_op jit(solution)/shard_map/ppermute | solution.py:32
  52.7 9.6 %collective-permute-start.7 = (f32[8,64,256]{2,1,0:T(8,128)S(1)}, f32[8,64,256]{2,1,0:T(8,128)S(1)}, u32[]{:S(2)}, u32[]{:S(2)}) collective-permute-start(f32[8,64,256]{2,1,0:T(8,128)S(1)} %bitcast.146), channel_id=1, source_target_pairs={{0,2},{2,0},{4,6},{6,4},{8,10},{10,8},{12,14},{14,12},{16,18},{18,... | collective-permute-start | bytes 1572872 | tf_op jit(solution)/shard_map/ppermute | solution.py:32
  52.8 10.6 %copy-start.2 = (f32[1024,64]{0,1:T(8,128)S(1)}, f32[1024,64]{0,1:T(8,128)}, u32[]{:S(2)}) copy-start(f32[1024,64]{0,1:T(8,128)} %param.9) | copy-start | bytes 786436
  69.9 2.0 %collective-permute-start.8 = (f32[2,2,2,64,256]{4,3,1,0,2:T(8,128)S(1)}, f32[2,2,2,64,256]{4,3,1,0,2:T(8,128)S(1)}, u32[]{:S(2)}, u32[]{:S(2)}) collective-permute-start(f32[2,2,2,64,256]{4,3,1,0,2:T(8,128)S(1)} %bitcast.151), channel_id=1, source_target_pairs={{0,2},{2,0},{4,6},{6,4},{8,10},{10,8},{12,14},{14,12},{16,18},{18,... | collective-permute-start | bytes 1572872 | tf_op jit(solution)/shard_map/ppermute | solution.py:21
  71.9 8.4 %collective-permute-start.9 = (f32[2,2,64,256]{3,2,1,0:T(8,128)S(1)}, f32[2,2,64,256]{3,2,1,0:T(8,128)S(1)}, u32[]{:S(2)}, u32[]{:S(2)}) collective-permute-start(f32[2,2,64,256]{3,2,1,0:T(8,128)S(1)} %dynamic-slice_bitcast_fusion.1), channel_id=1, source_target_pairs={{0,4},{2,6},{4,0},{6,2},{8,12},{10,14},{12,8},{14,10},{16,20},{18,... | collective-permute-start | bytes 786440 | tf_op jit(solution)/shard_map/ppermute | solution.py:21
  80.4 5.0 %collective-permute-start.10 = (f32[2,64,256]{2,1,0:T(8,128)S(1)}, f32[2,64,256]{2,1,0:T(8,128)S(1)}, u32[]{:S(2)}, u32[]{:S(2)}) collective-permute-start(f32[2,64,256]{2,1,0:T(8,128)S(1)} %dynamic-slice_bitcast_fusion.3), channel_id=1, source_target_pairs={{0,8},{2,10},{4,12},{6,14},{8,0},{10,2},{12,4},{14,6},{16,24},{18,... | collective-permute-start | bytes 393224 | tf_op jit(solution)/shard_map/ppermute | solution.py:21
  85.5 5.5 %collective-permute-start.11 = (f32[64,256]{1,0:T(8,128)S(1)}, f32[64,256]{1,0:T(8,128)S(1)}, u32[]{:S(2)}, u32[]{:S(2)}) collective-permute-start(f32[64,256]{1,0:T(8,128)S(1)} %dynamic-slice_bitcast_fusion.5), channel_id=1, source_target_pairs={{0,16},{2,18},{4,20},{6,22},{8,24},{10,26},{12,28},{14,30},{16,0},... | collective-permute-start | bytes 196616 | tf_op jit(solution)/shard_map/ppermute | solution.py:21
  91.0 5.5 %collective-permute-start.12 = (f32[1,64,256]{2,1,0:T(8,128)S(1)}, f32[1,64,256]{2,1,0:T(8,128)S(1)}, u32[]{:S(2)}, u32[]{:S(2)}) collective-permute-start(f32[1,64,256]{2,1,0:T(8,128)S(1)} %fusion.10), channel_id=1, source_target_pairs={{0,16},{2,18},{4,20},{6,22},{8,24},{10,26},{12,28},{14,30},{16,0},... | collective-permute-start | bytes 196616 | tf_op jit(solution)/shard_map/ppermute | solution.py:32
  96.5 5.0 %collective-permute-start.13 = (f32[2,64,256]{2,1,0:T(8,128)S(1)}, f32[2,64,256]{2,1,0:T(8,128)S(1)}, u32[]{:S(2)}, u32[]{:S(2)}) collective-permute-start(f32[2,64,256]{2,1,0:T(8,128)S(1)} %maximum_bitcast_fusion.1), channel_id=1, source_target_pairs={{0,8},{2,10},{4,12},{6,14},{8,0},{10,2},{12,4},{14,6},{16,24},{18,... | collective-permute-start | bytes 393224 | tf_op jit(solution)/shard_map/ppermute | solution.py:32
  101.7 6.4 %collective-permute-start.14 = (f32[4,64,256]{2,1,0:T(8,128)S(1)}, f32[4,64,256]{2,1,0:T(8,128)S(1)}, u32[]{:S(2)}, u32[]{:S(2)}) collective-permute-start(f32[4,64,256]{2,1,0:T(8,128)S(1)} %bitcast.149), channel_id=1, source_target_pairs={{0,4},{2,6},{4,0},{6,2},{8,12},{10,14},{12,8},{14,10},{16,20},{18,... | collective-permute-start | bytes 786440 | tf_op jit(solution)/shard_map/ppermute | solution.py:32
  108.2 2.0 %collective-permute-start.15 = (f32[8,64,256]{2,1,0:T(8,128)S(1)}, f32[8,64,256]{2,1,0:T(8,128)S(1)}, u32[]{:S(2)}, u32[]{:S(2)}) collective-permute-start(f32[8,64,256]{2,1,0:T(8,128)S(1)} %bitcast.147), channel_id=1, source_target_pairs={{0,2},{2,0},{4,6},{6,4},{8,10},{10,8},{12,14},{14,12},{16,18},{18,... | collective-permute-start | bytes 1572872 | tf_op jit(solution)/shard_map/ppermute | solution.py:32

commit v2 on v1

--- a/solution.py
+++ b/solution.py
@@ -36,8 +36,9 @@
     return y.reshape((-1,) + x.shape[1:])
 
 
-def make_shards(n):
+def make_shards(n, m):
     power_of_two = n > 1 and (n & (n - 1)) == 0
+    rhs_power_of_two = m > 1 and (m & (m - 1)) == 0
 
     def sum_scatter(x):
         if power_of_two:
@@ -50,18 +51,24 @@
         return lax.all_gather(x, "blk", axis=0, tiled=True)
 
     def shards(factor_panel, solved_before, right_side, diag_inverse, coupling):
-        inverse_full = lax.all_gather(diag_inverse, "rhs", axis=2, tiled=True)
+        if rhs_power_of_two:
+            pieces = doubling_gather(diag_inverse[None], "rhs", m)
+            inverse_full = jnp.concatenate(list(pieces), axis=2)
+        else:
+            inverse_full = lax.all_gather(diag_inverse, "rhs", axis=2, tiled=True)
         own_count = diag_inverse.shape[1]
         my_index = lax.axis_index("blk")
 
         def own_slice(matrix):
             return lax.dynamic_slice_in_dim(matrix, my_index * own_count, own_count, 0)
 
-        first_part = sum_scatter(product(factor_panel[0], solved_before))
+        rows = factor_panel.shape[1]
+        both_sums = product(factor_panel.reshape(2 * rows, -1), solved_before)
+        first_part = sum_scatter(both_sums[:rows])
         first_remains = gather(own_slice(right_side[0]) - first_part)
         first_block = product(inverse_full[0], first_remains)
         second_part = sum_scatter(
-            product(factor_panel[1], solved_before) + product(coupling, first_block)
+            both_sums[rows:] + product(coupling, first_block)
         )
         second_remains = gather(own_slice(right_side[1]) - second_part)
         second_block = product(inverse_full[1], second_remains)
@@ -79,5 +86,5 @@
         P(None, "blk"),
     )
     return jax.shard_map(
-        make_shards(mesh.shape["blk"]), mesh=mesh, in_specs=placed, out_specs=P(None, "blk", "rhs"), check_vma=False
+        make_shards(mesh.shape["blk"], mesh.shape["rhs"]), mesh=mesh, in_specs=placed, out_specs=P(None, "blk", "rhs"), check_vma=False
     )

time: 112 us -> 118 us (1.054)
  blocking collectives: 9.48 us -> 0 us
  waiting for transfers between devices: 48.8 us -> 57.3 us
  other arithmetic: 3.95 us -> 9.55 us
  local copies, waits for them, and re-layouts: 7.7 us -> 10.6 us
  matrix products: 13.2 us -> 11.4 us
    all_gather x1 -> x0, blocking collectives: 9.48 us -> none  [shards(): inverse_full = lax.all_gather(diag_inverse, 'rhs', axis=2, tiled=True)]
    ppermute x8 -> x9, waiting for transfers between devices: 22.5 us -> 31 us  [doubling_gather(): got = lax.ppermute(y, axis, [(i, i ^ 1 << j) for i in range(n)])]
    slice x1, local copies, waits for them, and re-layouts: 4.81 us -> 1.05 us  [shards(): first_part = sum_scatter(both_sums[:rows])]
    add x6, other arithmetic: 0.25 us -> 3.38 us  [halving_sum_scatter(): y = keep + got]
    unnamed x6, local copies, waits for them, and re-layouts: 0.01 us -> 2.23 us
    dynamic_slice x1 -> x2, local copies, waits for them, and re-layouts: 0.1 us -> 2.21 us  [halving_sum_scatter(): keep = lax.dynamic_index_in_dim(y, mine, bit_axis, keepdims=False)]
    dot_general x5 -> x4, matrix products: 13.2 us -> 11.4 us  [product(): jnp.dot(left, right, precision=lax.Precision.HIGHEST, preferred_element_t...]
    slice x1, local copies, waits for them, and re-layouts: 1.68 us -> 3.02 us  [shards(): second_remains = gather(own_slice(right_side[1]) - second_part)]
  transfers between devices with their start and end apart: 16 -> 17, of which waited for: 15 -> 15; matrix products, arithmetic and copies ran while one was open for 1% -> 3% of each run, Pallas kernels for 0% -> 0%
where the time goes in v2:
time: 118 us; the launch traced here: 117 us
  waiting for transfers between devices  57.3 us (49%)
  starting transfers between devices  28 us (24%)
  matrix products  11.4 us (10%)
  local copies, waits for them, and re-layouts  10.6 us (9%)
  other arithmetic  9.55 us (8%)
    ppermute x9, waiting for transfers between devices, doubling_gather(): got = lax.ppermute(y, axis, [(i, i ^ 1 << j) for i in range(n)])  31 us
    ppermute x8, waiting for transfers between devices, halving_sum_scatter(): got = lax.ppermute(send, axis, [(i, i ^ 1 << j) for i in range(n)])  26.3 us
    ppermute x8, starting transfers between devices, halving_sum_scatter(): got = lax.ppermute(send, axis, [(i, i ^ 1 << j) for i in range(n)])  14.4 us
    ppermute x9, starting transfers between devices, doubling_gather(): got = lax.ppermute(y, axis, [(i, i ^ 1 << j) for i in range(n)])  13.6 us
    dot_general x4, matrix products, product(): jnp.dot(left, right, precision=lax.Precision.HIGHEST, preferred_element_t...  11.4 us
    add x6, other arithmetic, halving_sum_scatter(): y = keep + got  3.38 us
    slice x1, local copies, waits for them, and re-layouts, shards(): second_remains = gather(own_slice(right_side[1]) - second_part)  3.02 us
    another operation x14, other arithmetic, doubling_gather(): y = jnp.stack([low, high], 1).reshape((-1,) + x.shape)  2.78 us
  transfers between devices with their start and end apart: 17, of which 15 were waited for; matrix products, arithmetic and copies ran while one was open for 3% of the time, Pallas kernels for 0%

profile of v2, /device:TPU:0, one launch (start us, length us, event | category | flops | bytes accessed | tf_op | source)
XLA Modules:
  0.0 117.0 jit_solution(18297368612155924148)
XLA Ops:
  1.2 9.0 %fusion.15 = f32[2048,256]{1,0:T(8,128)S(1)} fusion(f32[2048,1024]{1,0:T(8,128)} %bitcast.139, f32[1024,256]{1,0:T(8,128)S(1)} %copy-done), kind=kOutput, calls=%fused_computation.65 | convolution fusion | flops 6442450944 | bytes 11534336 | tf_op jit(solution)/shard_map/dot_general | solution.py:8
  11.3 2.1 %constant_dynamic-slice_fusion.3 = (f32[2,2,2,1,64,256]{5,4,3,2,1,0:T(8,128)}, f32[2,2,2,1,64,256]{5,4,3,2,1,0:T(8,128)S(1)}) fusion(f32[2,2,2,2,64,256]{5,4,3,2,1,0:T(8,128)} %bitcast.143, s32[]{:T(128)S(6)} %select_n.140, s32[]{:T(128)S(6)} %select_n.141), kind=kLoop, calls=%fused_computation.61 | loop fusion | bytes 2097160 | tf_op jit(solution)/shard_map/jit(dynamic_index_in_dim)/dynamic_slice | solution.py:19
  14.8 1.9 %collective-permute-done.1 = f32[2,2,2,64,256]{4,3,1,0,2:T(8,128)} collective-permute-done((f32[2,2,2,64,256]{4,3,1,0,2:T(8,128)}, f32[2,2,2,64,256]{4,3,1,0,2:T(8,128)}, u32[]{:S(2)}, u32[]{:S(2)}) %collective-permute-start.1) | collective-permute-done | bytes 524320 | tf_op jit(solution)/shard_map/ppermute | solution.py:21
  18.7 3.0 %collective-permute-start.2 = (f32[2,2,64,256]{3,2,1,0:T(8,128)S(1)}, f32[2,2,64,256]{3,2,1,0:T(8,128)}, u32[]{:S(2)}, u32[]{:S(2)}) collective-permute-start(f32[2,2,64,256]{3,2,1,0:T(8,128)S(1)} %dynamic-slice_bitcast_fusion.1), channel_id=1, source_target_pairs={{0,4},{2,6},{4,0},{6,2},{8,12},{10,14},{12,8},{14,10},{16,20},{18,... | collective-permute-start | bytes 786440 | tf_op jit(solution)/shard_map/ppermute | solution.py:21
  21.7 6.7 %collective-permute-done.2 = f32[2,2,64,256]{3,2,1,0:T(8,128)} collective-permute-done((f32[2,2,64,256]{3,2,1,0:T(8,128)S(1)}, f32[2,2,64,256]{3,2,1,0:T(8,128)}, u32[]{:S(2)}, u32[]{:S(2)}) %collective-permute-start.2) | collective-permute-done | bytes 262176 | tf_op jit(solution)/shard_map/ppermute | solution.py:21
  29.5 1.9 %collective-permute-start.3 = (f32[2,64,256]{2,1,0:T(8,128)S(1)}, f32[2,64,256]{2,1,0:T(8,128)}, u32[]{:S(2)}, u32[]{:S(2)}) collective-permute-start(f32[2,64,256]{2,1,0:T(8,128)S(1)} %dynamic-slice_bitcast_fusion.3), channel_id=1, source_target_pairs={{0,8},{2,10},{4,12},{6,14},{8,0},{10,2},{12,4},{14,6},{16,24},{18,... | collective-permute-start | bytes 393224 | tf_op jit(solution)/shard_map/ppermute | solution.py:21
  31.4 3.3 %collective-permute-done.3 = f32[2,64,256]{2,1,0:T(8,128)} collective-permute-done((f32[2,64,256]{2,1,0:T(8,128)S(1)}, f32[2,64,256]{2,1,0:T(8,128)}, u32[]{:S(2)}, u32[]{:S(2)}) %collective-permute-start.3) | collective-permute-done | bytes 131104 | tf_op jit(solution)/shard_map/ppermute | solution.py:21
  35.6 2.8 %collective-permute-start.4 = (f32[64,256]{1,0:T(8,128)S(1)}, f32[64,256]{1,0:T(8,128)S(1)}, u32[]{:S(2)}, u32[]{:S(2)}) collective-permute-start(f32[64,256]{1,0:T(8,128)S(1)} %dynamic-slice_bitcast_fusion.5), channel_id=1, source_target_pairs={{0,16},{2,18},{4,20},{6,22},{8,24},{10,26},{12,28},{14,30},{16,0},... | collective-permute-start | bytes 196616 | tf_op jit(solution)/shard_map/ppermute | solution.py:21
  38.5 3.0 %fusion.14 = (f32[1,1024,256]{2,1,0:T(8,128)}, f32[1,1024,256]{2,1,0:T(8,128)}) fusion(f32[2,1024,256]{2,1,0:T(8,128)} %param.7), kind=kLoop, calls=%fused_computation.64 | loop fusion | bytes 4194304 | tf_op jit(solution)/shard_map/slice | solution.py:73
  42.3 2.3 %collective-permute-start.5 = (f32[1,64,256]{2,1,0:T(8,128)S(1)}, f32[1,64,256]{2,1,0:T(8,128)S(1)}, u32[]{:S(2)}, u32[]{:S(2)}) collective-permute-start(f32[1,64,256]{2,1,0:T(8,128)S(1)} %fusion.11), channel_id=1, source_target_pairs={{0,16},{2,18},{4,20},{6,22},{8,24},{10,26},{12,28},{14,30},{16,0},... | collective-permute-start | bytes 196616 | tf_op jit(solution)/shard_map/ppermute | solution.py:32
  44.6 3.0 %collective-permute-done.5 = f32[1,64,256]{2,1,0:T(8,128)S(1)} collective-permute-done((f32[1,64,256]{2,1,0:T(8,128)S(1)}, f32[1,64,256]{2,1,0:T(8,128)S(1)}, u32[]{:S(2)}, u32[]{:S(2)}) %collective-permute-start.5) | collective-permute-done | bytes 65568 | tf_op jit(solution)/shard_map/ppermute | solution.py:32
  47.7 2.0 %collective-permute-start.6 = (f32[2,64,256]{2,1,0:T(8,128)S(1)}, f32[2,64,256]{2,1,0:T(8,128)S(1)}, u32[]{:S(2)}, u32[]{:S(2)}) collective-permute-start(f32[2,64,256]{2,1,0:T(8,128)S(1)} %maximum_bitcast_fusion), channel_id=1, source_target_pairs={{0,8},{2,10},{4,12},{6,14},{8,0},{10,2},{12,4},{14,6},{16,24},{18,... | collective-permute-start | bytes 393224 | tf_op jit(solution)/shard_map/ppermute | solution.py:32
  49.6 3.1 %collective-permute-done.6 = f32[2,64,256]{2,1,0:T(8,128)S(1)} collective-permute-done((f32[2,64,256]{2,1,0:T(8,128)S(1)}, f32[2,64,256]{2,1,0:T(8,128)S(1)}, u32[]{:S(2)}, u32[]{:S(2)}) %collective-permute-start.6) | collective-permute-done | bytes 131104 | tf_op jit(solution)/shard_map/ppermute | solution.py:32
  52.7 1.6 %collective-permute-start.7 = (f32[4,64,256]{2,1,0:T(8,128)S(1)}, f32[4,64,256]{2,1,0:T(8,128)}, u32[]{:S(2)}, u32[]{:S(2)}) collective-permute-start(f32[4,64,256]{2,1,0:T(8,128)S(1)} %bitcast.145), channel_id=1, source_target_pairs={{0,4},{2,6},{4,0},{6,2},{8,12},{10,14},{12,8},{14,10},{16,20},{18,... | collective-permute-start | bytes 786440 | tf_op jit(solution)/shard_map/ppermute | solution.py:32
  54.3 5.0 %collective-permute-done.7 = f32[4,64,256]{2,1,0:T(8,128)} collective-permute-done((f32[4,64,256]{2,1,0:T(8,128)S(1)}, f32[4,64,256]{2,1,0:T(8,128)}, u32[]{:S(2)}, u32[]{:S(2)}) %collective-permute-start.7) | collective-permute-done | bytes 262176 | tf_op jit(solution)/shard_map/ppermute | solution.py:32
  61.2 1.5 %collective-permute-start = (f32[1,1,2,64,512]{4,3,2,1,0:T(8,128)}, f32[1,1,2,64,512]{4,3,2,1,0:T(8,128)S(1)}, u32[]{:S(2)}, u32[]{:S(2)}) collective-permute-start(f32[1,1,2,64,512]{4,3,2,1,0:T(8,128)} %bitcast), channel_id=1, source_target_pairs={{0,1},{1,0},{2,3},{3,2},{4,5},{5,4},{6,7},{7,6},{8,9},{9,8},{10,11... | collective-permute-start | bytes 786440 | tf_op jit(solution)/shard_map/ppermute | solution.py:32
  62.7 7.4 %collective-permute-done = f32[1,1,2,64,512]{4,3,2,1,0:T(8,128)S(1)} collective-permute-done((f32[1,1,2,64,512]{4,3,2,1,0:T(8,128)}, f32[1,1,2,64,512]{4,3,2,1,0:T(8,128)S(1)}, u32[]{:S(2)}, u32[]{:S(2)}) %collective-permute-start) | collective-permute-done | bytes 262176 | tf_op jit(solution)/shard_map/ppermute | solution.py:32
  71.1 1.3 %select_bitcast_fusion.3 = (f32[8,1,64,256]{3,2,0,1:T(8,128)S(1)}, f32[8,1,64,256]{3,2,0,1:T(8,128)S(1)}) fusion(f32[8,64,256]{2,1,0:T(8,128)} %collective-permute-done.8, pred[]{:T(512)S(6)} %eq.11, f32[4,2,64,256]{3,2,1,0:T(8,128)} %copy.21), kind=kLoop, calls=%fused_computation.16 | loop fusion | flops 262144 | bytes 2097153 | tf_op jit(solution)/shard_map/stack | solution.py:35
  74.7 1.9 %collective-permute-done.9 = f32[2,2,2,64,256]{4,3,1,0,2:T(8,128)S(1)} collective-permute-done((f32[2,2,2,64,256]{4,3,1,0,2:T(8,128)S(1)}, f32[2,2,2,64,256]{4,3,1,0,2:T(8,128)S(1)}, u32[]{:S(2)}, u32[]{:S(2)}) %collective-permute-start.9) | collective-permute-done | bytes 524320 | tf_op jit(solution)/shard_map/ppermute | solution.py:21
  76.7 1.6 %collective-permute-start.10 = (f32[2,2,64,256]{3,2,1,0:T(8,128)S(1)}, f32[2,2,64,256]{3,2,1,0:T(8,128)S(1)}, u32[]{:S(2)}, u32[]{:S(2)}) collective-permute-start(f32[2,2,64,256]{3,2,1,0:T(8,128)S(1)} %dynamic-slice_bitcast_fusion), channel_id=1, source_target_pairs={{0,4},{2,6},{4,0},{6,2},{8,12},{10,14},{12,8},{14,10},{16,20},{18,... | collective-permute-start | bytes 786440 | tf_op jit(solution)/shard_map/ppermute | solution.py:21
  78.3 6.8 %collective-permute-done.10 = f32[2,2,64,256]{3,2,1,0:T(8,128)S(1)} collective-permute-done((f32[2,2,64,256]{3,2,1,0:T(8,128)S(1)}, f32[2,2,64,256]{3,2,1,0:T(8,128)S(1)}, u32[]{:S(2)}, u32[]{:S(2)}) %collective-permute-start.10) | collective-permute-done | bytes 262176 | tf_op jit(solution)/shard_map/ppermute | solution.py:21
  85.2 2.0 %collective-permute-start.11 = (f32[2,64,256]{2,1,0:T(8,128)S(1)}, f32[2,64,256]{2,1,0:T(8,128)S(1)}, u32[]{:S(2)}, u32[]{:S(2)}) collective-permute-start(f32[2,64,256]{2,1,0:T(8,128)S(1)} %dynamic-slice_bitcast_fusion.2), channel_id=1, source_target_pairs={{0,8},{2,10},{4,12},{6,14},{8,0},{10,2},{12,4},{14,6},{16,24},{18,... | collective-permute-start | bytes 393224 | tf_op jit(solution)/shard_map/ppermute | solution.py:21
  87.2 3.1 %collective-permute-done.11 = f32[2,64,256]{2,1,0:T(8,128)S(1)} collective-permute-done((f32[2,64,256]{2,1,0:T(8,128)S(1)}, f32[2,64,256]{2,1,0:T(8,128)S(1)}, u32[]{:S(2)}, u32[]{:S(2)}) %collective-permute-start.11) | collective-permute-done | bytes 131104 | tf_op jit(solution)/shard_map/ppermute | solution.py:21
  90.3 2.6 %collective-permute-start.12 = (f32[64,256]{1,0:T(8,128)S(1)}, f32[64,256]{1,0:T(8,128)S(1)}, u32[]{:S(2)}, u32[]{:S(2)}) collective-permute-start(f32[64,256]{1,0:T(8,128)S(1)} %dynamic-slice_bitcast_fusion.4), channel_id=1, source_target_pairs={{0,16},{2,18},{4,20},{6,22},{8,24},{10,26},{12,28},{14,30},{16,0},... | collective-permute-start | bytes 196616 | tf_op jit(solution)/shard_map/ppermute | solution.py:21
  92.9 2.6 %collective-permute-done.12 = f32[64,256]{1,0:T(8,128)S(1)} collective-permute-done((f32[64,256]{1,0:T(8,128)S(1)}, f32[64,256]{1,0:T(8,128)S(1)}, u32[]{:S(2)}, u32[]{:S(2)}) %collective-permute-start.12) | collective-permute-done | bytes 65568 | tf_op jit(solution)/shard_map/ppermute | solution.py:21
  96.4 2.7 %collective-permute-start.13 = (f32[1,64,256]{2,1,0:T(8,128)S(1)}, f32[1,64,256]{2,1,0:T(8,128)S(1)}, u32[]{:S(2)}, u32[]{:S(2)}) collective-permute-start(f32[1,64,256]{2,1,0:T(8,128)S(1)} %fusion.9), channel_id=1, source_target_pairs={{0,16},{2,18},{4,20},{6,22},{8,24},{10,26},{12,28},{14,30},{16,0},... | collective-permute-start | bytes 196616 | tf_op jit(solution)/shard_map/ppermute | solution.py:32
  99.1 2.7 %collective-permute-done.13 = f32[1,64,256]{2,1,0:T(8,128)S(1)} collective-permute-done((f32[1,64,256]{2,1,0:T(8,128)S(1)}, f32[1,64,256]{2,1,0:T(8,128)S(1)}, u32[]{:S(2)}, u32[]{:S(2)}) %collective-permute-start.13) | collective-permute-done | bytes 65568 | tf_op jit(solution)/shard_map/ppermute | solution.py:32
  101.8 2.0 %collective-permute-start.14 = (f32[2,64,256]{2,1,0:T(8,128)S(1)}, f32[2,64,256]{2,1,0:T(8,128)S(1)}, u32[]{:S(2)}, u32[]{:S(2)}) collective-permute-start(f32[2,64,256]{2,1,0:T(8,128)S(1)} %maximum_bitcast_fusion.1), channel_id=1, source_target_pairs={{0,8},{2,10},{4,12},{6,14},{8,0},{10,2},{12,4},{14,6},{16,24},{18,... | collective-permute-start | bytes 393224 | tf_op jit(solution)/shard_map/ppermute | solution.py:32
  103.8 3.0 %collective-permute-done.14 = f32[2,64,256]{2,1,0:T(8,128)S(1)} collective-permute-done((f32[2,64,256]{2,1,0:T(8,128)S(1)}, f32[2,64,256]{2,1,0:T(8,128)S(1)}, u32[]{:S(2)}, u32[]{:S(2)}) %collective-permute-start.14) | collective-permute-done | bytes 131104 | tf_op jit(solution)/shard_map/ppermute | solution.py:32
  106.9 1.6 %collective-permute-start.15 = (f32[4,64,256]{2,1,0:T(8,128)S(1)}, f32[4,64,256]{2,1,0:T(8,128)S(1)}, u32[]{:S(2)}, u32[]{:S(2)}) collective-permute-start(f32[4,64,256]{2,1,0:T(8,128)S(1)} %bitcast.146), channel_id=1, source_target_pairs={{0,4},{2,6},{4,0},{6,2},{8,12},{10,14},{12,8},{14,10},{16,20},{18,... | collective-permute-start | bytes 786440 | tf_op jit(solution)/shard_map/ppermute | solution.py:32
  108.5 4.9 %collective-permute-done.15 = f32[4,64,256]{2,1,0:T(8,128)S(1)} collective-permute-done((f32[4,64,256]{2,1,0:T(8,128)S(1)}, f32[4,64,256]{2,1,0:T(8,128)S(1)}, u32[]{:S(2)}, u32[]{:S(2)}) %collective-permute-start.15) | collective-permute-done | bytes 262176 | tf_op jit(solution)/shard_map/ppermute | solution.py:32
  113.5 1.9 %collective-permute-done.16 = f32[8,64,256]{2,1,0:T(8,128)S(1)} collective-permute-done((f32[8,64,256]{2,1,0:T(8,128)S(1)}, f32[8,64,256]{2,1,0:T(8,128)S(1)}, u32[]{:S(2)}, u32[]{:S(2)}) %collective-permute-start.16) | collective-permute-done | bytes 524320 | tf_op jit(solution)/shard_map/ppermute | solution.py:32
  (55 shorter events, 16.6 us)
Async XLA Ops:
  0.0 1.2 %copy-start = (f32[1024,256]{1,0:T(8,128)S(1)}, f32[1024,256]{1,0:T(8,128)}, u32[]{:S(2)}) copy-start(f32[1024,256]{1,0:T(8,128)} %param.6) | copy-start | bytes 3145732
  14.3 2.3 %collective-permute-start.1 = (f32[2,2,2,64,256]{4,3,1,0,2:T(8,128)}, f32[2,2,2,64,256]{4,3,1,0,2:T(8,128)}, u32[]{:S(2)}, u32[]{:S(2)}) collective-permute-start(f32[2,2,2,64,256]{4,3,1,0,2:T(8,128)} %bitcast.138), channel_id=1, source_target_pairs={{0,2},{2,0},{4,6},{6,4},{8,10},{10,8},{12,14},{14,12},{16,18},{18,... | collective-permute-start | bytes 1572872 | tf_op jit(solution)/shard_map/ppermute | solution.py:21
  17.9 0.8 copy-start.1
  18.7 9.7 %collective-permute-start.2 = (f32[2,2,64,256]{3,2,1,0:T(8,128)S(1)}, f32[2,2,64,256]{3,2,1,0:T(8,128)}, u32[]{:S(2)}, u32[]{:S(2)}) collective-permute-start(f32[2,2,64,256]{3,2,1,0:T(8,128)S(1)} %dynamic-slice_bitcast_fusion.1), channel_id=1, source_target_pairs={{0,4},{2,6},{4,0},{6,2},{8,12},{10,14},{12,8},{14,10},{16,20},{18,... | collective-permute-start | bytes 786440 | tf_op jit(solution)/shard_map/ppermute | solution.py:21
  29.5 5.2 %collective-permute-start.3 = (f32[2,64,256]{2,1,0:T(8,128)S(1)}, f32[2,64,256]{2,1,0:T(8,128)}, u32[]{:S(2)}, u32[]{:S(2)}) collective-permute-start(f32[2,64,256]{2,1,0:T(8,128)S(1)} %dynamic-slice_bitcast_fusion.3), channel_id=1, source_target_pairs={{0,8},{2,10},{4,12},{6,14},{8,0},{10,2},{12,4},{14,6},{16,24},{18,... | collective-permute-start | bytes 393224 | tf_op jit(solution)/shard_map/ppermute | solution.py:21
  35.6 5.8 %collective-permute-start.4 = (f32[64,256]{1,0:T(8,128)S(1)}, f32[64,256]{1,0:T(8,128)S(1)}, u32[]{:S(2)}, u32[]{:S(2)}) collective-permute-start(f32[64,256]{1,0:T(8,128)S(1)} %dynamic-slice_bitcast_fusion.5), channel_id=1, source_target_pairs={{0,16},{2,18},{4,20},{6,22},{8,24},{10,26},{12,28},{14,30},{16,0},... | collective-permute-start | bytes 196616 | tf_op jit(solution)/shard_map/ppermute | solution.py:21
  42.3 5.3 %collective-permute-start.5 = (f32[1,64,256]{2,1,0:T(8,128)S(1)}, f32[1,64,256]{2,1,0:T(8,128)S(1)}, u32[]{:S(2)}, u32[]{:S(2)}) collective-permute-start(f32[1,64,256]{2,1,0:T(8,128)S(1)} %fusion.11), channel_id=1, source_target_pairs={{0,16},{2,18},{4,20},{6,22},{8,24},{10,26},{12,28},{14,30},{16,0},... | collective-permute-start | bytes 196616 | tf_op jit(solution)/shard_map/ppermute | solution.py:32
  47.7 5.0 %collective-permute-start.6 = (f32[2,64,256]{2,1,0:T(8,128)S(1)}, f32[2,64,256]{2,1,0:T(8,128)S(1)}, u32[]{:S(2)}, u32[]{:S(2)}) collective-permute-start(f32[2,64,256]{2,1,0:T(8,128)S(1)} %maximum_bitcast_fusion), channel_id=1, source_target_pairs={{0,8},{2,10},{4,12},{6,14},{8,0},{10,2},{12,4},{14,6},{16,24},{18,... | collective-permute-start | bytes 393224 | tf_op jit(solution)/shard_map/ppermute | solution.py:32
  52.7 6.5 %collective-permute-start.7 = (f32[4,64,256]{2,1,0:T(8,128)S(1)}, f32[4,64,256]{2,1,0:T(8,128)}, u32[]{:S(2)}, u32[]{:S(2)}) collective-permute-start(f32[4,64,256]{2,1,0:T(8,128)S(1)} %bitcast.145), channel_id=1, source_target_pairs={{0,4},{2,6},{4,0},{6,2},{8,12},{10,14},{12,8},{14,10},{16,20},{18,... | collective-permute-start | bytes 786440 | tf_op jit(solution)/shard_map/ppermute | solution.py:32
  61.2 9.9 %collective-permute-start.8 = (f32[8,64,256]{2,1,0:T(8,128)}, f32[8,64,256]{2,1,0:T(8,128)}, u32[]{:S(2)}, u32[]{:S(2)}) collective-permute-start(f32[8,64,256]{2,1,0:T(8,128)} %bitcast.25), channel_id=1, source_target_pairs={{0,2},{2,0},{4,6},{6,4},{8,10},{10,8},{12,14},{14,12},{16,18},{18,... | collective-permute-start | bytes 1572872 | tf_op jit(solution)/shard_map/ppermute | solution.py:32
  61.2 8.9 %collective-permute-start = (f32[1,1,2,64,512]{4,3,2,1,0:T(8,128)}, f32[1,1,2,64,512]{4,3,2,1,0:T(8,128)S(1)}, u32[]{:S(2)}, u32[]{:S(2)}) collective-permute-start(f32[1,1,2,64,512]{4,3,2,1,0:T(8,128)} %bitcast), channel_id=1, source_target_pairs={{0,1},{1,0},{2,3},{3,2},{4,5},{5,4},{6,7},{7,6},{8,9},{9,8},{10,11... | collective-permute-start | bytes 786440 | tf_op jit(solution)/shard_map/ppermute | solution.py:32
  72.5 1.0 copy-start.2
  74.7 2.0 %collective-permute-start.9 = (f32[2,2,2,64,256]{4,3,1,0,2:T(8,128)S(1)}, f32[2,2,2,64,256]{4,3,1,0,2:T(8,128)S(1)}, u32[]{:S(2)}, u32[]{:S(2)}) collective-permute-start(f32[2,2,2,64,256]{4,3,1,0,2:T(8,128)S(1)} %bitcast.148), channel_id=1, source_target_pairs={{0,2},{2,0},{4,6},{6,4},{8,10},{10,8},{12,14},{14,12},{16,18},{18,... | collective-permute-start | bytes 1572872 | tf_op jit(solution)/shard_map/ppermute | solution.py:21
  76.7 8.4 %collective-permute-start.10 = (f32[2,2,64,256]{3,2,1,0:T(8,128)S(1)}, f32[2,2,64,256]{3,2,1,0:T(8,128)S(1)}, u32[]{:S(2)}, u32[]{:S(2)}) collective-permute-start(f32[2,2,64,256]{3,2,1,0:T(8,128)S(1)} %dynamic-slice_bitcast_fusion), channel_id=1, source_target_pairs={{0,4},{2,6},{4,0},{6,2},{8,12},{10,14},{12,8},{14,10},{16,20},{18,... | collective-permute-start | bytes 786440 | tf_op jit(solution)/shard_map/ppermute | solution.py:21
  85.2 5.0 %collective-permute-start.11 = (f32[2,64,256]{2,1,0:T(8,128)S(1)}, f32[2,64,256]{2,1,0:T(8,128)S(1)}, u32[]{:S(2)}, u32[]{:S(2)}) collective-permute-start(f32[2,64,256]{2,1,0:T(8,128)S(1)} %dynamic-slice_bitcast_fusion.2), channel_id=1, source_target_pairs={{0,8},{2,10},{4,12},{6,14},{8,0},{10,2},{12,4},{14,6},{16,24},{18,... | collective-permute-start | bytes 393224 | tf_op jit(solution)/shard_map/ppermute | solution.py:21
  90.3 5.2 %collective-permute-start.12 = (f32[64,256]{1,0:T(8,128)S(1)}, f32[64,256]{1,0:T(8,128)S(1)}, u32[]{:S(2)}, u32[]{:S(2)}) collective-permute-start(f32[64,256]{1,0:T(8,128)S(1)} %dynamic-slice_bitcast_fusion.4), channel_id=1, source_target_pairs={{0,16},{2,18},{4,20},{6,22},{8,24},{10,26},{12,28},{14,30},{16,0},... | collective-permute-start | bytes 196616 | tf_op jit(solution)/shard_map/ppermute | solution.py:21
  96.4 5.3 %collective-permute-start.13 = (f32[1,64,256]{2,1,0:T(8,128)S(1)}, f32[1,64,256]{2,1,0:T(8,128)S(1)}, u32[]{:S(2)}, u32[]{:S(2)}) collective-permute-start(f32[1,64,256]{2,1,0:T(8,128)S(1)} %fusion.9), channel_id=1, source_target_pairs={{0,16},{2,18},{4,20},{6,22},{8,24},{10,26},{12,28},{14,30},{16,0},... | collective-permute-start | bytes 196616 | tf_op jit(solution)/shard_map/ppermute | solution.py:32
  101.8 5.0 %collective-permute-start.14 = (f32[2,64,256]{2,1,0:T(8,128)S(1)}, f32[2,64,256]{2,1,0:T(8,128)S(1)}, u32[]{:S(2)}, u32[]{:S(2)}) collective-permute-start(f32[2,64,256]{2,1,0:T(8,128)S(1)} %maximum_bitcast_fusion.1), channel_id=1, source_target_pairs={{0,8},{2,10},{4,12},{6,14},{8,0},{10,2},{12,4},{14,6},{16,24},{18,... | collective-permute-start | bytes 393224 | tf_op jit(solution)/shard_map/ppermute | solution.py:32
  106.9 6.4 %collective-permute-start.15 = (f32[4,64,256]{2,1,0:T(8,128)S(1)}, f32[4,64,256]{2,1,0:T(8,128)S(1)}, u32[]{:S(2)}, u32[]{:S(2)}) collective-permute-start(f32[4,64,256]{2,1,0:T(8,128)S(1)} %bitcast.146), channel_id=1, source_target_pairs={{0,4},{2,6},{4,0},{6,2},{8,12},{10,14},{12,8},{14,10},{16,20},{18,... | collective-permute-start | bytes 786440 | tf_op jit(solution)/shard_map/ppermute | solution.py:32
  113.5 2.0 %collective-permute-start.16 = (f32[8,64,256]{2,1,0:T(8,128)S(1)}, f32[8,64,256]{2,1,0:T(8,128)S(1)}, u32[]{:S(2)}, u32[]{:S(2)}) collective-permute-start(f32[8,64,256]{2,1,0:T(8,128)S(1)} %bitcast.144), channel_id=1, source_target_pairs={{0,2},{2,0},{4,6},{6,4},{8,10},{10,8},{12,14},{14,12},{16,18},{18,... | collective-permute-start | bytes 1572872 | tf_op jit(solution)/shard_map/ppermute | solution.py:32

commit v3 on v2

--- a/solution.py
+++ b/solution.py
@@ -8,7 +8,7 @@
     return jnp.dot(left, right, precision=lax.Precision.HIGHEST, preferred_element_type=jnp.float32)
 
 
-def halving_sum_scatter(x, axis, n):
+def halving_sum_scatter(x, axis, n, riders=None):
     k = n.bit_length() - 1
     me = lax.axis_index(axis)
     rows = x.shape[0] // n
@@ -19,8 +19,10 @@
         keep = lax.dynamic_index_in_dim(y, mine, bit_axis, keepdims=False)
         send = lax.dynamic_index_in_dim(y, 1 - mine, bit_axis, keepdims=False)
         got = lax.ppermute(send, axis, [(i, i ^ (1 << j)) for i in range(n)])
+        if j == 1 and riders is not None:
+            got, riders = lax.optimization_barrier((got, riders))
         y = keep + got
-    return y.reshape((rows,) + x.shape[1:])
+    return y.reshape((rows,) + x.shape[1:]), riders
 
 
 def doubling_gather(x, axis, n):
@@ -40,10 +42,10 @@
     power_of_two = n > 1 and (n & (n - 1)) == 0
     rhs_power_of_two = m > 1 and (m & (m - 1)) == 0
 
-    def sum_scatter(x):
-        if power_of_two:
-            return halving_sum_scatter(x, "blk", n)
-        return lax.psum_scatter(x, "blk", scatter_dimension=0, tiled=True)
+    def sum_scatter(x, riders=None):
+        if power_of_two and n >= 4:
+            return halving_sum_scatter(x, "blk", n, riders)
+        return lax.psum_scatter(x, "blk", scatter_dimension=0, tiled=True), riders
 
     def gather(x):
         if power_of_two:
@@ -52,24 +54,23 @@
 
     def shards(factor_panel, solved_before, right_side, diag_inverse, coupling):
         if rhs_power_of_two:
-            pieces = doubling_gather(diag_inverse[None], "rhs", m)
-            inverse_full = jnp.concatenate(list(pieces), axis=2)
+            inverse_pieces = doubling_gather(diag_inverse[None], "rhs", m)
         else:
-            inverse_full = lax.all_gather(diag_inverse, "rhs", axis=2, tiled=True)
+            inverse_pieces = lax.all_gather(diag_inverse, "rhs", axis=0)
         own_count = diag_inverse.shape[1]
         my_index = lax.axis_index("blk")
 
         def own_slice(matrix):
             return lax.dynamic_slice_in_dim(matrix, my_index * own_count, own_count, 0)
 
-        rows = factor_panel.shape[1]
-        both_sums = product(factor_panel.reshape(2 * rows, -1), solved_before)
-        first_part = sum_scatter(both_sums[:rows])
+        first_sum = product(factor_panel[0], solved_before)
+        first_sum, inverse_pieces = lax.optimization_barrier((first_sum, inverse_pieces))
+        inverse_full = jnp.concatenate(list(inverse_pieces), axis=2)
+        panel_sum = product(factor_panel[1], solved_before)
+        first_part, panel_sum = sum_scatter(first_sum, panel_sum)
         first_remains = gather(own_slice(right_side[0]) - first_part)
         first_block = product(inverse_full[0], first_remains)
-        second_part = sum_scatter(
-            both_sums[rows:] + product(coupling, first_block)
-        )
+        second_part, _ = sum_scatter(panel_sum + product(coupling, first_block))
         second_remains = gather(own_slice(right_side[1]) - second_part)
         second_block = product(inverse_full[1], second_remains)
         return jnp.stack([first_block, second_block])

time: 118 us -> 97.3 us (0.82)
  waiting for transfers between devices: 57.3 us -> 47.4 us
  local copies, waits for them, and re-layouts: 10.6 us -> 3.78 us
  other arithmetic: 9.55 us -> 4.57 us
  matrix products: 11.4 us -> 12.8 us
    ppermute x8, waiting for transfers between devices: 26.3 us -> 20.7 us  [halving_sum_scatter(): got = lax.ppermute(send, axis, [(i, i ^ 1 << j) for i in range(n)])]
    ppermute x9, waiting for transfers between devices: 31 us -> 26.7 us  [doubling_gather(): got = lax.ppermute(y, axis, [(i, i ^ 1 << j) for i in range(n)])]
    add x6, other arithmetic: 3.38 us -> 0.25 us  [halving_sum_scatter(): y = keep + got]
    unnamed x6, local copies, waits for them, and re-layouts: 2.23 us -> 0.01 us
    dynamic_slice x2, local copies, waits for them, and re-layouts: 2.21 us -> 0.2 us  [halving_sum_scatter(): keep = lax.dynamic_index_in_dim(y, mine, bit_axis, keepdims=False)]
    ppermute x9, starting transfers between devices: 13.6 us -> 15.1 us  [doubling_gather(): got = lax.ppermute(y, axis, [(i, i ^ 1 << j) for i in range(n)])]
    dot_general x4 -> x5, matrix products: 11.4 us -> 12.8 us  [product(): jnp.dot(left, right, precision=lax.Precision.HIGHEST, preferred_element_t...]
    ppermute x8, starting transfers between devices: 14.4 us -> 13 us  [halving_sum_scatter(): got = lax.ppermute(send, axis, [(i, i ^ 1 << j) for i in range(n)])]
  transfers between devices with their start and end apart: 17 -> 17, of which waited for: 15 -> 16; matrix products, arithmetic and copies ran while one was open for 3% -> 14% of each run, Pallas kernels for 0% -> 0%
where the time goes in v3:
time: 97.3 us; the launch traced here: 97 us
  waiting for transfers between devices  47.4 us (49%)
  starting transfers between devices  28.1 us (29%)
  matrix products  12.8 us (13%)
  other arithmetic  4.57 us (5%)
  local copies, waits for them, and re-layouts  3.78 us (4%)
    ppermute x9, waiting for transfers between devices, doubling_gather(): got = lax.ppermute(y, axis, [(i, i ^ 1 << j) for i in range(n)])  26.7 us
    ppermute x8, waiting for transfers between devices, halving_sum_scatter(): got = lax.ppermute(send, axis, [(i, i ^ 1 << j) for i in range(n)])  20.7 us
    ppermute x9, starting transfers between devices, doubling_gather(): got = lax.ppermute(y, axis, [(i, i ^ 1 << j) for i in range(n)])  15.1 us
    ppermute x8, starting transfers between devices, halving_sum_scatter(): got = lax.ppermute(send, axis, [(i, i ^ 1 << j) for i in range(n)])  13 us
    dot_general x5, matrix products, product(): jnp.dot(left, right, precision=lax.Precision.HIGHEST, preferred_element_t...  12.8 us
    slice x1, local copies, waits for them, and re-layouts, shards(): second_remains = gather(own_slice(right_side[1]) - second_part)  3.04 us
  transfers between devices with their start and end apart: 17, of which 16 were waited for; matrix products, arithmetic and copies ran while one was open for 14% of the time, Pallas kernels for 0%

profile of v3, /device:TPU:0, one launch (start us, length us, event | category | flops | bytes accessed | tf_op | source)
XLA Modules:
  0.0 97.0 jit_solution(16073319038626640303)
XLA Ops:
  0.0 2.9 %collective-permute-start = (f32[1,1,2,64,512]{4,3,2,1,0:T(8,128)}, f32[1,1,2,64,512]{4,3,2,1,0:T(8,128)S(1)}, u32[]{:S(2)}, u32[]{:S(2)}) collective-permute-start(f32[1,1,2,64,512]{4,3,2,1,0:T(8,128)} %bitcast.159), channel_id=1, source_target_pairs={{0,1},{1,0},{2,3},{3,2},{4,5},{5,4},{6,7},{7,6},{8,9},{9,8},{10,11... | collective-permute-start | bytes 786440 | tf_op jit(solution)/shard_map/ppermute | solution.py:34
  2.9 5.2 %fusion.2 = f32[1024,256]{1,0:T(8,128)S(1)} fusion(f32[1024,256]{1,0:T(8,128)S(1)} %copy-done, f32[2,1024,1024]{2,1,0:T(8,128)} %param.5), kind=kOutput, calls=%fused_computation.2 | convolution fusion | flops 3221225472 | bytes 6291456 | tf_op jit(solution)/shard_map/dot_general | solution.py:8
  8.2 1.3 %collective-permute-done = f32[1,1,2,64,512]{4,3,2,1,0:T(8,128)S(1)} collective-permute-done((f32[1,1,2,64,512]{4,3,2,1,0:T(8,128)}, f32[1,1,2,64,512]{4,3,2,1,0:T(8,128)S(1)}, u32[]{:S(2)}, u32[]{:S(2)}) %collective-permute-start) | collective-permute-done | bytes 262176 | tf_op jit(solution)/shard_map/ppermute | solution.py:34
  9.8 1.9 %collective-permute-done.1 = f32[2,2,2,64,256]{4,3,1,0,2:T(8,128)S(1)} collective-permute-done((f32[2,2,2,64,256]{4,3,1,0,2:T(8,128)S(1)}, f32[2,2,2,64,256]{4,3,1,0,2:T(8,128)S(1)}, u32[]{:S(2)}, u32[]{:S(2)}) %collective-permute-start.1) | collective-permute-done | bytes 524320 | tf_op jit(solution)/shard_map/ppermute | solution.py:21
  11.8 1.8 %collective-permute-start.2 = (f32[2,2,64,256]{3,2,1,0:T(8,128)S(1)}, f32[2,2,64,256]{3,2,1,0:T(8,128)S(1)}, u32[]{:S(2)}, u32[]{:S(2)}) collective-permute-start(f32[2,2,64,256]{3,2,1,0:T(8,128)S(1)} %dynamic-slice_bitcast_fusion.1), channel_id=1, source_target_pairs={{0,4},{2,6},{4,0},{6,2},{8,12},{10,14},{12,8},{14,10},{16,20},{18,... | collective-permute-start | bytes 786440 | tf_op jit(solution)/shard_map/ppermute | solution.py:21
  13.7 5.2 %fusion = f32[1024,256]{1,0:T(8,128)S(1)} fusion(f32[1024,256]{1,0:T(8,128)S(1)} %copy-done, f32[2,1024,1024]{2,1,0:T(8,128)} %param.5), kind=kOutput, calls=%fused_computation | convolution fusion | flops 3221225472 | bytes 6291456 | tf_op jit(solution)/shard_map/dot_general | solution.py:8
  18.9 1.4 %collective-permute-done.2 = f32[2,2,64,256]{3,2,1,0:T(8,128)S(1)} collective-permute-done((f32[2,2,64,256]{3,2,1,0:T(8,128)S(1)}, f32[2,2,64,256]{3,2,1,0:T(8,128)S(1)}, u32[]{:S(2)}, u32[]{:S(2)}) %collective-permute-start.2) | collective-permute-done | bytes 262176 | tf_op jit(solution)/shard_map/ppermute | solution.py:21
  20.3 1.9 %collective-permute-start.3 = (f32[2,64,256]{2,1,0:T(8,128)S(1)}, f32[2,64,256]{2,1,0:T(8,128)S(1)}, u32[]{:S(2)}, u32[]{:S(2)}) collective-permute-start(f32[2,64,256]{2,1,0:T(8,128)S(1)} %dynamic-slice_bitcast_fusion.3), channel_id=1, source_target_pairs={{0,8},{2,10},{4,12},{6,14},{8,0},{10,2},{12,4},{14,6},{16,24},{18,... | collective-permute-start | bytes 393224 | tf_op jit(solution)/shard_map/ppermute | solution.py:21
  22.2 3.2 %collective-permute-done.3 = f32[2,64,256]{2,1,0:T(8,128)S(1)} collective-permute-done((f32[2,64,256]{2,1,0:T(8,128)S(1)}, f32[2,64,256]{2,1,0:T(8,128)S(1)}, u32[]{:S(2)}, u32[]{:S(2)}) %collective-permute-start.3) | collective-permute-done | bytes 131104 | tf_op jit(solution)/shard_map/ppermute | solution.py:21
  25.4 2.9 %collective-permute-start.4 = (f32[64,256]{1,0:T(8,128)S(1)}, f32[64,256]{1,0:T(8,128)S(1)}, u32[]{:S(2)}, u32[]{:S(2)}) collective-permute-start(f32[64,256]{1,0:T(8,128)S(1)} %dynamic-slice_bitcast_fusion.5), channel_id=1, source_target_pairs={{0,16},{2,18},{4,20},{6,22},{8,24},{10,26},{12,28},{14,30},{16,0},... | collective-permute-start | bytes 196616 | tf_op jit(solution)/shard_map/ppermute | solution.py:21
  28.3 3.0 %fusion.19 = (f32[1,1024,256]{2,1,0:T(8,128)}, f32[1,1024,256]{2,1,0:T(8,128)}) fusion(f32[2,1024,256]{2,1,0:T(8,128)} %param.7), kind=kLoop, calls=%fused_computation.72 | loop fusion | bytes 4194304 | tf_op jit(solution)/shard_map/slice | solution.py:74
  32.2 2.2 %collective-permute-start.5 = (f32[1,64,256]{2,1,0:T(8,128)S(1)}, f32[1,64,256]{2,1,0:T(8,128)S(1)}, u32[]{:S(2)}, u32[]{:S(2)}) collective-permute-start(f32[1,64,256]{2,1,0:T(8,128)S(1)} %fusion.16), channel_id=1, source_target_pairs={{0,16},{2,18},{4,20},{6,22},{8,24},{10,26},{12,28},{14,30},{16,0},... | collective-permute-start | bytes 196616 | tf_op jit(solution)/shard_map/ppermute | solution.py:34
  34.4 3.0 %collective-permute-done.5 = f32[1,64,256]{2,1,0:T(8,128)S(1)} collective-permute-done((f32[1,64,256]{2,1,0:T(8,128)S(1)}, f32[1,64,256]{2,1,0:T(8,128)S(1)}, u32[]{:S(2)}, u32[]{:S(2)}) %collective-permute-start.5) | collective-permute-done | bytes 65568 | tf_op jit(solution)/shard_map/ppermute | solution.py:34
  37.5 2.0 %collective-permute-start.6 = (f32[2,64,256]{2,1,0:T(8,128)S(1)}, f32[2,64,256]{2,1,0:T(8,128)S(1)}, u32[]{:S(2)}, u32[]{:S(2)}) collective-permute-start(f32[2,64,256]{2,1,0:T(8,128)S(1)} %maximum_bitcast_fusion.1), channel_id=1, source_target_pairs={{0,8},{2,10},{4,12},{6,14},{8,0},{10,2},{12,4},{14,6},{16,24},{18,... | collective-permute-start | bytes 393224 | tf_op jit(solution)/shard_map/ppermute | solution.py:34
  39.5 3.0 %collective-permute-done.6 = f32[2,64,256]{2,1,0:T(8,128)S(1)} collective-permute-done((f32[2,64,256]{2,1,0:T(8,128)S(1)}, f32[2,64,256]{2,1,0:T(8,128)S(1)}, u32[]{:S(2)}, u32[]{:S(2)}) %collective-permute-start.6) | collective-permute-done | bytes 131104 | tf_op jit(solution)/shard_map/ppermute | solution.py:34
  42.6 1.6 %collective-permute-start.7 = (f32[4,64,256]{2,1,0:T(8,128)S(1)}, f32[4,64,256]{2,1,0:T(8,128)S(1)}, u32[]{:S(2)}, u32[]{:S(2)}) collective-permute-start(f32[4,64,256]{2,1,0:T(8,128)S(1)} %bitcast.154), channel_id=1, source_target_pairs={{0,4},{2,6},{4,0},{6,2},{8,12},{10,14},{12,8},{14,10},{16,20},{18,... | collective-permute-start | bytes 786440 | tf_op jit(solution)/shard_map/ppermute | solution.py:34
  44.2 4.9 %collective-permute-done.7 = f32[4,64,256]{2,1,0:T(8,128)S(1)} collective-permute-done((f32[4,64,256]{2,1,0:T(8,128)S(1)}, f32[4,64,256]{2,1,0:T(8,128)S(1)}, u32[]{:S(2)}, u32[]{:S(2)}) %collective-permute-start.7) | collective-permute-done | bytes 262176 | tf_op jit(solution)/shard_map/ppermute | solution.py:34
  49.3 2.0 %collective-permute-done.8 = f32[8,64,256]{2,1,0:T(8,128)} collective-permute-done((f32[8,64,256]{2,1,0:T(8,128)S(1)}, f32[8,64,256]{2,1,0:T(8,128)}, u32[]{:S(2)}, u32[]{:S(2)}) %collective-permute-start.8) | collective-permute-done | bytes 524320 | tf_op jit(solution)/shard_map/ppermute | solution.py:34
  54.8 1.8 %collective-permute-done.9 = f32[2,2,2,64,256]{4,3,1,0,2:T(8,128)S(1)} collective-permute-done((f32[2,2,2,64,256]{4,3,1,0,2:T(8,128)S(1)}, f32[2,2,2,64,256]{4,3,1,0,2:T(8,128)S(1)}, u32[]{:S(2)}, u32[]{:S(2)}) %collective-permute-start.9) | collective-permute-done | bytes 524320 | tf_op jit(solution)/shard_map/ppermute | solution.py:21
  56.7 1.6 %collective-permute-start.10 = (f32[2,2,64,256]{3,2,1,0:T(8,128)S(1)}, f32[2,2,64,256]{3,2,1,0:T(8,128)S(1)}, u32[]{:S(2)}, u32[]{:S(2)}) collective-permute-start(f32[2,2,64,256]{3,2,1,0:T(8,128)S(1)} %dynamic-slice_bitcast_fusion), channel_id=1, source_target_pairs={{0,4},{2,6},{4,0},{6,2},{8,12},{10,14},{12,8},{14,10},{16,20},{18,... | collective-permute-start | bytes 786440 | tf_op jit(solution)/shard_map/ppermute | solution.py:21
  58.3 6.8 %collective-permute-done.10 = f32[2,2,64,256]{3,2,1,0:T(8,128)S(1)} collective-permute-done((f32[2,2,64,256]{3,2,1,0:T(8,128)S(1)}, f32[2,2,64,256]{3,2,1,0:T(8,128)S(1)}, u32[]{:S(2)}, u32[]{:S(2)}) %collective-permute-start.10) | collective-permute-done | bytes 262176 | tf_op jit(solution)/shard_map/ppermute | solution.py:21
  65.2 2.0 %collective-permute-start.11 = (f32[2,64,256]{2,1,0:T(8,128)S(1)}, f32[2,64,256]{2,1,0:T(8,128)S(1)}, u32[]{:S(2)}, u32[]{:S(2)}) collective-permute-start(f32[2,64,256]{2,1,0:T(8,128)S(1)} %dynamic-slice_bitcast_fusion.2), channel_id=1, source_target_pairs={{0,8},{2,10},{4,12},{6,14},{8,0},{10,2},{12,4},{14,6},{16,24},{18,... | collective-permute-start | bytes 393224 | tf_op jit(solution)/shard_map/ppermute | solution.py:21
  67.2 3.0 %collective-permute-done.11 = f32[2,64,256]{2,1,0:T(8,128)S(1)} collective-permute-done((f32[2,64,256]{2,1,0:T(8,128)S(1)}, f32[2,64,256]{2,1,0:T(8,128)S(1)}, u32[]{:S(2)}, u32[]{:S(2)}) %collective-permute-start.11) | collective-permute-done | bytes 131104 | tf_op jit(solution)/shard_map/ppermute | solution.py:21
  70.3 2.6 %collective-permute-start.12 = (f32[64,256]{1,0:T(8,128)S(1)}, f32[64,256]{1,0:T(8,128)S(1)}, u32[]{:S(2)}, u32[]{:S(2)}) collective-permute-start(f32[64,256]{1,0:T(8,128)S(1)} %dynamic-slice_bitcast_fusion.4), channel_id=1, source_target_pairs={{0,16},{2,18},{4,20},{6,22},{8,24},{10,26},{12,28},{14,30},{16,0},... | collective-permute-start | bytes 196616 | tf_op jit(solution)/shard_map/ppermute | solution.py:21
  72.9 2.6 %collective-permute-done.12 = f32[64,256]{1,0:T(8,128)S(1)} collective-permute-done((f32[64,256]{1,0:T(8,128)S(1)}, f32[64,256]{1,0:T(8,128)S(1)}, u32[]{:S(2)}, u32[]{:S(2)}) %collective-permute-start.12) | collective-permute-done | bytes 65568 | tf_op jit(solution)/shard_map/ppermute | solution.py:21
  76.3 2.6 %collective-permute-start.13 = (f32[1,64,256]{2,1,0:T(8,128)S(1)}, f32[1,64,256]{2,1,0:T(8,128)S(1)}, u32[]{:S(2)}, u32[]{:S(2)}) collective-permute-start(f32[1,64,256]{2,1,0:T(8,128)S(1)} %fusion.14), channel_id=1, source_target_pairs={{0,16},{2,18},{4,20},{6,22},{8,24},{10,26},{12,28},{14,30},{16,0},... | collective-permute-start | bytes 196616 | tf_op jit(solution)/shard_map/ppermute | solution.py:34
  79.0 2.7 %collective-permute-done.13 = f32[1,64,256]{2,1,0:T(8,128)S(1)} collective-permute-done((f32[1,64,256]{2,1,0:T(8,128)S(1)}, f32[1,64,256]{2,1,0:T(8,128)S(1)}, u32[]{:S(2)}, u32[]{:S(2)}) %collective-permute-start.13) | collective-permute-done | bytes 65568 | tf_op jit(solution)/shard_map/ppermute | solution.py:34
  81.7 2.0 %collective-permute-start.14 = (f32[2,64,256]{2,1,0:T(8,128)S(1)}, f32[2,64,256]{2,1,0:T(8,128)S(1)}, u32[]{:S(2)}, u32[]{:S(2)}) collective-permute-start(f32[2,64,256]{2,1,0:T(8,128)S(1)} %maximum_bitcast_fusion.2), channel_id=1, source_target_pairs={{0,8},{2,10},{4,12},{6,14},{8,0},{10,2},{12,4},{14,6},{16,24},{18,... | collective-permute-start | bytes 393224 | tf_op jit(solution)/shard_map/ppermute | solution.py:34
  83.7 3.0 %collective-permute-done.14 = f32[2,64,256]{2,1,0:T(8,128)S(1)} collective-permute-done((f32[2,64,256]{2,1,0:T(8,128)S(1)}, f32[2,64,256]{2,1,0:T(8,128)S(1)}, u32[]{:S(2)}, u32[]{:S(2)}) %collective-permute-start.14) | collective-permute-done | bytes 131104 | tf_op jit(solution)/shard_map/ppermute | solution.py:34
  86.8 1.6 %collective-permute-start.15 = (f32[4,64,256]{2,1,0:T(8,128)S(1)}, f32[4,64,256]{2,1,0:T(8,128)S(1)}, u32[]{:S(2)}, u32[]{:S(2)}) collective-permute-start(f32[4,64,256]{2,1,0:T(8,128)S(1)} %bitcast.155), channel_id=1, source_target_pairs={{0,4},{2,6},{4,0},{6,2},{8,12},{10,14},{12,8},{14,10},{16,20},{18,... | collective-permute-start | bytes 786440 | tf_op jit(solution)/shard_map/ppermute | solution.py:34
  88.4 4.9 %collective-permute-done.15 = f32[4,64,256]{2,1,0:T(8,128)S(1)} collective-permute-done((f32[4,64,256]{2,1,0:T(8,128)S(1)}, f32[4,64,256]{2,1,0:T(8,128)S(1)}, u32[]{:S(2)}, u32[]{:S(2)}) %collective-permute-start.15) | collective-permute-done | bytes 262176 | tf_op jit(solution)/shard_map/ppermute | solution.py:34
  93.5 1.9 %collective-permute-done.16 = f32[8,64,256]{2,1,0:T(8,128)S(1)} collective-permute-done((f32[8,64,256]{2,1,0:T(8,128)S(1)}, f32[8,64,256]{2,1,0:T(8,128)S(1)}, u32[]{:S(2)}, u32[]{:S(2)}) %collective-permute-start.16) | collective-permute-done | bytes 524320 | tf_op jit(solution)/shard_map/ppermute | solution.py:34
  (58 shorter events, 8.0 us)
Async XLA Ops:
  0.0 2.9 %copy-start = (f32[1024,256]{1,0:T(8,128)S(1)}, f32[1024,256]{1,0:T(8,128)}, u32[]{:S(2)}) copy-start(f32[1024,256]{1,0:T(8,128)} %param.6) | copy-start | bytes 3145732
  0.0 9.5 %copy-start.1 = (f32[2,64,512]{2,1,0:T(8,128)S(1)}, f32[2,64,512]{2,1,0:T(8,128)}, u32[]{:S(2)}) copy-start(f32[2,64,512]{2,1,0:T(8,128)} %param.8) | copy-start | bytes 786436
  0.0 9.5 %collective-permute-start = (f32[1,1,2,64,512]{4,3,2,1,0:T(8,128)}, f32[1,1,2,64,512]{4,3,2,1,0:T(8,128)S(1)}, u32[]{:S(2)}, u32[]{:S(2)}) collective-permute-start(f32[1,1,2,64,512]{4,3,2,1,0:T(8,128)} %bitcast.159), channel_id=1, source_target_pairs={{0,1},{1,0},{2,3},{3,2},{4,5},{5,4},{6,7},{7,6},{8,9},{9,8},{10,11... | collective-permute-start | bytes 786440 | tf_op jit(solution)/shard_map/ppermute | solution.py:34
  9.8 2.0 %collective-permute-start.1 = (f32[2,2,2,64,256]{4,3,1,0,2:T(8,128)S(1)}, f32[2,2,2,64,256]{4,3,1,0,2:T(8,128)S(1)}, u32[]{:S(2)}, u32[]{:S(2)}) collective-permute-start(f32[2,2,2,64,256]{4,3,1,0,2:T(8,128)S(1)} %bitcast.157), channel_id=1, source_target_pairs={{0,2},{2,0},{4,6},{6,4},{8,10},{10,8},{12,14},{14,12},{16,18},{18,... | collective-permute-start | bytes 1572872 | tf_op jit(solution)/shard_map/ppermute | solution.py:21
  11.8 8.4 %collective-permute-start.2 = (f32[2,2,64,256]{3,2,1,0:T(8,128)S(1)}, f32[2,2,64,256]{3,2,1,0:T(8,128)S(1)}, u32[]{:S(2)}, u32[]{:S(2)}) collective-permute-start(f32[2,2,64,256]{3,2,1,0:T(8,128)S(1)} %dynamic-slice_bitcast_fusion.1), channel_id=1, source_target_pairs={{0,4},{2,6},{4,0},{6,2},{8,12},{10,14},{12,8},{14,10},{16,20},{18,... | collective-permute-start | bytes 786440 | tf_op jit(solution)/shard_map/ppermute | solution.py:21
  20.3 5.0 %collective-permute-start.3 = (f32[2,64,256]{2,1,0:T(8,128)S(1)}, f32[2,64,256]{2,1,0:T(8,128)S(1)}, u32[]{:S(2)}, u32[]{:S(2)}) collective-permute-start(f32[2,64,256]{2,1,0:T(8,128)S(1)} %dynamic-slice_bitcast_fusion.3), channel_id=1, source_target_pairs={{0,8},{2,10},{4,12},{6,14},{8,0},{10,2},{12,4},{14,6},{16,24},{18,... | collective-permute-start | bytes 393224 | tf_op jit(solution)/shard_map/ppermute | solution.py:21
  25.4 5.9 %collective-permute-start.4 = (f32[64,256]{1,0:T(8,128)S(1)}, f32[64,256]{1,0:T(8,128)S(1)}, u32[]{:S(2)}, u32[]{:S(2)}) collective-permute-start(f32[64,256]{1,0:T(8,128)S(1)} %dynamic-slice_bitcast_fusion.5), channel_id=1, source_target_pairs={{0,16},{2,18},{4,20},{6,22},{8,24},{10,26},{12,28},{14,30},{16,0},... | collective-permute-start | bytes 196616 | tf_op jit(solution)/shard_map/ppermute | solution.py:21
  32.2 5.3 %collective-permute-start.5 = (f32[1,64,256]{2,1,0:T(8,128)S(1)}, f32[1,64,256]{2,1,0:T(8,128)S(1)}, u32[]{:S(2)}, u32[]{:S(2)}) collective-permute-start(f32[1,64,256]{2,1,0:T(8,128)S(1)} %fusion.16), channel_id=1, source_target_pairs={{0,16},{2,18},{4,20},{6,22},{8,24},{10,26},{12,28},{14,30},{16,0},... | collective-permute-start | bytes 196616 | tf_op jit(solution)/shard_map/ppermute | solution.py:34
  37.5 5.0 %collective-permute-start.6 = (f32[2,64,256]{2,1,0:T(8,128)S(1)}, f32[2,64,256]{2,1,0:T(8,128)S(1)}, u32[]{:S(2)}, u32[]{:S(2)}) collective-permute-start(f32[2,64,256]{2,1,0:T(8,128)S(1)} %maximum_bitcast_fusion.1), channel_id=1, source_target_pairs={{0,8},{2,10},{4,12},{6,14},{8,0},{10,2},{12,4},{14,6},{16,24},{18,... | collective-permute-start | bytes 393224 | tf_op jit(solution)/shard_map/ppermute | solution.py:34
  42.6 6.4 %collective-permute-start.7 = (f32[4,64,256]{2,1,0:T(8,128)S(1)}, f32[4,64,256]{2,1,0:T(8,128)S(1)}, u32[]{:S(2)}, u32[]{:S(2)}) collective-permute-start(f32[4,64,256]{2,1,0:T(8,128)S(1)} %bitcast.154), channel_id=1, source_target_pairs={{0,4},{2,6},{4,0},{6,2},{8,12},{10,14},{12,8},{14,10},{16,20},{18,... | collective-permute-start | bytes 786440 | tf_op jit(solution)/shard_map/ppermute | solution.py:34
  49.2 2.1 %collective-permute-start.8 = (f32[8,64,256]{2,1,0:T(8,128)S(1)}, f32[8,64,256]{2,1,0:T(8,128)}, u32[]{:S(2)}, u32[]{:S(2)}) collective-permute-start(f32[8,64,256]{2,1,0:T(8,128)S(1)} %bitcast.152), channel_id=1, source_target_pairs={{0,2},{2,0},{4,6},{6,4},{8,10},{10,8},{12,14},{14,12},{16,18},{18,... | collective-permute-start | bytes 1572872 | tf_op jit(solution)/shard_map/ppermute | solution.py:34
  49.3 4.0 %copy-start.2 = (f32[1024,64]{0,1:T(8,128)S(1)}, f32[1024,64]{0,1:T(8,128)}, u32[]{:S(2)}) copy-start(f32[1024,64]{0,1:T(8,128)} %param.9) | copy-start | bytes 786436
  54.6 2.0 %collective-permute-start.9 = (f32[2,2,2,64,256]{4,3,1,0,2:T(8,128)S(1)}, f32[2,2,2,64,256]{4,3,1,0,2:T(8,128)S(1)}, u32[]{:S(2)}, u32[]{:S(2)}) collective-permute-start(f32[2,2,2,64,256]{4,3,1,0,2:T(8,128)S(1)} %bitcast.158), channel_id=1, source_target_pairs={{0,2},{2,0},{4,6},{6,4},{8,10},{10,8},{12,14},{14,12},{16,18},{18,... | collective-permute-start | bytes 1572872 | tf_op jit(solution)/shard_map/ppermute | solution.py:21
  56.7 8.4 %collective-permute-start.10 = (f32[2,2,64,256]{3,2,1,0:T(8,128)S(1)}, f32[2,2,64,256]{3,2,1,0:T(8,128)S(1)}, u32[]{:S(2)}, u32[]{:S(2)}) collective-permute-start(f32[2,2,64,256]{3,2,1,0:T(8,128)S(1)} %dynamic-slice_bitcast_fusion), channel_id=1, source_target_pairs={{0,4},{2,6},{4,0},{6,2},{8,12},{10,14},{12,8},{14,10},{16,20},{18,... | collective-permute-start | bytes 786440 | tf_op jit(solution)/shard_map/ppermute | solution.py:21
  65.2 5.0 %collective-permute-start.11 = (f32[2,64,256]{2,1,0:T(8,128)S(1)}, f32[2,64,256]{2,1,0:T(8,128)S(1)}, u32[]{:S(2)}, u32[]{:S(2)}) collective-permute-start(f32[2,64,256]{2,1,0:T(8,128)S(1)} %dynamic-slice_bitcast_fusion.2), channel_id=1, source_target_pairs={{0,8},{2,10},{4,12},{6,14},{8,0},{10,2},{12,4},{14,6},{16,24},{18,... | collective-permute-start | bytes 393224 | tf_op jit(solution)/shard_map/ppermute | solution.py:21
  70.3 5.2 %collective-permute-start.12 = (f32[64,256]{1,0:T(8,128)S(1)}, f32[64,256]{1,0:T(8,128)S(1)}, u32[]{:S(2)}, u32[]{:S(2)}) collective-permute-start(f32[64,256]{1,0:T(8,128)S(1)} %dynamic-slice_bitcast_fusion.4), channel_id=1, source_target_pairs={{0,16},{2,18},{4,20},{6,22},{8,24},{10,26},{12,28},{14,30},{16,0},... | collective-permute-start | bytes 196616 | tf_op jit(solution)/shard_map/ppermute | solution.py:21
  76.3 5.3 %collective-permute-start.13 = (f32[1,64,256]{2,1,0:T(8,128)S(1)}, f32[1,64,256]{2,1,0:T(8,128)S(1)}, u32[]{:S(2)}, u32[]{:S(2)}) collective-permute-start(f32[1,64,256]{2,1,0:T(8,128)S(1)} %fusion.14), channel_id=1, source_target_pairs={{0,16},{2,18},{4,20},{6,22},{8,24},{10,26},{12,28},{14,30},{16,0},... | collective-permute-start | bytes 196616 | tf_op jit(solution)/shard_map/ppermute | solution.py:34
  81.7 5.0 %collective-permute-start.14 = (f32[2,64,256]{2,1,0:T(8,128)S(1)}, f32[2,64,256]{2,1,0:T(8,128)S(1)}, u32[]{:S(2)}, u32[]{:S(2)}) collective-permute-start(f32[2,64,256]{2,1,0:T(8,128)S(1)} %maximum_bitcast_fusion.2), channel_id=1, source_target_pairs={{0,8},{2,10},{4,12},{6,14},{8,0},{10,2},{12,4},{14,6},{16,24},{18,... | collective-permute-start | bytes 393224 | tf_op jit(solution)/shard_map/ppermute | solution.py:34
  86.8 6.4 %collective-permute-start.15 = (f32[4,64,256]{2,1,0:T(8,128)S(1)}, f32[4,64,256]{2,1,0:T(8,128)S(1)}, u32[]{:S(2)}, u32[]{:S(2)}) collective-permute-start(f32[4,64,256]{2,1,0:T(8,128)S(1)} %bitcast.155), channel_id=1, source_target_pairs={{0,4},{2,6},{4,0},{6,2},{8,12},{10,14},{12,8},{14,10},{16,20},{18,... | collective-permute-start | bytes 786440 | tf_op jit(solution)/shard_map/ppermute | solution.py:34
  93.4 2.0 %collective-permute-start.16 = (f32[8,64,256]{2,1,0:T(8,128)S(1)}, f32[8,64,256]{2,1,0:T(8,128)S(1)}, u32[]{:S(2)}, u32[]{:S(2)}) collective-permute-start(f32[8,64,256]{2,1,0:T(8,128)S(1)} %bitcast.153), channel_id=1, source_target_pairs={{0,2},{2,0},{4,6},{6,4},{8,10},{10,8},{12,14},{14,12},{16,18},{18,... | collective-permute-start | bytes 1572872 | tf_op jit(solution)/shard_map/ppermute | solution.py:34

commit v4 on v3

--- a/solution.py
+++ b/solution.py
@@ -25,11 +25,11 @@
     return y.reshape((rows,) + x.shape[1:]), riders
 
 
-def doubling_gather(x, axis, n):
+def doubling_gather(x, axis, n, stop=0):
     k = n.bit_length() - 1
     me = lax.axis_index(axis)
     y = x[None]
-    for j in reversed(range(k)):
+    for j in reversed(range(stop, k)):
         mine = (me >> j) & 1
         got = lax.ppermute(y, axis, [(i, i ^ (1 << j)) for i in range(n)])
         low = jnp.where(mine == 0, y, got)
@@ -53,26 +53,43 @@
         return lax.all_gather(x, "blk", axis=0, tiled=True)
 
     def shards(factor_panel, solved_before, right_side, diag_inverse, coupling):
-        if rhs_power_of_two:
-            inverse_pieces = doubling_gather(diag_inverse[None], "rhs", m)
-        else:
-            inverse_pieces = lax.all_gather(diag_inverse, "rhs", axis=0)
         own_count = diag_inverse.shape[1]
         my_index = lax.axis_index("blk")
+        if power_of_two:
+            partner_inverse = lax.ppermute(diag_inverse, "blk", [(i, i ^ 1) for i in range(n)])
+            both_inverse = jnp.stack([diag_inverse, partner_inverse])
+        else:
+            both_inverse = diag_inverse[None]
+        if rhs_power_of_two:
+            inverse_pieces = doubling_gather(both_inverse[None], "rhs", m)
+        else:
+            inverse_pieces = lax.all_gather(both_inverse, "rhs", axis=0)
+
+        def gather_apply(own_rows, mine_inverse, partner_rows_inverse):
+            if not power_of_two:
+                return product(mine_inverse, gather(own_rows))
+            half = doubling_gather(own_rows, "blk", n, stop=1)
+            core = my_index & 1
+
+            def pick(matrix):
+                split = matrix.reshape(matrix.shape[0], n // 2, 2, own_count)
+                return lax.dynamic_index_in_dim(split, core, 2, keepdims=False).reshape(matrix.shape[0], -1)
+
+            theirs = product(pick(partner_rows_inverse), half)
+            return product(pick(mine_inverse), half) + lax.ppermute(theirs, "blk", [(i, i ^ 1) for i in range(n)])
 
         def own_slice(matrix):
             return lax.dynamic_slice_in_dim(matrix, my_index * own_count, own_count, 0)
 
         first_sum = product(factor_panel[0], solved_before)
         first_sum, inverse_pieces = lax.optimization_barrier((first_sum, inverse_pieces))
-        inverse_full = jnp.concatenate(list(inverse_pieces), axis=2)
+        inverse_full = jnp.concatenate(list(inverse_pieces), axis=3)
+        partner_full = inverse_full[-1]
         panel_sum = product(factor_panel[1], solved_before)
         first_part, panel_sum = sum_scatter(first_sum, panel_sum)
-        first_remains = gather(own_slice(right_side[0]) - first_part)
-        first_block = product(inverse_full[0], first_remains)
+        first_block = gather_apply(own_slice(right_side[0]) - first_part, inverse_full[0, 0], partner_full[0])
         second_part, _ = sum_scatter(panel_sum + product(coupling, first_block))
-        second_remains = gather(own_slice(right_side[1]) - second_part)
-        second_block = product(inverse_full[1], second_remains)
+        second_block = gather_apply(own_slice(right_side[1]) - second_part, inverse_full[0, 1], partner_full[1])
         return jnp.stack([first_block, second_block])
 
     return shards

time: 97.3 us -> 110 us (1.13)
  local copies, waits for them, and re-layouts: 3.78 us -> 13.1 us
  other arithmetic: 4.57 us -> 7.01 us
  matrix products: 12.8 us -> 14.1 us
    dynamic_slice x0 -> x3, local copies, waits for them, and re-layouts: none -> 3.83 us  [pick(): lax.dynamic_index_in_dim(split, core, 2, keepdims=False)]
    another operation x1 -> x5, local copies, waits for them, and re-layouts: 0.04 us -> 3.49 us  [the longest x4 3.42 us: pick(): split = matrix.reshape(matrix.shape[0], n // 2, 2, own_count)]
    ppermute x9 -> x7, waiting for transfers between devices: 26.7 us -> 24.3 us  [doubling_gather(): got = lax.ppermute(y, axis, [(i, i ^ 1 << j) for i in range(n)])]
    reshape x0 -> x4, local copies, waits for them, and re-layouts: none -> 1.41 us  [pick(): lax.dynamic_index_in_dim(split, core, 2, keepdims=False)]
    ppermute x0 -> x3, waiting for transfers between devices: none -> 1.38 us  [the longest x1 1.37 us: shards(): lax.ppermute(diag_inverse, 'blk', [(i, i ^ 1) for i in range(n)])]
    dot_general x5 -> x7, matrix products: 12.8 us -> 14.1 us  [product(): jnp.dot(left, right, precision=lax.Precision.HIGHEST, preferred_element_t...]
    ppermute x8, waiting for transfers between devices: 20.7 us -> 21.9 us  [halving_sum_scatter(): got = lax.ppermute(send, axis, [(i, i ^ 1 << j) for i in range(n)])]
    ppermute x9 -> x7, starting transfers between devices: 15.1 us -> 14.1 us  [doubling_gather(): got = lax.ppermute(y, axis, [(i, i ^ 1 << j) for i in range(n)])]
  transfers between devices with their start and end apart: 17 -> 18, of which waited for: 16 -> 14; matrix products, arithmetic and copies ran while one was open for 14% -> 21% of each run, Pallas kernels for 0% -> 0%
where the time goes in v4:
time: 110 us; the launch traced here: 109 us
  waiting for transfers between devices  47.6 us (43%)
  starting transfers between devices  27.2 us (25%)
  matrix products  14.1 us (13%)
  local copies, waits for them, and re-layouts  13.1 us (12%)
  other arithmetic  7.01 us (6%)
    ppermute x7, waiting for transfers between devices, doubling_gather(): got = lax.ppermute(y, axis, [(i, i ^ 1 << j) for i in range(n)])  24.3 us
    ppermute x8, waiting for transfers between devices, halving_sum_scatter(): got = lax.ppermute(send, axis, [(i, i ^ 1 << j) for i in range(n)])  21.9 us
    ppermute x7, starting transfers between devices, doubling_gather(): got = lax.ppermute(y, axis, [(i, i ^ 1 << j) for i in range(n)])  14.1 us
    dot_general x7, matrix products, product(): jnp.dot(left, right, precision=lax.Precision.HIGHEST, preferred_element_t...  14.1 us
    ppermute x8, starting transfers between devices, halving_sum_scatter(): got = lax.ppermute(send, axis, [(i, i ^ 1 << j) for i in range(n)])  12.5 us
    dynamic_slice x3, local copies, waits for them, and re-layouts, pick(): lax.dynamic_index_in_dim(split, core, 2, keepdims=False)  3.83 us
    another operation x4, local copies, waits for them, and re-layouts, pick(): split = matrix.reshape(matrix.shape[0], n // 2, 2, own_count)  3.42 us
    slice x1, local copies, waits for them, and re-layouts, shards(): right_side[1]  3 us
  transfers between devices with their start and end apart: 18, of which 14 were waited for; matrix products, arithmetic and copies ran while one was open for 21% of the time, Pallas kernels for 0%

profile of v4, /device:TPU:0, one launch (start us, length us, event | category | flops | bytes accessed | tf_op | source)
XLA Modules:
  0.0 109.3 jit_solution(3325329313986179687)
XLA Ops:
  0.5 1.4 %collective-permute-done = f32[2,64,512]{2,1,0:T(8,128)S(1)} collective-permute-done((f32[2,64,512]{2,1,0:T(8,128)}, f32[2,64,512]{2,1,0:T(8,128)S(1)}, u32[]{:S(2)}, u32[]{:S(2)}) %collective-permute-start) | collective-permute-done | bytes 262176 | tf_op jit(solution)/shard_map/ppermute | solution.py:59
  2.8 2.9 %collective-permute-start.1 = (f32[1,1,2,2,64,512]{5,4,3,2,1,0:T(8,128)S(1)}, f32[1,1,2,2,64,512]{5,4,3,2,1,0:T(8,128)S(1)}, u32[]{:S(2)}, u32[]{:S(2)}) collective-permute-start(f32[1,1,2,2,64,512]{5,4,3,2,1,0:T(8,128)S(1)} %maximum_bitcast_fusion.1), channel_id=1, source_target_pairs={{0,1},{1,0},{2,3},{3,2},{4,5},{5,4},{6,7},{7,6},{8,9},{9,8},{10,11... | collective-permute-start | bytes 1572872 | tf_op jit(solution)/shard_map/ppermute | solution.py:34
  5.8 5.2 %fusion.2 = f32[1024,256]{1,0:T(8,128)S(1)} fusion(f32[1024,256]{1,0:T(8,128)S(1)} %copy-done, f32[2,1024,1024]{2,1,0:T(8,128)} %param.5), kind=kOutput, calls=%fused_computation.2 | convolution fusion | flops 3221225472 | bytes 6291456 | tf_op jit(solution)/shard_map/dot_general | solution.py:8
  11.0 7.0 %collective-permute-done.1 = f32[1,1,2,2,64,512]{5,4,3,2,1,0:T(8,128)S(1)} collective-permute-done((f32[1,1,2,2,64,512]{5,4,3,2,1,0:T(8,128)S(1)}, f32[1,1,2,2,64,512]{5,4,3,2,1,0:T(8,128)S(1)}, u32[]{:S(2)}, u32[]{:S(2)}) %collective-permute-start.1) | collective-permute-done | bytes 524320 | tf_op jit(solution)/shard_map/ppermute | solution.py:34
  19.2 2.1 %collective-permute-done.2 = f32[2,2,2,64,256]{4,3,1,0,2:T(8,128)S(1)} collective-permute-done((f32[2,2,2,64,256]{4,3,1,0,2:T(8,128)}, f32[2,2,2,64,256]{4,3,1,0,2:T(8,128)S(1)}, u32[]{:S(2)}, u32[]{:S(2)}) %collective-permute-start.2) | collective-permute-done | bytes 524320 | tf_op jit(solution)/shard_map/ppermute | solution.py:21
  21.4 1.8 %collective-permute-start.3 = (f32[2,2,64,256]{3,2,1,0:T(8,128)S(1)}, f32[2,2,64,256]{3,2,1,0:T(8,128)S(1)}, u32[]{:S(2)}, u32[]{:S(2)}) collective-permute-start(f32[2,2,64,256]{3,2,1,0:T(8,128)S(1)} %dynamic-slice_bitcast_fusion.1), channel_id=1, source_target_pairs={{0,4},{2,6},{4,0},{6,2},{8,12},{10,14},{12,8},{14,10},{16,20},{18,... | collective-permute-start | bytes 786440 | tf_op jit(solution)/shard_map/ppermute | solution.py:21
  23.3 5.4 %fusion = f32[1024,256]{1,0:T(8,128)S(1)} fusion(f32[1024,256]{1,0:T(8,128)S(1)} %copy-done, f32[2,1024,1024]{2,1,0:T(8,128)} %param.5), kind=kOutput, calls=%fused_computation | convolution fusion | flops 3221225472 | bytes 6291456 | tf_op jit(solution)/shard_map/dot_general | solution.py:8
  28.7 1.2 %collective-permute-done.3 = f32[2,2,64,256]{3,2,1,0:T(8,128)S(1)} collective-permute-done((f32[2,2,64,256]{3,2,1,0:T(8,128)S(1)}, f32[2,2,64,256]{3,2,1,0:T(8,128)S(1)}, u32[]{:S(2)}, u32[]{:S(2)}) %collective-permute-start.3) | collective-permute-done | bytes 262176 | tf_op jit(solution)/shard_map/ppermute | solution.py:21
  29.9 1.9 %collective-permute-start.4 = (f32[2,64,256]{2,1,0:T(8,128)S(1)}, f32[2,64,256]{2,1,0:T(8,128)}, u32[]{:S(2)}, u32[]{:S(2)}) collective-permute-start(f32[2,64,256]{2,1,0:T(8,128)S(1)} %dynamic-slice_bitcast_fusion.3), channel_id=1, source_target_pairs={{0,8},{2,10},{4,12},{6,14},{8,0},{10,2},{12,4},{14,6},{16,24},{18,... | collective-permute-start | bytes 393224 | tf_op jit(solution)/shard_map/ppermute | solution.py:21
  31.8 3.3 %collective-permute-done.4 = f32[2,64,256]{2,1,0:T(8,128)} collective-permute-done((f32[2,64,256]{2,1,0:T(8,128)S(1)}, f32[2,64,256]{2,1,0:T(8,128)}, u32[]{:S(2)}, u32[]{:S(2)}) %collective-permute-start.4) | collective-permute-done | bytes 131104 | tf_op jit(solution)/shard_map/ppermute | solution.py:21
  36.0 2.9 %collective-permute-start.5 = (f32[64,256]{1,0:T(8,128)S(1)}, f32[64,256]{1,0:T(8,128)S(1)}, u32[]{:S(2)}, u32[]{:S(2)}) collective-permute-start(f32[64,256]{1,0:T(8,128)S(1)} %dynamic-slice_bitcast_fusion.5), channel_id=1, source_target_pairs={{0,16},{2,18},{4,20},{6,22},{8,24},{10,26},{12,28},{14,30},{16,0},... | collective-permute-start | bytes 196616 | tf_op jit(solution)/shard_map/ppermute | solution.py:21
  38.9 3.0 %fusion.14 = (f32[1,1024,256]{2,1,0:T(8,128)}, f32[1,1024,256]{2,1,0:T(8,128)}) fusion(f32[2,1024,256]{2,1,0:T(8,128)} %param.7), kind=kLoop, calls=%fused_computation.73 | loop fusion | bytes 4194304 | tf_op jit(solution)/shard_map/slice | solution.py:92
  42.8 2.3 %collective-permute-start.6 = (f32[1,64,256]{2,1,0:T(8,128)S(1)}, f32[1,64,256]{2,1,0:T(8,128)S(1)}, u32[]{:S(2)}, u32[]{:S(2)}) collective-permute-start(f32[1,64,256]{2,1,0:T(8,128)S(1)} %fusion.13), channel_id=1, source_target_pairs={{0,16},{2,18},{4,20},{6,22},{8,24},{10,26},{12,28},{14,30},{16,0},... | collective-permute-start | bytes 196616 | tf_op jit(solution)/shard_map/ppermute | solution.py:34
  45.0 3.0 %collective-permute-done.6 = f32[1,64,256]{2,1,0:T(8,128)S(1)} collective-permute-done((f32[1,64,256]{2,1,0:T(8,128)S(1)}, f32[1,64,256]{2,1,0:T(8,128)S(1)}, u32[]{:S(2)}, u32[]{:S(2)}) %collective-permute-start.6) | collective-permute-done | bytes 65568 | tf_op jit(solution)/shard_map/ppermute | solution.py:34
  48.1 2.0 %collective-permute-start.7 = (f32[2,64,256]{2,1,0:T(8,128)S(1)}, f32[2,64,256]{2,1,0:T(8,128)S(1)}, u32[]{:S(2)}, u32[]{:S(2)}) collective-permute-start(f32[2,64,256]{2,1,0:T(8,128)S(1)} %maximum_bitcast_fusion.2), channel_id=1, source_target_pairs={{0,8},{2,10},{4,12},{6,14},{8,0},{10,2},{12,4},{14,6},{16,24},{18,... | collective-permute-start | bytes 393224 | tf_op jit(solution)/shard_map/ppermute | solution.py:34
  50.0 3.1 %collective-permute-done.7 = f32[2,64,256]{2,1,0:T(8,128)S(1)} collective-permute-done((f32[2,64,256]{2,1,0:T(8,128)S(1)}, f32[2,64,256]{2,1,0:T(8,128)S(1)}, u32[]{:S(2)}, u32[]{:S(2)}) %collective-permute-start.7) | collective-permute-done | bytes 131104 | tf_op jit(solution)/shard_map/ppermute | solution.py:34
  53.2 1.6 %collective-permute-start.8 = (f32[4,64,256]{2,1,0:T(8,128)S(1)}, f32[4,64,256]{2,1,0:T(8,128)}, u32[]{:S(2)}, u32[]{:S(2)}) collective-permute-start(f32[4,64,256]{2,1,0:T(8,128)S(1)} %bitcast.157), channel_id=1, source_target_pairs={{0,4},{2,6},{4,0},{6,2},{8,12},{10,14},{12,8},{14,10},{16,20},{18,... | collective-permute-start | bytes 786440 | tf_op jit(solution)/shard_map/ppermute | solution.py:34
  56.1 1.3 %reshape_squeeze.15 = f32[64,8,2,64]{3,2,1,0:T(2,128)S(1)} reshape(f32[1,1,64,1024]{3,2,1,0:T(8,128)} %get-tuple-element.18) | data formatting | bytes 524288 | tf_op jit(solution)/shard_map/reshape;squeeze | solution.py:75
  57.5 2.3 %dynamic-slice_reduce_fusion = (f32[64,8,64]{2,1,0:T(8,128)}, f32[64,8,64]{2,1,0:T(8,128)}) fusion(f32[64,8,2,64]{3,2,1,0:T(2,128)S(1)} %reshape_squeeze.15, s32[]{:T(128)S(6)} %select_n.122, f32[64,8,2,64]{3,2,1,0:T(2,128)S(1)} %reshape_squeeze.13), kind=kLoop, calls=%fused_computation.36 | loop fusion | bytes 524292 | tf_op jit(solution)/shard_map/jit(dynamic_index_in_dim)/dynamic_slice | solution.py:76
  62.4 1.3 %reshape_squeeze.12 = f32[64,8,2,64]{3,2,1,0:T(2,128)S(1)} reshape(f32[1,1,64,1024]{3,2,1,0:T(8,128)} %get-tuple-element.16) | data formatting | bytes 524288 | tf_op jit(solution)/shard_map/reshape;squeeze | solution.py:75
  65.0 2.0 %convolution_bitcast_fusion = f32[1024,256]{1,0:T(8,128)S(1)} fusion(f32[64,256]{1,0:T(8,128)S(1)} %convolution_add_fusion.1, f32[1024,64]{0,1:T(8,128)} %param.9), kind=kOutput, calls=%fused_computation.12 | convolution fusion | flops 201326592 | bytes 1376256 | tf_op jit(solution)/shard_map/dot_general | solution.py:8
  67.8 1.5 %collective-permute-done.10 = f32[2,2,2,64,256]{4,3,1,0,2:T(8,128)S(1)} collective-permute-done((f32[2,2,2,64,256]{4,3,1,0,2:T(8,128)S(1)}, f32[2,2,2,64,256]{4,3,1,0,2:T(8,128)S(1)}, u32[]{:S(2)}, u32[]{:S(2)}) %collective-permute-start.10) | collective-permute-done | bytes 524320 | tf_op jit(solution)/shard_map/ppermute | solution.py:21
  70.1 8.1 %collective-permute-done.11 = f32[2,2,64,256]{3,2,1,0:T(8,128)S(1)} collective-permute-done((f32[2,2,64,256]{3,2,1,0:T(8,128)S(1)}, f32[2,2,64,256]{3,2,1,0:T(8,128)S(1)}, u32[]{:S(2)}, u32[]{:S(2)}) %collective-permute-start.11) | collective-permute-done | bytes 262176 | tf_op jit(solution)/shard_map/ppermute | solution.py:21
  78.2 2.0 %collective-permute-start.12 = (f32[2,64,256]{2,1,0:T(8,128)S(1)}, f32[2,64,256]{2,1,0:T(8,128)S(1)}, u32[]{:S(2)}, u32[]{:S(2)}) collective-permute-start(f32[2,64,256]{2,1,0:T(8,128)S(1)} %dynamic-slice_bitcast_fusion.2), channel_id=1, source_target_pairs={{0,8},{2,10},{4,12},{6,14},{8,0},{10,2},{12,4},{14,6},{16,24},{18,... | collective-permute-start | bytes 393224 | tf_op jit(solution)/shard_map/ppermute | solution.py:21
  80.2 3.2 %collective-permute-done.12 = f32[2,64,256]{2,1,0:T(8,128)S(1)} collective-permute-done((f32[2,64,256]{2,1,0:T(8,128)S(1)}, f32[2,64,256]{2,1,0:T(8,128)S(1)}, u32[]{:S(2)}, u32[]{:S(2)}) %collective-permute-start.12) | collective-permute-done | bytes 131104 | tf_op jit(solution)/shard_map/ppermute | solution.py:21
  83.4 2.8 %collective-permute-start.13 = (f32[64,256]{1,0:T(8,128)S(1)}, f32[64,256]{1,0:T(8,128)S(1)}, u32[]{:S(2)}, u32[]{:S(2)}) collective-permute-start(f32[64,256]{1,0:T(8,128)S(1)} %dynamic-slice_bitcast_fusion.4), channel_id=1, source_target_pairs={{0,16},{2,18},{4,20},{6,22},{8,24},{10,26},{12,28},{14,30},{16,0},... | collective-permute-start | bytes 196616 | tf_op jit(solution)/shard_map/ppermute | solution.py:21
  86.2 2.5 %collective-permute-done.13 = f32[64,256]{1,0:T(8,128)S(1)} collective-permute-done((f32[64,256]{1,0:T(8,128)S(1)}, f32[64,256]{1,0:T(8,128)S(1)}, u32[]{:S(2)}, u32[]{:S(2)}) %collective-permute-start.13) | collective-permute-done | bytes 65568 | tf_op jit(solution)/shard_map/ppermute | solution.py:21
  89.5 2.8 %collective-permute-start.14 = (f32[1,64,256]{2,1,0:T(8,128)S(1)}, f32[1,64,256]{2,1,0:T(8,128)S(1)}, u32[]{:S(2)}, u32[]{:S(2)}) collective-permute-start(f32[1,64,256]{2,1,0:T(8,128)S(1)} %fusion.11), channel_id=1, source_target_pairs={{0,16},{2,18},{4,20},{6,22},{8,24},{10,26},{12,28},{14,30},{16,0},... | collective-permute-start | bytes 196616 | tf_op jit(solution)/shard_map/ppermute | solution.py:34
  92.3 2.5 %collective-permute-done.14 = f32[1,64,256]{2,1,0:T(8,128)S(1)} collective-permute-done((f32[1,64,256]{2,1,0:T(8,128)S(1)}, f32[1,64,256]{2,1,0:T(8,128)S(1)}, u32[]{:S(2)}, u32[]{:S(2)}) %collective-permute-start.14) | collective-permute-done | bytes 65568 | tf_op jit(solution)/shard_map/ppermute | solution.py:34
  94.8 2.0 %collective-permute-start.15 = (f32[2,64,256]{2,1,0:T(8,128)S(1)}, f32[2,64,256]{2,1,0:T(8,128)S(1)}, u32[]{:S(2)}, u32[]{:S(2)}) collective-permute-start(f32[2,64,256]{2,1,0:T(8,128)S(1)} %maximum_bitcast_fusion.3), channel_id=1, source_target_pairs={{0,8},{2,10},{4,12},{6,14},{8,0},{10,2},{12,4},{14,6},{16,24},{18,... | collective-permute-start | bytes 393224 | tf_op jit(solution)/shard_map/ppermute | solution.py:34
  96.8 3.1 %collective-permute-done.15 = f32[2,64,256]{2,1,0:T(8,128)S(1)} collective-permute-done((f32[2,64,256]{2,1,0:T(8,128)S(1)}, f32[2,64,256]{2,1,0:T(8,128)S(1)}, u32[]{:S(2)}, u32[]{:S(2)}) %collective-permute-start.15) | collective-permute-done | bytes 131104 | tf_op jit(solution)/shard_map/ppermute | solution.py:34
  100.6 5.7 %collective-permute-done.16 = f32[4,64,256]{2,1,0:T(8,128)S(1)} collective-permute-done((f32[4,64,256]{2,1,0:T(8,128)S(1)}, f32[4,64,256]{2,1,0:T(8,128)S(1)}, u32[]{:S(2)}, u32[]{:S(2)}) %collective-permute-start.16) | collective-permute-done | bytes 262176 | tf_op jit(solution)/shard_map/ppermute | solution.py:34
  (71 shorter events, 16.0 us)
Async XLA Ops:
  0.0 5.8 %copy-start = (f32[1024,256]{1,0:T(8,128)S(1)}, f32[1024,256]{1,0:T(8,128)}, u32[]{:S(2)}) copy-start(f32[1024,256]{1,0:T(8,128)} %param.6) | copy-start | bytes 3145732
  0.0 18.0 %copy-start.1 = (f32[2,64,512]{2,1,0:T(8,128)S(1)}, f32[2,64,512]{2,1,0:T(8,128)}, u32[]{:S(2)}) copy-start(f32[2,64,512]{2,1,0:T(8,128)} %param.8) | copy-start | bytes 786436
  0.0 1.8 %collective-permute-start = (f32[2,64,512]{2,1,0:T(8,128)}, f32[2,64,512]{2,1,0:T(8,128)S(1)}, u32[]{:S(2)}, u32[]{:S(2)}) collective-permute-start(f32[2,64,512]{2,1,0:T(8,128)} %param.8), channel_id=1, source_target_pairs={{0,2},{2,0},{4,6},{6,4},{8,10},{10,8},{12,14},{14,12},{16,18},{18,... | collective-permute-start | bytes 786440 | tf_op jit(solution)/shard_map/ppermute | solution.py:59
  2.8 15.2 %collective-permute-start.1 = (f32[1,1,2,2,64,512]{5,4,3,2,1,0:T(8,128)S(1)}, f32[1,1,2,2,64,512]{5,4,3,2,1,0:T(8,128)S(1)}, u32[]{:S(2)}, u32[]{:S(2)}) collective-permute-start(f32[1,1,2,2,64,512]{5,4,3,2,1,0:T(8,128)S(1)} %maximum_bitcast_fusion.1), channel_id=1, source_target_pairs={{0,1},{1,0},{2,3},{3,2},{4,5},{5,4},{6,7},{7,6},{8,9},{9,8},{10,11... | collective-permute-start | bytes 1572872 | tf_op jit(solution)/shard_map/ppermute | solution.py:34
  19.2 2.1 %collective-permute-start.2 = (f32[2,2,2,64,256]{4,3,1,0,2:T(8,128)}, f32[2,2,2,64,256]{4,3,1,0,2:T(8,128)S(1)}, u32[]{:S(2)}, u32[]{:S(2)}) collective-permute-start(f32[2,2,2,64,256]{4,3,1,0,2:T(8,128)} %bitcast.146), channel_id=1, source_target_pairs={{0,2},{2,0},{4,6},{6,4},{8,10},{10,8},{12,14},{14,12},{16,18},{18,... | collective-permute-start | bytes 1572872 | tf_op jit(solution)/shard_map/ppermute | solution.py:21
  21.4 8.4 %collective-permute-start.3 = (f32[2,2,64,256]{3,2,1,0:T(8,128)S(1)}, f32[2,2,64,256]{3,2,1,0:T(8,128)S(1)}, u32[]{:S(2)}, u32[]{:S(2)}) collective-permute-start(f32[2,2,64,256]{3,2,1,0:T(8,128)S(1)} %dynamic-slice_bitcast_fusion.1), channel_id=1, source_target_pairs={{0,4},{2,6},{4,0},{6,2},{8,12},{10,14},{12,8},{14,10},{16,20},{18,... | collective-permute-start | bytes 786440 | tf_op jit(solution)/shard_map/ppermute | solution.py:21
  29.9 5.1 %collective-permute-start.4 = (f32[2,64,256]{2,1,0:T(8,128)S(1)}, f32[2,64,256]{2,1,0:T(8,128)}, u32[]{:S(2)}, u32[]{:S(2)}) collective-permute-start(f32[2,64,256]{2,1,0:T(8,128)S(1)} %dynamic-slice_bitcast_fusion.3), channel_id=1, source_target_pairs={{0,8},{2,10},{4,12},{6,14},{8,0},{10,2},{12,4},{14,6},{16,24},{18,... | collective-permute-start | bytes 393224 | tf_op jit(solution)/shard_map/ppermute | solution.py:21
  36.0 5.9 %collective-permute-start.5 = (f32[64,256]{1,0:T(8,128)S(1)}, f32[64,256]{1,0:T(8,128)S(1)}, u32[]{:S(2)}, u32[]{:S(2)}) collective-permute-start(f32[64,256]{1,0:T(8,128)S(1)} %dynamic-slice_bitcast_fusion.5), channel_id=1, source_target_pairs={{0,16},{2,18},{4,20},{6,22},{8,24},{10,26},{12,28},{14,30},{16,0},... | collective-permute-start | bytes 196616 | tf_op jit(solution)/shard_map/ppermute | solution.py:21
  42.8 5.3 %collective-permute-start.6 = (f32[1,64,256]{2,1,0:T(8,128)S(1)}, f32[1,64,256]{2,1,0:T(8,128)S(1)}, u32[]{:S(2)}, u32[]{:S(2)}) collective-permute-start(f32[1,64,256]{2,1,0:T(8,128)S(1)} %fusion.13), channel_id=1, source_target_pairs={{0,16},{2,18},{4,20},{6,22},{8,24},{10,26},{12,28},{14,30},{16,0},... | collective-permute-start | bytes 196616 | tf_op jit(solution)/shard_map/ppermute | solution.py:34
  48.1 5.0 %collective-permute-start.7 = (f32[2,64,256]{2,1,0:T(8,128)S(1)}, f32[2,64,256]{2,1,0:T(8,128)S(1)}, u32[]{:S(2)}, u32[]{:S(2)}) collective-permute-start(f32[2,64,256]{2,1,0:T(8,128)S(1)} %maximum_bitcast_fusion.2), channel_id=1, source_target_pairs={{0,8},{2,10},{4,12},{6,14},{8,0},{10,2},{12,4},{14,6},{16,24},{18,... | collective-permute-start | bytes 393224 | tf_op jit(solution)/shard_map/ppermute | solution.py:34
  53.2 7.6 %collective-permute-start.8 = (f32[4,64,256]{2,1,0:T(8,128)S(1)}, f32[4,64,256]{2,1,0:T(8,128)}, u32[]{:S(2)}, u32[]{:S(2)}) collective-permute-start(f32[4,64,256]{2,1,0:T(8,128)S(1)} %bitcast.157), channel_id=1, source_target_pairs={{0,4},{2,6},{4,0},{6,2},{8,12},{10,14},{12,8},{14,10},{16,20},{18,... | collective-permute-start | bytes 786440 | tf_op jit(solution)/shard_map/ppermute | solution.py:34
  62.3 2.3 %collective-permute-start.9 = (f32[64,256]{1,0:T(8,128)S(1)}, f32[64,256]{1,0:T(8,128)S(1)}, u32[]{:S(2)}, u32[]{:S(2)}) collective-permute-start(f32[64,256]{1,0:T(8,128)S(1)} %fusion.15), channel_id=1, source_target_pairs={{0,2},{2,0},{4,6},{6,4},{8,10},{10,8},{12,14},{14,12},{16,18},{18,... | collective-permute-start | bytes 196616 | tf_op jit(solution)/shard_map/ppermute | solution.py:79
  67.1 33.4 %copy-start.2 = (f32[64,8,64]{2,1,0:T(8,128)S(1)}, f32[64,8,64]{2,1,0:T(8,128)}, u32[]{:S(2)}) copy-start(f32[64,8,64]{2,1,0:T(8,128)} %get-tuple-element.39) | copy-start | bytes 393220
  67.3 2.1 %collective-permute-start.10 = (f32[2,2,2,64,256]{4,3,1,0,2:T(8,128)S(1)}, f32[2,2,2,64,256]{4,3,1,0,2:T(8,128)S(1)}, u32[]{:S(2)}, u32[]{:S(2)}) collective-permute-start(f32[2,2,2,64,256]{4,3,1,0,2:T(8,128)S(1)} %bitcast.160), channel_id=1, source_target_pairs={{0,2},{2,0},{4,6},{6,4},{8,10},{10,8},{12,14},{14,12},{16,18},{18,... | collective-permute-start | bytes 1572872 | tf_op jit(solution)/shard_map/ppermute | solution.py:21
  69.5 37.5 %copy-start.3 = (f32[1,1,64,1024]{3,2,1,0:T(8,128)S(1)}, f32[1,1,64,1024]{3,2,1,0:T(8,128)}, u32[]{:S(2)}) copy-start(f32[1,1,64,1024]{3,2,1,0:T(8,128)} %get-tuple-element.15) | copy-start | bytes 786436
  69.5 8.7 %collective-permute-start.11 = (f32[2,2,64,256]{3,2,1,0:T(8,128)S(1)}, f32[2,2,64,256]{3,2,1,0:T(8,128)S(1)}, u32[]{:S(2)}, u32[]{:S(2)}) collective-permute-start(f32[2,2,64,256]{3,2,1,0:T(8,128)S(1)} %dynamic-slice_bitcast_fusion), channel_id=1, source_target_pairs={{0,4},{2,6},{4,0},{6,2},{8,12},{10,14},{12,8},{14,10},{16,20},{18,... | collective-permute-start | bytes 786440 | tf_op jit(solution)/shard_map/ppermute | solution.py:21
  78.2 5.2 %collective-permute-start.12 = (f32[2,64,256]{2,1,0:T(8,128)S(1)}, f32[2,64,256]{2,1,0:T(8,128)S(1)}, u32[]{:S(2)}, u32[]{:S(2)}) collective-permute-start(f32[2,64,256]{2,1,0:T(8,128)S(1)} %dynamic-slice_bitcast_fusion.2), channel_id=1, source_target_pairs={{0,8},{2,10},{4,12},{6,14},{8,0},{10,2},{12,4},{14,6},{16,24},{18,... | collective-permute-start | bytes 393224 | tf_op jit(solution)/shard_map/ppermute | solution.py:21
  83.4 5.2 %collective-permute-start.13 = (f32[64,256]{1,0:T(8,128)S(1)}, f32[64,256]{1,0:T(8,128)S(1)}, u32[]{:S(2)}, u32[]{:S(2)}) collective-permute-start(f32[64,256]{1,0:T(8,128)S(1)} %dynamic-slice_bitcast_fusion.4), channel_id=1, source_target_pairs={{0,16},{2,18},{4,20},{6,22},{8,24},{10,26},{12,28},{14,30},{16,0},... | collective-permute-start | bytes 196616 | tf_op jit(solution)/shard_map/ppermute | solution.py:21
  89.5 5.3 %collective-permute-start.14 = (f32[1,64,256]{2,1,0:T(8,128)S(1)}, f32[1,64,256]{2,1,0:T(8,128)S(1)}, u32[]{:S(2)}, u32[]{:S(2)}) collective-permute-start(f32[1,64,256]{2,1,0:T(8,128)S(1)} %fusion.11), channel_id=1, source_target_pairs={{0,16},{2,18},{4,20},{6,22},{8,24},{10,26},{12,28},{14,30},{16,0},... | collective-permute-start | bytes 196616 | tf_op jit(solution)/shard_map/ppermute | solution.py:34
  94.8 5.0 %collective-permute-start.15 = (f32[2,64,256]{2,1,0:T(8,128)S(1)}, f32[2,64,256]{2,1,0:T(8,128)S(1)}, u32[]{:S(2)}, u32[]{:S(2)}) collective-permute-start(f32[2,64,256]{2,1,0:T(8,128)S(1)} %maximum_bitcast_fusion.3), channel_id=1, source_target_pairs={{0,8},{2,10},{4,12},{6,14},{8,0},{10,2},{12,4},{14,6},{16,24},{18,... | collective-permute-start | bytes 393224 | tf_op jit(solution)/shard_map/ppermute | solution.py:34
  99.9 6.4 %collective-permute-start.16 = (f32[4,64,256]{2,1,0:T(8,128)S(1)}, f32[4,64,256]{2,1,0:T(8,128)S(1)}, u32[]{:S(2)}, u32[]{:S(2)}) collective-permute-start(f32[4,64,256]{2,1,0:T(8,128)S(1)} %bitcast.158), channel_id=1, source_target_pairs={{0,4},{2,6},{4,0},{6,2},{8,12},{10,14},{12,8},{14,10},{16,20},{18,... | collective-permute-start | bytes 786440 | tf_op jit(solution)/shard_map/ppermute | solution.py:34
  106.9 1.4 %collective-permute-start.17 = (f32[64,256]{1,0:T(8,128)S(1)}, f32[64,256]{1,0:T(8,128)S(1)}, u32[]{:S(2)}, u32[]{:S(2)}) collective-permute-start(f32[64,256]{1,0:T(8,128)S(1)} %fusion.16), channel_id=1, source_target_pairs={{0,2},{2,0},{4,6},{6,4},{8,10},{10,8},{12,14},{14,12},{16,18},{18,... | collective-permute-start | bytes 196616 | tf_op jit(solution)/shard_map/ppermute | solution.py:79

commit v5 on v3

--- a/solution.py
+++ b/solution.py
@@ -38,6 +38,34 @@
     return y.reshape((-1,) + x.shape[1:])
 
 
+def reduce_then_gather(x, right, axis, n, riders=None):
+    k = n.bit_length() - 1
+    me = lax.axis_index(axis)
+    rows = x.shape[0] // n
+    y = x.reshape((2,) * k + (rows,) + x.shape[1:])
+    r = right.reshape(y.shape)
+    for j in range(k - 1):
+        bit_axis = k - 1 - j
+        mine = (me >> j) & 1
+        keep = lax.dynamic_index_in_dim(y, mine, bit_axis, keepdims=False)
+        send = lax.dynamic_index_in_dim(y, 1 - mine, bit_axis, keepdims=False)
+        r = lax.dynamic_index_in_dim(r, mine, bit_axis, keepdims=False)
+        got = lax.ppermute(send, axis, [(i, i ^ (1 << j)) for i in range(n)])
+        if j == 1 and riders is not None:
+            got, riders = lax.optimization_barrier((got, riders))
+        y = keep + got
+    top = k - 1
+    y = y + lax.ppermute(y, axis, [(i, i ^ (1 << top)) for i in range(n)])
+    y = r - y
+    for j in reversed(range(k - 1)):
+        mine = (me >> j) & 1
+        got = lax.ppermute(y, axis, [(i, i ^ (1 << j)) for i in range(n)])
+        low = jnp.where(mine == 0, y, got)
+        high = jnp.where(mine == 0, got, y)
+        y = jnp.stack([low, high], k - 1 - j)
+    return y.reshape(x.shape), riders
+
+
 def make_shards(n, m):
     power_of_two = n > 1 and (n & (n - 1)) == 0
     rhs_power_of_two = m > 1 and (m & (m - 1)) == 0
@@ -67,11 +95,18 @@
         first_sum, inverse_pieces = lax.optimization_barrier((first_sum, inverse_pieces))
         inverse_full = jnp.concatenate(list(inverse_pieces), axis=2)
         panel_sum = product(factor_panel[1], solved_before)
-        first_part, panel_sum = sum_scatter(first_sum, panel_sum)
-        first_remains = gather(own_slice(right_side[0]) - first_part)
+        if power_of_two and n >= 4:
+            first_remains, panel_sum = reduce_then_gather(first_sum, right_side[0], "blk", n, panel_sum)
+        else:
+            first_part, panel_sum = sum_scatter(first_sum, panel_sum)
+            first_remains = gather(own_slice(right_side[0]) - first_part)
         first_block = product(inverse_full[0], first_remains)
-        second_part, _ = sum_scatter(panel_sum + product(coupling, first_block))
-        second_remains = gather(own_slice(right_side[1]) - second_part)
+        second_sum = panel_sum + product(coupling, first_block)
+        if power_of_two and n >= 4:
+            second_remains, _ = reduce_then_gather(second_sum, right_side[1], "blk", n)
+        else:
+            second_part, _ = sum_scatter(second_sum)
+            second_remains = gather(own_slice(right_side[1]) - second_part)
         second_block = product(inverse_full[1], second_remains)
         return jnp.stack([first_block, second_block])
 

time: 97.3 us -> 92.1 us (0.947)
  starting transfers between devices: 28.1 us -> 19 us
  waiting for transfers between devices: 47.4 us -> 49.9 us
  other arithmetic: 4.57 us -> 6.4 us
    ppermute x8 -> x14, waiting for transfers between devices: 20.7 us -> 48.5 us  [the longest x6 22.6 us: reduce_then_gather(): got = lax.ppermute(y, axis, [(i, i ^ 1 << j) for i in range(n)])]
    ppermute x9 -> x1, waiting for transfers between devices: 26.7 us -> 1.31 us  [doubling_gather(): got = lax.ppermute(y, axis, [(i, i ^ 1 << j) for i in range(n)])]
    ppermute x9 -> x1, starting transfers between devices: 15.1 us -> 2.94 us  [doubling_gather(): got = lax.ppermute(y, axis, [(i, i ^ 1 << j) for i in range(n)])]
    another operation x0 -> x12, other arithmetic: none -> 3.4 us  [reduce_then_gather(): y = jnp.stack([low, high], k - 1 - j)]
    ppermute x8 -> x14, starting transfers between devices: 13 us -> 16.1 us  [the longest x6 6.38 us: reduce_then_gather(): got = lax.ppermute(send, axis, [(i, i ^ 1 << j) for i in range(n)])]
    sub x0 -> x2, other arithmetic: none -> 1.86 us  [reduce_then_gather(): y = r - y]
    another operation x15 -> x1, other arithmetic: 1.75 us -> 0.04 us  [doubling_gather(): y = jnp.stack([low, high], 1).reshape((-1,) + x.shape)]
    broadcast_in_dim x2 -> x0, other arithmetic: 1.71 us -> none  [doubling_gather(): y = x[None]]
  transfers between devices with their start and end apart: 17 -> 15, of which waited for: 16 -> 15; matrix products, arithmetic and copies ran while one was open for 14% -> 15% of each run, Pallas kernels for 0% -> 0%
where the time goes in v5:
time: 92.1 us; the launch traced here: 91.9 us
  waiting for transfers between devices  49.9 us (54%)
  starting transfers between devices  19 us (21%)
  matrix products  12.8 us (14%)
  other arithmetic  6.4 us (7%)
  local copies, waits for them, and re-layouts  3.54 us (4%)
    ppermute x6, waiting for transfers between devices, reduce_then_gather(): got = lax.ppermute(y, axis, [(i, i ^ 1 << j) for i in range(n)])  22.6 us
    ppermute x6, waiting for transfers between devices, reduce_then_gather(): got = lax.ppermute(send, axis, [(i, i ^ 1 << j) for i in range(n)])  19.2 us
    dot_general x5, matrix products, product(): jnp.dot(left, right, precision=lax.Precision.HIGHEST, preferred_element_t...  12.8 us
    ppermute x2, waiting for transfers between devices, reduce_then_gather(): y = y + lax.ppermute(y, axis, [(i, i ^ 1 << top) for i in range(n)])  6.77 us
    ppermute x6, starting transfers between devices, reduce_then_gather(): got = lax.ppermute(send, axis, [(i, i ^ 1 << j) for i in range(n)])  6.38 us
    ppermute x2, starting transfers between devices, reduce_then_gather(): y = y + lax.ppermute(y, axis, [(i, i ^ 1 << top) for i in range(n)])  5.05 us
    ppermute x6, starting transfers between devices, reduce_then_gather(): got = lax.ppermute(y, axis, [(i, i ^ 1 << j) for i in range(n)])  4.66 us
    another operation x12, other arithmetic, reduce_then_gather(): y = jnp.stack([low, high], k - 1 - j)  3.4 us
  transfers between devices with their start and end apart: 15, of which 15 were waited for; matrix products, arithmetic and copies ran while one was open for 15% of the time, Pallas kernels for 0%

profile of v5, /device:TPU:0, one launch (start us, length us, event | category | flops | bytes accessed | tf_op | source)
XLA Modules:
  0.0 91.9 jit_solution(13655324299941995160)
XLA Ops:
  0.0 2.9 %collective-permute-start = (f32[1,1,2,64,512]{4,3,2,1,0:T(8,128)}, f32[1,1,2,64,512]{4,3,2,1,0:T(8,128)S(1)}, u32[]{:S(2)}, u32[]{:S(2)}) collective-permute-start(f32[1,1,2,64,512]{4,3,2,1,0:T(8,128)} %bitcast.123), channel_id=1, source_target_pairs={{0,1},{1,0},{2,3},{3,2},{4,5},{5,4},{6,7},{7,6},{8,9},{9,8},{10,11... | collective-permute-start | bytes 786440 | tf_op jit(solution)/shard_map/ppermute | solution.py:34
  2.9 5.2 %fusion.2 = f32[1024,256]{1,0:T(8,128)S(1)} fusion(f32[1024,256]{1,0:T(8,128)S(1)} %copy-done, f32[2,1024,1024]{2,1,0:T(8,128)} %param.5), kind=kOutput, calls=%fused_computation.2 | convolution fusion | flops 3221225472 | bytes 6291456 | tf_op jit(solution)/shard_map/dot_general | solution.py:8
  8.2 1.3 %collective-permute-done = f32[1,1,2,64,512]{4,3,2,1,0:T(8,128)S(1)} collective-permute-done((f32[1,1,2,64,512]{4,3,2,1,0:T(8,128)}, f32[1,1,2,64,512]{4,3,2,1,0:T(8,128)S(1)}, u32[]{:S(2)}, u32[]{:S(2)}) %collective-permute-start) | collective-permute-done | bytes 262176 | tf_op jit(solution)/shard_map/ppermute | solution.py:34
  9.8 1.9 %collective-permute-done.1 = f32[2,2,2,64,256]{4,3,1,0,2:T(8,128)S(1)} collective-permute-done((f32[2,2,2,64,256]{4,3,1,0,2:T(8,128)S(1)}, f32[2,2,2,64,256]{4,3,1,0,2:T(8,128)S(1)}, u32[]{:S(2)}, u32[]{:S(2)}) %collective-permute-start.1) | collective-permute-done | bytes 524320 | tf_op jit(solution)/shard_map/ppermute | solution.py:53
  11.8 1.8 %collective-permute-start.2 = (f32[2,2,64,256]{3,2,1,0:T(8,128)S(1)}, f32[2,2,64,256]{3,2,1,0:T(8,128)S(1)}, u32[]{:S(2)}, u32[]{:S(2)}) collective-permute-start(f32[2,2,64,256]{3,2,1,0:T(8,128)S(1)} %dynamic-slice_bitcast_fusion.1), channel_id=1, source_target_pairs={{0,4},{2,6},{4,0},{6,2},{8,12},{10,14},{12,8},{14,10},{16,20},{18,... | collective-permute-start | bytes 786440 | tf_op jit(solution)/shard_map/ppermute | solution.py:53
  13.7 5.2 %fusion = f32[1024,256]{1,0:T(8,128)S(1)} fusion(f32[1024,256]{1,0:T(8,128)S(1)} %copy-done, f32[2,1024,1024]{2,1,0:T(8,128)} %param.5), kind=kOutput, calls=%fused_computation | convolution fusion | flops 3221225472 | bytes 6291456 | tf_op jit(solution)/shard_map/dot_general | solution.py:8
  18.9 1.4 %collective-permute-done.2 = f32[2,2,64,256]{3,2,1,0:T(8,128)S(1)} collective-permute-done((f32[2,2,64,256]{3,2,1,0:T(8,128)S(1)}, f32[2,2,64,256]{3,2,1,0:T(8,128)S(1)}, u32[]{:S(2)}, u32[]{:S(2)}) %collective-permute-start.2) | collective-permute-done | bytes 262176 | tf_op jit(solution)/shard_map/ppermute | solution.py:53
  20.3 1.9 %collective-permute-start.3 = (f32[2,64,256]{2,1,0:T(8,128)S(1)}, f32[2,64,256]{2,1,0:T(8,128)S(1)}, u32[]{:S(2)}, u32[]{:S(2)}) collective-permute-start(f32[2,64,256]{2,1,0:T(8,128)S(1)} %dynamic-slice_bitcast_fusion.3), channel_id=1, source_target_pairs={{0,8},{2,10},{4,12},{6,14},{8,0},{10,2},{12,4},{14,6},{16,24},{18,... | collective-permute-start | bytes 393224 | tf_op jit(solution)/shard_map/ppermute | solution.py:53
  22.2 3.2 %collective-permute-done.3 = f32[2,64,256]{2,1,0:T(8,128)S(1)} collective-permute-done((f32[2,64,256]{2,1,0:T(8,128)S(1)}, f32[2,64,256]{2,1,0:T(8,128)S(1)}, u32[]{:S(2)}, u32[]{:S(2)}) %collective-permute-start.3) | collective-permute-done | bytes 131104 | tf_op jit(solution)/shard_map/ppermute | solution.py:53
  25.4 2.9 %collective-permute-start.4 = (f32[2,64,256]{2,1,0:T(8,128)S(1)}, f32[2,64,256]{2,1,0:T(8,128)S(1)}, u32[]{:S(2)}, u32[]{:S(2)}) collective-permute-start(f32[2,64,256]{2,1,0:T(8,128)S(1)} %bitcast_add_fusion.5), channel_id=1, source_target_pairs={{0,16},{2,18},{4,20},{6,22},{8,24},{10,26},{12,28},{14,30},{16,0},... | collective-permute-start | bytes 393224 | tf_op jit(solution)/shard_map/ppermute | solution.py:58
  28.3 3.0 %fusion.15 = (f32[1,1024,256]{2,1,0:T(8,128)}, f32[1,1024,256]{2,1,0:T(8,128)}) fusion(f32[2,1024,256]{2,1,0:T(8,128)} %param.7), kind=kLoop, calls=%fused_computation.60 | loop fusion | bytes 4194304 | tf_op jit(solution)/shard_map/slice | solution.py:106
  31.3 1.6 %collective-permute-done.4 = f32[2,64,256]{2,1,0:T(8,128)S(1)} collective-permute-done((f32[2,64,256]{2,1,0:T(8,128)S(1)}, f32[2,64,256]{2,1,0:T(8,128)S(1)}, u32[]{:S(2)}, u32[]{:S(2)}) %collective-permute-start.4) | collective-permute-done | bytes 131104 | tf_op jit(solution)/shard_map/ppermute | solution.py:58
  32.9 0.9 %bitcast_subtract_fusion.1 = f32[2,64,256]{2,1,0:T(8,128)S(1)} fusion(f32[2,64,256]{2,1,0:T(8,128)S(1)} %bitcast_add_fusion.5, f32[2,64,256]{2,1,0:T(8,128)S(1)} %collective-permute-done.4, f32[2,2,2,2,64,256]{5,4,3,2,1,0:T(8,128)} %bitcast.119, s32[]{:T(128)S(6)} %select_n.118, s32[]{:T(128)S(6)} %select_n.120, s32[]{:T(128)S(6)} %select_n.122), kind=kLoop, calls=%fused_computation.45 | loop fusion | flops 65536 | bytes 524300 | tf_op jit(solution)/shard_map/sub | solution.py:59
  34.6 4.2 %collective-permute-done.5 = f32[2,64,256]{2,1,0:T(8,128)S(1)} collective-permute-done((f32[2,64,256]{2,1,0:T(8,128)S(1)}, f32[2,64,256]{2,1,0:T(8,128)S(1)}, u32[]{:S(2)}, u32[]{:S(2)}) %collective-permute-start.5) | collective-permute-done | bytes 131104 | tf_op jit(solution)/shard_map/ppermute | solution.py:62
  38.9 1.6 %collective-permute-start.6 = (f32[2,2,64,256]{3,2,1,0:T(8,128)S(1)}, f32[2,2,64,256]{3,2,1,0:T(8,128)}, u32[]{:S(2)}, u32[]{:S(2)}) collective-permute-start(f32[2,2,64,256]{3,2,1,0:T(8,128)S(1)} %pad_maximum_fusion.5), channel_id=1, source_target_pairs={{0,4},{2,6},{4,0},{6,2},{8,12},{10,14},{12,8},{14,10},{16,20},{18,... | collective-permute-start | bytes 786440 | tf_op jit(solution)/shard_map/ppermute | solution.py:62
  40.5 4.9 %collective-permute-done.6 = f32[2,2,64,256]{3,2,1,0:T(8,128)} collective-permute-done((f32[2,2,64,256]{3,2,1,0:T(8,128)S(1)}, f32[2,2,64,256]{3,2,1,0:T(8,128)}, u32[]{:S(2)}, u32[]{:S(2)}) %collective-permute-start.6) | collective-permute-done | bytes 262176 | tf_op jit(solution)/shard_map/ppermute | solution.py:62
  45.4 1.0 %select_bitcast_fusion.7 = (f32[2,2,1,64,256]{4,3,2,1,0:T(8,128)S(1)}, f32[2,2,1,64,256]{4,3,2,1,0:T(8,128)S(1)}) fusion(f32[2,2,64,256]{3,2,1,0:T(8,128)} %collective-permute-done.6, pred[]{:T(512)S(6)} %eq.10, f32[2,1,64,256]{3,2,1,0:T(8,128)S(1)} %get-tuple-element.34, f32[2,1,64,256]{3,2,1,0:T(8,128)S(1)} %get-tuple-element.33), kind=kLoop, calls=%fused_computation.37 | loop fusion | flops 196608 | bytes 1048577 | tf_op jit(solution)/shard_map/stack | solution.py:65
  46.5 0.8 pad_maximum_fusion.2
  47.3 2.2 %collective-permute-done.7 = f32[2,2,2,64,256]{4,3,2,1,0:T(8,128)} collective-permute-done((f32[2,2,2,64,256]{4,3,2,1,0:T(8,128)}, f32[2,2,2,64,256]{4,3,2,1,0:T(8,128)}, u32[]{:S(2)}, u32[]{:S(2)}) %collective-permute-start.7) | collective-permute-done | bytes 524320 | tf_op jit(solution)/shard_map/ppermute | solution.py:62
  49.6 1.1 %select_bitcast_fusion.3 = (f32[2,2,2,1,64,256]{5,4,3,2,1,0:T(8,128)S(1)}, f32[2,2,2,1,64,256]{5,4,3,2,1,0:T(8,128)S(1)}) fusion(f32[2,2,2,64,256]{4,3,2,1,0:T(8,128)} %collective-permute-done.7, pred[]{:T(512)S(6)} %eq.9, f32[2,2,1,64,256]{4,3,2,1,0:T(8,128)S(1)} %get-tuple-element.28, f32[2,2,1,64,256]{4,3,2,1,0:T(8,128)S(1)} %get-tuple-element.27), kind=kLoop, calls=%fused_computation.22 | loop fusion | flops 393216 | bytes 2097153 | tf_op jit(solution)/shard_map/stack | solution.py:65
  51.4 1.0 %convolution_bitcast_fusion = f32[1024,256]{1,0:T(8,128)S(1)} fusion(f32[64,256]{1,0:T(8,128)S(1)} %fusion.8, f32[1024,64]{0,1:T(8,128)S(1)} %copy-done.2), kind=kOutput, calls=%fused_computation.6 | convolution fusion | flops 201326592 | bytes 1376256 | tf_op jit(solution)/shard_map/dot_general | solution.py:8
  53.0 1.8 %collective-permute-done.8 = f32[2,2,2,64,256]{4,3,1,0,2:T(8,128)S(1)} collective-permute-done((f32[2,2,2,64,256]{4,3,1,0,2:T(8,128)S(1)}, f32[2,2,2,64,256]{4,3,1,0,2:T(8,128)S(1)}, u32[]{:S(2)}, u32[]{:S(2)}) %collective-permute-start.8) | collective-permute-done | bytes 524320 | tf_op jit(solution)/shard_map/ppermute | solution.py:53
  54.8 1.6 %collective-permute-start.9 = (f32[2,2,64,256]{3,2,1,0:T(8,128)S(1)}, f32[2,2,64,256]{3,2,1,0:T(8,128)S(1)}, u32[]{:S(2)}, u32[]{:S(2)}) collective-permute-start(f32[2,2,64,256]{3,2,1,0:T(8,128)S(1)} %dynamic-slice_bitcast_fusion), channel_id=1, source_target_pairs={{0,4},{2,6},{4,0},{6,2},{8,12},{10,14},{12,8},{14,10},{16,20},{18,... | collective-permute-start | bytes 786440 | tf_op jit(solution)/shard_map/ppermute | solution.py:53
  56.5 6.8 %collective-permute-done.9 = f32[2,2,64,256]{3,2,1,0:T(8,128)S(1)} collective-permute-done((f32[2,2,64,256]{3,2,1,0:T(8,128)S(1)}, f32[2,2,64,256]{3,2,1,0:T(8,128)S(1)}, u32[]{:S(2)}, u32[]{:S(2)}) %collective-permute-start.9) | collective-permute-done | bytes 262176 | tf_op jit(solution)/shard_map/ppermute | solution.py:53
  64.1 4.2 %collective-permute-done.10 = f32[2,64,256]{2,1,0:T(8,128)S(1)} collective-permute-done((f32[2,64,256]{2,1,0:T(8,128)S(1)}, f32[2,64,256]{2,1,0:T(8,128)S(1)}, u32[]{:S(2)}, u32[]{:S(2)}) %collective-permute-start.10) | collective-permute-done | bytes 131104 | tf_op jit(solution)/shard_map/ppermute | solution.py:53
  68.4 2.2 %collective-permute-start.11 = (f32[2,64,256]{2,1,0:T(8,128)S(1)}, f32[2,64,256]{2,1,0:T(8,128)S(1)}, u32[]{:S(2)}, u32[]{:S(2)}) collective-permute-start(f32[2,64,256]{2,1,0:T(8,128)S(1)} %bitcast_add_fusion.4), channel_id=1, source_target_pairs={{0,16},{2,18},{4,20},{6,22},{8,24},{10,26},{12,28},{14,30},{16,0},... | collective-permute-start | bytes 393224 | tf_op jit(solution)/shard_map/ppermute | solution.py:58
  70.6 5.2 %collective-permute-done.11 = f32[2,64,256]{2,1,0:T(8,128)S(1)} collective-permute-done((f32[2,64,256]{2,1,0:T(8,128)S(1)}, f32[2,64,256]{2,1,0:T(8,128)S(1)}, u32[]{:S(2)}, u32[]{:S(2)}) %collective-permute-start.11) | collective-permute-done | bytes 131104 | tf_op jit(solution)/shard_map/ppermute | solution.py:58
  75.7 0.9 %bitcast_subtract_fusion = f32[2,64,256]{2,1,0:T(8,128)S(1)} fusion(f32[2,64,256]{2,1,0:T(8,128)S(1)} %bitcast_add_fusion.4, f32[2,64,256]{2,1,0:T(8,128)S(1)} %collective-permute-done.11, f32[2,2,2,2,64,256]{5,4,3,2,1,0:T(8,128)} %bitcast.118, s32[]{:T(128)S(6)} %select_n.118, s32[]{:T(128)S(6)} %select_n.120, s32[]{:T(128)S(6)} %select_n.122), kind=kLoop, calls=%fused_computation.44 | loop fusion | flops 65536 | bytes 524300 | tf_op jit(solution)/shard_map/sub | solution.py:59
  77.2 4.5 %collective-permute-done.12 = f32[2,64,256]{2,1,0:T(8,128)S(1)} collective-permute-done((f32[2,64,256]{2,1,0:T(8,128)S(1)}, f32[2,64,256]{2,1,0:T(8,128)S(1)}, u32[]{:S(2)}, u32[]{:S(2)}) %collective-permute-start.12) | collective-permute-done | bytes 131104 | tf_op jit(solution)/shard_map/ppermute | solution.py:62
  81.7 1.6 %collective-permute-start.13 = (f32[2,2,64,256]{3,2,1,0:T(8,128)S(1)}, f32[2,2,64,256]{3,2,1,0:T(8,128)S(1)}, u32[]{:S(2)}, u32[]{:S(2)}) collective-permute-start(f32[2,2,64,256]{3,2,1,0:T(8,128)S(1)} %pad_maximum_fusion.6), channel_id=1, source_target_pairs={{0,4},{2,6},{4,0},{6,2},{8,12},{10,14},{12,8},{14,10},{16,20},{18,... | collective-permute-start | bytes 786440 | tf_op jit(solution)/shard_map/ppermute | solution.py:62
  83.4 4.8 %collective-permute-done.13 = f32[2,2,64,256]{3,2,1,0:T(8,128)S(1)} collective-permute-done((f32[2,2,64,256]{3,2,1,0:T(8,128)S(1)}, f32[2,2,64,256]{3,2,1,0:T(8,128)S(1)}, u32[]{:S(2)}, u32[]{:S(2)}) %collective-permute-start.13) | collective-permute-done | bytes 262176 | tf_op jit(solution)/shard_map/ppermute | solution.py:62
  88.3 1.9 %collective-permute-done.14 = f32[2,2,2,64,256]{4,3,2,1,0:T(8,128)S(1)} collective-permute-done((f32[2,2,2,64,256]{4,3,2,1,0:T(8,128)S(1)}, f32[2,2,2,64,256]{4,3,2,1,0:T(8,128)S(1)}, u32[]{:S(2)}, u32[]{:S(2)}) %collective-permute-start.14) | collective-permute-done | bytes 524320 | tf_op jit(solution)/shard_map/ppermute | solution.py:62
  (44 shorter events, 5.8 us)
Async XLA Ops:
  0.0 2.9 %copy-start = (f32[1024,256]{1,0:T(8,128)S(1)}, f32[1024,256]{1,0:T(8,128)}, u32[]{:S(2)}) copy-start(f32[1024,256]{1,0:T(8,128)} %param.6) | copy-start | bytes 3145732
  0.0 9.5 %copy-start.1 = (f32[2,64,512]{2,1,0:T(8,128)S(1)}, f32[2,64,512]{2,1,0:T(8,128)}, u32[]{:S(2)}) copy-start(f32[2,64,512]{2,1,0:T(8,128)} %param.8) | copy-start | bytes 786436
  0.0 9.5 %collective-permute-start = (f32[1,1,2,64,512]{4,3,2,1,0:T(8,128)}, f32[1,1,2,64,512]{4,3,2,1,0:T(8,128)S(1)}, u32[]{:S(2)}, u32[]{:S(2)}) collective-permute-start(f32[1,1,2,64,512]{4,3,2,1,0:T(8,128)} %bitcast.123), channel_id=1, source_target_pairs={{0,1},{1,0},{2,3},{3,2},{4,5},{5,4},{6,7},{7,6},{8,9},{9,8},{10,11... | collective-permute-start | bytes 786440 | tf_op jit(solution)/shard_map/ppermute | solution.py:34
  9.8 2.0 %collective-permute-start.1 = (f32[2,2,2,64,256]{4,3,1,0,2:T(8,128)S(1)}, f32[2,2,2,64,256]{4,3,1,0,2:T(8,128)S(1)}, u32[]{:S(2)}, u32[]{:S(2)}) collective-permute-start(f32[2,2,2,64,256]{4,3,1,0,2:T(8,128)S(1)} %bitcast.121), channel_id=1, source_target_pairs={{0,2},{2,0},{4,6},{6,4},{8,10},{10,8},{12,14},{14,12},{16,18},{18,... | collective-permute-start | bytes 1572872 | tf_op jit(solution)/shard_map/ppermute | solution.py:53
  11.8 8.4 %collective-permute-start.2 = (f32[2,2,64,256]{3,2,1,0:T(8,128)S(1)}, f32[2,2,64,256]{3,2,1,0:T(8,128)S(1)}, u32[]{:S(2)}, u32[]{:S(2)}) collective-permute-start(f32[2,2,64,256]{3,2,1,0:T(8,128)S(1)} %dynamic-slice_bitcast_fusion.1), channel_id=1, source_target_pairs={{0,4},{2,6},{4,0},{6,2},{8,12},{10,14},{12,8},{14,10},{16,20},{18,... | collective-permute-start | bytes 786440 | tf_op jit(solution)/shard_map/ppermute | solution.py:53
  20.3 5.0 %collective-permute-start.3 = (f32[2,64,256]{2,1,0:T(8,128)S(1)}, f32[2,64,256]{2,1,0:T(8,128)S(1)}, u32[]{:S(2)}, u32[]{:S(2)}) collective-permute-start(f32[2,64,256]{2,1,0:T(8,128)S(1)} %dynamic-slice_bitcast_fusion.3), channel_id=1, source_target_pairs={{0,8},{2,10},{4,12},{6,14},{8,0},{10,2},{12,4},{14,6},{16,24},{18,... | collective-permute-start | bytes 393224 | tf_op jit(solution)/shard_map/ppermute | solution.py:53
  25.4 7.5 %collective-permute-start.4 = (f32[2,64,256]{2,1,0:T(8,128)S(1)}, f32[2,64,256]{2,1,0:T(8,128)S(1)}, u32[]{:S(2)}, u32[]{:S(2)}) collective-permute-start(f32[2,64,256]{2,1,0:T(8,128)S(1)} %bitcast_add_fusion.5), channel_id=1, source_target_pairs={{0,16},{2,18},{4,20},{6,22},{8,24},{10,26},{12,28},{14,30},{16,0},... | collective-permute-start | bytes 393224 | tf_op jit(solution)/shard_map/ppermute | solution.py:58
  33.8 5.0 %collective-permute-start.5 = (f32[2,64,256]{2,1,0:T(8,128)S(1)}, f32[2,64,256]{2,1,0:T(8,128)S(1)}, u32[]{:S(2)}, u32[]{:S(2)}) collective-permute-start(f32[2,64,256]{2,1,0:T(8,128)S(1)} %bitcast_subtract_fusion.1), channel_id=1, source_target_pairs={{0,8},{2,10},{4,12},{6,14},{8,0},{10,2},{12,4},{14,6},{16,24},{18,... | collective-permute-start | bytes 393224 | tf_op jit(solution)/shard_map/ppermute | solution.py:62
  38.9 6.5 %collective-permute-start.6 = (f32[2,2,64,256]{3,2,1,0:T(8,128)S(1)}, f32[2,2,64,256]{3,2,1,0:T(8,128)}, u32[]{:S(2)}, u32[]{:S(2)}) collective-permute-start(f32[2,2,64,256]{3,2,1,0:T(8,128)S(1)} %pad_maximum_fusion.5), channel_id=1, source_target_pairs={{0,4},{2,6},{4,0},{6,2},{8,12},{10,14},{12,8},{14,10},{16,20},{18,... | collective-permute-start | bytes 786440 | tf_op jit(solution)/shard_map/ppermute | solution.py:62
  46.4 5.0 %copy-start.2 = (f32[1024,64]{0,1:T(8,128)S(1)}, f32[1024,64]{0,1:T(8,128)}, u32[]{:S(2)}) copy-start(f32[1024,64]{0,1:T(8,128)} %param.9) | copy-start | bytes 786436
  47.3 2.3 %collective-permute-start.7 = (f32[2,2,2,64,256]{4,3,2,1,0:T(8,128)}, f32[2,2,2,64,256]{4,3,2,1,0:T(8,128)}, u32[]{:S(2)}, u32[]{:S(2)}) collective-permute-start(f32[2,2,2,64,256]{4,3,2,1,0:T(8,128)} %pad_maximum_fusion.2), channel_id=1, source_target_pairs={{0,2},{2,0},{4,6},{6,4},{8,10},{10,8},{12,14},{14,12},{16,18},{18,... | collective-permute-start | bytes 1572872 | tf_op jit(solution)/shard_map/ppermute | solution.py:62
  52.8 2.0 %collective-permute-start.8 = (f32[2,2,2,64,256]{4,3,1,0,2:T(8,128)S(1)}, f32[2,2,2,64,256]{4,3,1,0,2:T(8,128)S(1)}, u32[]{:S(2)}, u32[]{:S(2)}) collective-permute-start(f32[2,2,2,64,256]{4,3,1,0,2:T(8,128)S(1)} %bitcast.122), channel_id=1, source_target_pairs={{0,2},{2,0},{4,6},{6,4},{8,10},{10,8},{12,14},{14,12},{16,18},{18,... | collective-permute-start | bytes 1572872 | tf_op jit(solution)/shard_map/ppermute | solution.py:53
  54.8 8.4 %collective-permute-start.9 = (f32[2,2,64,256]{3,2,1,0:T(8,128)S(1)}, f32[2,2,64,256]{3,2,1,0:T(8,128)S(1)}, u32[]{:S(2)}, u32[]{:S(2)}) collective-permute-start(f32[2,2,64,256]{3,2,1,0:T(8,128)S(1)} %dynamic-slice_bitcast_fusion), channel_id=1, source_target_pairs={{0,4},{2,6},{4,0},{6,2},{8,12},{10,14},{12,8},{14,10},{16,20},{18,... | collective-permute-start | bytes 786440 | tf_op jit(solution)/shard_map/ppermute | solution.py:53
  63.3 5.0 %collective-permute-start.10 = (f32[2,64,256]{2,1,0:T(8,128)S(1)}, f32[2,64,256]{2,1,0:T(8,128)S(1)}, u32[]{:S(2)}, u32[]{:S(2)}) collective-permute-start(f32[2,64,256]{2,1,0:T(8,128)S(1)} %dynamic-slice_bitcast_fusion.2), channel_id=1, source_target_pairs={{0,8},{2,10},{4,12},{6,14},{8,0},{10,2},{12,4},{14,6},{16,24},{18,... | collective-permute-start | bytes 393224 | tf_op jit(solution)/shard_map/ppermute | solution.py:53
  68.4 7.3 %collective-permute-start.11 = (f32[2,64,256]{2,1,0:T(8,128)S(1)}, f32[2,64,256]{2,1,0:T(8,128)S(1)}, u32[]{:S(2)}, u32[]{:S(2)}) collective-permute-start(f32[2,64,256]{2,1,0:T(8,128)S(1)} %bitcast_add_fusion.4), channel_id=1, source_target_pairs={{0,16},{2,18},{4,20},{6,22},{8,24},{10,26},{12,28},{14,30},{16,0},... | collective-permute-start | bytes 393224 | tf_op jit(solution)/shard_map/ppermute | solution.py:58
  76.6 5.0 %collective-permute-start.12 = (f32[2,64,256]{2,1,0:T(8,128)S(1)}, f32[2,64,256]{2,1,0:T(8,128)S(1)}, u32[]{:S(2)}, u32[]{:S(2)}) collective-permute-start(f32[2,64,256]{2,1,0:T(8,128)S(1)} %bitcast_subtract_fusion), channel_id=1, source_target_pairs={{0,8},{2,10},{4,12},{6,14},{8,0},{10,2},{12,4},{14,6},{16,24},{18,... | collective-permute-start | bytes 393224 | tf_op jit(solution)/shard_map/ppermute | solution.py:62
  81.7 6.4 %collective-permute-start.13 = (f32[2,2,64,256]{3,2,1,0:T(8,128)S(1)}, f32[2,2,64,256]{3,2,1,0:T(8,128)S(1)}, u32[]{:S(2)}, u32[]{:S(2)}) collective-permute-start(f32[2,2,64,256]{3,2,1,0:T(8,128)S(1)} %pad_maximum_fusion.6), channel_id=1, source_target_pairs={{0,4},{2,6},{4,0},{6,2},{8,12},{10,14},{12,8},{14,10},{16,20},{18,... | collective-permute-start | bytes 786440 | tf_op jit(solution)/shard_map/ppermute | solution.py:62
  88.3 2.0 %collective-permute-start.14 = (f32[2,2,2,64,256]{4,3,2,1,0:T(8,128)S(1)}, f32[2,2,2,64,256]{4,3,2,1,0:T(8,128)S(1)}, u32[]{:S(2)}, u32[]{:S(2)}) collective-permute-start(f32[2,2,2,64,256]{4,3,2,1,0:T(8,128)S(1)} %pad_maximum_fusion.3), channel_id=1, source_target_pairs={{0,2},{2,0},{4,6},{6,4},{8,10},{10,8},{12,14},{14,12},{16,18},{18,... | collective-permute-start | bytes 1572872 | tf_op jit(solution)/shard_map/ppermute | solution.py:62

commit v6 on v5

--- a/solution.py
+++ b/solution.py
@@ -5,7 +5,7 @@
 
 
 def product(left, right):
-    return jnp.dot(left, right, precision=lax.Precision.HIGHEST, preferred_element_type=jnp.float32)
+    return jnp.dot(left, right, precision=lax.Precision.HIGH, preferred_element_type=jnp.float32)
 
 
 def halving_sum_scatter(x, axis, n, riders=None):

time: 92.1 us -> 91.3 us (level)
  matrix products: 12.8 us -> 9.41 us
  waiting for transfers between devices: 49.9 us -> 52.4 us
    dot_general x5, matrix products: 12.8 us -> 9.41 us  [product(): jnp.dot(left, right, precision=lax.Precision.HIGH, preferred_element_type...]
    ppermute x6, waiting for transfers between devices: 19.2 us -> 20.5 us  [reduce_then_gather(): got = lax.ppermute(send, axis, [(i, i ^ 1 << j) for i in range(n)])]
    ppermute x1, waiting for transfers between devices: 1.31 us -> 2.54 us  [doubling_gather(): got = lax.ppermute(y, axis, [(i, i ^ 1 << j) for i in range(n)])]
  transfers between devices with their start and end apart: 15 -> 15, of which waited for: 15 -> 15; matrix products, arithmetic and copies ran while one was open for 15% -> 12% of each run, Pallas kernels for 0% -> 0%
where the time goes in v6:
time: 91.3 us; the launch traced here: 91 us
  waiting for transfers between devices  52.4 us (57%)
  starting transfers between devices  19 us (21%)
  matrix products  9.41 us (10%)
  other arithmetic  6.39 us (7%)
  local copies, waits for them, and re-layouts  3.54 us (4%)
    ppermute x6, waiting for transfers between devices, reduce_then_gather(): got = lax.ppermute(y, axis, [(i, i ^ 1 << j) for i in range(n)])  22.6 us
    ppermute x6, waiting for transfers between devices, reduce_then_gather(): got = lax.ppermute(send, axis, [(i, i ^ 1 << j) for i in range(n)])  20.5 us
    dot_general x5, matrix products, product(): jnp.dot(left, right, precision=lax.Precision.HIGH, preferred_element_type...  9.41 us
    ppermute x2, waiting for transfers between devices, reduce_then_gather(): y = y + lax.ppermute(y, axis, [(i, i ^ 1 << top) for i in range(n)])  6.77 us
    ppermute x6, starting transfers between devices, reduce_then_gather(): got = lax.ppermute(send, axis, [(i, i ^ 1 << j) for i in range(n)])  6.36 us
    ppermute x2, starting transfers between devices, reduce_then_gather(): y = y + lax.ppermute(y, axis, [(i, i ^ 1 << top) for i in range(n)])  5.04 us
    ppermute x6, starting transfers between devices, reduce_then_gather(): got = lax.ppermute(y, axis, [(i, i ^ 1 << j) for i in range(n)])  4.64 us
    another operation x12, other arithmetic, reduce_then_gather(): y = jnp.stack([low, high], k - 1 - j)  3.4 us
  transfers between devices with their start and end apart: 15, of which 15 were waited for; matrix products, arithmetic and copies ran while one was open for 12% of the time, Pallas kernels for 0%

profile of v6, /device:TPU:0, one launch (start us, length us, event | category | flops | bytes accessed | tf_op | source)
XLA Modules:
  0.0 91.0 jit_solution(12833054112218259791)
XLA Ops:
  0.0 2.9 %collective-permute-start = (f32[1,1,2,64,512]{4,3,2,1,0:T(8,128)}, f32[1,1,2,64,512]{4,3,2,1,0:T(8,128)S(1)}, u32[]{:S(2)}, u32[]{:S(2)}) collective-permute-start(f32[1,1,2,64,512]{4,3,2,1,0:T(8,128)} %bitcast.123), channel_id=1, source_target_pairs={{0,1},{1,0},{2,3},{3,2},{4,5},{5,4},{6,7},{7,6},{8,9},{9,8},{10,11... | collective-permute-start | bytes 786440 | tf_op jit(solution)/shard_map/ppermute | solution.py:34
  2.9 4.0 %fusion.2 = f32[1024,256]{1,0:T(8,128)S(1)} fusion(f32[1024,256]{1,0:T(8,128)S(1)} %copy-done, f32[2,1024,1024]{2,1,0:T(8,128)} %param.5), kind=kOutput, calls=%fused_computation.2 | convolution fusion | flops 1610612736 | bytes 6291456 | tf_op jit(solution)/shard_map/dot_general | solution.py:8
  6.9 2.5 %collective-permute-done = f32[1,1,2,64,512]{4,3,2,1,0:T(8,128)S(1)} collective-permute-done((f32[1,1,2,64,512]{4,3,2,1,0:T(8,128)}, f32[1,1,2,64,512]{4,3,2,1,0:T(8,128)S(1)}, u32[]{:S(2)}, u32[]{:S(2)}) %collective-permute-start) | collective-permute-done | bytes 262176 | tf_op jit(solution)/shard_map/ppermute | solution.py:34
  9.8 1.9 %collective-permute-done.1 = f32[2,2,2,64,256]{4,3,1,0,2:T(8,128)S(1)} collective-permute-done((f32[2,2,2,64,256]{4,3,1,0,2:T(8,128)S(1)}, f32[2,2,2,64,256]{4,3,1,0,2:T(8,128)S(1)}, u32[]{:S(2)}, u32[]{:S(2)}) %collective-permute-start.1) | collective-permute-done | bytes 524320 | tf_op jit(solution)/shard_map/ppermute | solution.py:53
  11.8 1.8 %collective-permute-start.2 = (f32[2,2,64,256]{3,2,1,0:T(8,128)S(1)}, f32[2,2,64,256]{3,2,1,0:T(8,128)S(1)}, u32[]{:S(2)}, u32[]{:S(2)}) collective-permute-start(f32[2,2,64,256]{3,2,1,0:T(8,128)S(1)} %dynamic-slice_bitcast_fusion.1), channel_id=1, source_target_pairs={{0,4},{2,6},{4,0},{6,2},{8,12},{10,14},{12,8},{14,10},{16,20},{18,... | collective-permute-start | bytes 786440 | tf_op jit(solution)/shard_map/ppermute | solution.py:53
  13.7 4.0 %fusion = f32[1024,256]{1,0:T(8,128)S(1)} fusion(f32[1024,256]{1,0:T(8,128)S(1)} %copy-done, f32[2,1024,1024]{2,1,0:T(8,128)} %param.5), kind=kOutput, calls=%fused_computation | convolution fusion | flops 1610612736 | bytes 6291456 | tf_op jit(solution)/shard_map/dot_general | solution.py:8
  17.6 2.6 %collective-permute-done.2 = f32[2,2,64,256]{3,2,1,0:T(8,128)S(1)} collective-permute-done((f32[2,2,64,256]{3,2,1,0:T(8,128)S(1)}, f32[2,2,64,256]{3,2,1,0:T(8,128)S(1)}, u32[]{:S(2)}, u32[]{:S(2)}) %collective-permute-start.2) | collective-permute-done | bytes 262176 | tf_op jit(solution)/shard_map/ppermute | solution.py:53
  20.3 1.9 %collective-permute-start.3 = (f32[2,64,256]{2,1,0:T(8,128)S(1)}, f32[2,64,256]{2,1,0:T(8,128)S(1)}, u32[]{:S(2)}, u32[]{:S(2)}) collective-permute-start(f32[2,64,256]{2,1,0:T(8,128)S(1)} %dynamic-slice_bitcast_fusion.3), channel_id=1, source_target_pairs={{0,8},{2,10},{4,12},{6,14},{8,0},{10,2},{12,4},{14,6},{16,24},{18,... | collective-permute-start | bytes 393224 | tf_op jit(solution)/shard_map/ppermute | solution.py:53
  22.2 3.2 %collective-permute-done.3 = f32[2,64,256]{2,1,0:T(8,128)S(1)} collective-permute-done((f32[2,64,256]{2,1,0:T(8,128)S(1)}, f32[2,64,256]{2,1,0:T(8,128)S(1)}, u32[]{:S(2)}, u32[]{:S(2)}) %collective-permute-start.3) | collective-permute-done | bytes 131104 | tf_op jit(solution)/shard_map/ppermute | solution.py:53
  25.4 2.9 %collective-permute-start.4 = (f32[2,64,256]{2,1,0:T(8,128)S(1)}, f32[2,64,256]{2,1,0:T(8,128)S(1)}, u32[]{:S(2)}, u32[]{:S(2)}) collective-permute-start(f32[2,64,256]{2,1,0:T(8,128)S(1)} %bitcast_add_fusion.5), channel_id=1, source_target_pairs={{0,16},{2,18},{4,20},{6,22},{8,24},{10,26},{12,28},{14,30},{16,0},... | collective-permute-start | bytes 393224 | tf_op jit(solution)/shard_map/ppermute | solution.py:58
  28.3 3.0 %fusion.15 = (f32[1,1024,256]{2,1,0:T(8,128)}, f32[1,1024,256]{2,1,0:T(8,128)}) fusion(f32[2,1024,256]{2,1,0:T(8,128)} %param.7), kind=kLoop, calls=%fused_computation.60 | loop fusion | bytes 4194304 | tf_op jit(solution)/shard_map/slice | solution.py:106
  31.3 1.6 %collective-permute-done.4 = f32[2,64,256]{2,1,0:T(8,128)S(1)} collective-permute-done((f32[2,64,256]{2,1,0:T(8,128)S(1)}, f32[2,64,256]{2,1,0:T(8,128)S(1)}, u32[]{:S(2)}, u32[]{:S(2)}) %collective-permute-start.4) | collective-permute-done | bytes 131104 | tf_op jit(solution)/shard_map/ppermute | solution.py:58
  32.9 0.9 %bitcast_subtract_fusion.1 = f32[2,64,256]{2,1,0:T(8,128)S(1)} fusion(f32[2,64,256]{2,1,0:T(8,128)S(1)} %bitcast_add_fusion.5, f32[2,64,256]{2,1,0:T(8,128)S(1)} %collective-permute-done.4, f32[2,2,2,2,64,256]{5,4,3,2,1,0:T(8,128)} %bitcast.119, s32[]{:T(128)S(6)} %select_n.118, s32[]{:T(128)S(6)} %select_n.120, s32[]{:T(128)S(6)} %select_n.122), kind=kLoop, calls=%fused_computation.45 | loop fusion | flops 65536 | bytes 524300 | tf_op jit(solution)/shard_map/sub | solution.py:59
  33.8 0.8 collective-permute-start.5
  34.6 4.2 %collective-permute-done.5 = f32[2,64,256]{2,1,0:T(8,128)S(1)} collective-permute-done((f32[2,64,256]{2,1,0:T(8,128)S(1)}, f32[2,64,256]{2,1,0:T(8,128)S(1)}, u32[]{:S(2)}, u32[]{:S(2)}) %collective-permute-start.5) | collective-permute-done | bytes 131104 | tf_op jit(solution)/shard_map/ppermute | solution.py:62
  38.9 1.6 %collective-permute-start.6 = (f32[2,2,64,256]{3,2,1,0:T(8,128)S(1)}, f32[2,2,64,256]{3,2,1,0:T(8,128)}, u32[]{:S(2)}, u32[]{:S(2)}) collective-permute-start(f32[2,2,64,256]{3,2,1,0:T(8,128)S(1)} %pad_maximum_fusion.5), channel_id=1, source_target_pairs={{0,4},{2,6},{4,0},{6,2},{8,12},{10,14},{12,8},{14,10},{16,20},{18,... | collective-permute-start | bytes 786440 | tf_op jit(solution)/shard_map/ppermute | solution.py:62
  40.5 4.9 %collective-permute-done.6 = f32[2,2,64,256]{3,2,1,0:T(8,128)} collective-permute-done((f32[2,2,64,256]{3,2,1,0:T(8,128)S(1)}, f32[2,2,64,256]{3,2,1,0:T(8,128)}, u32[]{:S(2)}, u32[]{:S(2)}) %collective-permute-start.6) | collective-permute-done | bytes 262176 | tf_op jit(solution)/shard_map/ppermute | solution.py:62
  45.4 1.0 %select_bitcast_fusion.7 = (f32[2,2,1,64,256]{4,3,2,1,0:T(8,128)S(1)}, f32[2,2,1,64,256]{4,3,2,1,0:T(8,128)S(1)}) fusion(f32[2,2,64,256]{3,2,1,0:T(8,128)} %collective-permute-done.6, pred[]{:T(512)S(6)} %eq.10, f32[2,1,64,256]{3,2,1,0:T(8,128)S(1)} %get-tuple-element.34, f32[2,1,64,256]{3,2,1,0:T(8,128)S(1)} %get-tuple-element.33), kind=kLoop, calls=%fused_computation.37 | loop fusion | flops 196608 | bytes 1048577 | tf_op jit(solution)/shard_map/stack | solution.py:65
  46.5 0.8 pad_maximum_fusion.2
  47.3 2.2 %collective-permute-done.7 = f32[2,2,2,64,256]{4,3,2,1,0:T(8,128)} collective-permute-done((f32[2,2,2,64,256]{4,3,2,1,0:T(8,128)}, f32[2,2,2,64,256]{4,3,2,1,0:T(8,128)}, u32[]{:S(2)}, u32[]{:S(2)}) %collective-permute-start.7) | collective-permute-done | bytes 524320 | tf_op jit(solution)/shard_map/ppermute | solution.py:62
  49.6 1.1 %select_bitcast_fusion.3 = (f32[2,2,2,1,64,256]{5,4,3,2,1,0:T(8,128)S(1)}, f32[2,2,2,1,64,256]{5,4,3,2,1,0:T(8,128)S(1)}) fusion(f32[2,2,2,64,256]{4,3,2,1,0:T(8,128)} %collective-permute-done.7, pred[]{:T(512)S(6)} %eq.9, f32[2,2,1,64,256]{4,3,2,1,0:T(8,128)S(1)} %get-tuple-element.28, f32[2,2,1,64,256]{4,3,2,1,0:T(8,128)S(1)} %get-tuple-element.27), kind=kLoop, calls=%fused_computation.22 | loop fusion | flops 393216 | bytes 2097153 | tf_op jit(solution)/shard_map/stack | solution.py:65
  52.3 1.8 %collective-permute-done.8 = f32[2,2,2,64,256]{4,3,1,0,2:T(8,128)S(1)} collective-permute-done((f32[2,2,2,64,256]{4,3,1,0,2:T(8,128)S(1)}, f32[2,2,2,64,256]{4,3,1,0,2:T(8,128)S(1)}, u32[]{:S(2)}, u32[]{:S(2)}) %collective-permute-start.8) | collective-permute-done | bytes 524320 | tf_op jit(solution)/shard_map/ppermute | solution.py:53
  54.2 1.6 %collective-permute-start.9 = (f32[2,2,64,256]{3,2,1,0:T(8,128)S(1)}, f32[2,2,64,256]{3,2,1,0:T(8,128)S(1)}, u32[]{:S(2)}, u32[]{:S(2)}) collective-permute-start(f32[2,2,64,256]{3,2,1,0:T(8,128)S(1)} %dynamic-slice_bitcast_fusion), channel_id=1, source_target_pairs={{0,4},{2,6},{4,0},{6,2},{8,12},{10,14},{12,8},{14,10},{16,20},{18,... | collective-permute-start | bytes 786440 | tf_op jit(solution)/shard_map/ppermute | solution.py:53
  55.9 6.8 %collective-permute-done.9 = f32[2,2,64,256]{3,2,1,0:T(8,128)S(1)} collective-permute-done((f32[2,2,64,256]{3,2,1,0:T(8,128)S(1)}, f32[2,2,64,256]{3,2,1,0:T(8,128)S(1)}, u32[]{:S(2)}, u32[]{:S(2)}) %collective-permute-start.9) | collective-permute-done | bytes 262176 | tf_op jit(solution)/shard_map/ppermute | solution.py:53
  63.5 4.2 %collective-permute-done.10 = f32[2,64,256]{2,1,0:T(8,128)S(1)} collective-permute-done((f32[2,64,256]{2,1,0:T(8,128)S(1)}, f32[2,64,256]{2,1,0:T(8,128)S(1)}, u32[]{:S(2)}, u32[]{:S(2)}) %collective-permute-start.10) | collective-permute-done | bytes 131104 | tf_op jit(solution)/shard_map/ppermute | solution.py:53
  67.8 2.2 %collective-permute-start.11 = (f32[2,64,256]{2,1,0:T(8,128)S(1)}, f32[2,64,256]{2,1,0:T(8,128)S(1)}, u32[]{:S(2)}, u32[]{:S(2)}) collective-permute-start(f32[2,64,256]{2,1,0:T(8,128)S(1)} %bitcast_add_fusion.4), channel_id=1, source_target_pairs={{0,16},{2,18},{4,20},{6,22},{8,24},{10,26},{12,28},{14,30},{16,0},... | collective-permute-start | bytes 393224 | tf_op jit(solution)/shard_map/ppermute | solution.py:58
  69.9 5.2 %collective-permute-done.11 = f32[2,64,256]{2,1,0:T(8,128)S(1)} collective-permute-done((f32[2,64,256]{2,1,0:T(8,128)S(1)}, f32[2,64,256]{2,1,0:T(8,128)S(1)}, u32[]{:S(2)}, u32[]{:S(2)}) %collective-permute-start.11) | collective-permute-done | bytes 131104 | tf_op jit(solution)/shard_map/ppermute | solution.py:58
  75.1 0.9 %bitcast_subtract_fusion = f32[2,64,256]{2,1,0:T(8,128)S(1)} fusion(f32[2,64,256]{2,1,0:T(8,128)S(1)} %bitcast_add_fusion.4, f32[2,64,256]{2,1,0:T(8,128)S(1)} %collective-permute-done.11, f32[2,2,2,2,64,256]{5,4,3,2,1,0:T(8,128)} %bitcast.118, s32[]{:T(128)S(6)} %select_n.118, s32[]{:T(128)S(6)} %select_n.120, s32[]{:T(128)S(6)} %select_n.122), kind=kLoop, calls=%fused_computation.44 | loop fusion | flops 65536 | bytes 524300 | tf_op jit(solution)/shard_map/sub | solution.py:59
  76.5 4.5 %collective-permute-done.12 = f32[2,64,256]{2,1,0:T(8,128)S(1)} collective-permute-done((f32[2,64,256]{2,1,0:T(8,128)S(1)}, f32[2,64,256]{2,1,0:T(8,128)S(1)}, u32[]{:S(2)}, u32[]{:S(2)}) %collective-permute-start.12) | collective-permute-done | bytes 131104 | tf_op jit(solution)/shard_map/ppermute | solution.py:62
  81.1 1.6 %collective-permute-start.13 = (f32[2,2,64,256]{3,2,1,0:T(8,128)S(1)}, f32[2,2,64,256]{3,2,1,0:T(8,128)S(1)}, u32[]{:S(2)}, u32[]{:S(2)}) collective-permute-start(f32[2,2,64,256]{3,2,1,0:T(8,128)S(1)} %pad_maximum_fusion.6), channel_id=1, source_target_pairs={{0,4},{2,6},{4,0},{6,2},{8,12},{10,14},{12,8},{14,10},{16,20},{18,... | collective-permute-start | bytes 786440 | tf_op jit(solution)/shard_map/ppermute | solution.py:62
  82.7 4.8 %collective-permute-done.13 = f32[2,2,64,256]{3,2,1,0:T(8,128)S(1)} collective-permute-done((f32[2,2,64,256]{3,2,1,0:T(8,128)S(1)}, f32[2,2,64,256]{3,2,1,0:T(8,128)S(1)}, u32[]{:S(2)}, u32[]{:S(2)}) %collective-permute-start.13) | collective-permute-done | bytes 262176 | tf_op jit(solution)/shard_map/ppermute | solution.py:62
  87.7 1.9 %collective-permute-done.14 = f32[2,2,2,64,256]{4,3,2,1,0:T(8,128)S(1)} collective-permute-done((f32[2,2,2,64,256]{4,3,2,1,0:T(8,128)S(1)}, f32[2,2,2,64,256]{4,3,2,1,0:T(8,128)S(1)}, u32[]{:S(2)}, u32[]{:S(2)}) %collective-permute-start.14) | collective-permute-done | bytes 524320 | tf_op jit(solution)/shard_map/ppermute | solution.py:62
  (44 shorter events, 5.2 us)
Async XLA Ops:
  0.0 2.9 %copy-start = (f32[1024,256]{1,0:T(8,128)S(1)}, f32[1024,256]{1,0:T(8,128)}, u32[]{:S(2)}) copy-start(f32[1024,256]{1,0:T(8,128)} %param.6) | copy-start | bytes 3145732
  0.0 9.5 %copy-start.1 = (f32[2,64,512]{2,1,0:T(8,128)S(1)}, f32[2,64,512]{2,1,0:T(8,128)}, u32[]{:S(2)}) copy-start(f32[2,64,512]{2,1,0:T(8,128)} %param.8) | copy-start | bytes 786436
  0.0 9.5 %collective-permute-start = (f32[1,1,2,64,512]{4,3,2,1,0:T(8,128)}, f32[1,1,2,64,512]{4,3,2,1,0:T(8,128)S(1)}, u32[]{:S(2)}, u32[]{:S(2)}) collective-permute-start(f32[1,1,2,64,512]{4,3,2,1,0:T(8,128)} %bitcast.123), channel_id=1, source_target_pairs={{0,1},{1,0},{2,3},{3,2},{4,5},{5,4},{6,7},{7,6},{8,9},{9,8},{10,11... | collective-permute-start | bytes 786440 | tf_op jit(solution)/shard_map/ppermute | solution.py:34
  9.8 2.0 %collective-permute-start.1 = (f32[2,2,2,64,256]{4,3,1,0,2:T(8,128)S(1)}, f32[2,2,2,64,256]{4,3,1,0,2:T(8,128)S(1)}, u32[]{:S(2)}, u32[]{:S(2)}) collective-permute-start(f32[2,2,2,64,256]{4,3,1,0,2:T(8,128)S(1)} %bitcast.121), channel_id=1, source_target_pairs={{0,2},{2,0},{4,6},{6,4},{8,10},{10,8},{12,14},{14,12},{16,18},{18,... | collective-permute-start | bytes 1572872 | tf_op jit(solution)/shard_map/ppermute | solution.py:53
  11.8 8.4 %collective-permute-start.2 = (f32[2,2,64,256]{3,2,1,0:T(8,128)S(1)}, f32[2,2,64,256]{3,2,1,0:T(8,128)S(1)}, u32[]{:S(2)}, u32[]{:S(2)}) collective-permute-start(f32[2,2,64,256]{3,2,1,0:T(8,128)S(1)} %dynamic-slice_bitcast_fusion.1), channel_id=1, source_target_pairs={{0,4},{2,6},{4,0},{6,2},{8,12},{10,14},{12,8},{14,10},{16,20},{18,... | collective-permute-start | bytes 786440 | tf_op jit(solution)/shard_map/ppermute | solution.py:53
  20.3 5.0 %collective-permute-start.3 = (f32[2,64,256]{2,1,0:T(8,128)S(1)}, f32[2,64,256]{2,1,0:T(8,128)S(1)}, u32[]{:S(2)}, u32[]{:S(2)}) collective-permute-start(f32[2,64,256]{2,1,0:T(8,128)S(1)} %dynamic-slice_bitcast_fusion.3), channel_id=1, source_target_pairs={{0,8},{2,10},{4,12},{6,14},{8,0},{10,2},{12,4},{14,6},{16,24},{18,... | collective-permute-start | bytes 393224 | tf_op jit(solution)/shard_map/ppermute | solution.py:53
  25.4 7.5 %collective-permute-start.4 = (f32[2,64,256]{2,1,0:T(8,128)S(1)}, f32[2,64,256]{2,1,0:T(8,128)S(1)}, u32[]{:S(2)}, u32[]{:S(2)}) collective-permute-start(f32[2,64,256]{2,1,0:T(8,128)S(1)} %bitcast_add_fusion.5), channel_id=1, source_target_pairs={{0,16},{2,18},{4,20},{6,22},{8,24},{10,26},{12,28},{14,30},{16,0},... | collective-permute-start | bytes 393224 | tf_op jit(solution)/shard_map/ppermute | solution.py:58
  33.8 5.0 %collective-permute-start.5 = (f32[2,64,256]{2,1,0:T(8,128)S(1)}, f32[2,64,256]{2,1,0:T(8,128)S(1)}, u32[]{:S(2)}, u32[]{:S(2)}) collective-permute-start(f32[2,64,256]{2,1,0:T(8,128)S(1)} %bitcast_subtract_fusion.1), channel_id=1, source_target_pairs={{0,8},{2,10},{4,12},{6,14},{8,0},{10,2},{12,4},{14,6},{16,24},{18,... | collective-permute-start | bytes 393224 | tf_op jit(solution)/shard_map/ppermute | solution.py:62
  38.9 6.5 %collective-permute-start.6 = (f32[2,2,64,256]{3,2,1,0:T(8,128)S(1)}, f32[2,2,64,256]{3,2,1,0:T(8,128)}, u32[]{:S(2)}, u32[]{:S(2)}) collective-permute-start(f32[2,2,64,256]{3,2,1,0:T(8,128)S(1)} %pad_maximum_fusion.5), channel_id=1, source_target_pairs={{0,4},{2,6},{4,0},{6,2},{8,12},{10,14},{12,8},{14,10},{16,20},{18,... | collective-permute-start | bytes 786440 | tf_op jit(solution)/shard_map/ppermute | solution.py:62
  46.4 4.8 %copy-start.2 = (f32[1024,64]{0,1:T(8,128)S(1)}, f32[1024,64]{0,1:T(8,128)}, u32[]{:S(2)}) copy-start(f32[1024,64]{0,1:T(8,128)} %param.9) | copy-start | bytes 786436
  47.3 2.3 %collective-permute-start.7 = (f32[2,2,2,64,256]{4,3,2,1,0:T(8,128)}, f32[2,2,2,64,256]{4,3,2,1,0:T(8,128)}, u32[]{:S(2)}, u32[]{:S(2)}) collective-permute-start(f32[2,2,2,64,256]{4,3,2,1,0:T(8,128)} %pad_maximum_fusion.2), channel_id=1, source_target_pairs={{0,2},{2,0},{4,6},{6,4},{8,10},{10,8},{12,14},{14,12},{16,18},{18,... | collective-permute-start | bytes 1572872 | tf_op jit(solution)/shard_map/ppermute | solution.py:62
  52.1 2.0 %collective-permute-start.8 = (f32[2,2,2,64,256]{4,3,1,0,2:T(8,128)S(1)}, f32[2,2,2,64,256]{4,3,1,0,2:T(8,128)S(1)}, u32[]{:S(2)}, u32[]{:S(2)}) collective-permute-start(f32[2,2,2,64,256]{4,3,1,0,2:T(8,128)S(1)} %bitcast.122), channel_id=1, source_target_pairs={{0,2},{2,0},{4,6},{6,4},{8,10},{10,8},{12,14},{14,12},{16,18},{18,... | collective-permute-start | bytes 1572872 | tf_op jit(solution)/shard_map/ppermute | solution.py:53
  54.2 8.4 %collective-permute-start.9 = (f32[2,2,64,256]{3,2,1,0:T(8,128)S(1)}, f32[2,2,64,256]{3,2,1,0:T(8,128)S(1)}, u32[]{:S(2)}, u32[]{:S(2)}) collective-permute-start(f32[2,2,64,256]{3,2,1,0:T(8,128)S(1)} %dynamic-slice_bitcast_fusion), channel_id=1, source_target_pairs={{0,4},{2,6},{4,0},{6,2},{8,12},{10,14},{12,8},{14,10},{16,20},{18,... | collective-permute-start | bytes 786440 | tf_op jit(solution)/shard_map/ppermute | solution.py:53
  62.7 5.0 %collective-permute-start.10 = (f32[2,64,256]{2,1,0:T(8,128)S(1)}, f32[2,64,256]{2,1,0:T(8,128)S(1)}, u32[]{:S(2)}, u32[]{:S(2)}) collective-permute-start(f32[2,64,256]{2,1,0:T(8,128)S(1)} %dynamic-slice_bitcast_fusion.2), channel_id=1, source_target_pairs={{0,8},{2,10},{4,12},{6,14},{8,0},{10,2},{12,4},{14,6},{16,24},{18,... | collective-permute-start | bytes 393224 | tf_op jit(solution)/shard_map/ppermute | solution.py:53
  67.8 7.3 %collective-permute-start.11 = (f32[2,64,256]{2,1,0:T(8,128)S(1)}, f32[2,64,256]{2,1,0:T(8,128)S(1)}, u32[]{:S(2)}, u32[]{:S(2)}) collective-permute-start(f32[2,64,256]{2,1,0:T(8,128)S(1)} %bitcast_add_fusion.4), channel_id=1, source_target_pairs={{0,16},{2,18},{4,20},{6,22},{8,24},{10,26},{12,28},{14,30},{16,0},... | collective-permute-start | bytes 393224 | tf_op jit(solution)/shard_map/ppermute | solution.py:58
  76.0 5.0 %collective-permute-start.12 = (f32[2,64,256]{2,1,0:T(8,128)S(1)}, f32[2,64,256]{2,1,0:T(8,128)S(1)}, u32[]{:S(2)}, u32[]{:S(2)}) collective-permute-start(f32[2,64,256]{2,1,0:T(8,128)S(1)} %bitcast_subtract_fusion), channel_id=1, source_target_pairs={{0,8},{2,10},{4,12},{6,14},{8,0},{10,2},{12,4},{14,6},{16,24},{18,... | collective-permute-start | bytes 393224 | tf_op jit(solution)/shard_map/ppermute | solution.py:62
  81.1 6.4 %collective-permute-start.13 = (f32[2,2,64,256]{3,2,1,0:T(8,128)S(1)}, f32[2,2,64,256]{3,2,1,0:T(8,128)S(1)}, u32[]{:S(2)}, u32[]{:S(2)}) collective-permute-start(f32[2,2,64,256]{3,2,1,0:T(8,128)S(1)} %pad_maximum_fusion.6), channel_id=1, source_target_pairs={{0,4},{2,6},{4,0},{6,2},{8,12},{10,14},{12,8},{14,10},{16,20},{18,... | collective-permute-start | bytes 786440 | tf_op jit(solution)/shard_map/ppermute | solution.py:62
  87.6 2.0 %collective-permute-start.14 = (f32[2,2,2,64,256]{4,3,2,1,0:T(8,128)S(1)}, f32[2,2,2,64,256]{4,3,2,1,0:T(8,128)S(1)}, u32[]{:S(2)}, u32[]{:S(2)}) collective-permute-start(f32[2,2,2,64,256]{4,3,2,1,0:T(8,128)S(1)} %pad_maximum_fusion.3), channel_id=1, source_target_pairs={{0,2},{2,0},{4,6},{6,4},{8,10},{10,8},{12,14},{14,12},{16,18},{18,... | collective-permute-start | bytes 1572872 | tf_op jit(solution)/shard_map/ppermute | solution.py:62

commit v7 on v5

--- a/solution.py
+++ b/solution.py
@@ -66,6 +66,40 @@
     return y.reshape(x.shape), riders
 
 
+def halves_reduce_then_gather(keep, send, right, axis, n, hold=None, riders_of=None):
+    k = n.bit_length() - 1
+    me = lax.axis_index(axis)
+    half = keep.shape[0]
+    mine = me & 1
+    r = lax.dynamic_slice_in_dim(right, mine * half, half, 0)
+    got = lax.ppermute(send, axis, [(i, i ^ 1) for i in range(n)])
+    y = lax.optimization_barrier(keep) + got
+    riders = None
+    if riders_of is not None:
+        y, hold = lax.optimization_barrier((y, hold))
+        riders = riders_of(hold)
+    for j in range(1, k - 1):
+        half //= 2
+        mine = (me >> j) & 1
+        keep = lax.dynamic_slice_in_dim(y, mine * half, half, 0)
+        send = lax.dynamic_slice_in_dim(y, (1 - mine) * half, half, 0)
+        r = lax.dynamic_slice_in_dim(r, mine * half, half, 0)
+        got = lax.ppermute(send, axis, [(i, i ^ (1 << j)) for i in range(n)])
+        if j == 1 and riders is not None:
+            got, riders = lax.optimization_barrier((got, riders))
+        y = keep + got
+    top = k - 1
+    y = y + lax.ppermute(y, axis, [(i, i ^ (1 << top)) for i in range(n)])
+    y = r - y
+    for j in reversed(range(k - 1)):
+        mine = (me >> j) & 1
+        got = lax.ppermute(y, axis, [(i, i ^ (1 << j)) for i in range(n)])
+        low = jnp.where(mine == 0, y, got)
+        high = jnp.where(mine == 0, got, y)
+        y = jnp.concatenate([low, high], 0)
+    return y, riders
+
+
 def make_shards(n, m):
     power_of_two = n > 1 and (n & (n - 1)) == 0
     rhs_power_of_two = m > 1 and (m & (m - 1)) == 0
@@ -91,20 +125,37 @@
         def own_slice(matrix):
             return lax.dynamic_slice_in_dim(matrix, my_index * own_count, own_count, 0)
 
-        first_sum = product(factor_panel[0], solved_before)
-        first_sum, inverse_pieces = lax.optimization_barrier((first_sum, inverse_pieces))
-        inverse_full = jnp.concatenate(list(inverse_pieces), axis=2)
-        panel_sum = product(factor_panel[1], solved_before)
-        if power_of_two and n >= 4:
-            first_remains, panel_sum = reduce_then_gather(first_sum, right_side[0], "blk", n, panel_sum)
+        rows = factor_panel.shape[1]
+        split = power_of_two and n >= 4
+        if split:
+            core = my_index & 1
+
+            def rows_half(matrix, which):
+                return lax.dynamic_slice_in_dim(matrix, which * (rows // 2), rows // 2, 0)
+
+            stacked_panel = factor_panel.reshape(2 * rows, -1)
+            first_send = product(rows_half(stacked_panel, 1 - core), solved_before)
+            first_keep = product(rows_half(stacked_panel, core), solved_before)
+        else:
+            first_sum = product(factor_panel[0], solved_before)
+            first_sum, inverse_pieces = lax.optimization_barrier((first_sum, inverse_pieces))
+            panel_sum = product(factor_panel[1], solved_before)
+        if split:
+            first_remains, (panel_sum, inverse_pieces) = halves_reduce_then_gather(
+                first_keep, first_send, right_side[0], "blk", n, (solved_before, inverse_pieces),
+                lambda held: (product(factor_panel[1], held[0]), held[1]),
+            )
         else:
             first_part, panel_sum = sum_scatter(first_sum, panel_sum)
             first_remains = gather(own_slice(right_side[0]) - first_part)
+        inverse_full = jnp.concatenate(list(inverse_pieces), axis=2)
         first_block = product(inverse_full[0], first_remains)
-        second_sum = panel_sum + product(coupling, first_block)
-        if power_of_two and n >= 4:
-            second_remains, _ = reduce_then_gather(second_sum, right_side[1], "blk", n)
+        if split:
+            second_send = rows_half(panel_sum, 1 - core) + product(rows_half(coupling, 1 - core), first_block)
+            second_keep = rows_half(panel_sum, core) + product(rows_half(coupling, core), first_block)
+            second_remains, _ = halves_reduce_then_gather(second_keep, second_send, right_side[1], "blk", n)
         else:
+            second_sum = panel_sum + product(coupling, first_block)
             second_part, _ = sum_scatter(second_sum)
             second_remains = gather(own_slice(right_side[1]) - second_part)
         second_block = product(inverse_full[1], second_remains)

time: 92.1 us -> 92 us (level)
  matrix products: 12.8 us -> 17.2 us
  waiting for transfers between devices: 49.9 us -> 47 us
  starting transfers between devices: 19 us -> 18 us
    dot_general x5 -> x7, matrix products: 12.8 us -> 17.2 us  [product(): jnp.dot(left, right, precision=lax.Precision.HIGHEST, preferred_element_t...]
    another operation x12 -> x0, other arithmetic: 3.4 us -> none  [reduce_then_gather(): y = jnp.stack([low, high], k - 1 - j)]
    select_n x0 -> x6, other arithmetic: none -> 2.25 us  [halves_reduce_then_gather(): low = jnp.where(mine == 0, y, got)]
    ppermute x14, waiting for transfers between devices: 48.5 us -> 47 us  [the longest x6 22.8 us: halves_reduce_then_gather(): got = lax.ppermute(y, axis, [(i, i ^ 1 << j) for i in range(n)])]
    ppermute x1, waiting for transfers between devices: 1.31 us -> 0.01 us  [doubling_gather(): got = lax.ppermute(y, axis, [(i, i ^ 1 << j) for i in range(n)])]
    ppermute x14, starting transfers between devices: 16.1 us -> 15.1 us  [the longest x4 5.55 us: halves_reduce_then_gather(): got = lax.ppermute(send, axis, [(i, i ^ 1 << j) for i in range(n)])]
  transfers between devices with their start and end apart: 15 -> 15, of which waited for: 15 -> 13; matrix products, arithmetic and copies ran while one was open for 15% -> 19% of each run, Pallas kernels for 0% -> 0%
where the time goes in v7:
time: 92 us; the launch traced here: 91.7 us
  waiting for transfers between devices  47 us (51%)
  starting transfers between devices  18 us (20%)
  matrix products  17.2 us (19%)
  other arithmetic  6.02 us (7%)
  local copies, waits for them, and re-layouts  3.14 us (3%)
    ppermute x6, waiting for transfers between devices, halves_reduce_then_gather(): got = lax.ppermute(y, axis, [(i, i ^ 1 << j) for i in range(n)])  22.8 us
    dot_general x7, matrix products, product(): jnp.dot(left, right, precision=lax.Precision.HIGHEST, preferred_element_t...  17.2 us
    ppermute x4, waiting for transfers between devices, halves_reduce_then_gather(): got = lax.ppermute(send, axis, [(i, i ^ 1 << j) for i in range(n)])  16.6 us
    ppermute x2, waiting for transfers between devices, halves_reduce_then_gather(): y = y + lax.ppermute(y, axis, [(i, i ^ 1 << top) for i in range(n)])  7.41 us
    ppermute x4, starting transfers between devices, halves_reduce_then_gather(): got = lax.ppermute(send, axis, [(i, i ^ 1 << j) for i in range(n)])  5.55 us
    ppermute x2, starting transfers between devices, halves_reduce_then_gather(): y = y + lax.ppermute(y, axis, [(i, i ^ 1 << top) for i in range(n)])  4.92 us
    ppermute x6, starting transfers between devices, halves_reduce_then_gather(): got = lax.ppermute(y, axis, [(i, i ^ 1 << j) for i in range(n)])  4.42 us
    slice x1, local copies, waits for them, and re-layouts, shards(): right_side[1]  3.01 us
  transfers between devices with their start and end apart: 15, of which 13 were waited for; matrix products, arithmetic and copies ran while one was open for 19% of the time, Pallas kernels for 0%

profile of v7, /device:TPU:0, one launch (start us, length us, event | category | flops | bytes accessed | tf_op | source)
XLA Modules:
  0.0 91.7 jit_solution(1598238703288900735)
XLA Ops:
  0.0 2.9 %collective-permute-start.1 = (f32[1,1,2,64,512]{4,3,2,1,0:T(8,128)}, f32[1,1,2,64,512]{4,3,2,1,0:T(8,128)S(1)}, u32[]{:S(2)}, u32[]{:S(2)}) collective-permute-start(f32[1,1,2,64,512]{4,3,2,1,0:T(8,128)} %bitcast.42), channel_id=1, source_target_pairs={{0,1},{1,0},{2,3},{3,2},{4,5},{5,4},{6,7},{7,6},{8,9},{9,8},{10,11... | collective-permute-start | bytes 786440 | tf_op jit(solution)/shard_map/ppermute | solution.py:34
  2.9 4.2 %fusion.3 = f32[512,256]{1,0:T(8,128)} fusion(f32[1024,256]{1,0:T(8,128)S(1)} %copy-done, f32[2048,1024]{1,0:T(8,128)} %bitcast.39, s32[]{:T(128)S(6)} %select_n.115), kind=kOutput, calls=%fused_computation.3 | convolution fusion | flops 1610612736 | bytes 3670020 | tf_op jit(solution)/shard_map/dot_general | solution.py:8
  7.2 3.4 %fusion.5 = f32[512,256]{1,0:T(8,128)S(1)} fusion(f32[1024,256]{1,0:T(8,128)S(1)} %copy-done, f32[2048,1024]{1,0:T(8,128)} %bitcast.40, s32[]{:T(128)S(6)} %select_n.114), kind=kOutput, calls=%fused_computation.5 | convolution fusion | flops 1610612736 | bytes 3670020 | tf_op jit(solution)/shard_map/dot_general | solution.py:8
  10.8 1.6 %collective-permute-start.2 = (f32[256,256]{1,0:T(8,128)S(1)}, f32[256,256]{1,0:T(8,128)S(1)}, u32[]{:S(2)}, u32[]{:S(2)}) collective-permute-start(f32[256,256]{1,0:T(8,128)S(1)} %constant_dynamic-slice_fusion.3), channel_id=1, source_target_pairs={{0,4},{2,6},{4,0},{6,2},{8,12},{10,14},{12,8},{14,10},{16,20},{18,... | collective-permute-start | bytes 786440 | tf_op jit(solution)/shard_map/ppermute | solution.py:87
  12.4 5.3 %fusion.7 = f32[1024,256]{1,0:T(8,128)S(1)} fusion(f32[1024,256]{1,0:T(8,128)S(1)} %copy-done, f32[2,1024,1024]{2,1,0:T(8,128)} %param.5), kind=kOutput, calls=%fused_computation.7 | convolution fusion | flops 3221225472 | bytes 6291456 | tf_op jit(solution)/shard_map/dot_general | solution.py:8
  17.7 1.9 %collective-permute-done.2 = f32[256,256]{1,0:T(8,128)S(1)} collective-permute-done((f32[256,256]{1,0:T(8,128)S(1)}, f32[256,256]{1,0:T(8,128)S(1)}, u32[]{:S(2)}, u32[]{:S(2)}) %collective-permute-start.2) | collective-permute-done | bytes 262176 | tf_op jit(solution)/shard_map/ppermute | solution.py:87
  19.6 1.6 %collective-permute-start.3 = (f32[128,256]{1,0:T(8,128)S(1)}, f32[128,256]{1,0:T(8,128)S(1)}, u32[]{:S(2)}, u32[]{:S(2)}) collective-permute-start(f32[128,256]{1,0:T(8,128)S(1)} %constant_dynamic-slice_fusion.2), channel_id=1, source_target_pairs={{0,8},{2,10},{4,12},{6,14},{8,0},{10,2},{12,4},{14,6},{16,24},{18,... | collective-permute-start | bytes 393224 | tf_op jit(solution)/shard_map/ppermute | solution.py:87
  21.3 3.5 %collective-permute-done.3 = f32[128,256]{1,0:T(8,128)S(1)} collective-permute-done((f32[128,256]{1,0:T(8,128)S(1)}, f32[128,256]{1,0:T(8,128)S(1)}, u32[]{:S(2)}, u32[]{:S(2)}) %collective-permute-start.3) | collective-permute-done | bytes 131104 | tf_op jit(solution)/shard_map/ppermute | solution.py:87
  24.9 2.7 %collective-permute-start.4 = (f32[128,256]{1,0:T(8,128)S(1)}, f32[128,256]{1,0:T(8,128)S(1)}, u32[]{:S(2)}, u32[]{:S(2)}) collective-permute-start(f32[128,256]{1,0:T(8,128)S(1)} %dynamic-slice_add_fusion.5), channel_id=1, source_target_pairs={{0,16},{2,18},{4,20},{6,22},{8,24},{10,26},{12,28},{14,30},{16,0},... | collective-permute-start | bytes 393224 | tf_op jit(solution)/shard_map/ppermute | solution.py:92
  27.5 3.0 %fusion.37 = (f32[1,1024,256]{2,1,0:T(8,128)}, f32[1,1024,256]{2,1,0:T(8,128)}) fusion(f32[2,1024,256]{2,1,0:T(8,128)} %param.7), kind=kLoop, calls=%fused_computation.67 | loop fusion | bytes 4194304 | tf_op jit(solution)/shard_map/slice | solution.py:156
  30.5 2.3 %collective-permute-done.4 = f32[128,256]{1,0:T(8,128)S(1)} collective-permute-done((f32[128,256]{1,0:T(8,128)S(1)}, f32[128,256]{1,0:T(8,128)S(1)}, u32[]{:S(2)}, u32[]{:S(2)}) %collective-permute-start.4) | collective-permute-done | bytes 131104 | tf_op jit(solution)/shard_map/ppermute | solution.py:92
  32.9 0.9 %bitcast_subtract_fusion.1 = f32[128,256]{1,0:T(8,128)S(1)} fusion(f32[128,256]{1,0:T(8,128)S(1)} %dynamic-slice_add_fusion.5, f32[128,256]{1,0:T(8,128)S(1)} %collective-permute-done.4, f32[1,1024,256]{2,1,0:T(8,128)} %get-tuple-element.18, s32[]{:T(128)S(6)} %dynamic_slice.67), kind=kLoop, calls=%fused_computation.42 | loop fusion | flops 65536 | bytes 524292 | tf_op jit(solution)/shard_map/sub | solution.py:93
  34.5 4.3 %collective-permute-done.5 = f32[128,256]{1,0:T(8,128)S(1)} collective-permute-done((f32[128,256]{1,0:T(8,128)S(1)}, f32[128,256]{1,0:T(8,128)S(1)}, u32[]{:S(2)}, u32[]{:S(2)}) %collective-permute-start.5) | collective-permute-done | bytes 131104 | tf_op jit(solution)/shard_map/ppermute | solution.py:96
  38.9 1.6 %collective-permute-start.6 = (f32[256,256]{1,0:T(8,128)S(1)}, f32[256,256]{1,0:T(8,128)}, u32[]{:S(2)}, u32[]{:S(2)}) collective-permute-start(f32[256,256]{1,0:T(8,128)S(1)} %pad_maximum_fusion.3), channel_id=1, source_target_pairs={{0,4},{2,6},{4,0},{6,2},{8,12},{10,14},{12,8},{14,10},{16,20},{18,... | collective-permute-start | bytes 786440 | tf_op jit(solution)/shard_map/ppermute | solution.py:96
  40.5 5.0 %collective-permute-done.6 = f32[256,256]{1,0:T(8,128)} collective-permute-done((f32[256,256]{1,0:T(8,128)S(1)}, f32[256,256]{1,0:T(8,128)}, u32[]{:S(2)}, u32[]{:S(2)}) %collective-permute-start.6) | collective-permute-done | bytes 262176 | tf_op jit(solution)/shard_map/ppermute | solution.py:96
  45.4 1.0 %broadcast_select_fusion.7 = (f32[256,256]{1,0:T(8,128)S(1)}, f32[256,256]{1,0:T(8,128)S(1)}) fusion(f32[256,256]{1,0:T(8,128)} %collective-permute-done.6, pred[]{:T(512)S(6)} %eq.10, f32[128,256]{1,0:T(8,128)S(1)} %get-tuple-element.34, f32[128,256]{1,0:T(8,128)S(1)} %get-tuple-element.33), kind=kLoop, calls=%fused_computation.52 | loop fusion | flops 196608 | bytes 1048577 | tf_op jit(solution)/shard_map/jit(_where)/select_n | solution.py:97
  46.4 0.8 pad_maximum_fusion
  47.3 2.2 %collective-permute-done.7 = f32[512,256]{1,0:T(8,128)} collective-permute-done((f32[512,256]{1,0:T(8,128)}, f32[512,256]{1,0:T(8,128)}, u32[]{:S(2)}, u32[]{:S(2)}) %collective-permute-start.7) | collective-permute-done | bytes 524320 | tf_op jit(solution)/shard_map/ppermute | solution.py:96
  49.5 1.1 %broadcast_select_fusion.3 = (f32[512,256]{1,0:T(8,128)S(1)}, f32[512,256]{1,0:T(8,128)S(1)}) fusion(f32[512,256]{1,0:T(8,128)} %collective-permute-done.7, pred[]{:T(512)S(6)} %eq.9, f32[256,256]{1,0:T(8,128)S(1)} %get-tuple-element.28, f32[256,256]{1,0:T(8,128)S(1)} %get-tuple-element.27), kind=kLoop, calls=%fused_computation.39 | loop fusion | flops 393216 | bytes 2097153 | tf_op jit(solution)/shard_map/jit(_where)/select_n | solution.py:97
  51.3 1.5 %dynamic-slice_add_fusion = f32[512,256]{1,0:T(8,128)S(1)} fusion(f32[1024,256]{1,0:T(8,128)S(1)} %fusion.7, s32[]{:T(128)S(6)} %select_n.136, f32[64,256]{1,0:T(8,128)S(1)} %fusion.10, f32[1024,64]{0,1:T(8,128)} %param.9), kind=kOutput, calls=%fused_computation.21 | convolution fusion | flops 100794368 | bytes 1246208 | tf_op jit(solution)/shard_map/dot_general | solution.py:8
  53.0 1.5 %dynamic-slice_add_fusion.1 = f32[512,256]{1,0:T(8,128)S(1)} fusion(f32[1024,256]{1,0:T(8,128)S(1)} %fusion.7, s32[]{:T(128)S(6)} %select_n.127, f32[64,256]{1,0:T(8,128)S(1)} %fusion.10, f32[1024,64]{0,1:T(8,128)} %param.9), kind=kOutput, calls=%fused_computation.22 | convolution fusion | flops 100794368 | bytes 1246208 | tf_op jit(solution)/shard_map/dot_general | solution.py:8
  54.9 1.6 %collective-permute-start.9 = (f32[256,256]{1,0:T(8,128)S(1)}, f32[256,256]{1,0:T(8,128)S(1)}, u32[]{:S(2)}, u32[]{:S(2)}) collective-permute-start(f32[256,256]{1,0:T(8,128)S(1)} %constant_dynamic-slice_fusion), channel_id=1, source_target_pairs={{0,4},{2,6},{4,0},{6,2},{8,12},{10,14},{12,8},{14,10},{16,20},{18,... | collective-permute-start | bytes 786440 | tf_op jit(solution)/shard_map/ppermute | solution.py:87
  56.5 6.8 %collective-permute-done.9 = f32[256,256]{1,0:T(8,128)S(1)} collective-permute-done((f32[256,256]{1,0:T(8,128)S(1)}, f32[256,256]{1,0:T(8,128)S(1)}, u32[]{:S(2)}, u32[]{:S(2)}) %collective-permute-start.9) | collective-permute-done | bytes 262176 | tf_op jit(solution)/shard_map/ppermute | solution.py:87
  63.4 0.7 collective-permute-start.10
  64.1 4.3 %collective-permute-done.10 = f32[128,256]{1,0:T(8,128)S(1)} collective-permute-done((f32[128,256]{1,0:T(8,128)S(1)}, f32[128,256]{1,0:T(8,128)S(1)}, u32[]{:S(2)}, u32[]{:S(2)}) %collective-permute-start.10) | collective-permute-done | bytes 131104 | tf_op jit(solution)/shard_map/ppermute | solution.py:87
  68.4 2.3 %collective-permute-start.11 = (f32[128,256]{1,0:T(8,128)S(1)}, f32[128,256]{1,0:T(8,128)S(1)}, u32[]{:S(2)}, u32[]{:S(2)}) collective-permute-start(f32[128,256]{1,0:T(8,128)S(1)} %dynamic-slice_add_fusion.4), channel_id=1, source_target_pairs={{0,16},{2,18},{4,20},{6,22},{8,24},{10,26},{12,28},{14,30},{16,0},... | collective-permute-start | bytes 393224 | tf_op jit(solution)/shard_map/ppermute | solution.py:92
  70.7 5.1 %collective-permute-done.11 = f32[128,256]{1,0:T(8,128)S(1)} collective-permute-done((f32[128,256]{1,0:T(8,128)S(1)}, f32[128,256]{1,0:T(8,128)S(1)}, u32[]{:S(2)}, u32[]{:S(2)}) %collective-permute-start.11) | collective-permute-done | bytes 131104 | tf_op jit(solution)/shard_map/ppermute | solution.py:92
  75.8 0.9 %bitcast_subtract_fusion = f32[128,256]{1,0:T(8,128)S(1)} fusion(f32[128,256]{1,0:T(8,128)S(1)} %dynamic-slice_add_fusion.4, f32[128,256]{1,0:T(8,128)S(1)} %collective-permute-done.11, f32[1,1024,256]{2,1,0:T(8,128)} %get-tuple-element.17, s32[]{:T(128)S(6)} %dynamic_slice.67), kind=kLoop, calls=%fused_computation.41 | loop fusion | flops 65536 | bytes 524292 | tf_op jit(solution)/shard_map/sub | solution.py:93
  77.2 4.6 %collective-permute-done.12 = f32[128,256]{1,0:T(8,128)S(1)} collective-permute-done((f32[128,256]{1,0:T(8,128)S(1)}, f32[128,256]{1,0:T(8,128)S(1)}, u32[]{:S(2)}, u32[]{:S(2)}) %collective-permute-start.12) | collective-permute-done | bytes 131104 | tf_op jit(solution)/shard_map/ppermute | solution.py:96
  81.8 1.6 %collective-permute-start.13 = (f32[256,256]{1,0:T(8,128)S(1)}, f32[256,256]{1,0:T(8,128)S(1)}, u32[]{:S(2)}, u32[]{:S(2)}) collective-permute-start(f32[256,256]{1,0:T(8,128)S(1)} %pad_maximum_fusion.4), channel_id=1, source_target_pairs={{0,4},{2,6},{4,0},{6,2},{8,12},{10,14},{12,8},{14,10},{16,20},{18,... | collective-permute-start | bytes 786440 | tf_op jit(solution)/shard_map/ppermute | solution.py:96
  83.4 4.9 %collective-permute-done.13 = f32[256,256]{1,0:T(8,128)S(1)} collective-permute-done((f32[256,256]{1,0:T(8,128)S(1)}, f32[256,256]{1,0:T(8,128)S(1)}, u32[]{:S(2)}, u32[]{:S(2)}) %collective-permute-start.13) | collective-permute-done | bytes 262176 | tf_op jit(solution)/shard_map/ppermute | solution.py:96
  88.4 1.9 %collective-permute-done.14 = f32[512,256]{1,0:T(8,128)S(1)} collective-permute-done((f32[512,256]{1,0:T(8,128)S(1)}, f32[512,256]{1,0:T(8,128)S(1)}, u32[]{:S(2)}, u32[]{:S(2)}) %collective-permute-start.14) | collective-permute-done | bytes 524320 | tf_op jit(solution)/shard_map/ppermute | solution.py:96
  (36 shorter events, 4.3 us)
Async XLA Ops:
  0.0 2.9 %copy-start = (f32[1024,256]{1,0:T(8,128)S(1)}, f32[1024,256]{1,0:T(8,128)}, u32[]{:S(2)}) copy-start(f32[1024,256]{1,0:T(8,128)} %param.6) | copy-start | bytes 3145732
  0.0 10.6 %copy-start.1 = (f32[2,64,512]{2,1,0:T(8,128)S(1)}, f32[2,64,512]{2,1,0:T(8,128)}, u32[]{:S(2)}) copy-start(f32[2,64,512]{2,1,0:T(8,128)} %param.8) | copy-start | bytes 786436
  0.0 10.6 %collective-permute-start.1 = (f32[1,1,2,64,512]{4,3,2,1,0:T(8,128)}, f32[1,1,2,64,512]{4,3,2,1,0:T(8,128)S(1)}, u32[]{:S(2)}, u32[]{:S(2)}) collective-permute-start(f32[1,1,2,64,512]{4,3,2,1,0:T(8,128)} %bitcast.42), channel_id=1, source_target_pairs={{0,1},{1,0},{2,3},{3,2},{4,5},{5,4},{6,7},{7,6},{8,9},{9,8},{10,11... | collective-permute-start | bytes 786440 | tf_op jit(solution)/shard_map/ppermute | solution.py:34
  7.1 3.5 %collective-permute-start = (f32[512,256]{1,0:T(8,128)}, f32[512,256]{1,0:T(8,128)S(1)}, u32[]{:S(2)}, u32[]{:S(2)}) collective-permute-start(f32[512,256]{1,0:T(8,128)} %fusion.3), channel_id=1, source_target_pairs={{0,2},{2,0},{4,6},{6,4},{8,10},{10,8},{12,14},{14,12},{16,18},{18,... | collective-permute-start | bytes 1572872 | tf_op jit(solution)/shard_map/ppermute | solution.py:75
  10.8 8.8 %collective-permute-start.2 = (f32[256,256]{1,0:T(8,128)S(1)}, f32[256,256]{1,0:T(8,128)S(1)}, u32[]{:S(2)}, u32[]{:S(2)}) collective-permute-start(f32[256,256]{1,0:T(8,128)S(1)} %constant_dynamic-slice_fusion.3), channel_id=1, source_target_pairs={{0,4},{2,6},{4,0},{6,2},{8,12},{10,14},{12,8},{14,10},{16,20},{18,... | collective-permute-start | bytes 786440 | tf_op jit(solution)/shard_map/ppermute | solution.py:87
  19.6 5.2 %collective-permute-start.3 = (f32[128,256]{1,0:T(8,128)S(1)}, f32[128,256]{1,0:T(8,128)S(1)}, u32[]{:S(2)}, u32[]{:S(2)}) collective-permute-start(f32[128,256]{1,0:T(8,128)S(1)} %constant_dynamic-slice_fusion.2), channel_id=1, source_target_pairs={{0,8},{2,10},{4,12},{6,14},{8,0},{10,2},{12,4},{14,6},{16,24},{18,... | collective-permute-start | bytes 393224 | tf_op jit(solution)/shard_map/ppermute | solution.py:87
  24.9 8.0 %collective-permute-start.4 = (f32[128,256]{1,0:T(8,128)S(1)}, f32[128,256]{1,0:T(8,128)S(1)}, u32[]{:S(2)}, u32[]{:S(2)}) collective-permute-start(f32[128,256]{1,0:T(8,128)S(1)} %dynamic-slice_add_fusion.5), channel_id=1, source_target_pairs={{0,16},{2,18},{4,20},{6,22},{8,24},{10,26},{12,28},{14,30},{16,0},... | collective-permute-start | bytes 393224 | tf_op jit(solution)/shard_map/ppermute | solution.py:92
  33.8 5.0 %collective-permute-start.5 = (f32[128,256]{1,0:T(8,128)S(1)}, f32[128,256]{1,0:T(8,128)S(1)}, u32[]{:S(2)}, u32[]{:S(2)}) collective-permute-start(f32[128,256]{1,0:T(8,128)S(1)} %bitcast_subtract_fusion.1), channel_id=1, source_target_pairs={{0,8},{2,10},{4,12},{6,14},{8,0},{10,2},{12,4},{14,6},{16,24},{18,... | collective-permute-start | bytes 393224 | tf_op jit(solution)/shard_map/ppermute | solution.py:96
  38.9 6.5 %collective-permute-start.6 = (f32[256,256]{1,0:T(8,128)S(1)}, f32[256,256]{1,0:T(8,128)}, u32[]{:S(2)}, u32[]{:S(2)}) collective-permute-start(f32[256,256]{1,0:T(8,128)S(1)} %pad_maximum_fusion.3), channel_id=1, source_target_pairs={{0,4},{2,6},{4,0},{6,2},{8,12},{10,14},{12,8},{14,10},{16,20},{18,... | collective-permute-start | bytes 786440 | tf_op jit(solution)/shard_map/ppermute | solution.py:96
  47.3 2.3 %collective-permute-start.7 = (f32[512,256]{1,0:T(8,128)}, f32[512,256]{1,0:T(8,128)}, u32[]{:S(2)}, u32[]{:S(2)}) collective-permute-start(f32[512,256]{1,0:T(8,128)} %pad_maximum_fusion), channel_id=1, source_target_pairs={{0,2},{2,0},{4,6},{6,4},{8,10},{10,8},{12,14},{14,12},{16,18},{18,... | collective-permute-start | bytes 1572872 | tf_op jit(solution)/shard_map/ppermute | solution.py:96
  52.8 2.0 %collective-permute-start.8 = (f32[512,256]{1,0:T(8,128)S(1)}, f32[512,256]{1,0:T(8,128)S(1)}, u32[]{:S(2)}, u32[]{:S(2)}) collective-permute-start(f32[512,256]{1,0:T(8,128)S(1)} %dynamic-slice_add_fusion), channel_id=1, source_target_pairs={{0,2},{2,0},{4,6},{6,4},{8,10},{10,8},{12,14},{14,12},{16,18},{18,... | collective-permute-start | bytes 1572872 | tf_op jit(solution)/shard_map/ppermute | solution.py:75
  54.9 8.4 %collective-permute-start.9 = (f32[256,256]{1,0:T(8,128)S(1)}, f32[256,256]{1,0:T(8,128)S(1)}, u32[]{:S(2)}, u32[]{:S(2)}) collective-permute-start(f32[256,256]{1,0:T(8,128)S(1)} %constant_dynamic-slice_fusion), channel_id=1, source_target_pairs={{0,4},{2,6},{4,0},{6,2},{8,12},{10,14},{12,8},{14,10},{16,20},{18,... | collective-permute-start | bytes 786440 | tf_op jit(solution)/shard_map/ppermute | solution.py:87
  63.4 5.0 %collective-permute-start.10 = (f32[128,256]{1,0:T(8,128)S(1)}, f32[128,256]{1,0:T(8,128)S(1)}, u32[]{:S(2)}, u32[]{:S(2)}) collective-permute-start(f32[128,256]{1,0:T(8,128)S(1)} %constant_dynamic-slice_fusion.1), channel_id=1, source_target_pairs={{0,8},{2,10},{4,12},{6,14},{8,0},{10,2},{12,4},{14,6},{16,24},{18,... | collective-permute-start | bytes 393224 | tf_op jit(solution)/shard_map/ppermute | solution.py:87
  68.4 7.3 %collective-permute-start.11 = (f32[128,256]{1,0:T(8,128)S(1)}, f32[128,256]{1,0:T(8,128)S(1)}, u32[]{:S(2)}, u32[]{:S(2)}) collective-permute-start(f32[128,256]{1,0:T(8,128)S(1)} %dynamic-slice_add_fusion.4), channel_id=1, source_target_pairs={{0,16},{2,18},{4,20},{6,22},{8,24},{10,26},{12,28},{14,30},{16,0},... | collective-permute-start | bytes 393224 | tf_op jit(solution)/shard_map/ppermute | solution.py:92
  76.7 5.0 %collective-permute-start.12 = (f32[128,256]{1,0:T(8,128)S(1)}, f32[128,256]{1,0:T(8,128)S(1)}, u32[]{:S(2)}, u32[]{:S(2)}) collective-permute-start(f32[128,256]{1,0:T(8,128)S(1)} %bitcast_subtract_fusion), channel_id=1, source_target_pairs={{0,8},{2,10},{4,12},{6,14},{8,0},{10,2},{12,4},{14,6},{16,24},{18,... | collective-permute-start | bytes 393224 | tf_op jit(solution)/shard_map/ppermute | solution.py:96
  81.8 6.4 %collective-permute-start.13 = (f32[256,256]{1,0:T(8,128)S(1)}, f32[256,256]{1,0:T(8,128)S(1)}, u32[]{:S(2)}, u32[]{:S(2)}) collective-permute-start(f32[256,256]{1,0:T(8,128)S(1)} %pad_maximum_fusion.4), channel_id=1, source_target_pairs={{0,4},{2,6},{4,0},{6,2},{8,12},{10,14},{12,8},{14,10},{16,20},{18,... | collective-permute-start | bytes 786440 | tf_op jit(solution)/shard_map/ppermute | solution.py:96
  88.3 2.0 %collective-permute-start.14 = (f32[512,256]{1,0:T(8,128)S(1)}, f32[512,256]{1,0:T(8,128)S(1)}, u32[]{:S(2)}, u32[]{:S(2)}) collective-permute-start(f32[512,256]{1,0:T(8,128)S(1)} %pad_maximum_fusion.1), channel_id=1, source_target_pairs={{0,2},{2,0},{4,6},{6,4},{8,10},{10,8},{12,14},{14,12},{16,18},{18,... | collective-permute-start | bytes 1572872 | tf_op jit(solution)/shard_map/ppermute | solution.py:96

commit v8 on v5

--- a/solution.py
+++ b/solution.py
@@ -66,6 +66,38 @@
     return y.reshape(x.shape), riders
 
 
+def reduce_then_apply(x, right, inverse_rows, axis, n, riders=None):
+    k = n.bit_length() - 1
+    me = lax.axis_index(axis)
+    half = x.shape[0]
+    y, r = x, right
+    for j in range(k - 1):
+        half //= 2
+        mine = (me >> j) & 1
+        keep = lax.dynamic_slice_in_dim(y, mine * half, half, 0)
+        send = lax.dynamic_slice_in_dim(y, (1 - mine) * half, half, 0)
+        r = lax.dynamic_slice_in_dim(r, mine * half, half, 0)
+        got = lax.ppermute(send, axis, [(i, i ^ (1 << j)) for i in range(n)])
+        if j == 1 and riders is not None:
+            got, riders = lax.optimization_barrier((got, riders))
+        y = keep + got
+    top = k - 1
+    y = y + lax.ppermute(y, axis, [(i, i ^ (1 << top)) for i in range(n)])
+    y = r - y
+    for j in reversed(range(1, k - 1)):
+        mine = (me >> j) & 1
+        got = lax.ppermute(y, axis, [(i, i ^ (1 << j)) for i in range(n)])
+        low = jnp.where(mine == 0, y, got)
+        high = jnp.where(mine == 0, got, y)
+        y = jnp.concatenate([low, high], 0)
+    mine = me & 1
+    got = lax.ppermute(y, axis, [(i, i ^ 1) for i in range(n)])
+    half = y.shape[0]
+    own_columns = lax.dynamic_slice_in_dim(inverse_rows, mine * half, half, 1)
+    other_columns = lax.dynamic_slice_in_dim(inverse_rows, (1 - mine) * half, half, 1)
+    return product(own_columns, y) + product(other_columns, got), riders
+
+
 def make_shards(n, m):
     power_of_two = n > 1 and (n & (n - 1)) == 0
     rhs_power_of_two = m > 1 and (m & (m - 1)) == 0
@@ -96,18 +128,18 @@
         inverse_full = jnp.concatenate(list(inverse_pieces), axis=2)
         panel_sum = product(factor_panel[1], solved_before)
         if power_of_two and n >= 4:
-            first_remains, panel_sum = reduce_then_gather(first_sum, right_side[0], "blk", n, panel_sum)
+            first_block, panel_sum = reduce_then_apply(first_sum, right_side[0], inverse_full[0], "blk", n, panel_sum)
         else:
             first_part, panel_sum = sum_scatter(first_sum, panel_sum)
             first_remains = gather(own_slice(right_side[0]) - first_part)
-        first_block = product(inverse_full[0], first_remains)
+            first_block = product(inverse_full[0], first_remains)
         second_sum = panel_sum + product(coupling, first_block)
         if power_of_two and n >= 4:
-            second_remains, _ = reduce_then_gather(second_sum, right_side[1], "blk", n)
+            second_block, _ = reduce_then_apply(second_sum, right_side[1], inverse_full[1], "blk", n)
         else:
             second_part, _ = sum_scatter(second_sum)
             second_remains = gather(own_slice(right_side[1]) - second_part)
-        second_block = product(inverse_full[1], second_remains)
+            second_block = product(inverse_full[1], second_remains)
         return jnp.stack([first_block, second_block])
 
     return shards

time: 92.1 us -> 93.6 us (1.016)
  matrix products: 12.8 us -> 15 us
  other arithmetic: 6.4 us -> 4.99 us
    another operation x12 -> x0, other arithmetic: 3.4 us -> none  [reduce_then_gather(): y = jnp.stack([low, high], k - 1 - j)]
    dot_general x5 -> x7, matrix products: 12.8 us -> 15 us  [product(): jnp.dot(left, right, precision=lax.Precision.HIGHEST, preferred_element_t...]
    select_n x0 -> x4, other arithmetic: none -> 1.06 us  [reduce_then_apply(): low = jnp.where(mine == 0, y, got)]
  transfers between devices with their start and end apart: 15 -> 15, of which waited for: 15 -> 15; matrix products, arithmetic and copies ran while one was open for 15% -> 14% of each run, Pallas kernels for 0% -> 0%
where the time goes in v8:
time: 93.6 us; the launch traced here: 93.3 us
  waiting for transfers between devices  50.1 us (54%)
  starting transfers between devices  18.9 us (20%)
  matrix products  15 us (16%)
  other arithmetic  4.99 us (5%)
  local copies, waits for them, and re-layouts  4.03 us (4%)
    ppermute x6, waiting for transfers between devices, reduce_then_apply(): got = lax.ppermute(send, axis, [(i, i ^ 1 << j) for i in range(n)])  19.5 us
    ppermute x4, waiting for transfers between devices, reduce_then_apply(): got = lax.ppermute(y, axis, [(i, i ^ 1 << j) for i in range(n)])  18.5 us
    dot_general x7, matrix products, product(): jnp.dot(left, right, precision=lax.Precision.HIGHEST, preferred_element_t...  15 us
    ppermute x2, waiting for transfers between devices, reduce_then_apply(): y = y + lax.ppermute(y, axis, [(i, i ^ 1 << top) for i in range(n)])  6.79 us
    ppermute x6, starting transfers between devices, reduce_then_apply(): got = lax.ppermute(send, axis, [(i, i ^ 1 << j) for i in range(n)])  6.29 us
    ppermute x2, starting transfers between devices, reduce_then_apply(): y = y + lax.ppermute(y, axis, [(i, i ^ 1 << top) for i in range(n)])  5.05 us
    ppermute x4, starting transfers between devices, reduce_then_apply(): got = lax.ppermute(y, axis, [(i, i ^ 1 << j) for i in range(n)])  4.57 us
    ppermute x2, waiting for transfers between devices, reduce_then_apply(): got = lax.ppermute(y, axis, [(i, i ^ 1) for i in range(n)])  4.08 us
  transfers between devices with their start and end apart: 15, of which 15 were waited for; matrix products, arithmetic and copies ran while one was open for 14% of the time, Pallas kernels for 0%

profile of v8, /device:TPU:0, one launch (start us, length us, event | category | flops | bytes accessed | tf_op | source)
XLA Modules:
  0.0 93.3 jit_solution(1830866021466697903)
XLA Ops:
  0.0 2.9 %collective-permute-start = (f32[1,1,2,64,512]{4,3,2,1,0:T(8,128)}, f32[1,1,2,64,512]{4,3,2,1,0:T(8,128)S(1)}, u32[]{:S(2)}, u32[]{:S(2)}) collective-permute-start(f32[1,1,2,64,512]{4,3,2,1,0:T(8,128)} %bitcast.47), channel_id=1, source_target_pairs={{0,1},{1,0},{2,3},{3,2},{4,5},{5,4},{6,7},{7,6},{8,9},{9,8},{10,11... | collective-permute-start | bytes 786440 | tf_op jit(solution)/shard_map/ppermute | solution.py:34
  2.9 5.2 %fusion.2 = f32[1024,256]{1,0:T(8,128)S(1)} fusion(f32[1024,256]{1,0:T(8,128)S(1)} %copy-done, f32[2,1024,1024]{2,1,0:T(8,128)} %param.5), kind=kOutput, calls=%fused_computation.2 | convolution fusion | flops 3221225472 | bytes 6291456 | tf_op jit(solution)/shard_map/dot_general | solution.py:8
  8.2 1.3 %collective-permute-done = f32[1,1,2,64,512]{4,3,2,1,0:T(8,128)S(1)} collective-permute-done((f32[1,1,2,64,512]{4,3,2,1,0:T(8,128)}, f32[1,1,2,64,512]{4,3,2,1,0:T(8,128)S(1)}, u32[]{:S(2)}, u32[]{:S(2)}) %collective-permute-start) | collective-permute-done | bytes 262176 | tf_op jit(solution)/shard_map/ppermute | solution.py:34
  9.6 0.8 constant_dynamic-slice_fusion.5
  10.4 2.1 %collective-permute-done.1 = f32[512,256]{1,0:T(8,128)S(1)} collective-permute-done((f32[512,256]{1,0:T(8,128)}, f32[512,256]{1,0:T(8,128)S(1)}, u32[]{:S(2)}, u32[]{:S(2)}) %collective-permute-start.1) | collective-permute-done | bytes 524320 | tf_op jit(solution)/shard_map/ppermute | solution.py:80
  12.7 1.8 %collective-permute-start.2 = (f32[256,256]{1,0:T(8,128)S(1)}, f32[256,256]{1,0:T(8,128)S(1)}, u32[]{:S(2)}, u32[]{:S(2)}) collective-permute-start(f32[256,256]{1,0:T(8,128)S(1)} %constant_dynamic-slice_fusion.4), channel_id=1, source_target_pairs={{0,4},{2,6},{4,0},{6,2},{8,12},{10,14},{12,8},{14,10},{16,20},{18,... | collective-permute-start | bytes 786440 | tf_op jit(solution)/shard_map/ppermute | solution.py:80
  14.5 5.2 %fusion = f32[1024,256]{1,0:T(8,128)S(1)} fusion(f32[1024,256]{1,0:T(8,128)S(1)} %copy-done, f32[2,1024,1024]{2,1,0:T(8,128)} %param.5), kind=kOutput, calls=%fused_computation | convolution fusion | flops 3221225472 | bytes 6291456 | tf_op jit(solution)/shard_map/dot_general | solution.py:8
  19.7 1.4 %collective-permute-done.2 = f32[256,256]{1,0:T(8,128)S(1)} collective-permute-done((f32[256,256]{1,0:T(8,128)S(1)}, f32[256,256]{1,0:T(8,128)S(1)}, u32[]{:S(2)}, u32[]{:S(2)}) %collective-permute-start.2) | collective-permute-done | bytes 262176 | tf_op jit(solution)/shard_map/ppermute | solution.py:80
  21.1 1.9 %collective-permute-start.3 = (f32[128,256]{1,0:T(8,128)S(1)}, f32[128,256]{1,0:T(8,128)S(1)}, u32[]{:S(2)}, u32[]{:S(2)}) collective-permute-start(f32[128,256]{1,0:T(8,128)S(1)} %constant_dynamic-slice_fusion.3), channel_id=1, source_target_pairs={{0,8},{2,10},{4,12},{6,14},{8,0},{10,2},{12,4},{14,6},{16,24},{18,... | collective-permute-start | bytes 393224 | tf_op jit(solution)/shard_map/ppermute | solution.py:80
  23.0 3.2 %collective-permute-done.3 = f32[128,256]{1,0:T(8,128)S(1)} collective-permute-done((f32[128,256]{1,0:T(8,128)S(1)}, f32[128,256]{1,0:T(8,128)S(1)}, u32[]{:S(2)}, u32[]{:S(2)}) %collective-permute-start.3) | collective-permute-done | bytes 131104 | tf_op jit(solution)/shard_map/ppermute | solution.py:80
  26.2 2.9 %collective-permute-start.4 = (f32[128,256]{1,0:T(8,128)S(1)}, f32[128,256]{1,0:T(8,128)S(1)}, u32[]{:S(2)}, u32[]{:S(2)}) collective-permute-start(f32[128,256]{1,0:T(8,128)S(1)} %dynamic-slice_add_fusion.5), channel_id=1, source_target_pairs={{0,16},{2,18},{4,20},{6,22},{8,24},{10,26},{12,28},{14,30},{16,0},... | collective-permute-start | bytes 393224 | tf_op jit(solution)/shard_map/ppermute | solution.py:85
  29.1 3.0 %fusion.26 = (f32[1,1024,256]{2,1,0:T(8,128)}, f32[1,1024,256]{2,1,0:T(8,128)}) fusion(f32[2,1024,256]{2,1,0:T(8,128)} %param.7), kind=kLoop, calls=%fused_computation.65 | loop fusion | bytes 4194304 | tf_op jit(solution)/shard_map/slice | solution.py:138
  32.1 1.6 %collective-permute-done.4 = f32[128,256]{1,0:T(8,128)S(1)} collective-permute-done((f32[128,256]{1,0:T(8,128)S(1)}, f32[128,256]{1,0:T(8,128)S(1)}, u32[]{:S(2)}, u32[]{:S(2)}) %collective-permute-start.4) | collective-permute-done | bytes 131104 | tf_op jit(solution)/shard_map/ppermute | solution.py:85
  33.7 0.9 %bitcast_subtract_fusion.1 = f32[128,256]{1,0:T(8,128)S(1)} fusion(f32[128,256]{1,0:T(8,128)S(1)} %dynamic-slice_add_fusion.5, f32[128,256]{1,0:T(8,128)S(1)} %collective-permute-done.4, f32[1,1024,256]{2,1,0:T(8,128)} %get-tuple-element.14, s32[]{:T(128)S(6)} %dynamic_slice.80), kind=kLoop, calls=%fused_computation.39 | loop fusion | flops 65536 | bytes 524292 | tf_op jit(solution)/shard_map/sub | solution.py:86
  35.4 4.2 %collective-permute-done.5 = f32[128,256]{1,0:T(8,128)S(1)} collective-permute-done((f32[128,256]{1,0:T(8,128)S(1)}, f32[128,256]{1,0:T(8,128)S(1)}, u32[]{:S(2)}, u32[]{:S(2)}) %collective-permute-start.5) | collective-permute-done | bytes 131104 | tf_op jit(solution)/shard_map/ppermute | solution.py:89
  39.7 1.6 %collective-permute-start.6 = (f32[256,256]{1,0:T(8,128)S(1)}, f32[256,256]{1,0:T(8,128)}, u32[]{:S(2)}, u32[]{:S(2)}) collective-permute-start(f32[256,256]{1,0:T(8,128)S(1)} %pad_maximum_fusion.2), channel_id=1, source_target_pairs={{0,4},{2,6},{4,0},{6,2},{8,12},{10,14},{12,8},{14,10},{16,20},{18,... | collective-permute-start | bytes 786440 | tf_op jit(solution)/shard_map/ppermute | solution.py:89
  41.4 4.9 %collective-permute-done.6 = f32[256,256]{1,0:T(8,128)} collective-permute-done((f32[256,256]{1,0:T(8,128)S(1)}, f32[256,256]{1,0:T(8,128)}, u32[]{:S(2)}, u32[]{:S(2)}) %collective-permute-start.6) | collective-permute-done | bytes 262176 | tf_op jit(solution)/shard_map/ppermute | solution.py:89
  46.3 1.0 %broadcast_select_fusion.3 = (f32[256,256]{1,0:T(8,128)S(1)}, f32[256,256]{1,0:T(8,128)S(1)}) fusion(f32[256,256]{1,0:T(8,128)} %collective-permute-done.6, pred[]{:T(512)S(6)} %eq.7, f32[128,256]{1,0:T(8,128)S(1)} %get-tuple-element.26, f32[128,256]{1,0:T(8,128)S(1)} %get-tuple-element.25), kind=kLoop, calls=%fused_computation.48 | loop fusion | flops 196608 | bytes 1048577 | tf_op jit(solution)/shard_map/jit(_where)/select_n | solution.py:90
  48.2 2.2 %collective-permute-done.7 = f32[512,256]{1,0:T(8,128)} collective-permute-done((f32[512,256]{1,0:T(8,128)}, f32[512,256]{1,0:T(8,128)}, u32[]{:S(2)}, u32[]{:S(2)}) %collective-permute-start.7) | collective-permute-done | bytes 524320 | tf_op jit(solution)/shard_map/ppermute | solution.py:94
  50.3 1.4 %fusion.15 = f32[64,256]{1,0:T(8,128)S(1)} fusion(f32[512,256]{1,0:T(8,128)} %collective-permute-done.7, f32[1,64,1024]{2,1,0:T(8,128)S(1)} %fusion.7, s32[]{:T(128)S(6)} %select_n.115), kind=kOutput, calls=%fused_computation.37 | convolution fusion | flops 100663296 | bytes 720900 | tf_op jit(solution)/shard_map/dot_general | solution.py:8
  52.2 2.0 %convolution_bitcast_fusion = f32[1024,256]{1,0:T(8,128)S(1)} fusion(f32[64,256]{1,0:T(8,128)S(1)} %convolution_add_fusion.1, f32[1024,64]{0,1:T(8,128)} %param.9), kind=kOutput, calls=%fused_computation.6 | convolution fusion | flops 201326592 | bytes 1376256 | tf_op jit(solution)/shard_map/dot_general | solution.py:8
  54.5 1.8 %collective-permute-done.8 = f32[512,256]{1,0:T(8,128)S(1)} collective-permute-done((f32[512,256]{1,0:T(8,128)S(1)}, f32[512,256]{1,0:T(8,128)S(1)}, u32[]{:S(2)}, u32[]{:S(2)}) %collective-permute-start.8) | collective-permute-done | bytes 524320 | tf_op jit(solution)/shard_map/ppermute | solution.py:80
  56.4 1.6 %collective-permute-start.9 = (f32[256,256]{1,0:T(8,128)S(1)}, f32[256,256]{1,0:T(8,128)S(1)}, u32[]{:S(2)}, u32[]{:S(2)}) collective-permute-start(f32[256,256]{1,0:T(8,128)S(1)} %constant_dynamic-slice_fusion.1), channel_id=1, source_target_pairs={{0,4},{2,6},{4,0},{6,2},{8,12},{10,14},{12,8},{14,10},{16,20},{18,... | collective-permute-start | bytes 786440 | tf_op jit(solution)/shard_map/ppermute | solution.py:80
  58.1 6.8 %collective-permute-done.9 = f32[256,256]{1,0:T(8,128)S(1)} collective-permute-done((f32[256,256]{1,0:T(8,128)S(1)}, f32[256,256]{1,0:T(8,128)S(1)}, u32[]{:S(2)}, u32[]{:S(2)}) %collective-permute-start.9) | collective-permute-done | bytes 262176 | tf_op jit(solution)/shard_map/ppermute | solution.py:80
  65.7 4.3 %collective-permute-done.10 = f32[128,256]{1,0:T(8,128)S(1)} collective-permute-done((f32[128,256]{1,0:T(8,128)S(1)}, f32[128,256]{1,0:T(8,128)S(1)}, u32[]{:S(2)}, u32[]{:S(2)}) %collective-permute-start.10) | collective-permute-done | bytes 131104 | tf_op jit(solution)/shard_map/ppermute | solution.py:80
  70.0 2.2 %collective-permute-start.11 = (f32[128,256]{1,0:T(8,128)S(1)}, f32[128,256]{1,0:T(8,128)S(1)}, u32[]{:S(2)}, u32[]{:S(2)}) collective-permute-start(f32[128,256]{1,0:T(8,128)S(1)} %dynamic-slice_add_fusion.4), channel_id=1, source_target_pairs={{0,16},{2,18},{4,20},{6,22},{8,24},{10,26},{12,28},{14,30},{16,0},... | collective-permute-start | bytes 393224 | tf_op jit(solution)/shard_map/ppermute | solution.py:85
  72.1 5.2 %collective-permute-done.11 = f32[128,256]{1,0:T(8,128)S(1)} collective-permute-done((f32[128,256]{1,0:T(8,128)S(1)}, f32[128,256]{1,0:T(8,128)S(1)}, u32[]{:S(2)}, u32[]{:S(2)}) %collective-permute-start.11) | collective-permute-done | bytes 131104 | tf_op jit(solution)/shard_map/ppermute | solution.py:85
  77.3 0.9 %bitcast_subtract_fusion = f32[128,256]{1,0:T(8,128)S(1)} fusion(f32[128,256]{1,0:T(8,128)S(1)} %dynamic-slice_add_fusion.4, f32[128,256]{1,0:T(8,128)S(1)} %collective-permute-done.11, f32[1,1024,256]{2,1,0:T(8,128)} %get-tuple-element.13, s32[]{:T(128)S(6)} %dynamic_slice.80), kind=kLoop, calls=%fused_computation.36 | loop fusion | flops 65536 | bytes 524292 | tf_op jit(solution)/shard_map/sub | solution.py:86
  78.7 4.5 %collective-permute-done.12 = f32[128,256]{1,0:T(8,128)S(1)} collective-permute-done((f32[128,256]{1,0:T(8,128)S(1)}, f32[128,256]{1,0:T(8,128)S(1)}, u32[]{:S(2)}, u32[]{:S(2)}) %collective-permute-start.12) | collective-permute-done | bytes 131104 | tf_op jit(solution)/shard_map/ppermute | solution.py:89
  83.3 1.6 %collective-permute-start.13 = (f32[256,256]{1,0:T(8,128)S(1)}, f32[256,256]{1,0:T(8,128)S(1)}, u32[]{:S(2)}, u32[]{:S(2)}) collective-permute-start(f32[256,256]{1,0:T(8,128)S(1)} %pad_maximum_fusion.3), channel_id=1, source_target_pairs={{0,4},{2,6},{4,0},{6,2},{8,12},{10,14},{12,8},{14,10},{16,20},{18,... | collective-permute-start | bytes 786440 | tf_op jit(solution)/shard_map/ppermute | solution.py:89
  85.0 4.8 %collective-permute-done.13 = f32[256,256]{1,0:T(8,128)S(1)} collective-permute-done((f32[256,256]{1,0:T(8,128)S(1)}, f32[256,256]{1,0:T(8,128)S(1)}, u32[]{:S(2)}, u32[]{:S(2)}) %collective-permute-start.13) | collective-permute-done | bytes 262176 | tf_op jit(solution)/shard_map/ppermute | solution.py:89
  89.9 1.9 %collective-permute-done.14 = f32[512,256]{1,0:T(8,128)S(1)} collective-permute-done((f32[512,256]{1,0:T(8,128)S(1)}, f32[512,256]{1,0:T(8,128)S(1)}, u32[]{:S(2)}, u32[]{:S(2)}) %collective-permute-start.14) | collective-permute-done | bytes 524320 | tf_op jit(solution)/shard_map/ppermute | solution.py:94
  (38 shorter events, 5.9 us)
Async XLA Ops:
  0.0 2.9 %copy-start = (f32[1024,256]{1,0:T(8,128)S(1)}, f32[1024,256]{1,0:T(8,128)}, u32[]{:S(2)}) copy-start(f32[1024,256]{1,0:T(8,128)} %param.6) | copy-start | bytes 3145732
  0.0 9.5 %copy-start.1 = (f32[2,64,512]{2,1,0:T(8,128)S(1)}, f32[2,64,512]{2,1,0:T(8,128)}, u32[]{:S(2)}) copy-start(f32[2,64,512]{2,1,0:T(8,128)} %param.8) | copy-start | bytes 786436
  0.0 9.5 %collective-permute-start = (f32[1,1,2,64,512]{4,3,2,1,0:T(8,128)}, f32[1,1,2,64,512]{4,3,2,1,0:T(8,128)S(1)}, u32[]{:S(2)}, u32[]{:S(2)}) collective-permute-start(f32[1,1,2,64,512]{4,3,2,1,0:T(8,128)} %bitcast.47), channel_id=1, source_target_pairs={{0,1},{1,0},{2,3},{3,2},{4,5},{5,4},{6,7},{7,6},{8,9},{9,8},{10,11... | collective-permute-start | bytes 786440 | tf_op jit(solution)/shard_map/ppermute | solution.py:34
  10.4 2.1 %collective-permute-start.1 = (f32[512,256]{1,0:T(8,128)}, f32[512,256]{1,0:T(8,128)S(1)}, u32[]{:S(2)}, u32[]{:S(2)}) collective-permute-start(f32[512,256]{1,0:T(8,128)} %constant_dynamic-slice_fusion.5), channel_id=1, source_target_pairs={{0,2},{2,0},{4,6},{6,4},{8,10},{10,8},{12,14},{14,12},{16,18},{18,... | collective-permute-start | bytes 1572872 | tf_op jit(solution)/shard_map/ppermute | solution.py:80
  12.7 8.4 %collective-permute-start.2 = (f32[256,256]{1,0:T(8,128)S(1)}, f32[256,256]{1,0:T(8,128)S(1)}, u32[]{:S(2)}, u32[]{:S(2)}) collective-permute-start(f32[256,256]{1,0:T(8,128)S(1)} %constant_dynamic-slice_fusion.4), channel_id=1, source_target_pairs={{0,4},{2,6},{4,0},{6,2},{8,12},{10,14},{12,8},{14,10},{16,20},{18,... | collective-permute-start | bytes 786440 | tf_op jit(solution)/shard_map/ppermute | solution.py:80
  21.1 5.0 %collective-permute-start.3 = (f32[128,256]{1,0:T(8,128)S(1)}, f32[128,256]{1,0:T(8,128)S(1)}, u32[]{:S(2)}, u32[]{:S(2)}) collective-permute-start(f32[128,256]{1,0:T(8,128)S(1)} %constant_dynamic-slice_fusion.3), channel_id=1, source_target_pairs={{0,8},{2,10},{4,12},{6,14},{8,0},{10,2},{12,4},{14,6},{16,24},{18,... | collective-permute-start | bytes 393224 | tf_op jit(solution)/shard_map/ppermute | solution.py:80
  26.2 7.5 %collective-permute-start.4 = (f32[128,256]{1,0:T(8,128)S(1)}, f32[128,256]{1,0:T(8,128)S(1)}, u32[]{:S(2)}, u32[]{:S(2)}) collective-permute-start(f32[128,256]{1,0:T(8,128)S(1)} %dynamic-slice_add_fusion.5), channel_id=1, source_target_pairs={{0,16},{2,18},{4,20},{6,22},{8,24},{10,26},{12,28},{14,30},{16,0},... | collective-permute-start | bytes 393224 | tf_op jit(solution)/shard_map/ppermute | solution.py:85
  34.6 5.0 %collective-permute-start.5 = (f32[128,256]{1,0:T(8,128)S(1)}, f32[128,256]{1,0:T(8,128)S(1)}, u32[]{:S(2)}, u32[]{:S(2)}) collective-permute-start(f32[128,256]{1,0:T(8,128)S(1)} %bitcast_subtract_fusion.1), channel_id=1, source_target_pairs={{0,8},{2,10},{4,12},{6,14},{8,0},{10,2},{12,4},{14,6},{16,24},{18,... | collective-permute-start | bytes 393224 | tf_op jit(solution)/shard_map/ppermute | solution.py:89
  39.7 6.5 %collective-permute-start.6 = (f32[256,256]{1,0:T(8,128)S(1)}, f32[256,256]{1,0:T(8,128)}, u32[]{:S(2)}, u32[]{:S(2)}) collective-permute-start(f32[256,256]{1,0:T(8,128)S(1)} %pad_maximum_fusion.2), channel_id=1, source_target_pairs={{0,4},{2,6},{4,0},{6,2},{8,12},{10,14},{12,8},{14,10},{16,20},{18,... | collective-permute-start | bytes 786440 | tf_op jit(solution)/shard_map/ppermute | solution.py:89
  48.1 2.3 %collective-permute-start.7 = (f32[512,256]{1,0:T(8,128)}, f32[512,256]{1,0:T(8,128)}, u32[]{:S(2)}, u32[]{:S(2)}) collective-permute-start(f32[512,256]{1,0:T(8,128)} %pad_maximum_fusion), channel_id=1, source_target_pairs={{0,2},{2,0},{4,6},{6,4},{8,10},{10,8},{12,14},{14,12},{16,18},{18,... | collective-permute-start | bytes 1572872 | tf_op jit(solution)/shard_map/ppermute | solution.py:94
  54.3 2.0 %collective-permute-start.8 = (f32[512,256]{1,0:T(8,128)S(1)}, f32[512,256]{1,0:T(8,128)S(1)}, u32[]{:S(2)}, u32[]{:S(2)}) collective-permute-start(f32[512,256]{1,0:T(8,128)S(1)} %constant_dynamic-slice_fusion.2), channel_id=1, source_target_pairs={{0,2},{2,0},{4,6},{6,4},{8,10},{10,8},{12,14},{14,12},{16,18},{18,... | collective-permute-start | bytes 1572872 | tf_op jit(solution)/shard_map/ppermute | solution.py:80
  56.4 8.4 %collective-permute-start.9 = (f32[256,256]{1,0:T(8,128)S(1)}, f32[256,256]{1,0:T(8,128)S(1)}, u32[]{:S(2)}, u32[]{:S(2)}) collective-permute-start(f32[256,256]{1,0:T(8,128)S(1)} %constant_dynamic-slice_fusion.1), channel_id=1, source_target_pairs={{0,4},{2,6},{4,0},{6,2},{8,12},{10,14},{12,8},{14,10},{16,20},{18,... | collective-permute-start | bytes 786440 | tf_op jit(solution)/shard_map/ppermute | solution.py:80
  64.9 5.0 %collective-permute-start.10 = (f32[128,256]{1,0:T(8,128)S(1)}, f32[128,256]{1,0:T(8,128)S(1)}, u32[]{:S(2)}, u32[]{:S(2)}) collective-permute-start(f32[128,256]{1,0:T(8,128)S(1)} %constant_dynamic-slice_fusion), channel_id=1, source_target_pairs={{0,8},{2,10},{4,12},{6,14},{8,0},{10,2},{12,4},{14,6},{16,24},{18,... | collective-permute-start | bytes 393224 | tf_op jit(solution)/shard_map/ppermute | solution.py:80
  70.0 7.3 %collective-permute-start.11 = (f32[128,256]{1,0:T(8,128)S(1)}, f32[128,256]{1,0:T(8,128)S(1)}, u32[]{:S(2)}, u32[]{:S(2)}) collective-permute-start(f32[128,256]{1,0:T(8,128)S(1)} %dynamic-slice_add_fusion.4), channel_id=1, source_target_pairs={{0,16},{2,18},{4,20},{6,22},{8,24},{10,26},{12,28},{14,30},{16,0},... | collective-permute-start | bytes 393224 | tf_op jit(solution)/shard_map/ppermute | solution.py:85
  78.2 5.0 %collective-permute-start.12 = (f32[128,256]{1,0:T(8,128)S(1)}, f32[128,256]{1,0:T(8,128)S(1)}, u32[]{:S(2)}, u32[]{:S(2)}) collective-permute-start(f32[128,256]{1,0:T(8,128)S(1)} %bitcast_subtract_fusion), channel_id=1, source_target_pairs={{0,8},{2,10},{4,12},{6,14},{8,0},{10,2},{12,4},{14,6},{16,24},{18,... | collective-permute-start | bytes 393224 | tf_op jit(solution)/shard_map/ppermute | solution.py:89
  83.3 6.4 %collective-permute-start.13 = (f32[256,256]{1,0:T(8,128)S(1)}, f32[256,256]{1,0:T(8,128)S(1)}, u32[]{:S(2)}, u32[]{:S(2)}) collective-permute-start(f32[256,256]{1,0:T(8,128)S(1)} %pad_maximum_fusion.3), channel_id=1, source_target_pairs={{0,4},{2,6},{4,0},{6,2},{8,12},{10,14},{12,8},{14,10},{16,20},{18,... | collective-permute-start | bytes 786440 | tf_op jit(solution)/shard_map/ppermute | solution.py:89
  89.8 2.0 %collective-permute-start.14 = (f32[512,256]{1,0:T(8,128)S(1)}, f32[512,256]{1,0:T(8,128)S(1)}, u32[]{:S(2)}, u32[]{:S(2)}) collective-permute-start(f32[512,256]{1,0:T(8,128)S(1)} %pad_maximum_fusion.1), channel_id=1, source_target_pairs={{0,2},{2,0},{4,6},{6,4},{8,10},{10,8},{12,14},{14,12},{16,18},{18,... | collective-permute-start | bytes 1572872 | tf_op jit(solution)/shard_map/ppermute | solution.py:94

commit v9 on v8

--- a/solution.py
+++ b/solution.py
@@ -66,36 +66,29 @@
     return y.reshape(x.shape), riders
 
 
-def reduce_then_apply(x, right, inverse_rows, axis, n, riders=None):
-    k = n.bit_length() - 1
+def ordered_reduce_then_gather(x, right, axis, n, order, riders=None):
     me = lax.axis_index(axis)
-    half = x.shape[0]
     y, r = x, right
-    for j in range(k - 1):
-        half //= 2
+    for step, j in enumerate(order[:-1]):
+        half = y.shape[0] // 2
         mine = (me >> j) & 1
         keep = lax.dynamic_slice_in_dim(y, mine * half, half, 0)
         send = lax.dynamic_slice_in_dim(y, (1 - mine) * half, half, 0)
         r = lax.dynamic_slice_in_dim(r, mine * half, half, 0)
         got = lax.ppermute(send, axis, [(i, i ^ (1 << j)) for i in range(n)])
-        if j == 1 and riders is not None:
+        if step == 1 and riders is not None:
             got, riders = lax.optimization_barrier((got, riders))
         y = keep + got
-    top = k - 1
+    top = order[-1]
     y = y + lax.ppermute(y, axis, [(i, i ^ (1 << top)) for i in range(n)])
     y = r - y
-    for j in reversed(range(1, k - 1)):
+    for j in reversed(order[:-1]):
         mine = (me >> j) & 1
         got = lax.ppermute(y, axis, [(i, i ^ (1 << j)) for i in range(n)])
         low = jnp.where(mine == 0, y, got)
         high = jnp.where(mine == 0, got, y)
         y = jnp.concatenate([low, high], 0)
-    mine = me & 1
-    got = lax.ppermute(y, axis, [(i, i ^ 1) for i in range(n)])
-    half = y.shape[0]
-    own_columns = lax.dynamic_slice_in_dim(inverse_rows, mine * half, half, 1)
-    other_columns = lax.dynamic_slice_in_dim(inverse_rows, (1 - mine) * half, half, 1)
-    return product(own_columns, y) + product(other_columns, got), riders
+    return y, riders
 
 
 def make_shards(n, m):
@@ -128,16 +121,35 @@
         inverse_full = jnp.concatenate(list(inverse_pieces), axis=2)
         panel_sum = product(factor_panel[1], solved_before)
         if power_of_two and n >= 4:
-            first_block, panel_sum = reduce_then_apply(first_sum, right_side[0], inverse_full[0], "blk", n, panel_sum)
+            k = n.bit_length() - 1
+            orders = (list(range(k)), [0, 2, 1] + list(range(3, k)) if k >= 3 else list(range(k)))
+            width = first_sum.shape[1] // 2
+            columns = (slice(0, width), slice(width, 2 * width))
+            first_blocks = []
+            for chain, (order, cols) in enumerate(zip(orders, columns)):
+                remains, got_riders = ordered_reduce_then_gather(
+                    first_sum[:, cols], right_side[0][:, cols], "blk", n, order,
+                    (panel_sum, inverse_pieces) if chain == 0 else None,
+                )
+                if chain == 0:
+                    panel_sum, inverse_pieces = got_riders
+                first_blocks.append(remains)
+            inverse_full = jnp.concatenate(list(inverse_pieces), axis=2)
+            first_blocks = [product(inverse_full[0], remains) for remains in first_blocks]
+            second_blocks = []
+            for order, cols, block in zip(orders, columns, first_blocks):
+                remains, _ = ordered_reduce_then_gather(
+                    panel_sum[:, cols] + product(coupling, block), right_side[1][:, cols], "blk", n, order
+                )
+                second_blocks.append(product(inverse_full[1], remains))
+            first_block = jnp.concatenate(first_blocks, 1)
+            second_block = jnp.concatenate(second_blocks, 1)
         else:
+            inverse_full = jnp.concatenate(list(inverse_pieces), axis=2)
             first_part, panel_sum = sum_scatter(first_sum, panel_sum)
             first_remains = gather(own_slice(right_side[0]) - first_part)
             first_block = product(inverse_full[0], first_remains)
-        second_sum = panel_sum + product(coupling, first_block)
-        if power_of_two and n >= 4:
-            second_block, _ = reduce_then_apply(second_sum, right_side[1], inverse_full[1], "blk", n)
-        else:
-            second_part, _ = sum_scatter(second_sum)
+            second_part, _ = sum_scatter(panel_sum + product(coupling, first_block))
             second_remains = gather(own_slice(right_side[1]) - second_part)
             second_block = product(inverse_full[1], second_remains)
         return jnp.stack([first_block, second_block])

time: 93.6 us -> 81.5 us (0.87)
  waiting for transfers between devices: 50.1 us -> 29.1 us
  starting transfers between devices: 18.9 us -> 32.8 us
  other arithmetic: 4.99 us -> 2.41 us
  local copies, waits for them, and re-layouts: 4.03 us -> 2.18 us
    ppermute x14 -> x28, waiting for transfers between devices: 48.8 us -> 29.1 us  [the longest x12 14.8 us: ordered_reduce_then_gather(): got = lax.ppermute(y, axis, [(i, i ^ 1 << j) for i in range(n)])]
    ppermute x14 -> x28, starting transfers between devices: 16 us -> 29.9 us  [the longest x12 13.4 us: ordered_reduce_then_gather(): got = lax.ppermute(send, axis, [(i, i ^ 1 << j) for i in range(n)])]
    slice x1 -> x3, local copies, waits for them, and re-layouts: 3 us -> 0.21 us  [the longest x1 0.07 us: shards(): first_sum[:, cols]]
    sub x2 -> x4, other arithmetic: 1.87 us -> 0.07 us  [ordered_reduce_then_gather(): y = r - y]
    squeeze x0 -> x1, local copies, waits for them, and re-layouts: none -> 1.68 us  [shards(): right_side[1][:, cols]]
    ppermute x1, waiting for transfers between devices: 1.31 us -> 0.01 us  [doubling_gather(): got = lax.ppermute(y, axis, [(i, i ^ 1 << j) for i in range(n)])]
    another operation x1, other arithmetic: 0.04 us -> 0.99 us  [doubling_gather(): y = jnp.stack([low, high], 1).reshape((-1,) + x.shape)]
    dot_general x7 -> x8, matrix products: 15 us -> 14.2 us  [product(): jnp.dot(left, right, precision=lax.Precision.HIGHEST, preferred_element_t...]
  transfers between devices with their start and end apart: 15 -> 29, of which waited for: 15 -> 20; matrix products, arithmetic and copies ran while one was open for 14% -> 17% of each run, Pallas kernels for 0% -> 0%
where the time goes in v9:
time: 81.5 us; the launch traced here: 81.3 us
  starting transfers between devices  32.8 us (40%)
  waiting for transfers between devices  29.1 us (36%)
  matrix products  14.2 us (17%)
  other arithmetic  2.41 us (3%)
  local copies, waits for them, and re-layouts  2.18 us (3%)
    ppermute x12, waiting for transfers between devices, ordered_reduce_then_gather(): got = lax.ppermute(y, axis, [(i, i ^ 1 << j) for i in range(n)])  14.8 us
    dot_general x8, matrix products, product(): jnp.dot(left, right, precision=lax.Precision.HIGHEST, preferred_element_t...  14.2 us
    ppermute x12, starting transfers between devices, ordered_reduce_then_gather(): got = lax.ppermute(send, axis, [(i, i ^ 1 << j) for i in range(n)])  13.4 us
    ppermute x12, waiting for transfers between devices, ordered_reduce_then_gather(): got = lax.ppermute(send, axis, [(i, i ^ 1 << j) for i in range(n)])  9.21 us
    ppermute x4, starting transfers between devices, ordered_reduce_then_gather(): y = y + lax.ppermute(y, axis, [(i, i ^ 1 << top) for i in range(n)])  8.5 us
    ppermute x12, starting transfers between devices, ordered_reduce_then_gather(): got = lax.ppermute(y, axis, [(i, i ^ 1 << j) for i in range(n)])  8.01 us
    ppermute x4, waiting for transfers between devices, ordered_reduce_then_gather(): y = y + lax.ppermute(y, axis, [(i, i ^ 1 << top) for i in range(n)])  5.16 us
    ppermute x1, starting transfers between devices, doubling_gather(): got = lax.ppermute(y, axis, [(i, i ^ 1 << j) for i in range(n)])  2.94 us
  transfers between devices with their start and end apart: 29, of which 20 were waited for; matrix products, arithmetic and copies ran while one was open for 17% of the time, Pallas kernels for 0%

profile of v9, /device:TPU:0, one launch (start us, length us, event | category | flops | bytes accessed | tf_op | source)
XLA Modules:
  0.0 81.3 jit_solution(1745786172298311571)
XLA Ops:
  0.0 2.9 %collective-permute-start = (f32[1,1,2,64,512]{4,3,2,1,0:T(8,128)}, f32[1,1,2,64,512]{4,3,2,1,0:T(8,128)}, u32[]{:S(2)}, u32[]{:S(2)}) collective-permute-start(f32[1,1,2,64,512]{4,3,2,1,0:T(8,128)} %bitcast.45), channel_id=1, source_target_pairs={{0,1},{1,0},{2,3},{3,2},{4,5},{5,4},{6,7},{7,6},{8,9},{9,8},{10,11... | collective-permute-start | bytes 786440 | tf_op jit(solution)/shard_map/ppermute | solution.py:34
  2.9 5.2 %fusion.2 = f32[1024,256]{1,0:T(8,128)S(1)} fusion(f32[1024,256]{1,0:T(8,128)S(1)} %copy-done, f32[2,1024,1024]{2,1,0:T(8,128)} %param.5), kind=kOutput, calls=%fused_computation.2 | convolution fusion | flops 3221225472 | bytes 6291456 | tf_op jit(solution)/shard_map/dot_general | solution.py:8
  8.2 5.3 %fusion = f32[1024,256]{1,0:T(8,128)S(1)} fusion(f32[1024,256]{1,0:T(8,128)S(1)} %copy-done, f32[2,1024,1024]{2,1,0:T(8,128)} %param.5), kind=kOutput, calls=%fused_computation | convolution fusion | flops 3221225472 | bytes 6291456 | tf_op jit(solution)/shard_map/dot_general | solution.py:8
  13.5 1.7 %slice_bitcast_fusion = (f32[1024,256]{1,0:T(8,128)S(1)}, f32[1024,256]{1,0:T(8,128)S(1)}) fusion(f32[2,1024,256]{2,1,0:T(8,128)} %param.7), kind=kLoop, calls=%fused_computation.8 | loop fusion | bytes 4194304 | tf_op jit(solution)/shard_map/squeeze | solution.py:142
  18.0 1.6 %collective-permute-start.9 = (f32[256,128]{1,0:T(8,128)S(1)}, f32[256,128]{1,0:T(8,128)S(1)}, u32[]{:S(2)}, u32[]{:S(2)}) collective-permute-start(f32[256,128]{1,0:T(8,128)S(1)} %constant_dynamic-slice_fusion.7), channel_id=1, source_target_pairs={{0,8},{2,10},{4,12},{6,14},{8,0},{10,2},{12,4},{14,6},{16,24},{18,... | collective-permute-start | bytes 393224 | tf_op jit(solution)/shard_map/ppermute | solution.py:78
  19.8 1.6 %collective-permute-start.2 = (f32[256,128]{1,0:T(8,128)S(1)}, f32[256,128]{1,0:T(8,128)S(1)}, u32[]{:S(2)}, u32[]{:S(2)}) collective-permute-start(f32[256,128]{1,0:T(8,128)S(1)} %constant_dynamic-slice_fusion.10), channel_id=1, source_target_pairs={{0,4},{2,6},{4,0},{6,2},{8,12},{10,14},{12,8},{14,10},{16,20},{18,... | collective-permute-start | bytes 393224 | tf_op jit(solution)/shard_map/ppermute | solution.py:78
  21.3 2.3 %collective-permute-done.9 = f32[256,128]{1,0:T(8,128)S(1)} collective-permute-done((f32[256,128]{1,0:T(8,128)S(1)}, f32[256,128]{1,0:T(8,128)S(1)}, u32[]{:S(2)}, u32[]{:S(2)}) %collective-permute-start.9) | collective-permute-done | bytes 131104 | tf_op jit(solution)/shard_map/ppermute | solution.py:78
  23.7 1.6 %collective-permute-start.10 = (f32[128,128]{1,0:T(8,128)S(1)}, f32[128,128]{1,0:T(8,128)S(1)}, u32[]{:S(2)}, u32[]{:S(2)}) collective-permute-start(f32[128,128]{1,0:T(8,128)S(1)} %constant_dynamic-slice_fusion.6), channel_id=1, source_target_pairs={{0,4},{2,6},{4,0},{6,2},{8,12},{10,14},{12,8},{14,10},{16,20},{18,... | collective-permute-start | bytes 196616 | tf_op jit(solution)/shard_map/ppermute | solution.py:78
  25.4 1.6 %collective-permute-start.3 = (f32[128,128]{1,0:T(8,128)S(1)}, f32[128,128]{1,0:T(8,128)S(1)}, u32[]{:S(2)}, u32[]{:S(2)}) collective-permute-start(f32[128,128]{1,0:T(8,128)S(1)} %constant_dynamic-slice_fusion.9), channel_id=1, source_target_pairs={{0,8},{2,10},{4,12},{6,14},{8,0},{10,2},{12,4},{14,6},{16,24},{18,... | collective-permute-start | bytes 196616 | tf_op jit(solution)/shard_map/ppermute | solution.py:78
  28.0 2.7 %collective-permute-start.11 = (f32[128,128]{1,0:T(8,128)S(1)}, f32[128,128]{1,0:T(8,128)S(1)}, u32[]{:S(2)}, u32[]{:S(2)}) collective-permute-start(f32[128,128]{1,0:T(8,128)S(1)} %dynamic-slice_add_fusion.10), channel_id=1, source_target_pairs={{0,16},{2,18},{4,20},{6,22},{8,24},{10,26},{12,28},{14,30},{16,0},... | collective-permute-start | bytes 196616 | tf_op jit(solution)/shard_map/ppermute | solution.py:83
  30.7 2.1 %collective-permute-start.4 = (f32[128,128]{1,0:T(8,128)S(1)}, f32[128,128]{1,0:T(8,128)S(1)}, u32[]{:S(2)}, u32[]{:S(2)}) collective-permute-start(f32[128,128]{1,0:T(8,128)S(1)} %dynamic-slice_add_fusion.11), channel_id=1, source_target_pairs={{0,16},{2,18},{4,20},{6,22},{8,24},{10,26},{12,28},{14,30},{16,0},... | collective-permute-start | bytes 196616 | tf_op jit(solution)/shard_map/ppermute | solution.py:83
  32.8 2.1 %collective-permute-done.11 = f32[128,128]{1,0:T(8,128)S(1)} collective-permute-done((f32[128,128]{1,0:T(8,128)S(1)}, f32[128,128]{1,0:T(8,128)S(1)}, u32[]{:S(2)}, u32[]{:S(2)}) %collective-permute-start.11) | collective-permute-done | bytes 65568 | tf_op jit(solution)/shard_map/ppermute | solution.py:83
  35.0 1.6 %collective-permute-start.12 = (f32[128,128]{1,0:T(8,128)S(1)}, f32[128,128]{1,0:T(8,128)S(1)}, u32[]{:S(2)}, u32[]{:S(2)}) collective-permute-start(f32[128,128]{1,0:T(8,128)S(1)} %add_subtract_fusion.2), channel_id=1, source_target_pairs={{0,4},{2,6},{4,0},{6,2},{8,12},{10,14},{12,8},{14,10},{16,20},{18,... | collective-permute-start | bytes 196616 | tf_op jit(solution)/shard_map/ppermute | solution.py:87
  36.6 1.0 %collective-permute-start.5 = (f32[128,128]{1,0:T(8,128)S(1)}, f32[128,128]{1,0:T(8,128)S(1)}, u32[]{:S(2)}, u32[]{:S(2)}) collective-permute-start(f32[128,128]{1,0:T(8,128)S(1)} %add_subtract_fusion.3), channel_id=1, source_target_pairs={{0,8},{2,10},{4,12},{6,14},{8,0},{10,2},{12,4},{14,6},{16,24},{18,... | collective-permute-start | bytes 196616 | tf_op jit(solution)/shard_map/ppermute | solution.py:87
  37.6 1.8 %collective-permute-done.12 = f32[128,128]{1,0:T(8,128)S(1)} collective-permute-done((f32[128,128]{1,0:T(8,128)S(1)}, f32[128,128]{1,0:T(8,128)S(1)}, u32[]{:S(2)}, u32[]{:S(2)}) %collective-permute-start.12) | collective-permute-done | bytes 65568 | tf_op jit(solution)/shard_map/ppermute | solution.py:87
  39.7 1.2 %collective-permute-done.5 = f32[128,128]{1,0:T(8,128)S(1)} collective-permute-done((f32[128,128]{1,0:T(8,128)S(1)}, f32[128,128]{1,0:T(8,128)S(1)}, u32[]{:S(2)}, u32[]{:S(2)}) %collective-permute-start.5) | collective-permute-done | bytes 65568 | tf_op jit(solution)/shard_map/ppermute | solution.py:87
  41.9 2.6 %collective-permute-done.13 = f32[256,128]{1,0:T(8,128)S(1)} collective-permute-done((f32[256,128]{1,0:T(8,128)S(1)}, f32[256,128]{1,0:T(8,128)S(1)}, u32[]{:S(2)}, u32[]{:S(2)}) %collective-permute-start.13) | collective-permute-done | bytes 131104 | tf_op jit(solution)/shard_map/ppermute | solution.py:87
  44.6 1.4 %collective-permute-done.6 = f32[256,128]{1,0:T(8,128)S(1)} collective-permute-done((f32[256,128]{1,0:T(8,128)S(1)}, f32[256,128]{1,0:T(8,128)S(1)}, u32[]{:S(2)}, u32[]{:S(2)}) %collective-permute-start.6) | collective-permute-done | bytes 131104 | tf_op jit(solution)/shard_map/ppermute | solution.py:87
  46.6 1.0 %collective-permute-done.7 = f32[512,128]{1,0:T(8,128)S(1)} collective-permute-done((f32[512,128]{1,0:T(8,128)S(1)}, f32[512,128]{1,0:T(8,128)S(1)}, u32[]{:S(2)}, u32[]{:S(2)}) %collective-permute-start.7) | collective-permute-done | bytes 262176 | tf_op jit(solution)/shard_map/ppermute | solution.py:87
  51.8 1.0 %collective-permute-start.23 = (f32[256,128]{1,0:T(8,128)S(1)}, f32[256,128]{1,0:T(8,128)S(1)}, u32[]{:S(2)}, u32[]{:S(2)}) collective-permute-start(f32[256,128]{1,0:T(8,128)S(1)} %constant_dynamic-slice_fusion.1), channel_id=1, source_target_pairs={{0,8},{2,10},{4,12},{6,14},{8,0},{10,2},{12,4},{14,6},{16,24},{18,... | collective-permute-start | bytes 393224 | tf_op jit(solution)/shard_map/ppermute | solution.py:78
  52.9 1.8 %collective-permute-start.16 = (f32[256,128]{1,0:T(8,128)S(1)}, f32[256,128]{1,0:T(8,128)S(1)}, u32[]{:S(2)}, u32[]{:S(2)}) collective-permute-start(f32[256,128]{1,0:T(8,128)S(1)} %constant_dynamic-slice_fusion.4), channel_id=1, source_target_pairs={{0,4},{2,6},{4,0},{6,2},{8,12},{10,14},{12,8},{14,10},{16,20},{18,... | collective-permute-start | bytes 393224 | tf_op jit(solution)/shard_map/ppermute | solution.py:78
  54.7 2.7 %collective-permute-done.23 = f32[256,128]{1,0:T(8,128)S(1)} collective-permute-done((f32[256,128]{1,0:T(8,128)S(1)}, f32[256,128]{1,0:T(8,128)S(1)}, u32[]{:S(2)}, u32[]{:S(2)}) %collective-permute-start.23) | collective-permute-done | bytes 131104 | tf_op jit(solution)/shard_map/ppermute | solution.py:78
  57.5 1.0 %collective-permute-start.24 = (f32[128,128]{1,0:T(8,128)S(1)}, f32[128,128]{1,0:T(8,128)S(1)}, u32[]{:S(2)}, u32[]{:S(2)}) collective-permute-start(f32[128,128]{1,0:T(8,128)S(1)} %constant_dynamic-slice_fusion), channel_id=1, source_target_pairs={{0,4},{2,6},{4,0},{6,2},{8,12},{10,14},{12,8},{14,10},{16,20},{18,... | collective-permute-start | bytes 196616 | tf_op jit(solution)/shard_map/ppermute | solution.py:78
  58.6 1.8 %collective-permute-start.17 = (f32[128,128]{1,0:T(8,128)S(1)}, f32[128,128]{1,0:T(8,128)S(1)}, u32[]{:S(2)}, u32[]{:S(2)}) collective-permute-start(f32[128,128]{1,0:T(8,128)S(1)} %constant_dynamic-slice_fusion.3), channel_id=1, source_target_pairs={{0,8},{2,10},{4,12},{6,14},{8,0},{10,2},{12,4},{14,6},{16,24},{18,... | collective-permute-start | bytes 196616 | tf_op jit(solution)/shard_map/ppermute | solution.py:78
  60.4 1.5 %collective-permute-done.24 = f32[128,128]{1,0:T(8,128)S(1)} collective-permute-done((f32[128,128]{1,0:T(8,128)S(1)}, f32[128,128]{1,0:T(8,128)S(1)}, u32[]{:S(2)}, u32[]{:S(2)}) %collective-permute-start.24) | collective-permute-done | bytes 65568 | tf_op jit(solution)/shard_map/ppermute | solution.py:78
  61.8 1.9 %collective-permute-start.25 = (f32[128,128]{1,0:T(8,128)S(1)}, f32[128,128]{1,0:T(8,128)S(1)}, u32[]{:S(2)}, u32[]{:S(2)}) collective-permute-start(f32[128,128]{1,0:T(8,128)S(1)} %dynamic-slice_add_fusion.8), channel_id=1, source_target_pairs={{0,16},{2,18},{4,20},{6,22},{8,24},{10,26},{12,28},{14,30},{16,0},... | collective-permute-start | bytes 196616 | tf_op jit(solution)/shard_map/ppermute | solution.py:83
  63.8 1.8 %collective-permute-start.18 = (f32[128,128]{1,0:T(8,128)S(1)}, f32[128,128]{1,0:T(8,128)S(1)}, u32[]{:S(2)}, u32[]{:S(2)}) collective-permute-start(f32[128,128]{1,0:T(8,128)S(1)} %dynamic-slice_add_fusion.9), channel_id=1, source_target_pairs={{0,16},{2,18},{4,20},{6,22},{8,24},{10,26},{12,28},{14,30},{16,0},... | collective-permute-start | bytes 196616 | tf_op jit(solution)/shard_map/ppermute | solution.py:83
  65.6 2.6 %collective-permute-done.25 = f32[128,128]{1,0:T(8,128)S(1)} collective-permute-done((f32[128,128]{1,0:T(8,128)S(1)}, f32[128,128]{1,0:T(8,128)S(1)}, u32[]{:S(2)}, u32[]{:S(2)}) %collective-permute-start.25) | collective-permute-done | bytes 65568 | tf_op jit(solution)/shard_map/ppermute | solution.py:83
  69.1 1.5 %collective-permute-start.19 = (f32[128,128]{1,0:T(8,128)S(1)}, f32[128,128]{1,0:T(8,128)S(1)}, u32[]{:S(2)}, u32[]{:S(2)}) collective-permute-start(f32[128,128]{1,0:T(8,128)S(1)} %add_subtract_fusion.1), channel_id=1, source_target_pairs={{0,8},{2,10},{4,12},{6,14},{8,0},{10,2},{12,4},{14,6},{16,24},{18,... | collective-permute-start | bytes 196616 | tf_op jit(solution)/shard_map/ppermute | solution.py:87
  70.6 2.1 %collective-permute-done.26 = f32[128,128]{1,0:T(8,128)S(1)} collective-permute-done((f32[128,128]{1,0:T(8,128)S(1)}, f32[128,128]{1,0:T(8,128)S(1)}, u32[]{:S(2)}, u32[]{:S(2)}) %collective-permute-start.26) | collective-permute-done | bytes 65568 | tf_op jit(solution)/shard_map/ppermute | solution.py:87
  73.5 1.9 %collective-permute-start.20 = (f32[256,128]{1,0:T(8,128)S(1)}, f32[256,128]{1,0:T(8,128)S(1)}, u32[]{:S(2)}, u32[]{:S(2)}) collective-permute-start(f32[256,128]{1,0:T(8,128)S(1)} %pad_maximum_fusion.7), channel_id=1, source_target_pairs={{0,4},{2,6},{4,0},{6,2},{8,12},{10,14},{12,8},{14,10},{16,20},{18,... | collective-permute-start | bytes 393224 | tf_op jit(solution)/shard_map/ppermute | solution.py:87
  75.4 2.3 %collective-permute-done.27 = f32[256,128]{1,0:T(8,128)S(1)} collective-permute-done((f32[256,128]{1,0:T(8,128)S(1)}, f32[256,128]{1,0:T(8,128)S(1)}, u32[]{:S(2)}, u32[]{:S(2)}) %collective-permute-start.27) | collective-permute-done | bytes 131104 | tf_op jit(solution)/shard_map/ppermute | solution.py:87
  (97 shorter events, 15.4 us)
Async XLA Ops:
  0.0 2.9 %copy-start = (f32[1024,256]{1,0:T(8,128)S(1)}, f32[1024,256]{1,0:T(8,128)}, u32[]{:S(2)}) copy-start(f32[1024,256]{1,0:T(8,128)} %param.6) | copy-start | bytes 3145732
  0.0 15.2 %collective-permute-start = (f32[1,1,2,64,512]{4,3,2,1,0:T(8,128)}, f32[1,1,2,64,512]{4,3,2,1,0:T(8,128)}, u32[]{:S(2)}, u32[]{:S(2)}) collective-permute-start(f32[1,1,2,64,512]{4,3,2,1,0:T(8,128)} %bitcast.45), channel_id=1, source_target_pairs={{0,1},{1,0},{2,3},{3,2},{4,5},{5,4},{6,7},{7,6},{8,9},{9,8},{10,11... | collective-permute-start | bytes 786440 | tf_op jit(solution)/shard_map/ppermute | solution.py:34
  8.2 7.0 %copy-start.2 = (f32[2,64,512]{2,1,0:T(8,128)S(1)}, f32[2,64,512]{2,1,0:T(8,128)}, u32[]{:S(2)}) copy-start(f32[2,64,512]{2,1,0:T(8,128)} %param.8) | copy-start | bytes 786436
  16.4 1.6 %collective-permute-start.8 = (f32[512,128]{1,0:T(8,128)S(1)}, f32[512,128]{1,0:T(8,128)S(1)}, u32[]{:S(2)}, u32[]{:S(2)}) collective-permute-start(f32[512,128]{1,0:T(8,128)S(1)} %constant_dynamic-slice_fusion.8), channel_id=1, source_target_pairs={{0,2},{2,0},{4,6},{6,4},{8,10},{10,8},{12,14},{14,12},{16,18},{18,... | collective-permute-start | bytes 786440 | tf_op jit(solution)/shard_map/ppermute | solution.py:78
  16.6 3.1 %collective-permute-start.1 = (f32[512,128]{1,0:T(8,128)S(1)}, f32[512,128]{1,0:T(8,128)S(1)}, u32[]{:S(2)}, u32[]{:S(2)}) collective-permute-start(f32[512,128]{1,0:T(8,128)S(1)} %constant_dynamic-slice_fusion.11), channel_id=1, source_target_pairs={{0,2},{2,0},{4,6},{6,4},{8,10},{10,8},{12,14},{14,12},{16,18},{18,... | collective-permute-start | bytes 786440 | tf_op jit(solution)/shard_map/ppermute | solution.py:78
  18.0 5.6 %collective-permute-start.9 = (f32[256,128]{1,0:T(8,128)S(1)}, f32[256,128]{1,0:T(8,128)S(1)}, u32[]{:S(2)}, u32[]{:S(2)}) collective-permute-start(f32[256,128]{1,0:T(8,128)S(1)} %constant_dynamic-slice_fusion.7), channel_id=1, source_target_pairs={{0,8},{2,10},{4,12},{6,14},{8,0},{10,2},{12,4},{14,6},{16,24},{18,... | collective-permute-start | bytes 393224 | tf_op jit(solution)/shard_map/ppermute | solution.py:78
  19.8 5.5 %collective-permute-start.2 = (f32[256,128]{1,0:T(8,128)S(1)}, f32[256,128]{1,0:T(8,128)S(1)}, u32[]{:S(2)}, u32[]{:S(2)}) collective-permute-start(f32[256,128]{1,0:T(8,128)S(1)} %constant_dynamic-slice_fusion.10), channel_id=1, source_target_pairs={{0,4},{2,6},{4,0},{6,2},{8,12},{10,14},{12,8},{14,10},{16,20},{18,... | collective-permute-start | bytes 393224 | tf_op jit(solution)/shard_map/ppermute | solution.py:78
  23.7 4.3 %collective-permute-start.10 = (f32[128,128]{1,0:T(8,128)S(1)}, f32[128,128]{1,0:T(8,128)S(1)}, u32[]{:S(2)}, u32[]{:S(2)}) collective-permute-start(f32[128,128]{1,0:T(8,128)S(1)} %constant_dynamic-slice_fusion.6), channel_id=1, source_target_pairs={{0,4},{2,6},{4,0},{6,2},{8,12},{10,14},{12,8},{14,10},{16,20},{18,... | collective-permute-start | bytes 196616 | tf_op jit(solution)/shard_map/ppermute | solution.py:78
  25.4 22.8 %copy-start.1 = (f32[1024,64]{0,1:T(8,128)S(1)}, f32[1024,64]{0,1:T(8,128)}, u32[]{:S(2)}) copy-start(f32[1024,64]{0,1:T(8,128)} %param.9) | copy-start | bytes 786436
  25.4 5.3 %collective-permute-start.3 = (f32[128,128]{1,0:T(8,128)S(1)}, f32[128,128]{1,0:T(8,128)S(1)}, u32[]{:S(2)}, u32[]{:S(2)}) collective-permute-start(f32[128,128]{1,0:T(8,128)S(1)} %constant_dynamic-slice_fusion.9), channel_id=1, source_target_pairs={{0,8},{2,10},{4,12},{6,14},{8,0},{10,2},{12,4},{14,6},{16,24},{18,... | collective-permute-start | bytes 196616 | tf_op jit(solution)/shard_map/ppermute | solution.py:78
  28.0 6.9 %collective-permute-start.11 = (f32[128,128]{1,0:T(8,128)S(1)}, f32[128,128]{1,0:T(8,128)S(1)}, u32[]{:S(2)}, u32[]{:S(2)}) collective-permute-start(f32[128,128]{1,0:T(8,128)S(1)} %dynamic-slice_add_fusion.10), channel_id=1, source_target_pairs={{0,16},{2,18},{4,20},{6,22},{8,24},{10,26},{12,28},{14,30},{16,0},... | collective-permute-start | bytes 196616 | tf_op jit(solution)/shard_map/ppermute | solution.py:83
  30.7 5.8 %collective-permute-start.4 = (f32[128,128]{1,0:T(8,128)S(1)}, f32[128,128]{1,0:T(8,128)S(1)}, u32[]{:S(2)}, u32[]{:S(2)}) collective-permute-start(f32[128,128]{1,0:T(8,128)S(1)} %dynamic-slice_add_fusion.11), channel_id=1, source_target_pairs={{0,16},{2,18},{4,20},{6,22},{8,24},{10,26},{12,28},{14,30},{16,0},... | collective-permute-start | bytes 196616 | tf_op jit(solution)/shard_map/ppermute | solution.py:83
  35.0 4.4 %collective-permute-start.12 = (f32[128,128]{1,0:T(8,128)S(1)}, f32[128,128]{1,0:T(8,128)S(1)}, u32[]{:S(2)}, u32[]{:S(2)}) collective-permute-start(f32[128,128]{1,0:T(8,128)S(1)} %add_subtract_fusion.2), channel_id=1, source_target_pairs={{0,4},{2,6},{4,0},{6,2},{8,12},{10,14},{12,8},{14,10},{16,20},{18,... | collective-permute-start | bytes 196616 | tf_op jit(solution)/shard_map/ppermute | solution.py:87
  36.6 4.3 %collective-permute-start.5 = (f32[128,128]{1,0:T(8,128)S(1)}, f32[128,128]{1,0:T(8,128)S(1)}, u32[]{:S(2)}, u32[]{:S(2)}) collective-permute-start(f32[128,128]{1,0:T(8,128)S(1)} %add_subtract_fusion.3), channel_id=1, source_target_pairs={{0,8},{2,10},{4,12},{6,14},{8,0},{10,2},{12,4},{14,6},{16,24},{18,... | collective-permute-start | bytes 196616 | tf_op jit(solution)/shard_map/ppermute | solution.py:87
  39.4 5.0 %collective-permute-start.13 = (f32[256,128]{1,0:T(8,128)S(1)}, f32[256,128]{1,0:T(8,128)S(1)}, u32[]{:S(2)}, u32[]{:S(2)}) collective-permute-start(f32[256,128]{1,0:T(8,128)S(1)} %pad_maximum_fusion.6), channel_id=1, source_target_pairs={{0,8},{2,10},{4,12},{6,14},{8,0},{10,2},{12,4},{14,6},{16,24},{18,... | collective-permute-start | bytes 393224 | tf_op jit(solution)/shard_map/ppermute | solution.py:87
  41.0 5.0 %collective-permute-start.6 = (f32[256,128]{1,0:T(8,128)S(1)}, f32[256,128]{1,0:T(8,128)S(1)}, u32[]{:S(2)}, u32[]{:S(2)}) collective-permute-start(f32[256,128]{1,0:T(8,128)S(1)} %pad_maximum_fusion.5), channel_id=1, source_target_pairs={{0,4},{2,6},{4,0},{6,2},{8,12},{10,14},{12,8},{14,10},{16,20},{18,... | collective-permute-start | bytes 393224 | tf_op jit(solution)/shard_map/ppermute | solution.py:87
  44.5 1.6 %collective-permute-start.14 = (f32[512,128]{1,0:T(8,128)S(1)}, f32[512,128]{1,0:T(8,128)S(1)}, u32[]{:S(2)}, u32[]{:S(2)}) collective-permute-start(f32[512,128]{1,0:T(8,128)S(1)} %pad_maximum_fusion.2), channel_id=1, source_target_pairs={{0,2},{2,0},{4,6},{6,4},{8,10},{10,8},{12,14},{14,12},{16,18},{18,... | collective-permute-start | bytes 786440 | tf_op jit(solution)/shard_map/ppermute | solution.py:87
  46.0 1.6 %collective-permute-start.7 = (f32[512,128]{1,0:T(8,128)S(1)}, f32[512,128]{1,0:T(8,128)S(1)}, u32[]{:S(2)}, u32[]{:S(2)}) collective-permute-start(f32[512,128]{1,0:T(8,128)S(1)} %pad_maximum_fusion.1), channel_id=1, source_target_pairs={{0,2},{2,0},{4,6},{6,4},{8,10},{10,8},{12,14},{14,12},{16,18},{18,... | collective-permute-start | bytes 786440 | tf_op jit(solution)/shard_map/ppermute | solution.py:87
  50.2 1.6 %collective-permute-start.22 = (f32[512,128]{1,0:T(8,128)S(1)}, f32[512,128]{1,0:T(8,128)S(1)}, u32[]{:S(2)}, u32[]{:S(2)}) collective-permute-start(f32[512,128]{1,0:T(8,128)S(1)} %constant_dynamic-slice_fusion.2), channel_id=1, source_target_pairs={{0,2},{2,0},{4,6},{6,4},{8,10},{10,8},{12,14},{14,12},{16,18},{18,... | collective-permute-start | bytes 786440 | tf_op jit(solution)/shard_map/ppermute | solution.py:78
  50.5 2.4 %collective-permute-start.15 = (f32[512,128]{1,0:T(8,128)S(1)}, f32[512,128]{1,0:T(8,128)S(1)}, u32[]{:S(2)}, u32[]{:S(2)}) collective-permute-start(f32[512,128]{1,0:T(8,128)S(1)} %constant_dynamic-slice_fusion.5), channel_id=1, source_target_pairs={{0,2},{2,0},{4,6},{6,4},{8,10},{10,8},{12,14},{14,12},{16,18},{18,... | collective-permute-start | bytes 786440 | tf_op jit(solution)/shard_map/ppermute | solution.py:78
  51.8 5.6 %collective-permute-start.23 = (f32[256,128]{1,0:T(8,128)S(1)}, f32[256,128]{1,0:T(8,128)S(1)}, u32[]{:S(2)}, u32[]{:S(2)}) collective-permute-start(f32[256,128]{1,0:T(8,128)S(1)} %constant_dynamic-slice_fusion.1), channel_id=1, source_target_pairs={{0,8},{2,10},{4,12},{6,14},{8,0},{10,2},{12,4},{14,6},{16,24},{18,... | collective-permute-start | bytes 393224 | tf_op jit(solution)/shard_map/ppermute | solution.py:78
  52.9 5.6 %collective-permute-start.16 = (f32[256,128]{1,0:T(8,128)S(1)}, f32[256,128]{1,0:T(8,128)S(1)}, u32[]{:S(2)}, u32[]{:S(2)}) collective-permute-start(f32[256,128]{1,0:T(8,128)S(1)} %constant_dynamic-slice_fusion.4), channel_id=1, source_target_pairs={{0,4},{2,6},{4,0},{6,2},{8,12},{10,14},{12,8},{14,10},{16,20},{18,... | collective-permute-start | bytes 393224 | tf_op jit(solution)/shard_map/ppermute | solution.py:78
  57.5 4.3 %collective-permute-start.24 = (f32[128,128]{1,0:T(8,128)S(1)}, f32[128,128]{1,0:T(8,128)S(1)}, u32[]{:S(2)}, u32[]{:S(2)}) collective-permute-start(f32[128,128]{1,0:T(8,128)S(1)} %constant_dynamic-slice_fusion), channel_id=1, source_target_pairs={{0,4},{2,6},{4,0},{6,2},{8,12},{10,14},{12,8},{14,10},{16,20},{18,... | collective-permute-start | bytes 196616 | tf_op jit(solution)/shard_map/ppermute | solution.py:78
  58.6 5.2 %collective-permute-start.17 = (f32[128,128]{1,0:T(8,128)S(1)}, f32[128,128]{1,0:T(8,128)S(1)}, u32[]{:S(2)}, u32[]{:S(2)}) collective-permute-start(f32[128,128]{1,0:T(8,128)S(1)} %constant_dynamic-slice_fusion.3), channel_id=1, source_target_pairs={{0,8},{2,10},{4,12},{6,14},{8,0},{10,2},{12,4},{14,6},{16,24},{18,... | collective-permute-start | bytes 196616 | tf_op jit(solution)/shard_map/ppermute | solution.py:78
  61.8 6.3 %collective-permute-start.25 = (f32[128,128]{1,0:T(8,128)S(1)}, f32[128,128]{1,0:T(8,128)S(1)}, u32[]{:S(2)}, u32[]{:S(2)}) collective-permute-start(f32[128,128]{1,0:T(8,128)S(1)} %dynamic-slice_add_fusion.8), channel_id=1, source_target_pairs={{0,16},{2,18},{4,20},{6,22},{8,24},{10,26},{12,28},{14,30},{16,0},... | collective-permute-start | bytes 196616 | tf_op jit(solution)/shard_map/ppermute | solution.py:83
  63.8 5.3 %collective-permute-start.18 = (f32[128,128]{1,0:T(8,128)S(1)}, f32[128,128]{1,0:T(8,128)S(1)}, u32[]{:S(2)}, u32[]{:S(2)}) collective-permute-start(f32[128,128]{1,0:T(8,128)S(1)} %dynamic-slice_add_fusion.9), channel_id=1, source_target_pairs={{0,16},{2,18},{4,20},{6,22},{8,24},{10,26},{12,28},{14,30},{16,0},... | collective-permute-start | bytes 196616 | tf_op jit(solution)/shard_map/ppermute | solution.py:83
  68.2 4.5 %collective-permute-start.26 = (f32[128,128]{1,0:T(8,128)S(1)}, f32[128,128]{1,0:T(8,128)S(1)}, u32[]{:S(2)}, u32[]{:S(2)}) collective-permute-start(f32[128,128]{1,0:T(8,128)S(1)} %add_subtract_fusion), channel_id=1, source_target_pairs={{0,4},{2,6},{4,0},{6,2},{8,12},{10,14},{12,8},{14,10},{16,20},{18,... | collective-permute-start | bytes 196616 | tf_op jit(solution)/shard_map/ppermute | solution.py:87
  69.1 4.3 %collective-permute-start.19 = (f32[128,128]{1,0:T(8,128)S(1)}, f32[128,128]{1,0:T(8,128)S(1)}, u32[]{:S(2)}, u32[]{:S(2)}) collective-permute-start(f32[128,128]{1,0:T(8,128)S(1)} %add_subtract_fusion.1), channel_id=1, source_target_pairs={{0,8},{2,10},{4,12},{6,14},{8,0},{10,2},{12,4},{14,6},{16,24},{18,... | collective-permute-start | bytes 196616 | tf_op jit(solution)/shard_map/ppermute | solution.py:87
  72.7 5.0 %collective-permute-start.27 = (f32[256,128]{1,0:T(8,128)S(1)}, f32[256,128]{1,0:T(8,128)S(1)}, u32[]{:S(2)}, u32[]{:S(2)}) collective-permute-start(f32[256,128]{1,0:T(8,128)S(1)} %pad_maximum_fusion.8), channel_id=1, source_target_pairs={{0,8},{2,10},{4,12},{6,14},{8,0},{10,2},{12,4},{14,6},{16,24},{18,... | collective-permute-start | bytes 393224 | tf_op jit(solution)/shard_map/ppermute | solution.py:87
  73.5 5.0 %collective-permute-start.20 = (f32[256,128]{1,0:T(8,128)S(1)}, f32[256,128]{1,0:T(8,128)S(1)}, u32[]{:S(2)}, u32[]{:S(2)}) collective-permute-start(f32[256,128]{1,0:T(8,128)S(1)} %pad_maximum_fusion.7), channel_id=1, source_target_pairs={{0,4},{2,6},{4,0},{6,2},{8,12},{10,14},{12,8},{14,10},{16,20},{18,... | collective-permute-start | bytes 393224 | tf_op jit(solution)/shard_map/ppermute | solution.py:87
  77.8 1.6 %collective-permute-start.28 = (f32[512,128]{1,0:T(8,128)S(1)}, f32[512,128]{1,0:T(8,128)S(1)}, u32[]{:S(2)}, u32[]{:S(2)}) collective-permute-start(f32[512,128]{1,0:T(8,128)S(1)} %pad_maximum_fusion.4), channel_id=1, source_target_pairs={{0,2},{2,0},{4,6},{6,4},{8,10},{10,8},{12,14},{14,12},{16,18},{18,... | collective-permute-start | bytes 786440 | tf_op jit(solution)/shard_map/ppermute | solution.py:87
  78.5 1.6 %collective-permute-start.21 = (f32[512,128]{1,0:T(8,128)S(1)}, f32[512,128]{1,0:T(8,128)S(1)}, u32[]{:S(2)}, u32[]{:S(2)}) collective-permute-start(f32[512,128]{1,0:T(8,128)S(1)} %pad_maximum_fusion.3), channel_id=1, source_target_pairs={{0,2},{2,0},{4,6},{6,4},{8,10},{10,8},{12,14},{14,12},{16,18},{18,... | collective-permute-start | bytes 786440 | tf_op jit(solution)/shard_map/ppermute | solution.py:87

commit v10 on v9

--- a/solution.py
+++ b/solution.py
@@ -124,24 +124,36 @@
             k = n.bit_length() - 1
             orders = (list(range(k)), [0, 2, 1] + list(range(3, k)) if k >= 3 else list(range(k)))
             width = first_sum.shape[1] // 2
+            height = first_sum.shape[0] // 2
             columns = (slice(0, width), slice(width, 2 * width))
-            first_blocks = []
-            for chain, (order, cols) in enumerate(zip(orders, columns)):
+            row_parts = (slice(0, height), slice(height, 2 * height))
+            pieces = [(rows, cols, orders[(a + b) % 2]) for a, rows in enumerate(row_parts) for b, cols in enumerate(columns)]
+            first_remains = []
+            for chain, (rows, cols, order) in enumerate(pieces):
                 remains, got_riders = ordered_reduce_then_gather(
-                    first_sum[:, cols], right_side[0][:, cols], "blk", n, order,
+                    first_sum[rows, cols], right_side[0][rows, cols], "blk", n, order,
                     (panel_sum, inverse_pieces) if chain == 0 else None,
                 )
                 if chain == 0:
                     panel_sum, inverse_pieces = got_riders
-                first_blocks.append(remains)
+                first_remains.append(remains)
             inverse_full = jnp.concatenate(list(inverse_pieces), axis=2)
-            first_blocks = [product(inverse_full[0], remains) for remains in first_blocks]
-            second_blocks = []
-            for order, cols, block in zip(orders, columns, first_blocks):
+
+            def apply(matrix, parts):
+                return [
+                    sum(product(matrix[:, rows], parts[a * 2 + b]) for a, rows in enumerate(row_parts))
+                    for b in range(2)
+                ]
+
+            first_blocks = apply(inverse_full[0], first_remains)
+            second_remains = []
+            for rows, cols, order in pieces:
+                b = 0 if cols.start == 0 else 1
                 remains, _ = ordered_reduce_then_gather(
-                    panel_sum[:, cols] + product(coupling, block), right_side[1][:, cols], "blk", n, order
+                    panel_sum[rows, cols] + product(coupling[rows], first_blocks[b]), right_side[1][rows, cols], "blk", n, order
                 )
-                second_blocks.append(product(inverse_full[1], remains))
+                second_remains.append(remains)
+            second_blocks = apply(inverse_full[1], second_remains)
             first_block = jnp.concatenate(first_blocks, 1)
             second_block = jnp.concatenate(second_blocks, 1)
         else:

time: 81.5 us -> 90.2 us (1.11)
  starting transfers between devices: 32.8 us -> 54.3 us
  waiting for transfers between devices: 29.1 us -> 10.5 us
  other arithmetic: 2.41 us -> 4.99 us
  local copies, waits for them, and re-layouts: 2.18 us -> 3.72 us
  matrix products: 14.2 us -> 15.4 us
    ppermute x12 -> x24, starting transfers between devices: 8.01 us -> 18.4 us  [ordered_reduce_then_gather(): got = lax.ppermute(y, axis, [(i, i ^ 1 << j) for i in range(n)])]
    ppermute x12 -> x24, waiting for transfers between devices: 9.21 us -> 0.8 us  [ordered_reduce_then_gather(): got = lax.ppermute(send, axis, [(i, i ^ 1 << j) for i in range(n)])]
    ppermute x12 -> x24, starting transfers between devices: 13.4 us -> 20.7 us  [ordered_reduce_then_gather(): got = lax.ppermute(send, axis, [(i, i ^ 1 << j) for i in range(n)])]
    ppermute x12 -> x24, waiting for transfers between devices: 14.8 us -> 7.76 us  [ordered_reduce_then_gather(): got = lax.ppermute(y, axis, [(i, i ^ 1 << j) for i in range(n)])]
    ppermute x4 -> x8, starting transfers between devices: 8.5 us -> 12.2 us  [ordered_reduce_then_gather(): y = y + lax.ppermute(y, axis, [(i, i ^ 1 << top) for i in range(n)])]
    ppermute x4 -> x8, waiting for transfers between devices: 5.16 us -> 1.94 us  [ordered_reduce_then_gather(): y = y + lax.ppermute(y, axis, [(i, i ^ 1 << top) for i in range(n)])]
    sub x4 -> x8, other arithmetic: 0.07 us -> 2.4 us  [ordered_reduce_then_gather(): y = r - y]
    slice x3, local copies, waits for them, and re-layouts: 0.21 us -> 2.23 us  [the longest x1 1.26 us: shards(): right_side[0][rows, cols]]
  transfers between devices with their start and end apart: 29 -> 57, of which waited for: 20 -> 12; matrix products, arithmetic and copies ran while one was open for 17% -> 23% of each run, Pallas kernels for 0% -> 0%
where the time goes in v10:
time: 90.2 us; the launch traced here: 89.8 us
  starting transfers between devices  54.3 us (60%)
  matrix products  15.4 us (17%)
  waiting for transfers between devices  10.5 us (12%)
  other arithmetic  4.99 us (6%)
  local copies, waits for them, and re-layouts  3.72 us (4%)
    ppermute x24, starting transfers between devices, ordered_reduce_then_gather(): got = lax.ppermute(send, axis, [(i, i ^ 1 << j) for i in range(n)])  20.7 us
    ppermute x24, starting transfers between devices, ordered_reduce_then_gather(): got = lax.ppermute(y, axis, [(i, i ^ 1 << j) for i in range(n)])  18.4 us
    dot_general x14, matrix products, product(): jnp.dot(left, right, precision=lax.Precision.HIGHEST, preferred_element_t...  15.4 us
    ppermute x8, starting transfers between devices, ordered_reduce_then_gather(): y = y + lax.ppermute(y, axis, [(i, i ^ 1 << top) for i in range(n)])  12.2 us
    ppermute x24, waiting for transfers between devices, ordered_reduce_then_gather(): got = lax.ppermute(y, axis, [(i, i ^ 1 << j) for i in range(n)])  7.76 us
    ppermute x1, starting transfers between devices, doubling_gather(): got = lax.ppermute(y, axis, [(i, i ^ 1 << j) for i in range(n)])  2.94 us
    sub x8, other arithmetic, ordered_reduce_then_gather(): y = r - y  2.4 us
    ppermute x8, waiting for transfers between devices, ordered_reduce_then_gather(): y = y + lax.ppermute(y, axis, [(i, i ^ 1 << top) for i in range(n)])  1.94 us
  transfers between devices with their start and end apart: 57, of which 12 were waited for; matrix products, arithmetic and copies ran while one was open for 23% of the time, Pallas kernels for 0%

profile of v10, /device:TPU:0, one launch (start us, length us, event | category | flops | bytes accessed | tf_op | source)
XLA Modules:
  0.0 89.8 jit_solution(6671024310224742353)
XLA Ops:
  0.0 2.9 %collective-permute-start = (f32[1,1,2,64,512]{4,3,2,1,0:T(8,128)}, f32[1,1,2,64,512]{4,3,2,1,0:T(8,128)}, u32[]{:S(2)}, u32[]{:S(2)}) collective-permute-start(f32[1,1,2,64,512]{4,3,2,1,0:T(8,128)} %bitcast.53), channel_id=1, source_target_pairs={{0,1},{1,0},{2,3},{3,2},{4,5},{5,4},{6,7},{7,6},{8,9},{9,8},{10,11... | collective-permute-start | bytes 786440 | tf_op jit(solution)/shard_map/ppermute | solution.py:34
  2.9 5.2 %fusion = f32[1024,256]{1,0:T(8,128)S(1)} fusion(f32[1024,256]{1,0:T(8,128)S(1)} %copy-done, f32[2,1024,1024]{2,1,0:T(8,128)} %param.5), kind=kOutput, calls=%fused_computation | convolution fusion | flops 3221225472 | bytes 6291456 | tf_op jit(solution)/shard_map/dot_general | solution.py:8
  8.2 5.6 %fusion.2 = f32[1024,256]{1,0:T(8,128)S(1)} fusion(f32[1024,256]{1,0:T(8,128)S(1)} %copy-done, f32[2,1024,1024]{2,1,0:T(8,128)} %param.5), kind=kOutput, calls=%fused_computation.2 | convolution fusion | flops 3221225472 | bytes 6291456 | tf_op jit(solution)/shard_map/dot_general | solution.py:8
  13.8 1.1 %slice_bitcast_fusion = (f32[1024,256]{1,0:T(8,128)S(1)}, f32[1024,256]{1,0:T(8,128)}) fusion(f32[2,1024,256]{2,1,0:T(8,128)S(1)} %copy-done.1), kind=kLoop, calls=%fused_computation.14 | loop fusion | bytes 4194304 | tf_op jit(solution)/shard_map/squeeze | solution.py:153
  15.8 1.3 %fusion.66 = (f32[512,128]{1,0:T(8,128)S(1)}, f32[512,128]{1,0:T(8,128)S(1)}, f32[512,128]{1,0:T(8,128)S(1)}, f32[512,128]{1,0:T(8,128)S(1)}) fusion(f32[1024,256]{1,0:T(8,128)} %get-tuple-element.16), kind=kLoop, calls=%fused_computation.203 | loop fusion | bytes 2097152 | tf_op jit(solution)/shard_map/slice | solution.py:134
  19.8 1.6 %collective-permute-start.2 = (f32[128,128]{1,0:T(8,128)S(1)}, f32[128,128]{1,0:T(8,128)S(1)}, u32[]{:S(2)}, u32[]{:S(2)}) collective-permute-start(f32[128,128]{1,0:T(8,128)S(1)} %constant_dynamic-slice_fusion.22), channel_id=1, source_target_pairs={{0,4},{2,6},{4,0},{6,2},{8,12},{10,14},{12,8},{14,10},{16,20},{18,... | collective-permute-start | bytes 196616 | tf_op jit(solution)/shard_map/ppermute | solution.py:78
  21.4 1.6 %collective-permute-start.16 = (f32[128,128]{1,0:T(8,128)S(1)}, f32[128,128]{1,0:T(8,128)S(1)}, u32[]{:S(2)}, u32[]{:S(2)}) collective-permute-start(f32[128,128]{1,0:T(8,128)S(1)} %constant_dynamic-slice_fusion.16), channel_id=1, source_target_pairs={{0,8},{2,10},{4,12},{6,14},{8,0},{10,2},{12,4},{14,6},{16,24},{18,... | collective-permute-start | bytes 196616 | tf_op jit(solution)/shard_map/ppermute | solution.py:78
  24.3 1.6 %collective-permute-start.3 = (f32[64,128]{1,0:T(8,128)S(1)}, f32[64,128]{1,0:T(8,128)S(1)}, u32[]{:S(2)}, u32[]{:S(2)}) collective-permute-start(f32[64,128]{1,0:T(8,128)S(1)} %constant_dynamic-slice_fusion.21), channel_id=1, source_target_pairs={{0,8},{2,10},{4,12},{6,14},{8,0},{10,2},{12,4},{14,6},{16,24},{18,... | collective-permute-start | bytes 98312 | tf_op jit(solution)/shard_map/ppermute | solution.py:78
  26.0 2.1 %collective-permute-start.17 = (f32[64,128]{1,0:T(8,128)S(1)}, f32[64,128]{1,0:T(8,128)S(1)}, u32[]{:S(2)}, u32[]{:S(2)}) collective-permute-start(f32[64,128]{1,0:T(8,128)S(1)} %constant_dynamic-slice_fusion.15), channel_id=1, source_target_pairs={{0,4},{2,6},{4,0},{6,2},{8,12},{10,14},{12,8},{14,10},{16,20},{18,... | collective-permute-start | bytes 98312 | tf_op jit(solution)/shard_map/ppermute | solution.py:78
  28.3 1.7 %collective-permute-start.10 = (f32[64,128]{1,0:T(8,128)S(1)}, f32[64,128]{1,0:T(8,128)S(1)}, u32[]{:S(2)}, u32[]{:S(2)}) collective-permute-start(f32[64,128]{1,0:T(8,128)S(1)} %constant_dynamic-slice_fusion.18), channel_id=1, source_target_pairs={{0,4},{2,6},{4,0},{6,2},{8,12},{10,14},{12,8},{14,10},{16,20},{18,... | collective-permute-start | bytes 98312 | tf_op jit(solution)/shard_map/ppermute | solution.py:78
  30.0 2.7 %collective-permute-start.4 = (f32[64,128]{1,0:T(8,128)S(1)}, f32[64,128]{1,0:T(8,128)S(1)}, u32[]{:S(2)}, u32[]{:S(2)}) collective-permute-start(f32[64,128]{1,0:T(8,128)S(1)} %dynamic-slice_add_fusion.23), channel_id=1, source_target_pairs={{0,16},{2,18},{4,20},{6,22},{8,24},{10,26},{12,28},{14,30},{16,0},... | collective-permute-start | bytes 98312 | tf_op jit(solution)/shard_map/ppermute | solution.py:83
  33.1 2.7 %collective-permute-start.25 = (f32[64,128]{1,0:T(8,128)S(1)}, f32[64,128]{1,0:T(8,128)S(1)}, u32[]{:S(2)}, u32[]{:S(2)}) collective-permute-start(f32[64,128]{1,0:T(8,128)S(1)} %dynamic-slice_add_fusion.20), channel_id=1, source_target_pairs={{0,16},{2,18},{4,20},{6,22},{8,24},{10,26},{12,28},{14,30},{16,0},... | collective-permute-start | bytes 98312 | tf_op jit(solution)/shard_map/ppermute | solution.py:83
  36.2 1.9 %collective-permute-done.25 = f32[64,128]{1,0:T(8,128)S(1)} collective-permute-done((f32[64,128]{1,0:T(8,128)S(1)}, f32[64,128]{1,0:T(8,128)S(1)}, u32[]{:S(2)}, u32[]{:S(2)}) %collective-permute-start.25) | collective-permute-done | bytes 32800 | tf_op jit(solution)/shard_map/ppermute | solution.py:83
  39.2 1.1 %collective-permute-start.5 = (f32[64,128]{1,0:T(8,128)S(1)}, f32[64,128]{1,0:T(8,128)S(1)}, u32[]{:S(2)}, u32[]{:S(2)}) collective-permute-start(f32[64,128]{1,0:T(8,128)S(1)} %add_subtract_fusion.7), channel_id=1, source_target_pairs={{0,8},{2,10},{4,12},{6,14},{8,0},{10,2},{12,4},{14,6},{16,24},{18,... | collective-permute-start | bytes 98312 | tf_op jit(solution)/shard_map/ppermute | solution.py:87
  40.3 2.0 %collective-permute-start.19 = (f32[64,128]{1,0:T(8,128)S(1)}, f32[64,128]{1,0:T(8,128)S(1)}, u32[]{:S(2)}, u32[]{:S(2)}) collective-permute-start(f32[64,128]{1,0:T(8,128)S(1)} %add_subtract_fusion.5), channel_id=1, source_target_pairs={{0,4},{2,6},{4,0},{6,2},{8,12},{10,14},{12,8},{14,10},{16,20},{18,... | collective-permute-start | bytes 98312 | tf_op jit(solution)/shard_map/ppermute | solution.py:87
  42.5 2.0 %collective-permute-start.27 = (f32[128,128]{1,0:T(8,128)S(1)}, f32[128,128]{1,0:T(8,128)S(1)}, u32[]{:S(2)}, u32[]{:S(2)}) collective-permute-start(f32[128,128]{1,0:T(8,128)S(1)} %pad_maximum_fusion.13), channel_id=1, source_target_pairs={{0,4},{2,6},{4,0},{6,2},{8,12},{10,14},{12,8},{14,10},{16,20},{18,... | collective-permute-start | bytes 196616 | tf_op jit(solution)/shard_map/ppermute | solution.py:87
  44.9 1.9 %collective-permute-start.20 = (f32[128,128]{1,0:T(8,128)S(1)}, f32[128,128]{1,0:T(8,128)S(1)}, u32[]{:S(2)}, u32[]{:S(2)}) collective-permute-start(f32[128,128]{1,0:T(8,128)S(1)} %pad_maximum_fusion.12), channel_id=1, source_target_pairs={{0,8},{2,10},{4,12},{6,14},{8,0},{10,2},{12,4},{14,6},{16,24},{18,... | collective-permute-start | bytes 196616 | tf_op jit(solution)/shard_map/ppermute | solution.py:87
  47.2 1.8 %collective-permute-done.6 = f32[128,128]{1,0:T(8,128)S(1)} collective-permute-done((f32[128,128]{1,0:T(8,128)S(1)}, f32[128,128]{1,0:T(8,128)S(1)}, u32[]{:S(2)}, u32[]{:S(2)}) %collective-permute-start.6) | collective-permute-done | bytes 65568 | tf_op jit(solution)/shard_map/ppermute | solution.py:87
  49.0 2.0 %collective-permute-done.13 = f32[128,128]{1,0:T(8,128)S(1)} collective-permute-done((f32[128,128]{1,0:T(8,128)S(1)}, f32[128,128]{1,0:T(8,128)S(1)}, u32[]{:S(2)}, u32[]{:S(2)}) %collective-permute-start.13) | collective-permute-done | bytes 65568 | tf_op jit(solution)/shard_map/ppermute | solution.py:87
  58.5 1.5 %collective-permute-start.30 = (f32[128,128]{1,0:T(8,128)S(1)}, f32[128,128]{1,0:T(8,128)S(1)}, u32[]{:S(2)}, u32[]{:S(2)}) collective-permute-start(f32[128,128]{1,0:T(8,128)S(1)} %constant_dynamic-slice_fusion.10), channel_id=1, source_target_pairs={{0,4},{2,6},{4,0},{6,2},{8,12},{10,14},{12,8},{14,10},{16,20},{18,... | collective-permute-start | bytes 196616 | tf_op jit(solution)/shard_map/ppermute | solution.py:78
  60.7 1.5 %collective-permute-start.44 = (f32[128,128]{1,0:T(8,128)S(1)}, f32[128,128]{1,0:T(8,128)S(1)}, u32[]{:S(2)}, u32[]{:S(2)}) collective-permute-start(f32[128,128]{1,0:T(8,128)S(1)} %constant_dynamic-slice_fusion.4), channel_id=1, source_target_pairs={{0,8},{2,10},{4,12},{6,14},{8,0},{10,2},{12,4},{14,6},{16,24},{18,... | collective-permute-start | bytes 196616 | tf_op jit(solution)/shard_map/ppermute | solution.py:78
  63.3 1.3 %collective-permute-start.31 = (f32[64,128]{1,0:T(8,128)S(1)}, f32[64,128]{1,0:T(8,128)S(1)}, u32[]{:S(2)}, u32[]{:S(2)}) collective-permute-start(f32[64,128]{1,0:T(8,128)S(1)} %constant_dynamic-slice_fusion.9), channel_id=1, source_target_pairs={{0,8},{2,10},{4,12},{6,14},{8,0},{10,2},{12,4},{14,6},{16,24},{18,... | collective-permute-start | bytes 98312 | tf_op jit(solution)/shard_map/ppermute | solution.py:78
  65.7 1.2 %collective-permute-start.45 = (f32[64,128]{1,0:T(8,128)S(1)}, f32[64,128]{1,0:T(8,128)S(1)}, u32[]{:S(2)}, u32[]{:S(2)}) collective-permute-start(f32[64,128]{1,0:T(8,128)S(1)} %constant_dynamic-slice_fusion.3), channel_id=1, source_target_pairs={{0,4},{2,6},{4,0},{6,2},{8,12},{10,14},{12,8},{14,10},{16,20},{18,... | collective-permute-start | bytes 98312 | tf_op jit(solution)/shard_map/ppermute | solution.py:78
  66.9 1.8 %collective-permute-start.39 = (f32[64,128]{1,0:T(8,128)S(1)}, f32[64,128]{1,0:T(8,128)S(1)}, u32[]{:S(2)}, u32[]{:S(2)}) collective-permute-start(f32[64,128]{1,0:T(8,128)S(1)} %dynamic-slice_add_fusion.18), channel_id=1, source_target_pairs={{0,16},{2,18},{4,20},{6,22},{8,24},{10,26},{12,28},{14,30},{16,0},... | collective-permute-start | bytes 98312 | tf_op jit(solution)/shard_map/ppermute | solution.py:83
  68.8 1.2 %collective-permute-start.32 = (f32[64,128]{1,0:T(8,128)S(1)}, f32[64,128]{1,0:T(8,128)S(1)}, u32[]{:S(2)}, u32[]{:S(2)}) collective-permute-start(f32[64,128]{1,0:T(8,128)S(1)} %dynamic-slice_add_fusion.19), channel_id=1, source_target_pairs={{0,16},{2,18},{4,20},{6,22},{8,24},{10,26},{12,28},{14,30},{16,0},... | collective-permute-start | bytes 98312 | tf_op jit(solution)/shard_map/ppermute | solution.py:83
  70.0 1.8 %collective-permute-start.53 = (f32[64,128]{1,0:T(8,128)S(1)}, f32[64,128]{1,0:T(8,128)S(1)}, u32[]{:S(2)}, u32[]{:S(2)}) collective-permute-start(f32[64,128]{1,0:T(8,128)S(1)} %dynamic-slice_add_fusion.16), channel_id=1, source_target_pairs={{0,16},{2,18},{4,20},{6,22},{8,24},{10,26},{12,28},{14,30},{16,0},... | collective-permute-start | bytes 98312 | tf_op jit(solution)/shard_map/ppermute | solution.py:83
  71.9 1.2 %collective-permute-start.46 = (f32[64,128]{1,0:T(8,128)S(1)}, f32[64,128]{1,0:T(8,128)S(1)}, u32[]{:S(2)}, u32[]{:S(2)}) collective-permute-start(f32[64,128]{1,0:T(8,128)S(1)} %dynamic-slice_add_fusion.17), channel_id=1, source_target_pairs={{0,16},{2,18},{4,20},{6,22},{8,24},{10,26},{12,28},{14,30},{16,0},... | collective-permute-start | bytes 98312 | tf_op jit(solution)/shard_map/ppermute | solution.py:83
  75.6 1.3 %collective-permute-start.33 = (f32[64,128]{1,0:T(8,128)S(1)}, f32[64,128]{1,0:T(8,128)S(1)}, u32[]{:S(2)}, u32[]{:S(2)}) collective-permute-start(f32[64,128]{1,0:T(8,128)S(1)} %add_subtract_fusion.3), channel_id=1, source_target_pairs={{0,8},{2,10},{4,12},{6,14},{8,0},{10,2},{12,4},{14,6},{16,24},{18,... | collective-permute-start | bytes 98312 | tf_op jit(solution)/shard_map/ppermute | solution.py:87
  78.6 1.2 %collective-permute-start.47 = (f32[64,128]{1,0:T(8,128)S(1)}, f32[64,128]{1,0:T(8,128)S(1)}, u32[]{:S(2)}, u32[]{:S(2)}) collective-permute-start(f32[64,128]{1,0:T(8,128)S(1)} %add_subtract_fusion.1), channel_id=1, source_target_pairs={{0,4},{2,6},{4,0},{6,2},{8,12},{10,14},{12,8},{14,10},{16,20},{18,... | collective-permute-start | bytes 98312 | tf_op jit(solution)/shard_map/ppermute | solution.py:87
  80.8 1.2 %collective-permute-start.34 = (f32[128,128]{1,0:T(8,128)S(1)}, f32[128,128]{1,0:T(8,128)S(1)}, u32[]{:S(2)}, u32[]{:S(2)}) collective-permute-start(f32[128,128]{1,0:T(8,128)S(1)} %pad_maximum_fusion.14), channel_id=1, source_target_pairs={{0,4},{2,6},{4,0},{6,2},{8,12},{10,14},{12,8},{14,10},{16,20},{18,... | collective-permute-start | bytes 196616 | tf_op jit(solution)/shard_map/ppermute | solution.py:87
  83.0 1.2 %collective-permute-start.48 = (f32[128,128]{1,0:T(8,128)S(1)}, f32[128,128]{1,0:T(8,128)S(1)}, u32[]{:S(2)}, u32[]{:S(2)}) collective-permute-start(f32[128,128]{1,0:T(8,128)S(1)} %pad_maximum_fusion.16), channel_id=1, source_target_pairs={{0,8},{2,10},{4,12},{6,14},{8,0},{10,2},{12,4},{14,6},{16,24},{18,... | collective-permute-start | bytes 196616 | tf_op jit(solution)/shard_map/ppermute | solution.py:87
  85.3 1.1 %collective-permute-done.55 = f32[128,128]{1,0:T(8,128)S(1)} collective-permute-done((f32[128,128]{1,0:T(8,128)S(1)}, f32[128,128]{1,0:T(8,128)S(1)}, u32[]{:S(2)}, u32[]{:S(2)}) %collective-permute-start.55) | collective-permute-done | bytes 65568 | tf_op jit(solution)/shard_map/ppermute | solution.py:87
  (209 shorter events, 28.6 us)
Async XLA Ops:
  0.0 17.0 %collective-permute-start = (f32[1,1,2,64,512]{4,3,2,1,0:T(8,128)}, f32[1,1,2,64,512]{4,3,2,1,0:T(8,128)}, u32[]{:S(2)}, u32[]{:S(2)}) collective-permute-start(f32[1,1,2,64,512]{4,3,2,1,0:T(8,128)} %bitcast.53), channel_id=1, source_target_pairs={{0,1},{1,0},{2,3},{3,2},{4,5},{5,4},{6,7},{7,6},{8,9},{9,8},{10,11... | collective-permute-start | bytes 786440 | tf_op jit(solution)/shard_map/ppermute | solution.py:34
  19.0 4.6 %collective-permute-start.8 = (f32[256,128]{1,0:T(8,128)S(1)}, f32[256,128]{1,0:T(8,128)S(1)}, u32[]{:S(2)}, u32[]{:S(2)}) collective-permute-start(f32[256,128]{1,0:T(8,128)S(1)} %constant_dynamic-slice_fusion.20), channel_id=1, source_target_pairs={{0,2},{2,0},{4,6},{6,4},{8,10},{10,8},{12,14},{14,12},{16,18},{18,... | collective-permute-start | bytes 393224 | tf_op jit(solution)/shard_map/ppermute | solution.py:78
  21.4 4.6 %collective-permute-start.16 = (f32[128,128]{1,0:T(8,128)S(1)}, f32[128,128]{1,0:T(8,128)S(1)}, u32[]{:S(2)}, u32[]{:S(2)}) collective-permute-start(f32[128,128]{1,0:T(8,128)S(1)} %constant_dynamic-slice_fusion.16), channel_id=1, source_target_pairs={{0,8},{2,10},{4,12},{6,14},{8,0},{10,2},{12,4},{14,6},{16,24},{18,... | collective-permute-start | bytes 196616 | tf_op jit(solution)/shard_map/ppermute | solution.py:78
  23.1 5.0 %collective-permute-start.23 = (f32[128,128]{1,0:T(8,128)S(1)}, f32[128,128]{1,0:T(8,128)S(1)}, u32[]{:S(2)}, u32[]{:S(2)}) collective-permute-start(f32[128,128]{1,0:T(8,128)S(1)} %constant_dynamic-slice_fusion.13), channel_id=1, source_target_pairs={{0,4},{2,6},{4,0},{6,2},{8,12},{10,14},{12,8},{14,10},{16,20},{18,... | collective-permute-start | bytes 196616 | tf_op jit(solution)/shard_map/ppermute | solution.py:78
  23.7 4.5 %collective-permute-start.9 = (f32[128,128]{1,0:T(8,128)S(1)}, f32[128,128]{1,0:T(8,128)S(1)}, u32[]{:S(2)}, u32[]{:S(2)}) collective-permute-start(f32[128,128]{1,0:T(8,128)S(1)} %constant_dynamic-slice_fusion.19), channel_id=1, source_target_pairs={{0,8},{2,10},{4,12},{6,14},{8,0},{10,2},{12,4},{14,6},{16,24},{18,... | collective-permute-start | bytes 196616 | tf_op jit(solution)/shard_map/ppermute | solution.py:78
  24.3 5.7 %collective-permute-start.3 = (f32[64,128]{1,0:T(8,128)S(1)}, f32[64,128]{1,0:T(8,128)S(1)}, u32[]{:S(2)}, u32[]{:S(2)}) collective-permute-start(f32[64,128]{1,0:T(8,128)S(1)} %constant_dynamic-slice_fusion.21), channel_id=1, source_target_pairs={{0,8},{2,10},{4,12},{6,14},{8,0},{10,2},{12,4},{14,6},{16,24},{18,... | collective-permute-start | bytes 98312 | tf_op jit(solution)/shard_map/ppermute | solution.py:78
  26.0 6.7 %collective-permute-start.17 = (f32[64,128]{1,0:T(8,128)S(1)}, f32[64,128]{1,0:T(8,128)S(1)}, u32[]{:S(2)}, u32[]{:S(2)}) collective-permute-start(f32[64,128]{1,0:T(8,128)S(1)} %constant_dynamic-slice_fusion.15), channel_id=1, source_target_pairs={{0,4},{2,6},{4,0},{6,2},{8,12},{10,14},{12,8},{14,10},{16,20},{18,... | collective-permute-start | bytes 98312 | tf_op jit(solution)/shard_map/ppermute | solution.py:78
  28.1 5.0 %collective-permute-start.24 = (f32[64,128]{1,0:T(8,128)S(1)}, f32[64,128]{1,0:T(8,128)S(1)}, u32[]{:S(2)}, u32[]{:S(2)}) collective-permute-start(f32[64,128]{1,0:T(8,128)S(1)} %constant_dynamic-slice_fusion.12), channel_id=1, source_target_pairs={{0,8},{2,10},{4,12},{6,14},{8,0},{10,2},{12,4},{14,6},{16,24},{18,... | collective-permute-start | bytes 98312 | tf_op jit(solution)/shard_map/ppermute | solution.py:78
  28.3 7.5 %collective-permute-start.10 = (f32[64,128]{1,0:T(8,128)S(1)}, f32[64,128]{1,0:T(8,128)S(1)}, u32[]{:S(2)}, u32[]{:S(2)}) collective-permute-start(f32[64,128]{1,0:T(8,128)S(1)} %constant_dynamic-slice_fusion.18), channel_id=1, source_target_pairs={{0,4},{2,6},{4,0},{6,2},{8,12},{10,14},{12,8},{14,10},{16,20},{18,... | collective-permute-start | bytes 98312 | tf_op jit(solution)/shard_map/ppermute | solution.py:78
  30.0 9.2 %collective-permute-start.4 = (f32[64,128]{1,0:T(8,128)S(1)}, f32[64,128]{1,0:T(8,128)S(1)}, u32[]{:S(2)}, u32[]{:S(2)}) collective-permute-start(f32[64,128]{1,0:T(8,128)S(1)} %dynamic-slice_add_fusion.23), channel_id=1, source_target_pairs={{0,16},{2,18},{4,20},{6,22},{8,24},{10,26},{12,28},{14,30},{16,0},... | collective-permute-start | bytes 98312 | tf_op jit(solution)/shard_map/ppermute | solution.py:83
  32.7 7.6 %collective-permute-start.18 = (f32[64,128]{1,0:T(8,128)S(1)}, f32[64,128]{1,0:T(8,128)S(1)}, u32[]{:S(2)}, u32[]{:S(2)}) collective-permute-start(f32[64,128]{1,0:T(8,128)S(1)} %dynamic-slice_add_fusion.21), channel_id=1, source_target_pairs={{0,16},{2,18},{4,20},{6,22},{8,24},{10,26},{12,28},{14,30},{16,0},... | collective-permute-start | bytes 98312 | tf_op jit(solution)/shard_map/ppermute | solution.py:83
  33.1 5.0 %collective-permute-start.25 = (f32[64,128]{1,0:T(8,128)S(1)}, f32[64,128]{1,0:T(8,128)S(1)}, u32[]{:S(2)}, u32[]{:S(2)}) collective-permute-start(f32[64,128]{1,0:T(8,128)S(1)} %dynamic-slice_add_fusion.20), channel_id=1, source_target_pairs={{0,16},{2,18},{4,20},{6,22},{8,24},{10,26},{12,28},{14,30},{16,0},... | collective-permute-start | bytes 98312 | tf_op jit(solution)/shard_map/ppermute | solution.py:83
  35.8 6.6 %collective-permute-start.11 = (f32[64,128]{1,0:T(8,128)S(1)}, f32[64,128]{1,0:T(8,128)S(1)}, u32[]{:S(2)}, u32[]{:S(2)}) collective-permute-start(f32[64,128]{1,0:T(8,128)S(1)} %dynamic-slice_add_fusion.22), channel_id=1, source_target_pairs={{0,16},{2,18},{4,20},{6,22},{8,24},{10,26},{12,28},{14,30},{16,0},... | collective-permute-start | bytes 98312 | tf_op jit(solution)/shard_map/ppermute | solution.py:83
  39.2 5.3 %collective-permute-start.5 = (f32[64,128]{1,0:T(8,128)S(1)}, f32[64,128]{1,0:T(8,128)S(1)}, u32[]{:S(2)}, u32[]{:S(2)}) collective-permute-start(f32[64,128]{1,0:T(8,128)S(1)} %add_subtract_fusion.7), channel_id=1, source_target_pairs={{0,8},{2,10},{4,12},{6,14},{8,0},{10,2},{12,4},{14,6},{16,24},{18,... | collective-permute-start | bytes 98312 | tf_op jit(solution)/shard_map/ppermute | solution.py:87
  40.3 4.5 %collective-permute-start.19 = (f32[64,128]{1,0:T(8,128)S(1)}, f32[64,128]{1,0:T(8,128)S(1)}, u32[]{:S(2)}, u32[]{:S(2)}) collective-permute-start(f32[64,128]{1,0:T(8,128)S(1)} %add_subtract_fusion.5), channel_id=1, source_target_pairs={{0,4},{2,6},{4,0},{6,2},{8,12},{10,14},{12,8},{14,10},{16,20},{18,... | collective-permute-start | bytes 98312 | tf_op jit(solution)/shard_map/ppermute | solution.py:87
  42.5 4.5 %collective-permute-start.27 = (f32[128,128]{1,0:T(8,128)S(1)}, f32[128,128]{1,0:T(8,128)S(1)}, u32[]{:S(2)}, u32[]{:S(2)}) collective-permute-start(f32[128,128]{1,0:T(8,128)S(1)} %pad_maximum_fusion.13), channel_id=1, source_target_pairs={{0,4},{2,6},{4,0},{6,2},{8,12},{10,14},{12,8},{14,10},{16,20},{18,... | collective-permute-start | bytes 196616 | tf_op jit(solution)/shard_map/ppermute | solution.py:87
  44.9 6.3 %collective-permute-start.20 = (f32[128,128]{1,0:T(8,128)S(1)}, f32[128,128]{1,0:T(8,128)S(1)}, u32[]{:S(2)}, u32[]{:S(2)}) collective-permute-start(f32[128,128]{1,0:T(8,128)S(1)} %pad_maximum_fusion.12), channel_id=1, source_target_pairs={{0,8},{2,10},{4,12},{6,14},{8,0},{10,2},{12,4},{14,6},{16,24},{18,... | collective-permute-start | bytes 196616 | tf_op jit(solution)/shard_map/ppermute | solution.py:87
  47.1 7.3 %collective-permute-start.28 = (f32[256,128]{1,0:T(8,128)S(1)}, f32[256,128]{1,0:T(8,128)S(1)}, u32[]{:S(2)}, u32[]{:S(2)}) collective-permute-start(f32[256,128]{1,0:T(8,128)S(1)} %pad_maximum_fusion.4), channel_id=1, source_target_pairs={{0,2},{2,0},{4,6},{6,4},{8,10},{10,8},{12,14},{14,12},{16,18},{18,... | collective-permute-start | bytes 393224 | tf_op jit(solution)/shard_map/ppermute | solution.py:87
  57.7 4.5 %collective-permute-start.37 = (f32[128,128]{1,0:T(8,128)S(1)}, f32[128,128]{1,0:T(8,128)S(1)}, u32[]{:S(2)}, u32[]{:S(2)}) collective-permute-start(f32[128,128]{1,0:T(8,128)S(1)} %constant_dynamic-slice_fusion.7), channel_id=1, source_target_pairs={{0,8},{2,10},{4,12},{6,14},{8,0},{10,2},{12,4},{14,6},{16,24},{18,... | collective-permute-start | bytes 196616 | tf_op jit(solution)/shard_map/ppermute | solution.py:78
  58.5 4.8 %collective-permute-start.30 = (f32[128,128]{1,0:T(8,128)S(1)}, f32[128,128]{1,0:T(8,128)S(1)}, u32[]{:S(2)}, u32[]{:S(2)}) collective-permute-start(f32[128,128]{1,0:T(8,128)S(1)} %constant_dynamic-slice_fusion.10), channel_id=1, source_target_pairs={{0,4},{2,6},{4,0},{6,2},{8,12},{10,14},{12,8},{14,10},{16,20},{18,... | collective-permute-start | bytes 196616 | tf_op jit(solution)/shard_map/ppermute | solution.py:78
  60.1 4.7 %collective-permute-start.51 = (f32[128,128]{1,0:T(8,128)S(1)}, f32[128,128]{1,0:T(8,128)S(1)}, u32[]{:S(2)}, u32[]{:S(2)}) collective-permute-start(f32[128,128]{1,0:T(8,128)S(1)} %constant_dynamic-slice_fusion.1), channel_id=1, source_target_pairs={{0,4},{2,6},{4,0},{6,2},{8,12},{10,14},{12,8},{14,10},{16,20},{18,... | collective-permute-start | bytes 196616 | tf_op jit(solution)/shard_map/ppermute | solution.py:78
  60.7 5.0 %collective-permute-start.44 = (f32[128,128]{1,0:T(8,128)S(1)}, f32[128,128]{1,0:T(8,128)S(1)}, u32[]{:S(2)}, u32[]{:S(2)}) collective-permute-start(f32[128,128]{1,0:T(8,128)S(1)} %constant_dynamic-slice_fusion.4), channel_id=1, source_target_pairs={{0,8},{2,10},{4,12},{6,14},{8,0},{10,2},{12,4},{14,6},{16,24},{18,... | collective-permute-start | bytes 196616 | tf_op jit(solution)/shard_map/ppermute | solution.py:78
  62.2 4.7 %collective-permute-start.38 = (f32[64,128]{1,0:T(8,128)S(1)}, f32[64,128]{1,0:T(8,128)S(1)}, u32[]{:S(2)}, u32[]{:S(2)}) collective-permute-start(f32[64,128]{1,0:T(8,128)S(1)} %constant_dynamic-slice_fusion.6), channel_id=1, source_target_pairs={{0,4},{2,6},{4,0},{6,2},{8,12},{10,14},{12,8},{14,10},{16,20},{18,... | collective-permute-start | bytes 98312 | tf_op jit(solution)/shard_map/ppermute | solution.py:78
  63.3 5.4 %collective-permute-start.31 = (f32[64,128]{1,0:T(8,128)S(1)}, f32[64,128]{1,0:T(8,128)S(1)}, u32[]{:S(2)}, u32[]{:S(2)}) collective-permute-start(f32[64,128]{1,0:T(8,128)S(1)} %constant_dynamic-slice_fusion.9), channel_id=1, source_target_pairs={{0,8},{2,10},{4,12},{6,14},{8,0},{10,2},{12,4},{14,6},{16,24},{18,... | collective-permute-start | bytes 98312 | tf_op jit(solution)/shard_map/ppermute | solution.py:78
  64.8 5.2 %collective-permute-start.52 = (f32[64,128]{1,0:T(8,128)S(1)}, f32[64,128]{1,0:T(8,128)S(1)}, u32[]{:S(2)}, u32[]{:S(2)}) collective-permute-start(f32[64,128]{1,0:T(8,128)S(1)} %constant_dynamic-slice_fusion), channel_id=1, source_target_pairs={{0,8},{2,10},{4,12},{6,14},{8,0},{10,2},{12,4},{14,6},{16,24},{18,... | collective-permute-start | bytes 98312 | tf_op jit(solution)/shard_map/ppermute | solution.py:78
  65.7 6.1 %collective-permute-start.45 = (f32[64,128]{1,0:T(8,128)S(1)}, f32[64,128]{1,0:T(8,128)S(1)}, u32[]{:S(2)}, u32[]{:S(2)}) collective-permute-start(f32[64,128]{1,0:T(8,128)S(1)} %constant_dynamic-slice_fusion.3), channel_id=1, source_target_pairs={{0,4},{2,6},{4,0},{6,2},{8,12},{10,14},{12,8},{14,10},{16,20},{18,... | collective-permute-start | bytes 98312 | tf_op jit(solution)/shard_map/ppermute | solution.py:78
  66.9 6.2 %collective-permute-start.39 = (f32[64,128]{1,0:T(8,128)S(1)}, f32[64,128]{1,0:T(8,128)S(1)}, u32[]{:S(2)}, u32[]{:S(2)}) collective-permute-start(f32[64,128]{1,0:T(8,128)S(1)} %dynamic-slice_add_fusion.18), channel_id=1, source_target_pairs={{0,16},{2,18},{4,20},{6,22},{8,24},{10,26},{12,28},{14,30},{16,0},... | collective-permute-start | bytes 98312 | tf_op jit(solution)/shard_map/ppermute | solution.py:83
  68.8 6.0 %collective-permute-start.32 = (f32[64,128]{1,0:T(8,128)S(1)}, f32[64,128]{1,0:T(8,128)S(1)}, u32[]{:S(2)}, u32[]{:S(2)}) collective-permute-start(f32[64,128]{1,0:T(8,128)S(1)} %dynamic-slice_add_fusion.19), channel_id=1, source_target_pairs={{0,16},{2,18},{4,20},{6,22},{8,24},{10,26},{12,28},{14,30},{16,0},... | collective-permute-start | bytes 98312 | tf_op jit(solution)/shard_map/ppermute | solution.py:83
  70.0 6.8 %collective-permute-start.53 = (f32[64,128]{1,0:T(8,128)S(1)}, f32[64,128]{1,0:T(8,128)S(1)}, u32[]{:S(2)}, u32[]{:S(2)}) collective-permute-start(f32[64,128]{1,0:T(8,128)S(1)} %dynamic-slice_add_fusion.16), channel_id=1, source_target_pairs={{0,16},{2,18},{4,20},{6,22},{8,24},{10,26},{12,28},{14,30},{16,0},... | collective-permute-start | bytes 98312 | tf_op jit(solution)/shard_map/ppermute | solution.py:83
  71.9 6.7 %collective-permute-start.46 = (f32[64,128]{1,0:T(8,128)S(1)}, f32[64,128]{1,0:T(8,128)S(1)}, u32[]{:S(2)}, u32[]{:S(2)}) collective-permute-start(f32[64,128]{1,0:T(8,128)S(1)} %dynamic-slice_add_fusion.17), channel_id=1, source_target_pairs={{0,16},{2,18},{4,20},{6,22},{8,24},{10,26},{12,28},{14,30},{16,0},... | collective-permute-start | bytes 98312 | tf_op jit(solution)/shard_map/ppermute | solution.py:83
  73.9 5.9 %collective-permute-start.40 = (f32[64,128]{1,0:T(8,128)S(1)}, f32[64,128]{1,0:T(8,128)S(1)}, u32[]{:S(2)}, u32[]{:S(2)}) collective-permute-start(f32[64,128]{1,0:T(8,128)S(1)} %add_subtract_fusion.2), channel_id=1, source_target_pairs={{0,4},{2,6},{4,0},{6,2},{8,12},{10,14},{12,8},{14,10},{16,20},{18,... | collective-permute-start | bytes 98312 | tf_op jit(solution)/shard_map/ppermute | solution.py:87
  75.6 5.2 %collective-permute-start.33 = (f32[64,128]{1,0:T(8,128)S(1)}, f32[64,128]{1,0:T(8,128)S(1)}, u32[]{:S(2)}, u32[]{:S(2)}) collective-permute-start(f32[64,128]{1,0:T(8,128)S(1)} %add_subtract_fusion.3), channel_id=1, source_target_pairs={{0,8},{2,10},{4,12},{6,14},{8,0},{10,2},{12,4},{14,6},{16,24},{18,... | collective-permute-start | bytes 98312 | tf_op jit(solution)/shard_map/ppermute | solution.py:87
  (28 other events, 121.6 us)

commit v11 on v9

--- a/solution.py
+++ b/solution.py
@@ -66,7 +66,7 @@
     return y.reshape(x.shape), riders
 
 
-def ordered_reduce_then_gather(x, right, axis, n, order, riders=None):
+def ordered_reduce_then_gather(x, right, axis, n, order, riders=None, hold=None):
     me = lax.axis_index(axis)
     y, r = x, right
     for step, j in enumerate(order[:-1]):
@@ -79,6 +79,9 @@
         if step == 1 and riders is not None:
             got, riders = lax.optimization_barrier((got, riders))
         y = keep + got
+        if step == 0 and hold is not None:
+            y, held = lax.optimization_barrier((y, hold[0]))
+            riders = (hold[1](held), riders)
     top = order[-1]
     y = y + lax.ppermute(y, axis, [(i, i ^ (1 << top)) for i in range(n)])
     y = r - y
@@ -116,20 +119,32 @@
         def own_slice(matrix):
             return lax.dynamic_slice_in_dim(matrix, my_index * own_count, own_count, 0)
 
-        first_sum = product(factor_panel[0], solved_before)
-        first_sum, inverse_pieces = lax.optimization_barrier((first_sum, inverse_pieces))
-        inverse_full = jnp.concatenate(list(inverse_pieces), axis=2)
-        panel_sum = product(factor_panel[1], solved_before)
-        if power_of_two and n >= 4:
+        chained = power_of_two and n >= 4
+        if chained:
+            width = solved_before.shape[1] // 2
+            column_major = solved_before.reshape(solved_before.shape[0], 2, width)
+
+            def split_product(left, right):
+                return jnp.einsum(
+                    "ij,jbk->bik", left, right, precision=lax.Precision.HIGHEST, preferred_element_type=jnp.float32
+                )
+
+            first_sum = split_product(factor_panel[0], column_major)
+            first_sum, inverse_pieces = lax.optimization_barrier((first_sum, inverse_pieces))
+        else:
+            first_sum = product(factor_panel[0], solved_before)
+            first_sum, inverse_pieces = lax.optimization_barrier((first_sum, inverse_pieces))
+            panel_sum = product(factor_panel[1], solved_before)
+        if chained:
             k = n.bit_length() - 1
             orders = (list(range(k)), [0, 2, 1] + list(range(3, k)) if k >= 3 else list(range(k)))
-            width = first_sum.shape[1] // 2
             columns = (slice(0, width), slice(width, 2 * width))
             first_blocks = []
             for chain, (order, cols) in enumerate(zip(orders, columns)):
                 remains, got_riders = ordered_reduce_then_gather(
-                    first_sum[:, cols], right_side[0][:, cols], "blk", n, order,
-                    (panel_sum, inverse_pieces) if chain == 0 else None,
+                    first_sum[chain], right_side[0][:, cols], "blk", n, order,
+                    inverse_pieces if chain == 0 else None,
+                    (column_major, lambda held: split_product(factor_panel[1], held)) if chain == 0 else None,
                 )
                 if chain == 0:
                     panel_sum, inverse_pieces = got_riders
@@ -137,9 +152,9 @@
             inverse_full = jnp.concatenate(list(inverse_pieces), axis=2)
             first_blocks = [product(inverse_full[0], remains) for remains in first_blocks]
             second_blocks = []
-            for order, cols, block in zip(orders, columns, first_blocks):
+            for chain, (order, cols, block) in enumerate(zip(orders, columns, first_blocks)):
                 remains, _ = ordered_reduce_then_gather(
-                    panel_sum[:, cols] + product(coupling, block), right_side[1][:, cols], "blk", n, order
+                    panel_sum[chain] + product(coupling, block), right_side[1][:, cols], "blk", n, order
                 )
                 second_blocks.append(product(inverse_full[1], remains))
             first_block = jnp.concatenate(first_blocks, 1)

time: 81.5 us -> 95.8 us (1.18)
  waiting for transfers between devices: 29.1 us -> 38.8 us
  starting transfers between devices: 32.8 us -> 25.2 us
  matrix products: 14.2 us -> 20.3 us
  local copies, waits for them, and re-layouts: 2.18 us -> 7.89 us
    dot_general x0 -> x2, matrix products: none -> 16.3 us  [split_product(): jnp.einsum('ij,jbk->bik', left, right, precision=lax.Precision.HIGHEST, p...]
    dot_general x8 -> x6, matrix products: 14.2 us -> 3.96 us  [product(): jnp.dot(left, right, precision=lax.Precision.HIGHEST, preferred_element_t...]
    ppermute x12, waiting for transfers between devices: 9.21 us -> 15.3 us  [ordered_reduce_then_gather(): got = lax.ppermute(send, axis, [(i, i ^ 1 << j) for i in range(n)])]
    ppermute x12, starting transfers between devices: 13.4 us -> 9.42 us  [ordered_reduce_then_gather(): got = lax.ppermute(send, axis, [(i, i ^ 1 << j) for i in range(n)])]
    ppermute x4, waiting for transfers between devices: 5.16 us -> 8.47 us  [ordered_reduce_then_gather(): y = y + lax.ppermute(y, axis, [(i, i ^ 1 << top) for i in range(n)])]
    slice x1 -> x2, local copies, waits for them, and re-layouts: 0.07 us -> 2.81 us  [shards(): right_side[1][:, cols]]
    reshape x0 -> x1, local copies, waits for them, and re-layouts: none -> 2.74 us  [shards(): column_major = solved_before.reshape(solved_before.shape[0], 2, width)]
    ppermute x4, starting transfers between devices: 8.5 us -> 6.32 us  [ordered_reduce_then_gather(): y = y + lax.ppermute(y, axis, [(i, i ^ 1 << top) for i in range(n)])]
  transfers between devices with their start and end apart: 29 -> 29, of which waited for: 20 -> 20; matrix products, arithmetic and copies ran while one was open for 17% -> 28% of each run, Pallas kernels for 0% -> 0%
where the time goes in v11:
time: 95.8 us; the launch traced here: 95.6 us
  waiting for transfers between devices  38.8 us (41%)
  starting transfers between devices  25.2 us (26%)
  matrix products  20.3 us (21%)
  local copies, waits for them, and re-layouts  7.89 us (8%)
  other arithmetic  2.8 us (3%)
    dot_general x2, matrix products, split_product(): jnp.einsum('ij,jbk->bik', left, right, precision=lax.Precision.HIGHEST, p...  16.3 us
    ppermute x12, waiting for transfers between devices, ordered_reduce_then_gather(): got = lax.ppermute(send, axis, [(i, i ^ 1 << j) for i in range(n)])  15.3 us
    ppermute x12, waiting for transfers between devices, ordered_reduce_then_gather(): got = lax.ppermute(y, axis, [(i, i ^ 1 << j) for i in range(n)])  15 us
    ppermute x12, starting transfers between devices, ordered_reduce_then_gather(): got = lax.ppermute(send, axis, [(i, i ^ 1 << j) for i in range(n)])  9.42 us
    ppermute x4, waiting for transfers between devices, ordered_reduce_then_gather(): y = y + lax.ppermute(y, axis, [(i, i ^ 1 << top) for i in range(n)])  8.47 us
    ppermute x12, starting transfers between devices, ordered_reduce_then_gather(): got = lax.ppermute(y, axis, [(i, i ^ 1 << j) for i in range(n)])  6.53 us
    ppermute x4, starting transfers between devices, ordered_reduce_then_gather(): y = y + lax.ppermute(y, axis, [(i, i ^ 1 << top) for i in range(n)])  6.32 us
    dot_general x6, matrix products, product(): jnp.dot(left, right, precision=lax.Precision.HIGHEST, preferred_element_t...  3.96 us
  transfers between devices with their start and end apart: 29, of which 20 were waited for; matrix products, arithmetic and copies ran while one was open for 28% of the time, Pallas kernels for 0%

profile of v11, /device:TPU:0, one launch (start us, length us, event | category | flops | bytes accessed | tf_op | source)
XLA Modules:
  0.0 95.6 jit_solution(17533896527533632004)
XLA Ops:
  0.0 2.9 %collective-permute-start = (f32[1,1,2,64,512]{4,3,2,1,0:T(8,128)}, f32[1,1,2,64,512]{4,3,2,1,0:T(8,128)}, u32[]{:S(2)}, u32[]{:S(2)}) collective-permute-start(f32[1,1,2,64,512]{4,3,2,1,0:T(8,128)} %bitcast.74), channel_id=1, source_target_pairs={{0,1},{1,0},{2,3},{3,2},{4,5},{5,4},{6,7},{7,6},{8,9},{9,8},{10,11... | collective-permute-start | bytes 786440 | tf_op jit(solution)/shard_map/ppermute | solution.py:34
  2.9 2.7 %reshape.7 = f32[1024,2,128]{2,1,0:T(2,128)} reshape(f32[1024,256]{1,0:T(8,128)} %param.6) | data formatting | bytes 2097152 | tf_op jit(solution)/shard_map/reshape | solution.py:125
  5.7 2.7 %fusion.42 = (f32[1,1024,256]{2,1,0:T(8,128)S(1)}, f32[1,1024,256]{2,1,0:T(8,128)}) fusion(f32[2,1024,256]{2,1,0:T(8,128)} %param.7), kind=kLoop, calls=%fused_computation.109 | loop fusion | bytes 4194304 | tf_op jit(solution)/shard_map/slice | solution.py:157
  8.8 1.6 %copy.10 = f32[1,1024,256]{1,2,0:T(8,128)S(1)} copy(f32[1,1024,256]{2,1,0:T(8,128)} %get-tuple-element.20) | data formatting | bytes 2097152
  10.4 9.1 %fusion.6 = f32[2,1024,128]{1,2,0:T(8,128)S(1)} fusion(f32[2,1024,1024]{2,1,0:T(8,128)} %param.5, f32[1024,256]{1,0:T(8,128)S(1)} %copy-done.1), kind=kOutput, calls=%fused_computation.6 | convolution fusion | flops 3221225472 | bytes 6291456 | tf_op jit(solution)/shard_map/ij,jbk->bik/dot_general | solution.py:128
  19.5 1.0 %select_bitcast_fusion.1 = (f32[1,1,1,2,64,512]{5,4,3,2,1,0:T(8,128)S(1)}, f32[1,1,1,2,64,512]{5,4,3,2,1,0:T(8,128)S(1)}) fusion(f32[1,1,2,64,512]{4,3,2,1,0:T(8,128)} %collective-permute-done, pred[]{:T(512)S(6)} %eq.8, f32[2,64,512]{2,1,0:T(8,128)S(1)} %copy-done.3), kind=kLoop, calls=%fused_computation.51 | loop fusion | flops 131072 | bytes 1048577 | tf_op jit(solution)/shard_map/stack | solution.py:37
  22.3 1.6 %collective-permute-start.9 = (f32[256,128]{0,1:T(8,128)S(1)}, f32[256,128]{0,1:T(8,128)S(1)}, u32[]{:S(2)}, u32[]{:S(2)}) collective-permute-start(f32[256,128]{0,1:T(8,128)S(1)} %constant_dynamic-slice_fusion.7), channel_id=1, source_target_pairs={{0,8},{2,10},{4,12},{6,14},{8,0},{10,2},{12,4},{14,6},{16,24},{18,... | collective-permute-start | bytes 393224 | tf_op jit(solution)/shard_map/ppermute | solution.py:78
  24.0 7.3 %fusion.9 = f32[2,1024,128]{1,2,0:T(8,128)S(1)} fusion(f32[2,1024,1024]{2,1,0:T(8,128)S(1)} %bitcast.71, f32[1024,2,128]{2,1,0:T(2,128)S(1)} %copy-done.2), kind=kOutput, calls=%fused_computation.7 | convolution fusion | flops 3221225472 | bytes 6291456 | tf_op jit(solution)/shard_map/ij,jbk->bik/dot_general | solution.py:128
  31.3 1.6 %collective-permute-start.2 = (f32[256,128]{0,1:T(8,128)S(1)}, f32[256,128]{0,1:T(8,128)S(1)}, u32[]{:S(2)}, u32[]{:S(2)}) collective-permute-start(f32[256,128]{0,1:T(8,128)S(1)} %constant_dynamic-slice_fusion.9), channel_id=1, source_target_pairs={{0,4},{2,6},{4,0},{6,2},{8,12},{10,14},{12,8},{14,10},{16,20},{18,... | collective-permute-start | bytes 393224 | tf_op jit(solution)/shard_map/ppermute | solution.py:78
  33.5 3.8 %collective-permute-done.2 = f32[256,128]{0,1:T(8,128)S(1)} collective-permute-done((f32[256,128]{0,1:T(8,128)S(1)}, f32[256,128]{0,1:T(8,128)S(1)}, u32[]{:S(2)}, u32[]{:S(2)}) %collective-permute-start.2) | collective-permute-done | bytes 131104 | tf_op jit(solution)/shard_map/ppermute | solution.py:78
  38.2 3.5 %collective-permute-done.3 = f32[128,128]{0,1:T(8,128)S(1)} collective-permute-done((f32[128,128]{0,1:T(8,128)S(1)}, f32[128,128]{0,1:T(8,128)S(1)}, u32[]{:S(2)}, u32[]{:S(2)}) %collective-permute-start.3) | collective-permute-done | bytes 65568 | tf_op jit(solution)/shard_map/ppermute | solution.py:78
  41.8 3.1 %collective-permute-start.4 = (f32[128,128]{0,1:T(8,128)S(1)}, f32[128,128]{0,1:T(8,128)S(1)}, u32[]{:S(2)}, u32[]{:S(2)}) collective-permute-start(f32[128,128]{0,1:T(8,128)S(1)} %dynamic-slice_add_fusion.9), channel_id=1, source_target_pairs={{0,16},{2,18},{4,20},{6,22},{8,24},{10,26},{12,28},{14,30},{16,0},... | collective-permute-start | bytes 196616 | tf_op jit(solution)/shard_map/ppermute | solution.py:86
  44.9 2.8 %collective-permute-done.4 = f32[128,128]{0,1:T(8,128)S(1)} collective-permute-done((f32[128,128]{0,1:T(8,128)S(1)}, f32[128,128]{0,1:T(8,128)S(1)}, u32[]{:S(2)}, u32[]{:S(2)}) %collective-permute-start.4) | collective-permute-done | bytes 65568 | tf_op jit(solution)/shard_map/ppermute | solution.py:86
  48.0 2.5 %collective-permute-done.11 = f32[128,128]{0,1:T(8,128)S(1)} collective-permute-done((f32[128,128]{0,1:T(8,128)S(1)}, f32[128,128]{0,1:T(8,128)S(1)}, u32[]{:S(2)}, u32[]{:S(2)}) %collective-permute-start.11) | collective-permute-done | bytes 65568 | tf_op jit(solution)/shard_map/ppermute | solution.py:86
  50.6 1.6 %collective-permute-start.12 = (f32[128,128]{0,1:T(8,128)S(1)}, f32[128,128]{0,1:T(8,128)S(1)}, u32[]{:S(2)}, u32[]{:S(2)}) collective-permute-start(f32[128,128]{0,1:T(8,128)S(1)} %add_subtract_fusion.2), channel_id=1, source_target_pairs={{0,4},{2,6},{4,0},{6,2},{8,12},{10,14},{12,8},{14,10},{16,20},{18,... | collective-permute-start | bytes 196616 | tf_op jit(solution)/shard_map/ppermute | solution.py:90
  52.2 1.6 %collective-permute-start.6 = (f32[256,128]{0,1:T(8,128)S(1)}, f32[256,128]{0,1:T(8,128)S(1)}, u32[]{:S(2)}, u32[]{:S(2)}) collective-permute-start(f32[256,128]{0,1:T(8,128)S(1)} %pad_maximum_fusion.5), channel_id=1, source_target_pairs={{0,4},{2,6},{4,0},{6,2},{8,12},{10,14},{12,8},{14,10},{16,20},{18,... | collective-permute-start | bytes 393224 | tf_op jit(solution)/shard_map/ppermute | solution.py:90
  53.8 1.1 %collective-permute-done.12 = f32[128,128]{0,1:T(8,128)S(1)} collective-permute-done((f32[128,128]{0,1:T(8,128)S(1)}, f32[128,128]{0,1:T(8,128)S(1)}, u32[]{:S(2)}, u32[]{:S(2)}) %collective-permute-start.12) | collective-permute-done | bytes 65568 | tf_op jit(solution)/shard_map/ppermute | solution.py:90
  55.0 2.2 %collective-permute-done.6 = f32[256,128]{0,1:T(8,128)S(1)} collective-permute-done((f32[256,128]{0,1:T(8,128)S(1)}, f32[256,128]{0,1:T(8,128)S(1)}, u32[]{:S(2)}, u32[]{:S(2)}) %collective-permute-start.6) | collective-permute-done | bytes 131104 | tf_op jit(solution)/shard_map/ppermute | solution.py:90
  57.4 2.6 %collective-permute-done.13 = f32[256,128]{0,1:T(8,128)S(1)} collective-permute-done((f32[256,128]{0,1:T(8,128)S(1)}, f32[256,128]{0,1:T(8,128)S(1)}, u32[]{:S(2)}, u32[]{:S(2)}) %collective-permute-start.13) | collective-permute-done | bytes 131104 | tf_op jit(solution)/shard_map/ppermute | solution.py:90
  65.8 1.6 %collective-permute-start.16 = (f32[256,128]{0,1:T(8,128)S(1)}, f32[256,128]{0,1:T(8,128)S(1)}, u32[]{:S(2)}, u32[]{:S(2)}) collective-permute-start(f32[256,128]{0,1:T(8,128)S(1)} %constant_dynamic-slice_fusion.4), channel_id=1, source_target_pairs={{0,4},{2,6},{4,0},{6,2},{8,12},{10,14},{12,8},{14,10},{16,20},{18,... | collective-permute-start | bytes 393224 | tf_op jit(solution)/shard_map/ppermute | solution.py:78
  67.3 3.6 %collective-permute-done.23 = f32[256,128]{0,1:T(8,128)S(1)} collective-permute-done((f32[256,128]{0,1:T(8,128)S(1)}, f32[256,128]{0,1:T(8,128)S(1)}, u32[]{:S(2)}, u32[]{:S(2)}) %collective-permute-start.23) | collective-permute-done | bytes 131104 | tf_op jit(solution)/shard_map/ppermute | solution.py:78
  71.0 1.6 %collective-permute-start.24 = (f32[128,128]{0,1:T(8,128)S(1)}, f32[128,128]{0,1:T(8,128)S(1)}, u32[]{:S(2)}, u32[]{:S(2)}) collective-permute-start(f32[128,128]{0,1:T(8,128)S(1)} %constant_dynamic-slice_fusion), channel_id=1, source_target_pairs={{0,4},{2,6},{4,0},{6,2},{8,12},{10,14},{12,8},{14,10},{16,20},{18,... | collective-permute-start | bytes 196616 | tf_op jit(solution)/shard_map/ppermute | solution.py:78
  73.0 2.3 %collective-permute-done.24 = f32[128,128]{0,1:T(8,128)S(1)} collective-permute-done((f32[128,128]{0,1:T(8,128)S(1)}, f32[128,128]{0,1:T(8,128)S(1)}, u32[]{:S(2)}, u32[]{:S(2)}) %collective-permute-start.24) | collective-permute-done | bytes 65568 | tf_op jit(solution)/shard_map/ppermute | solution.py:78
  75.4 2.0 %collective-permute-start.25 = (f32[128,128]{0,1:T(8,128)S(1)}, f32[128,128]{0,1:T(8,128)S(1)}, u32[]{:S(2)}, u32[]{:S(2)}) collective-permute-start(f32[128,128]{0,1:T(8,128)S(1)} %dynamic-slice_add_fusion.6), channel_id=1, source_target_pairs={{0,16},{2,18},{4,20},{6,22},{8,24},{10,26},{12,28},{14,30},{16,0},... | collective-permute-start | bytes 196616 | tf_op jit(solution)/shard_map/ppermute | solution.py:86
  77.4 1.2 %collective-permute-start.18 = (f32[128,128]{0,1:T(8,128)S(1)}, f32[128,128]{0,1:T(8,128)S(1)}, u32[]{:S(2)}, u32[]{:S(2)}) collective-permute-start(f32[128,128]{0,1:T(8,128)S(1)} %dynamic-slice_add_fusion.7), channel_id=1, source_target_pairs={{0,16},{2,18},{4,20},{6,22},{8,24},{10,26},{12,28},{14,30},{16,0},... | collective-permute-start | bytes 196616 | tf_op jit(solution)/shard_map/ppermute | solution.py:86
  78.5 3.1 %collective-permute-done.25 = f32[128,128]{0,1:T(8,128)S(1)} collective-permute-done((f32[128,128]{0,1:T(8,128)S(1)}, f32[128,128]{0,1:T(8,128)S(1)}, u32[]{:S(2)}, u32[]{:S(2)}) %collective-permute-start.25) | collective-permute-done | bytes 65568 | tf_op jit(solution)/shard_map/ppermute | solution.py:86
  81.7 1.3 %collective-permute-start.26 = (f32[128,128]{0,1:T(8,128)S(1)}, f32[128,128]{0,1:T(8,128)S(1)}, u32[]{:S(2)}, u32[]{:S(2)}) collective-permute-start(f32[128,128]{0,1:T(8,128)S(1)} %add_subtract_fusion), channel_id=1, source_target_pairs={{0,4},{2,6},{4,0},{6,2},{8,12},{10,14},{12,8},{14,10},{16,20},{18,... | collective-permute-start | bytes 196616 | tf_op jit(solution)/shard_map/ppermute | solution.py:90
  83.2 2.8 %collective-permute-done.26 = f32[128,128]{0,1:T(8,128)S(1)} collective-permute-done((f32[128,128]{0,1:T(8,128)S(1)}, f32[128,128]{0,1:T(8,128)S(1)}, u32[]{:S(2)}, u32[]{:S(2)}) %collective-permute-start.26) | collective-permute-done | bytes 65568 | tf_op jit(solution)/shard_map/ppermute | solution.py:90
  86.2 1.3 %collective-permute-done.19 = f32[128,128]{0,1:T(8,128)S(1)} collective-permute-done((f32[128,128]{0,1:T(8,128)S(1)}, f32[128,128]{0,1:T(8,128)S(1)}, u32[]{:S(2)}, u32[]{:S(2)}) %collective-permute-start.19) | collective-permute-done | bytes 65568 | tf_op jit(solution)/shard_map/ppermute | solution.py:90
  87.5 1.5 %collective-permute-start.20 = (f32[256,128]{0,1:T(8,128)S(1)}, f32[256,128]{0,1:T(8,128)S(1)}, u32[]{:S(2)}, u32[]{:S(2)}) collective-permute-start(f32[256,128]{0,1:T(8,128)S(1)} %pad_maximum_fusion.7), channel_id=1, source_target_pairs={{0,4},{2,6},{4,0},{6,2},{8,12},{10,14},{12,8},{14,10},{16,20},{18,... | collective-permute-start | bytes 393224 | tf_op jit(solution)/shard_map/ppermute | solution.py:90
  89.0 2.1 %collective-permute-done.27 = f32[256,128]{0,1:T(8,128)S(1)} collective-permute-done((f32[256,128]{0,1:T(8,128)S(1)}, f32[256,128]{0,1:T(8,128)S(1)}, u32[]{:S(2)}, u32[]{:S(2)}) %collective-permute-start.27) | collective-permute-done | bytes 131104 | tf_op jit(solution)/shard_map/ppermute | solution.py:90
  91.2 1.3 %collective-permute-done.20 = f32[256,128]{0,1:T(8,128)S(1)} collective-permute-done((f32[256,128]{0,1:T(8,128)S(1)}, f32[256,128]{0,1:T(8,128)S(1)}, u32[]{:S(2)}, u32[]{:S(2)}) %collective-permute-start.20) | collective-permute-done | bytes 131104 | tf_op jit(solution)/shard_map/ppermute | solution.py:90
  (107 shorter events, 13.9 us)
Async XLA Ops:
  0.0 62.4 %copy-start = (f32[1024,64]{0,1:T(8,128)S(1)}, f32[1024,64]{0,1:T(8,128)}, u32[]{:S(2)}) copy-start(f32[1024,64]{0,1:T(8,128)} %param.9) | copy-start | bytes 786436
  0.0 19.4 %collective-permute-start = (f32[1,1,2,64,512]{4,3,2,1,0:T(8,128)}, f32[1,1,2,64,512]{4,3,2,1,0:T(8,128)}, u32[]{:S(2)}, u32[]{:S(2)}) collective-permute-start(f32[1,1,2,64,512]{4,3,2,1,0:T(8,128)} %bitcast.74), channel_id=1, source_target_pairs={{0,1},{1,0},{2,3},{3,2},{4,5},{5,4},{6,7},{7,6},{8,9},{9,8},{10,11... | collective-permute-start | bytes 786440 | tf_op jit(solution)/shard_map/ppermute | solution.py:34
  10.4 9.1 %copy-start.3 = (f32[2,64,512]{2,1,0:T(8,128)S(1)}, f32[2,64,512]{2,1,0:T(8,128)}, u32[]{:S(2)}) copy-start(f32[2,64,512]{2,1,0:T(8,128)} %param.8) | copy-start | bytes 786436
  10.4 13.6 %slice-start = ((s8[8388608]{0:T(1024)(128)(4,1)}), s8[4194304]{0:T(1024)(128)(4,1)S(1)}, s32[]{:S(2)}) async-start(s8[8388608]{0:T(1024)(128)(4,1)} %bitcast.70), calls=%async_computation | async-start | bytes 8388608
  20.6 1.6 %collective-permute-start.8 = (f32[512,128]{0,1:T(8,128)S(1)}, f32[512,128]{0,1:T(8,128)S(1)}, u32[]{:S(2)}, u32[]{:S(2)}) collective-permute-start(f32[512,128]{0,1:T(8,128)S(1)} %dynamic-slice_bitcast_fusion), channel_id=1, source_target_pairs={{0,2},{2,0},{4,6},{6,4},{8,10},{10,8},{12,14},{14,12},{16,18},{18,... | collective-permute-start | bytes 786440 | tf_op jit(solution)/shard_map/ppermute | solution.py:78
  20.8 3.1 %collective-permute-start.1 = (f32[512,128]{0,1:T(8,128)S(1)}, f32[512,128]{0,1:T(8,128)S(1)}, u32[]{:S(2)}, u32[]{:S(2)}) collective-permute-start(f32[512,128]{0,1:T(8,128)S(1)} %dynamic-slice_bitcast_fusion.1), channel_id=1, source_target_pairs={{0,2},{2,0},{4,6},{6,4},{8,10},{10,8},{12,14},{14,12},{16,18},{18,... | collective-permute-start | bytes 786440 | tf_op jit(solution)/shard_map/ppermute | solution.py:78
  22.3 10.6 %collective-permute-start.9 = (f32[256,128]{0,1:T(8,128)S(1)}, f32[256,128]{0,1:T(8,128)S(1)}, u32[]{:S(2)}, u32[]{:S(2)}) collective-permute-start(f32[256,128]{0,1:T(8,128)S(1)} %constant_dynamic-slice_fusion.7), channel_id=1, source_target_pairs={{0,8},{2,10},{4,12},{6,14},{8,0},{10,2},{12,4},{14,6},{16,24},{18,... | collective-permute-start | bytes 393224 | tf_op jit(solution)/shard_map/ppermute | solution.py:78
  31.3 6.0 %collective-permute-start.2 = (f32[256,128]{0,1:T(8,128)S(1)}, f32[256,128]{0,1:T(8,128)S(1)}, u32[]{:S(2)}, u32[]{:S(2)}) collective-permute-start(f32[256,128]{0,1:T(8,128)S(1)} %constant_dynamic-slice_fusion.9), channel_id=1, source_target_pairs={{0,4},{2,6},{4,0},{6,2},{8,12},{10,14},{12,8},{14,10},{16,20},{18,... | collective-permute-start | bytes 393224 | tf_op jit(solution)/shard_map/ppermute | solution.py:78
  33.0 11.9 %collective-permute-start.10 = (f32[128,128]{0,1:T(8,128)S(1)}, f32[128,128]{0,1:T(8,128)S(1)}, u32[]{:S(2)}, u32[]{:S(2)}) collective-permute-start(f32[128,128]{0,1:T(8,128)S(1)} %constant_dynamic-slice_fusion.6), channel_id=1, source_target_pairs={{0,4},{2,6},{4,0},{6,2},{8,12},{10,14},{12,8},{14,10},{16,20},{18,... | collective-permute-start | bytes 196616 | tf_op jit(solution)/shard_map/ppermute | solution.py:78
  37.4 4.3 %collective-permute-start.3 = (f32[128,128]{0,1:T(8,128)S(1)}, f32[128,128]{0,1:T(8,128)S(1)}, u32[]{:S(2)}, u32[]{:S(2)}) collective-permute-start(f32[128,128]{0,1:T(8,128)S(1)} %constant_dynamic-slice_fusion.8), channel_id=1, source_target_pairs={{0,8},{2,10},{4,12},{6,14},{8,0},{10,2},{12,4},{14,6},{16,24},{18,... | collective-permute-start | bytes 196616 | tf_op jit(solution)/shard_map/ppermute | solution.py:78
  41.8 6.0 %collective-permute-start.4 = (f32[128,128]{0,1:T(8,128)S(1)}, f32[128,128]{0,1:T(8,128)S(1)}, u32[]{:S(2)}, u32[]{:S(2)}) collective-permute-start(f32[128,128]{0,1:T(8,128)S(1)} %dynamic-slice_add_fusion.9), channel_id=1, source_target_pairs={{0,16},{2,18},{4,20},{6,22},{8,24},{10,26},{12,28},{14,30},{16,0},... | collective-permute-start | bytes 196616 | tf_op jit(solution)/shard_map/ppermute | solution.py:86
  44.8 5.6 %collective-permute-start.11 = (f32[128,128]{0,1:T(8,128)S(1)}, f32[128,128]{0,1:T(8,128)S(1)}, u32[]{:S(2)}, u32[]{:S(2)}) collective-permute-start(f32[128,128]{0,1:T(8,128)S(1)} %dynamic-slice_add_fusion.8), channel_id=1, source_target_pairs={{0,16},{2,18},{4,20},{6,22},{8,24},{10,26},{12,28},{14,30},{16,0},... | collective-permute-start | bytes 196616 | tf_op jit(solution)/shard_map/ppermute | solution.py:86
  47.9 4.3 %collective-permute-start.5 = (f32[128,128]{0,1:T(8,128)S(1)}, f32[128,128]{0,1:T(8,128)S(1)}, u32[]{:S(2)}, u32[]{:S(2)}) collective-permute-start(f32[128,128]{0,1:T(8,128)S(1)} %add_subtract_fusion.3), channel_id=1, source_target_pairs={{0,8},{2,10},{4,12},{6,14},{8,0},{10,2},{12,4},{14,6},{16,24},{18,... | collective-permute-start | bytes 196616 | tf_op jit(solution)/shard_map/ppermute | solution.py:90
  50.6 4.3 %collective-permute-start.12 = (f32[128,128]{0,1:T(8,128)S(1)}, f32[128,128]{0,1:T(8,128)S(1)}, u32[]{:S(2)}, u32[]{:S(2)}) collective-permute-start(f32[128,128]{0,1:T(8,128)S(1)} %add_subtract_fusion.2), channel_id=1, source_target_pairs={{0,4},{2,6},{4,0},{6,2},{8,12},{10,14},{12,8},{14,10},{16,20},{18,... | collective-permute-start | bytes 196616 | tf_op jit(solution)/shard_map/ppermute | solution.py:90
  52.2 5.0 %collective-permute-start.6 = (f32[256,128]{0,1:T(8,128)S(1)}, f32[256,128]{0,1:T(8,128)S(1)}, u32[]{:S(2)}, u32[]{:S(2)}) collective-permute-start(f32[256,128]{0,1:T(8,128)S(1)} %pad_maximum_fusion.5), channel_id=1, source_target_pairs={{0,4},{2,6},{4,0},{6,2},{8,12},{10,14},{12,8},{14,10},{16,20},{18,... | collective-permute-start | bytes 393224 | tf_op jit(solution)/shard_map/ppermute | solution.py:90
  54.9 5.0 %collective-permute-start.13 = (f32[256,128]{0,1:T(8,128)S(1)}, f32[256,128]{0,1:T(8,128)S(1)}, u32[]{:S(2)}, u32[]{:S(2)}) collective-permute-start(f32[256,128]{0,1:T(8,128)S(1)} %pad_maximum_fusion.6), channel_id=1, source_target_pairs={{0,8},{2,10},{4,12},{6,14},{8,0},{10,2},{12,4},{14,6},{16,24},{18,... | collective-permute-start | bytes 393224 | tf_op jit(solution)/shard_map/ppermute | solution.py:90
  57.3 2.8 %collective-permute-start.7 = (f32[512,128]{0,1:T(8,128)S(1)}, f32[512,128]{0,1:T(8,128)S(1)}, u32[]{:S(2)}, u32[]{:S(2)}) collective-permute-start(f32[512,128]{0,1:T(8,128)S(1)} %pad_maximum_fusion.1), channel_id=1, source_target_pairs={{0,2},{2,0},{4,6},{6,4},{8,10},{10,8},{12,14},{14,12},{16,18},{18,... | collective-permute-start | bytes 786440 | tf_op jit(solution)/shard_map/ppermute | solution.py:90
  60.0 1.6 %collective-permute-start.14 = (f32[512,128]{0,1:T(8,128)S(1)}, f32[512,128]{0,1:T(8,128)S(1)}, u32[]{:S(2)}, u32[]{:S(2)}) collective-permute-start(f32[512,128]{0,1:T(8,128)S(1)} %pad_maximum_fusion.2), channel_id=1, source_target_pairs={{0,2},{2,0},{4,6},{6,4},{8,10},{10,8},{12,14},{14,12},{16,18},{18,... | collective-permute-start | bytes 786440 | tf_op jit(solution)/shard_map/ppermute | solution.py:90
  63.7 1.6 %collective-permute-start.22 = (f32[512,128]{0,1:T(8,128)S(1)}, f32[512,128]{0,1:T(8,128)S(1)}, u32[]{:S(2)}, u32[]{:S(2)}) collective-permute-start(f32[512,128]{0,1:T(8,128)S(1)} %constant_dynamic-slice_fusion.2), channel_id=1, source_target_pairs={{0,2},{2,0},{4,6},{6,4},{8,10},{10,8},{12,14},{14,12},{16,18},{18,... | collective-permute-start | bytes 786440 | tf_op jit(solution)/shard_map/ppermute | solution.py:78
  64.0 1.7 %collective-permute-start.15 = (f32[512,128]{0,1:T(8,128)S(1)}, f32[512,128]{0,1:T(8,128)S(1)}, u32[]{:S(2)}, u32[]{:S(2)}) collective-permute-start(f32[512,128]{0,1:T(8,128)S(1)} %constant_dynamic-slice_fusion.5), channel_id=1, source_target_pairs={{0,2},{2,0},{4,6},{6,4},{8,10},{10,8},{12,14},{14,12},{16,18},{18,... | collective-permute-start | bytes 786440 | tf_op jit(solution)/shard_map/ppermute | solution.py:78
  65.4 5.6 %collective-permute-start.23 = (f32[256,128]{0,1:T(8,128)S(1)}, f32[256,128]{0,1:T(8,128)S(1)}, u32[]{:S(2)}, u32[]{:S(2)}) collective-permute-start(f32[256,128]{0,1:T(8,128)S(1)} %constant_dynamic-slice_fusion.1), channel_id=1, source_target_pairs={{0,8},{2,10},{4,12},{6,14},{8,0},{10,2},{12,4},{14,6},{16,24},{18,... | collective-permute-start | bytes 393224 | tf_op jit(solution)/shard_map/ppermute | solution.py:78
  65.8 6.9 %collective-permute-start.16 = (f32[256,128]{0,1:T(8,128)S(1)}, f32[256,128]{0,1:T(8,128)S(1)}, u32[]{:S(2)}, u32[]{:S(2)}) collective-permute-start(f32[256,128]{0,1:T(8,128)S(1)} %constant_dynamic-slice_fusion.4), channel_id=1, source_target_pairs={{0,4},{2,6},{4,0},{6,2},{8,12},{10,14},{12,8},{14,10},{16,20},{18,... | collective-permute-start | bytes 393224 | tf_op jit(solution)/shard_map/ppermute | solution.py:78
  71.0 4.3 %collective-permute-start.24 = (f32[128,128]{0,1:T(8,128)S(1)}, f32[128,128]{0,1:T(8,128)S(1)}, u32[]{:S(2)}, u32[]{:S(2)}) collective-permute-start(f32[128,128]{0,1:T(8,128)S(1)} %constant_dynamic-slice_fusion), channel_id=1, source_target_pairs={{0,4},{2,6},{4,0},{6,2},{8,12},{10,14},{12,8},{14,10},{16,20},{18,... | collective-permute-start | bytes 196616 | tf_op jit(solution)/shard_map/ppermute | solution.py:78
  72.7 4.7 %collective-permute-start.17 = (f32[128,128]{0,1:T(8,128)S(1)}, f32[128,128]{0,1:T(8,128)S(1)}, u32[]{:S(2)}, u32[]{:S(2)}) collective-permute-start(f32[128,128]{0,1:T(8,128)S(1)} %constant_dynamic-slice_fusion.3), channel_id=1, source_target_pairs={{0,8},{2,10},{4,12},{6,14},{8,0},{10,2},{12,4},{14,6},{16,24},{18,... | collective-permute-start | bytes 196616 | tf_op jit(solution)/shard_map/ppermute | solution.py:78
  75.4 6.2 %collective-permute-start.25 = (f32[128,128]{0,1:T(8,128)S(1)}, f32[128,128]{0,1:T(8,128)S(1)}, u32[]{:S(2)}, u32[]{:S(2)}) collective-permute-start(f32[128,128]{0,1:T(8,128)S(1)} %dynamic-slice_add_fusion.6), channel_id=1, source_target_pairs={{0,16},{2,18},{4,20},{6,22},{8,24},{10,26},{12,28},{14,30},{16,0},... | collective-permute-start | bytes 196616 | tf_op jit(solution)/shard_map/ppermute | solution.py:86
  77.4 5.7 %collective-permute-start.18 = (f32[128,128]{0,1:T(8,128)S(1)}, f32[128,128]{0,1:T(8,128)S(1)}, u32[]{:S(2)}, u32[]{:S(2)}) collective-permute-start(f32[128,128]{0,1:T(8,128)S(1)} %dynamic-slice_add_fusion.7), channel_id=1, source_target_pairs={{0,16},{2,18},{4,20},{6,22},{8,24},{10,26},{12,28},{14,30},{16,0},... | collective-permute-start | bytes 196616 | tf_op jit(solution)/shard_map/ppermute | solution.py:86
  81.7 4.3 %collective-permute-start.26 = (f32[128,128]{0,1:T(8,128)S(1)}, f32[128,128]{0,1:T(8,128)S(1)}, u32[]{:S(2)}, u32[]{:S(2)}) collective-permute-start(f32[128,128]{0,1:T(8,128)S(1)} %add_subtract_fusion), channel_id=1, source_target_pairs={{0,4},{2,6},{4,0},{6,2},{8,12},{10,14},{12,8},{14,10},{16,20},{18,... | collective-permute-start | bytes 196616 | tf_op jit(solution)/shard_map/ppermute | solution.py:90
  83.1 4.3 %collective-permute-start.19 = (f32[128,128]{0,1:T(8,128)S(1)}, f32[128,128]{0,1:T(8,128)S(1)}, u32[]{:S(2)}, u32[]{:S(2)}) collective-permute-start(f32[128,128]{0,1:T(8,128)S(1)} %add_subtract_fusion.1), channel_id=1, source_target_pairs={{0,8},{2,10},{4,12},{6,14},{8,0},{10,2},{12,4},{14,6},{16,24},{18,... | collective-permute-start | bytes 196616 | tf_op jit(solution)/shard_map/ppermute | solution.py:90
  86.1 5.0 %collective-permute-start.27 = (f32[256,128]{0,1:T(8,128)S(1)}, f32[256,128]{0,1:T(8,128)S(1)}, u32[]{:S(2)}, u32[]{:S(2)}) collective-permute-start(f32[256,128]{0,1:T(8,128)S(1)} %pad_maximum_fusion.8), channel_id=1, source_target_pairs={{0,8},{2,10},{4,12},{6,14},{8,0},{10,2},{12,4},{14,6},{16,24},{18,... | collective-permute-start | bytes 393224 | tf_op jit(solution)/shard_map/ppermute | solution.py:90
  87.5 5.0 %collective-permute-start.20 = (f32[256,128]{0,1:T(8,128)S(1)}, f32[256,128]{0,1:T(8,128)S(1)}, u32[]{:S(2)}, u32[]{:S(2)}) collective-permute-start(f32[256,128]{0,1:T(8,128)S(1)} %pad_maximum_fusion.7), channel_id=1, source_target_pairs={{0,4},{2,6},{4,0},{6,2},{8,12},{10,14},{12,8},{14,10},{16,20},{18,... | collective-permute-start | bytes 393224 | tf_op jit(solution)/shard_map/ppermute | solution.py:90
  91.2 1.6 %collective-permute-start.28 = (f32[512,128]{0,1:T(8,128)S(1)}, f32[512,128]{0,1:T(8,128)S(1)}, u32[]{:S(2)}, u32[]{:S(2)}) collective-permute-start(f32[512,128]{0,1:T(8,128)S(1)} %pad_maximum_fusion.4), channel_id=1, source_target_pairs={{0,2},{2,0},{4,6},{6,4},{8,10},{10,8},{12,14},{14,12},{16,18},{18,... | collective-permute-start | bytes 786440 | tf_op jit(solution)/shard_map/ppermute | solution.py:90
  92.6 1.6 %collective-permute-start.21 = (f32[512,128]{0,1:T(8,128)S(1)}, f32[512,128]{0,1:T(8,128)S(1)}, u32[]{:S(2)}, u32[]{:S(2)}) collective-permute-start(f32[512,128]{0,1:T(8,128)S(1)} %pad_maximum_fusion.3), channel_id=1, source_target_pairs={{0,2},{2,0},{4,6},{6,4},{8,10},{10,8},{12,14},{14,12},{16,18},{18,... | collective-permute-start | bytes 786440 | tf_op jit(solution)/shard_map/ppermute | solution.py:90
  (3 other events, 11.8 us)

commit v12 on v9

--- a/solution.py
+++ b/solution.py
@@ -66,7 +66,7 @@
     return y.reshape(x.shape), riders
 
 
-def ordered_reduce_then_gather(x, right, axis, n, order, riders=None):
+def ordered_reduce_then_gather(x, right, axis, n, order, riders=None, hold=None):
     me = lax.axis_index(axis)
     y, r = x, right
     for step, j in enumerate(order[:-1]):
@@ -79,6 +79,9 @@
         if step == 1 and riders is not None:
             got, riders = lax.optimization_barrier((got, riders))
         y = keep + got
+        if step == 0 and hold is not None:
+            y, held = lax.optimization_barrier((y, hold[0]))
+            riders = (hold[1](held), riders)
     top = order[-1]
     y = y + lax.ppermute(y, axis, [(i, i ^ (1 << top)) for i in range(n)])
     y = r - y
@@ -118,9 +121,10 @@
 
         first_sum = product(factor_panel[0], solved_before)
         first_sum, inverse_pieces = lax.optimization_barrier((first_sum, inverse_pieces))
-        inverse_full = jnp.concatenate(list(inverse_pieces), axis=2)
-        panel_sum = product(factor_panel[1], solved_before)
-        if power_of_two and n >= 4:
+        chained = power_of_two and n >= 4
+        if not chained:
+            panel_sum = product(factor_panel[1], solved_before)
+        if chained:
             k = n.bit_length() - 1
             orders = (list(range(k)), [0, 2, 1] + list(range(3, k)) if k >= 3 else list(range(k)))
             width = first_sum.shape[1] // 2
@@ -129,7 +133,8 @@
             for chain, (order, cols) in enumerate(zip(orders, columns)):
                 remains, got_riders = ordered_reduce_then_gather(
                     first_sum[:, cols], right_side[0][:, cols], "blk", n, order,
-                    (panel_sum, inverse_pieces) if chain == 0 else None,
+                    inverse_pieces if chain == 0 else None,
+                    (solved_before, lambda held: product(factor_panel[1], held)) if chain == 0 else None,
                 )
                 if chain == 0:
                     panel_sum, inverse_pieces = got_riders

time: 81.5 us -> 76.8 us (0.942)
  starting transfers between devices: 32.8 us -> 26.3 us
  waiting for transfers between devices: 29.1 us -> 33.6 us
  matrix products: 14.2 us -> 12.5 us
  other arithmetic: 2.41 us -> 1.47 us
    ppermute x12, starting transfers between devices: 13.4 us -> 10.3 us  [ordered_reduce_then_gather(): got = lax.ppermute(send, axis, [(i, i ^ 1 << j) for i in range(n)])]
    ppermute x4, starting transfers between devices: 8.5 us -> 6.59 us  [ordered_reduce_then_gather(): y = y + lax.ppermute(y, axis, [(i, i ^ 1 << top) for i in range(n)])]
    ppermute x4, waiting for transfers between devices: 5.16 us -> 6.99 us  [ordered_reduce_then_gather(): y = y + lax.ppermute(y, axis, [(i, i ^ 1 << top) for i in range(n)])]
    dot_general x8, matrix products: 14.2 us -> 12.5 us  [product(): jnp.dot(left, right, precision=lax.Precision.HIGHEST, preferred_element_t...]
    ppermute x12, waiting for transfers between devices: 14.8 us -> 16.4 us  [ordered_reduce_then_gather(): got = lax.ppermute(y, axis, [(i, i ^ 1 << j) for i in range(n)])]
    ppermute x12, starting transfers between devices: 8.01 us -> 6.44 us  [ordered_reduce_then_gather(): got = lax.ppermute(y, axis, [(i, i ^ 1 << j) for i in range(n)])]
    ppermute x12, waiting for transfers between devices: 9.21 us -> 10.3 us  [ordered_reduce_then_gather(): got = lax.ppermute(send, axis, [(i, i ^ 1 << j) for i in range(n)])]
    another operation x1, other arithmetic: 0.99 us -> 0.05 us  [doubling_gather(): y = jnp.stack([low, high], 1).reshape((-1,) + x.shape)]
  transfers between devices with their start and end apart: 29 -> 29, of which waited for: 20 -> 21; matrix products, arithmetic and copies ran while one was open for 17% -> 16% of each run, Pallas kernels for 0% -> 0%
where the time goes in v12:
time: 76.8 us; the launch traced here: 76.6 us
  waiting for transfers between devices  33.6 us (44%)
  starting transfers between devices  26.3 us (34%)
  matrix products  12.5 us (16%)
  local copies, waits for them, and re-layouts  2.18 us (3%)
  other arithmetic  1.47 us (2%)
    ppermute x12, waiting for transfers between devices, ordered_reduce_then_gather(): got = lax.ppermute(y, axis, [(i, i ^ 1 << j) for i in range(n)])  16.4 us
    dot_general x8, matrix products, product(): jnp.dot(left, right, precision=lax.Precision.HIGHEST, preferred_element_t...  12.5 us
    ppermute x12, starting transfers between devices, ordered_reduce_then_gather(): got = lax.ppermute(send, axis, [(i, i ^ 1 << j) for i in range(n)])  10.3 us
    ppermute x12, waiting for transfers between devices, ordered_reduce_then_gather(): got = lax.ppermute(send, axis, [(i, i ^ 1 << j) for i in range(n)])  10.3 us
    ppermute x4, waiting for transfers between devices, ordered_reduce_then_gather(): y = y + lax.ppermute(y, axis, [(i, i ^ 1 << top) for i in range(n)])  6.99 us
    ppermute x4, starting transfers between devices, ordered_reduce_then_gather(): y = y + lax.ppermute(y, axis, [(i, i ^ 1 << top) for i in range(n)])  6.59 us
    ppermute x12, starting transfers between devices, ordered_reduce_then_gather(): got = lax.ppermute(y, axis, [(i, i ^ 1 << j) for i in range(n)])  6.44 us
    ppermute x1, starting transfers between devices, doubling_gather(): got = lax.ppermute(y, axis, [(i, i ^ 1 << j) for i in range(n)])  2.94 us
  transfers between devices with their start and end apart: 29, of which 21 were waited for; matrix products, arithmetic and copies ran while one was open for 16% of the time, Pallas kernels for 0%

profile of v12, /device:TPU:0, one launch (start us, length us, event | category | flops | bytes accessed | tf_op | source)
XLA Modules:
  0.0 76.6 jit_solution(10894405519290591321)
XLA Ops:
  0.0 2.9 %collective-permute-start = (f32[1,1,2,64,512]{4,3,2,1,0:T(8,128)}, f32[1,1,2,64,512]{4,3,2,1,0:T(8,128)S(1)}, u32[]{:S(2)}, u32[]{:S(2)}) collective-permute-start(f32[1,1,2,64,512]{4,3,2,1,0:T(8,128)} %bitcast.49), channel_id=1, source_target_pairs={{0,1},{1,0},{2,3},{3,2},{4,5},{5,4},{6,7},{7,6},{8,9},{9,8},{10,11... | collective-permute-start | bytes 786440 | tf_op jit(solution)/shard_map/ppermute | solution.py:34
  2.9 5.3 %fusion.2 = f32[1024,256]{1,0:T(8,128)S(1)} fusion(f32[1024,256]{1,0:T(8,128)S(1)} %copy-done, f32[2,1024,1024]{2,1,0:T(8,128)} %param.5), kind=kOutput, calls=%fused_computation.2 | convolution fusion | flops 3221225472 | bytes 6291456 | tf_op jit(solution)/shard_map/dot_general | solution.py:8
  8.2 1.7 %slice_bitcast_fusion = (f32[1024,256]{1,0:T(8,128)S(1)}, f32[1024,256]{1,0:T(8,128)S(1)}) fusion(f32[2,1024,256]{2,1,0:T(8,128)} %param.7), kind=kLoop, calls=%fused_computation.9 | loop fusion | bytes 4194304 | tf_op jit(solution)/shard_map/squeeze | solution.py:147
  10.9 0.9 %collective-permute-done.8 = f32[512,128]{1,0:T(8,128)S(1)} collective-permute-done((f32[512,128]{1,0:T(8,128)S(1)}, f32[512,128]{1,0:T(8,128)S(1)}, u32[]{:S(2)}, u32[]{:S(2)}) %collective-permute-start.8) | collective-permute-done | bytes 262176 | tf_op jit(solution)/shard_map/ppermute | solution.py:78
  11.8 1.6 %collective-permute-start.9 = (f32[256,128]{1,0:T(8,128)S(1)}, f32[256,128]{1,0:T(8,128)S(1)}, u32[]{:S(2)}, u32[]{:S(2)}) collective-permute-start(f32[256,128]{1,0:T(8,128)S(1)} %constant_dynamic-slice_fusion.7), channel_id=1, source_target_pairs={{0,8},{2,10},{4,12},{6,14},{8,0},{10,2},{12,4},{14,6},{16,24},{18,... | collective-permute-start | bytes 393224 | tf_op jit(solution)/shard_map/ppermute | solution.py:78
  13.5 1.6 %collective-permute-start.2 = (f32[256,128]{1,0:T(8,128)S(1)}, f32[256,128]{1,0:T(8,128)S(1)}, u32[]{:S(2)}, u32[]{:S(2)}) collective-permute-start(f32[256,128]{1,0:T(8,128)S(1)} %constant_dynamic-slice_fusion.10), channel_id=1, source_target_pairs={{0,4},{2,6},{4,0},{6,2},{8,12},{10,14},{12,8},{14,10},{16,20},{18,... | collective-permute-start | bytes 393224 | tf_op jit(solution)/shard_map/ppermute | solution.py:78
  15.1 3.5 %fusion.6 = f32[1024,256]{1,0:T(8,128)S(1)} fusion(f32[1024,256]{1,0:T(8,128)S(1)} %copy-done, f32[2,1024,1024]{2,1,0:T(8,128)S(1)} %copy-done.1), kind=kOutput, calls=%fused_computation.6 | convolution fusion | flops 3221225472 | bytes 6291456 | tf_op jit(solution)/shard_map/dot_general | solution.py:8
  19.3 1.5 %collective-permute-start.3 = (f32[128,128]{1,0:T(8,128)S(1)}, f32[128,128]{1,0:T(8,128)S(1)}, u32[]{:S(2)}, u32[]{:S(2)}) collective-permute-start(f32[128,128]{1,0:T(8,128)S(1)} %constant_dynamic-slice_fusion.9), channel_id=1, source_target_pairs={{0,8},{2,10},{4,12},{6,14},{8,0},{10,2},{12,4},{14,6},{16,24},{18,... | collective-permute-start | bytes 196616 | tf_op jit(solution)/shard_map/ppermute | solution.py:78
  20.8 2.2 %collective-permute-done.10 = f32[128,128]{1,0:T(8,128)S(1)} collective-permute-done((f32[128,128]{1,0:T(8,128)S(1)}, f32[128,128]{1,0:T(8,128)S(1)}, u32[]{:S(2)}, u32[]{:S(2)}) %collective-permute-start.10) | collective-permute-done | bytes 65568 | tf_op jit(solution)/shard_map/ppermute | solution.py:78
  23.0 2.7 %collective-permute-start.11 = (f32[128,128]{1,0:T(8,128)S(1)}, f32[128,128]{1,0:T(8,128)S(1)}, u32[]{:S(2)}, u32[]{:S(2)}) collective-permute-start(f32[128,128]{1,0:T(8,128)S(1)} %dynamic-slice_add_fusion.10), channel_id=1, source_target_pairs={{0,16},{2,18},{4,20},{6,22},{8,24},{10,26},{12,28},{14,30},{16,0},... | collective-permute-start | bytes 196616 | tf_op jit(solution)/shard_map/ppermute | solution.py:86
  25.7 1.2 %collective-permute-start.4 = (f32[128,128]{1,0:T(8,128)S(1)}, f32[128,128]{1,0:T(8,128)S(1)}, u32[]{:S(2)}, u32[]{:S(2)}) collective-permute-start(f32[128,128]{1,0:T(8,128)S(1)} %dynamic-slice_add_fusion.11), channel_id=1, source_target_pairs={{0,16},{2,18},{4,20},{6,22},{8,24},{10,26},{12,28},{14,30},{16,0},... | collective-permute-start | bytes 196616 | tf_op jit(solution)/shard_map/ppermute | solution.py:86
  26.9 4.0 %collective-permute-done.11 = f32[128,128]{1,0:T(8,128)S(1)} collective-permute-done((f32[128,128]{1,0:T(8,128)S(1)}, f32[128,128]{1,0:T(8,128)S(1)}, u32[]{:S(2)}, u32[]{:S(2)}) %collective-permute-start.11) | collective-permute-done | bytes 65568 | tf_op jit(solution)/shard_map/ppermute | solution.py:86
  31.7 3.5 %collective-permute-done.12 = f32[128,128]{1,0:T(8,128)S(1)} collective-permute-done((f32[128,128]{1,0:T(8,128)S(1)}, f32[128,128]{1,0:T(8,128)S(1)}, u32[]{:S(2)}, u32[]{:S(2)}) %collective-permute-start.12) | collective-permute-done | bytes 65568 | tf_op jit(solution)/shard_map/ppermute | solution.py:90
  36.0 1.5 %collective-permute-start.6 = (f32[256,128]{1,0:T(8,128)S(1)}, f32[256,128]{1,0:T(8,128)S(1)}, u32[]{:S(2)}, u32[]{:S(2)}) collective-permute-start(f32[256,128]{1,0:T(8,128)S(1)} %pad_maximum_fusion.5), channel_id=1, source_target_pairs={{0,4},{2,6},{4,0},{6,2},{8,12},{10,14},{12,8},{14,10},{16,20},{18,... | collective-permute-start | bytes 393224 | tf_op jit(solution)/shard_map/ppermute | solution.py:90
  37.4 2.9 %collective-permute-done.13 = f32[256,128]{1,0:T(8,128)S(1)} collective-permute-done((f32[256,128]{1,0:T(8,128)S(1)}, f32[256,128]{1,0:T(8,128)S(1)}, u32[]{:S(2)}, u32[]{:S(2)}) %collective-permute-start.13) | collective-permute-done | bytes 131104 | tf_op jit(solution)/shard_map/ppermute | solution.py:90
  43.1 1.0 %convolution_bitcast_fusion = f32[1024,128]{1,0:T(8,128)S(1)} fusion(f32[64,128]{1,0:T(8,128)S(1)} %fusion.13, f32[1024,64]{0,1:T(8,128)S(1)} %copy-done.2), kind=kOutput, calls=%fused_computation.7 | convolution fusion | flops 100663296 | bytes 819200 | tf_op jit(solution)/shard_map/dot_general | solution.py:8
  44.2 1.0 %slice_add_fusion.1 = (f32[1024,128]{1,0:T(8,128)S(1)}, f32[1024,128]{1,0:T(8,128)S(1)}) fusion(f32[1024,256]{1,0:T(8,128)S(1)} %fusion.6, f32[1024,128]{1,0:T(8,128)S(1)} %convolution_bitcast_fusion, f32[64,128]{1,0:T(8,128)S(1)} %fusion.9, f32[1024,64]{0,1:T(8,128)S(1)} %copy-done.2), kind=kOutput, calls=%fused_computation.31 | convolution fusion | flops 100925440 | bytes 2916352 | tf_op jit(solution)/shard_map/dot_general | solution.py:8
  46.0 0.9 %collective-permute-done.22 = f32[512,128]{1,0:T(8,128)S(1)} collective-permute-done((f32[512,128]{1,0:T(8,128)S(1)}, f32[512,128]{1,0:T(8,128)S(1)}, u32[]{:S(2)}, u32[]{:S(2)}) %collective-permute-start.22) | collective-permute-done | bytes 262176 | tf_op jit(solution)/shard_map/ppermute | solution.py:78
  46.9 1.5 %collective-permute-start.23 = (f32[256,128]{1,0:T(8,128)S(1)}, f32[256,128]{1,0:T(8,128)S(1)}, u32[]{:S(2)}, u32[]{:S(2)}) collective-permute-start(f32[256,128]{1,0:T(8,128)S(1)} %constant_dynamic-slice_fusion.1), channel_id=1, source_target_pairs={{0,8},{2,10},{4,12},{6,14},{8,0},{10,2},{12,4},{14,6},{16,24},{18,... | collective-permute-start | bytes 393224 | tf_op jit(solution)/shard_map/ppermute | solution.py:78
  48.7 3.7 %collective-permute-done.23 = f32[256,128]{1,0:T(8,128)S(1)} collective-permute-done((f32[256,128]{1,0:T(8,128)S(1)}, f32[256,128]{1,0:T(8,128)S(1)}, u32[]{:S(2)}, u32[]{:S(2)}) %collective-permute-start.23) | collective-permute-done | bytes 131104 | tf_op jit(solution)/shard_map/ppermute | solution.py:78
  52.5 1.5 %collective-permute-start.24 = (f32[128,128]{1,0:T(8,128)S(1)}, f32[128,128]{1,0:T(8,128)S(1)}, u32[]{:S(2)}, u32[]{:S(2)}) collective-permute-start(f32[128,128]{1,0:T(8,128)S(1)} %constant_dynamic-slice_fusion), channel_id=1, source_target_pairs={{0,4},{2,6},{4,0},{6,2},{8,12},{10,14},{12,8},{14,10},{16,20},{18,... | collective-permute-start | bytes 196616 | tf_op jit(solution)/shard_map/ppermute | solution.py:78
  54.6 2.3 %collective-permute-done.24 = f32[128,128]{1,0:T(8,128)S(1)} collective-permute-done((f32[128,128]{1,0:T(8,128)S(1)}, f32[128,128]{1,0:T(8,128)S(1)}, u32[]{:S(2)}, u32[]{:S(2)}) %collective-permute-start.24) | collective-permute-done | bytes 65568 | tf_op jit(solution)/shard_map/ppermute | solution.py:78
  56.9 1.2 %collective-permute-start.25 = (f32[128,128]{1,0:T(8,128)S(1)}, f32[128,128]{1,0:T(8,128)S(1)}, u32[]{:S(2)}, u32[]{:S(2)}) collective-permute-start(f32[128,128]{1,0:T(8,128)S(1)} %dynamic-slice_add_fusion.8), channel_id=1, source_target_pairs={{0,16},{2,18},{4,20},{6,22},{8,24},{10,26},{12,28},{14,30},{16,0},... | collective-permute-start | bytes 196616 | tf_op jit(solution)/shard_map/ppermute | solution.py:86
  58.4 1.5 %collective-permute-start.18 = (f32[128,128]{1,0:T(8,128)S(1)}, f32[128,128]{1,0:T(8,128)S(1)}, u32[]{:S(2)}, u32[]{:S(2)}) collective-permute-start(f32[128,128]{1,0:T(8,128)S(1)} %dynamic-slice_add_fusion.9), channel_id=1, source_target_pairs={{0,16},{2,18},{4,20},{6,22},{8,24},{10,26},{12,28},{14,30},{16,0},... | collective-permute-start | bytes 196616 | tf_op jit(solution)/shard_map/ppermute | solution.py:86
  59.9 2.3 %collective-permute-done.25 = f32[128,128]{1,0:T(8,128)S(1)} collective-permute-done((f32[128,128]{1,0:T(8,128)S(1)}, f32[128,128]{1,0:T(8,128)S(1)}, u32[]{:S(2)}, u32[]{:S(2)}) %collective-permute-start.25) | collective-permute-done | bytes 65568 | tf_op jit(solution)/shard_map/ppermute | solution.py:86
  62.3 2.0 %collective-permute-start.26 = (f32[128,128]{1,0:T(8,128)S(1)}, f32[128,128]{1,0:T(8,128)S(1)}, u32[]{:S(2)}, u32[]{:S(2)}) collective-permute-start(f32[128,128]{1,0:T(8,128)S(1)} %add_subtract_fusion), channel_id=1, source_target_pairs={{0,4},{2,6},{4,0},{6,2},{8,12},{10,14},{12,8},{14,10},{16,20},{18,... | collective-permute-start | bytes 196616 | tf_op jit(solution)/shard_map/ppermute | solution.py:90
  64.6 2.0 %collective-permute-done.26 = f32[128,128]{1,0:T(8,128)S(1)} collective-permute-done((f32[128,128]{1,0:T(8,128)S(1)}, f32[128,128]{1,0:T(8,128)S(1)}, u32[]{:S(2)}, u32[]{:S(2)}) %collective-permute-start.26) | collective-permute-done | bytes 65568 | tf_op jit(solution)/shard_map/ppermute | solution.py:90
  66.6 1.3 %collective-permute-start.27 = (f32[256,128]{1,0:T(8,128)S(1)}, f32[256,128]{1,0:T(8,128)S(1)}, u32[]{:S(2)}, u32[]{:S(2)}) collective-permute-start(f32[256,128]{1,0:T(8,128)S(1)} %pad_maximum_fusion.8), channel_id=1, source_target_pairs={{0,8},{2,10},{4,12},{6,14},{8,0},{10,2},{12,4},{14,6},{16,24},{18,... | collective-permute-start | bytes 393224 | tf_op jit(solution)/shard_map/ppermute | solution.py:90
  68.7 0.9 %collective-permute-start.20 = (f32[256,128]{1,0:T(8,128)S(1)}, f32[256,128]{1,0:T(8,128)S(1)}, u32[]{:S(2)}, u32[]{:S(2)}) collective-permute-start(f32[256,128]{1,0:T(8,128)S(1)} %pad_maximum_fusion.7), channel_id=1, source_target_pairs={{0,4},{2,6},{4,0},{6,2},{8,12},{10,14},{12,8},{14,10},{16,20},{18,... | collective-permute-start | bytes 393224 | tf_op jit(solution)/shard_map/ppermute | solution.py:90
  69.6 2.1 %collective-permute-done.27 = f32[256,128]{1,0:T(8,128)S(1)} collective-permute-done((f32[256,128]{1,0:T(8,128)S(1)}, f32[256,128]{1,0:T(8,128)S(1)}, u32[]{:S(2)}, u32[]{:S(2)}) %collective-permute-start.27) | collective-permute-done | bytes 131104 | tf_op jit(solution)/shard_map/ppermute | solution.py:90
  71.8 2.0 %collective-permute-done.20 = f32[256,128]{1,0:T(8,128)S(1)} collective-permute-done((f32[256,128]{1,0:T(8,128)S(1)}, f32[256,128]{1,0:T(8,128)S(1)}, u32[]{:S(2)}, u32[]{:S(2)}) %collective-permute-start.20) | collective-permute-done | bytes 131104 | tf_op jit(solution)/shard_map/ppermute | solution.py:90
  74.4 1.0 %collective-permute-done.21 = f32[512,128]{1,0:T(8,128)S(1)} collective-permute-done((f32[512,128]{1,0:T(8,128)S(1)}, f32[512,128]{1,0:T(8,128)S(1)}, u32[]{:S(2)}, u32[]{:S(2)}) %collective-permute-start.21) | collective-permute-done | bytes 262176 | tf_op jit(solution)/shard_map/ppermute | solution.py:90
  (99 shorter events, 11.1 us)
Async XLA Ops:
  0.0 9.9 %collective-permute-start = (f32[1,1,2,64,512]{4,3,2,1,0:T(8,128)}, f32[1,1,2,64,512]{4,3,2,1,0:T(8,128)S(1)}, u32[]{:S(2)}, u32[]{:S(2)}) collective-permute-start(f32[1,1,2,64,512]{4,3,2,1,0:T(8,128)} %bitcast.49), channel_id=1, source_target_pairs={{0,1},{1,0},{2,3},{3,2},{4,5},{5,4},{6,7},{7,6},{8,9},{9,8},{10,11... | collective-permute-start | bytes 786440 | tf_op jit(solution)/shard_map/ppermute | solution.py:34
  2.9 7.0 %copy-start.3 = (f32[2,64,512]{2,1,0:T(8,128)S(1)}, f32[2,64,512]{2,1,0:T(8,128)}, u32[]{:S(2)}) copy-start(f32[2,64,512]{2,1,0:T(8,128)} %param.8) | copy-start | bytes 786436
  10.0 5.1 %copy-start.1 = (f32[2,1024,1024]{2,1,0:T(8,128)S(1)}, f32[2,1024,1024]{2,1,0:T(8,128)}, u32[]{:S(2)}) copy-start(f32[2,1024,1024]{2,1,0:T(8,128)} %param.5) | copy-start | bytes 25165828
  10.2 1.6 %collective-permute-start.8 = (f32[512,128]{1,0:T(8,128)S(1)}, f32[512,128]{1,0:T(8,128)S(1)}, u32[]{:S(2)}, u32[]{:S(2)}) collective-permute-start(f32[512,128]{1,0:T(8,128)S(1)} %constant_dynamic-slice_fusion.8), channel_id=1, source_target_pairs={{0,2},{2,0},{4,6},{6,4},{8,10},{10,8},{12,14},{14,12},{16,18},{18,... | collective-permute-start | bytes 786440 | tf_op jit(solution)/shard_map/ppermute | solution.py:78
  10.4 3.1 %collective-permute-start.1 = (f32[512,128]{1,0:T(8,128)S(1)}, f32[512,128]{1,0:T(8,128)S(1)}, u32[]{:S(2)}, u32[]{:S(2)}) collective-permute-start(f32[512,128]{1,0:T(8,128)S(1)} %constant_dynamic-slice_fusion.11), channel_id=1, source_target_pairs={{0,2},{2,0},{4,6},{6,4},{8,10},{10,8},{12,14},{14,12},{16,18},{18,... | collective-permute-start | bytes 786440 | tf_op jit(solution)/shard_map/ppermute | solution.py:78
  11.8 6.8 %collective-permute-start.9 = (f32[256,128]{1,0:T(8,128)S(1)}, f32[256,128]{1,0:T(8,128)S(1)}, u32[]{:S(2)}, u32[]{:S(2)}) collective-permute-start(f32[256,128]{1,0:T(8,128)S(1)} %constant_dynamic-slice_fusion.7), channel_id=1, source_target_pairs={{0,8},{2,10},{4,12},{6,14},{8,0},{10,2},{12,4},{14,6},{16,24},{18,... | collective-permute-start | bytes 393224 | tf_op jit(solution)/shard_map/ppermute | solution.py:78
  13.5 5.7 %collective-permute-start.2 = (f32[256,128]{1,0:T(8,128)S(1)}, f32[256,128]{1,0:T(8,128)S(1)}, u32[]{:S(2)}, u32[]{:S(2)}) collective-permute-start(f32[256,128]{1,0:T(8,128)S(1)} %constant_dynamic-slice_fusion.10), channel_id=1, source_target_pairs={{0,4},{2,6},{4,0},{6,2},{8,12},{10,14},{12,8},{14,10},{16,20},{18,... | collective-permute-start | bytes 393224 | tf_op jit(solution)/shard_map/ppermute | solution.py:78
  18.6 4.3 %collective-permute-start.10 = (f32[128,128]{1,0:T(8,128)S(1)}, f32[128,128]{1,0:T(8,128)S(1)}, u32[]{:S(2)}, u32[]{:S(2)}) collective-permute-start(f32[128,128]{1,0:T(8,128)S(1)} %constant_dynamic-slice_fusion.6), channel_id=1, source_target_pairs={{0,4},{2,6},{4,0},{6,2},{8,12},{10,14},{12,8},{14,10},{16,20},{18,... | collective-permute-start | bytes 196616 | tf_op jit(solution)/shard_map/ppermute | solution.py:78
  19.3 23.8 %copy-start.2 = (f32[1024,64]{0,1:T(8,128)S(1)}, f32[1024,64]{0,1:T(8,128)}, u32[]{:S(2)}) copy-start(f32[1024,64]{0,1:T(8,128)} %param.9) | copy-start | bytes 786436
  19.3 6.3 %collective-permute-start.3 = (f32[128,128]{1,0:T(8,128)S(1)}, f32[128,128]{1,0:T(8,128)S(1)}, u32[]{:S(2)}, u32[]{:S(2)}) collective-permute-start(f32[128,128]{1,0:T(8,128)S(1)} %constant_dynamic-slice_fusion.9), channel_id=1, source_target_pairs={{0,8},{2,10},{4,12},{6,14},{8,0},{10,2},{12,4},{14,6},{16,24},{18,... | collective-permute-start | bytes 196616 | tf_op jit(solution)/shard_map/ppermute | solution.py:78
  23.0 7.9 %collective-permute-start.11 = (f32[128,128]{1,0:T(8,128)S(1)}, f32[128,128]{1,0:T(8,128)S(1)}, u32[]{:S(2)}, u32[]{:S(2)}) collective-permute-start(f32[128,128]{1,0:T(8,128)S(1)} %dynamic-slice_add_fusion.10), channel_id=1, source_target_pairs={{0,16},{2,18},{4,20},{6,22},{8,24},{10,26},{12,28},{14,30},{16,0},... | collective-permute-start | bytes 196616 | tf_op jit(solution)/shard_map/ppermute | solution.py:86
  25.7 5.9 %collective-permute-start.4 = (f32[128,128]{1,0:T(8,128)S(1)}, f32[128,128]{1,0:T(8,128)S(1)}, u32[]{:S(2)}, u32[]{:S(2)}) collective-permute-start(f32[128,128]{1,0:T(8,128)S(1)} %dynamic-slice_add_fusion.11), channel_id=1, source_target_pairs={{0,16},{2,18},{4,20},{6,22},{8,24},{10,26},{12,28},{14,30},{16,0},... | collective-permute-start | bytes 196616 | tf_op jit(solution)/shard_map/ppermute | solution.py:86
  30.9 4.3 %collective-permute-start.12 = (f32[128,128]{1,0:T(8,128)S(1)}, f32[128,128]{1,0:T(8,128)S(1)}, u32[]{:S(2)}, u32[]{:S(2)}) collective-permute-start(f32[128,128]{1,0:T(8,128)S(1)} %add_subtract_fusion.2), channel_id=1, source_target_pairs={{0,4},{2,6},{4,0},{6,2},{8,12},{10,14},{12,8},{14,10},{16,20},{18,... | collective-permute-start | bytes 196616 | tf_op jit(solution)/shard_map/ppermute | solution.py:90
  31.6 4.3 %collective-permute-start.5 = (f32[128,128]{1,0:T(8,128)S(1)}, f32[128,128]{1,0:T(8,128)S(1)}, u32[]{:S(2)}, u32[]{:S(2)}) collective-permute-start(f32[128,128]{1,0:T(8,128)S(1)} %add_subtract_fusion.3), channel_id=1, source_target_pairs={{0,8},{2,10},{4,12},{6,14},{8,0},{10,2},{12,4},{14,6},{16,24},{18,... | collective-permute-start | bytes 196616 | tf_op jit(solution)/shard_map/ppermute | solution.py:90
  35.3 5.0 %collective-permute-start.13 = (f32[256,128]{1,0:T(8,128)S(1)}, f32[256,128]{1,0:T(8,128)S(1)}, u32[]{:S(2)}, u32[]{:S(2)}) collective-permute-start(f32[256,128]{1,0:T(8,128)S(1)} %pad_maximum_fusion.6), channel_id=1, source_target_pairs={{0,8},{2,10},{4,12},{6,14},{8,0},{10,2},{12,4},{14,6},{16,24},{18,... | collective-permute-start | bytes 393224 | tf_op jit(solution)/shard_map/ppermute | solution.py:90
  36.0 5.0 %collective-permute-start.6 = (f32[256,128]{1,0:T(8,128)S(1)}, f32[256,128]{1,0:T(8,128)S(1)}, u32[]{:S(2)}, u32[]{:S(2)}) collective-permute-start(f32[256,128]{1,0:T(8,128)S(1)} %pad_maximum_fusion.5), channel_id=1, source_target_pairs={{0,4},{2,6},{4,0},{6,2},{8,12},{10,14},{12,8},{14,10},{16,20},{18,... | collective-permute-start | bytes 393224 | tf_op jit(solution)/shard_map/ppermute | solution.py:90
  40.4 1.6 %collective-permute-start.14 = (f32[512,128]{1,0:T(8,128)S(1)}, f32[512,128]{1,0:T(8,128)S(1)}, u32[]{:S(2)}, u32[]{:S(2)}) collective-permute-start(f32[512,128]{1,0:T(8,128)S(1)} %pad_maximum_fusion.2), channel_id=1, source_target_pairs={{0,2},{2,0},{4,6},{6,4},{8,10},{10,8},{12,14},{14,12},{16,18},{18,... | collective-permute-start | bytes 786440 | tf_op jit(solution)/shard_map/ppermute | solution.py:90
  41.1 1.6 %collective-permute-start.7 = (f32[512,128]{1,0:T(8,128)S(1)}, f32[512,128]{1,0:T(8,128)S(1)}, u32[]{:S(2)}, u32[]{:S(2)}) collective-permute-start(f32[512,128]{1,0:T(8,128)S(1)} %pad_maximum_fusion.1), channel_id=1, source_target_pairs={{0,2},{2,0},{4,6},{6,4},{8,10},{10,8},{12,14},{14,12},{16,18},{18,... | collective-permute-start | bytes 786440 | tf_op jit(solution)/shard_map/ppermute | solution.py:90
  45.2 1.6 %collective-permute-start.22 = (f32[512,128]{1,0:T(8,128)S(1)}, f32[512,128]{1,0:T(8,128)S(1)}, u32[]{:S(2)}, u32[]{:S(2)}) collective-permute-start(f32[512,128]{1,0:T(8,128)S(1)} %constant_dynamic-slice_fusion.2), channel_id=1, source_target_pairs={{0,2},{2,0},{4,6},{6,4},{8,10},{10,8},{12,14},{14,12},{16,18},{18,... | collective-permute-start | bytes 786440 | tf_op jit(solution)/shard_map/ppermute | solution.py:78
  45.5 2.8 %collective-permute-start.15 = (f32[512,128]{1,0:T(8,128)S(1)}, f32[512,128]{1,0:T(8,128)S(1)}, u32[]{:S(2)}, u32[]{:S(2)}) collective-permute-start(f32[512,128]{1,0:T(8,128)S(1)} %constant_dynamic-slice_fusion.5), channel_id=1, source_target_pairs={{0,2},{2,0},{4,6},{6,4},{8,10},{10,8},{12,14},{14,12},{16,18},{18,... | collective-permute-start | bytes 786440 | tf_op jit(solution)/shard_map/ppermute | solution.py:78
  46.9 5.6 %collective-permute-start.23 = (f32[256,128]{1,0:T(8,128)S(1)}, f32[256,128]{1,0:T(8,128)S(1)}, u32[]{:S(2)}, u32[]{:S(2)}) collective-permute-start(f32[256,128]{1,0:T(8,128)S(1)} %constant_dynamic-slice_fusion.1), channel_id=1, source_target_pairs={{0,8},{2,10},{4,12},{6,14},{8,0},{10,2},{12,4},{14,6},{16,24},{18,... | collective-permute-start | bytes 393224 | tf_op jit(solution)/shard_map/ppermute | solution.py:78
  48.4 5.6 %collective-permute-start.16 = (f32[256,128]{1,0:T(8,128)S(1)}, f32[256,128]{1,0:T(8,128)S(1)}, u32[]{:S(2)}, u32[]{:S(2)}) collective-permute-start(f32[256,128]{1,0:T(8,128)S(1)} %constant_dynamic-slice_fusion.4), channel_id=1, source_target_pairs={{0,4},{2,6},{4,0},{6,2},{8,12},{10,14},{12,8},{14,10},{16,20},{18,... | collective-permute-start | bytes 393224 | tf_op jit(solution)/shard_map/ppermute | solution.py:78
  52.5 4.3 %collective-permute-start.24 = (f32[128,128]{1,0:T(8,128)S(1)}, f32[128,128]{1,0:T(8,128)S(1)}, u32[]{:S(2)}, u32[]{:S(2)}) collective-permute-start(f32[128,128]{1,0:T(8,128)S(1)} %constant_dynamic-slice_fusion), channel_id=1, source_target_pairs={{0,4},{2,6},{4,0},{6,2},{8,12},{10,14},{12,8},{14,10},{16,20},{18,... | collective-permute-start | bytes 196616 | tf_op jit(solution)/shard_map/ppermute | solution.py:78
  54.0 4.3 %collective-permute-start.17 = (f32[128,128]{1,0:T(8,128)S(1)}, f32[128,128]{1,0:T(8,128)S(1)}, u32[]{:S(2)}, u32[]{:S(2)}) collective-permute-start(f32[128,128]{1,0:T(8,128)S(1)} %constant_dynamic-slice_fusion.3), channel_id=1, source_target_pairs={{0,8},{2,10},{4,12},{6,14},{8,0},{10,2},{12,4},{14,6},{16,24},{18,... | collective-permute-start | bytes 196616 | tf_op jit(solution)/shard_map/ppermute | solution.py:78
  56.9 5.4 %collective-permute-start.25 = (f32[128,128]{1,0:T(8,128)S(1)}, f32[128,128]{1,0:T(8,128)S(1)}, u32[]{:S(2)}, u32[]{:S(2)}) collective-permute-start(f32[128,128]{1,0:T(8,128)S(1)} %dynamic-slice_add_fusion.8), channel_id=1, source_target_pairs={{0,16},{2,18},{4,20},{6,22},{8,24},{10,26},{12,28},{14,30},{16,0},... | collective-permute-start | bytes 196616 | tf_op jit(solution)/shard_map/ppermute | solution.py:86
  58.4 6.0 %collective-permute-start.18 = (f32[128,128]{1,0:T(8,128)S(1)}, f32[128,128]{1,0:T(8,128)S(1)}, u32[]{:S(2)}, u32[]{:S(2)}) collective-permute-start(f32[128,128]{1,0:T(8,128)S(1)} %dynamic-slice_add_fusion.9), channel_id=1, source_target_pairs={{0,16},{2,18},{4,20},{6,22},{8,24},{10,26},{12,28},{14,30},{16,0},... | collective-permute-start | bytes 196616 | tf_op jit(solution)/shard_map/ppermute | solution.py:86
  62.3 4.3 %collective-permute-start.26 = (f32[128,128]{1,0:T(8,128)S(1)}, f32[128,128]{1,0:T(8,128)S(1)}, u32[]{:S(2)}, u32[]{:S(2)}) collective-permute-start(f32[128,128]{1,0:T(8,128)S(1)} %add_subtract_fusion), channel_id=1, source_target_pairs={{0,4},{2,6},{4,0},{6,2},{8,12},{10,14},{12,8},{14,10},{16,20},{18,... | collective-permute-start | bytes 196616 | tf_op jit(solution)/shard_map/ppermute | solution.py:90
  64.4 4.3 %collective-permute-start.19 = (f32[128,128]{1,0:T(8,128)S(1)}, f32[128,128]{1,0:T(8,128)S(1)}, u32[]{:S(2)}, u32[]{:S(2)}) collective-permute-start(f32[128,128]{1,0:T(8,128)S(1)} %add_subtract_fusion.1), channel_id=1, source_target_pairs={{0,8},{2,10},{4,12},{6,14},{8,0},{10,2},{12,4},{14,6},{16,24},{18,... | collective-permute-start | bytes 196616 | tf_op jit(solution)/shard_map/ppermute | solution.py:90
  66.6 5.0 %collective-permute-start.27 = (f32[256,128]{1,0:T(8,128)S(1)}, f32[256,128]{1,0:T(8,128)S(1)}, u32[]{:S(2)}, u32[]{:S(2)}) collective-permute-start(f32[256,128]{1,0:T(8,128)S(1)} %pad_maximum_fusion.8), channel_id=1, source_target_pairs={{0,8},{2,10},{4,12},{6,14},{8,0},{10,2},{12,4},{14,6},{16,24},{18,... | collective-permute-start | bytes 393224 | tf_op jit(solution)/shard_map/ppermute | solution.py:90
  68.7 5.0 %collective-permute-start.20 = (f32[256,128]{1,0:T(8,128)S(1)}, f32[256,128]{1,0:T(8,128)S(1)}, u32[]{:S(2)}, u32[]{:S(2)}) collective-permute-start(f32[256,128]{1,0:T(8,128)S(1)} %pad_maximum_fusion.7), channel_id=1, source_target_pairs={{0,4},{2,6},{4,0},{6,2},{8,12},{10,14},{12,8},{14,10},{16,20},{18,... | collective-permute-start | bytes 393224 | tf_op jit(solution)/shard_map/ppermute | solution.py:90
  71.7 2.2 %collective-permute-start.28 = (f32[512,128]{1,0:T(8,128)S(1)}, f32[512,128]{1,0:T(8,128)S(1)}, u32[]{:S(2)}, u32[]{:S(2)}) collective-permute-start(f32[512,128]{1,0:T(8,128)S(1)} %pad_maximum_fusion.4), channel_id=1, source_target_pairs={{0,2},{2,0},{4,6},{6,4},{8,10},{10,8},{12,14},{14,12},{16,18},{18,... | collective-permute-start | bytes 786440 | tf_op jit(solution)/shard_map/ppermute | solution.py:90
  73.8 1.6 %collective-permute-start.21 = (f32[512,128]{1,0:T(8,128)S(1)}, f32[512,128]{1,0:T(8,128)S(1)}, u32[]{:S(2)}, u32[]{:S(2)}) collective-permute-start(f32[512,128]{1,0:T(8,128)S(1)} %pad_maximum_fusion.3), channel_id=1, source_target_pairs={{0,2},{2,0},{4,6},{6,4},{8,10},{10,8},{12,14},{14,12},{16,18},{18,... | collective-permute-start | bytes 786440 | tf_op jit(solution)/shard_map/ppermute | solution.py:90
  (1 other events, 2.9 us)

commit v13 on v12

--- a/solution.py
+++ b/solution.py
@@ -66,15 +66,18 @@
     return y.reshape(x.shape), riders
 
 
-def ordered_reduce_then_gather(x, right, axis, n, order, riders=None, hold=None):
+def ordered_reduce_then_gather(x, right, axis, n, order, riders=None, hold=None, width=None, column=0):
     me = lax.axis_index(axis)
     y, r = x, right
+    if width is None:
+        width = x.shape[1]
     for step, j in enumerate(order[:-1]):
         half = y.shape[0] // 2
         mine = (me >> j) & 1
-        keep = lax.dynamic_slice_in_dim(y, mine * half, half, 0)
-        send = lax.dynamic_slice_in_dim(y, (1 - mine) * half, half, 0)
-        r = lax.dynamic_slice_in_dim(r, mine * half, half, 0)
+        keep = lax.dynamic_slice(y, (mine * half, column), (half, width))
+        send = lax.dynamic_slice(y, ((1 - mine) * half, column), (half, width))
+        r = lax.dynamic_slice(r, (mine * half, column), (half, width))
+        column = 0
         got = lax.ppermute(send, axis, [(i, i ^ (1 << j)) for i in range(n)])
         if step == 1 and riders is not None:
             got, riders = lax.optimization_barrier((got, riders))
@@ -132,9 +135,10 @@
             first_blocks = []
             for chain, (order, cols) in enumerate(zip(orders, columns)):
                 remains, got_riders = ordered_reduce_then_gather(
-                    first_sum[:, cols], right_side[0][:, cols], "blk", n, order,
+                    first_sum, right_side[0], "blk", n, order,
                     inverse_pieces if chain == 0 else None,
                     (solved_before, lambda held: product(factor_panel[1], held)) if chain == 0 else None,
+                    width, cols.start,
                 )
                 if chain == 0:
                     panel_sum, inverse_pieces = got_riders

time: 76.8 us -> 88.1 us (1.15)
  waiting for transfers between devices: 33.6 us -> 38 us
  other arithmetic: 1.47 us -> 5.74 us
  matrix products: 12.5 us -> 14.4 us
  local copies, waits for them, and re-layouts: 2.18 us -> 3.16 us
    ppermute x12, waiting for transfers between devices: 10.3 us -> 14.3 us  [ordered_reduce_then_gather(): got = lax.ppermute(send, axis, [(i, i ^ 1 << j) for i in range(n)])]
    ppermute x4, starting transfers between devices: 6.59 us -> 9.39 us  [ordered_reduce_then_gather(): y = y + lax.ppermute(y, axis, [(i, i ^ 1 << top) for i in range(n)])]
    dot_general x8, matrix products: 12.5 us -> 14.4 us  [product(): jnp.dot(left, right, precision=lax.Precision.HIGHEST, preferred_element_t...]
    ppermute x12, starting transfers between devices: 10.3 us -> 8.43 us  [ordered_reduce_then_gather(): got = lax.ppermute(send, axis, [(i, i ^ 1 << j) for i in range(n)])]
    ppermute x4, waiting for transfers between devices: 6.99 us -> 5.1 us  [ordered_reduce_then_gather(): y = y + lax.ppermute(y, axis, [(i, i ^ 1 << top) for i in range(n)])]
    concatenate x8, other arithmetic: 0.12 us -> 1.54 us  [ordered_reduce_then_gather(): y = jnp.concatenate([low, high], 0)]
    ppermute x1, waiting for transfers between devices: 0.01 us -> 1.31 us  [doubling_gather(): got = lax.ppermute(y, axis, [(i, i ^ 1 << j) for i in range(n)])]
    ppermute x12, starting transfers between devices: 6.44 us -> 5.34 us  [ordered_reduce_then_gather(): got = lax.ppermute(y, axis, [(i, i ^ 1 << j) for i in range(n)])]
  transfers between devices with their start and end apart: 29 -> 29, of which waited for: 21 -> 22; matrix products, arithmetic and copies ran while one was open for 16% -> 18% of each run, Pallas kernels for 0% -> 0%
where the time goes in v13:
time: 88.1 us; the launch traced here: 87.9 us
  waiting for transfers between devices  38 us (43%)
  starting transfers between devices  26.1 us (30%)
  matrix products  14.4 us (16%)
  other arithmetic  5.74 us (7%)
  local copies, waits for them, and re-layouts  3.16 us (4%)
    ppermute x12, waiting for transfers between devices, ordered_reduce_then_gather(): got = lax.ppermute(y, axis, [(i, i ^ 1 << j) for i in range(n)])  17.3 us
    dot_general x8, matrix products, product(): jnp.dot(left, right, precision=lax.Precision.HIGHEST, preferred_element_t...  14.4 us
    ppermute x12, waiting for transfers between devices, ordered_reduce_then_gather(): got = lax.ppermute(send, axis, [(i, i ^ 1 << j) for i in range(n)])  14.3 us
    ppermute x4, starting transfers between devices, ordered_reduce_then_gather(): y = y + lax.ppermute(y, axis, [(i, i ^ 1 << top) for i in range(n)])  9.39 us
    ppermute x12, starting transfers between devices, ordered_reduce_then_gather(): got = lax.ppermute(send, axis, [(i, i ^ 1 << j) for i in range(n)])  8.43 us
    ppermute x12, starting transfers between devices, ordered_reduce_then_gather(): got = lax.ppermute(y, axis, [(i, i ^ 1 << j) for i in range(n)])  5.34 us
    ppermute x4, waiting for transfers between devices, ordered_reduce_then_gather(): y = y + lax.ppermute(y, axis, [(i, i ^ 1 << top) for i in range(n)])  5.1 us
    ppermute x1, starting transfers between devices, doubling_gather(): got = lax.ppermute(y, axis, [(i, i ^ 1 << j) for i in range(n)])  2.94 us
  transfers between devices with their start and end apart: 29, of which 22 were waited for; matrix products, arithmetic and copies ran while one was open for 18% of the time, Pallas kernels for 0%

profile of v13, /device:TPU:0, one launch (start us, length us, event | category | flops | bytes accessed | tf_op | source)
XLA Modules:
  0.0 87.9 jit_solution(3909234082073100995)
XLA Ops:
  0.0 2.9 %collective-permute-start = (f32[1,1,2,64,512]{4,3,2,1,0:T(8,128)}, f32[1,1,2,64,512]{4,3,2,1,0:T(8,128)S(1)}, u32[]{:S(2)}, u32[]{:S(2)}) collective-permute-start(f32[1,1,2,64,512]{4,3,2,1,0:T(8,128)} %bitcast.51), channel_id=1, source_target_pairs={{0,1},{1,0},{2,3},{3,2},{4,5},{5,4},{6,7},{7,6},{8,9},{9,8},{10,11... | collective-permute-start | bytes 786440 | tf_op jit(solution)/shard_map/ppermute | solution.py:34
  2.9 5.2 %fusion.2 = f32[1024,256]{1,0:T(8,128)S(1)} fusion(f32[1024,256]{1,0:T(8,128)S(1)} %copy-done, f32[2,1024,1024]{2,1,0:T(8,128)} %param.5), kind=kOutput, calls=%fused_computation.2 | convolution fusion | flops 3221225472 | bytes 6291456 | tf_op jit(solution)/shard_map/dot_general | solution.py:8
  8.2 1.3 %collective-permute-done = f32[1,1,2,64,512]{4,3,2,1,0:T(8,128)S(1)} collective-permute-done((f32[1,1,2,64,512]{4,3,2,1,0:T(8,128)}, f32[1,1,2,64,512]{4,3,2,1,0:T(8,128)S(1)}, u32[]{:S(2)}, u32[]{:S(2)}) %collective-permute-start) | collective-permute-done | bytes 262176 | tf_op jit(solution)/shard_map/ppermute | solution.py:34
  10.5 1.5 %collective-permute-done.1 = f32[512,128]{1,0:T(8,128)S(1)} collective-permute-done((f32[512,128]{1,0:T(8,128)S(1)}, f32[512,128]{1,0:T(8,128)S(1)}, u32[]{:S(2)}, u32[]{:S(2)}) %collective-permute-start.1) | collective-permute-done | bytes 262176 | tf_op jit(solution)/shard_map/ppermute | solution.py:81
  12.1 1.8 %collective-permute-start.2 = (f32[256,128]{1,0:T(8,128)S(1)}, f32[256,128]{1,0:T(8,128)S(1)}, u32[]{:S(2)}, u32[]{:S(2)}) collective-permute-start(f32[256,128]{1,0:T(8,128)S(1)} %constant_dynamic-slice_fusion.9), channel_id=1, source_target_pairs={{0,4},{2,6},{4,0},{6,2},{8,12},{10,14},{12,8},{14,10},{16,20},{18,... | collective-permute-start | bytes 393224 | tf_op jit(solution)/shard_map/ppermute | solution.py:81
  13.9 5.5 %fusion.6 = f32[1024,256]{1,0:T(8,128)S(1)} fusion(f32[1024,256]{1,0:T(8,128)S(1)} %copy-done, f32[2,1024,1024]{2,1,0:T(8,128)} %param.5), kind=kOutput, calls=%fused_computation.6 | convolution fusion | flops 3221225472 | bytes 6291456 | tf_op jit(solution)/shard_map/dot_general | solution.py:8
  19.5 1.7 %collective-permute-start.9 = (f32[256,128]{1,0:T(8,128)S(1)}, f32[256,128]{1,0:T(8,128)S(1)}, u32[]{:S(2)}, u32[]{:S(2)}) collective-permute-start(f32[256,128]{1,0:T(8,128)S(1)} %constant_dynamic-slice_fusion.7), channel_id=1, source_target_pairs={{0,8},{2,10},{4,12},{6,14},{8,0},{10,2},{12,4},{14,6},{16,24},{18,... | collective-permute-start | bytes 393224 | tf_op jit(solution)/shard_map/ppermute | solution.py:81
  21.7 4.2 %collective-permute-done.9 = f32[256,128]{1,0:T(8,128)S(1)} collective-permute-done((f32[256,128]{1,0:T(8,128)S(1)}, f32[256,128]{1,0:T(8,128)S(1)}, u32[]{:S(2)}, u32[]{:S(2)}) %collective-permute-start.9) | collective-permute-done | bytes 131104 | tf_op jit(solution)/shard_map/ppermute | solution.py:81
  26.7 2.7 %collective-permute-start.4 = (f32[128,128]{1,0:T(8,128)S(1)}, f32[128,128]{1,0:T(8,128)S(1)}, u32[]{:S(2)}, u32[]{:S(2)}) collective-permute-start(f32[128,128]{1,0:T(8,128)S(1)} %dynamic-slice_add_fusion.11), channel_id=1, source_target_pairs={{0,16},{2,18},{4,20},{6,22},{8,24},{10,26},{12,28},{14,30},{16,0},... | collective-permute-start | bytes 196616 | tf_op jit(solution)/shard_map/ppermute | solution.py:89
  30.3 2.7 %collective-permute-start.11 = (f32[128,128]{1,0:T(8,128)S(1)}, f32[128,128]{1,0:T(8,128)S(1)}, u32[]{:S(2)}, u32[]{:S(2)}) collective-permute-start(f32[128,128]{1,0:T(8,128)S(1)} %dynamic-slice_add_fusion.10), channel_id=1, source_target_pairs={{0,16},{2,18},{4,20},{6,22},{8,24},{10,26},{12,28},{14,30},{16,0},... | collective-permute-start | bytes 196616 | tf_op jit(solution)/shard_map/ppermute | solution.py:89
  32.9 1.1 %slice_bitcast_fusion = (f32[1024,256]{1,0:T(8,128)S(1)}, f32[1,1024,256]{2,1,0:T(8,128)}) fusion(f32[2,1024,256]{2,1,0:T(8,128)S(1)} %copy-done.1), kind=kLoop, calls=%fused_computation.9 | loop fusion | bytes 4194304 | tf_op jit(solution)/shard_map/squeeze | solution.py:151
  34.1 1.4 %collective-permute-done.11 = f32[128,128]{1,0:T(8,128)S(1)} collective-permute-done((f32[128,128]{1,0:T(8,128)S(1)}, f32[128,128]{1,0:T(8,128)S(1)}, u32[]{:S(2)}, u32[]{:S(2)}) %collective-permute-start.11) | collective-permute-done | bytes 65568 | tf_op jit(solution)/shard_map/ppermute | solution.py:89
  36.4 1.6 %collective-permute-start.5 = (f32[128,128]{1,0:T(8,128)S(1)}, f32[128,128]{1,0:T(8,128)S(1)}, u32[]{:S(2)}, u32[]{:S(2)}) collective-permute-start(f32[128,128]{1,0:T(8,128)S(1)} %get-tuple-element.25), channel_id=1, source_target_pairs={{0,8},{2,10},{4,12},{6,14},{8,0},{10,2},{12,4},{14,6},{16,24},{18,... | collective-permute-start | bytes 196616 | tf_op jit(solution)/shard_map/ppermute | solution.py:93
  38.6 2.2 %collective-permute-done.5 = f32[128,128]{1,0:T(8,128)S(1)} collective-permute-done((f32[128,128]{1,0:T(8,128)S(1)}, f32[128,128]{1,0:T(8,128)S(1)}, u32[]{:S(2)}, u32[]{:S(2)}) %collective-permute-start.5) | collective-permute-done | bytes 65568 | tf_op jit(solution)/shard_map/ppermute | solution.py:93
  41.4 1.6 %collective-permute-done.12 = f32[128,128]{1,0:T(8,128)S(1)} collective-permute-done((f32[128,128]{1,0:T(8,128)S(1)}, f32[128,128]{1,0:T(8,128)S(1)}, u32[]{:S(2)}, u32[]{:S(2)}) %collective-permute-start.12) | collective-permute-done | bytes 65568 | tf_op jit(solution)/shard_map/ppermute | solution.py:93
  43.5 2.3 %collective-permute-done.6 = f32[256,128]{1,0:T(8,128)S(1)} collective-permute-done((f32[256,128]{1,0:T(8,128)S(1)}, f32[256,128]{1,0:T(8,128)S(1)}, u32[]{:S(2)}, u32[]{:S(2)}) %collective-permute-start.6) | collective-permute-done | bytes 131104 | tf_op jit(solution)/shard_map/ppermute | solution.py:93
  46.6 1.5 %collective-permute-done.13 = f32[256,128]{1,0:T(8,128)S(1)} collective-permute-done((f32[256,128]{1,0:T(8,128)S(1)}, f32[256,128]{1,0:T(8,128)S(1)}, u32[]{:S(2)}, u32[]{:S(2)}) %collective-permute-start.13) | collective-permute-done | bytes 131104 | tf_op jit(solution)/shard_map/ppermute | solution.py:93
  49.5 1.1 %slice_bitcast_fusion.1 = (f32[2,64,512]{2,1,0:T(8,128)S(1)}, f32[2,64,512]{2,1,0:T(8,128)S(1)}) fusion(f32[2,2,64,512]{3,2,1,0:T(8,128)} %maximum_bitcast_fusion), kind=kLoop, calls=%fused_computation.42 | loop fusion | bytes 1048576 | tf_op jit(solution)/shard_map/unstack | solution.py:146
  51.4 1.2 %broadcast_select_fusion.5 = (f32[512,128]{1,0:T(8,128)S(1)}, f32[512,128]{1,0:T(8,128)S(1)}, f32[512,128]{1,0:T(8,128)S(1)}, f32[512,128]{1,0:T(8,128)S(1)}) fusion(f32[512,128]{1,0:T(8,128)} %collective-permute-done.14, pred[]{:T(512)S(6)} %eq.9, f32[256,128]{1,0:T(8,128)} %copy-done.2, f32[256,128]{1,0:T(8,128)S(1)} %get-tuple-element.47, ...), kind=kLoop, calls=%fused_computation.61 | loop fusion | flops 393216 | bytes 2097153 | tf_op jit(solution)/shard_map/jit(_where)/select_n | solution.py:94
  54.4 1.0 %slice_add_fusion.1 = (f32[1024,128]{1,0:T(8,128)S(1)}, f32[1024,128]{1,0:T(8,128)S(1)}) fusion(f32[1024,256]{1,0:T(8,128)S(1)} %fusion.6, f32[1024,128]{1,0:T(8,128)S(1)} %convolution_bitcast_fusion, f32[64,128]{1,0:T(8,128)S(1)} %fusion.9, f32[1024,64]{0,1:T(8,128)S(1)} %copy-done.3), kind=kOutput, calls=%fused_computation.30 | convolution fusion | flops 100925440 | bytes 2916352 | tf_op jit(solution)/shard_map/dot_general | solution.py:8
  57.7 1.1 %collective-permute-start.16 = (f32[256,128]{1,0:T(8,128)S(1)}, f32[256,128]{1,0:T(8,128)S(1)}, u32[]{:S(2)}, u32[]{:S(2)}) collective-permute-start(f32[256,128]{1,0:T(8,128)S(1)} %constant_dynamic-slice_fusion.4), channel_id=1, source_target_pairs={{0,4},{2,6},{4,0},{6,2},{8,12},{10,14},{12,8},{14,10},{16,20},{18,... | collective-permute-start | bytes 393224 | tf_op jit(solution)/shard_map/ppermute | solution.py:81
  58.8 3.9 %collective-permute-done.23 = f32[256,128]{1,0:T(8,128)S(1)} collective-permute-done((f32[256,128]{1,0:T(8,128)S(1)}, f32[256,128]{1,0:T(8,128)S(1)}, u32[]{:S(2)}, u32[]{:S(2)}) %collective-permute-start.23) | collective-permute-done | bytes 131104 | tf_op jit(solution)/shard_map/ppermute | solution.py:81
  63.3 1.4 %collective-permute-start.17 = (f32[128,128]{1,0:T(8,128)S(1)}, f32[128,128]{1,0:T(8,128)S(1)}, u32[]{:S(2)}, u32[]{:S(2)}) collective-permute-start(f32[128,128]{1,0:T(8,128)S(1)} %constant_dynamic-slice_fusion.3), channel_id=1, source_target_pairs={{0,8},{2,10},{4,12},{6,14},{8,0},{10,2},{12,4},{14,6},{16,24},{18,... | collective-permute-start | bytes 196616 | tf_op jit(solution)/shard_map/ppermute | solution.py:81
  64.7 2.4 %collective-permute-done.24 = f32[128,128]{1,0:T(8,128)S(1)} collective-permute-done((f32[128,128]{1,0:T(8,128)S(1)}, f32[128,128]{1,0:T(8,128)S(1)}, u32[]{:S(2)}, u32[]{:S(2)}) %collective-permute-start.24) | collective-permute-done | bytes 65568 | tf_op jit(solution)/shard_map/ppermute | solution.py:81
  67.1 2.6 %collective-permute-start.25 = (f32[128,128]{1,0:T(8,128)S(1)}, f32[128,128]{1,0:T(8,128)S(1)}, u32[]{:S(2)}, u32[]{:S(2)}) collective-permute-start(f32[128,128]{1,0:T(8,128)S(1)} %dynamic-slice_add_fusion.8), channel_id=1, source_target_pairs={{0,16},{2,18},{4,20},{6,22},{8,24},{10,26},{12,28},{14,30},{16,0},... | collective-permute-start | bytes 196616 | tf_op jit(solution)/shard_map/ppermute | solution.py:89
  69.7 1.5 %collective-permute-start.18 = (f32[128,128]{1,0:T(8,128)S(1)}, f32[128,128]{1,0:T(8,128)S(1)}, u32[]{:S(2)}, u32[]{:S(2)}) collective-permute-start(f32[128,128]{1,0:T(8,128)S(1)} %dynamic-slice_add_fusion.9), channel_id=1, source_target_pairs={{0,16},{2,18},{4,20},{6,22},{8,24},{10,26},{12,28},{14,30},{16,0},... | collective-permute-start | bytes 196616 | tf_op jit(solution)/shard_map/ppermute | solution.py:89
  71.2 2.8 %collective-permute-done.25 = f32[128,128]{1,0:T(8,128)S(1)} collective-permute-done((f32[128,128]{1,0:T(8,128)S(1)}, f32[128,128]{1,0:T(8,128)S(1)}, u32[]{:S(2)}, u32[]{:S(2)}) %collective-permute-start.25) | collective-permute-done | bytes 65568 | tf_op jit(solution)/shard_map/ppermute | solution.py:89
  76.3 2.0 %collective-permute-done.26 = f32[128,128]{1,0:T(8,128)S(1)} collective-permute-done((f32[128,128]{1,0:T(8,128)S(1)}, f32[128,128]{1,0:T(8,128)S(1)}, u32[]{:S(2)}, u32[]{:S(2)}) %collective-permute-start.26) | collective-permute-done | bytes 65568 | tf_op jit(solution)/shard_map/ppermute | solution.py:93
  78.4 1.6 %collective-permute-done.19 = f32[128,128]{1,0:T(8,128)S(1)} collective-permute-done((f32[128,128]{1,0:T(8,128)S(1)}, f32[128,128]{1,0:T(8,128)S(1)}, u32[]{:S(2)}, u32[]{:S(2)}) %collective-permute-start.19) | collective-permute-done | bytes 65568 | tf_op jit(solution)/shard_map/ppermute | solution.py:93
  80.5 2.9 %collective-permute-done.27 = f32[256,128]{1,0:T(8,128)S(1)} collective-permute-done((f32[256,128]{1,0:T(8,128)S(1)}, f32[256,128]{1,0:T(8,128)S(1)}, u32[]{:S(2)}, u32[]{:S(2)}) %collective-permute-start.27) | collective-permute-done | bytes 131104 | tf_op jit(solution)/shard_map/ppermute | solution.py:93
  83.5 1.6 %collective-permute-done.20 = f32[256,128]{1,0:T(8,128)S(1)} collective-permute-done((f32[256,128]{1,0:T(8,128)S(1)}, f32[256,128]{1,0:T(8,128)S(1)}, u32[]{:S(2)}, u32[]{:S(2)}) %collective-permute-start.20) | collective-permute-done | bytes 131104 | tf_op jit(solution)/shard_map/ppermute | solution.py:93
  85.7 1.0 %collective-permute-done.21 = f32[512,128]{1,0:T(8,128)S(1)} collective-permute-done((f32[512,128]{1,0:T(8,128)S(1)}, f32[512,128]{1,0:T(8,128)S(1)}, u32[]{:S(2)}, u32[]{:S(2)}) %collective-permute-start.21) | collective-permute-done | bytes 262176 | tf_op jit(solution)/shard_map/ppermute | solution.py:93
  (97 shorter events, 18.3 us)
Async XLA Ops:
  0.0 9.5 %copy-start.4 = (f32[2,64,512]{2,1,0:T(8,128)S(1)}, f32[2,64,512]{2,1,0:T(8,128)}, u32[]{:S(2)}) copy-start(f32[2,64,512]{2,1,0:T(8,128)} %param.8) | copy-start | bytes 786436
  0.0 9.5 %collective-permute-start = (f32[1,1,2,64,512]{4,3,2,1,0:T(8,128)}, f32[1,1,2,64,512]{4,3,2,1,0:T(8,128)S(1)}, u32[]{:S(2)}, u32[]{:S(2)}) collective-permute-start(f32[1,1,2,64,512]{4,3,2,1,0:T(8,128)} %bitcast.51), channel_id=1, source_target_pairs={{0,1},{1,0},{2,3},{3,2},{4,5},{5,4},{6,7},{7,6},{8,9},{9,8},{10,11... | collective-permute-start | bytes 786440 | tf_op jit(solution)/shard_map/ppermute | solution.py:34
  10.4 1.6 %collective-permute-start.1 = (f32[512,128]{1,0:T(8,128)S(1)}, f32[512,128]{1,0:T(8,128)S(1)}, u32[]{:S(2)}, u32[]{:S(2)}) collective-permute-start(f32[512,128]{1,0:T(8,128)S(1)} %constant_dynamic-slice_fusion.10), channel_id=1, source_target_pairs={{0,2},{2,0},{4,6},{6,4},{8,10},{10,8},{12,14},{14,12},{16,18},{18,... | collective-permute-start | bytes 786440 | tf_op jit(solution)/shard_map/ppermute | solution.py:81
  12.1 7.3 %collective-permute-start.2 = (f32[256,128]{1,0:T(8,128)S(1)}, f32[256,128]{1,0:T(8,128)S(1)}, u32[]{:S(2)}, u32[]{:S(2)}) collective-permute-start(f32[256,128]{1,0:T(8,128)S(1)} %constant_dynamic-slice_fusion.9), channel_id=1, source_target_pairs={{0,4},{2,6},{4,0},{6,2},{8,12},{10,14},{12,8},{14,10},{16,20},{18,... | collective-permute-start | bytes 393224 | tf_op jit(solution)/shard_map/ppermute | solution.py:81
  13.9 19.0 %copy-start.1 = (f32[2,1024,256]{2,1,0:T(8,128)S(1)}, f32[2,1024,256]{2,1,0:T(8,128)}, u32[]{:S(2)}) copy-start(f32[2,1024,256]{2,1,0:T(8,128)} %param.7) | copy-start | bytes 6291460
  13.9 5.5 %collective-permute-start.8 = (f32[512,128]{1,0:T(8,128)S(1)}, f32[512,128]{1,0:T(8,128)S(1)}, u32[]{:S(2)}, u32[]{:S(2)}) collective-permute-start(f32[512,128]{1,0:T(8,128)S(1)} %get-tuple-element.28), channel_id=1, source_target_pairs={{0,2},{2,0},{4,6},{6,4},{8,10},{10,8},{12,14},{14,12},{16,18},{18,... | collective-permute-start | bytes 786440 | tf_op jit(solution)/shard_map/ppermute | solution.py:81
  19.5 6.4 %collective-permute-start.9 = (f32[256,128]{1,0:T(8,128)S(1)}, f32[256,128]{1,0:T(8,128)S(1)}, u32[]{:S(2)}, u32[]{:S(2)}) collective-permute-start(f32[256,128]{1,0:T(8,128)S(1)} %constant_dynamic-slice_fusion.7), channel_id=1, source_target_pairs={{0,8},{2,10},{4,12},{6,14},{8,0},{10,2},{12,4},{14,6},{16,24},{18,... | collective-permute-start | bytes 393224 | tf_op jit(solution)/shard_map/ppermute | solution.py:81
  21.2 5.5 %collective-permute-start.3 = (f32[128,128]{1,0:T(8,128)S(1)}, f32[128,128]{1,0:T(8,128)S(1)}, u32[]{:S(2)}, u32[]{:S(2)}) collective-permute-start(f32[128,128]{1,0:T(8,128)S(1)} %constant_dynamic-slice_fusion.8), channel_id=1, source_target_pairs={{0,8},{2,10},{4,12},{6,14},{8,0},{10,2},{12,4},{14,6},{16,24},{18,... | collective-permute-start | bytes 196616 | tf_op jit(solution)/shard_map/ppermute | solution.py:81
  25.9 4.3 %collective-permute-start.10 = (f32[128,128]{1,0:T(8,128)S(1)}, f32[128,128]{1,0:T(8,128)S(1)}, u32[]{:S(2)}, u32[]{:S(2)}) collective-permute-start(f32[128,128]{1,0:T(8,128)S(1)} %constant_dynamic-slice_fusion.6), channel_id=1, source_target_pairs={{0,4},{2,6},{4,0},{6,2},{8,12},{10,14},{12,8},{14,10},{16,20},{18,... | collective-permute-start | bytes 196616 | tf_op jit(solution)/shard_map/ppermute | solution.py:81
  26.7 7.3 %collective-permute-start.4 = (f32[128,128]{1,0:T(8,128)S(1)}, f32[128,128]{1,0:T(8,128)S(1)}, u32[]{:S(2)}, u32[]{:S(2)}) collective-permute-start(f32[128,128]{1,0:T(8,128)S(1)} %dynamic-slice_add_fusion.11), channel_id=1, source_target_pairs={{0,16},{2,18},{4,20},{6,22},{8,24},{10,26},{12,28},{14,30},{16,0},... | collective-permute-start | bytes 196616 | tf_op jit(solution)/shard_map/ppermute | solution.py:89
  30.3 5.2 %collective-permute-start.11 = (f32[128,128]{1,0:T(8,128)S(1)}, f32[128,128]{1,0:T(8,128)S(1)}, u32[]{:S(2)}, u32[]{:S(2)}) collective-permute-start(f32[128,128]{1,0:T(8,128)S(1)} %dynamic-slice_add_fusion.10), channel_id=1, source_target_pairs={{0,16},{2,18},{4,20},{6,22},{8,24},{10,26},{12,28},{14,30},{16,0},... | collective-permute-start | bytes 196616 | tf_op jit(solution)/shard_map/ppermute | solution.py:89
  36.4 4.3 %collective-permute-start.5 = (f32[128,128]{1,0:T(8,128)S(1)}, f32[128,128]{1,0:T(8,128)S(1)}, u32[]{:S(2)}, u32[]{:S(2)}) collective-permute-start(f32[128,128]{1,0:T(8,128)S(1)} %get-tuple-element.25), channel_id=1, source_target_pairs={{0,8},{2,10},{4,12},{6,14},{8,0},{10,2},{12,4},{14,6},{16,24},{18,... | collective-permute-start | bytes 196616 | tf_op jit(solution)/shard_map/ppermute | solution.py:93
  38.1 4.9 %collective-permute-start.12 = (f32[128,128]{1,0:T(8,128)S(1)}, f32[128,128]{1,0:T(8,128)S(1)}, u32[]{:S(2)}, u32[]{:S(2)}) collective-permute-start(f32[128,128]{1,0:T(8,128)S(1)} %get-tuple-element.26), channel_id=1, source_target_pairs={{0,4},{2,6},{4,0},{6,2},{8,12},{10,14},{12,8},{14,10},{16,20},{18,... | collective-permute-start | bytes 196616 | tf_op jit(solution)/shard_map/ppermute | solution.py:93
  40.8 5.0 %collective-permute-start.6 = (f32[256,128]{1,0:T(8,128)S(1)}, f32[256,128]{1,0:T(8,128)S(1)}, u32[]{:S(2)}, u32[]{:S(2)}) collective-permute-start(f32[256,128]{1,0:T(8,128)S(1)} %pad_maximum_fusion.5), channel_id=1, source_target_pairs={{0,4},{2,6},{4,0},{6,2},{8,12},{10,14},{12,8},{14,10},{16,20},{18,... | collective-permute-start | bytes 393224 | tf_op jit(solution)/shard_map/ppermute | solution.py:93
  43.0 5.0 %collective-permute-start.13 = (f32[256,128]{1,0:T(8,128)S(1)}, f32[256,128]{1,0:T(8,128)S(1)}, u32[]{:S(2)}, u32[]{:S(2)}) collective-permute-start(f32[256,128]{1,0:T(8,128)S(1)} %pad_maximum_fusion.6), channel_id=1, source_target_pairs={{0,8},{2,10},{4,12},{6,14},{8,0},{10,2},{12,4},{14,6},{16,24},{18,... | collective-permute-start | bytes 393224 | tf_op jit(solution)/shard_map/ppermute | solution.py:93
  46.6 4.0 %collective-permute-start.7 = (f32[512,128]{1,0:T(8,128)}, f32[512,128]{1,0:T(8,128)}, u32[]{:S(2)}, u32[]{:S(2)}) collective-permute-start(f32[512,128]{1,0:T(8,128)} %pad_maximum_fusion.1), channel_id=1, source_target_pairs={{0,2},{2,0},{4,6},{6,4},{8,10},{10,8},{12,14},{14,12},{16,18},{18,... | collective-permute-start | bytes 786440 | tf_op jit(solution)/shard_map/ppermute | solution.py:93
  49.5 1.9 %collective-permute-start.14 = (f32[512,128]{1,0:T(8,128)}, f32[512,128]{1,0:T(8,128)}, u32[]{:S(2)}, u32[]{:S(2)}) collective-permute-start(f32[512,128]{1,0:T(8,128)} %pad_maximum_fusion.2), channel_id=1, source_target_pairs={{0,2},{2,0},{4,6},{6,4},{8,10},{10,8},{12,14},{14,12},{16,18},{18,... | collective-permute-start | bytes 786440 | tf_op jit(solution)/shard_map/ppermute | solution.py:93
  49.5 3.9 %copy-start.3 = (f32[1024,64]{0,1:T(8,128)S(1)}, f32[1024,64]{0,1:T(8,128)}, u32[]{:S(2)}) copy-start(f32[1024,64]{0,1:T(8,128)} %param.9) | copy-start | bytes 786436
  55.5 1.6 %collective-permute-start.22 = (f32[512,128]{1,0:T(8,128)S(1)}, f32[512,128]{1,0:T(8,128)S(1)}, u32[]{:S(2)}, u32[]{:S(2)}) collective-permute-start(f32[512,128]{1,0:T(8,128)S(1)} %constant_dynamic-slice_fusion.2), channel_id=1, source_target_pairs={{0,2},{2,0},{4,6},{6,4},{8,10},{10,8},{12,14},{14,12},{16,18},{18,... | collective-permute-start | bytes 786440 | tf_op jit(solution)/shard_map/ppermute | solution.py:81
  55.8 1.8 %collective-permute-start.15 = (f32[512,128]{1,0:T(8,128)S(1)}, f32[512,128]{1,0:T(8,128)S(1)}, u32[]{:S(2)}, u32[]{:S(2)}) collective-permute-start(f32[512,128]{1,0:T(8,128)S(1)} %constant_dynamic-slice_fusion.5), channel_id=1, source_target_pairs={{0,2},{2,0},{4,6},{6,4},{8,10},{10,8},{12,14},{14,12},{16,18},{18,... | collective-permute-start | bytes 786440 | tf_op jit(solution)/shard_map/ppermute | solution.py:81
  57.1 5.6 %collective-permute-start.23 = (f32[256,128]{1,0:T(8,128)S(1)}, f32[256,128]{1,0:T(8,128)S(1)}, u32[]{:S(2)}, u32[]{:S(2)}) collective-permute-start(f32[256,128]{1,0:T(8,128)S(1)} %constant_dynamic-slice_fusion.1), channel_id=1, source_target_pairs={{0,8},{2,10},{4,12},{6,14},{8,0},{10,2},{12,4},{14,6},{16,24},{18,... | collective-permute-start | bytes 393224 | tf_op jit(solution)/shard_map/ppermute | solution.py:81
  57.7 5.6 %collective-permute-start.16 = (f32[256,128]{1,0:T(8,128)S(1)}, f32[256,128]{1,0:T(8,128)S(1)}, u32[]{:S(2)}, u32[]{:S(2)}) collective-permute-start(f32[256,128]{1,0:T(8,128)S(1)} %constant_dynamic-slice_fusion.4), channel_id=1, source_target_pairs={{0,4},{2,6},{4,0},{6,2},{8,12},{10,14},{12,8},{14,10},{16,20},{18,... | collective-permute-start | bytes 393224 | tf_op jit(solution)/shard_map/ppermute | solution.py:81
  62.8 4.3 %collective-permute-start.24 = (f32[128,128]{1,0:T(8,128)S(1)}, f32[128,128]{1,0:T(8,128)S(1)}, u32[]{:S(2)}, u32[]{:S(2)}) collective-permute-start(f32[128,128]{1,0:T(8,128)S(1)} %constant_dynamic-slice_fusion), channel_id=1, source_target_pairs={{0,4},{2,6},{4,0},{6,2},{8,12},{10,14},{12,8},{14,10},{16,20},{18,... | collective-permute-start | bytes 196616 | tf_op jit(solution)/shard_map/ppermute | solution.py:81
  63.3 6.4 %collective-permute-start.17 = (f32[128,128]{1,0:T(8,128)S(1)}, f32[128,128]{1,0:T(8,128)S(1)}, u32[]{:S(2)}, u32[]{:S(2)}) collective-permute-start(f32[128,128]{1,0:T(8,128)S(1)} %constant_dynamic-slice_fusion.3), channel_id=1, source_target_pairs={{0,8},{2,10},{4,12},{6,14},{8,0},{10,2},{12,4},{14,6},{16,24},{18,... | collective-permute-start | bytes 196616 | tf_op jit(solution)/shard_map/ppermute | solution.py:81
  67.1 6.9 %collective-permute-start.25 = (f32[128,128]{1,0:T(8,128)S(1)}, f32[128,128]{1,0:T(8,128)S(1)}, u32[]{:S(2)}, u32[]{:S(2)}) collective-permute-start(f32[128,128]{1,0:T(8,128)S(1)} %dynamic-slice_add_fusion.8), channel_id=1, source_target_pairs={{0,16},{2,18},{4,20},{6,22},{8,24},{10,26},{12,28},{14,30},{16,0},... | collective-permute-start | bytes 196616 | tf_op jit(solution)/shard_map/ppermute | solution.py:89
  69.7 5.9 %collective-permute-start.18 = (f32[128,128]{1,0:T(8,128)S(1)}, f32[128,128]{1,0:T(8,128)S(1)}, u32[]{:S(2)}, u32[]{:S(2)}) collective-permute-start(f32[128,128]{1,0:T(8,128)S(1)} %dynamic-slice_add_fusion.9), channel_id=1, source_target_pairs={{0,16},{2,18},{4,20},{6,22},{8,24},{10,26},{12,28},{14,30},{16,0},... | collective-permute-start | bytes 196616 | tf_op jit(solution)/shard_map/ppermute | solution.py:89
  74.0 4.3 %collective-permute-start.26 = (f32[128,128]{1,0:T(8,128)S(1)}, f32[128,128]{1,0:T(8,128)S(1)}, u32[]{:S(2)}, u32[]{:S(2)}) collective-permute-start(f32[128,128]{1,0:T(8,128)S(1)} %add_subtract_fusion), channel_id=1, source_target_pairs={{0,4},{2,6},{4,0},{6,2},{8,12},{10,14},{12,8},{14,10},{16,20},{18,... | collective-permute-start | bytes 196616 | tf_op jit(solution)/shard_map/ppermute | solution.py:93
  75.7 4.3 %collective-permute-start.19 = (f32[128,128]{1,0:T(8,128)S(1)}, f32[128,128]{1,0:T(8,128)S(1)}, u32[]{:S(2)}, u32[]{:S(2)}) collective-permute-start(f32[128,128]{1,0:T(8,128)S(1)} %add_subtract_fusion.1), channel_id=1, source_target_pairs={{0,8},{2,10},{4,12},{6,14},{8,0},{10,2},{12,4},{14,6},{16,24},{18,... | collective-permute-start | bytes 196616 | tf_op jit(solution)/shard_map/ppermute | solution.py:93
  78.4 5.0 %collective-permute-start.27 = (f32[256,128]{1,0:T(8,128)S(1)}, f32[256,128]{1,0:T(8,128)S(1)}, u32[]{:S(2)}, u32[]{:S(2)}) collective-permute-start(f32[256,128]{1,0:T(8,128)S(1)} %pad_maximum_fusion.8), channel_id=1, source_target_pairs={{0,8},{2,10},{4,12},{6,14},{8,0},{10,2},{12,4},{14,6},{16,24},{18,... | collective-permute-start | bytes 393224 | tf_op jit(solution)/shard_map/ppermute | solution.py:93
  80.0 5.0 %collective-permute-start.20 = (f32[256,128]{1,0:T(8,128)S(1)}, f32[256,128]{1,0:T(8,128)S(1)}, u32[]{:S(2)}, u32[]{:S(2)}) collective-permute-start(f32[256,128]{1,0:T(8,128)S(1)} %pad_maximum_fusion.7), channel_id=1, source_target_pairs={{0,4},{2,6},{4,0},{6,2},{8,12},{10,14},{12,8},{14,10},{16,20},{18,... | collective-permute-start | bytes 393224 | tf_op jit(solution)/shard_map/ppermute | solution.py:93
  83.4 1.8 %collective-permute-start.28 = (f32[512,128]{1,0:T(8,128)S(1)}, f32[512,128]{1,0:T(8,128)S(1)}, u32[]{:S(2)}, u32[]{:S(2)}) collective-permute-start(f32[512,128]{1,0:T(8,128)S(1)} %pad_maximum_fusion.4), channel_id=1, source_target_pairs={{0,2},{2,0},{4,6},{6,4},{8,10},{10,8},{12,14},{14,12},{16,18},{18,... | collective-permute-start | bytes 786440 | tf_op jit(solution)/shard_map/ppermute | solution.py:93
  85.1 1.6 %collective-permute-start.21 = (f32[512,128]{1,0:T(8,128)S(1)}, f32[512,128]{1,0:T(8,128)S(1)}, u32[]{:S(2)}, u32[]{:S(2)}) collective-permute-start(f32[512,128]{1,0:T(8,128)S(1)} %pad_maximum_fusion.3), channel_id=1, source_target_pairs={{0,2},{2,0},{4,6},{6,4},{8,10},{10,8},{12,14},{14,12},{16,18},{18,... | collective-permute-start | bytes 786440 | tf_op jit(solution)/shard_map/ppermute | solution.py:93
  (2 other events, 3.6 us)

commit v14 on v12

--- a/solution.py
+++ b/solution.py
@@ -119,20 +119,25 @@
         def own_slice(matrix):
             return lax.dynamic_slice_in_dim(matrix, my_index * own_count, own_count, 0)
 
-        first_sum = product(factor_panel[0], solved_before)
-        first_sum, inverse_pieces = lax.optimization_barrier((first_sum, inverse_pieces))
         chained = power_of_two and n >= 4
+        if chained:
+            width = solved_before.shape[1] // 2
+            first_sums = [product(factor_panel[0], solved_before[:, :width])]
+            second_input, inverse_pieces = lax.optimization_barrier((first_sums[0], (solved_before, inverse_pieces)))[1]
+            first_sums.append(product(factor_panel[0], second_input[:, width:]))
+        else:
+            first_sum = product(factor_panel[0], solved_before)
+            first_sum, inverse_pieces = lax.optimization_barrier((first_sum, inverse_pieces))
         if not chained:
             panel_sum = product(factor_panel[1], solved_before)
         if chained:
             k = n.bit_length() - 1
             orders = (list(range(k)), [0, 2, 1] + list(range(3, k)) if k >= 3 else list(range(k)))
-            width = first_sum.shape[1] // 2
             columns = (slice(0, width), slice(width, 2 * width))
             first_blocks = []
             for chain, (order, cols) in enumerate(zip(orders, columns)):
                 remains, got_riders = ordered_reduce_then_gather(
-                    first_sum[:, cols], right_side[0][:, cols], "blk", n, order,
+                    first_sums[chain], right_side[0][:, cols], "blk", n, order,
                     inverse_pieces if chain == 0 else None,
                     (solved_before, lambda held: product(factor_panel[1], held)) if chain == 0 else None,
                 )

time: 76.8 us -> 89.8 us (1.17)
  matrix products: 12.5 us -> 19.8 us
  other arithmetic: 1.47 us -> 3.5 us
  starting transfers between devices: 26.3 us -> 27.9 us
  waiting for transfers between devices: 33.6 us -> 34.9 us
    dot_general x8 -> x9, matrix products: 12.5 us -> 19.8 us  [product(): jnp.dot(left, right, precision=lax.Precision.HIGHEST, preferred_element_t...]
    ppermute x4, starting transfers between devices: 6.59 us -> 8.7 us  [ordered_reduce_then_gather(): y = y + lax.ppermute(y, axis, [(i, i ^ 1 << top) for i in range(n)])]
    ppermute x4, waiting for transfers between devices: 6.99 us -> 8.49 us  [ordered_reduce_then_gather(): y = y + lax.ppermute(y, axis, [(i, i ^ 1 << top) for i in range(n)])]
    ppermute x12, starting transfers between devices: 10.3 us -> 8.94 us  [ordered_reduce_then_gather(): got = lax.ppermute(send, axis, [(i, i ^ 1 << j) for i in range(n)])]
    another operation x1, other arithmetic: 0.05 us -> 1.13 us  [doubling_gather(): y = jnp.stack([low, high], 1).reshape((-1,) + x.shape)]
    add x12, other arithmetic: 0.24 us -> 1.19 us  [ordered_reduce_then_gather(): y = keep + got]
  transfers between devices with their start and end apart: 29 -> 29, of which waited for: 21 -> 19; matrix products, arithmetic and copies ran while one was open for 16% -> 25% of each run, Pallas kernels for 0% -> 0%
where the time goes in v14:
time: 89.8 us; the launch traced here: 89.6 us
  waiting for transfers between devices  34.9 us (39%)
  starting transfers between devices  27.9 us (31%)
  matrix products  19.8 us (22%)
  other arithmetic  3.5 us (4%)
  local copies, waits for them, and re-layouts  3.03 us (3%)
    dot_general x9, matrix products, product(): jnp.dot(left, right, precision=lax.Precision.HIGHEST, preferred_element_t...  19.8 us
    ppermute x12, waiting for transfers between devices, ordered_reduce_then_gather(): got = lax.ppermute(y, axis, [(i, i ^ 1 << j) for i in range(n)])  16 us
    ppermute x12, waiting for transfers between devices, ordered_reduce_then_gather(): got = lax.ppermute(send, axis, [(i, i ^ 1 << j) for i in range(n)])  10.3 us
    ppermute x12, starting transfers between devices, ordered_reduce_then_gather(): got = lax.ppermute(send, axis, [(i, i ^ 1 << j) for i in range(n)])  8.94 us
    ppermute x4, starting transfers between devices, ordered_reduce_then_gather(): y = y + lax.ppermute(y, axis, [(i, i ^ 1 << top) for i in range(n)])  8.7 us
    ppermute x4, waiting for transfers between devices, ordered_reduce_then_gather(): y = y + lax.ppermute(y, axis, [(i, i ^ 1 << top) for i in range(n)])  8.49 us
    ppermute x12, starting transfers between devices, ordered_reduce_then_gather(): got = lax.ppermute(y, axis, [(i, i ^ 1 << j) for i in range(n)])  7.3 us
    ppermute x1, starting transfers between devices, doubling_gather(): got = lax.ppermute(y, axis, [(i, i ^ 1 << j) for i in range(n)])  2.94 us
  transfers between devices with their start and end apart: 29, of which 19 were waited for; matrix products, arithmetic and copies ran while one was open for 25% of the time, Pallas kernels for 0%

profile of v14, /device:TPU:0, one launch (start us, length us, event | category | flops | bytes accessed | tf_op | source)
XLA Modules:
  0.0 89.6 jit_solution(3706907666196652576)
XLA Ops:
  0.0 2.9 %collective-permute-start.2 = (f32[1,1,2,64,512]{4,3,2,1,0:T(8,128)}, f32[1,1,2,64,512]{4,3,2,1,0:T(8,128)}, u32[]{:S(2)}, u32[]{:S(2)}) collective-permute-start(f32[1,1,2,64,512]{4,3,2,1,0:T(8,128)} %bitcast.54), channel_id=1, source_target_pairs={{0,1},{1,0},{2,3},{3,2},{4,5},{5,4},{6,7},{7,6},{8,9},{9,8},{10,11... | collective-permute-start | bytes 786440 | tf_op jit(solution)/shard_map/ppermute | solution.py:34
  2.9 5.3 %fusion.4 = f32[1024,128]{1,0:T(8,128)S(1)} fusion(f32[2,1024,1024]{2,1,0:T(8,128)} %param.5, f32[1024,256]{1,0:T(8,128)} %param.6), kind=kOutput, calls=%fused_computation.4 | convolution fusion | flops 1610612736 | bytes 5242880 | tf_op jit(solution)/shard_map/dot_general | solution.py:8
  9.1 1.8 %slice_bitcast_fusion = (f32[1024,256]{1,0:T(8,128)S(1)}, f32[1024,256]{1,0:T(8,128)S(1)}) fusion(f32[2,1024,256]{2,1,0:T(8,128)} %param.7), kind=kLoop, calls=%fused_computation.12 | loop fusion | bytes 4194304 | tf_op jit(solution)/shard_map/squeeze | solution.py:152
  11.0 1.1 %select_bitcast_fusion.1 = (f32[1,1,1,2,64,512]{5,4,3,2,1,0:T(8,128)S(1)}, f32[1,1,1,2,64,512]{5,4,3,2,1,0:T(8,128)S(1)}) fusion(f32[1,1,2,64,512]{4,3,2,1,0:T(8,128)} %collective-permute-done.2, pred[]{:T(512)S(6)} %eq.8, f32[2,64,512]{2,1,0:T(8,128)} %param.8), kind=kLoop, calls=%fused_computation.52 | loop fusion | flops 131072 | bytes 1048577 | tf_op jit(solution)/shard_map/stack | solution.py:37
  12.2 5.2 %fusion.2 = f32[128,1024]{0,1:T(8,128)S(1)} fusion(f32[2,1024,1024]{2,1,0:T(8,128)} %param.5, f32[1024,256]{1,0:T(8,128)S(1)} %copy-done.1), kind=kOutput, calls=%fused_computation.2 | convolution fusion | flops 1610612736 | bytes 5242880 | tf_op jit(solution)/shard_map/dot_general | solution.py:8
  18.0 1.0 %dynamic-slice_add_fusion.2 = f32[512,128]{1,0:T(8,128)S(1)} fusion(f32[512,128]{1,0:T(8,128)} %collective-permute-done, f32[1024,128]{1,0:T(8,128)S(1)} %copy-done.3, s32[]{:T(128)S(6)} %select_n.190), kind=kLoop, calls=%fused_computation.53 | loop fusion | flops 65536 | bytes 786436 | tf_op jit(solution)/shard_map/add | solution.py:81
  19.0 1.6 %collective-permute-start.1 = (f32[256,128]{1,0:T(8,128)S(1)}, f32[256,128]{1,0:T(8,128)S(1)}, u32[]{:S(2)}, u32[]{:S(2)}) collective-permute-start(f32[256,128]{1,0:T(8,128)S(1)} %constant_dynamic-slice_fusion.9), channel_id=1, source_target_pairs={{0,4},{2,6},{4,0},{6,2},{8,12},{10,14},{12,8},{14,10},{16,20},{18,... | collective-permute-start | bytes 393224 | tf_op jit(solution)/shard_map/ppermute | solution.py:78
  20.6 5.5 %fusion.9 = f32[1024,256]{1,0:T(8,128)S(1)} fusion(f32[1024,256]{1,0:T(8,128)S(1)} %copy-done.1, f32[2,1024,1024]{2,1,0:T(8,128)} %param.5), kind=kOutput, calls=%fused_computation.9 | convolution fusion | flops 3221225472 | bytes 6291456 | tf_op jit(solution)/shard_map/dot_general | solution.py:8
  26.1 1.6 %collective-permute-start.3 = (f32[128,128]{1,0:T(8,128)S(1)}, f32[128,128]{1,0:T(8,128)S(1)}, u32[]{:S(2)}, u32[]{:S(2)}) collective-permute-start(f32[128,128]{1,0:T(8,128)S(1)} %constant_dynamic-slice_fusion.8), channel_id=1, source_target_pairs={{0,8},{2,10},{4,12},{6,14},{8,0},{10,2},{12,4},{14,6},{16,24},{18,... | collective-permute-start | bytes 196616 | tf_op jit(solution)/shard_map/ppermute | solution.py:78
  28.4 2.4 %collective-permute-done.3 = f32[128,128]{1,0:T(8,128)S(1)} collective-permute-done((f32[128,128]{1,0:T(8,128)S(1)}, f32[128,128]{1,0:T(8,128)S(1)}, u32[]{:S(2)}, u32[]{:S(2)}) %collective-permute-start.3) | collective-permute-done | bytes 65568 | tf_op jit(solution)/shard_map/ppermute | solution.py:78
  30.8 2.7 %collective-permute-start.4 = (f32[128,128]{1,0:T(8,128)S(1)}, f32[128,128]{1,0:T(8,128)S(1)}, u32[]{:S(2)}, u32[]{:S(2)}) collective-permute-start(f32[128,128]{1,0:T(8,128)S(1)} %dynamic-slice_add_fusion.10), channel_id=1, source_target_pairs={{0,16},{2,18},{4,20},{6,22},{8,24},{10,26},{12,28},{14,30},{16,0},... | collective-permute-start | bytes 196616 | tf_op jit(solution)/shard_map/ppermute | solution.py:86
  34.6 1.6 %collective-permute-done.4 = f32[128,128]{1,0:T(8,128)S(1)} collective-permute-done((f32[128,128]{1,0:T(8,128)S(1)}, f32[128,128]{1,0:T(8,128)S(1)}, u32[]{:S(2)}, u32[]{:S(2)}) %collective-permute-start.4) | collective-permute-done | bytes 65568 | tf_op jit(solution)/shard_map/ppermute | solution.py:86
  36.2 1.9 %collective-permute-start.5 = (f32[128,128]{1,0:T(8,128)S(1)}, f32[128,128]{1,0:T(8,128)S(1)}, u32[]{:S(2)}, u32[]{:S(2)}) collective-permute-start(f32[128,128]{1,0:T(8,128)S(1)} %add_subtract_fusion.3), channel_id=1, source_target_pairs={{0,8},{2,10},{4,12},{6,14},{8,0},{10,2},{12,4},{14,6},{16,24},{18,... | collective-permute-start | bytes 196616 | tf_op jit(solution)/shard_map/ppermute | solution.py:90
  38.4 2.7 %collective-permute-start.11 = (f32[128,128]{1,0:T(8,128)S(1)}, f32[128,128]{1,0:T(8,128)S(1)}, u32[]{:S(2)}, u32[]{:S(2)}) collective-permute-start(f32[128,128]{1,0:T(8,128)S(1)} %dynamic-slice_add_fusion.9), channel_id=1, source_target_pairs={{0,16},{2,18},{4,20},{6,22},{8,24},{10,26},{12,28},{14,30},{16,0},... | collective-permute-start | bytes 196616 | tf_op jit(solution)/shard_map/ppermute | solution.py:86
  41.1 2.5 %collective-permute-done.11 = f32[128,128]{1,0:T(8,128)S(1)} collective-permute-done((f32[128,128]{1,0:T(8,128)S(1)}, f32[128,128]{1,0:T(8,128)S(1)}, u32[]{:S(2)}, u32[]{:S(2)}) %collective-permute-start.11) | collective-permute-done | bytes 65568 | tf_op jit(solution)/shard_map/ppermute | solution.py:86
  44.2 1.6 %collective-permute-start.6 = (f32[256,128]{1,0:T(8,128)S(1)}, f32[256,128]{1,0:T(8,128)S(1)}, u32[]{:S(2)}, u32[]{:S(2)}) collective-permute-start(f32[256,128]{1,0:T(8,128)S(1)} %pad_maximum_fusion.5), channel_id=1, source_target_pairs={{0,4},{2,6},{4,0},{6,2},{8,12},{10,14},{12,8},{14,10},{16,20},{18,... | collective-permute-start | bytes 393224 | tf_op jit(solution)/shard_map/ppermute | solution.py:90
  45.8 2.2 %collective-permute-done.12 = f32[128,128]{1,0:T(8,128)S(1)} collective-permute-done((f32[128,128]{1,0:T(8,128)S(1)}, f32[128,128]{1,0:T(8,128)S(1)}, u32[]{:S(2)}, u32[]{:S(2)}) %collective-permute-start.12) | collective-permute-done | bytes 65568 | tf_op jit(solution)/shard_map/ppermute | solution.py:90
  48.0 1.5 %collective-permute-start.13 = (f32[256,128]{1,0:T(8,128)S(1)}, f32[256,128]{1,0:T(8,128)S(1)}, u32[]{:S(2)}, u32[]{:S(2)}) collective-permute-start(f32[256,128]{1,0:T(8,128)S(1)} %pad_maximum_fusion.6), channel_id=1, source_target_pairs={{0,8},{2,10},{4,12},{6,14},{8,0},{10,2},{12,4},{14,6},{16,24},{18,... | collective-permute-start | bytes 393224 | tf_op jit(solution)/shard_map/ppermute | solution.py:90
  49.6 3.4 %collective-permute-done.13 = f32[256,128]{1,0:T(8,128)S(1)} collective-permute-done((f32[256,128]{1,0:T(8,128)S(1)}, f32[256,128]{1,0:T(8,128)S(1)}, u32[]{:S(2)}, u32[]{:S(2)}) %collective-permute-start.13) | collective-permute-done | bytes 131104 | tf_op jit(solution)/shard_map/ppermute | solution.py:90
  53.6 1.0 %collective-permute-done.14 = f32[512,128]{1,0:T(8,128)S(1)} collective-permute-done((f32[512,128]{1,0:T(8,128)S(1)}, f32[512,128]{1,0:T(8,128)S(1)}, u32[]{:S(2)}, u32[]{:S(2)}) %collective-permute-start.14) | collective-permute-done | bytes 262176 | tf_op jit(solution)/shard_map/ppermute | solution.py:90
  55.2 1.0 %convolution_bitcast_fusion = f32[1024,128]{1,0:T(8,128)S(1)} fusion(f32[64,128]{1,0:T(8,128)S(1)} %fusion.16, f32[1024,64]{0,1:T(8,128)S(1)} %copy-done), kind=kOutput, calls=%fused_computation.10 | convolution fusion | flops 100663296 | bytes 819200 | tf_op jit(solution)/shard_map/dot_general | solution.py:8
  56.2 1.0 %slice_add_fusion.1 = (f32[1024,128]{1,0:T(8,128)S(1)}, f32[1024,128]{1,0:T(8,128)S(1)}) fusion(f32[1024,256]{1,0:T(8,128)S(1)} %fusion.9, f32[1024,128]{1,0:T(8,128)S(1)} %convolution_bitcast_fusion, f32[64,128]{1,0:T(8,128)S(1)} %fusion.12, f32[1024,64]{0,1:T(8,128)S(1)} %copy-done), kind=kOutput, calls=%fused_computation.34 | convolution fusion | flops 100925440 | bytes 2916352 | tf_op jit(solution)/shard_map/dot_general | solution.py:8
  58.9 1.5 %collective-permute-start.23 = (f32[256,128]{1,0:T(8,128)S(1)}, f32[256,128]{1,0:T(8,128)S(1)}, u32[]{:S(2)}, u32[]{:S(2)}) collective-permute-start(f32[256,128]{1,0:T(8,128)S(1)} %constant_dynamic-slice_fusion.1), channel_id=1, source_target_pairs={{0,8},{2,10},{4,12},{6,14},{8,0},{10,2},{12,4},{14,6},{16,24},{18,... | collective-permute-start | bytes 393224 | tf_op jit(solution)/shard_map/ppermute | solution.py:78
  61.0 3.4 %collective-permute-done.23 = f32[256,128]{1,0:T(8,128)S(1)} collective-permute-done((f32[256,128]{1,0:T(8,128)S(1)}, f32[256,128]{1,0:T(8,128)S(1)}, u32[]{:S(2)}, u32[]{:S(2)}) %collective-permute-start.23) | collective-permute-done | bytes 131104 | tf_op jit(solution)/shard_map/ppermute | solution.py:78
  66.7 2.2 %collective-permute-done.24 = f32[128,128]{1,0:T(8,128)S(1)} collective-permute-done((f32[128,128]{1,0:T(8,128)S(1)}, f32[128,128]{1,0:T(8,128)S(1)}, u32[]{:S(2)}, u32[]{:S(2)}) %collective-permute-start.24) | collective-permute-done | bytes 65568 | tf_op jit(solution)/shard_map/ppermute | solution.py:78
  68.9 2.7 %collective-permute-start.25 = (f32[128,128]{1,0:T(8,128)S(1)}, f32[128,128]{1,0:T(8,128)S(1)}, u32[]{:S(2)}, u32[]{:S(2)}) collective-permute-start(f32[128,128]{1,0:T(8,128)S(1)} %dynamic-slice_add_fusion.7), channel_id=1, source_target_pairs={{0,16},{2,18},{4,20},{6,22},{8,24},{10,26},{12,28},{14,30},{16,0},... | collective-permute-start | bytes 196616 | tf_op jit(solution)/shard_map/ppermute | solution.py:86
  72.2 3.4 %collective-permute-done.25 = f32[128,128]{1,0:T(8,128)S(1)} collective-permute-done((f32[128,128]{1,0:T(8,128)S(1)}, f32[128,128]{1,0:T(8,128)S(1)}, u32[]{:S(2)}, u32[]{:S(2)}) %collective-permute-start.25) | collective-permute-done | bytes 65568 | tf_op jit(solution)/shard_map/ppermute | solution.py:86
  77.4 2.6 %collective-permute-done.26 = f32[128,128]{1,0:T(8,128)S(1)} collective-permute-done((f32[128,128]{1,0:T(8,128)S(1)}, f32[128,128]{1,0:T(8,128)S(1)}, u32[]{:S(2)}, u32[]{:S(2)}) %collective-permute-start.26) | collective-permute-done | bytes 65568 | tf_op jit(solution)/shard_map/ppermute | solution.py:90
  80.1 1.6 %collective-permute-done.19 = f32[128,128]{1,0:T(8,128)S(1)} collective-permute-done((f32[128,128]{1,0:T(8,128)S(1)}, f32[128,128]{1,0:T(8,128)S(1)}, u32[]{:S(2)}, u32[]{:S(2)}) %collective-permute-start.19) | collective-permute-done | bytes 65568 | tf_op jit(solution)/shard_map/ppermute | solution.py:90
  82.3 2.8 %collective-permute-done.27 = f32[256,128]{1,0:T(8,128)S(1)} collective-permute-done((f32[256,128]{1,0:T(8,128)S(1)}, f32[256,128]{1,0:T(8,128)S(1)}, u32[]{:S(2)}, u32[]{:S(2)}) %collective-permute-start.27) | collective-permute-done | bytes 131104 | tf_op jit(solution)/shard_map/ppermute | solution.py:90
  85.2 1.6 %collective-permute-done.20 = f32[256,128]{1,0:T(8,128)S(1)} collective-permute-done((f32[256,128]{1,0:T(8,128)S(1)}, f32[256,128]{1,0:T(8,128)S(1)}, u32[]{:S(2)}, u32[]{:S(2)}) %collective-permute-start.20) | collective-permute-done | bytes 131104 | tf_op jit(solution)/shard_map/ppermute | solution.py:90
  87.4 1.0 %collective-permute-done.21 = f32[512,128]{1,0:T(8,128)S(1)} collective-permute-done((f32[512,128]{1,0:T(8,128)S(1)}, f32[512,128]{1,0:T(8,128)S(1)}, u32[]{:S(2)}, u32[]{:S(2)}) %collective-permute-start.21) | collective-permute-done | bytes 262176 | tf_op jit(solution)/shard_map/ppermute | solution.py:90
  (99 shorter events, 14.8 us)
Async XLA Ops:
  0.0 55.2 %copy-start = (f32[1024,64]{0,1:T(8,128)S(1)}, f32[1024,64]{0,1:T(8,128)}, u32[]{:S(2)}) copy-start(f32[1024,64]{0,1:T(8,128)} %param.9) | copy-start | bytes 786436
  0.0 11.0 %collective-permute-start.2 = (f32[1,1,2,64,512]{4,3,2,1,0:T(8,128)}, f32[1,1,2,64,512]{4,3,2,1,0:T(8,128)}, u32[]{:S(2)}, u32[]{:S(2)}) collective-permute-start(f32[1,1,2,64,512]{4,3,2,1,0:T(8,128)} %bitcast.54), channel_id=1, source_target_pairs={{0,1},{1,0},{2,3},{3,2},{4,5},{5,4},{6,7},{7,6},{8,9},{9,8},{10,11... | collective-permute-start | bytes 786440 | tf_op jit(solution)/shard_map/ppermute | solution.py:34
  9.0 8.9 %collective-permute-start = (f32[512,128]{1,0:T(8,128)}, f32[512,128]{1,0:T(8,128)}, u32[]{:S(2)}, u32[]{:S(2)}) collective-permute-start(f32[512,128]{1,0:T(8,128)} %constant_dynamic-slice_fusion.10), channel_id=1, source_target_pairs={{0,2},{2,0},{4,6},{6,4},{8,10},{10,8},{12,14},{14,12},{16,18},{18,... | collective-permute-start | bytes 786440 | tf_op jit(solution)/shard_map/ppermute | solution.py:78
  9.1 3.1 %copy-start.1 = (f32[1024,256]{1,0:T(8,128)S(1)}, f32[1024,256]{1,0:T(8,128)}, u32[]{:S(2)}) copy-start(f32[1024,256]{1,0:T(8,128)} %param.6) | copy-start | bytes 3145732
  11.0 7.0 %copy-start.3 = (f32[1024,128]{1,0:T(8,128)S(1)}, f32[1024,128]{1,0:T(8,128)}, u32[]{:S(2)}) copy-start(f32[1024,128]{1,0:T(8,128)} %copy-done.2) | copy-start | bytes 1572868
  17.5 10.3 %collective-permute-start.8 = (f32[512,128]{1,0:T(8,128)S(1)}, f32[512,128]{1,0:T(8,128)S(1)}, u32[]{:S(2)}, u32[]{:S(2)}) collective-permute-start(f32[512,128]{1,0:T(8,128)S(1)} %dynamic-slice_bitcast_fusion), channel_id=1, source_target_pairs={{0,2},{2,0},{4,6},{6,4},{8,10},{10,8},{12,14},{14,12},{16,18},{18,... | collective-permute-start | bytes 786440 | tf_op jit(solution)/shard_map/ppermute | solution.py:78
  19.0 7.1 %collective-permute-start.1 = (f32[256,128]{1,0:T(8,128)S(1)}, f32[256,128]{1,0:T(8,128)S(1)}, u32[]{:S(2)}, u32[]{:S(2)}) collective-permute-start(f32[256,128]{1,0:T(8,128)S(1)} %constant_dynamic-slice_fusion.9), channel_id=1, source_target_pairs={{0,4},{2,6},{4,0},{6,2},{8,12},{10,14},{12,8},{14,10},{16,20},{18,... | collective-permute-start | bytes 393224 | tf_op jit(solution)/shard_map/ppermute | solution.py:78
  26.1 4.7 %collective-permute-start.3 = (f32[128,128]{1,0:T(8,128)S(1)}, f32[128,128]{1,0:T(8,128)S(1)}, u32[]{:S(2)}, u32[]{:S(2)}) collective-permute-start(f32[128,128]{1,0:T(8,128)S(1)} %constant_dynamic-slice_fusion.8), channel_id=1, source_target_pairs={{0,8},{2,10},{4,12},{6,14},{8,0},{10,2},{12,4},{14,6},{16,24},{18,... | collective-permute-start | bytes 196616 | tf_op jit(solution)/shard_map/ppermute | solution.py:78
  27.9 6.1 %collective-permute-start.9 = (f32[256,128]{1,0:T(8,128)S(1)}, f32[256,128]{1,0:T(8,128)S(1)}, u32[]{:S(2)}, u32[]{:S(2)}) collective-permute-start(f32[256,128]{1,0:T(8,128)S(1)} %constant_dynamic-slice_fusion.7), channel_id=1, source_target_pairs={{0,8},{2,10},{4,12},{6,14},{8,0},{10,2},{12,4},{14,6},{16,24},{18,... | collective-permute-start | bytes 393224 | tf_op jit(solution)/shard_map/ppermute | solution.py:78
  30.8 5.3 %collective-permute-start.4 = (f32[128,128]{1,0:T(8,128)S(1)}, f32[128,128]{1,0:T(8,128)S(1)}, u32[]{:S(2)}, u32[]{:S(2)}) collective-permute-start(f32[128,128]{1,0:T(8,128)S(1)} %dynamic-slice_add_fusion.10), channel_id=1, source_target_pairs={{0,16},{2,18},{4,20},{6,22},{8,24},{10,26},{12,28},{14,30},{16,0},... | collective-permute-start | bytes 196616 | tf_op jit(solution)/shard_map/ppermute | solution.py:86
  34.0 4.3 %collective-permute-start.10 = (f32[128,128]{1,0:T(8,128)S(1)}, f32[128,128]{1,0:T(8,128)S(1)}, u32[]{:S(2)}, u32[]{:S(2)}) collective-permute-start(f32[128,128]{1,0:T(8,128)S(1)} %constant_dynamic-slice_fusion.6), channel_id=1, source_target_pairs={{0,4},{2,6},{4,0},{6,2},{8,12},{10,14},{12,8},{14,10},{16,20},{18,... | collective-permute-start | bytes 196616 | tf_op jit(solution)/shard_map/ppermute | solution.py:78
  36.2 4.8 %collective-permute-start.5 = (f32[128,128]{1,0:T(8,128)S(1)}, f32[128,128]{1,0:T(8,128)S(1)}, u32[]{:S(2)}, u32[]{:S(2)}) collective-permute-start(f32[128,128]{1,0:T(8,128)S(1)} %add_subtract_fusion.3), channel_id=1, source_target_pairs={{0,8},{2,10},{4,12},{6,14},{8,0},{10,2},{12,4},{14,6},{16,24},{18,... | collective-permute-start | bytes 196616 | tf_op jit(solution)/shard_map/ppermute | solution.py:90
  38.4 5.2 %collective-permute-start.11 = (f32[128,128]{1,0:T(8,128)S(1)}, f32[128,128]{1,0:T(8,128)S(1)}, u32[]{:S(2)}, u32[]{:S(2)}) collective-permute-start(f32[128,128]{1,0:T(8,128)S(1)} %dynamic-slice_add_fusion.9), channel_id=1, source_target_pairs={{0,16},{2,18},{4,20},{6,22},{8,24},{10,26},{12,28},{14,30},{16,0},... | collective-permute-start | bytes 196616 | tf_op jit(solution)/shard_map/ppermute | solution.py:86
  43.6 4.3 %collective-permute-start.12 = (f32[128,128]{1,0:T(8,128)S(1)}, f32[128,128]{1,0:T(8,128)S(1)}, u32[]{:S(2)}, u32[]{:S(2)}) collective-permute-start(f32[128,128]{1,0:T(8,128)S(1)} %add_subtract_fusion.2), channel_id=1, source_target_pairs={{0,4},{2,6},{4,0},{6,2},{8,12},{10,14},{12,8},{14,10},{16,20},{18,... | collective-permute-start | bytes 196616 | tf_op jit(solution)/shard_map/ppermute | solution.py:90
  44.2 5.3 %collective-permute-start.6 = (f32[256,128]{1,0:T(8,128)S(1)}, f32[256,128]{1,0:T(8,128)S(1)}, u32[]{:S(2)}, u32[]{:S(2)}) collective-permute-start(f32[256,128]{1,0:T(8,128)S(1)} %pad_maximum_fusion.5), channel_id=1, source_target_pairs={{0,4},{2,6},{4,0},{6,2},{8,12},{10,14},{12,8},{14,10},{16,20},{18,... | collective-permute-start | bytes 393224 | tf_op jit(solution)/shard_map/ppermute | solution.py:90
  48.0 5.0 %collective-permute-start.13 = (f32[256,128]{1,0:T(8,128)S(1)}, f32[256,128]{1,0:T(8,128)S(1)}, u32[]{:S(2)}, u32[]{:S(2)}) collective-permute-start(f32[256,128]{1,0:T(8,128)S(1)} %pad_maximum_fusion.6), channel_id=1, source_target_pairs={{0,8},{2,10},{4,12},{6,14},{8,0},{10,2},{12,4},{14,6},{16,24},{18,... | collective-permute-start | bytes 393224 | tf_op jit(solution)/shard_map/ppermute | solution.py:90
  49.6 3.6 %collective-permute-start.7 = (f32[512,128]{1,0:T(8,128)S(1)}, f32[512,128]{1,0:T(8,128)S(1)}, u32[]{:S(2)}, u32[]{:S(2)}) collective-permute-start(f32[512,128]{1,0:T(8,128)S(1)} %pad_maximum_fusion.1), channel_id=1, source_target_pairs={{0,2},{2,0},{4,6},{6,4},{8,10},{10,8},{12,14},{14,12},{16,18},{18,... | collective-permute-start | bytes 786440 | tf_op jit(solution)/shard_map/ppermute | solution.py:90
  53.1 1.6 %collective-permute-start.14 = (f32[512,128]{1,0:T(8,128)S(1)}, f32[512,128]{1,0:T(8,128)S(1)}, u32[]{:S(2)}, u32[]{:S(2)}) collective-permute-start(f32[512,128]{1,0:T(8,128)S(1)} %pad_maximum_fusion.2), channel_id=1, source_target_pairs={{0,2},{2,0},{4,6},{6,4},{8,10},{10,8},{12,14},{14,12},{16,18},{18,... | collective-permute-start | bytes 786440 | tf_op jit(solution)/shard_map/ppermute | solution.py:90
  57.2 1.6 %collective-permute-start.22 = (f32[512,128]{1,0:T(8,128)S(1)}, f32[512,128]{1,0:T(8,128)S(1)}, u32[]{:S(2)}, u32[]{:S(2)}) collective-permute-start(f32[512,128]{1,0:T(8,128)S(1)} %constant_dynamic-slice_fusion.2), channel_id=1, source_target_pairs={{0,2},{2,0},{4,6},{6,4},{8,10},{10,8},{12,14},{14,12},{16,18},{18,... | collective-permute-start | bytes 786440 | tf_op jit(solution)/shard_map/ppermute | solution.py:78
  57.5 2.9 %collective-permute-start.15 = (f32[512,128]{1,0:T(8,128)S(1)}, f32[512,128]{1,0:T(8,128)S(1)}, u32[]{:S(2)}, u32[]{:S(2)}) collective-permute-start(f32[512,128]{1,0:T(8,128)S(1)} %constant_dynamic-slice_fusion.5), channel_id=1, source_target_pairs={{0,2},{2,0},{4,6},{6,4},{8,10},{10,8},{12,14},{14,12},{16,18},{18,... | collective-permute-start | bytes 786440 | tf_op jit(solution)/shard_map/ppermute | solution.py:78
  58.9 5.6 %collective-permute-start.23 = (f32[256,128]{1,0:T(8,128)S(1)}, f32[256,128]{1,0:T(8,128)S(1)}, u32[]{:S(2)}, u32[]{:S(2)}) collective-permute-start(f32[256,128]{1,0:T(8,128)S(1)} %constant_dynamic-slice_fusion.1), channel_id=1, source_target_pairs={{0,8},{2,10},{4,12},{6,14},{8,0},{10,2},{12,4},{14,6},{16,24},{18,... | collective-permute-start | bytes 393224 | tf_op jit(solution)/shard_map/ppermute | solution.py:78
  60.5 5.3 %collective-permute-start.16 = (f32[256,128]{1,0:T(8,128)S(1)}, f32[256,128]{1,0:T(8,128)S(1)}, u32[]{:S(2)}, u32[]{:S(2)}) collective-permute-start(f32[256,128]{1,0:T(8,128)S(1)} %constant_dynamic-slice_fusion.4), channel_id=1, source_target_pairs={{0,4},{2,6},{4,0},{6,2},{8,12},{10,14},{12,8},{14,10},{16,20},{18,... | collective-permute-start | bytes 393224 | tf_op jit(solution)/shard_map/ppermute | solution.py:78
  64.5 4.3 %collective-permute-start.24 = (f32[128,128]{1,0:T(8,128)S(1)}, f32[128,128]{1,0:T(8,128)S(1)}, u32[]{:S(2)}, u32[]{:S(2)}) collective-permute-start(f32[128,128]{1,0:T(8,128)S(1)} %constant_dynamic-slice_fusion), channel_id=1, source_target_pairs={{0,4},{2,6},{4,0},{6,2},{8,12},{10,14},{12,8},{14,10},{16,20},{18,... | collective-permute-start | bytes 196616 | tf_op jit(solution)/shard_map/ppermute | solution.py:78
  65.8 5.7 %collective-permute-start.17 = (f32[128,128]{1,0:T(8,128)S(1)}, f32[128,128]{1,0:T(8,128)S(1)}, u32[]{:S(2)}, u32[]{:S(2)}) collective-permute-start(f32[128,128]{1,0:T(8,128)S(1)} %constant_dynamic-slice_fusion.3), channel_id=1, source_target_pairs={{0,8},{2,10},{4,12},{6,14},{8,0},{10,2},{12,4},{14,6},{16,24},{18,... | collective-permute-start | bytes 196616 | tf_op jit(solution)/shard_map/ppermute | solution.py:78
  68.9 6.8 %collective-permute-start.25 = (f32[128,128]{1,0:T(8,128)S(1)}, f32[128,128]{1,0:T(8,128)S(1)}, u32[]{:S(2)}, u32[]{:S(2)}) collective-permute-start(f32[128,128]{1,0:T(8,128)S(1)} %dynamic-slice_add_fusion.7), channel_id=1, source_target_pairs={{0,16},{2,18},{4,20},{6,22},{8,24},{10,26},{12,28},{14,30},{16,0},... | collective-permute-start | bytes 196616 | tf_op jit(solution)/shard_map/ppermute | solution.py:86
  71.6 5.8 %collective-permute-start.18 = (f32[128,128]{1,0:T(8,128)S(1)}, f32[128,128]{1,0:T(8,128)S(1)}, u32[]{:S(2)}, u32[]{:S(2)}) collective-permute-start(f32[128,128]{1,0:T(8,128)S(1)} %dynamic-slice_add_fusion.8), channel_id=1, source_target_pairs={{0,16},{2,18},{4,20},{6,22},{8,24},{10,26},{12,28},{14,30},{16,0},... | collective-permute-start | bytes 196616 | tf_op jit(solution)/shard_map/ppermute | solution.py:86
  75.7 4.3 %collective-permute-start.26 = (f32[128,128]{1,0:T(8,128)S(1)}, f32[128,128]{1,0:T(8,128)S(1)}, u32[]{:S(2)}, u32[]{:S(2)}) collective-permute-start(f32[128,128]{1,0:T(8,128)S(1)} %add_subtract_fusion), channel_id=1, source_target_pairs={{0,4},{2,6},{4,0},{6,2},{8,12},{10,14},{12,8},{14,10},{16,20},{18,... | collective-permute-start | bytes 196616 | tf_op jit(solution)/shard_map/ppermute | solution.py:90
  77.4 4.3 %collective-permute-start.19 = (f32[128,128]{1,0:T(8,128)S(1)}, f32[128,128]{1,0:T(8,128)S(1)}, u32[]{:S(2)}, u32[]{:S(2)}) collective-permute-start(f32[128,128]{1,0:T(8,128)S(1)} %add_subtract_fusion.1), channel_id=1, source_target_pairs={{0,8},{2,10},{4,12},{6,14},{8,0},{10,2},{12,4},{14,6},{16,24},{18,... | collective-permute-start | bytes 196616 | tf_op jit(solution)/shard_map/ppermute | solution.py:90
  80.0 5.0 %collective-permute-start.27 = (f32[256,128]{1,0:T(8,128)S(1)}, f32[256,128]{1,0:T(8,128)S(1)}, u32[]{:S(2)}, u32[]{:S(2)}) collective-permute-start(f32[256,128]{1,0:T(8,128)S(1)} %pad_maximum_fusion.8), channel_id=1, source_target_pairs={{0,8},{2,10},{4,12},{6,14},{8,0},{10,2},{12,4},{14,6},{16,24},{18,... | collective-permute-start | bytes 393224 | tf_op jit(solution)/shard_map/ppermute | solution.py:90
  81.7 5.0 %collective-permute-start.20 = (f32[256,128]{1,0:T(8,128)S(1)}, f32[256,128]{1,0:T(8,128)S(1)}, u32[]{:S(2)}, u32[]{:S(2)}) collective-permute-start(f32[256,128]{1,0:T(8,128)S(1)} %pad_maximum_fusion.7), channel_id=1, source_target_pairs={{0,4},{2,6},{4,0},{6,2},{8,12},{10,14},{12,8},{14,10},{16,20},{18,... | collective-permute-start | bytes 393224 | tf_op jit(solution)/shard_map/ppermute | solution.py:90
  85.1 1.8 %collective-permute-start.28 = (f32[512,128]{1,0:T(8,128)S(1)}, f32[512,128]{1,0:T(8,128)S(1)}, u32[]{:S(2)}, u32[]{:S(2)}) collective-permute-start(f32[512,128]{1,0:T(8,128)S(1)} %pad_maximum_fusion.4), channel_id=1, source_target_pairs={{0,2},{2,0},{4,6},{6,4},{8,10},{10,8},{12,14},{14,12},{16,18},{18,... | collective-permute-start | bytes 786440 | tf_op jit(solution)/shard_map/ppermute | solution.py:90
  86.8 1.6 %collective-permute-start.21 = (f32[512,128]{1,0:T(8,128)S(1)}, f32[512,128]{1,0:T(8,128)S(1)}, u32[]{:S(2)}, u32[]{:S(2)}) collective-permute-start(f32[512,128]{1,0:T(8,128)S(1)} %pad_maximum_fusion.3), channel_id=1, source_target_pairs={{0,2},{2,0},{4,6},{6,4},{8,10},{10,8},{12,14},{14,12},{16,18},{18,... | collective-permute-start | bytes 786440 | tf_op jit(solution)/shard_map/ppermute | solution.py:90
  (1 other events, 0.9 us)

commit v15 on v13

--- a/solution.py
+++ b/solution.py
@@ -135,10 +135,11 @@
             first_blocks = []
             for chain, (order, cols) in enumerate(zip(orders, columns)):
                 remains, got_riders = ordered_reduce_then_gather(
-                    first_sum, right_side[0], "blk", n, order,
+                    first_sum if chain == 0 else first_sum[:, cols], right_side[0] if chain == 0 else right_side[0][:, cols],
+                    "blk", n, order,
                     inverse_pieces if chain == 0 else None,
                     (solved_before, lambda held: product(factor_panel[1], held)) if chain == 0 else None,
-                    width, cols.start,
+                    width if chain == 0 else None,
                 )
                 if chain == 0:
                     panel_sum, inverse_pieces = got_riders

time: 88.1 us -> 83.5 us (0.948)
  waiting for transfers between devices: 38 us -> 33.3 us
  starting transfers between devices: 26.1 us -> 27.6 us
    ppermute x12, waiting for transfers between devices: 14.3 us -> 9.03 us  [ordered_reduce_then_gather(): got = lax.ppermute(send, axis, [(i, i ^ 1 << j) for i in range(n)])]
    ppermute x4, waiting for transfers between devices: 5.1 us -> 8.45 us  [ordered_reduce_then_gather(): y = y + lax.ppermute(y, axis, [(i, i ^ 1 << top) for i in range(n)])]
    ppermute x4, starting transfers between devices: 9.39 us -> 6.33 us  [ordered_reduce_then_gather(): y = y + lax.ppermute(y, axis, [(i, i ^ 1 << top) for i in range(n)])]
    ppermute x12, starting transfers between devices: 8.43 us -> 11.2 us  [ordered_reduce_then_gather(): got = lax.ppermute(send, axis, [(i, i ^ 1 << j) for i in range(n)])]
    ppermute x12, waiting for transfers between devices: 17.3 us -> 14.6 us  [ordered_reduce_then_gather(): got = lax.ppermute(y, axis, [(i, i ^ 1 << j) for i in range(n)])]
    slice x0 -> x3, local copies, waits for them, and re-layouts: none -> 2.1 us  [the longest x1 1.24 us: shards(): right_side[0]]
    ppermute x12, starting transfers between devices: 5.34 us -> 7.12 us  [ordered_reduce_then_gather(): got = lax.ppermute(y, axis, [(i, i ^ 1 << j) for i in range(n)])]
    concatenate x8, other arithmetic: 1.54 us -> 0.12 us  [ordered_reduce_then_gather(): y = jnp.concatenate([low, high], 0)]
  transfers between devices with their start and end apart: 29 -> 29, of which waited for: 22 -> 19; matrix products, arithmetic and copies ran while one was open for 18% -> 21% of each run, Pallas kernels for 0% -> 0%
where the time goes in v15:
time: 83.5 us; the launch traced here: 83.3 us
  waiting for transfers between devices  33.3 us (40%)
  starting transfers between devices  27.6 us (33%)
  matrix products  14.5 us (17%)
  other arithmetic  5 us (6%)
  local copies, waits for them, and re-layouts  2.45 us (3%)
    ppermute x12, waiting for transfers between devices, ordered_reduce_then_gather(): got = lax.ppermute(y, axis, [(i, i ^ 1 << j) for i in range(n)])  14.6 us
    dot_general x8, matrix products, product(): jnp.dot(left, right, precision=lax.Precision.HIGHEST, preferred_element_t...  14.5 us
    ppermute x12, starting transfers between devices, ordered_reduce_then_gather(): got = lax.ppermute(send, axis, [(i, i ^ 1 << j) for i in range(n)])  11.2 us
    ppermute x12, waiting for transfers between devices, ordered_reduce_then_gather(): got = lax.ppermute(send, axis, [(i, i ^ 1 << j) for i in range(n)])  9.03 us
    ppermute x4, waiting for transfers between devices, ordered_reduce_then_gather(): y = y + lax.ppermute(y, axis, [(i, i ^ 1 << top) for i in range(n)])  8.45 us
    ppermute x12, starting transfers between devices, ordered_reduce_then_gather(): got = lax.ppermute(y, axis, [(i, i ^ 1 << j) for i in range(n)])  7.12 us
    ppermute x4, starting transfers between devices, ordered_reduce_then_gather(): y = y + lax.ppermute(y, axis, [(i, i ^ 1 << top) for i in range(n)])  6.33 us
    ppermute x1, starting transfers between devices, doubling_gather(): got = lax.ppermute(y, axis, [(i, i ^ 1 << j) for i in range(n)])  2.94 us
  transfers between devices with their start and end apart: 29, of which 19 were waited for; matrix products, arithmetic and copies ran while one was open for 21% of the time, Pallas kernels for 0%

profile of v15, /device:TPU:0, one launch (start us, length us, event | category | flops | bytes accessed | tf_op | source)
XLA Modules:
  0.0 83.3 jit_solution(4025826638858655965)
XLA Ops:
  0.0 2.9 %collective-permute-start = (f32[1,1,2,64,512]{4,3,2,1,0:T(8,128)}, f32[1,1,2,64,512]{4,3,2,1,0:T(8,128)S(1)}, u32[]{:S(2)}, u32[]{:S(2)}) collective-permute-start(f32[1,1,2,64,512]{4,3,2,1,0:T(8,128)} %bitcast.51), channel_id=1, source_target_pairs={{0,1},{1,0},{2,3},{3,2},{4,5},{5,4},{6,7},{7,6},{8,9},{9,8},{10,11... | collective-permute-start | bytes 786440 | tf_op jit(solution)/shard_map/ppermute | solution.py:34
  2.9 5.4 %fusion.2 = f32[1024,256]{1,0:T(8,128)S(1)} fusion(f32[1024,256]{1,0:T(8,128)S(1)} %copy-done, f32[2,1024,1024]{2,1,0:T(8,128)} %param.5), kind=kOutput, calls=%fused_computation.2 | convolution fusion | flops 3221225472 | bytes 6291456 | tf_op jit(solution)/shard_map/dot_general | solution.py:8
  8.3 1.2 %collective-permute-done = f32[1,1,2,64,512]{4,3,2,1,0:T(8,128)S(1)} collective-permute-done((f32[1,1,2,64,512]{4,3,2,1,0:T(8,128)}, f32[1,1,2,64,512]{4,3,2,1,0:T(8,128)S(1)}, u32[]{:S(2)}, u32[]{:S(2)}) %collective-permute-start) | collective-permute-done | bytes 262176 | tf_op jit(solution)/shard_map/ppermute | solution.py:34
  10.5 1.2 %fusion.36 = (f32[1,1024,256]{2,1,0:T(8,128)}, f32[1024,256]{1,0:T(8,128)S(1)}, f32[1024,256]{1,0:T(8,128)S(1)}) fusion(f32[2,1024,256]{2,1,0:T(8,128)S(1)} %copy-done.1), kind=kLoop, calls=%fused_computation.107 | loop fusion | bytes 5242880 | tf_op jit(solution)/shard_map/slice | solution.py:138
  14.2 1.8 %collective-permute-start.2 = (f32[256,128]{1,0:T(8,128)S(1)}, f32[256,128]{1,0:T(8,128)S(1)}, u32[]{:S(2)}, u32[]{:S(2)}) collective-permute-start(f32[256,128]{1,0:T(8,128)S(1)} %constant_dynamic-slice_fusion.10), channel_id=1, source_target_pairs={{0,4},{2,6},{4,0},{6,2},{8,12},{10,14},{12,8},{14,10},{16,20},{18,... | collective-permute-start | bytes 393224 | tf_op jit(solution)/shard_map/ppermute | solution.py:81
  16.1 1.6 %collective-permute-start.9 = (f32[256,128]{1,0:T(8,128)S(1)}, f32[256,128]{1,0:T(8,128)S(1)}, u32[]{:S(2)}, u32[]{:S(2)}) collective-permute-start(f32[256,128]{1,0:T(8,128)S(1)} %constant_dynamic-slice_fusion.7), channel_id=1, source_target_pairs={{0,8},{2,10},{4,12},{6,14},{8,0},{10,2},{12,4},{14,6},{16,24},{18,... | collective-permute-start | bytes 393224 | tf_op jit(solution)/shard_map/ppermute | solution.py:81
  17.7 5.3 %fusion.6 = f32[1024,256]{1,0:T(8,128)S(1)} fusion(f32[1024,256]{1,0:T(8,128)S(1)} %copy-done, f32[2,1024,1024]{2,1,0:T(8,128)} %param.5), kind=kOutput, calls=%fused_computation.6 | convolution fusion | flops 3221225472 | bytes 6291456 | tf_op jit(solution)/shard_map/dot_general | solution.py:8
  24.1 4.0 %collective-permute-done.3 = f32[128,128]{1,0:T(8,128)S(1)} collective-permute-done((f32[128,128]{1,0:T(8,128)S(1)}, f32[128,128]{1,0:T(8,128)S(1)}, u32[]{:S(2)}, u32[]{:S(2)}) %collective-permute-start.3) | collective-permute-done | bytes 65568 | tf_op jit(solution)/shard_map/ppermute | solution.py:81
  28.1 3.1 %collective-permute-start.4 = (f32[128,128]{1,0:T(8,128)S(1)}, f32[128,128]{1,0:T(8,128)S(1)}, u32[]{:S(2)}, u32[]{:S(2)}) collective-permute-start(f32[128,128]{1,0:T(8,128)S(1)} %dynamic-slice_add_fusion.11), channel_id=1, source_target_pairs={{0,16},{2,18},{4,20},{6,22},{8,24},{10,26},{12,28},{14,30},{16,0},... | collective-permute-start | bytes 196616 | tf_op jit(solution)/shard_map/ppermute | solution.py:89
  31.3 3.7 %collective-permute-done.4 = f32[128,128]{1,0:T(8,128)S(1)} collective-permute-done((f32[128,128]{1,0:T(8,128)S(1)}, f32[128,128]{1,0:T(8,128)S(1)}, u32[]{:S(2)}, u32[]{:S(2)}) %collective-permute-start.4) | collective-permute-done | bytes 65568 | tf_op jit(solution)/shard_map/ppermute | solution.py:89
  37.5 1.6 %collective-permute-start.12 = (f32[128,128]{1,0:T(8,128)S(1)}, f32[128,128]{1,0:T(8,128)S(1)}, u32[]{:S(2)}, u32[]{:S(2)}) collective-permute-start(f32[128,128]{1,0:T(8,128)S(1)} %add_subtract_fusion.2), channel_id=1, source_target_pairs={{0,4},{2,6},{4,0},{6,2},{8,12},{10,14},{12,8},{14,10},{16,20},{18,... | collective-permute-start | bytes 196616 | tf_op jit(solution)/shard_map/ppermute | solution.py:93
  39.1 1.2 %collective-permute-done.5 = f32[128,128]{1,0:T(8,128)S(1)} collective-permute-done((f32[128,128]{1,0:T(8,128)S(1)}, f32[128,128]{1,0:T(8,128)S(1)}, u32[]{:S(2)}, u32[]{:S(2)}) %collective-permute-start.5) | collective-permute-done | bytes 65568 | tf_op jit(solution)/shard_map/ppermute | solution.py:93
  40.3 1.7 %collective-permute-start.6 = (f32[256,128]{1,0:T(8,128)S(1)}, f32[256,128]{1,0:T(8,128)S(1)}, u32[]{:S(2)}, u32[]{:S(2)}) collective-permute-start(f32[256,128]{1,0:T(8,128)S(1)} %pad_maximum_fusion.5), channel_id=1, source_target_pairs={{0,4},{2,6},{4,0},{6,2},{8,12},{10,14},{12,8},{14,10},{16,20},{18,... | collective-permute-start | bytes 393224 | tf_op jit(solution)/shard_map/ppermute | solution.py:93
  42.2 1.1 %collective-permute-start.13 = (f32[256,128]{1,0:T(8,128)S(1)}, f32[256,128]{1,0:T(8,128)S(1)}, u32[]{:S(2)}, u32[]{:S(2)}) collective-permute-start(f32[256,128]{1,0:T(8,128)S(1)} %pad_maximum_fusion.6), channel_id=1, source_target_pairs={{0,8},{2,10},{4,12},{6,14},{8,0},{10,2},{12,4},{14,6},{16,24},{18,... | collective-permute-start | bytes 393224 | tf_op jit(solution)/shard_map/ppermute | solution.py:93
  43.3 2.0 %collective-permute-done.6 = f32[256,128]{1,0:T(8,128)S(1)} collective-permute-done((f32[256,128]{1,0:T(8,128)S(1)}, f32[256,128]{1,0:T(8,128)S(1)}, u32[]{:S(2)}, u32[]{:S(2)}) %collective-permute-start.6) | collective-permute-done | bytes 131104 | tf_op jit(solution)/shard_map/ppermute | solution.py:93
  45.4 1.8 %collective-permute-done.13 = f32[256,128]{1,0:T(8,128)S(1)} collective-permute-done((f32[256,128]{1,0:T(8,128)S(1)}, f32[256,128]{1,0:T(8,128)S(1)}, u32[]{:S(2)}, u32[]{:S(2)}) %collective-permute-start.13) | collective-permute-done | bytes 131104 | tf_op jit(solution)/shard_map/ppermute | solution.py:93
  47.9 1.0 %collective-permute-done.14 = f32[512,128]{1,0:T(8,128)S(1)} collective-permute-done((f32[512,128]{1,0:T(8,128)S(1)}, f32[512,128]{1,0:T(8,128)S(1)}, u32[]{:S(2)}, u32[]{:S(2)}) %collective-permute-start.14) | collective-permute-done | bytes 262176 | tf_op jit(solution)/shard_map/ppermute | solution.py:93
  53.1 1.2 %collective-permute-start.16 = (f32[256,128]{1,0:T(8,128)S(1)}, f32[256,128]{1,0:T(8,128)S(1)}, u32[]{:S(2)}, u32[]{:S(2)}) collective-permute-start(f32[256,128]{1,0:T(8,128)S(1)} %constant_dynamic-slice_fusion.4), channel_id=1, source_target_pairs={{0,4},{2,6},{4,0},{6,2},{8,12},{10,14},{12,8},{14,10},{16,20},{18,... | collective-permute-start | bytes 393224 | tf_op jit(solution)/shard_map/ppermute | solution.py:81
  54.4 1.6 %collective-permute-start.23 = (f32[256,128]{1,0:T(8,128)S(1)}, f32[256,128]{1,0:T(8,128)S(1)}, u32[]{:S(2)}, u32[]{:S(2)}) collective-permute-start(f32[256,128]{1,0:T(8,128)S(1)} %constant_dynamic-slice_fusion.1), channel_id=1, source_target_pairs={{0,8},{2,10},{4,12},{6,14},{8,0},{10,2},{12,4},{14,6},{16,24},{18,... | collective-permute-start | bytes 393224 | tf_op jit(solution)/shard_map/ppermute | solution.py:81
  56.0 2.7 %collective-permute-done.16 = f32[256,128]{1,0:T(8,128)S(1)} collective-permute-done((f32[256,128]{1,0:T(8,128)S(1)}, f32[256,128]{1,0:T(8,128)S(1)}, u32[]{:S(2)}, u32[]{:S(2)}) %collective-permute-start.16) | collective-permute-done | bytes 131104 | tf_op jit(solution)/shard_map/ppermute | solution.py:81
  58.8 1.1 %collective-permute-start.17 = (f32[128,128]{1,0:T(8,128)S(1)}, f32[128,128]{1,0:T(8,128)S(1)}, u32[]{:S(2)}, u32[]{:S(2)}) collective-permute-start(f32[128,128]{1,0:T(8,128)S(1)} %constant_dynamic-slice_fusion.3), channel_id=1, source_target_pairs={{0,8},{2,10},{4,12},{6,14},{8,0},{10,2},{12,4},{14,6},{16,24},{18,... | collective-permute-start | bytes 196616 | tf_op jit(solution)/shard_map/ppermute | solution.py:81
  59.9 1.7 %collective-permute-start.24 = (f32[128,128]{1,0:T(8,128)S(1)}, f32[128,128]{1,0:T(8,128)S(1)}, u32[]{:S(2)}, u32[]{:S(2)}) collective-permute-start(f32[128,128]{1,0:T(8,128)S(1)} %constant_dynamic-slice_fusion), channel_id=1, source_target_pairs={{0,4},{2,6},{4,0},{6,2},{8,12},{10,14},{12,8},{14,10},{16,20},{18,... | collective-permute-start | bytes 196616 | tf_op jit(solution)/shard_map/ppermute | solution.py:81
  61.6 1.5 %collective-permute-done.17 = f32[128,128]{1,0:T(8,128)S(1)} collective-permute-done((f32[128,128]{1,0:T(8,128)S(1)}, f32[128,128]{1,0:T(8,128)S(1)}, u32[]{:S(2)}, u32[]{:S(2)}) %collective-permute-start.17) | collective-permute-done | bytes 65568 | tf_op jit(solution)/shard_map/ppermute | solution.py:81
  63.1 2.0 %collective-permute-start.18 = (f32[128,128]{1,0:T(8,128)S(1)}, f32[128,128]{1,0:T(8,128)S(1)}, u32[]{:S(2)}, u32[]{:S(2)}) collective-permute-start(f32[128,128]{1,0:T(8,128)S(1)} %dynamic-slice_add_fusion.9), channel_id=1, source_target_pairs={{0,16},{2,18},{4,20},{6,22},{8,24},{10,26},{12,28},{14,30},{16,0},... | collective-permute-start | bytes 196616 | tf_op jit(solution)/shard_map/ppermute | solution.py:89
  65.1 1.2 %collective-permute-start.25 = (f32[128,128]{1,0:T(8,128)S(1)}, f32[128,128]{1,0:T(8,128)S(1)}, u32[]{:S(2)}, u32[]{:S(2)}) collective-permute-start(f32[128,128]{1,0:T(8,128)S(1)} %dynamic-slice_add_fusion.8), channel_id=1, source_target_pairs={{0,16},{2,18},{4,20},{6,22},{8,24},{10,26},{12,28},{14,30},{16,0},... | collective-permute-start | bytes 196616 | tf_op jit(solution)/shard_map/ppermute | solution.py:89
  66.3 3.2 %collective-permute-done.18 = f32[128,128]{1,0:T(8,128)S(1)} collective-permute-done((f32[128,128]{1,0:T(8,128)S(1)}, f32[128,128]{1,0:T(8,128)S(1)}, u32[]{:S(2)}, u32[]{:S(2)}) %collective-permute-start.18) | collective-permute-done | bytes 65568 | tf_op jit(solution)/shard_map/ppermute | solution.py:89
  71.3 2.5 %collective-permute-done.19 = f32[128,128]{1,0:T(8,128)S(1)} collective-permute-done((f32[128,128]{1,0:T(8,128)S(1)}, f32[128,128]{1,0:T(8,128)S(1)}, u32[]{:S(2)}, u32[]{:S(2)}) %collective-permute-start.19) | collective-permute-done | bytes 65568 | tf_op jit(solution)/shard_map/ppermute | solution.py:93
  74.3 1.1 %collective-permute-done.26 = f32[128,128]{1,0:T(8,128)S(1)} collective-permute-done((f32[128,128]{1,0:T(8,128)S(1)}, f32[128,128]{1,0:T(8,128)S(1)}, u32[]{:S(2)}, u32[]{:S(2)}) %collective-permute-start.26) | collective-permute-done | bytes 65568 | tf_op jit(solution)/shard_map/ppermute | solution.py:93
  75.4 1.1 %collective-permute-start.27 = (f32[256,128]{1,0:T(8,128)S(1)}, f32[256,128]{1,0:T(8,128)S(1)}, u32[]{:S(2)}, u32[]{:S(2)}) collective-permute-start(f32[256,128]{1,0:T(8,128)S(1)} %pad_maximum_fusion.8), channel_id=1, source_target_pairs={{0,8},{2,10},{4,12},{6,14},{8,0},{10,2},{12,4},{14,6},{16,24},{18,... | collective-permute-start | bytes 393224 | tf_op jit(solution)/shard_map/ppermute | solution.py:93
  76.5 2.3 %collective-permute-done.20 = f32[256,128]{1,0:T(8,128)S(1)} collective-permute-done((f32[256,128]{1,0:T(8,128)S(1)}, f32[256,128]{1,0:T(8,128)S(1)}, u32[]{:S(2)}, u32[]{:S(2)}) %collective-permute-start.20) | collective-permute-done | bytes 131104 | tf_op jit(solution)/shard_map/ppermute | solution.py:93
  79.0 1.5 %collective-permute-done.27 = f32[256,128]{1,0:T(8,128)S(1)} collective-permute-done((f32[256,128]{1,0:T(8,128)S(1)}, f32[256,128]{1,0:T(8,128)S(1)}, u32[]{:S(2)}, u32[]{:S(2)}) %collective-permute-start.27) | collective-permute-done | bytes 131104 | tf_op jit(solution)/shard_map/ppermute | solution.py:93
  81.1 1.0 %collective-permute-done.28 = f32[512,128]{1,0:T(8,128)S(1)} collective-permute-done((f32[512,128]{1,0:T(8,128)S(1)}, f32[512,128]{1,0:T(8,128)S(1)}, u32[]{:S(2)}, u32[]{:S(2)}) %collective-permute-start.28) | collective-permute-done | bytes 262176 | tf_op jit(solution)/shard_map/ppermute | solution.py:93
  (101 shorter events, 16.5 us)
Async XLA Ops:
  0.0 9.5 %copy-start.4 = (f32[2,64,512]{2,1,0:T(8,128)S(1)}, f32[2,64,512]{2,1,0:T(8,128)}, u32[]{:S(2)}) copy-start(f32[2,64,512]{2,1,0:T(8,128)} %param.8) | copy-start | bytes 786436
  0.0 9.5 %collective-permute-start = (f32[1,1,2,64,512]{4,3,2,1,0:T(8,128)}, f32[1,1,2,64,512]{4,3,2,1,0:T(8,128)S(1)}, u32[]{:S(2)}, u32[]{:S(2)}) collective-permute-start(f32[1,1,2,64,512]{4,3,2,1,0:T(8,128)} %bitcast.51), channel_id=1, source_target_pairs={{0,1},{1,0},{2,3},{3,2},{4,5},{5,4},{6,7},{7,6},{8,9},{9,8},{10,11... | collective-permute-start | bytes 786440 | tf_op jit(solution)/shard_map/ppermute | solution.py:34
  10.4 2.8 %collective-permute-start.1 = (f32[512,128]{1,0:T(8,128)S(1)}, f32[512,128]{1,0:T(8,128)}, u32[]{:S(2)}, u32[]{:S(2)}) collective-permute-start(f32[512,128]{1,0:T(8,128)S(1)} %constant_dynamic-slice_fusion.11), channel_id=1, source_target_pairs={{0,2},{2,0},{4,6},{6,4},{8,10},{10,8},{12,14},{14,12},{16,18},{18,... | collective-permute-start | bytes 786440 | tf_op jit(solution)/shard_map/ppermute | solution.py:81
  12.7 3.4 %collective-permute-start.8 = (f32[512,128]{1,0:T(8,128)S(1)}, f32[512,128]{1,0:T(8,128)S(1)}, u32[]{:S(2)}, u32[]{:S(2)}) collective-permute-start(f32[512,128]{1,0:T(8,128)S(1)} %constant_dynamic-slice_fusion.8), channel_id=1, source_target_pairs={{0,2},{2,0},{4,6},{6,4},{8,10},{10,8},{12,14},{14,12},{16,18},{18,... | collective-permute-start | bytes 786440 | tf_op jit(solution)/shard_map/ppermute | solution.py:81
  14.2 9.8 %copy-start.2 = (f32[2,2,64,512]{3,2,1,0:T(8,128)S(1)}, f32[2,2,64,512]{3,2,1,0:T(8,128)}, u32[]{:S(2)}) copy-start(f32[2,2,64,512]{3,2,1,0:T(8,128)} %maximum_bitcast_fusion) | copy-start | bytes 1572868
  14.2 9.5 %collective-permute-start.2 = (f32[256,128]{1,0:T(8,128)S(1)}, f32[256,128]{1,0:T(8,128)S(1)}, u32[]{:S(2)}, u32[]{:S(2)}) collective-permute-start(f32[256,128]{1,0:T(8,128)S(1)} %constant_dynamic-slice_fusion.10), channel_id=1, source_target_pairs={{0,4},{2,6},{4,0},{6,2},{8,12},{10,14},{12,8},{14,10},{16,20},{18,... | collective-permute-start | bytes 393224 | tf_op jit(solution)/shard_map/ppermute | solution.py:81
  16.1 7.0 %collective-permute-start.9 = (f32[256,128]{1,0:T(8,128)S(1)}, f32[256,128]{1,0:T(8,128)S(1)}, u32[]{:S(2)}, u32[]{:S(2)}) collective-permute-start(f32[256,128]{1,0:T(8,128)S(1)} %constant_dynamic-slice_fusion.7), channel_id=1, source_target_pairs={{0,8},{2,10},{4,12},{6,14},{8,0},{10,2},{12,4},{14,6},{16,24},{18,... | collective-permute-start | bytes 393224 | tf_op jit(solution)/shard_map/ppermute | solution.py:81
  23.1 8.1 %collective-permute-start.10 = (f32[128,128]{1,0:T(8,128)S(1)}, f32[128,128]{1,0:T(8,128)S(1)}, u32[]{:S(2)}, u32[]{:S(2)}) collective-permute-start(f32[128,128]{1,0:T(8,128)S(1)} %constant_dynamic-slice_fusion.6), channel_id=1, source_target_pairs={{0,4},{2,6},{4,0},{6,2},{8,12},{10,14},{12,8},{14,10},{16,20},{18,... | collective-permute-start | bytes 196616 | tf_op jit(solution)/shard_map/ppermute | solution.py:81
  23.8 4.3 %collective-permute-start.3 = (f32[128,128]{1,0:T(8,128)S(1)}, f32[128,128]{1,0:T(8,128)S(1)}, u32[]{:S(2)}, u32[]{:S(2)}) collective-permute-start(f32[128,128]{1,0:T(8,128)S(1)} %constant_dynamic-slice_fusion.9), channel_id=1, source_target_pairs={{0,8},{2,10},{4,12},{6,14},{8,0},{10,2},{12,4},{14,6},{16,24},{18,... | collective-permute-start | bytes 196616 | tf_op jit(solution)/shard_map/ppermute | solution.py:81
  24.1 25.3 %copy-start.3 = (f32[1024,64]{0,1:T(8,128)S(1)}, f32[1024,64]{0,1:T(8,128)}, u32[]{:S(2)}) copy-start(f32[1024,64]{0,1:T(8,128)} %param.9) | copy-start | bytes 786436
  28.1 6.9 %collective-permute-start.4 = (f32[128,128]{1,0:T(8,128)S(1)}, f32[128,128]{1,0:T(8,128)S(1)}, u32[]{:S(2)}, u32[]{:S(2)}) collective-permute-start(f32[128,128]{1,0:T(8,128)S(1)} %dynamic-slice_add_fusion.11), channel_id=1, source_target_pairs={{0,16},{2,18},{4,20},{6,22},{8,24},{10,26},{12,28},{14,30},{16,0},... | collective-permute-start | bytes 196616 | tf_op jit(solution)/shard_map/ppermute | solution.py:89
  31.2 5.4 %collective-permute-start.11 = (f32[128,128]{1,0:T(8,128)S(1)}, f32[128,128]{1,0:T(8,128)S(1)}, u32[]{:S(2)}, u32[]{:S(2)}) collective-permute-start(f32[128,128]{1,0:T(8,128)S(1)} %dynamic-slice_add_fusion.10), channel_id=1, source_target_pairs={{0,16},{2,18},{4,20},{6,22},{8,24},{10,26},{12,28},{14,30},{16,0},... | collective-permute-start | bytes 196616 | tf_op jit(solution)/shard_map/ppermute | solution.py:89
  35.9 4.3 %collective-permute-start.5 = (f32[128,128]{1,0:T(8,128)S(1)}, f32[128,128]{1,0:T(8,128)S(1)}, u32[]{:S(2)}, u32[]{:S(2)}) collective-permute-start(f32[128,128]{1,0:T(8,128)S(1)} %bitcast_subtract_fusion), channel_id=1, source_target_pairs={{0,8},{2,10},{4,12},{6,14},{8,0},{10,2},{12,4},{14,6},{16,24},{18,... | collective-permute-start | bytes 196616 | tf_op jit(solution)/shard_map/ppermute | solution.py:93
  37.5 4.7 %collective-permute-start.12 = (f32[128,128]{1,0:T(8,128)S(1)}, f32[128,128]{1,0:T(8,128)S(1)}, u32[]{:S(2)}, u32[]{:S(2)}) collective-permute-start(f32[128,128]{1,0:T(8,128)S(1)} %add_subtract_fusion.2), channel_id=1, source_target_pairs={{0,4},{2,6},{4,0},{6,2},{8,12},{10,14},{12,8},{14,10},{16,20},{18,... | collective-permute-start | bytes 196616 | tf_op jit(solution)/shard_map/ppermute | solution.py:93
  40.3 5.0 %collective-permute-start.6 = (f32[256,128]{1,0:T(8,128)S(1)}, f32[256,128]{1,0:T(8,128)S(1)}, u32[]{:S(2)}, u32[]{:S(2)}) collective-permute-start(f32[256,128]{1,0:T(8,128)S(1)} %pad_maximum_fusion.5), channel_id=1, source_target_pairs={{0,4},{2,6},{4,0},{6,2},{8,12},{10,14},{12,8},{14,10},{16,20},{18,... | collective-permute-start | bytes 393224 | tf_op jit(solution)/shard_map/ppermute | solution.py:93
  42.2 5.0 %collective-permute-start.13 = (f32[256,128]{1,0:T(8,128)S(1)}, f32[256,128]{1,0:T(8,128)S(1)}, u32[]{:S(2)}, u32[]{:S(2)}) collective-permute-start(f32[256,128]{1,0:T(8,128)S(1)} %pad_maximum_fusion.6), channel_id=1, source_target_pairs={{0,8},{2,10},{4,12},{6,14},{8,0},{10,2},{12,4},{14,6},{16,24},{18,... | collective-permute-start | bytes 393224 | tf_op jit(solution)/shard_map/ppermute | solution.py:93
  45.4 2.0 %collective-permute-start.7 = (f32[512,128]{1,0:T(8,128)S(1)}, f32[512,128]{1,0:T(8,128)S(1)}, u32[]{:S(2)}, u32[]{:S(2)}) collective-permute-start(f32[512,128]{1,0:T(8,128)S(1)} %pad_maximum_fusion.1), channel_id=1, source_target_pairs={{0,2},{2,0},{4,6},{6,4},{8,10},{10,8},{12,14},{14,12},{16,18},{18,... | collective-permute-start | bytes 786440 | tf_op jit(solution)/shard_map/ppermute | solution.py:93
  47.3 1.6 %collective-permute-start.14 = (f32[512,128]{1,0:T(8,128)S(1)}, f32[512,128]{1,0:T(8,128)S(1)}, u32[]{:S(2)}, u32[]{:S(2)}) collective-permute-start(f32[512,128]{1,0:T(8,128)S(1)} %pad_maximum_fusion.2), channel_id=1, source_target_pairs={{0,2},{2,0},{4,6},{6,4},{8,10},{10,8},{12,14},{14,12},{16,18},{18,... | collective-permute-start | bytes 786440 | tf_op jit(solution)/shard_map/ppermute | solution.py:93
  51.4 1.6 %collective-permute-start.15 = (f32[512,128]{1,0:T(8,128)S(1)}, f32[512,128]{1,0:T(8,128)S(1)}, u32[]{:S(2)}, u32[]{:S(2)}) collective-permute-start(f32[512,128]{1,0:T(8,128)S(1)} %constant_dynamic-slice_fusion.5), channel_id=1, source_target_pairs={{0,2},{2,0},{4,6},{6,4},{8,10},{10,8},{12,14},{14,12},{16,18},{18,... | collective-permute-start | bytes 786440 | tf_op jit(solution)/shard_map/ppermute | solution.py:81
  51.8 2.6 %collective-permute-start.22 = (f32[512,128]{1,0:T(8,128)S(1)}, f32[512,128]{1,0:T(8,128)S(1)}, u32[]{:S(2)}, u32[]{:S(2)}) collective-permute-start(f32[512,128]{1,0:T(8,128)S(1)} %constant_dynamic-slice_fusion.2), channel_id=1, source_target_pairs={{0,2},{2,0},{4,6},{6,4},{8,10},{10,8},{12,14},{14,12},{16,18},{18,... | collective-permute-start | bytes 786440 | tf_op jit(solution)/shard_map/ppermute | solution.py:81
  53.1 5.6 %collective-permute-start.16 = (f32[256,128]{1,0:T(8,128)S(1)}, f32[256,128]{1,0:T(8,128)S(1)}, u32[]{:S(2)}, u32[]{:S(2)}) collective-permute-start(f32[256,128]{1,0:T(8,128)S(1)} %constant_dynamic-slice_fusion.4), channel_id=1, source_target_pairs={{0,4},{2,6},{4,0},{6,2},{8,12},{10,14},{12,8},{14,10},{16,20},{18,... | collective-permute-start | bytes 393224 | tf_op jit(solution)/shard_map/ppermute | solution.py:81
  54.4 5.5 %collective-permute-start.23 = (f32[256,128]{1,0:T(8,128)S(1)}, f32[256,128]{1,0:T(8,128)S(1)}, u32[]{:S(2)}, u32[]{:S(2)}) collective-permute-start(f32[256,128]{1,0:T(8,128)S(1)} %constant_dynamic-slice_fusion.1), channel_id=1, source_target_pairs={{0,8},{2,10},{4,12},{6,14},{8,0},{10,2},{12,4},{14,6},{16,24},{18,... | collective-permute-start | bytes 393224 | tf_op jit(solution)/shard_map/ppermute | solution.py:81
  58.8 4.3 %collective-permute-start.17 = (f32[128,128]{1,0:T(8,128)S(1)}, f32[128,128]{1,0:T(8,128)S(1)}, u32[]{:S(2)}, u32[]{:S(2)}) collective-permute-start(f32[128,128]{1,0:T(8,128)S(1)} %constant_dynamic-slice_fusion.3), channel_id=1, source_target_pairs={{0,8},{2,10},{4,12},{6,14},{8,0},{10,2},{12,4},{14,6},{16,24},{18,... | collective-permute-start | bytes 196616 | tf_op jit(solution)/shard_map/ppermute | solution.py:81
  59.9 5.1 %collective-permute-start.24 = (f32[128,128]{1,0:T(8,128)S(1)}, f32[128,128]{1,0:T(8,128)S(1)}, u32[]{:S(2)}, u32[]{:S(2)}) collective-permute-start(f32[128,128]{1,0:T(8,128)S(1)} %constant_dynamic-slice_fusion), channel_id=1, source_target_pairs={{0,4},{2,6},{4,0},{6,2},{8,12},{10,14},{12,8},{14,10},{16,20},{18,... | collective-permute-start | bytes 196616 | tf_op jit(solution)/shard_map/ppermute | solution.py:81
  63.1 6.3 %collective-permute-start.18 = (f32[128,128]{1,0:T(8,128)S(1)}, f32[128,128]{1,0:T(8,128)S(1)}, u32[]{:S(2)}, u32[]{:S(2)}) collective-permute-start(f32[128,128]{1,0:T(8,128)S(1)} %dynamic-slice_add_fusion.9), channel_id=1, source_target_pairs={{0,16},{2,18},{4,20},{6,22},{8,24},{10,26},{12,28},{14,30},{16,0},... | collective-permute-start | bytes 196616 | tf_op jit(solution)/shard_map/ppermute | solution.py:89
  65.1 5.4 %collective-permute-start.25 = (f32[128,128]{1,0:T(8,128)S(1)}, f32[128,128]{1,0:T(8,128)S(1)}, u32[]{:S(2)}, u32[]{:S(2)}) collective-permute-start(f32[128,128]{1,0:T(8,128)S(1)} %dynamic-slice_add_fusion.8), channel_id=1, source_target_pairs={{0,16},{2,18},{4,20},{6,22},{8,24},{10,26},{12,28},{14,30},{16,0},... | collective-permute-start | bytes 196616 | tf_op jit(solution)/shard_map/ppermute | solution.py:89
  69.5 4.3 %collective-permute-start.19 = (f32[128,128]{1,0:T(8,128)S(1)}, f32[128,128]{1,0:T(8,128)S(1)}, u32[]{:S(2)}, u32[]{:S(2)}) collective-permute-start(f32[128,128]{1,0:T(8,128)S(1)} %add_subtract_fusion.1), channel_id=1, source_target_pairs={{0,8},{2,10},{4,12},{6,14},{8,0},{10,2},{12,4},{14,6},{16,24},{18,... | collective-permute-start | bytes 196616 | tf_op jit(solution)/shard_map/ppermute | solution.py:93
  70.5 4.9 %collective-permute-start.26 = (f32[128,128]{1,0:T(8,128)S(1)}, f32[128,128]{1,0:T(8,128)S(1)}, u32[]{:S(2)}, u32[]{:S(2)}) collective-permute-start(f32[128,128]{1,0:T(8,128)S(1)} %add_subtract_fusion), channel_id=1, source_target_pairs={{0,4},{2,6},{4,0},{6,2},{8,12},{10,14},{12,8},{14,10},{16,20},{18,... | collective-permute-start | bytes 196616 | tf_op jit(solution)/shard_map/ppermute | solution.py:93
  73.8 5.0 %collective-permute-start.20 = (f32[256,128]{1,0:T(8,128)S(1)}, f32[256,128]{1,0:T(8,128)S(1)}, u32[]{:S(2)}, u32[]{:S(2)}) collective-permute-start(f32[256,128]{1,0:T(8,128)S(1)} %pad_maximum_fusion.7), channel_id=1, source_target_pairs={{0,4},{2,6},{4,0},{6,2},{8,12},{10,14},{12,8},{14,10},{16,20},{18,... | collective-permute-start | bytes 393224 | tf_op jit(solution)/shard_map/ppermute | solution.py:93
  75.4 5.0 %collective-permute-start.27 = (f32[256,128]{1,0:T(8,128)S(1)}, f32[256,128]{1,0:T(8,128)S(1)}, u32[]{:S(2)}, u32[]{:S(2)}) collective-permute-start(f32[256,128]{1,0:T(8,128)S(1)} %pad_maximum_fusion.8), channel_id=1, source_target_pairs={{0,8},{2,10},{4,12},{6,14},{8,0},{10,2},{12,4},{14,6},{16,24},{18,... | collective-permute-start | bytes 393224 | tf_op jit(solution)/shard_map/ppermute | solution.py:93
  78.9 1.7 %collective-permute-start.21 = (f32[512,128]{1,0:T(8,128)S(1)}, f32[512,128]{1,0:T(8,128)S(1)}, u32[]{:S(2)}, u32[]{:S(2)}) collective-permute-start(f32[512,128]{1,0:T(8,128)S(1)} %pad_maximum_fusion.3), channel_id=1, source_target_pairs={{0,2},{2,0},{4,6},{6,4},{8,10},{10,8},{12,14},{14,12},{16,18},{18,... | collective-permute-start | bytes 786440 | tf_op jit(solution)/shard_map/ppermute | solution.py:93
  80.5 1.6 %collective-permute-start.28 = (f32[512,128]{1,0:T(8,128)S(1)}, f32[512,128]{1,0:T(8,128)S(1)}, u32[]{:S(2)}, u32[]{:S(2)}) collective-permute-start(f32[512,128]{1,0:T(8,128)S(1)} %pad_maximum_fusion.4), channel_id=1, source_target_pairs={{0,2},{2,0},{4,6},{6,4},{8,10},{10,8},{12,14},{14,12},{16,18},{18,... | collective-permute-start | bytes 786440 | tf_op jit(solution)/shard_map/ppermute | solution.py:93
  (2 other events, 10.5 us)

commit v16 on v12

--- a/solution.py
+++ b/solution.py
@@ -109,10 +109,6 @@
         return lax.all_gather(x, "blk", axis=0, tiled=True)
 
     def shards(factor_panel, solved_before, right_side, diag_inverse, coupling):
-        if rhs_power_of_two:
-            inverse_pieces = doubling_gather(diag_inverse[None], "rhs", m)
-        else:
-            inverse_pieces = lax.all_gather(diag_inverse, "rhs", axis=0)
         own_count = diag_inverse.shape[1]
         my_index = lax.axis_index("blk")
 
@@ -120,7 +116,11 @@
             return lax.dynamic_slice_in_dim(matrix, my_index * own_count, own_count, 0)
 
         first_sum = product(factor_panel[0], solved_before)
-        first_sum, inverse_pieces = lax.optimization_barrier((first_sum, inverse_pieces))
+        first_sum, held_inverse = lax.optimization_barrier((first_sum, diag_inverse))
+        if rhs_power_of_two:
+            inverse_pieces = doubling_gather(held_inverse[None], "rhs", m)
+        else:
+            inverse_pieces = lax.all_gather(held_inverse, "rhs", axis=0)
         chained = power_of_two and n >= 4
         if not chained:
             panel_sum = product(factor_panel[1], solved_before)

time: 76.8 us -> 82.8 us (1.078)
  starting transfers between devices: 26.3 us -> 21.7 us
  waiting for transfers between devices: 33.6 us -> 37.4 us
  other arithmetic: 1.47 us -> 4.56 us
  local copies, waits for them, and re-layouts: 2.18 us -> 4.16 us
  matrix products: 12.5 us -> 14.3 us
    ppermute x12, starting transfers between devices: 6.44 us -> 3.65 us  [ordered_reduce_then_gather(): got = lax.ppermute(y, axis, [(i, i ^ 1 << j) for i in range(n)])]
    ppermute x12, waiting for transfers between devices: 16.4 us -> 18.7 us  [ordered_reduce_then_gather(): got = lax.ppermute(y, axis, [(i, i ^ 1 << j) for i in range(n)])]
    add x12, other arithmetic: 0.24 us -> 2.3 us  [ordered_reduce_then_gather(): y = keep + got]
    dot_general x8, matrix products: 12.5 us -> 14.3 us  [product(): jnp.dot(left, right, precision=lax.Precision.HIGHEST, preferred_element_t...]
    ppermute x12, starting transfers between devices: 10.3 us -> 8.66 us  [ordered_reduce_then_gather(): got = lax.ppermute(send, axis, [(i, i ^ 1 << j) for i in range(n)])]
    unnamed x8, local copies, waits for them, and re-layouts: 0.02 us -> 1.24 us
    another operation x1, other arithmetic: 0.05 us -> 1.07 us  [doubling_gather(): y = jnp.stack([low, high], 1).reshape((-1,) + x.shape)]
  transfers between devices with their start and end apart: 29 -> 29, of which waited for: 21 -> 19; matrix products, arithmetic and copies ran while one was open for 16% -> 15% of each run, Pallas kernels for 0% -> 0%
where the time goes in v16:
time: 82.8 us; the launch traced here: 82.6 us
  waiting for transfers between devices  37.4 us (45%)
  starting transfers between devices  21.7 us (26%)
  matrix products  14.3 us (17%)
  other arithmetic  4.56 us (6%)
  local copies, waits for them, and re-layouts  4.16 us (5%)
    ppermute x12, waiting for transfers between devices, ordered_reduce_then_gather(): got = lax.ppermute(y, axis, [(i, i ^ 1 << j) for i in range(n)])  18.7 us
    dot_general x8, matrix products, product(): jnp.dot(left, right, precision=lax.Precision.HIGHEST, preferred_element_t...  14.3 us
    ppermute x12, waiting for transfers between devices, ordered_reduce_then_gather(): got = lax.ppermute(send, axis, [(i, i ^ 1 << j) for i in range(n)])  10.9 us
    ppermute x12, starting transfers between devices, ordered_reduce_then_gather(): got = lax.ppermute(send, axis, [(i, i ^ 1 << j) for i in range(n)])  8.66 us
    ppermute x4, waiting for transfers between devices, ordered_reduce_then_gather(): y = y + lax.ppermute(y, axis, [(i, i ^ 1 << top) for i in range(n)])  7.73 us
    ppermute x4, starting transfers between devices, ordered_reduce_then_gather(): y = y + lax.ppermute(y, axis, [(i, i ^ 1 << top) for i in range(n)])  6.4 us
    ppermute x12, starting transfers between devices, ordered_reduce_then_gather(): got = lax.ppermute(y, axis, [(i, i ^ 1 << j) for i in range(n)])  3.65 us
    ppermute x1, starting transfers between devices, doubling_gather(): got = lax.ppermute(y, axis, [(i, i ^ 1 << j) for i in range(n)])  2.94 us
  transfers between devices with their start and end apart: 29, of which 19 were waited for; matrix products, arithmetic and copies ran while one was open for 15% of the time, Pallas kernels for 0%

profile of v16, /device:TPU:0, one launch (start us, length us, event | category | flops | bytes accessed | tf_op | source)
XLA Modules:
  0.0 82.6 jit_solution(3001319817858787388)
XLA Ops:
  0.0 1.2 %copy-done = f32[1024,256]{1,0:T(8,128)S(1)} copy-done((f32[1024,256]{1,0:T(8,128)S(1)}, f32[1024,256]{1,0:T(8,128)}, u32[]{:S(2)}) %copy-start) | copy-done | bytes 1048600
  1.2 5.2 %fusion.2 = f32[1024,256]{1,0:T(8,128)S(1)} fusion(f32[1024,256]{1,0:T(8,128)S(1)} %copy-done, f32[2,1024,1024]{2,1,0:T(8,128)} %param.5), kind=kOutput, calls=%fused_computation.2 | convolution fusion | flops 3221225472 | bytes 6291456 | tf_op jit(solution)/shard_map/dot_general | solution.py:8
  8.0 2.9 %collective-permute-start.2 = (f32[1,1,2,64,512]{4,3,2,1,0:T(8,128)}, f32[1,1,2,64,512]{4,3,2,1,0:T(8,128)}, u32[]{:S(2)}, u32[]{:S(2)}) collective-permute-start(f32[1,1,2,64,512]{4,3,2,1,0:T(8,128)} %bitcast.3), channel_id=1, source_target_pairs={{0,1},{1,0},{2,3},{3,2},{4,5},{5,4},{6,7},{7,6},{8,9},{9,8},{10,11... | collective-permute-start | bytes 786440 | tf_op jit(solution)/shard_map/ppermute | solution.py:34
  10.9 1.7 %slice_bitcast_fusion = (f32[1024,256]{1,0:T(8,128)S(1)}, f32[1024,256]{1,0:T(8,128)S(1)}) fusion(f32[2,1024,256]{2,1,0:T(8,128)} %param.7), kind=kLoop, calls=%fused_computation.9 | loop fusion | bytes 4194304 | tf_op jit(solution)/shard_map/squeeze | solution.py:147
  12.7 1.1 %dynamic-slice_add_fusion.2 = f32[512,128]{1,0:T(8,128)S(1)} fusion(f32[512,128]{1,0:T(8,128)} %collective-permute-done.8, f32[1024,128]{1,0:T(8,128)} %copy-done.2, s32[]{:T(128)S(6)} %select_n.190), kind=kLoop, calls=%fused_computation.42 | loop fusion | flops 65536 | bytes 786436 | tf_op jit(solution)/shard_map/add | solution.py:81
  13.8 1.6 %collective-permute-start.9 = (f32[256,128]{1,0:T(8,128)S(1)}, f32[256,128]{1,0:T(8,128)S(1)}, u32[]{:S(2)}, u32[]{:S(2)}) collective-permute-start(f32[256,128]{1,0:T(8,128)S(1)} %constant_dynamic-slice_fusion.7), channel_id=1, source_target_pairs={{0,8},{2,10},{4,12},{6,14},{8,0},{10,2},{12,4},{14,6},{16,24},{18,... | collective-permute-start | bytes 393224 | tf_op jit(solution)/shard_map/ppermute | solution.py:78
  15.5 1.1 %dynamic-slice_add_fusion.3 = f32[512,128]{1,0:T(8,128)S(1)} fusion(f32[512,128]{1,0:T(8,128)} %collective-permute-done, f32[1024,128]{1,0:T(8,128)} %copy-done.1, s32[]{:T(128)S(6)} %select_n.190), kind=kLoop, calls=%fused_computation.47 | loop fusion | flops 65536 | bytes 786436 | tf_op jit(solution)/shard_map/add | solution.py:81
  16.5 1.6 %collective-permute-start.1 = (f32[256,128]{1,0:T(8,128)S(1)}, f32[256,128]{1,0:T(8,128)S(1)}, u32[]{:S(2)}, u32[]{:S(2)}) collective-permute-start(f32[256,128]{1,0:T(8,128)S(1)} %constant_dynamic-slice_fusion.10), channel_id=1, source_target_pairs={{0,4},{2,6},{4,0},{6,2},{8,12},{10,14},{12,8},{14,10},{16,20},{18,... | collective-permute-start | bytes 393224 | tf_op jit(solution)/shard_map/ppermute | solution.py:78
  18.1 5.3 %fusion.6 = f32[1024,256]{1,0:T(8,128)S(1)} fusion(f32[1024,256]{1,0:T(8,128)S(1)} %copy-done, f32[2,1024,1024]{2,1,0:T(8,128)} %param.5), kind=kOutput, calls=%fused_computation.6 | convolution fusion | flops 3221225472 | bytes 6291456 | tf_op jit(solution)/shard_map/dot_general | solution.py:8
  23.5 1.1 %select_bitcast_fusion.1 = (f32[1,1,1,2,64,512]{5,4,3,2,1,0:T(8,128)S(1)}, f32[1,1,1,2,64,512]{5,4,3,2,1,0:T(8,128)S(1)}) fusion(f32[1,1,2,64,512]{4,3,2,1,0:T(8,128)} %collective-permute-done.2, pred[]{:T(512)S(6)} %eq.8, f32[2,64,512]{2,1,0:T(8,128)} %param.8), kind=kLoop, calls=%fused_computation.46 | loop fusion | flops 131072 | bytes 1048577 | tf_op jit(solution)/shard_map/stack | solution.py:37
  25.8 3.1 %collective-permute-done.10 = f32[128,128]{1,0:T(8,128)S(1)} collective-permute-done((f32[128,128]{1,0:T(8,128)S(1)}, f32[128,128]{1,0:T(8,128)S(1)}, u32[]{:S(2)}, u32[]{:S(2)}) %collective-permute-start.10) | collective-permute-done | bytes 65568 | tf_op jit(solution)/shard_map/ppermute | solution.py:78
  29.0 2.7 %collective-permute-start.11 = (f32[128,128]{1,0:T(8,128)S(1)}, f32[128,128]{1,0:T(8,128)S(1)}, u32[]{:S(2)}, u32[]{:S(2)}) collective-permute-start(f32[128,128]{1,0:T(8,128)S(1)} %dynamic-slice_add_fusion.10), channel_id=1, source_target_pairs={{0,16},{2,18},{4,20},{6,22},{8,24},{10,26},{12,28},{14,30},{16,0},... | collective-permute-start | bytes 196616 | tf_op jit(solution)/shard_map/ppermute | solution.py:86
  31.7 0.9 %collective-permute-start.4 = (f32[128,128]{1,0:T(8,128)S(1)}, f32[128,128]{1,0:T(8,128)S(1)}, u32[]{:S(2)}, u32[]{:S(2)}) collective-permute-start(f32[128,128]{1,0:T(8,128)S(1)} %dynamic-slice_add_fusion.11), channel_id=1, source_target_pairs={{0,16},{2,18},{4,20},{6,22},{8,24},{10,26},{12,28},{14,30},{16,0},... | collective-permute-start | bytes 196616 | tf_op jit(solution)/shard_map/ppermute | solution.py:86
  32.6 3.1 %collective-permute-done.11 = f32[128,128]{1,0:T(8,128)S(1)} collective-permute-done((f32[128,128]{1,0:T(8,128)S(1)}, f32[128,128]{1,0:T(8,128)S(1)}, u32[]{:S(2)}, u32[]{:S(2)}) %collective-permute-start.11) | collective-permute-done | bytes 65568 | tf_op jit(solution)/shard_map/ppermute | solution.py:86
  36.3 1.2 %collective-permute-done.4 = f32[128,128]{1,0:T(8,128)S(1)} collective-permute-done((f32[128,128]{1,0:T(8,128)S(1)}, f32[128,128]{1,0:T(8,128)S(1)}, u32[]{:S(2)}, u32[]{:S(2)}) %collective-permute-start.4) | collective-permute-done | bytes 65568 | tf_op jit(solution)/shard_map/ppermute | solution.py:86
  37.6 2.5 %collective-permute-done.12 = f32[128,128]{1,0:T(8,128)S(1)} collective-permute-done((f32[128,128]{1,0:T(8,128)S(1)}, f32[128,128]{1,0:T(8,128)S(1)}, u32[]{:S(2)}, u32[]{:S(2)}) %collective-permute-start.12) | collective-permute-done | bytes 65568 | tf_op jit(solution)/shard_map/ppermute | solution.py:90
  40.2 1.6 %collective-permute-done.5 = f32[128,128]{1,0:T(8,128)S(1)} collective-permute-done((f32[128,128]{1,0:T(8,128)S(1)}, f32[128,128]{1,0:T(8,128)S(1)}, u32[]{:S(2)}, u32[]{:S(2)}) %collective-permute-start.5) | collective-permute-done | bytes 65568 | tf_op jit(solution)/shard_map/ppermute | solution.py:90
  42.5 2.7 %collective-permute-done.13 = f32[256,128]{1,0:T(8,128)S(1)} collective-permute-done((f32[256,128]{1,0:T(8,128)S(1)}, f32[256,128]{1,0:T(8,128)S(1)}, u32[]{:S(2)}, u32[]{:S(2)}) %collective-permute-start.13) | collective-permute-done | bytes 131104 | tf_op jit(solution)/shard_map/ppermute | solution.py:90
  45.3 1.6 %collective-permute-done.6 = f32[256,128]{1,0:T(8,128)S(1)} collective-permute-done((f32[256,128]{1,0:T(8,128)S(1)}, f32[256,128]{1,0:T(8,128)S(1)}, u32[]{:S(2)}, u32[]{:S(2)}) %collective-permute-start.6) | collective-permute-done | bytes 131104 | tf_op jit(solution)/shard_map/ppermute | solution.py:90
  47.5 1.0 %collective-permute-done.7 = f32[512,128]{1,0:T(8,128)S(1)} collective-permute-done((f32[512,128]{1,0:T(8,128)S(1)}, f32[512,128]{1,0:T(8,128)S(1)}, u32[]{:S(2)}, u32[]{:S(2)}) %collective-permute-start.7) | collective-permute-done | bytes 262176 | tf_op jit(solution)/shard_map/ppermute | solution.py:90
  49.1 1.0 %convolution_bitcast_fusion = f32[1024,128]{1,0:T(8,128)S(1)} fusion(f32[64,128]{1,0:T(8,128)S(1)} %fusion.13, f32[1024,64]{0,1:T(8,128)S(1)} %copy-done.3), kind=kOutput, calls=%fused_computation.7 | convolution fusion | flops 100663296 | bytes 819200 | tf_op jit(solution)/shard_map/dot_general | solution.py:8
  50.1 1.0 %slice_add_fusion.1 = (f32[1024,128]{1,0:T(8,128)S(1)}, f32[1024,128]{1,0:T(8,128)S(1)}) fusion(f32[1024,256]{1,0:T(8,128)S(1)} %fusion.6, f32[1024,128]{1,0:T(8,128)S(1)} %convolution_bitcast_fusion, f32[64,128]{1,0:T(8,128)S(1)} %fusion.9, f32[1024,64]{0,1:T(8,128)S(1)} %copy-done.3), kind=kOutput, calls=%fused_computation.31 | convolution fusion | flops 100925440 | bytes 2916352 | tf_op jit(solution)/shard_map/dot_general | solution.py:8
  54.1 4.3 %collective-permute-done.23 = f32[256,128]{1,0:T(8,128)S(1)} collective-permute-done((f32[256,128]{1,0:T(8,128)S(1)}, f32[256,128]{1,0:T(8,128)S(1)}, u32[]{:S(2)}, u32[]{:S(2)}) %collective-permute-start.23) | collective-permute-done | bytes 131104 | tf_op jit(solution)/shard_map/ppermute | solution.py:78
  59.1 1.3 %collective-permute-start.17 = (f32[128,128]{1,0:T(8,128)S(1)}, f32[128,128]{1,0:T(8,128)S(1)}, u32[]{:S(2)}, u32[]{:S(2)}) collective-permute-start(f32[128,128]{1,0:T(8,128)S(1)} %constant_dynamic-slice_fusion.3), channel_id=1, source_target_pairs={{0,8},{2,10},{4,12},{6,14},{8,0},{10,2},{12,4},{14,6},{16,24},{18,... | collective-permute-start | bytes 196616 | tf_op jit(solution)/shard_map/ppermute | solution.py:78
  60.4 2.4 %collective-permute-done.24 = f32[128,128]{1,0:T(8,128)S(1)} collective-permute-done((f32[128,128]{1,0:T(8,128)S(1)}, f32[128,128]{1,0:T(8,128)S(1)}, u32[]{:S(2)}, u32[]{:S(2)}) %collective-permute-start.24) | collective-permute-done | bytes 65568 | tf_op jit(solution)/shard_map/ppermute | solution.py:78
  63.4 2.4 %collective-permute-start.18 = (f32[128,128]{1,0:T(8,128)S(1)}, f32[128,128]{1,0:T(8,128)S(1)}, u32[]{:S(2)}, u32[]{:S(2)}) collective-permute-start(f32[128,128]{1,0:T(8,128)S(1)} %dynamic-slice_add_fusion.9), channel_id=1, source_target_pairs={{0,16},{2,18},{4,20},{6,22},{8,24},{10,26},{12,28},{14,30},{16,0},... | collective-permute-start | bytes 196616 | tf_op jit(solution)/shard_map/ppermute | solution.py:86
  65.8 2.9 %collective-permute-done.25 = f32[128,128]{1,0:T(8,128)S(1)} collective-permute-done((f32[128,128]{1,0:T(8,128)S(1)}, f32[128,128]{1,0:T(8,128)S(1)}, u32[]{:S(2)}, u32[]{:S(2)}) %collective-permute-start.25) | collective-permute-done | bytes 65568 | tf_op jit(solution)/shard_map/ppermute | solution.py:86
  70.8 2.3 %collective-permute-done.26 = f32[128,128]{1,0:T(8,128)S(1)} collective-permute-done((f32[128,128]{1,0:T(8,128)S(1)}, f32[128,128]{1,0:T(8,128)S(1)}, u32[]{:S(2)}, u32[]{:S(2)}) %collective-permute-start.26) | collective-permute-done | bytes 65568 | tf_op jit(solution)/shard_map/ppermute | solution.py:90
  73.2 1.5 %collective-permute-done.19 = f32[128,128]{1,0:T(8,128)S(1)} collective-permute-done((f32[128,128]{1,0:T(8,128)S(1)}, f32[128,128]{1,0:T(8,128)S(1)}, u32[]{:S(2)}, u32[]{:S(2)}) %collective-permute-start.19) | collective-permute-done | bytes 65568 | tf_op jit(solution)/shard_map/ppermute | solution.py:90
  75.3 2.8 %collective-permute-done.27 = f32[256,128]{1,0:T(8,128)S(1)} collective-permute-done((f32[256,128]{1,0:T(8,128)S(1)}, f32[256,128]{1,0:T(8,128)S(1)}, u32[]{:S(2)}, u32[]{:S(2)}) %collective-permute-start.27) | collective-permute-done | bytes 131104 | tf_op jit(solution)/shard_map/ppermute | solution.py:90
  78.3 1.5 %collective-permute-done.20 = f32[256,128]{1,0:T(8,128)S(1)} collective-permute-done((f32[256,128]{1,0:T(8,128)S(1)}, f32[256,128]{1,0:T(8,128)S(1)}, u32[]{:S(2)}, u32[]{:S(2)}) %collective-permute-start.20) | collective-permute-done | bytes 131104 | tf_op jit(solution)/shard_map/ppermute | solution.py:90
  80.4 1.0 %collective-permute-done.21 = f32[512,128]{1,0:T(8,128)S(1)} collective-permute-done((f32[512,128]{1,0:T(8,128)S(1)}, f32[512,128]{1,0:T(8,128)S(1)}, u32[]{:S(2)}, u32[]{:S(2)}) %collective-permute-start.21) | collective-permute-done | bytes 262176 | tf_op jit(solution)/shard_map/ppermute | solution.py:90
  (99 shorter events, 14.2 us)
Async XLA Ops:
  6.5 4.4 %copy-start.1 = (f32[1024,128]{1,0:T(8,128)}, f32[1024,128]{1,0:T(8,128)S(1)}, u32[]{:S(2)}) copy-start(f32[1024,128]{1,0:T(8,128)S(1)} %get-tuple-element.27) | copy-start | bytes 1572868
  6.5 4.4 %copy-start.2 = (f32[1024,128]{1,0:T(8,128)}, f32[1024,128]{1,0:T(8,128)S(1)}, u32[]{:S(2)}) copy-start(f32[1024,128]{1,0:T(8,128)S(1)} %get-tuple-element.28) | copy-start | bytes 1572868
  7.4 5.3 %collective-permute-start.8 = (f32[512,128]{1,0:T(8,128)}, f32[512,128]{1,0:T(8,128)}, u32[]{:S(2)}, u32[]{:S(2)}) collective-permute-start(f32[512,128]{1,0:T(8,128)} %constant_dynamic-slice_fusion.8), channel_id=1, source_target_pairs={{0,2},{2,0},{4,6},{6,4},{8,10},{10,8},{12,14},{14,12},{16,18},{18,... | collective-permute-start | bytes 786440 | tf_op jit(solution)/shard_map/ppermute | solution.py:78
  7.9 7.6 %collective-permute-start = (f32[512,128]{1,0:T(8,128)S(1)}, f32[512,128]{1,0:T(8,128)}, u32[]{:S(2)}, u32[]{:S(2)}) collective-permute-start(f32[512,128]{1,0:T(8,128)S(1)} %constant_dynamic-slice_fusion.11), channel_id=1, source_target_pairs={{0,2},{2,0},{4,6},{6,4},{8,10},{10,8},{12,14},{14,12},{16,18},{18,... | collective-permute-start | bytes 786440 | tf_op jit(solution)/shard_map/ppermute | solution.py:78
  8.0 15.5 %collective-permute-start.2 = (f32[1,1,2,64,512]{4,3,2,1,0:T(8,128)}, f32[1,1,2,64,512]{4,3,2,1,0:T(8,128)}, u32[]{:S(2)}, u32[]{:S(2)}) collective-permute-start(f32[1,1,2,64,512]{4,3,2,1,0:T(8,128)} %bitcast.3), channel_id=1, source_target_pairs={{0,1},{1,0},{2,3},{3,2},{4,5},{5,4},{6,7},{7,6},{8,9},{9,8},{10,11... | collective-permute-start | bytes 786440 | tf_op jit(solution)/shard_map/ppermute | solution.py:34
  13.8 10.8 %collective-permute-start.9 = (f32[256,128]{1,0:T(8,128)S(1)}, f32[256,128]{1,0:T(8,128)S(1)}, u32[]{:S(2)}, u32[]{:S(2)}) collective-permute-start(f32[256,128]{1,0:T(8,128)S(1)} %constant_dynamic-slice_fusion.7), channel_id=1, source_target_pairs={{0,8},{2,10},{4,12},{6,14},{8,0},{10,2},{12,4},{14,6},{16,24},{18,... | collective-permute-start | bytes 393224 | tf_op jit(solution)/shard_map/ppermute | solution.py:78
  16.5 8.7 %collective-permute-start.1 = (f32[256,128]{1,0:T(8,128)S(1)}, f32[256,128]{1,0:T(8,128)S(1)}, u32[]{:S(2)}, u32[]{:S(2)}) collective-permute-start(f32[256,128]{1,0:T(8,128)S(1)} %constant_dynamic-slice_fusion.10), channel_id=1, source_target_pairs={{0,4},{2,6},{4,0},{6,2},{8,12},{10,14},{12,8},{14,10},{16,20},{18,... | collective-permute-start | bytes 393224 | tf_op jit(solution)/shard_map/ppermute | solution.py:78
  24.7 4.3 %collective-permute-start.10 = (f32[128,128]{1,0:T(8,128)S(1)}, f32[128,128]{1,0:T(8,128)S(1)}, u32[]{:S(2)}, u32[]{:S(2)}) collective-permute-start(f32[128,128]{1,0:T(8,128)S(1)} %constant_dynamic-slice_fusion.6), channel_id=1, source_target_pairs={{0,4},{2,6},{4,0},{6,2},{8,12},{10,14},{12,8},{14,10},{16,20},{18,... | collective-permute-start | bytes 196616 | tf_op jit(solution)/shard_map/ppermute | solution.py:78
  25.3 23.7 %copy-start.3 = (f32[1024,64]{0,1:T(8,128)S(1)}, f32[1024,64]{0,1:T(8,128)}, u32[]{:S(2)}) copy-start(f32[1024,64]{0,1:T(8,128)} %param.9) | copy-start | bytes 786436
  25.3 6.3 %collective-permute-start.3 = (f32[128,128]{1,0:T(8,128)S(1)}, f32[128,128]{1,0:T(8,128)S(1)}, u32[]{:S(2)}, u32[]{:S(2)}) collective-permute-start(f32[128,128]{1,0:T(8,128)S(1)} %constant_dynamic-slice_fusion.9), channel_id=1, source_target_pairs={{0,8},{2,10},{4,12},{6,14},{8,0},{10,2},{12,4},{14,6},{16,24},{18,... | collective-permute-start | bytes 196616 | tf_op jit(solution)/shard_map/ppermute | solution.py:78
  29.0 6.7 %collective-permute-start.11 = (f32[128,128]{1,0:T(8,128)S(1)}, f32[128,128]{1,0:T(8,128)S(1)}, u32[]{:S(2)}, u32[]{:S(2)}) collective-permute-start(f32[128,128]{1,0:T(8,128)S(1)} %dynamic-slice_add_fusion.10), channel_id=1, source_target_pairs={{0,16},{2,18},{4,20},{6,22},{8,24},{10,26},{12,28},{14,30},{16,0},... | collective-permute-start | bytes 196616 | tf_op jit(solution)/shard_map/ppermute | solution.py:86
  31.7 5.8 %collective-permute-start.4 = (f32[128,128]{1,0:T(8,128)S(1)}, f32[128,128]{1,0:T(8,128)S(1)}, u32[]{:S(2)}, u32[]{:S(2)}) collective-permute-start(f32[128,128]{1,0:T(8,128)S(1)} %dynamic-slice_add_fusion.11), channel_id=1, source_target_pairs={{0,16},{2,18},{4,20},{6,22},{8,24},{10,26},{12,28},{14,30},{16,0},... | collective-permute-start | bytes 196616 | tf_op jit(solution)/shard_map/ppermute | solution.py:86
  35.8 4.3 %collective-permute-start.12 = (f32[128,128]{1,0:T(8,128)S(1)}, f32[128,128]{1,0:T(8,128)S(1)}, u32[]{:S(2)}, u32[]{:S(2)}) collective-permute-start(f32[128,128]{1,0:T(8,128)S(1)} %add_subtract_fusion.2), channel_id=1, source_target_pairs={{0,4},{2,6},{4,0},{6,2},{8,12},{10,14},{12,8},{14,10},{16,20},{18,... | collective-permute-start | bytes 196616 | tf_op jit(solution)/shard_map/ppermute | solution.py:90
  37.5 4.3 %collective-permute-start.5 = (f32[128,128]{1,0:T(8,128)S(1)}, f32[128,128]{1,0:T(8,128)S(1)}, u32[]{:S(2)}, u32[]{:S(2)}) collective-permute-start(f32[128,128]{1,0:T(8,128)S(1)} %add_subtract_fusion.3), channel_id=1, source_target_pairs={{0,8},{2,10},{4,12},{6,14},{8,0},{10,2},{12,4},{14,6},{16,24},{18,... | collective-permute-start | bytes 196616 | tf_op jit(solution)/shard_map/ppermute | solution.py:90
  40.1 5.0 %collective-permute-start.13 = (f32[256,128]{1,0:T(8,128)S(1)}, f32[256,128]{1,0:T(8,128)S(1)}, u32[]{:S(2)}, u32[]{:S(2)}) collective-permute-start(f32[256,128]{1,0:T(8,128)S(1)} %pad_maximum_fusion.6), channel_id=1, source_target_pairs={{0,8},{2,10},{4,12},{6,14},{8,0},{10,2},{12,4},{14,6},{16,24},{18,... | collective-permute-start | bytes 393224 | tf_op jit(solution)/shard_map/ppermute | solution.py:90
  41.9 5.0 %collective-permute-start.6 = (f32[256,128]{1,0:T(8,128)S(1)}, f32[256,128]{1,0:T(8,128)S(1)}, u32[]{:S(2)}, u32[]{:S(2)}) collective-permute-start(f32[256,128]{1,0:T(8,128)S(1)} %pad_maximum_fusion.5), channel_id=1, source_target_pairs={{0,4},{2,6},{4,0},{6,2},{8,12},{10,14},{12,8},{14,10},{16,20},{18,... | collective-permute-start | bytes 393224 | tf_op jit(solution)/shard_map/ppermute | solution.py:90
  45.2 1.8 %collective-permute-start.14 = (f32[512,128]{1,0:T(8,128)S(1)}, f32[512,128]{1,0:T(8,128)S(1)}, u32[]{:S(2)}, u32[]{:S(2)}) collective-permute-start(f32[512,128]{1,0:T(8,128)S(1)} %pad_maximum_fusion.2), channel_id=1, source_target_pairs={{0,2},{2,0},{4,6},{6,4},{8,10},{10,8},{12,14},{14,12},{16,18},{18,... | collective-permute-start | bytes 786440 | tf_op jit(solution)/shard_map/ppermute | solution.py:90
  47.0 1.6 %collective-permute-start.7 = (f32[512,128]{1,0:T(8,128)S(1)}, f32[512,128]{1,0:T(8,128)S(1)}, u32[]{:S(2)}, u32[]{:S(2)}) collective-permute-start(f32[512,128]{1,0:T(8,128)S(1)} %pad_maximum_fusion.1), channel_id=1, source_target_pairs={{0,2},{2,0},{4,6},{6,4},{8,10},{10,8},{12,14},{14,12},{16,18},{18,... | collective-permute-start | bytes 786440 | tf_op jit(solution)/shard_map/ppermute | solution.py:90
  51.1 1.6 %collective-permute-start.22 = (f32[512,128]{1,0:T(8,128)S(1)}, f32[512,128]{1,0:T(8,128)S(1)}, u32[]{:S(2)}, u32[]{:S(2)}) collective-permute-start(f32[512,128]{1,0:T(8,128)S(1)} %constant_dynamic-slice_fusion.2), channel_id=1, source_target_pairs={{0,2},{2,0},{4,6},{6,4},{8,10},{10,8},{12,14},{14,12},{16,18},{18,... | collective-permute-start | bytes 786440 | tf_op jit(solution)/shard_map/ppermute | solution.py:78
  51.4 2.0 %collective-permute-start.15 = (f32[512,128]{1,0:T(8,128)S(1)}, f32[512,128]{1,0:T(8,128)S(1)}, u32[]{:S(2)}, u32[]{:S(2)}) collective-permute-start(f32[512,128]{1,0:T(8,128)S(1)} %constant_dynamic-slice_fusion.5), channel_id=1, source_target_pairs={{0,2},{2,0},{4,6},{6,4},{8,10},{10,8},{12,14},{14,12},{16,18},{18,... | collective-permute-start | bytes 786440 | tf_op jit(solution)/shard_map/ppermute | solution.py:78
  52.8 5.6 %collective-permute-start.23 = (f32[256,128]{1,0:T(8,128)S(1)}, f32[256,128]{1,0:T(8,128)S(1)}, u32[]{:S(2)}, u32[]{:S(2)}) collective-permute-start(f32[256,128]{1,0:T(8,128)S(1)} %constant_dynamic-slice_fusion.1), channel_id=1, source_target_pairs={{0,8},{2,10},{4,12},{6,14},{8,0},{10,2},{12,4},{14,6},{16,24},{18,... | collective-permute-start | bytes 393224 | tf_op jit(solution)/shard_map/ppermute | solution.py:78
  53.5 5.5 %collective-permute-start.16 = (f32[256,128]{1,0:T(8,128)S(1)}, f32[256,128]{1,0:T(8,128)S(1)}, u32[]{:S(2)}, u32[]{:S(2)}) collective-permute-start(f32[256,128]{1,0:T(8,128)S(1)} %constant_dynamic-slice_fusion.4), channel_id=1, source_target_pairs={{0,4},{2,6},{4,0},{6,2},{8,12},{10,14},{12,8},{14,10},{16,20},{18,... | collective-permute-start | bytes 393224 | tf_op jit(solution)/shard_map/ppermute | solution.py:78
  58.4 4.3 %collective-permute-start.24 = (f32[128,128]{1,0:T(8,128)S(1)}, f32[128,128]{1,0:T(8,128)S(1)}, u32[]{:S(2)}, u32[]{:S(2)}) collective-permute-start(f32[128,128]{1,0:T(8,128)S(1)} %constant_dynamic-slice_fusion), channel_id=1, source_target_pairs={{0,4},{2,6},{4,0},{6,2},{8,12},{10,14},{12,8},{14,10},{16,20},{18,... | collective-permute-start | bytes 196616 | tf_op jit(solution)/shard_map/ppermute | solution.py:78
  59.1 4.3 %collective-permute-start.17 = (f32[128,128]{1,0:T(8,128)S(1)}, f32[128,128]{1,0:T(8,128)S(1)}, u32[]{:S(2)}, u32[]{:S(2)}) collective-permute-start(f32[128,128]{1,0:T(8,128)S(1)} %constant_dynamic-slice_fusion.3), channel_id=1, source_target_pairs={{0,8},{2,10},{4,12},{6,14},{8,0},{10,2},{12,4},{14,6},{16,24},{18,... | collective-permute-start | bytes 196616 | tf_op jit(solution)/shard_map/ppermute | solution.py:78
  62.8 5.9 %collective-permute-start.25 = (f32[128,128]{1,0:T(8,128)S(1)}, f32[128,128]{1,0:T(8,128)S(1)}, u32[]{:S(2)}, u32[]{:S(2)}) collective-permute-start(f32[128,128]{1,0:T(8,128)S(1)} %dynamic-slice_add_fusion.8), channel_id=1, source_target_pairs={{0,16},{2,18},{4,20},{6,22},{8,24},{10,26},{12,28},{14,30},{16,0},... | collective-permute-start | bytes 196616 | tf_op jit(solution)/shard_map/ppermute | solution.py:86
  63.4 6.7 %collective-permute-start.18 = (f32[128,128]{1,0:T(8,128)S(1)}, f32[128,128]{1,0:T(8,128)S(1)}, u32[]{:S(2)}, u32[]{:S(2)}) collective-permute-start(f32[128,128]{1,0:T(8,128)S(1)} %dynamic-slice_add_fusion.9), channel_id=1, source_target_pairs={{0,16},{2,18},{4,20},{6,22},{8,24},{10,26},{12,28},{14,30},{16,0},... | collective-permute-start | bytes 196616 | tf_op jit(solution)/shard_map/ppermute | solution.py:86
  68.7 4.3 %collective-permute-start.26 = (f32[128,128]{1,0:T(8,128)S(1)}, f32[128,128]{1,0:T(8,128)S(1)}, u32[]{:S(2)}, u32[]{:S(2)}) collective-permute-start(f32[128,128]{1,0:T(8,128)S(1)} %add_subtract_fusion), channel_id=1, source_target_pairs={{0,4},{2,6},{4,0},{6,2},{8,12},{10,14},{12,8},{14,10},{16,20},{18,... | collective-permute-start | bytes 196616 | tf_op jit(solution)/shard_map/ppermute | solution.py:90
  70.1 4.6 %collective-permute-start.19 = (f32[128,128]{1,0:T(8,128)S(1)}, f32[128,128]{1,0:T(8,128)S(1)}, u32[]{:S(2)}, u32[]{:S(2)}) collective-permute-start(f32[128,128]{1,0:T(8,128)S(1)} %add_subtract_fusion.1), channel_id=1, source_target_pairs={{0,8},{2,10},{4,12},{6,14},{8,0},{10,2},{12,4},{14,6},{16,24},{18,... | collective-permute-start | bytes 196616 | tf_op jit(solution)/shard_map/ppermute | solution.py:90
  73.1 5.0 %collective-permute-start.27 = (f32[256,128]{1,0:T(8,128)S(1)}, f32[256,128]{1,0:T(8,128)S(1)}, u32[]{:S(2)}, u32[]{:S(2)}) collective-permute-start(f32[256,128]{1,0:T(8,128)S(1)} %pad_maximum_fusion.8), channel_id=1, source_target_pairs={{0,8},{2,10},{4,12},{6,14},{8,0},{10,2},{12,4},{14,6},{16,24},{18,... | collective-permute-start | bytes 393224 | tf_op jit(solution)/shard_map/ppermute | solution.py:90
  74.7 5.0 %collective-permute-start.20 = (f32[256,128]{1,0:T(8,128)S(1)}, f32[256,128]{1,0:T(8,128)S(1)}, u32[]{:S(2)}, u32[]{:S(2)}) collective-permute-start(f32[256,128]{1,0:T(8,128)S(1)} %pad_maximum_fusion.7), channel_id=1, source_target_pairs={{0,4},{2,6},{4,0},{6,2},{8,12},{10,14},{12,8},{14,10},{16,20},{18,... | collective-permute-start | bytes 393224 | tf_op jit(solution)/shard_map/ppermute | solution.py:90
  78.2 1.7 %collective-permute-start.28 = (f32[512,128]{1,0:T(8,128)S(1)}, f32[512,128]{1,0:T(8,128)S(1)}, u32[]{:S(2)}, u32[]{:S(2)}) collective-permute-start(f32[512,128]{1,0:T(8,128)S(1)} %pad_maximum_fusion.4), channel_id=1, source_target_pairs={{0,2},{2,0},{4,6},{6,4},{8,10},{10,8},{12,14},{14,12},{16,18},{18,... | collective-permute-start | bytes 786440 | tf_op jit(solution)/shard_map/ppermute | solution.py:90
  79.8 1.6 %collective-permute-start.21 = (f32[512,128]{1,0:T(8,128)S(1)}, f32[512,128]{1,0:T(8,128)S(1)}, u32[]{:S(2)}, u32[]{:S(2)}) collective-permute-start(f32[512,128]{1,0:T(8,128)S(1)} %pad_maximum_fusion.3), channel_id=1, source_target_pairs={{0,2},{2,0},{4,6},{6,4},{8,10},{10,8},{12,14},{14,12},{16,18},{18,... | collective-permute-start | bytes 786440 | tf_op jit(solution)/shard_map/ppermute | solution.py:90
  (1 other events, 1.2 us)

commit v17 on v12

--- a/solution.py
+++ b/solution.py
@@ -94,6 +94,47 @@
     return y, riders
 
 
+def paired_reduce_then_gather(xs, rights, axis, n, orders, riders=None, hold=None):
+    me = lax.axis_index(axis)
+    core_pairs = [(i, i ^ 1) for i in range(n)]
+    mine = me & 1
+    half = xs[0].shape[0] // 2
+    keeps = [lax.dynamic_slice_in_dim(x, mine * half, half, 0) for x in xs]
+    sends = [lax.dynamic_slice_in_dim(x, (1 - mine) * half, half, 0) for x in xs]
+    rs = [lax.dynamic_slice_in_dim(r, mine * half, half, 0) for r in rights]
+    got = lax.ppermute(jnp.stack(sends), axis, core_pairs)
+    ys = [keeps[c] + got[c] for c in range(2)]
+    if hold is not None:
+        ys[0], held = lax.optimization_barrier((ys[0], hold[0]))
+        riders = (hold[1](held), riders)
+    for c in range(2):
+        y, r = ys[c], rs[c]
+        order = orders[c]
+        for step, j in enumerate(order[1:-1], start=1):
+            half = y.shape[0] // 2
+            bit = (me >> j) & 1
+            keep = lax.dynamic_slice_in_dim(y, bit * half, half, 0)
+            send = lax.dynamic_slice_in_dim(y, (1 - bit) * half, half, 0)
+            r = lax.dynamic_slice_in_dim(r, bit * half, half, 0)
+            got = lax.ppermute(send, axis, [(i, i ^ (1 << j)) for i in range(n)])
+            if step == 1 and c == 0 and riders is not None:
+                got, riders = lax.optimization_barrier((got, riders))
+            y = keep + got
+        top = order[-1]
+        y = y + lax.ppermute(y, axis, [(i, i ^ (1 << top)) for i in range(n)])
+        y = r - y
+        for j in reversed(order[1:-1]):
+            bit = (me >> j) & 1
+            got = lax.ppermute(y, axis, [(i, i ^ (1 << j)) for i in range(n)])
+            y = jnp.concatenate([jnp.where(bit == 0, y, got), jnp.where(bit == 0, got, y)], 0)
+        ys[c] = y
+    got = lax.ppermute(jnp.stack(ys), axis, core_pairs)
+    outs = [
+        jnp.concatenate([jnp.where(mine == 0, ys[c], got[c]), jnp.where(mine == 0, got[c], ys[c])], 0) for c in range(2)
+    ]
+    return outs, riders
+
+
 def make_shards(n, m):
     power_of_two = n > 1 and (n & (n - 1)) == 0
     rhs_power_of_two = m > 1 and (m & (m - 1)) == 0
@@ -129,24 +170,17 @@
             orders = (list(range(k)), [0, 2, 1] + list(range(3, k)) if k >= 3 else list(range(k)))
             width = first_sum.shape[1] // 2
             columns = (slice(0, width), slice(width, 2 * width))
-            first_blocks = []
-            for chain, (order, cols) in enumerate(zip(orders, columns)):
-                remains, got_riders = ordered_reduce_then_gather(
-                    first_sum[:, cols], right_side[0][:, cols], "blk", n, order,
-                    inverse_pieces if chain == 0 else None,
-                    (solved_before, lambda held: product(factor_panel[1], held)) if chain == 0 else None,
-                )
-                if chain == 0:
-                    panel_sum, inverse_pieces = got_riders
-                first_blocks.append(remains)
+            first_remains, (panel_sum, inverse_pieces) = paired_reduce_then_gather(
+                [first_sum[:, cols] for cols in columns], [right_side[0][:, cols] for cols in columns], "blk", n, orders,
+                inverse_pieces, (solved_before, lambda held: product(factor_panel[1], held)),
+            )
             inverse_full = jnp.concatenate(list(inverse_pieces), axis=2)
-            first_blocks = [product(inverse_full[0], remains) for remains in first_blocks]
-            second_blocks = []
-            for order, cols, block in zip(orders, columns, first_blocks):
-                remains, _ = ordered_reduce_then_gather(
-                    panel_sum[:, cols] + product(coupling, block), right_side[1][:, cols], "blk", n, order
-                )
-                second_blocks.append(product(inverse_full[1], remains))
+            first_blocks = [product(inverse_full[0], remains) for remains in first_remains]
+            second_remains, _ = paired_reduce_then_gather(
+                [panel_sum[:, cols] + product(coupling, block) for cols, block in zip(columns, first_blocks)],
+                [right_side[1][:, cols] for cols in columns], "blk", n, orders,
+            )
+            second_blocks = [product(inverse_full[1], remains) for remains in second_remains]
             first_block = jnp.concatenate(first_blocks, 1)
             second_block = jnp.concatenate(second_blocks, 1)
         else:

time: 76.8 us -> 83 us (1.081)
  waiting for transfers between devices: 33.6 us -> 40.3 us
  starting transfers between devices: 26.3 us -> 22.9 us
  other arithmetic: 1.47 us -> 4.27 us
    ppermute x28 -> x24, waiting for transfers between devices: 33.6 us -> 39.2 us  [the longest x8 16.3 us: paired_reduce_then_gather(): got = lax.ppermute(y, axis, [(i, i ^ 1 << j) for i in range(n)])]
    ppermute x28 -> x24, starting transfers between devices: 23.4 us -> 20 us  [the longest x8 9.05 us: paired_reduce_then_gather(): got = lax.ppermute(send, axis, [(i, i ^ 1 << j) for i in range(n)])]
    squeeze x1, local copies, waits for them, and re-layouts: 1.68 us -> 0.14 us  [shards(): right_side[1][:, cols]]
    ppermute x1, waiting for transfers between devices: 0.01 us -> 1.14 us  [doubling_gather(): got = lax.ppermute(y, axis, [(i, i ^ 1 << j) for i in range(n)])]
    another operation x1, local copies, waits for them, and re-layouts: 0.03 us -> 1.11 us  [shards(): inverse_full = jnp.concatenate(list(inverse_pieces), axis=2)]
    select_n x12 -> x10, other arithmetic: 0.28 us -> 1.33 us  [the longest x2 1.2 us: paired_reduce_then_gather(): jnp.where(mine == 0, ys[c], got[c])]
    another operation x0 -> x8, other arithmetic: none -> 1.01 us  [the longest x6 0.94 us: paired_reduce_then_gather(): got = lax.ppermute(jnp.stack(ys), axis, core_pairs)]
  transfers between devices with their start and end apart: 29 -> 25, of which waited for: 21 -> 20; matrix products, arithmetic and copies ran while one was open for 16% -> 13% of each run, Pallas kernels for 0% -> 0%
where the time goes in v17:
time: 83 us; the launch traced here: 82.9 us
  waiting for transfers between devices  40.3 us (49%)
  starting transfers between devices  22.9 us (28%)
  matrix products  12.6 us (15%)
  other arithmetic  4.27 us (5%)
  local copies, waits for them, and re-layouts  2.35 us (3%)
    ppermute x8, waiting for transfers between devices, paired_reduce_then_gather(): got = lax.ppermute(y, axis, [(i, i ^ 1 << j) for i in range(n)])  16.3 us
    dot_general x8, matrix products, product(): jnp.dot(left, right, precision=lax.Precision.HIGHEST, preferred_element_t...  12.6 us
    ppermute x8, starting transfers between devices, paired_reduce_then_gather(): got = lax.ppermute(send, axis, [(i, i ^ 1 << j) for i in range(n)])  9.05 us
    ppermute x8, waiting for transfers between devices, paired_reduce_then_gather(): got = lax.ppermute(send, axis, [(i, i ^ 1 << j) for i in range(n)])  8.48 us
    ppermute x4, waiting for transfers between devices, paired_reduce_then_gather(): y = y + lax.ppermute(y, axis, [(i, i ^ 1 << top) for i in range(n)])  7.97 us
    ppermute x4, starting transfers between devices, paired_reduce_then_gather(): y = y + lax.ppermute(y, axis, [(i, i ^ 1 << top) for i in range(n)])  6.96 us
    ppermute x8, starting transfers between devices, paired_reduce_then_gather(): got = lax.ppermute(y, axis, [(i, i ^ 1 << j) for i in range(n)])  3.6 us
    ppermute x2, waiting for transfers between devices, paired_reduce_then_gather(): got = lax.ppermute(jnp.stack(sends), axis, core_pairs)  3.44 us
  transfers between devices with their start and end apart: 25, of which 20 were waited for; matrix products, arithmetic and copies ran while one was open for 13% of the time, Pallas kernels for 0%

profile of v17, /device:TPU:0, one launch (start us, length us, event | category | flops | bytes accessed | tf_op | source)
XLA Modules:
  0.0 82.9 jit_solution(14103087462334331191)
XLA Ops:
  0.0 2.9 %collective-permute-start = (f32[1,1,2,64,512]{4,3,2,1,0:T(8,128)}, f32[1,1,2,64,512]{4,3,2,1,0:T(8,128)S(1)}, u32[]{:S(2)}, u32[]{:S(2)}) collective-permute-start(f32[1,1,2,64,512]{4,3,2,1,0:T(8,128)} %bitcast.107), channel_id=1, source_target_pairs={{0,1},{1,0},{2,3},{3,2},{4,5},{5,4},{6,7},{7,6},{8,9},{9,8},{10,11... | collective-permute-start | bytes 786440 | tf_op jit(solution)/shard_map/ppermute | solution.py:34
  2.9 5.4 %fusion.2 = f32[1024,256]{1,0:T(8,128)S(1)} fusion(f32[1024,256]{1,0:T(8,128)S(1)} %copy-done, f32[2,1024,1024]{2,1,0:T(8,128)} %param.5), kind=kOutput, calls=%fused_computation.2 | convolution fusion | flops 3221225472 | bytes 6291456 | tf_op jit(solution)/shard_map/dot_general | solution.py:8
  8.3 1.1 %collective-permute-done = f32[1,1,2,64,512]{4,3,2,1,0:T(8,128)S(1)} collective-permute-done((f32[1,1,2,64,512]{4,3,2,1,0:T(8,128)}, f32[1,1,2,64,512]{4,3,2,1,0:T(8,128)S(1)}, u32[]{:S(2)}, u32[]{:S(2)}) %collective-permute-start) | collective-permute-done | bytes 262176 | tf_op jit(solution)/shard_map/ppermute | solution.py:34
  10.9 1.7 %collective-permute-done.1 = f32[2,512,128]{2,1,0:T(8,128)S(1)} collective-permute-done((f32[2,512,128]{2,1,0:T(8,128)S(1)}, f32[2,512,128]{2,1,0:T(8,128)S(1)}, u32[]{:S(2)}, u32[]{:S(2)}) %collective-permute-start.1) | collective-permute-done | bytes 524320 | tf_op jit(solution)/shard_map/ppermute | solution.py:105
  12.6 1.9 %collective-permute-start.7 = (f32[256,128]{1,0:T(8,128)S(1)}, f32[256,128]{1,0:T(8,128)S(1)}, u32[]{:S(2)}, u32[]{:S(2)}) collective-permute-start(f32[256,128]{1,0:T(8,128)S(1)} %constant_dynamic-slice_fusion.5), channel_id=1, source_target_pairs={{0,8},{2,10},{4,12},{6,14},{8,0},{10,2},{12,4},{14,6},{16,24},{18,... | collective-permute-start | bytes 393224 | tf_op jit(solution)/shard_map/ppermute | solution.py:119
  14.5 1.6 %collective-permute-start.2 = (f32[256,128]{1,0:T(8,128)S(1)}, f32[256,128]{1,0:T(8,128)S(1)}, u32[]{:S(2)}, u32[]{:S(2)}) collective-permute-start(f32[256,128]{1,0:T(8,128)S(1)} %constant_dynamic-slice_fusion.7), channel_id=1, source_target_pairs={{0,4},{2,6},{4,0},{6,2},{8,12},{10,14},{12,8},{14,10},{16,20},{18,... | collective-permute-start | bytes 393224 | tf_op jit(solution)/shard_map/ppermute | solution.py:119
  16.1 3.5 %fusion.6 = f32[1024,256]{1,0:T(8,128)S(1)} fusion(f32[1024,256]{1,0:T(8,128)S(1)} %copy-done, f32[2,1024,1024]{2,1,0:T(8,128)S(1)} %bitcast.106), kind=kOutput, calls=%fused_computation.6 | convolution fusion | flops 3221225472 | bytes 6291456 | tf_op jit(solution)/shard_map/dot_general | solution.py:8
  20.2 1.5 %collective-permute-start.3 = (f32[128,128]{1,0:T(8,128)S(1)}, f32[128,128]{1,0:T(8,128)S(1)}, u32[]{:S(2)}, u32[]{:S(2)}) collective-permute-start(f32[128,128]{1,0:T(8,128)S(1)} %constant_dynamic-slice_fusion.6), channel_id=1, source_target_pairs={{0,8},{2,10},{4,12},{6,14},{8,0},{10,2},{12,4},{14,6},{16,24},{18,... | collective-permute-start | bytes 196616 | tf_op jit(solution)/shard_map/ppermute | solution.py:119
  21.8 2.2 %collective-permute-done.8 = f32[128,128]{1,0:T(8,128)S(1)} collective-permute-done((f32[128,128]{1,0:T(8,128)S(1)}, f32[128,128]{1,0:T(8,128)S(1)}, u32[]{:S(2)}, u32[]{:S(2)}) %collective-permute-start.8) | collective-permute-done | bytes 65568 | tf_op jit(solution)/shard_map/ppermute | solution.py:119
  24.0 2.7 %collective-permute-start.9 = (f32[128,128]{1,0:T(8,128)S(1)}, f32[128,128]{1,0:T(8,128)S(1)}, u32[]{:S(2)}, u32[]{:S(2)}) collective-permute-start(f32[128,128]{1,0:T(8,128)S(1)} %dynamic-slice_add_fusion.6), channel_id=1, source_target_pairs={{0,16},{2,18},{4,20},{6,22},{8,24},{10,26},{12,28},{14,30},{16,0},... | collective-permute-start | bytes 196616 | tf_op jit(solution)/shard_map/ppermute | solution.py:124
  26.6 1.2 %collective-permute-start.4 = (f32[128,128]{1,0:T(8,128)S(1)}, f32[128,128]{1,0:T(8,128)S(1)}, u32[]{:S(2)}, u32[]{:S(2)}) collective-permute-start(f32[128,128]{1,0:T(8,128)S(1)} %dynamic-slice_add_fusion.7), channel_id=1, source_target_pairs={{0,16},{2,18},{4,20},{6,22},{8,24},{10,26},{12,28},{14,30},{16,0},... | collective-permute-start | bytes 196616 | tf_op jit(solution)/shard_map/ppermute | solution.py:124
  27.9 3.2 %collective-permute-done.9 = f32[128,128]{1,0:T(8,128)S(1)} collective-permute-done((f32[128,128]{1,0:T(8,128)S(1)}, f32[128,128]{1,0:T(8,128)S(1)}, u32[]{:S(2)}, u32[]{:S(2)}) %collective-permute-start.9) | collective-permute-done | bytes 65568 | tf_op jit(solution)/shard_map/ppermute | solution.py:124
  32.6 2.8 %collective-permute-done.10 = f32[128,128]{1,0:T(8,128)S(1)} collective-permute-done((f32[128,128]{1,0:T(8,128)S(1)}, f32[128,128]{1,0:T(8,128)S(1)}, u32[]{:S(2)}, u32[]{:S(2)}) %collective-permute-start.10) | collective-permute-done | bytes 65568 | tf_op jit(solution)/shard_map/ppermute | solution.py:128
  35.5 1.3 %collective-permute-done.5 = f32[128,128]{1,0:T(8,128)S(1)} collective-permute-done((f32[128,128]{1,0:T(8,128)S(1)}, f32[128,128]{1,0:T(8,128)S(1)}, u32[]{:S(2)}, u32[]{:S(2)}) %collective-permute-start.5) | collective-permute-done | bytes 65568 | tf_op jit(solution)/shard_map/ppermute | solution.py:128
  37.6 2.9 %collective-permute-done.11 = f32[256,128]{1,0:T(8,128)S(1)} collective-permute-done((f32[256,128]{1,0:T(8,128)S(1)}, f32[256,128]{1,0:T(8,128)S(1)}, u32[]{:S(2)}, u32[]{:S(2)}) %collective-permute-start.11) | collective-permute-done | bytes 131104 | tf_op jit(solution)/shard_map/ppermute | solution.py:128
  40.5 1.4 %collective-permute-done.6 = f32[256,128]{1,0:T(8,128)S(1)} collective-permute-done((f32[256,128]{1,0:T(8,128)S(1)}, f32[256,128]{1,0:T(8,128)S(1)}, u32[]{:S(2)}, u32[]{:S(2)}) %collective-permute-start.6) | collective-permute-done | bytes 131104 | tf_op jit(solution)/shard_map/ppermute | solution.py:128
  43.4 1.1 %slice_bitcast_fusion.10 = (f32[2,64,512]{2,1,0:T(8,128)S(1)}, f32[2,64,512]{2,1,0:T(8,128)S(1)}) fusion(f32[2,2,64,512]{3,2,1,0:T(8,128)} %maximum_bitcast_fusion), kind=kLoop, calls=%fused_computation.58 | loop fusion | bytes 1048576 | tf_op jit(solution)/shard_map/unstack | solution.py:177
  44.5 1.1 %collective-permute-done.12 = f32[2,512,128]{2,1,0:T(8,128)} collective-permute-done((f32[2,512,128]{2,1,0:T(8,128)}, f32[2,512,128]{2,1,0:T(8,128)}, u32[]{:S(2)}, u32[]{:S(2)}) %collective-permute-start.12) | collective-permute-done | bytes 524320 | tf_op jit(solution)/shard_map/ppermute | solution.py:131
  45.7 1.1 %fusion.33 = (f32[512,128]{1,0:T(8,128)S(1)}, f32[512,128]{1,0:T(8,128)S(1)}, f32[512,128]{1,0:T(8,128)S(1)}, f32[512,128]{1,0:T(8,128)S(1)}) fusion(f32[2,512,128]{2,1,0:T(8,128)} %collective-permute-done.12, f32[256,128]{1,0:T(8,128)} %copy-done.2, f32[256,128]{1,0:T(8,128)S(1)} %get-tuple-element.53, pred[]{:T(512)S(6)} %eq.9, ...), kind=kLoop, calls=%fused_computation.65 | loop fusion | flops 393216 | bytes 2097153 | tf_op jit(solution)/shard_map/jit(_where)/select_n | solution.py:133
  50.0 1.8 %collective-permute-done.13 = f32[2,512,128]{2,1,0:T(8,128)S(1)} collective-permute-done((f32[2,512,128]{2,1,0:T(8,128)S(1)}, f32[2,512,128]{2,1,0:T(8,128)S(1)}, u32[]{:S(2)}, u32[]{:S(2)}) %collective-permute-start.13) | collective-permute-done | bytes 524320 | tf_op jit(solution)/shard_map/ppermute | solution.py:105
  53.6 3.9 %collective-permute-done.14 = f32[256,128]{1,0:T(8,128)S(1)} collective-permute-done((f32[256,128]{1,0:T(8,128)S(1)}, f32[256,128]{1,0:T(8,128)S(1)}, u32[]{:S(2)}, u32[]{:S(2)}) %collective-permute-start.14) | collective-permute-done | bytes 131104 | tf_op jit(solution)/shard_map/ppermute | solution.py:119
  58.4 1.2 %collective-permute-start.20 = (f32[128,128]{1,0:T(8,128)S(1)}, f32[128,128]{1,0:T(8,128)S(1)}, u32[]{:S(2)}, u32[]{:S(2)}) collective-permute-start(f32[128,128]{1,0:T(8,128)S(1)} %constant_dynamic-slice_fusion), channel_id=1, source_target_pairs={{0,4},{2,6},{4,0},{6,2},{8,12},{10,14},{12,8},{14,10},{16,20},{18,... | collective-permute-start | bytes 196616 | tf_op jit(solution)/shard_map/ppermute | solution.py:119
  59.5 2.4 %collective-permute-done.15 = f32[128,128]{1,0:T(8,128)S(1)} collective-permute-done((f32[128,128]{1,0:T(8,128)S(1)}, f32[128,128]{1,0:T(8,128)S(1)}, u32[]{:S(2)}, u32[]{:S(2)}) %collective-permute-start.15) | collective-permute-done | bytes 65568 | tf_op jit(solution)/shard_map/ppermute | solution.py:119
  61.9 1.4 %collective-permute-start.16 = (f32[128,128]{1,0:T(8,128)S(1)}, f32[128,128]{1,0:T(8,128)S(1)}, u32[]{:S(2)}, u32[]{:S(2)}) collective-permute-start(f32[128,128]{1,0:T(8,128)S(1)} %dynamic-slice_add_fusion.5), channel_id=1, source_target_pairs={{0,16},{2,18},{4,20},{6,22},{8,24},{10,26},{12,28},{14,30},{16,0},... | collective-permute-start | bytes 196616 | tf_op jit(solution)/shard_map/ppermute | solution.py:124
  63.3 1.7 %collective-permute-start.21 = (f32[128,128]{1,0:T(8,128)S(1)}, f32[128,128]{1,0:T(8,128)S(1)}, u32[]{:S(2)}, u32[]{:S(2)}) collective-permute-start(f32[128,128]{1,0:T(8,128)S(1)} %dynamic-slice_add_fusion.4), channel_id=1, source_target_pairs={{0,16},{2,18},{4,20},{6,22},{8,24},{10,26},{12,28},{14,30},{16,0},... | collective-permute-start | bytes 196616 | tf_op jit(solution)/shard_map/ppermute | solution.py:124
  65.0 2.9 %collective-permute-done.16 = f32[128,128]{1,0:T(8,128)S(1)} collective-permute-done((f32[128,128]{1,0:T(8,128)S(1)}, f32[128,128]{1,0:T(8,128)S(1)}, u32[]{:S(2)}, u32[]{:S(2)}) %collective-permute-start.16) | collective-permute-done | bytes 65568 | tf_op jit(solution)/shard_map/ppermute | solution.py:124
  68.0 1.2 %collective-permute-done.21 = f32[128,128]{1,0:T(8,128)S(1)} collective-permute-done((f32[128,128]{1,0:T(8,128)S(1)}, f32[128,128]{1,0:T(8,128)S(1)}, u32[]{:S(2)}, u32[]{:S(2)}) %collective-permute-start.21) | collective-permute-done | bytes 65568 | tf_op jit(solution)/shard_map/ppermute | solution.py:124
  70.1 2.1 %collective-permute-done.17 = f32[128,128]{1,0:T(8,128)S(1)} collective-permute-done((f32[128,128]{1,0:T(8,128)S(1)}, f32[128,128]{1,0:T(8,128)S(1)}, u32[]{:S(2)}, u32[]{:S(2)}) %collective-permute-start.17) | collective-permute-done | bytes 65568 | tf_op jit(solution)/shard_map/ppermute | solution.py:128
  73.0 1.1 %collective-permute-done.22 = f32[128,128]{1,0:T(8,128)S(1)} collective-permute-done((f32[128,128]{1,0:T(8,128)S(1)}, f32[128,128]{1,0:T(8,128)S(1)}, u32[]{:S(2)}, u32[]{:S(2)}) %collective-permute-start.22) | collective-permute-done | bytes 65568 | tf_op jit(solution)/shard_map/ppermute | solution.py:128
  74.4 2.9 %collective-permute-done.18 = f32[256,128]{1,0:T(8,128)S(1)} collective-permute-done((f32[256,128]{1,0:T(8,128)S(1)}, f32[256,128]{1,0:T(8,128)S(1)}, u32[]{:S(2)}, u32[]{:S(2)}) %collective-permute-start.18) | collective-permute-done | bytes 131104 | tf_op jit(solution)/shard_map/ppermute | solution.py:128
  77.3 1.9 %collective-permute-done.23 = f32[256,128]{1,0:T(8,128)S(1)} collective-permute-done((f32[256,128]{1,0:T(8,128)S(1)}, f32[256,128]{1,0:T(8,128)S(1)}, u32[]{:S(2)}, u32[]{:S(2)}) %collective-permute-start.23) | collective-permute-done | bytes 131104 | tf_op jit(solution)/shard_map/ppermute | solution.py:128
  79.4 1.9 %collective-permute-done.24 = f32[2,512,128]{2,1,0:T(8,128)S(1)} collective-permute-done((f32[2,512,128]{2,1,0:T(8,128)S(1)}, f32[2,512,128]{2,1,0:T(8,128)S(1)}, u32[]{:S(2)}, u32[]{:S(2)}) %collective-permute-start.24) | collective-permute-done | bytes 524320 | tf_op jit(solution)/shard_map/ppermute | solution.py:131
  (98 shorter events, 15.7 us)
Async XLA Ops:
  0.0 2.9 %copy-start = (f32[1024,256]{1,0:T(8,128)S(1)}, f32[1024,256]{1,0:T(8,128)}, u32[]{:S(2)}) copy-start(f32[1024,256]{1,0:T(8,128)} %param.6) | copy-start | bytes 3145732
  0.0 9.5 %copy-start.4 = (f32[2,64,512]{2,1,0:T(8,128)S(1)}, f32[2,64,512]{2,1,0:T(8,128)}, u32[]{:S(2)}) copy-start(f32[2,64,512]{2,1,0:T(8,128)} %param.8) | copy-start | bytes 786436
  0.0 9.5 %collective-permute-start = (f32[1,1,2,64,512]{4,3,2,1,0:T(8,128)}, f32[1,1,2,64,512]{4,3,2,1,0:T(8,128)S(1)}, u32[]{:S(2)}, u32[]{:S(2)}) collective-permute-start(f32[1,1,2,64,512]{4,3,2,1,0:T(8,128)} %bitcast.107), channel_id=1, source_target_pairs={{0,1},{1,0},{2,3},{3,2},{4,5},{5,4},{6,7},{7,6},{8,9},{9,8},{10,11... | collective-permute-start | bytes 786440 | tf_op jit(solution)/shard_map/ppermute | solution.py:34
  2.9 13.2 %slice-start = ((s8[8388608]{0:T(1024)(128)(4,1)}), s8[4194304]{0:T(1024)(128)(4,1)S(1)}, s32[]{:S(2)}) async-start(s8[8388608]{0:T(1024)(128)(4,1)} %bitcast.105), calls=%async_computation | async-start | bytes 8388608
  8.3 2.3 %copy-start.1 = (f32[2,1024,256]{2,1,0:T(8,128)S(1)}, f32[2,1024,256]{2,1,0:T(8,128)}, u32[]{:S(2)}) copy-start(f32[2,1024,256]{2,1,0:T(8,128)} %param.7) | copy-start | bytes 6291460
  10.5 5.6 %slice-start.1 = ((s8[8388608]{0:T(1024)(128)(4,1)}), s8[4194304]{0:T(1024)(128)(4,1)S(1)}, s32[]{:S(2)}) async-start(s8[8388608]{0:T(1024)(128)(4,1)} %bitcast.105), calls=%async_computation.1 | async-start | bytes 8388608
  10.6 2.0 %collective-permute-start.1 = (f32[2,512,128]{2,1,0:T(8,128)S(1)}, f32[2,512,128]{2,1,0:T(8,128)S(1)}, u32[]{:S(2)}, u32[]{:S(2)}) collective-permute-start(f32[2,512,128]{2,1,0:T(8,128)S(1)} %pad_maximum_fusion), channel_id=1, source_target_pairs={{0,2},{2,0},{4,6},{6,4},{8,10},{10,8},{12,14},{14,12},{16,18},{18,... | collective-permute-start | bytes 1572872 | tf_op jit(solution)/shard_map/ppermute | solution.py:105
  12.6 6.9 %collective-permute-start.7 = (f32[256,128]{1,0:T(8,128)S(1)}, f32[256,128]{1,0:T(8,128)S(1)}, u32[]{:S(2)}, u32[]{:S(2)}) collective-permute-start(f32[256,128]{1,0:T(8,128)S(1)} %constant_dynamic-slice_fusion.5), channel_id=1, source_target_pairs={{0,8},{2,10},{4,12},{6,14},{8,0},{10,2},{12,4},{14,6},{16,24},{18,... | collective-permute-start | bytes 393224 | tf_op jit(solution)/shard_map/ppermute | solution.py:119
  14.5 5.7 %collective-permute-start.2 = (f32[256,128]{1,0:T(8,128)S(1)}, f32[256,128]{1,0:T(8,128)S(1)}, u32[]{:S(2)}, u32[]{:S(2)}) collective-permute-start(f32[256,128]{1,0:T(8,128)S(1)} %constant_dynamic-slice_fusion.7), channel_id=1, source_target_pairs={{0,4},{2,6},{4,0},{6,2},{8,12},{10,14},{12,8},{14,10},{16,20},{18,... | collective-permute-start | bytes 393224 | tf_op jit(solution)/shard_map/ppermute | solution.py:119
  19.6 4.3 %collective-permute-start.8 = (f32[128,128]{1,0:T(8,128)S(1)}, f32[128,128]{1,0:T(8,128)S(1)}, u32[]{:S(2)}, u32[]{:S(2)}) collective-permute-start(f32[128,128]{1,0:T(8,128)S(1)} %constant_dynamic-slice_fusion.4), channel_id=1, source_target_pairs={{0,4},{2,6},{4,0},{6,2},{8,12},{10,14},{12,8},{14,10},{16,20},{18,... | collective-permute-start | bytes 196616 | tf_op jit(solution)/shard_map/ppermute | solution.py:119
  20.2 6.4 %collective-permute-start.3 = (f32[128,128]{1,0:T(8,128)S(1)}, f32[128,128]{1,0:T(8,128)S(1)}, u32[]{:S(2)}, u32[]{:S(2)}) collective-permute-start(f32[128,128]{1,0:T(8,128)S(1)} %constant_dynamic-slice_fusion.6), channel_id=1, source_target_pairs={{0,8},{2,10},{4,12},{6,14},{8,0},{10,2},{12,4},{14,6},{16,24},{18,... | collective-permute-start | bytes 196616 | tf_op jit(solution)/shard_map/ppermute | solution.py:119
  24.0 7.1 %collective-permute-start.9 = (f32[128,128]{1,0:T(8,128)S(1)}, f32[128,128]{1,0:T(8,128)S(1)}, u32[]{:S(2)}, u32[]{:S(2)}) collective-permute-start(f32[128,128]{1,0:T(8,128)S(1)} %dynamic-slice_add_fusion.6), channel_id=1, source_target_pairs={{0,16},{2,18},{4,20},{6,22},{8,24},{10,26},{12,28},{14,30},{16,0},... | collective-permute-start | bytes 196616 | tf_op jit(solution)/shard_map/ppermute | solution.py:124
  26.6 5.8 %collective-permute-start.4 = (f32[128,128]{1,0:T(8,128)S(1)}, f32[128,128]{1,0:T(8,128)S(1)}, u32[]{:S(2)}, u32[]{:S(2)}) collective-permute-start(f32[128,128]{1,0:T(8,128)S(1)} %dynamic-slice_add_fusion.7), channel_id=1, source_target_pairs={{0,16},{2,18},{4,20},{6,22},{8,24},{10,26},{12,28},{14,30},{16,0},... | collective-permute-start | bytes 196616 | tf_op jit(solution)/shard_map/ppermute | solution.py:124
  31.1 4.3 %collective-permute-start.10 = (f32[128,128]{1,0:T(8,128)S(1)}, f32[128,128]{1,0:T(8,128)S(1)}, u32[]{:S(2)}, u32[]{:S(2)}) collective-permute-start(f32[128,128]{1,0:T(8,128)S(1)} %add_subtract_fusion.2), channel_id=1, source_target_pairs={{0,4},{2,6},{4,0},{6,2},{8,12},{10,14},{12,8},{14,10},{16,20},{18,... | collective-permute-start | bytes 196616 | tf_op jit(solution)/shard_map/ppermute | solution.py:128
  32.5 4.3 %collective-permute-start.5 = (f32[128,128]{1,0:T(8,128)S(1)}, f32[128,128]{1,0:T(8,128)S(1)}, u32[]{:S(2)}, u32[]{:S(2)}) collective-permute-start(f32[128,128]{1,0:T(8,128)S(1)} %add_subtract_fusion.3), channel_id=1, source_target_pairs={{0,8},{2,10},{4,12},{6,14},{8,0},{10,2},{12,4},{14,6},{16,24},{18,... | collective-permute-start | bytes 196616 | tf_op jit(solution)/shard_map/ppermute | solution.py:128
  35.4 5.0 %collective-permute-start.11 = (f32[256,128]{1,0:T(8,128)S(1)}, f32[256,128]{1,0:T(8,128)S(1)}, u32[]{:S(2)}, u32[]{:S(2)}) collective-permute-start(f32[256,128]{1,0:T(8,128)S(1)} %pad_maximum_fusion.10), channel_id=1, source_target_pairs={{0,8},{2,10},{4,12},{6,14},{8,0},{10,2},{12,4},{14,6},{16,24},{18,... | collective-permute-start | bytes 393224 | tf_op jit(solution)/shard_map/ppermute | solution.py:128
  36.9 5.0 %collective-permute-start.6 = (f32[256,128]{1,0:T(8,128)S(1)}, f32[256,128]{1,0:T(8,128)S(1)}, u32[]{:S(2)}, u32[]{:S(2)}) collective-permute-start(f32[256,128]{1,0:T(8,128)S(1)} %pad_maximum_fusion.9), channel_id=1, source_target_pairs={{0,4},{2,6},{4,0},{6,2},{8,12},{10,14},{12,8},{14,10},{16,20},{18,... | collective-permute-start | bytes 393224 | tf_op jit(solution)/shard_map/ppermute | solution.py:128
  41.9 0.7 copy-start.2
  43.4 2.3 %collective-permute-start.12 = (f32[2,512,128]{2,1,0:T(8,128)}, f32[2,512,128]{2,1,0:T(8,128)}, u32[]{:S(2)}, u32[]{:S(2)}) collective-permute-start(f32[2,512,128]{2,1,0:T(8,128)} %pad_maximum_fusion.1), channel_id=1, source_target_pairs={{0,2},{2,0},{4,6},{6,4},{8,10},{10,8},{12,14},{14,12},{16,18},{18,... | collective-permute-start | bytes 1572872 | tf_op jit(solution)/shard_map/ppermute | solution.py:131
  43.4 4.3 %copy-start.3 = (f32[1024,64]{0,1:T(8,128)S(1)}, f32[1024,64]{0,1:T(8,128)}, u32[]{:S(2)}) copy-start(f32[1024,64]{0,1:T(8,128)} %param.9) | copy-start | bytes 786436
  49.8 2.0 %collective-permute-start.13 = (f32[2,512,128]{2,1,0:T(8,128)S(1)}, f32[2,512,128]{2,1,0:T(8,128)S(1)}, u32[]{:S(2)}, u32[]{:S(2)}) collective-permute-start(f32[2,512,128]{2,1,0:T(8,128)S(1)} %pad_maximum_fusion.2), channel_id=1, source_target_pairs={{0,2},{2,0},{4,6},{6,4},{8,10},{10,8},{12,14},{14,12},{16,18},{18,... | collective-permute-start | bytes 1572872 | tf_op jit(solution)/shard_map/ppermute | solution.py:105
  51.9 5.6 %collective-permute-start.14 = (f32[256,128]{1,0:T(8,128)S(1)}, f32[256,128]{1,0:T(8,128)S(1)}, u32[]{:S(2)}, u32[]{:S(2)}) collective-permute-start(f32[256,128]{1,0:T(8,128)S(1)} %constant_dynamic-slice_fusion.3), channel_id=1, source_target_pairs={{0,4},{2,6},{4,0},{6,2},{8,12},{10,14},{12,8},{14,10},{16,20},{18,... | collective-permute-start | bytes 393224 | tf_op jit(solution)/shard_map/ppermute | solution.py:119
  52.8 5.6 %collective-permute-start.19 = (f32[256,128]{1,0:T(8,128)S(1)}, f32[256,128]{1,0:T(8,128)S(1)}, u32[]{:S(2)}, u32[]{:S(2)}) collective-permute-start(f32[256,128]{1,0:T(8,128)S(1)} %constant_dynamic-slice_fusion.1), channel_id=1, source_target_pairs={{0,8},{2,10},{4,12},{6,14},{8,0},{10,2},{12,4},{14,6},{16,24},{18,... | collective-permute-start | bytes 393224 | tf_op jit(solution)/shard_map/ppermute | solution.py:119
  57.6 4.3 %collective-permute-start.15 = (f32[128,128]{1,0:T(8,128)S(1)}, f32[128,128]{1,0:T(8,128)S(1)}, u32[]{:S(2)}, u32[]{:S(2)}) collective-permute-start(f32[128,128]{1,0:T(8,128)S(1)} %constant_dynamic-slice_fusion.2), channel_id=1, source_target_pairs={{0,8},{2,10},{4,12},{6,14},{8,0},{10,2},{12,4},{14,6},{16,24},{18,... | collective-permute-start | bytes 196616 | tf_op jit(solution)/shard_map/ppermute | solution.py:119
  58.4 4.9 %collective-permute-start.20 = (f32[128,128]{1,0:T(8,128)S(1)}, f32[128,128]{1,0:T(8,128)S(1)}, u32[]{:S(2)}, u32[]{:S(2)}) collective-permute-start(f32[128,128]{1,0:T(8,128)S(1)} %constant_dynamic-slice_fusion), channel_id=1, source_target_pairs={{0,4},{2,6},{4,0},{6,2},{8,12},{10,14},{12,8},{14,10},{16,20},{18,... | collective-permute-start | bytes 196616 | tf_op jit(solution)/shard_map/ppermute | solution.py:119
  61.9 6.0 %collective-permute-start.16 = (f32[128,128]{1,0:T(8,128)S(1)}, f32[128,128]{1,0:T(8,128)S(1)}, u32[]{:S(2)}, u32[]{:S(2)}) collective-permute-start(f32[128,128]{1,0:T(8,128)S(1)} %dynamic-slice_add_fusion.5), channel_id=1, source_target_pairs={{0,16},{2,18},{4,20},{6,22},{8,24},{10,26},{12,28},{14,30},{16,0},... | collective-permute-start | bytes 196616 | tf_op jit(solution)/shard_map/ppermute | solution.py:124
  63.3 6.0 %collective-permute-start.21 = (f32[128,128]{1,0:T(8,128)S(1)}, f32[128,128]{1,0:T(8,128)S(1)}, u32[]{:S(2)}, u32[]{:S(2)}) collective-permute-start(f32[128,128]{1,0:T(8,128)S(1)} %dynamic-slice_add_fusion.4), channel_id=1, source_target_pairs={{0,16},{2,18},{4,20},{6,22},{8,24},{10,26},{12,28},{14,30},{16,0},... | collective-permute-start | bytes 196616 | tf_op jit(solution)/shard_map/ppermute | solution.py:124
  67.9 4.3 %collective-permute-start.17 = (f32[128,128]{1,0:T(8,128)S(1)}, f32[128,128]{1,0:T(8,128)S(1)}, u32[]{:S(2)}, u32[]{:S(2)}) collective-permute-start(f32[128,128]{1,0:T(8,128)S(1)} %add_subtract_fusion.1), channel_id=1, source_target_pairs={{0,8},{2,10},{4,12},{6,14},{8,0},{10,2},{12,4},{14,6},{16,24},{18,... | collective-permute-start | bytes 196616 | tf_op jit(solution)/shard_map/ppermute | solution.py:128
  69.3 4.9 %collective-permute-start.22 = (f32[128,128]{1,0:T(8,128)S(1)}, f32[128,128]{1,0:T(8,128)S(1)}, u32[]{:S(2)}, u32[]{:S(2)}) collective-permute-start(f32[128,128]{1,0:T(8,128)S(1)} %add_subtract_fusion), channel_id=1, source_target_pairs={{0,4},{2,6},{4,0},{6,2},{8,12},{10,14},{12,8},{14,10},{16,20},{18,... | collective-permute-start | bytes 196616 | tf_op jit(solution)/shard_map/ppermute | solution.py:128
  72.3 5.0 %collective-permute-start.18 = (f32[256,128]{1,0:T(8,128)S(1)}, f32[256,128]{1,0:T(8,128)S(1)}, u32[]{:S(2)}, u32[]{:S(2)}) collective-permute-start(f32[256,128]{1,0:T(8,128)S(1)} %pad_maximum_fusion.11), channel_id=1, source_target_pairs={{0,4},{2,6},{4,0},{6,2},{8,12},{10,14},{12,8},{14,10},{16,20},{18,... | collective-permute-start | bytes 393224 | tf_op jit(solution)/shard_map/ppermute | solution.py:128
  74.2 5.0 %collective-permute-start.23 = (f32[256,128]{1,0:T(8,128)S(1)}, f32[256,128]{1,0:T(8,128)S(1)}, u32[]{:S(2)}, u32[]{:S(2)}) collective-permute-start(f32[256,128]{1,0:T(8,128)S(1)} %pad_maximum_fusion.12), channel_id=1, source_target_pairs={{0,8},{2,10},{4,12},{6,14},{8,0},{10,2},{12,4},{14,6},{16,24},{18,... | collective-permute-start | bytes 393224 | tf_op jit(solution)/shard_map/ppermute | solution.py:128
  79.3 2.0 %collective-permute-start.24 = (f32[2,512,128]{2,1,0:T(8,128)S(1)}, f32[2,512,128]{2,1,0:T(8,128)S(1)}, u32[]{:S(2)}, u32[]{:S(2)}) collective-permute-start(f32[2,512,128]{2,1,0:T(8,128)S(1)} %pad_maximum_fusion.3), channel_id=1, source_target_pairs={{0,2},{2,0},{4,6},{6,4},{8,10},{10,8},{12,14},{14,12},{16,18},{18,... | collective-permute-start | bytes 1572872 | tf_op jit(solution)/shard_map/ppermute | solution.py:131

commit v18 on v16

--- a/solution.py
+++ b/solution.py
@@ -109,6 +109,11 @@
         return lax.all_gather(x, "blk", axis=0, tiled=True)
 
     def shards(factor_panel, solved_before, right_side, diag_inverse, coupling):
+        def gather_inverse(inverse):
+            if rhs_power_of_two:
+                return doubling_gather(inverse[None], "rhs", m)
+            return lax.all_gather(inverse, "rhs", axis=0)
+
         own_count = diag_inverse.shape[1]
         my_index = lax.axis_index("blk")
 
@@ -116,13 +121,10 @@
             return lax.dynamic_slice_in_dim(matrix, my_index * own_count, own_count, 0)
 
         first_sum = product(factor_panel[0], solved_before)
-        first_sum, held_inverse = lax.optimization_barrier((first_sum, diag_inverse))
-        if rhs_power_of_two:
-            inverse_pieces = doubling_gather(held_inverse[None], "rhs", m)
-        else:
-            inverse_pieces = lax.all_gather(held_inverse, "rhs", axis=0)
         chained = power_of_two and n >= 4
         if not chained:
+            inverse_pieces = gather_inverse(diag_inverse)
+            first_sum, inverse_pieces = lax.optimization_barrier((first_sum, inverse_pieces))
             panel_sum = product(factor_panel[1], solved_before)
         if chained:
             k = n.bit_length() - 1
@@ -133,11 +135,12 @@
             for chain, (order, cols) in enumerate(zip(orders, columns)):
                 remains, got_riders = ordered_reduce_then_gather(
                     first_sum[:, cols], right_side[0][:, cols], "blk", n, order,
-                    inverse_pieces if chain == 0 else None,
-                    (solved_before, lambda held: product(factor_panel[1], held)) if chain == 0 else None,
+                    None,
+                    ((solved_before, diag_inverse), lambda held: (product(factor_panel[1], held[0]), gather_inverse(held[1])))
+                    if chain == 0 else None,
                 )
                 if chain == 0:
-                    panel_sum, inverse_pieces = got_riders
+                    (panel_sum, inverse_pieces), _ = got_riders
                 first_blocks.append(remains)
             inverse_full = jnp.concatenate(list(inverse_pieces), axis=2)
             first_blocks = [product(inverse_full[0], remains) for remains in first_blocks]

time: 82.8 us -> 87.9 us (1.062)
  starting transfers between devices: 21.7 us -> 25.7 us
  waiting for transfers between devices: 37.4 us -> 39.5 us
  other arithmetic: 4.56 us -> 3.53 us
    ppermute x12, waiting for transfers between devices: 10.9 us -> 15.4 us  [ordered_reduce_then_gather(): got = lax.ppermute(send, axis, [(i, i ^ 1 << j) for i in range(n)])]
    ppermute x12, starting transfers between devices: 3.65 us -> 7.2 us  [ordered_reduce_then_gather(): got = lax.ppermute(y, axis, [(i, i ^ 1 << j) for i in range(n)])]
    ppermute x12, waiting for transfers between devices: 18.7 us -> 15.2 us  [ordered_reduce_then_gather(): got = lax.ppermute(y, axis, [(i, i ^ 1 << j) for i in range(n)])]
    ppermute x12, starting transfers between devices: 8.66 us -> 11.8 us  [ordered_reduce_then_gather(): got = lax.ppermute(send, axis, [(i, i ^ 1 << j) for i in range(n)])]
    ppermute x4, starting transfers between devices: 6.4 us -> 5.06 us  [ordered_reduce_then_gather(): y = y + lax.ppermute(y, axis, [(i, i ^ 1 << top) for i in range(n)])]
    ppermute x1, starting transfers between devices: 2.94 us -> 1.64 us  [doubling_gather(): got = lax.ppermute(y, axis, [(i, i ^ 1 << j) for i in range(n)])]
    ppermute x4, waiting for transfers between devices: 7.73 us -> 8.84 us  [ordered_reduce_then_gather(): y = y + lax.ppermute(y, axis, [(i, i ^ 1 << top) for i in range(n)])]
    another operation x1, other arithmetic: 1.07 us -> 0.04 us  [doubling_gather(): y = jnp.stack([low, high], 1).reshape((-1,) + x.shape)]
  transfers between devices with their start and end apart: 29 -> 29, of which waited for: 19 -> 18; matrix products, arithmetic and copies ran while one was open for 15% -> 14% of each run, Pallas kernels for 0% -> 0%
where the time goes in v18:
time: 87.9 us; the launch traced here: 87.7 us
  waiting for transfers between devices  39.5 us (45%)
  starting transfers between devices  25.7 us (29%)
  matrix products  14.3 us (16%)
  local copies, waits for them, and re-layouts  4.16 us (5%)
  other arithmetic  3.53 us (4%)
    ppermute x12, waiting for transfers between devices, ordered_reduce_then_gather(): got = lax.ppermute(send, axis, [(i, i ^ 1 << j) for i in range(n)])  15.4 us
    ppermute x12, waiting for transfers between devices, ordered_reduce_then_gather(): got = lax.ppermute(y, axis, [(i, i ^ 1 << j) for i in range(n)])  15.2 us
    dot_general x8, matrix products, product(): jnp.dot(left, right, precision=lax.Precision.HIGHEST, preferred_element_t...  14.3 us
    ppermute x12, starting transfers between devices, ordered_reduce_then_gather(): got = lax.ppermute(send, axis, [(i, i ^ 1 << j) for i in range(n)])  11.8 us
    ppermute x4, waiting for transfers between devices, ordered_reduce_then_gather(): y = y + lax.ppermute(y, axis, [(i, i ^ 1 << top) for i in range(n)])  8.84 us
    ppermute x12, starting transfers between devices, ordered_reduce_then_gather(): got = lax.ppermute(y, axis, [(i, i ^ 1 << j) for i in range(n)])  7.2 us
    ppermute x4, starting transfers between devices, ordered_reduce_then_gather(): y = y + lax.ppermute(y, axis, [(i, i ^ 1 << top) for i in range(n)])  5.06 us
    add x12, other arithmetic, ordered_reduce_then_gather(): y = keep + got  2.3 us
  transfers between devices with their start and end apart: 29, of which 18 were waited for; matrix products, arithmetic and copies ran while one was open for 14% of the time, Pallas kernels for 0%

profile of v18, /device:TPU:0, one launch (start us, length us, event | category | flops | bytes accessed | tf_op | source)
XLA Modules:
  0.0 87.7 jit_solution(17402974006141464537)
XLA Ops:
  0.0 1.2 %copy-done = f32[1024,256]{1,0:T(8,128)S(1)} copy-done((f32[1024,256]{1,0:T(8,128)S(1)}, f32[1024,256]{1,0:T(8,128)}, u32[]{:S(2)}) %copy-start) | copy-done | bytes 1048600
  1.2 5.2 %fusion.2 = f32[1024,256]{1,0:T(8,128)S(1)} fusion(f32[1024,256]{1,0:T(8,128)S(1)} %copy-done, f32[2,1024,1024]{2,1,0:T(8,128)} %param.5), kind=kOutput, calls=%fused_computation.2 | convolution fusion | flops 3221225472 | bytes 6291456 | tf_op jit(solution)/shard_map/dot_general | solution.py:8
  8.0 1.7 %slice_bitcast_fusion = (f32[1024,256]{1,0:T(8,128)S(1)}, f32[1024,256]{1,0:T(8,128)S(1)}) fusion(f32[2,1024,256]{2,1,0:T(8,128)} %param.7), kind=kLoop, calls=%fused_computation.9 | loop fusion | bytes 4194304 | tf_op jit(solution)/shard_map/squeeze | solution.py:150
  9.8 1.1 %dynamic-slice_add_fusion.2 = f32[512,128]{1,0:T(8,128)S(1)} fusion(f32[512,128]{1,0:T(8,128)} %collective-permute-done.8, f32[1024,128]{1,0:T(8,128)} %copy-done.2, s32[]{:T(128)S(6)} %select_n.190), kind=kLoop, calls=%fused_computation.42 | loop fusion | flops 65536 | bytes 786436 | tf_op jit(solution)/shard_map/add | solution.py:81
  10.9 3.1 %collective-permute-start.9 = (f32[256,128]{1,0:T(8,128)S(1)}, f32[256,128]{1,0:T(8,128)S(1)}, u32[]{:S(2)}, u32[]{:S(2)}) collective-permute-start(f32[256,128]{1,0:T(8,128)S(1)} %constant_dynamic-slice_fusion.7), channel_id=1, source_target_pairs={{0,8},{2,10},{4,12},{6,14},{8,0},{10,2},{12,4},{14,6},{16,24},{18,... | collective-permute-start | bytes 393224 | tf_op jit(solution)/shard_map/ppermute | solution.py:78
  14.0 1.1 %dynamic-slice_add_fusion.3 = f32[512,128]{1,0:T(8,128)S(1)} fusion(f32[512,128]{1,0:T(8,128)} %collective-permute-done, f32[1024,128]{1,0:T(8,128)} %copy-done.1, s32[]{:T(128)S(6)} %select_n.190), kind=kLoop, calls=%fused_computation.47 | loop fusion | flops 65536 | bytes 786436 | tf_op jit(solution)/shard_map/add | solution.py:81
  15.0 2.7 %collective-permute-done.9 = f32[256,128]{1,0:T(8,128)S(1)} collective-permute-done((f32[256,128]{1,0:T(8,128)S(1)}, f32[256,128]{1,0:T(8,128)S(1)}, u32[]{:S(2)}, u32[]{:S(2)}) %collective-permute-start.9) | collective-permute-done | bytes 131104 | tf_op jit(solution)/shard_map/ppermute | solution.py:78
  17.7 1.7 %collective-permute-start.10 = (f32[128,128]{1,0:T(8,128)S(1)}, f32[128,128]{1,0:T(8,128)S(1)}, u32[]{:S(2)}, u32[]{:S(2)}) collective-permute-start(f32[128,128]{1,0:T(8,128)S(1)} %constant_dynamic-slice_fusion.6), channel_id=1, source_target_pairs={{0,4},{2,6},{4,0},{6,2},{8,12},{10,14},{12,8},{14,10},{16,20},{18,... | collective-permute-start | bytes 196616 | tf_op jit(solution)/shard_map/ppermute | solution.py:78
  19.9 1.6 %collective-permute-start.2 = (f32[1,1,2,64,512]{4,3,2,1,0:T(8,128)S(1)}, f32[1,1,2,64,512]{4,3,2,1,0:T(8,128)S(1)}, u32[]{:S(2)}, u32[]{:S(2)}) collective-permute-start(f32[1,1,2,64,512]{4,3,2,1,0:T(8,128)S(1)} %bitcast.49), channel_id=1, source_target_pairs={{0,1},{1,0},{2,3},{3,2},{4,5},{5,4},{6,7},{7,6},{8,9},{9,8},{10,11... | collective-permute-start | bytes 786440 | tf_op jit(solution)/shard_map/ppermute | solution.py:34
  21.6 1.2 %collective-permute-done.10 = f32[128,128]{1,0:T(8,128)S(1)} collective-permute-done((f32[128,128]{1,0:T(8,128)S(1)}, f32[128,128]{1,0:T(8,128)S(1)}, u32[]{:S(2)}, u32[]{:S(2)}) %collective-permute-start.10) | collective-permute-done | bytes 65568 | tf_op jit(solution)/shard_map/ppermute | solution.py:78
  22.8 2.7 %collective-permute-start.11 = (f32[128,128]{1,0:T(8,128)S(1)}, f32[128,128]{1,0:T(8,128)S(1)}, u32[]{:S(2)}, u32[]{:S(2)}) collective-permute-start(f32[128,128]{1,0:T(8,128)S(1)} %dynamic-slice_add_fusion.10), channel_id=1, source_target_pairs={{0,16},{2,18},{4,20},{6,22},{8,24},{10,26},{12,28},{14,30},{16,0},... | collective-permute-start | bytes 196616 | tf_op jit(solution)/shard_map/ppermute | solution.py:86
  25.5 5.3 %fusion.6 = f32[1024,256]{1,0:T(8,128)S(1)} fusion(f32[1024,256]{1,0:T(8,128)S(1)} %copy-done, f32[2,1024,1024]{2,1,0:T(8,128)} %param.5), kind=kOutput, calls=%fused_computation.6 | convolution fusion | flops 3221225472 | bytes 6291456 | tf_op jit(solution)/shard_map/dot_general | solution.py:8
  30.9 1.3 %collective-permute-start.12 = (f32[128,128]{1,0:T(8,128)S(1)}, f32[128,128]{1,0:T(8,128)S(1)}, u32[]{:S(2)}, u32[]{:S(2)}) collective-permute-start(f32[128,128]{1,0:T(8,128)S(1)} %add_subtract_fusion.2), channel_id=1, source_target_pairs={{0,4},{2,6},{4,0},{6,2},{8,12},{10,14},{12,8},{14,10},{16,20},{18,... | collective-permute-start | bytes 196616 | tf_op jit(solution)/shard_map/ppermute | solution.py:90
  32.4 1.6 %collective-permute-start.3 = (f32[128,128]{1,0:T(8,128)S(1)}, f32[128,128]{1,0:T(8,128)S(1)}, u32[]{:S(2)}, u32[]{:S(2)}) collective-permute-start(f32[128,128]{1,0:T(8,128)S(1)} %constant_dynamic-slice_fusion.9), channel_id=1, source_target_pairs={{0,8},{2,10},{4,12},{6,14},{8,0},{10,2},{12,4},{14,6},{16,24},{18,... | collective-permute-start | bytes 196616 | tf_op jit(solution)/shard_map/ppermute | solution.py:78
  34.1 3.4 %collective-permute-done.3 = f32[128,128]{1,0:T(8,128)S(1)} collective-permute-done((f32[128,128]{1,0:T(8,128)S(1)}, f32[128,128]{1,0:T(8,128)S(1)}, u32[]{:S(2)}, u32[]{:S(2)}) %collective-permute-start.3) | collective-permute-done | bytes 65568 | tf_op jit(solution)/shard_map/ppermute | solution.py:78
  37.5 5.5 %collective-permute-done.4 = f32[128,128]{1,0:T(8,128)S(1)} collective-permute-done((f32[128,128]{1,0:T(8,128)S(1)}, f32[128,128]{1,0:T(8,128)S(1)}, u32[]{:S(2)}, u32[]{:S(2)}) %collective-permute-start.4) | collective-permute-done | bytes 65568 | tf_op jit(solution)/shard_map/ppermute | solution.py:86
  44.0 1.2 %collective-permute-start.13 = (f32[256,128]{1,0:T(8,128)S(1)}, f32[256,128]{1,0:T(8,128)S(1)}, u32[]{:S(2)}, u32[]{:S(2)}) collective-permute-start(f32[256,128]{1,0:T(8,128)S(1)} %pad_maximum_fusion.6), channel_id=1, source_target_pairs={{0,8},{2,10},{4,12},{6,14},{8,0},{10,2},{12,4},{14,6},{16,24},{18,... | collective-permute-start | bytes 393224 | tf_op jit(solution)/shard_map/ppermute | solution.py:90
  45.2 2.2 %collective-permute-done.5 = f32[128,128]{1,0:T(8,128)S(1)} collective-permute-done((f32[128,128]{1,0:T(8,128)S(1)}, f32[128,128]{1,0:T(8,128)S(1)}, u32[]{:S(2)}, u32[]{:S(2)}) %collective-permute-start.5) | collective-permute-done | bytes 65568 | tf_op jit(solution)/shard_map/ppermute | solution.py:90
  47.4 1.2 %collective-permute-start.6 = (f32[256,128]{1,0:T(8,128)S(1)}, f32[256,128]{1,0:T(8,128)S(1)}, u32[]{:S(2)}, u32[]{:S(2)}) collective-permute-start(f32[256,128]{1,0:T(8,128)S(1)} %pad_maximum_fusion.5), channel_id=1, source_target_pairs={{0,4},{2,6},{4,0},{6,2},{8,12},{10,14},{12,8},{14,10},{16,20},{18,... | collective-permute-start | bytes 393224 | tf_op jit(solution)/shard_map/ppermute | solution.py:90
  49.2 3.2 %collective-permute-done.6 = f32[256,128]{1,0:T(8,128)S(1)} collective-permute-done((f32[256,128]{1,0:T(8,128)S(1)}, f32[256,128]{1,0:T(8,128)S(1)}, u32[]{:S(2)}, u32[]{:S(2)}) %collective-permute-start.6) | collective-permute-done | bytes 131104 | tf_op jit(solution)/shard_map/ppermute | solution.py:90
  54.6 1.0 %slice_add_fusion.1 = (f32[1024,128]{1,0:T(8,128)S(1)}, f32[1024,128]{1,0:T(8,128)S(1)}) fusion(f32[1024,256]{1,0:T(8,128)S(1)} %fusion.6, f32[1024,128]{1,0:T(8,128)S(1)} %convolution_bitcast_fusion, f32[64,128]{1,0:T(8,128)S(1)} %fusion.9, f32[1024,64]{0,1:T(8,128)S(1)} %copy-done.3), kind=kOutput, calls=%fused_computation.31 | convolution fusion | flops 100925440 | bytes 2916352 | tf_op jit(solution)/shard_map/dot_general | solution.py:8
  59.2 4.0 %collective-permute-done.23 = f32[256,128]{1,0:T(8,128)S(1)} collective-permute-done((f32[256,128]{1,0:T(8,128)S(1)}, f32[256,128]{1,0:T(8,128)S(1)}, u32[]{:S(2)}, u32[]{:S(2)}) %collective-permute-start.23) | collective-permute-done | bytes 131104 | tf_op jit(solution)/shard_map/ppermute | solution.py:78
  63.3 1.2 %collective-permute-start.24 = (f32[128,128]{1,0:T(8,128)S(1)}, f32[128,128]{1,0:T(8,128)S(1)}, u32[]{:S(2)}, u32[]{:S(2)}) collective-permute-start(f32[128,128]{1,0:T(8,128)S(1)} %constant_dynamic-slice_fusion), channel_id=1, source_target_pairs={{0,4},{2,6},{4,0},{6,2},{8,12},{10,14},{12,8},{14,10},{16,20},{18,... | collective-permute-start | bytes 196616 | tf_op jit(solution)/shard_map/ppermute | solution.py:78
  65.2 2.4 %collective-permute-done.24 = f32[128,128]{1,0:T(8,128)S(1)} collective-permute-done((f32[128,128]{1,0:T(8,128)S(1)}, f32[128,128]{1,0:T(8,128)S(1)}, u32[]{:S(2)}, u32[]{:S(2)}) %collective-permute-start.24) | collective-permute-done | bytes 65568 | tf_op jit(solution)/shard_map/ppermute | solution.py:78
  68.9 1.8 %collective-permute-start.18 = (f32[128,128]{1,0:T(8,128)S(1)}, f32[128,128]{1,0:T(8,128)S(1)}, u32[]{:S(2)}, u32[]{:S(2)}) collective-permute-start(f32[128,128]{1,0:T(8,128)S(1)} %dynamic-slice_add_fusion.9), channel_id=1, source_target_pairs={{0,16},{2,18},{4,20},{6,22},{8,24},{10,26},{12,28},{14,30},{16,0},... | collective-permute-start | bytes 196616 | tf_op jit(solution)/shard_map/ppermute | solution.py:86
  70.7 3.1 %collective-permute-done.25 = f32[128,128]{1,0:T(8,128)S(1)} collective-permute-done((f32[128,128]{1,0:T(8,128)S(1)}, f32[128,128]{1,0:T(8,128)S(1)}, u32[]{:S(2)}, u32[]{:S(2)}) %collective-permute-start.25) | collective-permute-done | bytes 65568 | tf_op jit(solution)/shard_map/ppermute | solution.py:86
  73.8 1.1 %collective-permute-start.26 = (f32[128,128]{1,0:T(8,128)S(1)}, f32[128,128]{1,0:T(8,128)S(1)}, u32[]{:S(2)}, u32[]{:S(2)}) collective-permute-start(f32[128,128]{1,0:T(8,128)S(1)} %add_subtract_fusion), channel_id=1, source_target_pairs={{0,4},{2,6},{4,0},{6,2},{8,12},{10,14},{12,8},{14,10},{16,20},{18,... | collective-permute-start | bytes 196616 | tf_op jit(solution)/shard_map/ppermute | solution.py:90
  75.4 2.8 %collective-permute-done.26 = f32[128,128]{1,0:T(8,128)S(1)} collective-permute-done((f32[128,128]{1,0:T(8,128)S(1)}, f32[128,128]{1,0:T(8,128)S(1)}, u32[]{:S(2)}, u32[]{:S(2)}) %collective-permute-start.26) | collective-permute-done | bytes 65568 | tf_op jit(solution)/shard_map/ppermute | solution.py:90
  78.3 1.5 %collective-permute-done.19 = f32[128,128]{1,0:T(8,128)S(1)} collective-permute-done((f32[128,128]{1,0:T(8,128)S(1)}, f32[128,128]{1,0:T(8,128)S(1)}, u32[]{:S(2)}, u32[]{:S(2)}) %collective-permute-start.19) | collective-permute-done | bytes 65568 | tf_op jit(solution)/shard_map/ppermute | solution.py:90
  80.7 2.5 %collective-permute-done.27 = f32[256,128]{1,0:T(8,128)S(1)} collective-permute-done((f32[256,128]{1,0:T(8,128)S(1)}, f32[256,128]{1,0:T(8,128)S(1)}, u32[]{:S(2)}, u32[]{:S(2)}) %collective-permute-start.27) | collective-permute-done | bytes 131104 | tf_op jit(solution)/shard_map/ppermute | solution.py:90
  83.4 1.5 %collective-permute-done.20 = f32[256,128]{1,0:T(8,128)S(1)} collective-permute-done((f32[256,128]{1,0:T(8,128)S(1)}, f32[256,128]{1,0:T(8,128)S(1)}, u32[]{:S(2)}, u32[]{:S(2)}) %collective-permute-start.20) | collective-permute-done | bytes 131104 | tf_op jit(solution)/shard_map/ppermute | solution.py:90
  85.5 1.0 %collective-permute-done.21 = f32[512,128]{1,0:T(8,128)S(1)} collective-permute-done((f32[512,128]{1,0:T(8,128)S(1)}, f32[512,128]{1,0:T(8,128)S(1)}, u32[]{:S(2)}, u32[]{:S(2)}) %collective-permute-start.21) | collective-permute-done | bytes 262176 | tf_op jit(solution)/shard_map/ppermute | solution.py:90
  (101 shorter events, 14.9 us)
Async XLA Ops:
  6.5 1.4 %copy-start.1 = (f32[1024,128]{1,0:T(8,128)}, f32[1024,128]{1,0:T(8,128)S(1)}, u32[]{:S(2)}) copy-start(f32[1024,128]{1,0:T(8,128)S(1)} %get-tuple-element.25) | copy-start | bytes 1572868
  7.4 2.4 %collective-permute-start.8 = (f32[512,128]{1,0:T(8,128)}, f32[512,128]{1,0:T(8,128)}, u32[]{:S(2)}, u32[]{:S(2)}) collective-permute-start(f32[512,128]{1,0:T(8,128)} %constant_dynamic-slice_fusion.8), channel_id=1, source_target_pairs={{0,2},{2,0},{4,6},{6,4},{8,10},{10,8},{12,14},{14,12},{16,18},{18,... | collective-permute-start | bytes 786440 | tf_op jit(solution)/shard_map/ppermute | solution.py:78
  7.8 6.1 %collective-permute-start = (f32[512,128]{1,0:T(8,128)S(1)}, f32[512,128]{1,0:T(8,128)}, u32[]{:S(2)}, u32[]{:S(2)}) collective-permute-start(f32[512,128]{1,0:T(8,128)S(1)} %constant_dynamic-slice_fusion.11), channel_id=1, source_target_pairs={{0,2},{2,0},{4,6},{6,4},{8,10},{10,8},{12,14},{14,12},{16,18},{18,... | collective-permute-start | bytes 786440 | tf_op jit(solution)/shard_map/ppermute | solution.py:78
  9.7 10.2 %copy-start.4 = (f32[2,64,512]{2,1,0:T(8,128)S(1)}, f32[2,64,512]{2,1,0:T(8,128)}, u32[]{:S(2)}) copy-start(f32[2,64,512]{2,1,0:T(8,128)} %param.8) | copy-start | bytes 786436
  10.9 6.8 %collective-permute-start.9 = (f32[256,128]{1,0:T(8,128)S(1)}, f32[256,128]{1,0:T(8,128)S(1)}, u32[]{:S(2)}, u32[]{:S(2)}) collective-permute-start(f32[256,128]{1,0:T(8,128)S(1)} %constant_dynamic-slice_fusion.7), channel_id=1, source_target_pairs={{0,8},{2,10},{4,12},{6,14},{8,0},{10,2},{12,4},{14,6},{16,24},{18,... | collective-permute-start | bytes 393224 | tf_op jit(solution)/shard_map/ppermute | solution.py:78
  17.7 5.0 %collective-permute-start.10 = (f32[128,128]{1,0:T(8,128)S(1)}, f32[128,128]{1,0:T(8,128)S(1)}, u32[]{:S(2)}, u32[]{:S(2)}) collective-permute-start(f32[128,128]{1,0:T(8,128)S(1)} %constant_dynamic-slice_fusion.6), channel_id=1, source_target_pairs={{0,4},{2,6},{4,0},{6,2},{8,12},{10,14},{12,8},{14,10},{16,20},{18,... | collective-permute-start | bytes 196616 | tf_op jit(solution)/shard_map/ppermute | solution.py:78
  19.5 12.8 %collective-permute-start.1 = (f32[256,128]{1,0:T(8,128)S(1)}, f32[256,128]{1,0:T(8,128)S(1)}, u32[]{:S(2)}, u32[]{:S(2)}) collective-permute-start(f32[256,128]{1,0:T(8,128)S(1)} %constant_dynamic-slice_fusion.10), channel_id=1, source_target_pairs={{0,4},{2,6},{4,0},{6,2},{8,12},{10,14},{12,8},{14,10},{16,20},{18,... | collective-permute-start | bytes 393224 | tf_op jit(solution)/shard_map/ppermute | solution.py:78
  19.9 12.3 %collective-permute-start.2 = (f32[1,1,2,64,512]{4,3,2,1,0:T(8,128)S(1)}, f32[1,1,2,64,512]{4,3,2,1,0:T(8,128)S(1)}, u32[]{:S(2)}, u32[]{:S(2)}) collective-permute-start(f32[1,1,2,64,512]{4,3,2,1,0:T(8,128)S(1)} %bitcast.49), channel_id=1, source_target_pairs={{0,1},{1,0},{2,3},{3,2},{4,5},{5,4},{6,7},{7,6},{8,9},{9,8},{10,11... | collective-permute-start | bytes 786440 | tf_op jit(solution)/shard_map/ppermute | solution.py:34
  22.8 8.1 %collective-permute-start.11 = (f32[128,128]{1,0:T(8,128)S(1)}, f32[128,128]{1,0:T(8,128)S(1)}, u32[]{:S(2)}, u32[]{:S(2)}) collective-permute-start(f32[128,128]{1,0:T(8,128)S(1)} %dynamic-slice_add_fusion.10), channel_id=1, source_target_pairs={{0,16},{2,18},{4,20},{6,22},{8,24},{10,26},{12,28},{14,30},{16,0},... | collective-permute-start | bytes 196616 | tf_op jit(solution)/shard_map/ppermute | solution.py:86
  30.9 6.6 %collective-permute-start.12 = (f32[128,128]{1,0:T(8,128)S(1)}, f32[128,128]{1,0:T(8,128)S(1)}, u32[]{:S(2)}, u32[]{:S(2)}) collective-permute-start(f32[128,128]{1,0:T(8,128)S(1)} %add_subtract_fusion.2), channel_id=1, source_target_pairs={{0,4},{2,6},{4,0},{6,2},{8,12},{10,14},{12,8},{14,10},{16,20},{18,... | collective-permute-start | bytes 196616 | tf_op jit(solution)/shard_map/ppermute | solution.py:90
  32.3 20.8 %copy-start.3 = (f32[1024,64]{0,1:T(8,128)S(1)}, f32[1024,64]{0,1:T(8,128)}, u32[]{:S(2)}) copy-start(f32[1024,64]{0,1:T(8,128)} %param.9) | copy-start | bytes 786436
  32.4 5.0 %collective-permute-start.3 = (f32[128,128]{1,0:T(8,128)S(1)}, f32[128,128]{1,0:T(8,128)S(1)}, u32[]{:S(2)}, u32[]{:S(2)}) collective-permute-start(f32[128,128]{1,0:T(8,128)S(1)} %constant_dynamic-slice_fusion.9), channel_id=1, source_target_pairs={{0,8},{2,10},{4,12},{6,14},{8,0},{10,2},{12,4},{14,6},{16,24},{18,... | collective-permute-start | bytes 196616 | tf_op jit(solution)/shard_map/ppermute | solution.py:78
  37.4 5.6 %collective-permute-start.4 = (f32[128,128]{1,0:T(8,128)S(1)}, f32[128,128]{1,0:T(8,128)S(1)}, u32[]{:S(2)}, u32[]{:S(2)}) collective-permute-start(f32[128,128]{1,0:T(8,128)S(1)} %dynamic-slice_add_fusion.11), channel_id=1, source_target_pairs={{0,16},{2,18},{4,20},{6,22},{8,24},{10,26},{12,28},{14,30},{16,0},... | collective-permute-start | bytes 196616 | tf_op jit(solution)/shard_map/ppermute | solution.py:86
  43.0 4.3 %collective-permute-start.5 = (f32[128,128]{1,0:T(8,128)S(1)}, f32[128,128]{1,0:T(8,128)S(1)}, u32[]{:S(2)}, u32[]{:S(2)}) collective-permute-start(f32[128,128]{1,0:T(8,128)S(1)} %add_subtract_fusion.3), channel_id=1, source_target_pairs={{0,8},{2,10},{4,12},{6,14},{8,0},{10,2},{12,4},{14,6},{16,24},{18,... | collective-permute-start | bytes 196616 | tf_op jit(solution)/shard_map/ppermute | solution.py:90
  44.0 5.0 %collective-permute-start.13 = (f32[256,128]{1,0:T(8,128)S(1)}, f32[256,128]{1,0:T(8,128)S(1)}, u32[]{:S(2)}, u32[]{:S(2)}) collective-permute-start(f32[256,128]{1,0:T(8,128)S(1)} %pad_maximum_fusion.6), channel_id=1, source_target_pairs={{0,8},{2,10},{4,12},{6,14},{8,0},{10,2},{12,4},{14,6},{16,24},{18,... | collective-permute-start | bytes 393224 | tf_op jit(solution)/shard_map/ppermute | solution.py:90
  47.4 5.0 %collective-permute-start.6 = (f32[256,128]{1,0:T(8,128)S(1)}, f32[256,128]{1,0:T(8,128)S(1)}, u32[]{:S(2)}, u32[]{:S(2)}) collective-permute-start(f32[256,128]{1,0:T(8,128)S(1)} %pad_maximum_fusion.5), channel_id=1, source_target_pairs={{0,4},{2,6},{4,0},{6,2},{8,12},{10,14},{12,8},{14,10},{16,20},{18,... | collective-permute-start | bytes 393224 | tf_op jit(solution)/shard_map/ppermute | solution.py:90
  49.1 3.5 %collective-permute-start.14 = (f32[512,128]{1,0:T(8,128)S(1)}, f32[512,128]{1,0:T(8,128)S(1)}, u32[]{:S(2)}, u32[]{:S(2)}) collective-permute-start(f32[512,128]{1,0:T(8,128)S(1)} %pad_maximum_fusion.2), channel_id=1, source_target_pairs={{0,2},{2,0},{4,6},{6,4},{8,10},{10,8},{12,14},{14,12},{16,18},{18,... | collective-permute-start | bytes 786440 | tf_op jit(solution)/shard_map/ppermute | solution.py:90
  52.5 1.6 %collective-permute-start.7 = (f32[512,128]{1,0:T(8,128)S(1)}, f32[512,128]{1,0:T(8,128)S(1)}, u32[]{:S(2)}, u32[]{:S(2)}) collective-permute-start(f32[512,128]{1,0:T(8,128)S(1)} %pad_maximum_fusion.1), channel_id=1, source_target_pairs={{0,2},{2,0},{4,6},{6,4},{8,10},{10,8},{12,14},{14,12},{16,18},{18,... | collective-permute-start | bytes 786440 | tf_op jit(solution)/shard_map/ppermute | solution.py:90
  55.6 1.7 %collective-permute-start.22 = (f32[512,128]{1,0:T(8,128)S(1)}, f32[512,128]{1,0:T(8,128)S(1)}, u32[]{:S(2)}, u32[]{:S(2)}) collective-permute-start(f32[512,128]{1,0:T(8,128)S(1)} %constant_dynamic-slice_fusion.2), channel_id=1, source_target_pairs={{0,2},{2,0},{4,6},{6,4},{8,10},{10,8},{12,14},{14,12},{16,18},{18,... | collective-permute-start | bytes 786440 | tf_op jit(solution)/shard_map/ppermute | solution.py:78
  56.3 2.1 %collective-permute-start.15 = (f32[512,128]{1,0:T(8,128)S(1)}, f32[512,128]{1,0:T(8,128)S(1)}, u32[]{:S(2)}, u32[]{:S(2)}) collective-permute-start(f32[512,128]{1,0:T(8,128)S(1)} %constant_dynamic-slice_fusion.5), channel_id=1, source_target_pairs={{0,2},{2,0},{4,6},{6,4},{8,10},{10,8},{12,14},{14,12},{16,18},{18,... | collective-permute-start | bytes 786440 | tf_op jit(solution)/shard_map/ppermute | solution.py:78
  57.4 5.8 %collective-permute-start.23 = (f32[256,128]{1,0:T(8,128)S(1)}, f32[256,128]{1,0:T(8,128)S(1)}, u32[]{:S(2)}, u32[]{:S(2)}) collective-permute-start(f32[256,128]{1,0:T(8,128)S(1)} %constant_dynamic-slice_fusion.1), channel_id=1, source_target_pairs={{0,8},{2,10},{4,12},{6,14},{8,0},{10,2},{12,4},{14,6},{16,24},{18,... | collective-permute-start | bytes 393224 | tf_op jit(solution)/shard_map/ppermute | solution.py:78
  58.5 6.0 %collective-permute-start.16 = (f32[256,128]{1,0:T(8,128)S(1)}, f32[256,128]{1,0:T(8,128)S(1)}, u32[]{:S(2)}, u32[]{:S(2)}) collective-permute-start(f32[256,128]{1,0:T(8,128)S(1)} %constant_dynamic-slice_fusion.4), channel_id=1, source_target_pairs={{0,4},{2,6},{4,0},{6,2},{8,12},{10,14},{12,8},{14,10},{16,20},{18,... | collective-permute-start | bytes 393224 | tf_op jit(solution)/shard_map/ppermute | solution.py:78
  63.3 4.3 %collective-permute-start.24 = (f32[128,128]{1,0:T(8,128)S(1)}, f32[128,128]{1,0:T(8,128)S(1)}, u32[]{:S(2)}, u32[]{:S(2)}) collective-permute-start(f32[128,128]{1,0:T(8,128)S(1)} %constant_dynamic-slice_fusion), channel_id=1, source_target_pairs={{0,4},{2,6},{4,0},{6,2},{8,12},{10,14},{12,8},{14,10},{16,20},{18,... | collective-permute-start | bytes 196616 | tf_op jit(solution)/shard_map/ppermute | solution.py:78
  64.5 4.3 %collective-permute-start.17 = (f32[128,128]{1,0:T(8,128)S(1)}, f32[128,128]{1,0:T(8,128)S(1)}, u32[]{:S(2)}, u32[]{:S(2)}) collective-permute-start(f32[128,128]{1,0:T(8,128)S(1)} %constant_dynamic-slice_fusion.3), channel_id=1, source_target_pairs={{0,8},{2,10},{4,12},{6,14},{8,0},{10,2},{12,4},{14,6},{16,24},{18,... | collective-permute-start | bytes 196616 | tf_op jit(solution)/shard_map/ppermute | solution.py:78
  67.6 6.2 %collective-permute-start.25 = (f32[128,128]{1,0:T(8,128)S(1)}, f32[128,128]{1,0:T(8,128)S(1)}, u32[]{:S(2)}, u32[]{:S(2)}) collective-permute-start(f32[128,128]{1,0:T(8,128)S(1)} %dynamic-slice_add_fusion.8), channel_id=1, source_target_pairs={{0,16},{2,18},{4,20},{6,22},{8,24},{10,26},{12,28},{14,30},{16,0},... | collective-permute-start | bytes 196616 | tf_op jit(solution)/shard_map/ppermute | solution.py:86
  68.9 6.4 %collective-permute-start.18 = (f32[128,128]{1,0:T(8,128)S(1)}, f32[128,128]{1,0:T(8,128)S(1)}, u32[]{:S(2)}, u32[]{:S(2)}) collective-permute-start(f32[128,128]{1,0:T(8,128)S(1)} %dynamic-slice_add_fusion.9), channel_id=1, source_target_pairs={{0,16},{2,18},{4,20},{6,22},{8,24},{10,26},{12,28},{14,30},{16,0},... | collective-permute-start | bytes 196616 | tf_op jit(solution)/shard_map/ppermute | solution.py:86
  73.8 4.3 %collective-permute-start.26 = (f32[128,128]{1,0:T(8,128)S(1)}, f32[128,128]{1,0:T(8,128)S(1)}, u32[]{:S(2)}, u32[]{:S(2)}) collective-permute-start(f32[128,128]{1,0:T(8,128)S(1)} %add_subtract_fusion), channel_id=1, source_target_pairs={{0,4},{2,6},{4,0},{6,2},{8,12},{10,14},{12,8},{14,10},{16,20},{18,... | collective-permute-start | bytes 196616 | tf_op jit(solution)/shard_map/ppermute | solution.py:90
  75.2 4.6 %collective-permute-start.19 = (f32[128,128]{1,0:T(8,128)S(1)}, f32[128,128]{1,0:T(8,128)S(1)}, u32[]{:S(2)}, u32[]{:S(2)}) collective-permute-start(f32[128,128]{1,0:T(8,128)S(1)} %add_subtract_fusion.1), channel_id=1, source_target_pairs={{0,8},{2,10},{4,12},{6,14},{8,0},{10,2},{12,4},{14,6},{16,24},{18,... | collective-permute-start | bytes 196616 | tf_op jit(solution)/shard_map/ppermute | solution.py:90
  78.2 5.0 %collective-permute-start.27 = (f32[256,128]{1,0:T(8,128)S(1)}, f32[256,128]{1,0:T(8,128)S(1)}, u32[]{:S(2)}, u32[]{:S(2)}) collective-permute-start(f32[256,128]{1,0:T(8,128)S(1)} %pad_maximum_fusion.8), channel_id=1, source_target_pairs={{0,8},{2,10},{4,12},{6,14},{8,0},{10,2},{12,4},{14,6},{16,24},{18,... | collective-permute-start | bytes 393224 | tf_op jit(solution)/shard_map/ppermute | solution.py:90
  79.8 5.0 %collective-permute-start.20 = (f32[256,128]{1,0:T(8,128)S(1)}, f32[256,128]{1,0:T(8,128)S(1)}, u32[]{:S(2)}, u32[]{:S(2)}) collective-permute-start(f32[256,128]{1,0:T(8,128)S(1)} %pad_maximum_fusion.7), channel_id=1, source_target_pairs={{0,4},{2,6},{4,0},{6,2},{8,12},{10,14},{12,8},{14,10},{16,20},{18,... | collective-permute-start | bytes 393224 | tf_op jit(solution)/shard_map/ppermute | solution.py:90
  83.3 1.7 %collective-permute-start.28 = (f32[512,128]{1,0:T(8,128)S(1)}, f32[512,128]{1,0:T(8,128)S(1)}, u32[]{:S(2)}, u32[]{:S(2)}) collective-permute-start(f32[512,128]{1,0:T(8,128)S(1)} %pad_maximum_fusion.4), channel_id=1, source_target_pairs={{0,2},{2,0},{4,6},{6,4},{8,10},{10,8},{12,14},{14,12},{16,18},{18,... | collective-permute-start | bytes 786440 | tf_op jit(solution)/shard_map/ppermute | solution.py:90
  84.9 1.6 %collective-permute-start.21 = (f32[512,128]{1,0:T(8,128)S(1)}, f32[512,128]{1,0:T(8,128)S(1)}, u32[]{:S(2)}, u32[]{:S(2)}) collective-permute-start(f32[512,128]{1,0:T(8,128)S(1)} %pad_maximum_fusion.3), channel_id=1, source_target_pairs={{0,2},{2,0},{4,6},{6,4},{8,10},{10,8},{12,14},{14,12},{16,18},{18,... | collective-permute-start | bytes 786440 | tf_op jit(solution)/shard_map/ppermute | solution.py:90
  (2 other events, 2.6 us)

commit v19 on v12

--- a/solution.py
+++ b/solution.py
@@ -133,10 +133,10 @@
             for chain, (order, cols) in enumerate(zip(orders, columns)):
                 remains, got_riders = ordered_reduce_then_gather(
                     first_sum[:, cols], right_side[0][:, cols], "blk", n, order,
-                    inverse_pieces if chain == 0 else None,
-                    (solved_before, lambda held: product(factor_panel[1], held)) if chain == 0 else None,
+                    inverse_pieces if chain == 1 else None,
+                    (solved_before, lambda held: product(factor_panel[1], held)) if chain == 1 else None,
                 )
-                if chain == 0:
+                if chain == 1:
                     panel_sum, inverse_pieces = got_riders
                 first_blocks.append(remains)
             inverse_full = jnp.concatenate(list(inverse_pieces), axis=2)

time: 76.8 us -> 77.3 us (level)
  waiting for transfers between devices: 33.6 us -> 38.3 us
  starting transfers between devices: 26.3 us -> 22.1 us
    ppermute x12, starting transfers between devices: 6.44 us -> 2.99 us  [ordered_reduce_then_gather(): got = lax.ppermute(y, axis, [(i, i ^ 1 << j) for i in range(n)])]
    ppermute x4, waiting for transfers between devices: 6.99 us -> 9.37 us  [ordered_reduce_then_gather(): y = y + lax.ppermute(y, axis, [(i, i ^ 1 << top) for i in range(n)])]
    ppermute x12, waiting for transfers between devices: 16.4 us -> 18.5 us  [ordered_reduce_then_gather(): got = lax.ppermute(y, axis, [(i, i ^ 1 << j) for i in range(n)])]
  transfers between devices with their start and end apart: 29 -> 29, of which waited for: 21 -> 19; matrix products, arithmetic and copies ran while one was open for 16% -> 16% of each run, Pallas kernels for 0% -> 0%
where the time goes in v19:
time: 77.3 us; the launch traced here: 77.1 us
  waiting for transfers between devices  38.3 us (50%)
  starting transfers between devices  22.1 us (29%)
  matrix products  12.5 us (16%)
  local copies, waits for them, and re-layouts  2.18 us (3%)
  other arithmetic  1.48 us (2%)
    ppermute x12, waiting for transfers between devices, ordered_reduce_then_gather(): got = lax.ppermute(y, axis, [(i, i ^ 1 << j) for i in range(n)])  18.5 us
    dot_general x8, matrix products, product(): jnp.dot(left, right, precision=lax.Precision.HIGHEST, preferred_element_t...  12.5 us
    ppermute x12, waiting for transfers between devices, ordered_reduce_then_gather(): got = lax.ppermute(send, axis, [(i, i ^ 1 << j) for i in range(n)])  10.4 us
    ppermute x12, starting transfers between devices, ordered_reduce_then_gather(): got = lax.ppermute(send, axis, [(i, i ^ 1 << j) for i in range(n)])  9.88 us
    ppermute x4, waiting for transfers between devices, ordered_reduce_then_gather(): y = y + lax.ppermute(y, axis, [(i, i ^ 1 << top) for i in range(n)])  9.37 us
    ppermute x4, starting transfers between devices, ordered_reduce_then_gather(): y = y + lax.ppermute(y, axis, [(i, i ^ 1 << top) for i in range(n)])  6.31 us
    ppermute x12, starting transfers between devices, ordered_reduce_then_gather(): got = lax.ppermute(y, axis, [(i, i ^ 1 << j) for i in range(n)])  2.99 us
    ppermute x1, starting transfers between devices, doubling_gather(): got = lax.ppermute(y, axis, [(i, i ^ 1 << j) for i in range(n)])  2.94 us
  transfers between devices with their start and end apart: 29, of which 19 were waited for; matrix products, arithmetic and copies ran while one was open for 16% of the time, Pallas kernels for 0%

profile of v19, /device:TPU:0, one launch (start us, length us, event | category | flops | bytes accessed | tf_op | source)
XLA Modules:
  0.0 77.1 jit_solution(1598123936119569620)
XLA Ops:
  0.0 2.9 %collective-permute-start = (f32[1,1,2,64,512]{4,3,2,1,0:T(8,128)}, f32[1,1,2,64,512]{4,3,2,1,0:T(8,128)S(1)}, u32[]{:S(2)}, u32[]{:S(2)}) collective-permute-start(f32[1,1,2,64,512]{4,3,2,1,0:T(8,128)} %bitcast.49), channel_id=1, source_target_pairs={{0,1},{1,0},{2,3},{3,2},{4,5},{5,4},{6,7},{7,6},{8,9},{9,8},{10,11... | collective-permute-start | bytes 786440 | tf_op jit(solution)/shard_map/ppermute | solution.py:34
  2.9 5.3 %fusion.2 = f32[1024,256]{1,0:T(8,128)S(1)} fusion(f32[1024,256]{1,0:T(8,128)S(1)} %copy-done, f32[2,1024,1024]{2,1,0:T(8,128)} %param.5), kind=kOutput, calls=%fused_computation.2 | convolution fusion | flops 3221225472 | bytes 6291456 | tf_op jit(solution)/shard_map/dot_general | solution.py:8
  8.2 1.7 %slice_bitcast_fusion = (f32[1024,256]{1,0:T(8,128)S(1)}, f32[1024,256]{1,0:T(8,128)S(1)}) fusion(f32[2,1024,256]{2,1,0:T(8,128)} %param.7), kind=kLoop, calls=%fused_computation.9 | loop fusion | bytes 4194304 | tf_op jit(solution)/shard_map/squeeze | solution.py:147
  10.9 0.9 %collective-permute-done.3 = f32[512,128]{1,0:T(8,128)S(1)} collective-permute-done((f32[512,128]{1,0:T(8,128)S(1)}, f32[512,128]{1,0:T(8,128)S(1)}, u32[]{:S(2)}, u32[]{:S(2)}) %collective-permute-start.3) | collective-permute-done | bytes 262176 | tf_op jit(solution)/shard_map/ppermute | solution.py:78
  11.8 1.6 %collective-permute-start.4 = (f32[256,128]{1,0:T(8,128)S(1)}, f32[256,128]{1,0:T(8,128)S(1)}, u32[]{:S(2)}, u32[]{:S(2)}) collective-permute-start(f32[256,128]{1,0:T(8,128)S(1)} %constant_dynamic-slice_fusion.8), channel_id=1, source_target_pairs={{0,4},{2,6},{4,0},{6,2},{8,12},{10,14},{12,8},{14,10},{16,20},{18,... | collective-permute-start | bytes 393224 | tf_op jit(solution)/shard_map/ppermute | solution.py:78
  13.5 1.6 %collective-permute-start.2 = (f32[256,128]{1,0:T(8,128)S(1)}, f32[256,128]{1,0:T(8,128)S(1)}, u32[]{:S(2)}, u32[]{:S(2)}) collective-permute-start(f32[256,128]{1,0:T(8,128)S(1)} %constant_dynamic-slice_fusion.10), channel_id=1, source_target_pairs={{0,8},{2,10},{4,12},{6,14},{8,0},{10,2},{12,4},{14,6},{16,24},{18,... | collective-permute-start | bytes 393224 | tf_op jit(solution)/shard_map/ppermute | solution.py:78
  15.1 3.5 %fusion.6 = f32[1024,256]{1,0:T(8,128)S(1)} fusion(f32[1024,256]{1,0:T(8,128)S(1)} %copy-done, f32[2,1024,1024]{2,1,0:T(8,128)S(1)} %copy-done.1), kind=kOutput, calls=%fused_computation.6 | convolution fusion | flops 3221225472 | bytes 6291456 | tf_op jit(solution)/shard_map/dot_general | solution.py:8
  19.3 1.5 %collective-permute-start.10 = (f32[128,128]{1,0:T(8,128)S(1)}, f32[128,128]{1,0:T(8,128)S(1)}, u32[]{:S(2)}, u32[]{:S(2)}) collective-permute-start(f32[128,128]{1,0:T(8,128)S(1)} %constant_dynamic-slice_fusion.6), channel_id=1, source_target_pairs={{0,4},{2,6},{4,0},{6,2},{8,12},{10,14},{12,8},{14,10},{16,20},{18,... | collective-permute-start | bytes 196616 | tf_op jit(solution)/shard_map/ppermute | solution.py:78
  20.8 2.2 %collective-permute-done.5 = f32[128,128]{1,0:T(8,128)S(1)} collective-permute-done((f32[128,128]{1,0:T(8,128)S(1)}, f32[128,128]{1,0:T(8,128)S(1)}, u32[]{:S(2)}, u32[]{:S(2)}) %collective-permute-start.5) | collective-permute-done | bytes 65568 | tf_op jit(solution)/shard_map/ppermute | solution.py:78
  23.0 2.9 %collective-permute-start.6 = (f32[128,128]{1,0:T(8,128)S(1)}, f32[128,128]{1,0:T(8,128)S(1)}, u32[]{:S(2)}, u32[]{:S(2)}) collective-permute-start(f32[128,128]{1,0:T(8,128)S(1)} %dynamic-slice_add_fusion.11), channel_id=1, source_target_pairs={{0,16},{2,18},{4,20},{6,22},{8,24},{10,26},{12,28},{14,30},{16,0},... | collective-permute-start | bytes 196616 | tf_op jit(solution)/shard_map/ppermute | solution.py:86
  26.3 3.9 %collective-permute-done.6 = f32[128,128]{1,0:T(8,128)S(1)} collective-permute-done((f32[128,128]{1,0:T(8,128)S(1)}, f32[128,128]{1,0:T(8,128)S(1)}, u32[]{:S(2)}, u32[]{:S(2)}) %collective-permute-start.6) | collective-permute-done | bytes 65568 | tf_op jit(solution)/shard_map/ppermute | solution.py:86
  30.3 1.3 %collective-permute-done.11 = f32[128,128]{1,0:T(8,128)S(1)} collective-permute-done((f32[128,128]{1,0:T(8,128)S(1)}, f32[128,128]{1,0:T(8,128)S(1)}, u32[]{:S(2)}, u32[]{:S(2)}) %collective-permute-start.11) | collective-permute-done | bytes 65568 | tf_op jit(solution)/shard_map/ppermute | solution.py:86
  31.7 2.8 %collective-permute-done.7 = f32[128,128]{1,0:T(8,128)S(1)} collective-permute-done((f32[128,128]{1,0:T(8,128)S(1)}, f32[128,128]{1,0:T(8,128)S(1)}, u32[]{:S(2)}, u32[]{:S(2)}) %collective-permute-start.7) | collective-permute-done | bytes 65568 | tf_op jit(solution)/shard_map/ppermute | solution.py:90
  34.5 0.8 %collective-permute-start.8 = (f32[256,128]{1,0:T(8,128)S(1)}, f32[256,128]{1,0:T(8,128)S(1)}, u32[]{:S(2)}, u32[]{:S(2)}) collective-permute-start(f32[256,128]{1,0:T(8,128)S(1)} %pad_maximum_fusion.5), channel_id=1, source_target_pairs={{0,4},{2,6},{4,0},{6,2},{8,12},{10,14},{12,8},{14,10},{16,20},{18,... | collective-permute-start | bytes 393224 | tf_op jit(solution)/shard_map/ppermute | solution.py:90
  36.7 2.9 %collective-permute-done.8 = f32[256,128]{1,0:T(8,128)S(1)} collective-permute-done((f32[256,128]{1,0:T(8,128)S(1)}, f32[256,128]{1,0:T(8,128)S(1)}, u32[]{:S(2)}, u32[]{:S(2)}) %collective-permute-start.8) | collective-permute-done | bytes 131104 | tf_op jit(solution)/shard_map/ppermute | solution.py:90
  39.7 1.4 %collective-permute-done.13 = f32[256,128]{1,0:T(8,128)S(1)} collective-permute-done((f32[256,128]{1,0:T(8,128)S(1)}, f32[256,128]{1,0:T(8,128)S(1)}, u32[]{:S(2)}, u32[]{:S(2)}) %collective-permute-start.13) | collective-permute-done | bytes 131104 | tf_op jit(solution)/shard_map/ppermute | solution.py:90
  41.7 1.0 %collective-permute-done.14 = f32[512,128]{1,0:T(8,128)S(1)} collective-permute-done((f32[512,128]{1,0:T(8,128)S(1)}, f32[512,128]{1,0:T(8,128)S(1)}, u32[]{:S(2)}, u32[]{:S(2)}) %collective-permute-start.14) | collective-permute-done | bytes 262176 | tf_op jit(solution)/shard_map/ppermute | solution.py:90
  43.3 1.0 %convolution_bitcast_fusion = f32[1024,128]{1,0:T(8,128)S(1)} fusion(f32[64,128]{1,0:T(8,128)S(1)} %fusion.13, f32[1024,64]{0,1:T(8,128)S(1)} %copy-done.2), kind=kOutput, calls=%fused_computation.7 | convolution fusion | flops 100663296 | bytes 819200 | tf_op jit(solution)/shard_map/dot_general | solution.py:8
  44.3 1.0 %slice_add_fusion.1 = (f32[1024,128]{1,0:T(8,128)S(1)}, f32[1024,128]{1,0:T(8,128)S(1)}) fusion(f32[1024,256]{1,0:T(8,128)S(1)} %fusion.6, f32[1024,128]{1,0:T(8,128)S(1)} %convolution_bitcast_fusion, f32[64,128]{1,0:T(8,128)S(1)} %fusion.9, f32[1024,64]{0,1:T(8,128)S(1)} %copy-done.2), kind=kOutput, calls=%fused_computation.31 | convolution fusion | flops 100925440 | bytes 2916352 | tf_op jit(solution)/shard_map/dot_general | solution.py:8
  46.1 0.9 %collective-permute-done.15 = f32[512,128]{1,0:T(8,128)S(1)} collective-permute-done((f32[512,128]{1,0:T(8,128)S(1)}, f32[512,128]{1,0:T(8,128)S(1)}, u32[]{:S(2)}, u32[]{:S(2)}) %collective-permute-start.15) | collective-permute-done | bytes 262176 | tf_op jit(solution)/shard_map/ppermute | solution.py:78
  48.5 4.1 %collective-permute-done.16 = f32[256,128]{1,0:T(8,128)S(1)} collective-permute-done((f32[256,128]{1,0:T(8,128)S(1)}, f32[256,128]{1,0:T(8,128)S(1)}, u32[]{:S(2)}, u32[]{:S(2)}) %collective-permute-start.16) | collective-permute-done | bytes 131104 | tf_op jit(solution)/shard_map/ppermute | solution.py:78
  53.3 1.2 %collective-permute-start.24 = (f32[128,128]{1,0:T(8,128)S(1)}, f32[128,128]{1,0:T(8,128)S(1)}, u32[]{:S(2)}, u32[]{:S(2)}) collective-permute-start(f32[128,128]{1,0:T(8,128)S(1)} %constant_dynamic-slice_fusion), channel_id=1, source_target_pairs={{0,4},{2,6},{4,0},{6,2},{8,12},{10,14},{12,8},{14,10},{16,20},{18,... | collective-permute-start | bytes 196616 | tf_op jit(solution)/shard_map/ppermute | solution.py:78
  54.6 2.4 %collective-permute-done.17 = f32[128,128]{1,0:T(8,128)S(1)} collective-permute-done((f32[128,128]{1,0:T(8,128)S(1)}, f32[128,128]{1,0:T(8,128)S(1)}, u32[]{:S(2)}, u32[]{:S(2)}) %collective-permute-start.17) | collective-permute-done | bytes 65568 | tf_op jit(solution)/shard_map/ppermute | solution.py:78
  57.0 1.0 %collective-permute-start.18 = (f32[128,128]{1,0:T(8,128)S(1)}, f32[128,128]{1,0:T(8,128)S(1)}, u32[]{:S(2)}, u32[]{:S(2)}) collective-permute-start(f32[128,128]{1,0:T(8,128)S(1)} %dynamic-slice_add_fusion.9), channel_id=1, source_target_pairs={{0,16},{2,18},{4,20},{6,22},{8,24},{10,26},{12,28},{14,30},{16,0},... | collective-permute-start | bytes 196616 | tf_op jit(solution)/shard_map/ppermute | solution.py:86
  58.0 2.1 %collective-permute-start.25 = (f32[128,128]{1,0:T(8,128)S(1)}, f32[128,128]{1,0:T(8,128)S(1)}, u32[]{:S(2)}, u32[]{:S(2)}) collective-permute-start(f32[128,128]{1,0:T(8,128)S(1)} %dynamic-slice_add_fusion.8), channel_id=1, source_target_pairs={{0,16},{2,18},{4,20},{6,22},{8,24},{10,26},{12,28},{14,30},{16,0},... | collective-permute-start | bytes 196616 | tf_op jit(solution)/shard_map/ppermute | solution.py:86
  60.0 2.9 %collective-permute-done.18 = f32[128,128]{1,0:T(8,128)S(1)} collective-permute-done((f32[128,128]{1,0:T(8,128)S(1)}, f32[128,128]{1,0:T(8,128)S(1)}, u32[]{:S(2)}, u32[]{:S(2)}) %collective-permute-start.18) | collective-permute-done | bytes 65568 | tf_op jit(solution)/shard_map/ppermute | solution.py:86
  63.0 1.3 %collective-permute-done.25 = f32[128,128]{1,0:T(8,128)S(1)} collective-permute-done((f32[128,128]{1,0:T(8,128)S(1)}, f32[128,128]{1,0:T(8,128)S(1)}, u32[]{:S(2)}, u32[]{:S(2)}) %collective-permute-start.25) | collective-permute-done | bytes 65568 | tf_op jit(solution)/shard_map/ppermute | solution.py:86
  64.4 2.9 %collective-permute-done.19 = f32[128,128]{1,0:T(8,128)S(1)} collective-permute-done((f32[128,128]{1,0:T(8,128)S(1)}, f32[128,128]{1,0:T(8,128)S(1)}, u32[]{:S(2)}, u32[]{:S(2)}) %collective-permute-start.19) | collective-permute-done | bytes 65568 | tf_op jit(solution)/shard_map/ppermute | solution.py:90
  68.0 1.2 %collective-permute-done.26 = f32[128,128]{1,0:T(8,128)S(1)} collective-permute-done((f32[128,128]{1,0:T(8,128)S(1)}, f32[128,128]{1,0:T(8,128)S(1)}, u32[]{:S(2)}, u32[]{:S(2)}) %collective-permute-start.26) | collective-permute-done | bytes 65568 | tf_op jit(solution)/shard_map/ppermute | solution.py:90
  69.5 2.9 %collective-permute-done.20 = f32[256,128]{1,0:T(8,128)S(1)} collective-permute-done((f32[256,128]{1,0:T(8,128)S(1)}, f32[256,128]{1,0:T(8,128)S(1)}, u32[]{:S(2)}, u32[]{:S(2)}) %collective-permute-start.20) | collective-permute-done | bytes 131104 | tf_op jit(solution)/shard_map/ppermute | solution.py:90
  72.5 1.7 %collective-permute-done.27 = f32[256,128]{1,0:T(8,128)S(1)} collective-permute-done((f32[256,128]{1,0:T(8,128)S(1)}, f32[256,128]{1,0:T(8,128)S(1)}, u32[]{:S(2)}, u32[]{:S(2)}) %collective-permute-start.27) | collective-permute-done | bytes 131104 | tf_op jit(solution)/shard_map/ppermute | solution.py:90
  74.9 1.0 %collective-permute-done.28 = f32[512,128]{1,0:T(8,128)S(1)} collective-permute-done((f32[512,128]{1,0:T(8,128)S(1)}, f32[512,128]{1,0:T(8,128)S(1)}, u32[]{:S(2)}, u32[]{:S(2)}) %collective-permute-start.28) | collective-permute-done | bytes 262176 | tf_op jit(solution)/shard_map/ppermute | solution.py:90
  (99 shorter events, 10.9 us)
Async XLA Ops:
  0.0 9.9 %collective-permute-start = (f32[1,1,2,64,512]{4,3,2,1,0:T(8,128)}, f32[1,1,2,64,512]{4,3,2,1,0:T(8,128)S(1)}, u32[]{:S(2)}, u32[]{:S(2)}) collective-permute-start(f32[1,1,2,64,512]{4,3,2,1,0:T(8,128)} %bitcast.49), channel_id=1, source_target_pairs={{0,1},{1,0},{2,3},{3,2},{4,5},{5,4},{6,7},{7,6},{8,9},{9,8},{10,11... | collective-permute-start | bytes 786440 | tf_op jit(solution)/shard_map/ppermute | solution.py:34
  2.9 7.0 %copy-start.3 = (f32[2,64,512]{2,1,0:T(8,128)S(1)}, f32[2,64,512]{2,1,0:T(8,128)}, u32[]{:S(2)}) copy-start(f32[2,64,512]{2,1,0:T(8,128)} %param.8) | copy-start | bytes 786436
  10.0 5.1 %copy-start.1 = (f32[2,1024,1024]{2,1,0:T(8,128)S(1)}, f32[2,1024,1024]{2,1,0:T(8,128)}, u32[]{:S(2)}) copy-start(f32[2,1024,1024]{2,1,0:T(8,128)} %param.5) | copy-start | bytes 25165828
  10.2 1.6 %collective-permute-start.3 = (f32[512,128]{1,0:T(8,128)S(1)}, f32[512,128]{1,0:T(8,128)S(1)}, u32[]{:S(2)}, u32[]{:S(2)}) collective-permute-start(f32[512,128]{1,0:T(8,128)S(1)} %constant_dynamic-slice_fusion.9), channel_id=1, source_target_pairs={{0,2},{2,0},{4,6},{6,4},{8,10},{10,8},{12,14},{14,12},{16,18},{18,... | collective-permute-start | bytes 786440 | tf_op jit(solution)/shard_map/ppermute | solution.py:78
  10.4 3.1 %collective-permute-start.1 = (f32[512,128]{1,0:T(8,128)S(1)}, f32[512,128]{1,0:T(8,128)S(1)}, u32[]{:S(2)}, u32[]{:S(2)}) collective-permute-start(f32[512,128]{1,0:T(8,128)S(1)} %constant_dynamic-slice_fusion.11), channel_id=1, source_target_pairs={{0,2},{2,0},{4,6},{6,4},{8,10},{10,8},{12,14},{14,12},{16,18},{18,... | collective-permute-start | bytes 786440 | tf_op jit(solution)/shard_map/ppermute | solution.py:78
  11.8 6.8 %collective-permute-start.4 = (f32[256,128]{1,0:T(8,128)S(1)}, f32[256,128]{1,0:T(8,128)S(1)}, u32[]{:S(2)}, u32[]{:S(2)}) collective-permute-start(f32[256,128]{1,0:T(8,128)S(1)} %constant_dynamic-slice_fusion.8), channel_id=1, source_target_pairs={{0,4},{2,6},{4,0},{6,2},{8,12},{10,14},{12,8},{14,10},{16,20},{18,... | collective-permute-start | bytes 393224 | tf_op jit(solution)/shard_map/ppermute | solution.py:78
  13.5 5.7 %collective-permute-start.2 = (f32[256,128]{1,0:T(8,128)S(1)}, f32[256,128]{1,0:T(8,128)S(1)}, u32[]{:S(2)}, u32[]{:S(2)}) collective-permute-start(f32[256,128]{1,0:T(8,128)S(1)} %constant_dynamic-slice_fusion.10), channel_id=1, source_target_pairs={{0,8},{2,10},{4,12},{6,14},{8,0},{10,2},{12,4},{14,6},{16,24},{18,... | collective-permute-start | bytes 393224 | tf_op jit(solution)/shard_map/ppermute | solution.py:78
  18.6 4.3 %collective-permute-start.5 = (f32[128,128]{1,0:T(8,128)S(1)}, f32[128,128]{1,0:T(8,128)S(1)}, u32[]{:S(2)}, u32[]{:S(2)}) collective-permute-start(f32[128,128]{1,0:T(8,128)S(1)} %constant_dynamic-slice_fusion.7), channel_id=1, source_target_pairs={{0,8},{2,10},{4,12},{6,14},{8,0},{10,2},{12,4},{14,6},{16,24},{18,... | collective-permute-start | bytes 196616 | tf_op jit(solution)/shard_map/ppermute | solution.py:78
  19.3 24.0 %copy-start.2 = (f32[1024,64]{0,1:T(8,128)S(1)}, f32[1024,64]{0,1:T(8,128)}, u32[]{:S(2)}) copy-start(f32[1024,64]{0,1:T(8,128)} %param.9) | copy-start | bytes 786436
  19.3 6.6 %collective-permute-start.10 = (f32[128,128]{1,0:T(8,128)S(1)}, f32[128,128]{1,0:T(8,128)S(1)}, u32[]{:S(2)}, u32[]{:S(2)}) collective-permute-start(f32[128,128]{1,0:T(8,128)S(1)} %constant_dynamic-slice_fusion.6), channel_id=1, source_target_pairs={{0,4},{2,6},{4,0},{6,2},{8,12},{10,14},{12,8},{14,10},{16,20},{18,... | collective-permute-start | bytes 196616 | tf_op jit(solution)/shard_map/ppermute | solution.py:78
  23.0 7.2 %collective-permute-start.6 = (f32[128,128]{1,0:T(8,128)S(1)}, f32[128,128]{1,0:T(8,128)S(1)}, u32[]{:S(2)}, u32[]{:S(2)}) collective-permute-start(f32[128,128]{1,0:T(8,128)S(1)} %dynamic-slice_add_fusion.11), channel_id=1, source_target_pairs={{0,16},{2,18},{4,20},{6,22},{8,24},{10,26},{12,28},{14,30},{16,0},... | collective-permute-start | bytes 196616 | tf_op jit(solution)/shard_map/ppermute | solution.py:86
  25.9 5.7 %collective-permute-start.11 = (f32[128,128]{1,0:T(8,128)S(1)}, f32[128,128]{1,0:T(8,128)S(1)}, u32[]{:S(2)}, u32[]{:S(2)}) collective-permute-start(f32[128,128]{1,0:T(8,128)S(1)} %dynamic-slice_add_fusion.10), channel_id=1, source_target_pairs={{0,16},{2,18},{4,20},{6,22},{8,24},{10,26},{12,28},{14,30},{16,0},... | collective-permute-start | bytes 196616 | tf_op jit(solution)/shard_map/ppermute | solution.py:86
  30.2 4.3 %collective-permute-start.7 = (f32[128,128]{1,0:T(8,128)S(1)}, f32[128,128]{1,0:T(8,128)S(1)}, u32[]{:S(2)}, u32[]{:S(2)}) collective-permute-start(f32[128,128]{1,0:T(8,128)S(1)} %add_subtract_fusion.3), channel_id=1, source_target_pairs={{0,8},{2,10},{4,12},{6,14},{8,0},{10,2},{12,4},{14,6},{16,24},{18,... | collective-permute-start | bytes 196616 | tf_op jit(solution)/shard_map/ppermute | solution.py:90
  31.6 4.4 %collective-permute-start.12 = (f32[128,128]{1,0:T(8,128)S(1)}, f32[128,128]{1,0:T(8,128)S(1)}, u32[]{:S(2)}, u32[]{:S(2)}) collective-permute-start(f32[128,128]{1,0:T(8,128)S(1)} %add_subtract_fusion.2), channel_id=1, source_target_pairs={{0,4},{2,6},{4,0},{6,2},{8,12},{10,14},{12,8},{14,10},{16,20},{18,... | collective-permute-start | bytes 196616 | tf_op jit(solution)/shard_map/ppermute | solution.py:90
  34.5 5.0 %collective-permute-start.8 = (f32[256,128]{1,0:T(8,128)S(1)}, f32[256,128]{1,0:T(8,128)S(1)}, u32[]{:S(2)}, u32[]{:S(2)}) collective-permute-start(f32[256,128]{1,0:T(8,128)S(1)} %pad_maximum_fusion.5), channel_id=1, source_target_pairs={{0,4},{2,6},{4,0},{6,2},{8,12},{10,14},{12,8},{14,10},{16,20},{18,... | collective-permute-start | bytes 393224 | tf_op jit(solution)/shard_map/ppermute | solution.py:90
  36.1 5.0 %collective-permute-start.13 = (f32[256,128]{1,0:T(8,128)S(1)}, f32[256,128]{1,0:T(8,128)S(1)}, u32[]{:S(2)}, u32[]{:S(2)}) collective-permute-start(f32[256,128]{1,0:T(8,128)S(1)} %pad_maximum_fusion.6), channel_id=1, source_target_pairs={{0,8},{2,10},{4,12},{6,14},{8,0},{10,2},{12,4},{14,6},{16,24},{18,... | collective-permute-start | bytes 393224 | tf_op jit(solution)/shard_map/ppermute | solution.py:90
  39.6 1.6 %collective-permute-start.9 = (f32[512,128]{1,0:T(8,128)S(1)}, f32[512,128]{1,0:T(8,128)S(1)}, u32[]{:S(2)}, u32[]{:S(2)}) collective-permute-start(f32[512,128]{1,0:T(8,128)S(1)} %pad_maximum_fusion.1), channel_id=1, source_target_pairs={{0,2},{2,0},{4,6},{6,4},{8,10},{10,8},{12,14},{14,12},{16,18},{18,... | collective-permute-start | bytes 786440 | tf_op jit(solution)/shard_map/ppermute | solution.py:90
  41.2 1.6 %collective-permute-start.14 = (f32[512,128]{1,0:T(8,128)S(1)}, f32[512,128]{1,0:T(8,128)S(1)}, u32[]{:S(2)}, u32[]{:S(2)}) collective-permute-start(f32[512,128]{1,0:T(8,128)S(1)} %pad_maximum_fusion.2), channel_id=1, source_target_pairs={{0,2},{2,0},{4,6},{6,4},{8,10},{10,8},{12,14},{14,12},{16,18},{18,... | collective-permute-start | bytes 786440 | tf_op jit(solution)/shard_map/ppermute | solution.py:90
  45.3 1.6 %collective-permute-start.15 = (f32[512,128]{1,0:T(8,128)S(1)}, f32[512,128]{1,0:T(8,128)S(1)}, u32[]{:S(2)}, u32[]{:S(2)}) collective-permute-start(f32[512,128]{1,0:T(8,128)S(1)} %constant_dynamic-slice_fusion.5), channel_id=1, source_target_pairs={{0,2},{2,0},{4,6},{6,4},{8,10},{10,8},{12,14},{14,12},{16,18},{18,... | collective-permute-start | bytes 786440 | tf_op jit(solution)/shard_map/ppermute | solution.py:78
  45.6 2.0 %collective-permute-start.22 = (f32[512,128]{1,0:T(8,128)S(1)}, f32[512,128]{1,0:T(8,128)S(1)}, u32[]{:S(2)}, u32[]{:S(2)}) collective-permute-start(f32[512,128]{1,0:T(8,128)S(1)} %constant_dynamic-slice_fusion.2), channel_id=1, source_target_pairs={{0,2},{2,0},{4,6},{6,4},{8,10},{10,8},{12,14},{14,12},{16,18},{18,... | collective-permute-start | bytes 786440 | tf_op jit(solution)/shard_map/ppermute | solution.py:78
  47.0 5.6 %collective-permute-start.16 = (f32[256,128]{1,0:T(8,128)S(1)}, f32[256,128]{1,0:T(8,128)S(1)}, u32[]{:S(2)}, u32[]{:S(2)}) collective-permute-start(f32[256,128]{1,0:T(8,128)S(1)} %constant_dynamic-slice_fusion.4), channel_id=1, source_target_pairs={{0,4},{2,6},{4,0},{6,2},{8,12},{10,14},{12,8},{14,10},{16,20},{18,... | collective-permute-start | bytes 393224 | tf_op jit(solution)/shard_map/ppermute | solution.py:78
  47.7 5.6 %collective-permute-start.23 = (f32[256,128]{1,0:T(8,128)S(1)}, f32[256,128]{1,0:T(8,128)S(1)}, u32[]{:S(2)}, u32[]{:S(2)}) collective-permute-start(f32[256,128]{1,0:T(8,128)S(1)} %constant_dynamic-slice_fusion.1), channel_id=1, source_target_pairs={{0,8},{2,10},{4,12},{6,14},{8,0},{10,2},{12,4},{14,6},{16,24},{18,... | collective-permute-start | bytes 393224 | tf_op jit(solution)/shard_map/ppermute | solution.py:78
  52.6 4.3 %collective-permute-start.17 = (f32[128,128]{1,0:T(8,128)S(1)}, f32[128,128]{1,0:T(8,128)S(1)}, u32[]{:S(2)}, u32[]{:S(2)}) collective-permute-start(f32[128,128]{1,0:T(8,128)S(1)} %constant_dynamic-slice_fusion.3), channel_id=1, source_target_pairs={{0,8},{2,10},{4,12},{6,14},{8,0},{10,2},{12,4},{14,6},{16,24},{18,... | collective-permute-start | bytes 196616 | tf_op jit(solution)/shard_map/ppermute | solution.py:78
  53.3 4.6 %collective-permute-start.24 = (f32[128,128]{1,0:T(8,128)S(1)}, f32[128,128]{1,0:T(8,128)S(1)}, u32[]{:S(2)}, u32[]{:S(2)}) collective-permute-start(f32[128,128]{1,0:T(8,128)S(1)} %constant_dynamic-slice_fusion), channel_id=1, source_target_pairs={{0,4},{2,6},{4,0},{6,2},{8,12},{10,14},{12,8},{14,10},{16,20},{18,... | collective-permute-start | bytes 196616 | tf_op jit(solution)/shard_map/ppermute | solution.py:78
  57.0 6.0 %collective-permute-start.18 = (f32[128,128]{1,0:T(8,128)S(1)}, f32[128,128]{1,0:T(8,128)S(1)}, u32[]{:S(2)}, u32[]{:S(2)}) collective-permute-start(f32[128,128]{1,0:T(8,128)S(1)} %dynamic-slice_add_fusion.9), channel_id=1, source_target_pairs={{0,16},{2,18},{4,20},{6,22},{8,24},{10,26},{12,28},{14,30},{16,0},... | collective-permute-start | bytes 196616 | tf_op jit(solution)/shard_map/ppermute | solution.py:86
  58.0 6.3 %collective-permute-start.25 = (f32[128,128]{1,0:T(8,128)S(1)}, f32[128,128]{1,0:T(8,128)S(1)}, u32[]{:S(2)}, u32[]{:S(2)}) collective-permute-start(f32[128,128]{1,0:T(8,128)S(1)} %dynamic-slice_add_fusion.8), channel_id=1, source_target_pairs={{0,16},{2,18},{4,20},{6,22},{8,24},{10,26},{12,28},{14,30},{16,0},... | collective-permute-start | bytes 196616 | tf_op jit(solution)/shard_map/ppermute | solution.py:86
  63.0 4.4 %collective-permute-start.19 = (f32[128,128]{1,0:T(8,128)S(1)}, f32[128,128]{1,0:T(8,128)S(1)}, u32[]{:S(2)}, u32[]{:S(2)}) collective-permute-start(f32[128,128]{1,0:T(8,128)S(1)} %add_subtract_fusion.1), channel_id=1, source_target_pairs={{0,8},{2,10},{4,12},{6,14},{8,0},{10,2},{12,4},{14,6},{16,24},{18,... | collective-permute-start | bytes 196616 | tf_op jit(solution)/shard_map/ppermute | solution.py:90
  64.3 4.9 %collective-permute-start.26 = (f32[128,128]{1,0:T(8,128)S(1)}, f32[128,128]{1,0:T(8,128)S(1)}, u32[]{:S(2)}, u32[]{:S(2)}) collective-permute-start(f32[128,128]{1,0:T(8,128)S(1)} %add_subtract_fusion), channel_id=1, source_target_pairs={{0,4},{2,6},{4,0},{6,2},{8,12},{10,14},{12,8},{14,10},{16,20},{18,... | collective-permute-start | bytes 196616 | tf_op jit(solution)/shard_map/ppermute | solution.py:90
  67.4 5.0 %collective-permute-start.20 = (f32[256,128]{1,0:T(8,128)S(1)}, f32[256,128]{1,0:T(8,128)S(1)}, u32[]{:S(2)}, u32[]{:S(2)}) collective-permute-start(f32[256,128]{1,0:T(8,128)S(1)} %pad_maximum_fusion.7), channel_id=1, source_target_pairs={{0,4},{2,6},{4,0},{6,2},{8,12},{10,14},{12,8},{14,10},{16,20},{18,... | collective-permute-start | bytes 393224 | tf_op jit(solution)/shard_map/ppermute | solution.py:90
  69.2 5.0 %collective-permute-start.27 = (f32[256,128]{1,0:T(8,128)S(1)}, f32[256,128]{1,0:T(8,128)S(1)}, u32[]{:S(2)}, u32[]{:S(2)}) collective-permute-start(f32[256,128]{1,0:T(8,128)S(1)} %pad_maximum_fusion.8), channel_id=1, source_target_pairs={{0,8},{2,10},{4,12},{6,14},{8,0},{10,2},{12,4},{14,6},{16,24},{18,... | collective-permute-start | bytes 393224 | tf_op jit(solution)/shard_map/ppermute | solution.py:90
  72.5 1.9 %collective-permute-start.21 = (f32[512,128]{1,0:T(8,128)S(1)}, f32[512,128]{1,0:T(8,128)S(1)}, u32[]{:S(2)}, u32[]{:S(2)}) collective-permute-start(f32[512,128]{1,0:T(8,128)S(1)} %pad_maximum_fusion.3), channel_id=1, source_target_pairs={{0,2},{2,0},{4,6},{6,4},{8,10},{10,8},{12,14},{14,12},{16,18},{18,... | collective-permute-start | bytes 786440 | tf_op jit(solution)/shard_map/ppermute | solution.py:90
  74.3 1.6 %collective-permute-start.28 = (f32[512,128]{1,0:T(8,128)S(1)}, f32[512,128]{1,0:T(8,128)S(1)}, u32[]{:S(2)}, u32[]{:S(2)}) collective-permute-start(f32[512,128]{1,0:T(8,128)S(1)} %pad_maximum_fusion.4), channel_id=1, source_target_pairs={{0,2},{2,0},{4,6},{6,4},{8,10},{10,8},{12,14},{14,12},{16,18},{18,... | collective-permute-start | bytes 786440 | tf_op jit(solution)/shard_map/ppermute | solution.py:90
  (1 other events, 2.9 us)

commit v20 on v12

--- a/solution.py
+++ b/solution.py
@@ -129,12 +129,16 @@
             orders = (list(range(k)), [0, 2, 1] + list(range(3, k)) if k >= 3 else list(range(k)))
             width = first_sum.shape[1] // 2
             columns = (slice(0, width), slice(width, 2 * width))
+
+            def column_halves(matrix):
+                return tuple(matrix[:, cols] for cols in columns)
+
             first_blocks = []
             for chain, (order, cols) in enumerate(zip(orders, columns)):
                 remains, got_riders = ordered_reduce_then_gather(
                     first_sum[:, cols], right_side[0][:, cols], "blk", n, order,
                     inverse_pieces if chain == 0 else None,
-                    (solved_before, lambda held: product(factor_panel[1], held)) if chain == 0 else None,
+                    (solved_before, lambda held: column_halves(product(factor_panel[1], held))) if chain == 0 else None,
                 )
                 if chain == 0:
                     panel_sum, inverse_pieces = got_riders
@@ -142,9 +146,9 @@
             inverse_full = jnp.concatenate(list(inverse_pieces), axis=2)
             first_blocks = [product(inverse_full[0], remains) for remains in first_blocks]
             second_blocks = []
-            for order, cols, block in zip(orders, columns, first_blocks):
+            for chain, (order, cols, block) in enumerate(zip(orders, columns, first_blocks)):
                 remains, _ = ordered_reduce_then_gather(
-                    panel_sum[:, cols] + product(coupling, block), right_side[1][:, cols], "blk", n, order
+                    panel_sum[chain] + product(coupling, block), right_side[1][:, cols], "blk", n, order
                 )
                 second_blocks.append(product(inverse_full[1], remains))
             first_block = jnp.concatenate(first_blocks, 1)

time: 76.8 us -> 76 us (0.990)
  waiting for transfers between devices: 33.6 us -> 30.6 us
  starting transfers between devices: 26.3 us -> 28.3 us
    ppermute x12, waiting for transfers between devices: 10.3 us -> 8.08 us  [ordered_reduce_then_gather(): got = lax.ppermute(send, axis, [(i, i ^ 1 << j) for i in range(n)])]
    ppermute x12, waiting for transfers between devices: 16.4 us -> 15.2 us  [ordered_reduce_then_gather(): got = lax.ppermute(y, axis, [(i, i ^ 1 << j) for i in range(n)])]
    ppermute x12, starting transfers between devices: 10.3 us -> 11.5 us  [ordered_reduce_then_gather(): got = lax.ppermute(send, axis, [(i, i ^ 1 << j) for i in range(n)])]
  transfers between devices with their start and end apart: 29 -> 29, of which waited for: 21 -> 20; matrix products, arithmetic and copies ran while one was open for 16% -> 20% of each run, Pallas kernels for 0% -> 0%
where the time goes in v20:
time: 76 us; the launch traced here: 75.8 us
  waiting for transfers between devices  30.6 us (40%)
  starting transfers between devices  28.3 us (37%)
  matrix products  12.6 us (17%)
  local copies, waits for them, and re-layouts  2.26 us (3%)
  other arithmetic  1.56 us (2%)
    ppermute x12, waiting for transfers between devices, ordered_reduce_then_gather(): got = lax.ppermute(y, axis, [(i, i ^ 1 << j) for i in range(n)])  15.2 us
    dot_general x8, matrix products, product(): jnp.dot(left, right, precision=lax.Precision.HIGHEST, preferred_element_t...  12.6 us
    ppermute x12, starting transfers between devices, ordered_reduce_then_gather(): got = lax.ppermute(send, axis, [(i, i ^ 1 << j) for i in range(n)])  11.5 us
    ppermute x12, waiting for transfers between devices, ordered_reduce_then_gather(): got = lax.ppermute(send, axis, [(i, i ^ 1 << j) for i in range(n)])  8.08 us
    ppermute x4, waiting for transfers between devices, ordered_reduce_then_gather(): y = y + lax.ppermute(y, axis, [(i, i ^ 1 << top) for i in range(n)])  7.31 us
    ppermute x4, starting transfers between devices, ordered_reduce_then_gather(): y = y + lax.ppermute(y, axis, [(i, i ^ 1 << top) for i in range(n)])  7.05 us
    ppermute x12, starting transfers between devices, ordered_reduce_then_gather(): got = lax.ppermute(y, axis, [(i, i ^ 1 << j) for i in range(n)])  6.85 us
    ppermute x1, starting transfers between devices, doubling_gather(): got = lax.ppermute(y, axis, [(i, i ^ 1 << j) for i in range(n)])  2.94 us
  transfers between devices with their start and end apart: 29, of which 20 were waited for; matrix products, arithmetic and copies ran while one was open for 20% of the time, Pallas kernels for 0%

profile of v20, /device:TPU:0, one launch (start us, length us, event | category | flops | bytes accessed | tf_op | source)
XLA Modules:
  0.0 75.8 jit_solution(2546138267780696671)
XLA Ops:
  0.0 2.9 %collective-permute-start = (f32[1,1,2,64,512]{4,3,2,1,0:T(8,128)}, f32[1,1,2,64,512]{4,3,2,1,0:T(8,128)S(1)}, u32[]{:S(2)}, u32[]{:S(2)}) collective-permute-start(f32[1,1,2,64,512]{4,3,2,1,0:T(8,128)} %bitcast.51), channel_id=1, source_target_pairs={{0,1},{1,0},{2,3},{3,2},{4,5},{5,4},{6,7},{7,6},{8,9},{9,8},{10,11... | collective-permute-start | bytes 786440 | tf_op jit(solution)/shard_map/ppermute | solution.py:34
  2.9 1.7 %slice_bitcast_fusion = (f32[1024,256]{1,0:T(8,128)S(1)}, f32[1024,256]{1,0:T(8,128)S(1)}) fusion(f32[2,1024,256]{2,1,0:T(8,128)} %param.7), kind=kLoop, calls=%fused_computation.9 | loop fusion | bytes 4194304 | tf_op jit(solution)/shard_map/squeeze | solution.py:151
  4.7 5.4 %fusion.2 = f32[1024,256]{1,0:T(8,128)S(1)} fusion(f32[1024,256]{1,0:T(8,128)S(1)} %copy-done, f32[2,1024,1024]{2,1,0:T(8,128)} %param.5), kind=kOutput, calls=%fused_computation.2 | convolution fusion | flops 3221225472 | bytes 6291456 | tf_op jit(solution)/shard_map/dot_general | solution.py:8
  12.0 1.6 %collective-permute-start.2 = (f32[256,128]{1,0:T(8,128)S(1)}, f32[256,128]{1,0:T(8,128)S(1)}, u32[]{:S(2)}, u32[]{:S(2)}) collective-permute-start(f32[256,128]{1,0:T(8,128)S(1)} %constant_dynamic-slice_fusion.10), channel_id=1, source_target_pairs={{0,4},{2,6},{4,0},{6,2},{8,12},{10,14},{12,8},{14,10},{16,20},{18,... | collective-permute-start | bytes 393224 | tf_op jit(solution)/shard_map/ppermute | solution.py:78
  13.7 1.6 %collective-permute-start.9 = (f32[256,128]{1,0:T(8,128)S(1)}, f32[256,128]{1,0:T(8,128)S(1)}, u32[]{:S(2)}, u32[]{:S(2)}) collective-permute-start(f32[256,128]{1,0:T(8,128)S(1)} %constant_dynamic-slice_fusion.7), channel_id=1, source_target_pairs={{0,8},{2,10},{4,12},{6,14},{8,0},{10,2},{12,4},{14,6},{16,24},{18,... | collective-permute-start | bytes 393224 | tf_op jit(solution)/shard_map/ppermute | solution.py:78
  15.3 3.5 %fusion.6 = f32[1024,256]{1,0:T(8,128)S(1)} fusion(f32[1024,256]{1,0:T(8,128)S(1)} %copy-done, f32[2,1024,1024]{2,1,0:T(8,128)S(1)} %bitcast.50), kind=kOutput, calls=%fused_computation.6 | convolution fusion | flops 3221225472 | bytes 6291456 | tf_op jit(solution)/shard_map/dot_general | solution.py:8
  19.9 1.6 %collective-permute-start.3 = (f32[128,128]{1,0:T(8,128)S(1)}, f32[128,128]{1,0:T(8,128)S(1)}, u32[]{:S(2)}, u32[]{:S(2)}) collective-permute-start(f32[128,128]{1,0:T(8,128)S(1)} %constant_dynamic-slice_fusion.9), channel_id=1, source_target_pairs={{0,8},{2,10},{4,12},{6,14},{8,0},{10,2},{12,4},{14,6},{16,24},{18,... | collective-permute-start | bytes 196616 | tf_op jit(solution)/shard_map/ppermute | solution.py:78
  21.6 1.8 %collective-permute-done.10 = f32[128,128]{1,0:T(8,128)S(1)} collective-permute-done((f32[128,128]{1,0:T(8,128)S(1)}, f32[128,128]{1,0:T(8,128)S(1)}, u32[]{:S(2)}, u32[]{:S(2)}) %collective-permute-start.10) | collective-permute-done | bytes 65568 | tf_op jit(solution)/shard_map/ppermute | solution.py:78
  23.4 2.7 %collective-permute-start.11 = (f32[128,128]{1,0:T(8,128)S(1)}, f32[128,128]{1,0:T(8,128)S(1)}, u32[]{:S(2)}, u32[]{:S(2)}) collective-permute-start(f32[128,128]{1,0:T(8,128)S(1)} %dynamic-slice_add_fusion.10), channel_id=1, source_target_pairs={{0,16},{2,18},{4,20},{6,22},{8,24},{10,26},{12,28},{14,30},{16,0},... | collective-permute-start | bytes 196616 | tf_op jit(solution)/shard_map/ppermute | solution.py:86
  26.1 1.3 %collective-permute-start.4 = (f32[128,128]{1,0:T(8,128)S(1)}, f32[128,128]{1,0:T(8,128)S(1)}, u32[]{:S(2)}, u32[]{:S(2)}) collective-permute-start(f32[128,128]{1,0:T(8,128)S(1)} %dynamic-slice_add_fusion.11), channel_id=1, source_target_pairs={{0,16},{2,18},{4,20},{6,22},{8,24},{10,26},{12,28},{14,30},{16,0},... | collective-permute-start | bytes 196616 | tf_op jit(solution)/shard_map/ppermute | solution.py:86
  27.4 3.1 %collective-permute-done.11 = f32[128,128]{1,0:T(8,128)S(1)} collective-permute-done((f32[128,128]{1,0:T(8,128)S(1)}, f32[128,128]{1,0:T(8,128)S(1)}, u32[]{:S(2)}, u32[]{:S(2)}) %collective-permute-start.11) | collective-permute-done | bytes 65568 | tf_op jit(solution)/shard_map/ppermute | solution.py:86
  31.3 2.1 %collective-permute-start.5 = (f32[128,128]{1,0:T(8,128)S(1)}, f32[128,128]{1,0:T(8,128)S(1)}, u32[]{:S(2)}, u32[]{:S(2)}) collective-permute-start(f32[128,128]{1,0:T(8,128)S(1)} %add_subtract_fusion.3), channel_id=1, source_target_pairs={{0,8},{2,10},{4,12},{6,14},{8,0},{10,2},{12,4},{14,6},{16,24},{18,... | collective-permute-start | bytes 196616 | tf_op jit(solution)/shard_map/ppermute | solution.py:90
  33.4 1.4 %collective-permute-done.12 = f32[128,128]{1,0:T(8,128)S(1)} collective-permute-done((f32[128,128]{1,0:T(8,128)S(1)}, f32[128,128]{1,0:T(8,128)S(1)}, u32[]{:S(2)}, u32[]{:S(2)}) %collective-permute-start.12) | collective-permute-done | bytes 65568 | tf_op jit(solution)/shard_map/ppermute | solution.py:90
  34.9 0.9 %collective-permute-done.5 = f32[128,128]{1,0:T(8,128)S(1)} collective-permute-done((f32[128,128]{1,0:T(8,128)S(1)}, f32[128,128]{1,0:T(8,128)S(1)}, u32[]{:S(2)}, u32[]{:S(2)}) %collective-permute-start.5) | collective-permute-done | bytes 65568 | tf_op jit(solution)/shard_map/ppermute | solution.py:90
  35.9 1.2 %collective-permute-start.6 = (f32[256,128]{1,0:T(8,128)S(1)}, f32[256,128]{1,0:T(8,128)S(1)}, u32[]{:S(2)}, u32[]{:S(2)}) collective-permute-start(f32[256,128]{1,0:T(8,128)S(1)} %pad_maximum_fusion.5), channel_id=1, source_target_pairs={{0,4},{2,6},{4,0},{6,2},{8,12},{10,14},{12,8},{14,10},{16,20},{18,... | collective-permute-start | bytes 393224 | tf_op jit(solution)/shard_map/ppermute | solution.py:90
  37.0 2.9 %collective-permute-done.13 = f32[256,128]{1,0:T(8,128)S(1)} collective-permute-done((f32[256,128]{1,0:T(8,128)S(1)}, f32[256,128]{1,0:T(8,128)S(1)}, u32[]{:S(2)}, u32[]{:S(2)}) %collective-permute-start.13) | collective-permute-done | bytes 131104 | tf_op jit(solution)/shard_map/ppermute | solution.py:90
  40.0 0.9 %collective-permute-done.6 = f32[256,128]{1,0:T(8,128)S(1)} collective-permute-done((f32[256,128]{1,0:T(8,128)S(1)}, f32[256,128]{1,0:T(8,128)S(1)}, u32[]{:S(2)}, u32[]{:S(2)}) %collective-permute-start.6) | collective-permute-done | bytes 131104 | tf_op jit(solution)/shard_map/ppermute | solution.py:90
  42.0 1.0 %convolution_bitcast_fusion = f32[1024,128]{1,0:T(8,128)S(1)} fusion(f32[64,128]{1,0:T(8,128)S(1)} %fusion.13, f32[1024,64]{0,1:T(8,128)S(1)} %copy-done.1), kind=kOutput, calls=%fused_computation.7 | convolution fusion | flops 100663296 | bytes 819200 | tf_op jit(solution)/shard_map/dot_general | solution.py:8
  43.8 1.0 %convolution_bitcast_fusion.1 = f32[1024,128]{1,0:T(8,128)S(1)} fusion(f32[64,128]{1,0:T(8,128)S(1)} %fusion.9, f32[1024,64]{0,1:T(8,128)S(1)} %copy-done.1), kind=kOutput, calls=%fused_computation.8 | convolution fusion | flops 100663296 | bytes 819200 | tf_op jit(solution)/shard_map/dot_general | solution.py:8
  45.4 1.4 %collective-permute-start.23 = (f32[256,128]{1,0:T(8,128)S(1)}, f32[256,128]{1,0:T(8,128)S(1)}, u32[]{:S(2)}, u32[]{:S(2)}) collective-permute-start(f32[256,128]{1,0:T(8,128)S(1)} %constant_dynamic-slice_fusion.1), channel_id=1, source_target_pairs={{0,8},{2,10},{4,12},{6,14},{8,0},{10,2},{12,4},{14,6},{16,24},{18,... | collective-permute-start | bytes 393224 | tf_op jit(solution)/shard_map/ppermute | solution.py:78
  47.6 3.4 %collective-permute-done.23 = f32[256,128]{1,0:T(8,128)S(1)} collective-permute-done((f32[256,128]{1,0:T(8,128)S(1)}, f32[256,128]{1,0:T(8,128)S(1)}, u32[]{:S(2)}, u32[]{:S(2)}) %collective-permute-start.23) | collective-permute-done | bytes 131104 | tf_op jit(solution)/shard_map/ppermute | solution.py:78
  51.1 1.1 %collective-permute-start.24 = (f32[128,128]{1,0:T(8,128)S(1)}, f32[128,128]{1,0:T(8,128)S(1)}, u32[]{:S(2)}, u32[]{:S(2)}) collective-permute-start(f32[128,128]{1,0:T(8,128)S(1)} %constant_dynamic-slice_fusion), channel_id=1, source_target_pairs={{0,4},{2,6},{4,0},{6,2},{8,12},{10,14},{12,8},{14,10},{16,20},{18,... | collective-permute-start | bytes 196616 | tf_op jit(solution)/shard_map/ppermute | solution.py:78
  52.6 1.4 %collective-permute-start.17 = (f32[128,128]{1,0:T(8,128)S(1)}, f32[128,128]{1,0:T(8,128)S(1)}, u32[]{:S(2)}, u32[]{:S(2)}) collective-permute-start(f32[128,128]{1,0:T(8,128)S(1)} %constant_dynamic-slice_fusion.3), channel_id=1, source_target_pairs={{0,8},{2,10},{4,12},{6,14},{8,0},{10,2},{12,4},{14,6},{16,24},{18,... | collective-permute-start | bytes 196616 | tf_op jit(solution)/shard_map/ppermute | solution.py:78
  54.0 1.4 %collective-permute-done.24 = f32[128,128]{1,0:T(8,128)S(1)} collective-permute-done((f32[128,128]{1,0:T(8,128)S(1)}, f32[128,128]{1,0:T(8,128)S(1)}, u32[]{:S(2)}, u32[]{:S(2)}) %collective-permute-start.24) | collective-permute-done | bytes 65568 | tf_op jit(solution)/shard_map/ppermute | solution.py:78
  55.4 1.9 %collective-permute-start.25 = (f32[128,128]{1,0:T(8,128)S(1)}, f32[128,128]{1,0:T(8,128)S(1)}, u32[]{:S(2)}, u32[]{:S(2)}) collective-permute-start(f32[128,128]{1,0:T(8,128)S(1)} %dynamic-slice_add_fusion.8), channel_id=1, source_target_pairs={{0,16},{2,18},{4,20},{6,22},{8,24},{10,26},{12,28},{14,30},{16,0},... | collective-permute-start | bytes 196616 | tf_op jit(solution)/shard_map/ppermute | solution.py:86
  57.4 1.2 %collective-permute-start.18 = (f32[128,128]{1,0:T(8,128)S(1)}, f32[128,128]{1,0:T(8,128)S(1)}, u32[]{:S(2)}, u32[]{:S(2)}) collective-permute-start(f32[128,128]{1,0:T(8,128)S(1)} %dynamic-slice_add_fusion.9), channel_id=1, source_target_pairs={{0,16},{2,18},{4,20},{6,22},{8,24},{10,26},{12,28},{14,30},{16,0},... | collective-permute-start | bytes 196616 | tf_op jit(solution)/shard_map/ppermute | solution.py:86
  58.6 3.6 %collective-permute-done.25 = f32[128,128]{1,0:T(8,128)S(1)} collective-permute-done((f32[128,128]{1,0:T(8,128)S(1)}, f32[128,128]{1,0:T(8,128)S(1)}, u32[]{:S(2)}, u32[]{:S(2)}) %collective-permute-start.25) | collective-permute-done | bytes 65568 | tf_op jit(solution)/shard_map/ppermute | solution.py:86
  64.2 2.4 %collective-permute-done.26 = f32[128,128]{1,0:T(8,128)S(1)} collective-permute-done((f32[128,128]{1,0:T(8,128)S(1)}, f32[128,128]{1,0:T(8,128)S(1)}, u32[]{:S(2)}, u32[]{:S(2)}) %collective-permute-start.26) | collective-permute-done | bytes 65568 | tf_op jit(solution)/shard_map/ppermute | solution.py:90
  66.8 1.1 %collective-permute-done.19 = f32[128,128]{1,0:T(8,128)S(1)} collective-permute-done((f32[128,128]{1,0:T(8,128)S(1)}, f32[128,128]{1,0:T(8,128)S(1)}, u32[]{:S(2)}, u32[]{:S(2)}) %collective-permute-start.19) | collective-permute-done | bytes 65568 | tf_op jit(solution)/shard_map/ppermute | solution.py:90
  68.8 2.8 %collective-permute-done.27 = f32[256,128]{1,0:T(8,128)S(1)} collective-permute-done((f32[256,128]{1,0:T(8,128)S(1)}, f32[256,128]{1,0:T(8,128)S(1)}, u32[]{:S(2)}, u32[]{:S(2)}) %collective-permute-start.27) | collective-permute-done | bytes 131104 | tf_op jit(solution)/shard_map/ppermute | solution.py:90
  71.7 1.3 %collective-permute-done.20 = f32[256,128]{1,0:T(8,128)S(1)} collective-permute-done((f32[256,128]{1,0:T(8,128)S(1)}, f32[256,128]{1,0:T(8,128)S(1)}, u32[]{:S(2)}, u32[]{:S(2)}) %collective-permute-start.20) | collective-permute-done | bytes 131104 | tf_op jit(solution)/shard_map/ppermute | solution.py:90
  73.7 0.9 %collective-permute-done.21 = f32[512,128]{1,0:T(8,128)S(1)} collective-permute-done((f32[512,128]{1,0:T(8,128)S(1)}, f32[512,128]{1,0:T(8,128)S(1)}, u32[]{:S(2)}, u32[]{:S(2)}) %collective-permute-start.21) | collective-permute-done | bytes 262176 | tf_op jit(solution)/shard_map/ppermute | solution.py:90
  (105 shorter events, 12.9 us)
Async XLA Ops:
  0.0 10.2 %collective-permute-start = (f32[1,1,2,64,512]{4,3,2,1,0:T(8,128)}, f32[1,1,2,64,512]{4,3,2,1,0:T(8,128)S(1)}, u32[]{:S(2)}, u32[]{:S(2)}) collective-permute-start(f32[1,1,2,64,512]{4,3,2,1,0:T(8,128)} %bitcast.51), channel_id=1, source_target_pairs={{0,1},{1,0},{2,3},{3,2},{4,5},{5,4},{6,7},{7,6},{8,9},{9,8},{10,11... | collective-permute-start | bytes 786440 | tf_op jit(solution)/shard_map/ppermute | solution.py:34
  4.6 5.5 %copy-start.2 = (f32[2,64,512]{2,1,0:T(8,128)S(1)}, f32[2,64,512]{2,1,0:T(8,128)}, u32[]{:S(2)}) copy-start(f32[2,64,512]{2,1,0:T(8,128)} %param.8) | copy-start | bytes 786436
  4.7 10.7 %slice-start = ((s8[8388608]{0:T(1024)(128)(4,1)}), s8[4194304]{0:T(1024)(128)(4,1)S(1)}, s32[]{:S(2)}) async-start(s8[8388608]{0:T(1024)(128)(4,1)} %bitcast.49), calls=%async_computation | async-start | bytes 8388608
  10.4 1.6 %collective-permute-start.1 = (f32[512,128]{1,0:T(8,128)S(1)}, f32[512,128]{1,0:T(8,128)S(1)}, u32[]{:S(2)}, u32[]{:S(2)}) collective-permute-start(f32[512,128]{1,0:T(8,128)S(1)} %constant_dynamic-slice_fusion.11), channel_id=1, source_target_pairs={{0,2},{2,0},{4,6},{6,4},{8,10},{10,8},{12,14},{14,12},{16,18},{18,... | collective-permute-start | bytes 786440 | tf_op jit(solution)/shard_map/ppermute | solution.py:78
  10.6 3.0 %collective-permute-start.8 = (f32[512,128]{1,0:T(8,128)S(1)}, f32[512,128]{1,0:T(8,128)S(1)}, u32[]{:S(2)}, u32[]{:S(2)}) collective-permute-start(f32[512,128]{1,0:T(8,128)S(1)} %constant_dynamic-slice_fusion.8), channel_id=1, source_target_pairs={{0,2},{2,0},{4,6},{6,4},{8,10},{10,8},{12,14},{14,12},{16,18},{18,... | collective-permute-start | bytes 786440 | tf_op jit(solution)/shard_map/ppermute | solution.py:78
  12.0 7.8 %collective-permute-start.2 = (f32[256,128]{1,0:T(8,128)S(1)}, f32[256,128]{1,0:T(8,128)S(1)}, u32[]{:S(2)}, u32[]{:S(2)}) collective-permute-start(f32[256,128]{1,0:T(8,128)S(1)} %constant_dynamic-slice_fusion.10), channel_id=1, source_target_pairs={{0,4},{2,6},{4,0},{6,2},{8,12},{10,14},{12,8},{14,10},{16,20},{18,... | collective-permute-start | bytes 393224 | tf_op jit(solution)/shard_map/ppermute | solution.py:78
  13.7 5.3 %collective-permute-start.9 = (f32[256,128]{1,0:T(8,128)S(1)}, f32[256,128]{1,0:T(8,128)S(1)}, u32[]{:S(2)}, u32[]{:S(2)}) collective-permute-start(f32[256,128]{1,0:T(8,128)S(1)} %constant_dynamic-slice_fusion.7), channel_id=1, source_target_pairs={{0,8},{2,10},{4,12},{6,14},{8,0},{10,2},{12,4},{14,6},{16,24},{18,... | collective-permute-start | bytes 393224 | tf_op jit(solution)/shard_map/ppermute | solution.py:78
  18.9 23.2 %copy-start.1 = (f32[1024,64]{0,1:T(8,128)S(1)}, f32[1024,64]{0,1:T(8,128)}, u32[]{:S(2)}) copy-start(f32[1024,64]{0,1:T(8,128)} %param.9) | copy-start | bytes 786436
  19.0 4.3 %collective-permute-start.10 = (f32[128,128]{1,0:T(8,128)S(1)}, f32[128,128]{1,0:T(8,128)S(1)}, u32[]{:S(2)}, u32[]{:S(2)}) collective-permute-start(f32[128,128]{1,0:T(8,128)S(1)} %constant_dynamic-slice_fusion.6), channel_id=1, source_target_pairs={{0,4},{2,6},{4,0},{6,2},{8,12},{10,14},{12,8},{14,10},{16,20},{18,... | collective-permute-start | bytes 196616 | tf_op jit(solution)/shard_map/ppermute | solution.py:78
  19.9 6.2 %collective-permute-start.3 = (f32[128,128]{1,0:T(8,128)S(1)}, f32[128,128]{1,0:T(8,128)S(1)}, u32[]{:S(2)}, u32[]{:S(2)}) collective-permute-start(f32[128,128]{1,0:T(8,128)S(1)} %constant_dynamic-slice_fusion.9), channel_id=1, source_target_pairs={{0,8},{2,10},{4,12},{6,14},{8,0},{10,2},{12,4},{14,6},{16,24},{18,... | collective-permute-start | bytes 196616 | tf_op jit(solution)/shard_map/ppermute | solution.py:78
  23.4 7.1 %collective-permute-start.11 = (f32[128,128]{1,0:T(8,128)S(1)}, f32[128,128]{1,0:T(8,128)S(1)}, u32[]{:S(2)}, u32[]{:S(2)}) collective-permute-start(f32[128,128]{1,0:T(8,128)S(1)} %dynamic-slice_add_fusion.10), channel_id=1, source_target_pairs={{0,16},{2,18},{4,20},{6,22},{8,24},{10,26},{12,28},{14,30},{16,0},... | collective-permute-start | bytes 196616 | tf_op jit(solution)/shard_map/ppermute | solution.py:86
  26.1 5.2 %collective-permute-start.4 = (f32[128,128]{1,0:T(8,128)S(1)}, f32[128,128]{1,0:T(8,128)S(1)}, u32[]{:S(2)}, u32[]{:S(2)}) collective-permute-start(f32[128,128]{1,0:T(8,128)S(1)} %dynamic-slice_add_fusion.11), channel_id=1, source_target_pairs={{0,16},{2,18},{4,20},{6,22},{8,24},{10,26},{12,28},{14,30},{16,0},... | collective-permute-start | bytes 196616 | tf_op jit(solution)/shard_map/ppermute | solution.py:86
  30.5 4.3 %collective-permute-start.12 = (f32[128,128]{1,0:T(8,128)S(1)}, f32[128,128]{1,0:T(8,128)S(1)}, u32[]{:S(2)}, u32[]{:S(2)}) collective-permute-start(f32[128,128]{1,0:T(8,128)S(1)} %add_subtract_fusion.2), channel_id=1, source_target_pairs={{0,4},{2,6},{4,0},{6,2},{8,12},{10,14},{12,8},{14,10},{16,20},{18,... | collective-permute-start | bytes 196616 | tf_op jit(solution)/shard_map/ppermute | solution.py:90
  31.3 4.5 %collective-permute-start.5 = (f32[128,128]{1,0:T(8,128)S(1)}, f32[128,128]{1,0:T(8,128)S(1)}, u32[]{:S(2)}, u32[]{:S(2)}) collective-permute-start(f32[128,128]{1,0:T(8,128)S(1)} %add_subtract_fusion.3), channel_id=1, source_target_pairs={{0,8},{2,10},{4,12},{6,14},{8,0},{10,2},{12,4},{14,6},{16,24},{18,... | collective-permute-start | bytes 196616 | tf_op jit(solution)/shard_map/ppermute | solution.py:90
  34.9 5.0 %collective-permute-start.13 = (f32[256,128]{1,0:T(8,128)S(1)}, f32[256,128]{1,0:T(8,128)S(1)}, u32[]{:S(2)}, u32[]{:S(2)}) collective-permute-start(f32[256,128]{1,0:T(8,128)S(1)} %pad_maximum_fusion.6), channel_id=1, source_target_pairs={{0,8},{2,10},{4,12},{6,14},{8,0},{10,2},{12,4},{14,6},{16,24},{18,... | collective-permute-start | bytes 393224 | tf_op jit(solution)/shard_map/ppermute | solution.py:90
  35.9 5.0 %collective-permute-start.6 = (f32[256,128]{1,0:T(8,128)S(1)}, f32[256,128]{1,0:T(8,128)S(1)}, u32[]{:S(2)}, u32[]{:S(2)}) collective-permute-start(f32[256,128]{1,0:T(8,128)S(1)} %pad_maximum_fusion.5), channel_id=1, source_target_pairs={{0,4},{2,6},{4,0},{6,2},{8,12},{10,14},{12,8},{14,10},{16,20},{18,... | collective-permute-start | bytes 393224 | tf_op jit(solution)/shard_map/ppermute | solution.py:90
  40.0 1.6 %collective-permute-start.14 = (f32[512,128]{1,0:T(8,128)S(1)}, f32[512,128]{1,0:T(8,128)S(1)}, u32[]{:S(2)}, u32[]{:S(2)}) collective-permute-start(f32[512,128]{1,0:T(8,128)S(1)} %pad_maximum_fusion.2), channel_id=1, source_target_pairs={{0,2},{2,0},{4,6},{6,4},{8,10},{10,8},{12,14},{14,12},{16,18},{18,... | collective-permute-start | bytes 786440 | tf_op jit(solution)/shard_map/ppermute | solution.py:90
  40.9 2.4 %collective-permute-start.7 = (f32[512,128]{1,0:T(8,128)S(1)}, f32[512,128]{1,0:T(8,128)S(1)}, u32[]{:S(2)}, u32[]{:S(2)}) collective-permute-start(f32[512,128]{1,0:T(8,128)S(1)} %pad_maximum_fusion.1), channel_id=1, source_target_pairs={{0,2},{2,0},{4,6},{6,4},{8,10},{10,8},{12,14},{14,12},{16,18},{18,... | collective-permute-start | bytes 786440 | tf_op jit(solution)/shard_map/ppermute | solution.py:90
  43.2 2.2 %collective-permute-start.22 = (f32[512,128]{1,0:T(8,128)S(1)}, f32[512,128]{1,0:T(8,128)S(1)}, u32[]{:S(2)}, u32[]{:S(2)}) collective-permute-start(f32[512,128]{1,0:T(8,128)S(1)} %constant_dynamic-slice_fusion.2), channel_id=1, source_target_pairs={{0,2},{2,0},{4,6},{6,4},{8,10},{10,8},{12,14},{14,12},{16,18},{18,... | collective-permute-start | bytes 786440 | tf_op jit(solution)/shard_map/ppermute | solution.py:78
  44.9 1.9 %collective-permute-start.15 = (f32[512,128]{1,0:T(8,128)S(1)}, f32[512,128]{1,0:T(8,128)S(1)}, u32[]{:S(2)}, u32[]{:S(2)}) collective-permute-start(f32[512,128]{1,0:T(8,128)S(1)} %constant_dynamic-slice_fusion.5), channel_id=1, source_target_pairs={{0,2},{2,0},{4,6},{6,4},{8,10},{10,8},{12,14},{14,12},{16,18},{18,... | collective-permute-start | bytes 786440 | tf_op jit(solution)/shard_map/ppermute | solution.py:78
  45.4 5.6 %collective-permute-start.23 = (f32[256,128]{1,0:T(8,128)S(1)}, f32[256,128]{1,0:T(8,128)S(1)}, u32[]{:S(2)}, u32[]{:S(2)}) collective-permute-start(f32[256,128]{1,0:T(8,128)S(1)} %constant_dynamic-slice_fusion.1), channel_id=1, source_target_pairs={{0,8},{2,10},{4,12},{6,14},{8,0},{10,2},{12,4},{14,6},{16,24},{18,... | collective-permute-start | bytes 393224 | tf_op jit(solution)/shard_map/ppermute | solution.py:78
  46.9 5.7 %collective-permute-start.16 = (f32[256,128]{1,0:T(8,128)S(1)}, f32[256,128]{1,0:T(8,128)S(1)}, u32[]{:S(2)}, u32[]{:S(2)}) collective-permute-start(f32[256,128]{1,0:T(8,128)S(1)} %constant_dynamic-slice_fusion.4), channel_id=1, source_target_pairs={{0,4},{2,6},{4,0},{6,2},{8,12},{10,14},{12,8},{14,10},{16,20},{18,... | collective-permute-start | bytes 393224 | tf_op jit(solution)/shard_map/ppermute | solution.py:78
  51.1 4.3 %collective-permute-start.24 = (f32[128,128]{1,0:T(8,128)S(1)}, f32[128,128]{1,0:T(8,128)S(1)}, u32[]{:S(2)}, u32[]{:S(2)}) collective-permute-start(f32[128,128]{1,0:T(8,128)S(1)} %constant_dynamic-slice_fusion), channel_id=1, source_target_pairs={{0,4},{2,6},{4,0},{6,2},{8,12},{10,14},{12,8},{14,10},{16,20},{18,... | collective-permute-start | bytes 196616 | tf_op jit(solution)/shard_map/ppermute | solution.py:78
  52.6 4.7 %collective-permute-start.17 = (f32[128,128]{1,0:T(8,128)S(1)}, f32[128,128]{1,0:T(8,128)S(1)}, u32[]{:S(2)}, u32[]{:S(2)}) collective-permute-start(f32[128,128]{1,0:T(8,128)S(1)} %constant_dynamic-slice_fusion.3), channel_id=1, source_target_pairs={{0,8},{2,10},{4,12},{6,14},{8,0},{10,2},{12,4},{14,6},{16,24},{18,... | collective-permute-start | bytes 196616 | tf_op jit(solution)/shard_map/ppermute | solution.py:78
  55.4 6.7 %collective-permute-start.25 = (f32[128,128]{1,0:T(8,128)S(1)}, f32[128,128]{1,0:T(8,128)S(1)}, u32[]{:S(2)}, u32[]{:S(2)}) collective-permute-start(f32[128,128]{1,0:T(8,128)S(1)} %dynamic-slice_add_fusion.8), channel_id=1, source_target_pairs={{0,16},{2,18},{4,20},{6,22},{8,24},{10,26},{12,28},{14,30},{16,0},... | collective-permute-start | bytes 196616 | tf_op jit(solution)/shard_map/ppermute | solution.py:86
  57.4 6.2 %collective-permute-start.18 = (f32[128,128]{1,0:T(8,128)S(1)}, f32[128,128]{1,0:T(8,128)S(1)}, u32[]{:S(2)}, u32[]{:S(2)}) collective-permute-start(f32[128,128]{1,0:T(8,128)S(1)} %dynamic-slice_add_fusion.9), channel_id=1, source_target_pairs={{0,16},{2,18},{4,20},{6,22},{8,24},{10,26},{12,28},{14,30},{16,0},... | collective-permute-start | bytes 196616 | tf_op jit(solution)/shard_map/ppermute | solution.py:86
  62.2 4.3 %collective-permute-start.26 = (f32[128,128]{1,0:T(8,128)S(1)}, f32[128,128]{1,0:T(8,128)S(1)}, u32[]{:S(2)}, u32[]{:S(2)}) collective-permute-start(f32[128,128]{1,0:T(8,128)S(1)} %add_subtract_fusion), channel_id=1, source_target_pairs={{0,4},{2,6},{4,0},{6,2},{8,12},{10,14},{12,8},{14,10},{16,20},{18,... | collective-permute-start | bytes 196616 | tf_op jit(solution)/shard_map/ppermute | solution.py:90
  63.6 4.3 %collective-permute-start.19 = (f32[128,128]{1,0:T(8,128)S(1)}, f32[128,128]{1,0:T(8,128)S(1)}, u32[]{:S(2)}, u32[]{:S(2)}) collective-permute-start(f32[128,128]{1,0:T(8,128)S(1)} %add_subtract_fusion.1), channel_id=1, source_target_pairs={{0,8},{2,10},{4,12},{6,14},{8,0},{10,2},{12,4},{14,6},{16,24},{18,... | collective-permute-start | bytes 196616 | tf_op jit(solution)/shard_map/ppermute | solution.py:90
  66.6 5.0 %collective-permute-start.27 = (f32[256,128]{1,0:T(8,128)S(1)}, f32[256,128]{1,0:T(8,128)S(1)}, u32[]{:S(2)}, u32[]{:S(2)}) collective-permute-start(f32[256,128]{1,0:T(8,128)S(1)} %pad_maximum_fusion.8), channel_id=1, source_target_pairs={{0,8},{2,10},{4,12},{6,14},{8,0},{10,2},{12,4},{14,6},{16,24},{18,... | collective-permute-start | bytes 393224 | tf_op jit(solution)/shard_map/ppermute | solution.py:90
  68.0 5.0 %collective-permute-start.20 = (f32[256,128]{1,0:T(8,128)S(1)}, f32[256,128]{1,0:T(8,128)S(1)}, u32[]{:S(2)}, u32[]{:S(2)}) collective-permute-start(f32[256,128]{1,0:T(8,128)S(1)} %pad_maximum_fusion.7), channel_id=1, source_target_pairs={{0,4},{2,6},{4,0},{6,2},{8,12},{10,14},{12,8},{14,10},{16,20},{18,... | collective-permute-start | bytes 393224 | tf_op jit(solution)/shard_map/ppermute | solution.py:90
  71.6 1.6 %collective-permute-start.28 = (f32[512,128]{1,0:T(8,128)S(1)}, f32[512,128]{1,0:T(8,128)S(1)}, u32[]{:S(2)}, u32[]{:S(2)}) collective-permute-start(f32[512,128]{1,0:T(8,128)S(1)} %pad_maximum_fusion.4), channel_id=1, source_target_pairs={{0,2},{2,0},{4,6},{6,4},{8,10},{10,8},{12,14},{14,12},{16,18},{18,... | collective-permute-start | bytes 786440 | tf_op jit(solution)/shard_map/ppermute | solution.py:90
  73.0 1.6 %collective-permute-start.21 = (f32[512,128]{1,0:T(8,128)S(1)}, f32[512,128]{1,0:T(8,128)S(1)}, u32[]{:S(2)}, u32[]{:S(2)}) collective-permute-start(f32[512,128]{1,0:T(8,128)S(1)} %pad_maximum_fusion.3), channel_id=1, source_target_pairs={{0,2},{2,0},{4,6},{6,4},{8,10},{10,8},{12,14},{14,12},{16,18},{18,... | collective-permute-start | bytes 786440 | tf_op jit(solution)/shard_map/ppermute | solution.py:90
  (2 other events, 9.8 us)

commit v21 on v20

--- a/solution.py
+++ b/solution.py
@@ -68,13 +68,13 @@
 
 def ordered_reduce_then_gather(x, right, axis, n, order, riders=None, hold=None):
     me = lax.axis_index(axis)
-    y, r = x, right
+    y, offset, held = x, 0, None
     for step, j in enumerate(order[:-1]):
         half = y.shape[0] // 2
         mine = (me >> j) & 1
         keep = lax.dynamic_slice_in_dim(y, mine * half, half, 0)
         send = lax.dynamic_slice_in_dim(y, (1 - mine) * half, half, 0)
-        r = lax.dynamic_slice_in_dim(r, mine * half, half, 0)
+        offset = offset + mine * half
         got = lax.ppermute(send, axis, [(i, i ^ (1 << j)) for i in range(n)])
         if step == 1 and riders is not None:
             got, riders = lax.optimization_barrier((got, riders))
@@ -84,7 +84,9 @@
             riders = (hold[1](held), riders)
     top = order[-1]
     y = y + lax.ppermute(y, axis, [(i, i ^ (1 << top)) for i in range(n)])
-    y = r - y
+    if callable(right):
+        right = right(held)
+    y = lax.dynamic_slice_in_dim(right, offset, y.shape[0], 0) - y
     for j in reversed(order[:-1]):
         mine = (me >> j) & 1
         got = lax.ppermute(y, axis, [(i, i ^ (1 << j)) for i in range(n)])
@@ -135,20 +137,21 @@
 
             first_blocks = []
             for chain, (order, cols) in enumerate(zip(orders, columns)):
-                remains, got_riders = ordered_reduce_then_gather(
-                    first_sum[:, cols], right_side[0][:, cols], "blk", n, order,
-                    inverse_pieces if chain == 0 else None,
-                    (solved_before, lambda held: column_halves(product(factor_panel[1], held))) if chain == 0 else None,
-                )
                 if chain == 0:
-                    panel_sum, inverse_pieces = got_riders
+                    remains, got_riders = ordered_reduce_then_gather(
+                        first_sum[:, cols], lambda held, cols=cols: held[1][0][:, cols], "blk", n, order, inverse_pieces,
+                        ((solved_before, right_side), lambda held: (column_halves(product(factor_panel[1], held[0])), held[1])),
+                    )
+                    (panel_sum, right_held), inverse_pieces = got_riders
+                else:
+                    remains, _ = ordered_reduce_then_gather(first_sum[:, cols], right_held[0][:, cols], "blk", n, order)
                 first_blocks.append(remains)
             inverse_full = jnp.concatenate(list(inverse_pieces), axis=2)
             first_blocks = [product(inverse_full[0], remains) for remains in first_blocks]
             second_blocks = []
             for chain, (order, cols, block) in enumerate(zip(orders, columns, first_blocks)):
                 remains, _ = ordered_reduce_then_gather(
-                    panel_sum[chain] + product(coupling, block), right_side[1][:, cols], "blk", n, order
+                    panel_sum[chain] + product(coupling, block), right_held[1][:, cols], "blk", n, order
                 )
                 second_blocks.append(product(inverse_full[1], remains))
             first_block = jnp.concatenate(first_blocks, 1)

time: 76 us -> 78.5 us (1.033)
  waiting for transfers between devices: 30.6 us -> 35.4 us
  starting transfers between devices: 28.3 us -> 25.7 us
  matrix products: 12.6 us -> 14.3 us
  local copies, waits for them, and re-layouts: 2.26 us -> 0.75 us
    ppermute x12, waiting for transfers between devices: 8.08 us -> 11.4 us  [ordered_reduce_then_gather(): got = lax.ppermute(send, axis, [(i, i ^ 1 << j) for i in range(n)])]
    ppermute x12, starting transfers between devices: 11.5 us -> 8.92 us  [ordered_reduce_then_gather(): got = lax.ppermute(send, axis, [(i, i ^ 1 << j) for i in range(n)])]
    ppermute x4, waiting for transfers between devices: 7.31 us -> 9.61 us  [ordered_reduce_then_gather(): y = y + lax.ppermute(y, axis, [(i, i ^ 1 << top) for i in range(n)])]
    ppermute x12, waiting for transfers between devices: 15.2 us -> 13.1 us  [ordered_reduce_then_gather(): got = lax.ppermute(y, axis, [(i, i ^ 1 << j) for i in range(n)])]
    dot_general x8, matrix products: 12.6 us -> 14.3 us  [product(): jnp.dot(left, right, precision=lax.Precision.HIGHEST, preferred_element_t...]
    squeeze x1 -> x2, local copies, waits for them, and re-layouts: 1.68 us -> 0.21 us  [the longest x1 0.14 us: shards(): right_held[1][:, cols]]
    ppermute x1, waiting for transfers between devices: 0.01 us -> 1.31 us  [doubling_gather(): got = lax.ppermute(y, axis, [(i, i ^ 1 << j) for i in range(n)])]
    ppermute x4, starting transfers between devices: 7.05 us -> 6.19 us  [ordered_reduce_then_gather(): y = y + lax.ppermute(y, axis, [(i, i ^ 1 << top) for i in range(n)])]
  transfers between devices with their start and end apart: 29 -> 29, of which waited for: 20 -> 19; matrix products, arithmetic and copies ran while one was open for 20% -> 19% of each run, Pallas kernels for 0% -> 0%
where the time goes in v21:
time: 78.5 us; the launch traced here: 78.4 us
  waiting for transfers between devices  35.4 us (45%)
  starting transfers between devices  25.7 us (33%)
  matrix products  14.3 us (18%)
  other arithmetic  1.56 us (2%)
    dot_general x8, matrix products, product(): jnp.dot(left, right, precision=lax.Precision.HIGHEST, preferred_element_t...  14.3 us
    ppermute x12, waiting for transfers between devices, ordered_reduce_then_gather(): got = lax.ppermute(y, axis, [(i, i ^ 1 << j) for i in range(n)])  13.1 us
    ppermute x12, waiting for transfers between devices, ordered_reduce_then_gather(): got = lax.ppermute(send, axis, [(i, i ^ 1 << j) for i in range(n)])  11.4 us
    ppermute x4, waiting for transfers between devices, ordered_reduce_then_gather(): y = y + lax.ppermute(y, axis, [(i, i ^ 1 << top) for i in range(n)])  9.61 us
    ppermute x12, starting transfers between devices, ordered_reduce_then_gather(): got = lax.ppermute(send, axis, [(i, i ^ 1 << j) for i in range(n)])  8.92 us
    ppermute x12, starting transfers between devices, ordered_reduce_then_gather(): got = lax.ppermute(y, axis, [(i, i ^ 1 << j) for i in range(n)])  7.67 us
    ppermute x4, starting transfers between devices, ordered_reduce_then_gather(): y = y + lax.ppermute(y, axis, [(i, i ^ 1 << top) for i in range(n)])  6.19 us
    ppermute x1, starting transfers between devices, doubling_gather(): got = lax.ppermute(y, axis, [(i, i ^ 1 << j) for i in range(n)])  2.94 us
  transfers between devices with their start and end apart: 29, of which 19 were waited for; matrix products, arithmetic and copies ran while one was open for 19% of the time, Pallas kernels for 0%

profile of v21, /device:TPU:0, one launch (start us, length us, event | category | flops | bytes accessed | tf_op | source)
XLA Modules:
  0.0 78.4 jit_solution(7029058919371395256)
XLA Ops:
  0.0 2.9 %collective-permute-start = (f32[1,1,2,64,512]{4,3,2,1,0:T(8,128)}, f32[1,1,2,64,512]{4,3,2,1,0:T(8,128)S(1)}, u32[]{:S(2)}, u32[]{:S(2)}) collective-permute-start(f32[1,1,2,64,512]{4,3,2,1,0:T(8,128)} %bitcast.51), channel_id=1, source_target_pairs={{0,1},{1,0},{2,3},{3,2},{4,5},{5,4},{6,7},{7,6},{8,9},{9,8},{10,11... | collective-permute-start | bytes 786440 | tf_op jit(solution)/shard_map/ppermute | solution.py:34
  2.9 5.2 %fusion.2 = f32[1024,256]{1,0:T(8,128)S(1)} fusion(f32[1024,256]{1,0:T(8,128)S(1)} %copy-done, f32[2,1024,1024]{2,1,0:T(8,128)} %param.5), kind=kOutput, calls=%fused_computation.2 | convolution fusion | flops 3221225472 | bytes 6291456 | tf_op jit(solution)/shard_map/dot_general | solution.py:8
  8.2 1.3 %collective-permute-done = f32[1,1,2,64,512]{4,3,2,1,0:T(8,128)S(1)} collective-permute-done((f32[1,1,2,64,512]{4,3,2,1,0:T(8,128)}, f32[1,1,2,64,512]{4,3,2,1,0:T(8,128)S(1)}, u32[]{:S(2)}, u32[]{:S(2)}) %collective-permute-start) | collective-permute-done | bytes 262176 | tf_op jit(solution)/shard_map/ppermute | solution.py:34
  10.4 0.9 %collective-permute-done.1 = f32[512,128]{1,0:T(8,128)S(1)} collective-permute-done((f32[512,128]{1,0:T(8,128)S(1)}, f32[512,128]{1,0:T(8,128)S(1)}, u32[]{:S(2)}, u32[]{:S(2)}) %collective-permute-start.1) | collective-permute-done | bytes 262176 | tf_op jit(solution)/shard_map/ppermute | solution.py:78
  11.4 1.8 %collective-permute-start.2 = (f32[256,128]{1,0:T(8,128)S(1)}, f32[256,128]{1,0:T(8,128)S(1)}, u32[]{:S(2)}, u32[]{:S(2)}) collective-permute-start(f32[256,128]{1,0:T(8,128)S(1)} %constant_dynamic-slice_fusion.10), channel_id=1, source_target_pairs={{0,4},{2,6},{4,0},{6,2},{8,12},{10,14},{12,8},{14,10},{16,20},{18,... | collective-permute-start | bytes 393224 | tf_op jit(solution)/shard_map/ppermute | solution.py:78
  13.2 1.6 %collective-permute-start.9 = (f32[256,128]{1,0:T(8,128)S(1)}, f32[256,128]{1,0:T(8,128)S(1)}, u32[]{:S(2)}, u32[]{:S(2)}) collective-permute-start(f32[256,128]{1,0:T(8,128)S(1)} %constant_dynamic-slice_fusion.7), channel_id=1, source_target_pairs={{0,8},{2,10},{4,12},{6,14},{8,0},{10,2},{12,4},{14,6},{16,24},{18,... | collective-permute-start | bytes 393224 | tf_op jit(solution)/shard_map/ppermute | solution.py:78
  14.9 5.3 %fusion.6 = f32[1024,256]{1,0:T(8,128)S(1)} fusion(f32[1024,256]{1,0:T(8,128)S(1)} %copy-done, f32[2,1024,1024]{2,1,0:T(8,128)} %param.5), kind=kOutput, calls=%fused_computation.6 | convolution fusion | flops 3221225472 | bytes 6291456 | tf_op jit(solution)/shard_map/dot_general | solution.py:8
  21.7 3.7 %collective-permute-done.3 = f32[128,128]{1,0:T(8,128)S(1)} collective-permute-done((f32[128,128]{1,0:T(8,128)S(1)}, f32[128,128]{1,0:T(8,128)S(1)}, u32[]{:S(2)}, u32[]{:S(2)}) %collective-permute-start.3) | collective-permute-done | bytes 65568 | tf_op jit(solution)/shard_map/ppermute | solution.py:78
  25.4 3.0 %collective-permute-start.4 = (f32[128,128]{1,0:T(8,128)S(1)}, f32[128,128]{1,0:T(8,128)S(1)}, u32[]{:S(2)}, u32[]{:S(2)}) collective-permute-start(f32[128,128]{1,0:T(8,128)S(1)} %dynamic-slice_add_fusion.11), channel_id=1, source_target_pairs={{0,16},{2,18},{4,20},{6,22},{8,24},{10,26},{12,28},{14,30},{16,0},... | collective-permute-start | bytes 196616 | tf_op jit(solution)/shard_map/ppermute | solution.py:86
  28.6 3.9 %collective-permute-done.4 = f32[128,128]{1,0:T(8,128)S(1)} collective-permute-done((f32[128,128]{1,0:T(8,128)S(1)}, f32[128,128]{1,0:T(8,128)S(1)}, u32[]{:S(2)}, u32[]{:S(2)}) %collective-permute-start.4) | collective-permute-done | bytes 65568 | tf_op jit(solution)/shard_map/ppermute | solution.py:86
  32.5 1.6 %collective-permute-done.11 = f32[128,128]{1,0:T(8,128)S(1)} collective-permute-done((f32[128,128]{1,0:T(8,128)S(1)}, f32[128,128]{1,0:T(8,128)S(1)}, u32[]{:S(2)}, u32[]{:S(2)}) %collective-permute-start.11) | collective-permute-done | bytes 65568 | tf_op jit(solution)/shard_map/ppermute | solution.py:86
  34.1 1.4 %collective-permute-start.12 = (f32[128,128]{1,0:T(8,128)S(1)}, f32[128,128]{1,0:T(8,128)S(1)}, u32[]{:S(2)}, u32[]{:S(2)}) collective-permute-start(f32[128,128]{1,0:T(8,128)S(1)} %add_subtract_fusion.2), channel_id=1, source_target_pairs={{0,4},{2,6},{4,0},{6,2},{8,12},{10,14},{12,8},{14,10},{16,20},{18,... | collective-permute-start | bytes 196616 | tf_op jit(solution)/shard_map/ppermute | solution.py:92
  35.5 1.2 %collective-permute-done.5 = f32[128,128]{1,0:T(8,128)S(1)} collective-permute-done((f32[128,128]{1,0:T(8,128)S(1)}, f32[128,128]{1,0:T(8,128)S(1)}, u32[]{:S(2)}, u32[]{:S(2)}) %collective-permute-start.5) | collective-permute-done | bytes 65568 | tf_op jit(solution)/shard_map/ppermute | solution.py:92
  36.8 1.8 %collective-permute-start.6 = (f32[256,128]{1,0:T(8,128)S(1)}, f32[256,128]{1,0:T(8,128)S(1)}, u32[]{:S(2)}, u32[]{:S(2)}) collective-permute-start(f32[256,128]{1,0:T(8,128)S(1)} %pad_maximum_fusion.5), channel_id=1, source_target_pairs={{0,4},{2,6},{4,0},{6,2},{8,12},{10,14},{12,8},{14,10},{16,20},{18,... | collective-permute-start | bytes 393224 | tf_op jit(solution)/shard_map/ppermute | solution.py:92
  39.0 2.9 %collective-permute-done.6 = f32[256,128]{1,0:T(8,128)S(1)} collective-permute-done((f32[256,128]{1,0:T(8,128)S(1)}, f32[256,128]{1,0:T(8,128)S(1)}, u32[]{:S(2)}, u32[]{:S(2)}) %collective-permute-start.6) | collective-permute-done | bytes 131104 | tf_op jit(solution)/shard_map/ppermute | solution.py:92
  42.0 1.8 %collective-permute-done.13 = f32[256,128]{1,0:T(8,128)S(1)} collective-permute-done((f32[256,128]{1,0:T(8,128)S(1)}, f32[256,128]{1,0:T(8,128)S(1)}, u32[]{:S(2)}, u32[]{:S(2)}) %collective-permute-start.13) | collective-permute-done | bytes 131104 | tf_op jit(solution)/shard_map/ppermute | solution.py:92
  44.4 1.0 %convolution_bitcast_fusion.1 = f32[1024,128]{1,0:T(8,128)S(1)} fusion(f32[64,128]{1,0:T(8,128)S(1)} %fusion.9, f32[1024,64]{0,1:T(8,128)S(1)} %copy-done.3), kind=kOutput, calls=%fused_computation.8 | convolution fusion | flops 100663296 | bytes 819200 | tf_op jit(solution)/shard_map/dot_general | solution.py:8
  46.6 1.0 %convolution_bitcast_fusion = f32[1024,128]{1,0:T(8,128)S(1)} fusion(f32[64,128]{1,0:T(8,128)S(1)} %fusion.13, f32[1024,64]{0,1:T(8,128)S(1)} %copy-done.3), kind=kOutput, calls=%fused_computation.7 | convolution fusion | flops 100663296 | bytes 819200 | tf_op jit(solution)/shard_map/dot_general | solution.py:8
  47.8 1.3 %collective-permute-start.16 = (f32[256,128]{1,0:T(8,128)S(1)}, f32[256,128]{1,0:T(8,128)S(1)}, u32[]{:S(2)}, u32[]{:S(2)}) collective-permute-start(f32[256,128]{1,0:T(8,128)S(1)} %constant_dynamic-slice_fusion.4), channel_id=1, source_target_pairs={{0,4},{2,6},{4,0},{6,2},{8,12},{10,14},{12,8},{14,10},{16,20},{18,... | collective-permute-start | bytes 393224 | tf_op jit(solution)/shard_map/ppermute | solution.py:78
  49.9 3.9 %collective-permute-done.16 = f32[256,128]{1,0:T(8,128)S(1)} collective-permute-done((f32[256,128]{1,0:T(8,128)S(1)}, f32[256,128]{1,0:T(8,128)S(1)}, u32[]{:S(2)}, u32[]{:S(2)}) %collective-permute-start.16) | collective-permute-done | bytes 131104 | tf_op jit(solution)/shard_map/ppermute | solution.py:78
  55.0 1.3 %collective-permute-start.24 = (f32[128,128]{1,0:T(8,128)S(1)}, f32[128,128]{1,0:T(8,128)S(1)}, u32[]{:S(2)}, u32[]{:S(2)}) collective-permute-start(f32[128,128]{1,0:T(8,128)S(1)} %constant_dynamic-slice_fusion), channel_id=1, source_target_pairs={{0,4},{2,6},{4,0},{6,2},{8,12},{10,14},{12,8},{14,10},{16,20},{18,... | collective-permute-start | bytes 196616 | tf_op jit(solution)/shard_map/ppermute | solution.py:78
  56.3 1.9 %collective-permute-done.17 = f32[128,128]{1,0:T(8,128)S(1)} collective-permute-done((f32[128,128]{1,0:T(8,128)S(1)}, f32[128,128]{1,0:T(8,128)S(1)}, u32[]{:S(2)}, u32[]{:S(2)}) %collective-permute-start.17) | collective-permute-done | bytes 65568 | tf_op jit(solution)/shard_map/ppermute | solution.py:78
  58.2 1.3 %collective-permute-start.18 = (f32[128,128]{1,0:T(8,128)S(1)}, f32[128,128]{1,0:T(8,128)S(1)}, u32[]{:S(2)}, u32[]{:S(2)}) collective-permute-start(f32[128,128]{1,0:T(8,128)S(1)} %dynamic-slice_add_fusion.9), channel_id=1, source_target_pairs={{0,16},{2,18},{4,20},{6,22},{8,24},{10,26},{12,28},{14,30},{16,0},... | collective-permute-start | bytes 196616 | tf_op jit(solution)/shard_map/ppermute | solution.py:86
  59.4 1.8 %collective-permute-start.25 = (f32[128,128]{1,0:T(8,128)S(1)}, f32[128,128]{1,0:T(8,128)S(1)}, u32[]{:S(2)}, u32[]{:S(2)}) collective-permute-start(f32[128,128]{1,0:T(8,128)S(1)} %dynamic-slice_add_fusion.8), channel_id=1, source_target_pairs={{0,16},{2,18},{4,20},{6,22},{8,24},{10,26},{12,28},{14,30},{16,0},... | collective-permute-start | bytes 196616 | tf_op jit(solution)/shard_map/ppermute | solution.py:86
  61.2 3.0 %collective-permute-done.18 = f32[128,128]{1,0:T(8,128)S(1)} collective-permute-done((f32[128,128]{1,0:T(8,128)S(1)}, f32[128,128]{1,0:T(8,128)S(1)}, u32[]{:S(2)}, u32[]{:S(2)}) %collective-permute-start.18) | collective-permute-done | bytes 65568 | tf_op jit(solution)/shard_map/ppermute | solution.py:86
  64.3 1.2 %collective-permute-done.25 = f32[128,128]{1,0:T(8,128)S(1)} collective-permute-done((f32[128,128]{1,0:T(8,128)S(1)}, f32[128,128]{1,0:T(8,128)S(1)}, u32[]{:S(2)}, u32[]{:S(2)}) %collective-permute-start.25) | collective-permute-done | bytes 65568 | tf_op jit(solution)/shard_map/ppermute | solution.py:86
  65.5 1.7 %collective-permute-start.26 = (f32[128,128]{1,0:T(8,128)S(1)}, f32[128,128]{1,0:T(8,128)S(1)}, u32[]{:S(2)}, u32[]{:S(2)}) collective-permute-start(f32[128,128]{1,0:T(8,128)S(1)} %add_subtract_fusion), channel_id=1, source_target_pairs={{0,4},{2,6},{4,0},{6,2},{8,12},{10,14},{12,8},{14,10},{16,20},{18,... | collective-permute-start | bytes 196616 | tf_op jit(solution)/shard_map/ppermute | solution.py:92
  67.2 1.4 %collective-permute-done.19 = f32[128,128]{1,0:T(8,128)S(1)} collective-permute-done((f32[128,128]{1,0:T(8,128)S(1)}, f32[128,128]{1,0:T(8,128)S(1)}, u32[]{:S(2)}, u32[]{:S(2)}) %collective-permute-start.19) | collective-permute-done | bytes 65568 | tf_op jit(solution)/shard_map/ppermute | solution.py:92
  68.6 1.8 %collective-permute-start.20 = (f32[256,128]{1,0:T(8,128)S(1)}, f32[256,128]{1,0:T(8,128)S(1)}, u32[]{:S(2)}, u32[]{:S(2)}) collective-permute-start(f32[256,128]{1,0:T(8,128)S(1)} %pad_maximum_fusion.7), channel_id=1, source_target_pairs={{0,4},{2,6},{4,0},{6,2},{8,12},{10,14},{12,8},{14,10},{16,20},{18,... | collective-permute-start | bytes 393224 | tf_op jit(solution)/shard_map/ppermute | solution.py:92
  70.8 2.9 %collective-permute-done.20 = f32[256,128]{1,0:T(8,128)S(1)} collective-permute-done((f32[256,128]{1,0:T(8,128)S(1)}, f32[256,128]{1,0:T(8,128)S(1)}, u32[]{:S(2)}, u32[]{:S(2)}) %collective-permute-start.20) | collective-permute-done | bytes 131104 | tf_op jit(solution)/shard_map/ppermute | solution.py:92
  73.8 1.7 %collective-permute-done.27 = f32[256,128]{1,0:T(8,128)S(1)} collective-permute-done((f32[256,128]{1,0:T(8,128)S(1)}, f32[256,128]{1,0:T(8,128)S(1)}, u32[]{:S(2)}, u32[]{:S(2)}) %collective-permute-start.27) | collective-permute-done | bytes 131104 | tf_op jit(solution)/shard_map/ppermute | solution.py:92
  76.2 1.0 %collective-permute-done.28 = f32[512,128]{1,0:T(8,128)S(1)} collective-permute-done((f32[512,128]{1,0:T(8,128)S(1)}, f32[512,128]{1,0:T(8,128)S(1)}, u32[]{:S(2)}, u32[]{:S(2)}) %collective-permute-start.28) | collective-permute-done | bytes 262176 | tf_op jit(solution)/shard_map/ppermute | solution.py:92
  (107 shorter events, 9.2 us)
Async XLA Ops:
  0.0 9.5 %collective-permute-start = (f32[1,1,2,64,512]{4,3,2,1,0:T(8,128)}, f32[1,1,2,64,512]{4,3,2,1,0:T(8,128)S(1)}, u32[]{:S(2)}, u32[]{:S(2)}) collective-permute-start(f32[1,1,2,64,512]{4,3,2,1,0:T(8,128)} %bitcast.51), channel_id=1, source_target_pairs={{0,1},{1,0},{2,3},{3,2},{4,5},{5,4},{6,7},{7,6},{8,9},{9,8},{10,11... | collective-permute-start | bytes 786440 | tf_op jit(solution)/shard_map/ppermute | solution.py:34
  9.7 1.6 %collective-permute-start.1 = (f32[512,128]{1,0:T(8,128)S(1)}, f32[512,128]{1,0:T(8,128)S(1)}, u32[]{:S(2)}, u32[]{:S(2)}) collective-permute-start(f32[512,128]{1,0:T(8,128)S(1)} %constant_dynamic-slice_fusion.11), channel_id=1, source_target_pairs={{0,2},{2,0},{4,6},{6,4},{8,10},{10,8},{12,14},{14,12},{16,18},{18,... | collective-permute-start | bytes 786440 | tf_op jit(solution)/shard_map/ppermute | solution.py:78
  9.9 10.3 %copy-start.1 = (f32[2,1024,256]{2,1,0:T(8,128)S(1)}, f32[2,1024,256]{2,1,0:T(8,128)}, u32[]{:S(2)}) copy-start(f32[2,1024,256]{2,1,0:T(8,128)} %param.7) | copy-start | bytes 6291460
  9.9 3.3 %collective-permute-start.8 = (f32[512,128]{1,0:T(8,128)S(1)}, f32[512,128]{1,0:T(8,128)S(1)}, u32[]{:S(2)}, u32[]{:S(2)}) collective-permute-start(f32[512,128]{1,0:T(8,128)S(1)} %constant_dynamic-slice_fusion.8), channel_id=1, source_target_pairs={{0,2},{2,0},{4,6},{6,4},{8,10},{10,8},{12,14},{14,12},{16,18},{18,... | collective-permute-start | bytes 786440 | tf_op jit(solution)/shard_map/ppermute | solution.py:78
  11.4 9.6 %collective-permute-start.2 = (f32[256,128]{1,0:T(8,128)S(1)}, f32[256,128]{1,0:T(8,128)S(1)}, u32[]{:S(2)}, u32[]{:S(2)}) collective-permute-start(f32[256,128]{1,0:T(8,128)S(1)} %constant_dynamic-slice_fusion.10), channel_id=1, source_target_pairs={{0,4},{2,6},{4,0},{6,2},{8,12},{10,14},{12,8},{14,10},{16,20},{18,... | collective-permute-start | bytes 393224 | tf_op jit(solution)/shard_map/ppermute | solution.py:78
  13.2 7.1 %collective-permute-start.9 = (f32[256,128]{1,0:T(8,128)S(1)}, f32[256,128]{1,0:T(8,128)S(1)}, u32[]{:S(2)}, u32[]{:S(2)}) collective-permute-start(f32[256,128]{1,0:T(8,128)S(1)} %constant_dynamic-slice_fusion.7), channel_id=1, source_target_pairs={{0,8},{2,10},{4,12},{6,14},{8,0},{10,2},{12,4},{14,6},{16,24},{18,... | collective-permute-start | bytes 393224 | tf_op jit(solution)/shard_map/ppermute | solution.py:78
  20.4 8.0 %collective-permute-start.10 = (f32[128,128]{1,0:T(8,128)S(1)}, f32[128,128]{1,0:T(8,128)S(1)}, u32[]{:S(2)}, u32[]{:S(2)}) collective-permute-start(f32[128,128]{1,0:T(8,128)S(1)} %constant_dynamic-slice_fusion.6), channel_id=1, source_target_pairs={{0,4},{2,6},{4,0},{6,2},{8,12},{10,14},{12,8},{14,10},{16,20},{18,... | collective-permute-start | bytes 196616 | tf_op jit(solution)/shard_map/ppermute | solution.py:78
  21.1 4.3 %collective-permute-start.3 = (f32[128,128]{1,0:T(8,128)S(1)}, f32[128,128]{1,0:T(8,128)S(1)}, u32[]{:S(2)}, u32[]{:S(2)}) collective-permute-start(f32[128,128]{1,0:T(8,128)S(1)} %constant_dynamic-slice_fusion.9), channel_id=1, source_target_pairs={{0,8},{2,10},{4,12},{6,14},{8,0},{10,2},{12,4},{14,6},{16,24},{18,... | collective-permute-start | bytes 196616 | tf_op jit(solution)/shard_map/ppermute | solution.py:78
  21.5 10.9 %slice-start = ((f32[1024,256]{1,0:T(8,128)}), f32[1024,128]{1,0:T(8,128)S(1)}, s32[]{:S(2)}) async-start(f32[1024,256]{1,0:T(8,128)} %copy-done.2), calls=%async_computation | async-start | bytes 1048576 | tf_op jit(solution)/shard_map/slice | solution.py:142
  21.6 22.8 %copy-start.3 = (f32[1024,64]{0,1:T(8,128)S(1)}, f32[1024,64]{0,1:T(8,128)}, u32[]{:S(2)}) copy-start(f32[1024,64]{0,1:T(8,128)} %param.9) | copy-start | bytes 786436
  25.4 7.0 %collective-permute-start.4 = (f32[128,128]{1,0:T(8,128)S(1)}, f32[128,128]{1,0:T(8,128)S(1)}, u32[]{:S(2)}, u32[]{:S(2)}) collective-permute-start(f32[128,128]{1,0:T(8,128)S(1)} %dynamic-slice_add_fusion.11), channel_id=1, source_target_pairs={{0,16},{2,18},{4,20},{6,22},{8,24},{10,26},{12,28},{14,30},{16,0},... | collective-permute-start | bytes 196616 | tf_op jit(solution)/shard_map/ppermute | solution.py:86
  28.5 5.6 %collective-permute-start.11 = (f32[128,128]{1,0:T(8,128)S(1)}, f32[128,128]{1,0:T(8,128)S(1)}, u32[]{:S(2)}, u32[]{:S(2)}) collective-permute-start(f32[128,128]{1,0:T(8,128)S(1)} %dynamic-slice_add_fusion.10), channel_id=1, source_target_pairs={{0,16},{2,18},{4,20},{6,22},{8,24},{10,26},{12,28},{14,30},{16,0},... | collective-permute-start | bytes 196616 | tf_op jit(solution)/shard_map/ppermute | solution.py:86
  32.4 4.3 %collective-permute-start.5 = (f32[128,128]{1,0:T(8,128)S(1)}, f32[128,128]{1,0:T(8,128)S(1)}, u32[]{:S(2)}, u32[]{:S(2)}) collective-permute-start(f32[128,128]{1,0:T(8,128)S(1)} %add_subtract_fusion.3), channel_id=1, source_target_pairs={{0,8},{2,10},{4,12},{6,14},{8,0},{10,2},{12,4},{14,6},{16,24},{18,... | collective-permute-start | bytes 196616 | tf_op jit(solution)/shard_map/ppermute | solution.py:92
  34.1 4.6 %collective-permute-start.12 = (f32[128,128]{1,0:T(8,128)S(1)}, f32[128,128]{1,0:T(8,128)S(1)}, u32[]{:S(2)}, u32[]{:S(2)}) collective-permute-start(f32[128,128]{1,0:T(8,128)S(1)} %add_subtract_fusion.2), channel_id=1, source_target_pairs={{0,4},{2,6},{4,0},{6,2},{8,12},{10,14},{12,8},{14,10},{16,20},{18,... | collective-permute-start | bytes 196616 | tf_op jit(solution)/shard_map/ppermute | solution.py:92
  36.8 5.0 %collective-permute-start.6 = (f32[256,128]{1,0:T(8,128)S(1)}, f32[256,128]{1,0:T(8,128)S(1)}, u32[]{:S(2)}, u32[]{:S(2)}) collective-permute-start(f32[256,128]{1,0:T(8,128)S(1)} %pad_maximum_fusion.5), channel_id=1, source_target_pairs={{0,4},{2,6},{4,0},{6,2},{8,12},{10,14},{12,8},{14,10},{16,20},{18,... | collective-permute-start | bytes 393224 | tf_op jit(solution)/shard_map/ppermute | solution.py:92
  38.7 5.0 %collective-permute-start.13 = (f32[256,128]{1,0:T(8,128)S(1)}, f32[256,128]{1,0:T(8,128)S(1)}, u32[]{:S(2)}, u32[]{:S(2)}) collective-permute-start(f32[256,128]{1,0:T(8,128)S(1)} %pad_maximum_fusion.6), channel_id=1, source_target_pairs={{0,8},{2,10},{4,12},{6,14},{8,0},{10,2},{12,4},{14,6},{16,24},{18,... | collective-permute-start | bytes 393224 | tf_op jit(solution)/shard_map/ppermute | solution.py:92
  41.9 2.0 %collective-permute-start.7 = (f32[512,128]{1,0:T(8,128)S(1)}, f32[512,128]{1,0:T(8,128)S(1)}, u32[]{:S(2)}, u32[]{:S(2)}) collective-permute-start(f32[512,128]{1,0:T(8,128)S(1)} %pad_maximum_fusion.1), channel_id=1, source_target_pairs={{0,2},{2,0},{4,6},{6,4},{8,10},{10,8},{12,14},{14,12},{16,18},{18,... | collective-permute-start | bytes 786440 | tf_op jit(solution)/shard_map/ppermute | solution.py:92
  43.8 2.2 %collective-permute-start.14 = (f32[512,128]{1,0:T(8,128)S(1)}, f32[512,128]{1,0:T(8,128)S(1)}, u32[]{:S(2)}, u32[]{:S(2)}) collective-permute-start(f32[512,128]{1,0:T(8,128)S(1)} %pad_maximum_fusion.2), channel_id=1, source_target_pairs={{0,2},{2,0},{4,6},{6,4},{8,10},{10,8},{12,14},{14,12},{16,18},{18,... | collective-permute-start | bytes 786440 | tf_op jit(solution)/shard_map/ppermute | solution.py:92
  45.5 2.2 %collective-permute-start.15 = (f32[512,128]{1,0:T(8,128)S(1)}, f32[512,128]{1,0:T(8,128)S(1)}, u32[]{:S(2)}, u32[]{:S(2)}) collective-permute-start(f32[512,128]{1,0:T(8,128)S(1)} %constant_dynamic-slice_fusion.5), channel_id=1, source_target_pairs={{0,2},{2,0},{4,6},{6,4},{8,10},{10,8},{12,14},{14,12},{16,18},{18,... | collective-permute-start | bytes 786440 | tf_op jit(solution)/shard_map/ppermute | solution.py:78
  47.7 1.6 %collective-permute-start.22 = (f32[512,128]{1,0:T(8,128)S(1)}, f32[512,128]{1,0:T(8,128)S(1)}, u32[]{:S(2)}, u32[]{:S(2)}) collective-permute-start(f32[512,128]{1,0:T(8,128)S(1)} %constant_dynamic-slice_fusion.2), channel_id=1, source_target_pairs={{0,2},{2,0},{4,6},{6,4},{8,10},{10,8},{12,14},{14,12},{16,18},{18,... | collective-permute-start | bytes 786440 | tf_op jit(solution)/shard_map/ppermute | solution.py:78
  47.8 6.0 %collective-permute-start.16 = (f32[256,128]{1,0:T(8,128)S(1)}, f32[256,128]{1,0:T(8,128)S(1)}, u32[]{:S(2)}, u32[]{:S(2)}) collective-permute-start(f32[256,128]{1,0:T(8,128)S(1)} %constant_dynamic-slice_fusion.4), channel_id=1, source_target_pairs={{0,4},{2,6},{4,0},{6,2},{8,12},{10,14},{12,8},{14,10},{16,20},{18,... | collective-permute-start | bytes 393224 | tf_op jit(solution)/shard_map/ppermute | solution.py:78
  49.3 5.6 %collective-permute-start.23 = (f32[256,128]{1,0:T(8,128)S(1)}, f32[256,128]{1,0:T(8,128)S(1)}, u32[]{:S(2)}, u32[]{:S(2)}) collective-permute-start(f32[256,128]{1,0:T(8,128)S(1)} %constant_dynamic-slice_fusion.1), channel_id=1, source_target_pairs={{0,8},{2,10},{4,12},{6,14},{8,0},{10,2},{12,4},{14,6},{16,24},{18,... | collective-permute-start | bytes 393224 | tf_op jit(solution)/shard_map/ppermute | solution.py:78
  53.8 4.3 %collective-permute-start.17 = (f32[128,128]{1,0:T(8,128)S(1)}, f32[128,128]{1,0:T(8,128)S(1)}, u32[]{:S(2)}, u32[]{:S(2)}) collective-permute-start(f32[128,128]{1,0:T(8,128)S(1)} %constant_dynamic-slice_fusion.3), channel_id=1, source_target_pairs={{0,8},{2,10},{4,12},{6,14},{8,0},{10,2},{12,4},{14,6},{16,24},{18,... | collective-permute-start | bytes 196616 | tf_op jit(solution)/shard_map/ppermute | solution.py:78
  55.0 4.4 %collective-permute-start.24 = (f32[128,128]{1,0:T(8,128)S(1)}, f32[128,128]{1,0:T(8,128)S(1)}, u32[]{:S(2)}, u32[]{:S(2)}) collective-permute-start(f32[128,128]{1,0:T(8,128)S(1)} %constant_dynamic-slice_fusion), channel_id=1, source_target_pairs={{0,4},{2,6},{4,0},{6,2},{8,12},{10,14},{12,8},{14,10},{16,20},{18,... | collective-permute-start | bytes 196616 | tf_op jit(solution)/shard_map/ppermute | solution.py:78
  58.2 6.1 %collective-permute-start.18 = (f32[128,128]{1,0:T(8,128)S(1)}, f32[128,128]{1,0:T(8,128)S(1)}, u32[]{:S(2)}, u32[]{:S(2)}) collective-permute-start(f32[128,128]{1,0:T(8,128)S(1)} %dynamic-slice_add_fusion.9), channel_id=1, source_target_pairs={{0,16},{2,18},{4,20},{6,22},{8,24},{10,26},{12,28},{14,30},{16,0},... | collective-permute-start | bytes 196616 | tf_op jit(solution)/shard_map/ppermute | solution.py:86
  59.4 6.1 %collective-permute-start.25 = (f32[128,128]{1,0:T(8,128)S(1)}, f32[128,128]{1,0:T(8,128)S(1)}, u32[]{:S(2)}, u32[]{:S(2)}) collective-permute-start(f32[128,128]{1,0:T(8,128)S(1)} %dynamic-slice_add_fusion.8), channel_id=1, source_target_pairs={{0,16},{2,18},{4,20},{6,22},{8,24},{10,26},{12,28},{14,30},{16,0},... | collective-permute-start | bytes 196616 | tf_op jit(solution)/shard_map/ppermute | solution.py:86
  64.3 4.3 %collective-permute-start.19 = (f32[128,128]{1,0:T(8,128)S(1)}, f32[128,128]{1,0:T(8,128)S(1)}, u32[]{:S(2)}, u32[]{:S(2)}) collective-permute-start(f32[128,128]{1,0:T(8,128)S(1)} %add_subtract_fusion.1), channel_id=1, source_target_pairs={{0,8},{2,10},{4,12},{6,14},{8,0},{10,2},{12,4},{14,6},{16,24},{18,... | collective-permute-start | bytes 196616 | tf_op jit(solution)/shard_map/ppermute | solution.py:92
  65.5 5.0 %collective-permute-start.26 = (f32[128,128]{1,0:T(8,128)S(1)}, f32[128,128]{1,0:T(8,128)S(1)}, u32[]{:S(2)}, u32[]{:S(2)}) collective-permute-start(f32[128,128]{1,0:T(8,128)S(1)} %add_subtract_fusion), channel_id=1, source_target_pairs={{0,4},{2,6},{4,0},{6,2},{8,12},{10,14},{12,8},{14,10},{16,20},{18,... | collective-permute-start | bytes 196616 | tf_op jit(solution)/shard_map/ppermute | solution.py:92
  68.6 5.0 %collective-permute-start.20 = (f32[256,128]{1,0:T(8,128)S(1)}, f32[256,128]{1,0:T(8,128)S(1)}, u32[]{:S(2)}, u32[]{:S(2)}) collective-permute-start(f32[256,128]{1,0:T(8,128)S(1)} %pad_maximum_fusion.7), channel_id=1, source_target_pairs={{0,4},{2,6},{4,0},{6,2},{8,12},{10,14},{12,8},{14,10},{16,20},{18,... | collective-permute-start | bytes 393224 | tf_op jit(solution)/shard_map/ppermute | solution.py:92
  70.5 5.0 %collective-permute-start.27 = (f32[256,128]{1,0:T(8,128)S(1)}, f32[256,128]{1,0:T(8,128)S(1)}, u32[]{:S(2)}, u32[]{:S(2)}) collective-permute-start(f32[256,128]{1,0:T(8,128)S(1)} %pad_maximum_fusion.8), channel_id=1, source_target_pairs={{0,8},{2,10},{4,12},{6,14},{8,0},{10,2},{12,4},{14,6},{16,24},{18,... | collective-permute-start | bytes 393224 | tf_op jit(solution)/shard_map/ppermute | solution.py:92
  73.7 2.0 %collective-permute-start.21 = (f32[512,128]{1,0:T(8,128)S(1)}, f32[512,128]{1,0:T(8,128)S(1)}, u32[]{:S(2)}, u32[]{:S(2)}) collective-permute-start(f32[512,128]{1,0:T(8,128)S(1)} %pad_maximum_fusion.3), channel_id=1, source_target_pairs={{0,2},{2,0},{4,6},{6,4},{8,10},{10,8},{12,14},{14,12},{16,18},{18,... | collective-permute-start | bytes 786440 | tf_op jit(solution)/shard_map/ppermute | solution.py:92
  75.6 1.6 %collective-permute-start.28 = (f32[512,128]{1,0:T(8,128)S(1)}, f32[512,128]{1,0:T(8,128)S(1)}, u32[]{:S(2)}, u32[]{:S(2)}) collective-permute-start(f32[512,128]{1,0:T(8,128)S(1)} %pad_maximum_fusion.4), channel_id=1, source_target_pairs={{0,2},{2,0},{4,6},{6,4},{8,10},{10,8},{12,14},{14,12},{16,18},{18,... | collective-permute-start | bytes 786440 | tf_op jit(solution)/shard_map/ppermute | solution.py:92
  (3 other events, 13.6 us)

commit v22 on v20

--- a/solution.py
+++ b/solution.py
@@ -151,8 +151,7 @@
                     panel_sum[chain] + product(coupling, block), right_side[1][:, cols], "blk", n, order
                 )
                 second_blocks.append(product(inverse_full[1], remains))
-            first_block = jnp.concatenate(first_blocks, 1)
-            second_block = jnp.concatenate(second_blocks, 1)
+            return jnp.concatenate([jnp.stack(pair) for pair in zip(first_blocks, second_blocks)], 2)
         else:
             inverse_full = jnp.concatenate(list(inverse_pieces), axis=2)
             first_part, panel_sum = sum_scatter(first_sum, panel_sum)

time: 76 us -> 75.9 us (level)
  no operation moved by 1% of the time
where the time goes in v22:
time: 75.9 us; the launch traced here: 75.8 us
  waiting for transfers between devices  30.6 us (40%)
  starting transfers between devices  28.3 us (37%)
  matrix products  12.6 us (17%)
  local copies, waits for them, and re-layouts  2.26 us (3%)
  other arithmetic  1.55 us (2%)
    ppermute x12, waiting for transfers between devices, ordered_reduce_then_gather(): got = lax.ppermute(y, axis, [(i, i ^ 1 << j) for i in range(n)])  15.2 us
    dot_general x8, matrix products, product(): jnp.dot(left, right, precision=lax.Precision.HIGHEST, preferred_element_t...  12.6 us
    ppermute x12, starting transfers between devices, ordered_reduce_then_gather(): got = lax.ppermute(send, axis, [(i, i ^ 1 << j) for i in range(n)])  11.5 us
    ppermute x12, waiting for transfers between devices, ordered_reduce_then_gather(): got = lax.ppermute(send, axis, [(i, i ^ 1 << j) for i in range(n)])  8.08 us
    ppermute x4, waiting for transfers between devices, ordered_reduce_then_gather(): y = y + lax.ppermute(y, axis, [(i, i ^ 1 << top) for i in range(n)])  7.31 us
    ppermute x4, starting transfers between devices, ordered_reduce_then_gather(): y = y + lax.ppermute(y, axis, [(i, i ^ 1 << top) for i in range(n)])  7.05 us
    ppermute x12, starting transfers between devices, ordered_reduce_then_gather(): got = lax.ppermute(y, axis, [(i, i ^ 1 << j) for i in range(n)])  6.85 us
    ppermute x1, starting transfers between devices, doubling_gather(): got = lax.ppermute(y, axis, [(i, i ^ 1 << j) for i in range(n)])  2.94 us
  transfers between devices with their start and end apart: 29, of which 20 were waited for; matrix products, arithmetic and copies ran while one was open for 20% of the time, Pallas kernels for 0%

profile of v22, /device:TPU:0, one launch (start us, length us, event | category | flops | bytes accessed | tf_op | source)
XLA Modules:
  0.0 75.8 jit_solution(18044331616900820874)
XLA Ops:
  0.0 2.9 %collective-permute-start = (f32[1,1,2,64,512]{4,3,2,1,0:T(8,128)}, f32[1,1,2,64,512]{4,3,2,1,0:T(8,128)S(1)}, u32[]{:S(2)}, u32[]{:S(2)}) collective-permute-start(f32[1,1,2,64,512]{4,3,2,1,0:T(8,128)} %bitcast.55), channel_id=1, source_target_pairs={{0,1},{1,0},{2,3},{3,2},{4,5},{5,4},{6,7},{7,6},{8,9},{9,8},{10,11... | collective-permute-start | bytes 786440 | tf_op jit(solution)/shard_map/ppermute | solution.py:34
  2.9 1.7 %slice_bitcast_fusion = (f32[1024,256]{1,0:T(8,128)S(1)}, f32[1024,256]{1,0:T(8,128)S(1)}) fusion(f32[2,1024,256]{2,1,0:T(8,128)} %param.7), kind=kLoop, calls=%fused_computation.11 | loop fusion | bytes 4194304 | tf_op jit(solution)/shard_map/squeeze | solution.py:151
  4.7 5.4 %fusion.2 = f32[1024,256]{1,0:T(8,128)S(1)} fusion(f32[1024,256]{1,0:T(8,128)S(1)} %copy-done, f32[2,1024,1024]{2,1,0:T(8,128)} %param.5), kind=kOutput, calls=%fused_computation.2 | convolution fusion | flops 3221225472 | bytes 6291456 | tf_op jit(solution)/shard_map/dot_general | solution.py:8
  12.0 1.6 %collective-permute-start.2 = (f32[256,128]{1,0:T(8,128)S(1)}, f32[256,128]{1,0:T(8,128)S(1)}, u32[]{:S(2)}, u32[]{:S(2)}) collective-permute-start(f32[256,128]{1,0:T(8,128)S(1)} %constant_dynamic-slice_fusion.10), channel_id=1, source_target_pairs={{0,4},{2,6},{4,0},{6,2},{8,12},{10,14},{12,8},{14,10},{16,20},{18,... | collective-permute-start | bytes 393224 | tf_op jit(solution)/shard_map/ppermute | solution.py:78
  13.7 1.6 %collective-permute-start.16 = (f32[256,128]{1,0:T(8,128)S(1)}, f32[256,128]{1,0:T(8,128)S(1)}, u32[]{:S(2)}, u32[]{:S(2)}) collective-permute-start(f32[256,128]{1,0:T(8,128)S(1)} %constant_dynamic-slice_fusion.4), channel_id=1, source_target_pairs={{0,8},{2,10},{4,12},{6,14},{8,0},{10,2},{12,4},{14,6},{16,24},{18,... | collective-permute-start | bytes 393224 | tf_op jit(solution)/shard_map/ppermute | solution.py:78
  15.3 3.5 %fusion.6 = f32[1024,256]{1,0:T(8,128)S(1)} fusion(f32[1024,256]{1,0:T(8,128)S(1)} %copy-done, f32[2,1024,1024]{2,1,0:T(8,128)S(1)} %bitcast.52), kind=kOutput, calls=%fused_computation.6 | convolution fusion | flops 3221225472 | bytes 6291456 | tf_op jit(solution)/shard_map/dot_general | solution.py:8
  19.9 1.6 %collective-permute-start.3 = (f32[128,128]{1,0:T(8,128)S(1)}, f32[128,128]{1,0:T(8,128)S(1)}, u32[]{:S(2)}, u32[]{:S(2)}) collective-permute-start(f32[128,128]{1,0:T(8,128)S(1)} %constant_dynamic-slice_fusion.9), channel_id=1, source_target_pairs={{0,8},{2,10},{4,12},{6,14},{8,0},{10,2},{12,4},{14,6},{16,24},{18,... | collective-permute-start | bytes 196616 | tf_op jit(solution)/shard_map/ppermute | solution.py:78
  21.6 1.8 %collective-permute-done.17 = f32[128,128]{1,0:T(8,128)S(1)} collective-permute-done((f32[128,128]{1,0:T(8,128)S(1)}, f32[128,128]{1,0:T(8,128)S(1)}, u32[]{:S(2)}, u32[]{:S(2)}) %collective-permute-start.17) | collective-permute-done | bytes 65568 | tf_op jit(solution)/shard_map/ppermute | solution.py:78
  23.4 2.7 %collective-permute-start.18 = (f32[128,128]{1,0:T(8,128)S(1)}, f32[128,128]{1,0:T(8,128)S(1)}, u32[]{:S(2)}, u32[]{:S(2)}) collective-permute-start(f32[128,128]{1,0:T(8,128)S(1)} %dynamic-slice_add_fusion.9), channel_id=1, source_target_pairs={{0,16},{2,18},{4,20},{6,22},{8,24},{10,26},{12,28},{14,30},{16,0},... | collective-permute-start | bytes 196616 | tf_op jit(solution)/shard_map/ppermute | solution.py:86
  26.1 1.3 %collective-permute-start.4 = (f32[128,128]{1,0:T(8,128)S(1)}, f32[128,128]{1,0:T(8,128)S(1)}, u32[]{:S(2)}, u32[]{:S(2)}) collective-permute-start(f32[128,128]{1,0:T(8,128)S(1)} %dynamic-slice_add_fusion.11), channel_id=1, source_target_pairs={{0,16},{2,18},{4,20},{6,22},{8,24},{10,26},{12,28},{14,30},{16,0},... | collective-permute-start | bytes 196616 | tf_op jit(solution)/shard_map/ppermute | solution.py:86
  27.4 3.1 %collective-permute-done.18 = f32[128,128]{1,0:T(8,128)S(1)} collective-permute-done((f32[128,128]{1,0:T(8,128)S(1)}, f32[128,128]{1,0:T(8,128)S(1)}, u32[]{:S(2)}, u32[]{:S(2)}) %collective-permute-start.18) | collective-permute-done | bytes 65568 | tf_op jit(solution)/shard_map/ppermute | solution.py:86
  31.3 2.1 %collective-permute-start.5 = (f32[128,128]{1,0:T(8,128)S(1)}, f32[128,128]{1,0:T(8,128)S(1)}, u32[]{:S(2)}, u32[]{:S(2)}) collective-permute-start(f32[128,128]{1,0:T(8,128)S(1)} %add_subtract_fusion.3), channel_id=1, source_target_pairs={{0,8},{2,10},{4,12},{6,14},{8,0},{10,2},{12,4},{14,6},{16,24},{18,... | collective-permute-start | bytes 196616 | tf_op jit(solution)/shard_map/ppermute | solution.py:90
  33.4 1.4 %collective-permute-done.19 = f32[128,128]{1,0:T(8,128)S(1)} collective-permute-done((f32[128,128]{1,0:T(8,128)S(1)}, f32[128,128]{1,0:T(8,128)S(1)}, u32[]{:S(2)}, u32[]{:S(2)}) %collective-permute-start.19) | collective-permute-done | bytes 65568 | tf_op jit(solution)/shard_map/ppermute | solution.py:90
  34.9 0.9 %collective-permute-done.5 = f32[128,128]{1,0:T(8,128)S(1)} collective-permute-done((f32[128,128]{1,0:T(8,128)S(1)}, f32[128,128]{1,0:T(8,128)S(1)}, u32[]{:S(2)}, u32[]{:S(2)}) %collective-permute-start.5) | collective-permute-done | bytes 65568 | tf_op jit(solution)/shard_map/ppermute | solution.py:90
  35.9 1.2 %collective-permute-start.6 = (f32[256,128]{1,0:T(8,128)S(1)}, f32[256,128]{1,0:T(8,128)S(1)}, u32[]{:S(2)}, u32[]{:S(2)}) collective-permute-start(f32[256,128]{1,0:T(8,128)S(1)} %pad_maximum_fusion.5), channel_id=1, source_target_pairs={{0,4},{2,6},{4,0},{6,2},{8,12},{10,14},{12,8},{14,10},{16,20},{18,... | collective-permute-start | bytes 393224 | tf_op jit(solution)/shard_map/ppermute | solution.py:90
  37.0 2.9 %collective-permute-done.20 = f32[256,128]{1,0:T(8,128)S(1)} collective-permute-done((f32[256,128]{1,0:T(8,128)S(1)}, f32[256,128]{1,0:T(8,128)S(1)}, u32[]{:S(2)}, u32[]{:S(2)}) %collective-permute-start.20) | collective-permute-done | bytes 131104 | tf_op jit(solution)/shard_map/ppermute | solution.py:90
  40.0 0.9 %collective-permute-done.6 = f32[256,128]{1,0:T(8,128)S(1)} collective-permute-done((f32[256,128]{1,0:T(8,128)S(1)}, f32[256,128]{1,0:T(8,128)S(1)}, u32[]{:S(2)}, u32[]{:S(2)}) %collective-permute-start.6) | collective-permute-done | bytes 131104 | tf_op jit(solution)/shard_map/ppermute | solution.py:90
  42.0 1.0 %convolution_bitcast_fusion = f32[1024,128]{1,0:T(8,128)S(1)} fusion(f32[64,128]{1,0:T(8,128)S(1)} %fusion.16, f32[1024,64]{0,1:T(8,128)S(1)} %copy-done.1), kind=kOutput, calls=%fused_computation.7 | convolution fusion | flops 100663296 | bytes 819200 | tf_op jit(solution)/shard_map/dot_general | solution.py:8
  43.8 1.0 %convolution_bitcast_fusion.1 = f32[1024,128]{1,0:T(8,128)S(1)} fusion(f32[64,128]{1,0:T(8,128)S(1)} %fusion.9, f32[1024,64]{0,1:T(8,128)S(1)} %copy-done.1), kind=kOutput, calls=%fused_computation.8 | convolution fusion | flops 100663296 | bytes 819200 | tf_op jit(solution)/shard_map/dot_general | solution.py:8
  45.4 1.4 %collective-permute-start.23 = (f32[256,128]{1,0:T(8,128)S(1)}, f32[256,128]{1,0:T(8,128)S(1)}, u32[]{:S(2)}, u32[]{:S(2)}) collective-permute-start(f32[256,128]{1,0:T(8,128)S(1)} %constant_dynamic-slice_fusion.1), channel_id=1, source_target_pairs={{0,8},{2,10},{4,12},{6,14},{8,0},{10,2},{12,4},{14,6},{16,24},{18,... | collective-permute-start | bytes 393224 | tf_op jit(solution)/shard_map/ppermute | solution.py:78
  47.6 3.4 %collective-permute-done.23 = f32[256,128]{1,0:T(8,128)S(1)} collective-permute-done((f32[256,128]{1,0:T(8,128)S(1)}, f32[256,128]{1,0:T(8,128)S(1)}, u32[]{:S(2)}, u32[]{:S(2)}) %collective-permute-start.23) | collective-permute-done | bytes 131104 | tf_op jit(solution)/shard_map/ppermute | solution.py:78
  51.1 1.1 %collective-permute-start.24 = (f32[128,128]{1,0:T(8,128)S(1)}, f32[128,128]{1,0:T(8,128)S(1)}, u32[]{:S(2)}, u32[]{:S(2)}) collective-permute-start(f32[128,128]{1,0:T(8,128)S(1)} %constant_dynamic-slice_fusion), channel_id=1, source_target_pairs={{0,4},{2,6},{4,0},{6,2},{8,12},{10,14},{12,8},{14,10},{16,20},{18,... | collective-permute-start | bytes 196616 | tf_op jit(solution)/shard_map/ppermute | solution.py:78
  52.6 1.4 %collective-permute-start.10 = (f32[128,128]{1,0:T(8,128)S(1)}, f32[128,128]{1,0:T(8,128)S(1)}, u32[]{:S(2)}, u32[]{:S(2)}) collective-permute-start(f32[128,128]{1,0:T(8,128)S(1)} %constant_dynamic-slice_fusion.6), channel_id=1, source_target_pairs={{0,8},{2,10},{4,12},{6,14},{8,0},{10,2},{12,4},{14,6},{16,24},{18,... | collective-permute-start | bytes 196616 | tf_op jit(solution)/shard_map/ppermute | solution.py:78
  54.0 1.4 %collective-permute-done.24 = f32[128,128]{1,0:T(8,128)S(1)} collective-permute-done((f32[128,128]{1,0:T(8,128)S(1)}, f32[128,128]{1,0:T(8,128)S(1)}, u32[]{:S(2)}, u32[]{:S(2)}) %collective-permute-start.24) | collective-permute-done | bytes 65568 | tf_op jit(solution)/shard_map/ppermute | solution.py:78
  55.4 1.9 %collective-permute-start.25 = (f32[128,128]{1,0:T(8,128)S(1)}, f32[128,128]{1,0:T(8,128)S(1)}, u32[]{:S(2)}, u32[]{:S(2)}) collective-permute-start(f32[128,128]{1,0:T(8,128)S(1)} %dynamic-slice_add_fusion.8), channel_id=1, source_target_pairs={{0,16},{2,18},{4,20},{6,22},{8,24},{10,26},{12,28},{14,30},{16,0},... | collective-permute-start | bytes 196616 | tf_op jit(solution)/shard_map/ppermute | solution.py:86
  57.4 1.2 %collective-permute-start.11 = (f32[128,128]{1,0:T(8,128)S(1)}, f32[128,128]{1,0:T(8,128)S(1)}, u32[]{:S(2)}, u32[]{:S(2)}) collective-permute-start(f32[128,128]{1,0:T(8,128)S(1)} %dynamic-slice_add_fusion.10), channel_id=1, source_target_pairs={{0,16},{2,18},{4,20},{6,22},{8,24},{10,26},{12,28},{14,30},{16,0},... | collective-permute-start | bytes 196616 | tf_op jit(solution)/shard_map/ppermute | solution.py:86
  58.6 3.6 %collective-permute-done.25 = f32[128,128]{1,0:T(8,128)S(1)} collective-permute-done((f32[128,128]{1,0:T(8,128)S(1)}, f32[128,128]{1,0:T(8,128)S(1)}, u32[]{:S(2)}, u32[]{:S(2)}) %collective-permute-start.25) | collective-permute-done | bytes 65568 | tf_op jit(solution)/shard_map/ppermute | solution.py:86
  64.2 2.4 %collective-permute-done.26 = f32[128,128]{1,0:T(8,128)S(1)} collective-permute-done((f32[128,128]{1,0:T(8,128)S(1)}, f32[128,128]{1,0:T(8,128)S(1)}, u32[]{:S(2)}, u32[]{:S(2)}) %collective-permute-start.26) | collective-permute-done | bytes 65568 | tf_op jit(solution)/shard_map/ppermute | solution.py:90
  66.8 1.1 %collective-permute-done.12 = f32[128,128]{1,0:T(8,128)S(1)} collective-permute-done((f32[128,128]{1,0:T(8,128)S(1)}, f32[128,128]{1,0:T(8,128)S(1)}, u32[]{:S(2)}, u32[]{:S(2)}) %collective-permute-start.12) | collective-permute-done | bytes 65568 | tf_op jit(solution)/shard_map/ppermute | solution.py:90
  68.8 2.8 %collective-permute-done.27 = f32[256,128]{1,0:T(8,128)S(1)} collective-permute-done((f32[256,128]{1,0:T(8,128)S(1)}, f32[256,128]{1,0:T(8,128)S(1)}, u32[]{:S(2)}, u32[]{:S(2)}) %collective-permute-start.27) | collective-permute-done | bytes 131104 | tf_op jit(solution)/shard_map/ppermute | solution.py:90
  71.7 1.3 %collective-permute-done.13 = f32[256,128]{1,0:T(8,128)S(1)} collective-permute-done((f32[256,128]{1,0:T(8,128)S(1)}, f32[256,128]{1,0:T(8,128)S(1)}, u32[]{:S(2)}, u32[]{:S(2)}) %collective-permute-start.13) | collective-permute-done | bytes 131104 | tf_op jit(solution)/shard_map/ppermute | solution.py:90
  73.7 0.9 %collective-permute-done.14 = f32[512,128]{1,0:T(8,128)S(1)} collective-permute-done((f32[512,128]{1,0:T(8,128)S(1)}, f32[512,128]{1,0:T(8,128)S(1)}, u32[]{:S(2)}, u32[]{:S(2)}) %collective-permute-start.14) | collective-permute-done | bytes 262176 | tf_op jit(solution)/shard_map/ppermute | solution.py:90
  (104 shorter events, 12.9 us)
Async XLA Ops:
  0.0 10.2 %collective-permute-start = (f32[1,1,2,64,512]{4,3,2,1,0:T(8,128)}, f32[1,1,2,64,512]{4,3,2,1,0:T(8,128)S(1)}, u32[]{:S(2)}, u32[]{:S(2)}) collective-permute-start(f32[1,1,2,64,512]{4,3,2,1,0:T(8,128)} %bitcast.55), channel_id=1, source_target_pairs={{0,1},{1,0},{2,3},{3,2},{4,5},{5,4},{6,7},{7,6},{8,9},{9,8},{10,11... | collective-permute-start | bytes 786440 | tf_op jit(solution)/shard_map/ppermute | solution.py:34
  4.6 5.5 %copy-start.2 = (f32[2,64,512]{2,1,0:T(8,128)S(1)}, f32[2,64,512]{2,1,0:T(8,128)}, u32[]{:S(2)}) copy-start(f32[2,64,512]{2,1,0:T(8,128)} %param.8) | copy-start | bytes 786436
  4.7 10.7 %slice-start = ((s8[8388608]{0:T(1024)(128)(4,1)}), s8[4194304]{0:T(1024)(128)(4,1)S(1)}, s32[]{:S(2)}) async-start(s8[8388608]{0:T(1024)(128)(4,1)} %bitcast.51), calls=%async_computation | async-start | bytes 8388608
  10.4 1.6 %collective-permute-start.1 = (f32[512,128]{1,0:T(8,128)S(1)}, f32[512,128]{1,0:T(8,128)S(1)}, u32[]{:S(2)}, u32[]{:S(2)}) collective-permute-start(f32[512,128]{1,0:T(8,128)S(1)} %constant_dynamic-slice_fusion.11), channel_id=1, source_target_pairs={{0,2},{2,0},{4,6},{6,4},{8,10},{10,8},{12,14},{14,12},{16,18},{18,... | collective-permute-start | bytes 786440 | tf_op jit(solution)/shard_map/ppermute | solution.py:78
  10.6 3.0 %collective-permute-start.15 = (f32[512,128]{1,0:T(8,128)S(1)}, f32[512,128]{1,0:T(8,128)S(1)}, u32[]{:S(2)}, u32[]{:S(2)}) collective-permute-start(f32[512,128]{1,0:T(8,128)S(1)} %constant_dynamic-slice_fusion.5), channel_id=1, source_target_pairs={{0,2},{2,0},{4,6},{6,4},{8,10},{10,8},{12,14},{14,12},{16,18},{18,... | collective-permute-start | bytes 786440 | tf_op jit(solution)/shard_map/ppermute | solution.py:78
  12.0 7.8 %collective-permute-start.2 = (f32[256,128]{1,0:T(8,128)S(1)}, f32[256,128]{1,0:T(8,128)S(1)}, u32[]{:S(2)}, u32[]{:S(2)}) collective-permute-start(f32[256,128]{1,0:T(8,128)S(1)} %constant_dynamic-slice_fusion.10), channel_id=1, source_target_pairs={{0,4},{2,6},{4,0},{6,2},{8,12},{10,14},{12,8},{14,10},{16,20},{18,... | collective-permute-start | bytes 393224 | tf_op jit(solution)/shard_map/ppermute | solution.py:78
  13.7 5.3 %collective-permute-start.16 = (f32[256,128]{1,0:T(8,128)S(1)}, f32[256,128]{1,0:T(8,128)S(1)}, u32[]{:S(2)}, u32[]{:S(2)}) collective-permute-start(f32[256,128]{1,0:T(8,128)S(1)} %constant_dynamic-slice_fusion.4), channel_id=1, source_target_pairs={{0,8},{2,10},{4,12},{6,14},{8,0},{10,2},{12,4},{14,6},{16,24},{18,... | collective-permute-start | bytes 393224 | tf_op jit(solution)/shard_map/ppermute | solution.py:78
  18.9 23.2 %copy-start.1 = (f32[1024,64]{0,1:T(8,128)S(1)}, f32[1024,64]{0,1:T(8,128)}, u32[]{:S(2)}) copy-start(f32[1024,64]{0,1:T(8,128)} %param.9) | copy-start | bytes 786436
  19.0 4.3 %collective-permute-start.17 = (f32[128,128]{1,0:T(8,128)S(1)}, f32[128,128]{1,0:T(8,128)S(1)}, u32[]{:S(2)}, u32[]{:S(2)}) collective-permute-start(f32[128,128]{1,0:T(8,128)S(1)} %constant_dynamic-slice_fusion.3), channel_id=1, source_target_pairs={{0,4},{2,6},{4,0},{6,2},{8,12},{10,14},{12,8},{14,10},{16,20},{18,... | collective-permute-start | bytes 196616 | tf_op jit(solution)/shard_map/ppermute | solution.py:78
  19.9 6.2 %collective-permute-start.3 = (f32[128,128]{1,0:T(8,128)S(1)}, f32[128,128]{1,0:T(8,128)S(1)}, u32[]{:S(2)}, u32[]{:S(2)}) collective-permute-start(f32[128,128]{1,0:T(8,128)S(1)} %constant_dynamic-slice_fusion.9), channel_id=1, source_target_pairs={{0,8},{2,10},{4,12},{6,14},{8,0},{10,2},{12,4},{14,6},{16,24},{18,... | collective-permute-start | bytes 196616 | tf_op jit(solution)/shard_map/ppermute | solution.py:78
  23.4 7.1 %collective-permute-start.18 = (f32[128,128]{1,0:T(8,128)S(1)}, f32[128,128]{1,0:T(8,128)S(1)}, u32[]{:S(2)}, u32[]{:S(2)}) collective-permute-start(f32[128,128]{1,0:T(8,128)S(1)} %dynamic-slice_add_fusion.9), channel_id=1, source_target_pairs={{0,16},{2,18},{4,20},{6,22},{8,24},{10,26},{12,28},{14,30},{16,0},... | collective-permute-start | bytes 196616 | tf_op jit(solution)/shard_map/ppermute | solution.py:86
  26.1 5.2 %collective-permute-start.4 = (f32[128,128]{1,0:T(8,128)S(1)}, f32[128,128]{1,0:T(8,128)S(1)}, u32[]{:S(2)}, u32[]{:S(2)}) collective-permute-start(f32[128,128]{1,0:T(8,128)S(1)} %dynamic-slice_add_fusion.11), channel_id=1, source_target_pairs={{0,16},{2,18},{4,20},{6,22},{8,24},{10,26},{12,28},{14,30},{16,0},... | collective-permute-start | bytes 196616 | tf_op jit(solution)/shard_map/ppermute | solution.py:86
  30.5 4.3 %collective-permute-start.19 = (f32[128,128]{1,0:T(8,128)S(1)}, f32[128,128]{1,0:T(8,128)S(1)}, u32[]{:S(2)}, u32[]{:S(2)}) collective-permute-start(f32[128,128]{1,0:T(8,128)S(1)} %add_subtract_fusion.1), channel_id=1, source_target_pairs={{0,4},{2,6},{4,0},{6,2},{8,12},{10,14},{12,8},{14,10},{16,20},{18,... | collective-permute-start | bytes 196616 | tf_op jit(solution)/shard_map/ppermute | solution.py:90
  31.3 4.5 %collective-permute-start.5 = (f32[128,128]{1,0:T(8,128)S(1)}, f32[128,128]{1,0:T(8,128)S(1)}, u32[]{:S(2)}, u32[]{:S(2)}) collective-permute-start(f32[128,128]{1,0:T(8,128)S(1)} %add_subtract_fusion.3), channel_id=1, source_target_pairs={{0,8},{2,10},{4,12},{6,14},{8,0},{10,2},{12,4},{14,6},{16,24},{18,... | collective-permute-start | bytes 196616 | tf_op jit(solution)/shard_map/ppermute | solution.py:90
  34.9 5.0 %collective-permute-start.20 = (f32[256,128]{1,0:T(8,128)S(1)}, f32[256,128]{1,0:T(8,128)S(1)}, u32[]{:S(2)}, u32[]{:S(2)}) collective-permute-start(f32[256,128]{1,0:T(8,128)S(1)} %pad_maximum_fusion.7), channel_id=1, source_target_pairs={{0,8},{2,10},{4,12},{6,14},{8,0},{10,2},{12,4},{14,6},{16,24},{18,... | collective-permute-start | bytes 393224 | tf_op jit(solution)/shard_map/ppermute | solution.py:90
  35.9 5.0 %collective-permute-start.6 = (f32[256,128]{1,0:T(8,128)S(1)}, f32[256,128]{1,0:T(8,128)S(1)}, u32[]{:S(2)}, u32[]{:S(2)}) collective-permute-start(f32[256,128]{1,0:T(8,128)S(1)} %pad_maximum_fusion.5), channel_id=1, source_target_pairs={{0,4},{2,6},{4,0},{6,2},{8,12},{10,14},{12,8},{14,10},{16,20},{18,... | collective-permute-start | bytes 393224 | tf_op jit(solution)/shard_map/ppermute | solution.py:90
  40.0 1.6 %collective-permute-start.21 = (f32[512,128]{1,0:T(8,128)S(1)}, f32[512,128]{1,0:T(8,128)S(1)}, u32[]{:S(2)}, u32[]{:S(2)}) collective-permute-start(f32[512,128]{1,0:T(8,128)S(1)} %pad_maximum_fusion.3), channel_id=1, source_target_pairs={{0,2},{2,0},{4,6},{6,4},{8,10},{10,8},{12,14},{14,12},{16,18},{18,... | collective-permute-start | bytes 786440 | tf_op jit(solution)/shard_map/ppermute | solution.py:90
  40.9 2.4 %collective-permute-start.7 = (f32[512,128]{1,0:T(8,128)S(1)}, f32[512,128]{1,0:T(8,128)S(1)}, u32[]{:S(2)}, u32[]{:S(2)}) collective-permute-start(f32[512,128]{1,0:T(8,128)S(1)} %pad_maximum_fusion.1), channel_id=1, source_target_pairs={{0,2},{2,0},{4,6},{6,4},{8,10},{10,8},{12,14},{14,12},{16,18},{18,... | collective-permute-start | bytes 786440 | tf_op jit(solution)/shard_map/ppermute | solution.py:90
  43.2 2.2 %collective-permute-start.22 = (f32[512,128]{1,0:T(8,128)S(1)}, f32[512,128]{1,0:T(8,128)S(1)}, u32[]{:S(2)}, u32[]{:S(2)}) collective-permute-start(f32[512,128]{1,0:T(8,128)S(1)} %constant_dynamic-slice_fusion.2), channel_id=1, source_target_pairs={{0,2},{2,0},{4,6},{6,4},{8,10},{10,8},{12,14},{14,12},{16,18},{18,... | collective-permute-start | bytes 786440 | tf_op jit(solution)/shard_map/ppermute | solution.py:78
  44.9 1.9 %collective-permute-start.8 = (f32[512,128]{1,0:T(8,128)S(1)}, f32[512,128]{1,0:T(8,128)S(1)}, u32[]{:S(2)}, u32[]{:S(2)}) collective-permute-start(f32[512,128]{1,0:T(8,128)S(1)} %constant_dynamic-slice_fusion.8), channel_id=1, source_target_pairs={{0,2},{2,0},{4,6},{6,4},{8,10},{10,8},{12,14},{14,12},{16,18},{18,... | collective-permute-start | bytes 786440 | tf_op jit(solution)/shard_map/ppermute | solution.py:78
  45.4 5.6 %collective-permute-start.23 = (f32[256,128]{1,0:T(8,128)S(1)}, f32[256,128]{1,0:T(8,128)S(1)}, u32[]{:S(2)}, u32[]{:S(2)}) collective-permute-start(f32[256,128]{1,0:T(8,128)S(1)} %constant_dynamic-slice_fusion.1), channel_id=1, source_target_pairs={{0,8},{2,10},{4,12},{6,14},{8,0},{10,2},{12,4},{14,6},{16,24},{18,... | collective-permute-start | bytes 393224 | tf_op jit(solution)/shard_map/ppermute | solution.py:78
  46.9 5.7 %collective-permute-start.9 = (f32[256,128]{1,0:T(8,128)S(1)}, f32[256,128]{1,0:T(8,128)S(1)}, u32[]{:S(2)}, u32[]{:S(2)}) collective-permute-start(f32[256,128]{1,0:T(8,128)S(1)} %constant_dynamic-slice_fusion.7), channel_id=1, source_target_pairs={{0,4},{2,6},{4,0},{6,2},{8,12},{10,14},{12,8},{14,10},{16,20},{18,... | collective-permute-start | bytes 393224 | tf_op jit(solution)/shard_map/ppermute | solution.py:78
  51.1 4.3 %collective-permute-start.24 = (f32[128,128]{1,0:T(8,128)S(1)}, f32[128,128]{1,0:T(8,128)S(1)}, u32[]{:S(2)}, u32[]{:S(2)}) collective-permute-start(f32[128,128]{1,0:T(8,128)S(1)} %constant_dynamic-slice_fusion), channel_id=1, source_target_pairs={{0,4},{2,6},{4,0},{6,2},{8,12},{10,14},{12,8},{14,10},{16,20},{18,... | collective-permute-start | bytes 196616 | tf_op jit(solution)/shard_map/ppermute | solution.py:78
  52.6 4.7 %collective-permute-start.10 = (f32[128,128]{1,0:T(8,128)S(1)}, f32[128,128]{1,0:T(8,128)S(1)}, u32[]{:S(2)}, u32[]{:S(2)}) collective-permute-start(f32[128,128]{1,0:T(8,128)S(1)} %constant_dynamic-slice_fusion.6), channel_id=1, source_target_pairs={{0,8},{2,10},{4,12},{6,14},{8,0},{10,2},{12,4},{14,6},{16,24},{18,... | collective-permute-start | bytes 196616 | tf_op jit(solution)/shard_map/ppermute | solution.py:78
  55.4 6.7 %collective-permute-start.25 = (f32[128,128]{1,0:T(8,128)S(1)}, f32[128,128]{1,0:T(8,128)S(1)}, u32[]{:S(2)}, u32[]{:S(2)}) collective-permute-start(f32[128,128]{1,0:T(8,128)S(1)} %dynamic-slice_add_fusion.8), channel_id=1, source_target_pairs={{0,16},{2,18},{4,20},{6,22},{8,24},{10,26},{12,28},{14,30},{16,0},... | collective-permute-start | bytes 196616 | tf_op jit(solution)/shard_map/ppermute | solution.py:86
  57.4 6.2 %collective-permute-start.11 = (f32[128,128]{1,0:T(8,128)S(1)}, f32[128,128]{1,0:T(8,128)S(1)}, u32[]{:S(2)}, u32[]{:S(2)}) collective-permute-start(f32[128,128]{1,0:T(8,128)S(1)} %dynamic-slice_add_fusion.10), channel_id=1, source_target_pairs={{0,16},{2,18},{4,20},{6,22},{8,24},{10,26},{12,28},{14,30},{16,0},... | collective-permute-start | bytes 196616 | tf_op jit(solution)/shard_map/ppermute | solution.py:86
  62.2 4.3 %collective-permute-start.26 = (f32[128,128]{1,0:T(8,128)S(1)}, f32[128,128]{1,0:T(8,128)S(1)}, u32[]{:S(2)}, u32[]{:S(2)}) collective-permute-start(f32[128,128]{1,0:T(8,128)S(1)} %add_subtract_fusion), channel_id=1, source_target_pairs={{0,4},{2,6},{4,0},{6,2},{8,12},{10,14},{12,8},{14,10},{16,20},{18,... | collective-permute-start | bytes 196616 | tf_op jit(solution)/shard_map/ppermute | solution.py:90
  63.6 4.3 %collective-permute-start.12 = (f32[128,128]{1,0:T(8,128)S(1)}, f32[128,128]{1,0:T(8,128)S(1)}, u32[]{:S(2)}, u32[]{:S(2)}) collective-permute-start(f32[128,128]{1,0:T(8,128)S(1)} %add_subtract_fusion.2), channel_id=1, source_target_pairs={{0,8},{2,10},{4,12},{6,14},{8,0},{10,2},{12,4},{14,6},{16,24},{18,... | collective-permute-start | bytes 196616 | tf_op jit(solution)/shard_map/ppermute | solution.py:90
  66.6 5.0 %collective-permute-start.27 = (f32[256,128]{1,0:T(8,128)S(1)}, f32[256,128]{1,0:T(8,128)S(1)}, u32[]{:S(2)}, u32[]{:S(2)}) collective-permute-start(f32[256,128]{1,0:T(8,128)S(1)} %pad_maximum_fusion.8), channel_id=1, source_target_pairs={{0,8},{2,10},{4,12},{6,14},{8,0},{10,2},{12,4},{14,6},{16,24},{18,... | collective-permute-start | bytes 393224 | tf_op jit(solution)/shard_map/ppermute | solution.py:90
  68.0 5.0 %collective-permute-start.13 = (f32[256,128]{1,0:T(8,128)S(1)}, f32[256,128]{1,0:T(8,128)S(1)}, u32[]{:S(2)}, u32[]{:S(2)}) collective-permute-start(f32[256,128]{1,0:T(8,128)S(1)} %pad_maximum_fusion.6), channel_id=1, source_target_pairs={{0,4},{2,6},{4,0},{6,2},{8,12},{10,14},{12,8},{14,10},{16,20},{18,... | collective-permute-start | bytes 393224 | tf_op jit(solution)/shard_map/ppermute | solution.py:90
  71.6 1.6 %collective-permute-start.28 = (f32[512,128]{1,0:T(8,128)S(1)}, f32[512,128]{1,0:T(8,128)S(1)}, u32[]{:S(2)}, u32[]{:S(2)}) collective-permute-start(f32[512,128]{1,0:T(8,128)S(1)} %pad_maximum_fusion.4), channel_id=1, source_target_pairs={{0,2},{2,0},{4,6},{6,4},{8,10},{10,8},{12,14},{14,12},{16,18},{18,... | collective-permute-start | bytes 786440 | tf_op jit(solution)/shard_map/ppermute | solution.py:90
  73.0 1.6 %collective-permute-start.14 = (f32[512,128]{1,0:T(8,128)S(1)}, f32[512,128]{1,0:T(8,128)S(1)}, u32[]{:S(2)}, u32[]{:S(2)}) collective-permute-start(f32[512,128]{1,0:T(8,128)S(1)} %pad_maximum_fusion.2), channel_id=1, source_target_pairs={{0,2},{2,0},{4,6},{6,4},{8,10},{10,8},{12,14},{14,12},{16,18},{18,... | collective-permute-start | bytes 786440 | tf_op jit(solution)/shard_map/ppermute | solution.py:90
  (2 other events, 9.8 us)

commit v23 on v20

--- a/solution.py
+++ b/solution.py
@@ -146,7 +146,7 @@
             inverse_full = jnp.concatenate(list(inverse_pieces), axis=2)
             first_blocks = [product(inverse_full[0], remains) for remains in first_blocks]
             second_blocks = []
-            for chain, (order, cols, block) in enumerate(zip(orders, columns, first_blocks)):
+            for chain, (order, cols, block) in enumerate(zip(orders[::-1], columns, first_blocks)):
                 remains, _ = ordered_reduce_then_gather(
                     panel_sum[chain] + product(coupling, block), right_side[1][:, cols], "blk", n, order
                 )

time: 76 us -> 75.7 us (level)
  waiting for transfers between devices: 30.6 us -> 29.2 us
  starting transfers between devices: 28.3 us -> 29.5 us
    ppermute x12, waiting for transfers between devices: 15.2 us -> 14 us  [ordered_reduce_then_gather(): got = lax.ppermute(y, axis, [(i, i ^ 1 << j) for i in range(n)])]
    ppermute x12, starting transfers between devices: 6.85 us -> 7.65 us  [ordered_reduce_then_gather(): got = lax.ppermute(y, axis, [(i, i ^ 1 << j) for i in range(n)])]
  transfers between devices with their start and end apart: 29 -> 29, of which waited for: 20 -> 19; matrix products, arithmetic and copies ran while one was open for 20% -> 20% of each run, Pallas kernels for 0% -> 0%
where the time goes in v23:
time: 75.7 us; the launch traced here: 75.6 us
  starting transfers between devices  29.5 us (39%)
  waiting for transfers between devices  29.2 us (39%)
  matrix products  12.6 us (17%)
  local copies, waits for them, and re-layouts  2.26 us (3%)
  other arithmetic  1.56 us (2%)
    ppermute x12, waiting for transfers between devices, ordered_reduce_then_gather(): got = lax.ppermute(y, axis, [(i, i ^ 1 << j) for i in range(n)])  14 us
    dot_general x8, matrix products, product(): jnp.dot(left, right, precision=lax.Precision.HIGHEST, preferred_element_t...  12.6 us
    ppermute x12, starting transfers between devices, ordered_reduce_then_gather(): got = lax.ppermute(send, axis, [(i, i ^ 1 << j) for i in range(n)])  11.5 us
    ppermute x12, waiting for transfers between devices, ordered_reduce_then_gather(): got = lax.ppermute(send, axis, [(i, i ^ 1 << j) for i in range(n)])  8 us
    ppermute x12, starting transfers between devices, ordered_reduce_then_gather(): got = lax.ppermute(y, axis, [(i, i ^ 1 << j) for i in range(n)])  7.65 us
    ppermute x4, starting transfers between devices, ordered_reduce_then_gather(): y = y + lax.ppermute(y, axis, [(i, i ^ 1 << top) for i in range(n)])  7.32 us
    ppermute x4, waiting for transfers between devices, ordered_reduce_then_gather(): y = y + lax.ppermute(y, axis, [(i, i ^ 1 << top) for i in range(n)])  7.18 us
    ppermute x1, starting transfers between devices, doubling_gather(): got = lax.ppermute(y, axis, [(i, i ^ 1 << j) for i in range(n)])  2.94 us
  transfers between devices with their start and end apart: 29, of which 19 were waited for; matrix products, arithmetic and copies ran while one was open for 20% of the time, Pallas kernels for 0%

profile of v23, /device:TPU:0, one launch (start us, length us, event | category | flops | bytes accessed | tf_op | source)
XLA Modules:
  0.0 75.6 jit_solution(11471005565289045956)
XLA Ops:
  0.0 2.9 %collective-permute-start = (f32[1,1,2,64,512]{4,3,2,1,0:T(8,128)}, f32[1,1,2,64,512]{4,3,2,1,0:T(8,128)S(1)}, u32[]{:S(2)}, u32[]{:S(2)}) collective-permute-start(f32[1,1,2,64,512]{4,3,2,1,0:T(8,128)} %bitcast.51), channel_id=1, source_target_pairs={{0,1},{1,0},{2,3},{3,2},{4,5},{5,4},{6,7},{7,6},{8,9},{9,8},{10,11... | collective-permute-start | bytes 786440 | tf_op jit(solution)/shard_map/ppermute | solution.py:34
  2.9 1.7 %slice_bitcast_fusion = (f32[1024,256]{1,0:T(8,128)S(1)}, f32[1024,256]{1,0:T(8,128)S(1)}) fusion(f32[2,1024,256]{2,1,0:T(8,128)} %param.7), kind=kLoop, calls=%fused_computation.9 | loop fusion | bytes 4194304 | tf_op jit(solution)/shard_map/squeeze | solution.py:151
  4.7 5.4 %fusion.2 = f32[1024,256]{1,0:T(8,128)S(1)} fusion(f32[1024,256]{1,0:T(8,128)S(1)} %copy-done, f32[2,1024,1024]{2,1,0:T(8,128)} %param.5), kind=kOutput, calls=%fused_computation.2 | convolution fusion | flops 3221225472 | bytes 6291456 | tf_op jit(solution)/shard_map/dot_general | solution.py:8
  11.1 0.9 %collective-permute-done.1 = f32[512,128]{1,0:T(8,128)S(1)} collective-permute-done((f32[512,128]{1,0:T(8,128)S(1)}, f32[512,128]{1,0:T(8,128)S(1)}, u32[]{:S(2)}, u32[]{:S(2)}) %collective-permute-start.1) | collective-permute-done | bytes 262176 | tf_op jit(solution)/shard_map/ppermute | solution.py:78
  12.0 1.6 %collective-permute-start.2 = (f32[256,128]{1,0:T(8,128)S(1)}, f32[256,128]{1,0:T(8,128)S(1)}, u32[]{:S(2)}, u32[]{:S(2)}) collective-permute-start(f32[256,128]{1,0:T(8,128)S(1)} %constant_dynamic-slice_fusion.10), channel_id=1, source_target_pairs={{0,4},{2,6},{4,0},{6,2},{8,12},{10,14},{12,8},{14,10},{16,20},{18,... | collective-permute-start | bytes 393224 | tf_op jit(solution)/shard_map/ppermute | solution.py:78
  13.7 1.6 %collective-permute-start.9 = (f32[256,128]{1,0:T(8,128)S(1)}, f32[256,128]{1,0:T(8,128)S(1)}, u32[]{:S(2)}, u32[]{:S(2)}) collective-permute-start(f32[256,128]{1,0:T(8,128)S(1)} %constant_dynamic-slice_fusion.7), channel_id=1, source_target_pairs={{0,8},{2,10},{4,12},{6,14},{8,0},{10,2},{12,4},{14,6},{16,24},{18,... | collective-permute-start | bytes 393224 | tf_op jit(solution)/shard_map/ppermute | solution.py:78
  15.3 3.5 %fusion.6 = f32[1024,256]{1,0:T(8,128)S(1)} fusion(f32[1024,256]{1,0:T(8,128)S(1)} %copy-done, f32[2,1024,1024]{2,1,0:T(8,128)S(1)} %bitcast.50), kind=kOutput, calls=%fused_computation.6 | convolution fusion | flops 3221225472 | bytes 6291456 | tf_op jit(solution)/shard_map/dot_general | solution.py:8
  19.9 1.6 %collective-permute-start.3 = (f32[128,128]{1,0:T(8,128)S(1)}, f32[128,128]{1,0:T(8,128)S(1)}, u32[]{:S(2)}, u32[]{:S(2)}) collective-permute-start(f32[128,128]{1,0:T(8,128)S(1)} %constant_dynamic-slice_fusion.9), channel_id=1, source_target_pairs={{0,8},{2,10},{4,12},{6,14},{8,0},{10,2},{12,4},{14,6},{16,24},{18,... | collective-permute-start | bytes 196616 | tf_op jit(solution)/shard_map/ppermute | solution.py:78
  21.6 1.8 %collective-permute-done.10 = f32[128,128]{1,0:T(8,128)S(1)} collective-permute-done((f32[128,128]{1,0:T(8,128)S(1)}, f32[128,128]{1,0:T(8,128)S(1)}, u32[]{:S(2)}, u32[]{:S(2)}) %collective-permute-start.10) | collective-permute-done | bytes 65568 | tf_op jit(solution)/shard_map/ppermute | solution.py:78
  23.4 2.7 %collective-permute-start.11 = (f32[128,128]{1,0:T(8,128)S(1)}, f32[128,128]{1,0:T(8,128)S(1)}, u32[]{:S(2)}, u32[]{:S(2)}) collective-permute-start(f32[128,128]{1,0:T(8,128)S(1)} %dynamic-slice_add_fusion.10), channel_id=1, source_target_pairs={{0,16},{2,18},{4,20},{6,22},{8,24},{10,26},{12,28},{14,30},{16,0},... | collective-permute-start | bytes 196616 | tf_op jit(solution)/shard_map/ppermute | solution.py:86
  26.1 1.3 %collective-permute-start.4 = (f32[128,128]{1,0:T(8,128)S(1)}, f32[128,128]{1,0:T(8,128)S(1)}, u32[]{:S(2)}, u32[]{:S(2)}) collective-permute-start(f32[128,128]{1,0:T(8,128)S(1)} %dynamic-slice_add_fusion.11), channel_id=1, source_target_pairs={{0,16},{2,18},{4,20},{6,22},{8,24},{10,26},{12,28},{14,30},{16,0},... | collective-permute-start | bytes 196616 | tf_op jit(solution)/shard_map/ppermute | solution.py:86
  27.4 3.1 %collective-permute-done.11 = f32[128,128]{1,0:T(8,128)S(1)} collective-permute-done((f32[128,128]{1,0:T(8,128)S(1)}, f32[128,128]{1,0:T(8,128)S(1)}, u32[]{:S(2)}, u32[]{:S(2)}) %collective-permute-start.11) | collective-permute-done | bytes 65568 | tf_op jit(solution)/shard_map/ppermute | solution.py:86
  31.3 2.1 %collective-permute-start.5 = (f32[128,128]{1,0:T(8,128)S(1)}, f32[128,128]{1,0:T(8,128)S(1)}, u32[]{:S(2)}, u32[]{:S(2)}) collective-permute-start(f32[128,128]{1,0:T(8,128)S(1)} %add_subtract_fusion.3), channel_id=1, source_target_pairs={{0,8},{2,10},{4,12},{6,14},{8,0},{10,2},{12,4},{14,6},{16,24},{18,... | collective-permute-start | bytes 196616 | tf_op jit(solution)/shard_map/ppermute | solution.py:90
  33.4 1.4 %collective-permute-done.12 = f32[128,128]{1,0:T(8,128)S(1)} collective-permute-done((f32[128,128]{1,0:T(8,128)S(1)}, f32[128,128]{1,0:T(8,128)S(1)}, u32[]{:S(2)}, u32[]{:S(2)}) %collective-permute-start.12) | collective-permute-done | bytes 65568 | tf_op jit(solution)/shard_map/ppermute | solution.py:90
  34.9 0.9 %collective-permute-done.5 = f32[128,128]{1,0:T(8,128)S(1)} collective-permute-done((f32[128,128]{1,0:T(8,128)S(1)}, f32[128,128]{1,0:T(8,128)S(1)}, u32[]{:S(2)}, u32[]{:S(2)}) %collective-permute-start.5) | collective-permute-done | bytes 65568 | tf_op jit(solution)/shard_map/ppermute | solution.py:90
  35.9 1.2 %collective-permute-start.6 = (f32[256,128]{1,0:T(8,128)S(1)}, f32[256,128]{1,0:T(8,128)S(1)}, u32[]{:S(2)}, u32[]{:S(2)}) collective-permute-start(f32[256,128]{1,0:T(8,128)S(1)} %pad_maximum_fusion.5), channel_id=1, source_target_pairs={{0,4},{2,6},{4,0},{6,2},{8,12},{10,14},{12,8},{14,10},{16,20},{18,... | collective-permute-start | bytes 393224 | tf_op jit(solution)/shard_map/ppermute | solution.py:90
  37.0 2.9 %collective-permute-done.13 = f32[256,128]{1,0:T(8,128)S(1)} collective-permute-done((f32[256,128]{1,0:T(8,128)S(1)}, f32[256,128]{1,0:T(8,128)S(1)}, u32[]{:S(2)}, u32[]{:S(2)}) %collective-permute-start.13) | collective-permute-done | bytes 131104 | tf_op jit(solution)/shard_map/ppermute | solution.py:90
  40.0 0.9 %collective-permute-done.6 = f32[256,128]{1,0:T(8,128)S(1)} collective-permute-done((f32[256,128]{1,0:T(8,128)S(1)}, f32[256,128]{1,0:T(8,128)S(1)}, u32[]{:S(2)}, u32[]{:S(2)}) %collective-permute-start.6) | collective-permute-done | bytes 131104 | tf_op jit(solution)/shard_map/ppermute | solution.py:90
  42.0 1.0 %convolution_bitcast_fusion = f32[1024,128]{1,0:T(8,128)S(1)} fusion(f32[64,128]{1,0:T(8,128)S(1)} %fusion.13, f32[1024,64]{0,1:T(8,128)S(1)} %copy-done.1), kind=kOutput, calls=%fused_computation.7 | convolution fusion | flops 100663296 | bytes 819200 | tf_op jit(solution)/shard_map/dot_general | solution.py:8
  43.8 1.0 %convolution_bitcast_fusion.1 = f32[1024,128]{1,0:T(8,128)S(1)} fusion(f32[64,128]{1,0:T(8,128)S(1)} %fusion.9, f32[1024,64]{0,1:T(8,128)S(1)} %copy-done.1), kind=kOutput, calls=%fused_computation.8 | convolution fusion | flops 100663296 | bytes 819200 | tf_op jit(solution)/shard_map/dot_general | solution.py:8
  46.6 1.7 %collective-permute-start.16 = (f32[256,128]{1,0:T(8,128)S(1)}, f32[256,128]{1,0:T(8,128)S(1)}, u32[]{:S(2)}, u32[]{:S(2)}) collective-permute-start(f32[256,128]{1,0:T(8,128)S(1)} %constant_dynamic-slice_fusion.4), channel_id=1, source_target_pairs={{0,8},{2,10},{4,12},{6,14},{8,0},{10,2},{12,4},{14,6},{16,24},{18,... | collective-permute-start | bytes 393224 | tf_op jit(solution)/shard_map/ppermute | solution.py:78
  48.3 2.7 %collective-permute-done.23 = f32[256,128]{1,0:T(8,128)S(1)} collective-permute-done((f32[256,128]{1,0:T(8,128)S(1)}, f32[256,128]{1,0:T(8,128)S(1)}, u32[]{:S(2)}, u32[]{:S(2)}) %collective-permute-start.23) | collective-permute-done | bytes 131104 | tf_op jit(solution)/shard_map/ppermute | solution.py:78
  51.1 1.7 %collective-permute-start.24 = (f32[128,128]{1,0:T(8,128)S(1)}, f32[128,128]{1,0:T(8,128)S(1)}, u32[]{:S(2)}, u32[]{:S(2)}) collective-permute-start(f32[128,128]{1,0:T(8,128)S(1)} %constant_dynamic-slice_fusion), channel_id=1, source_target_pairs={{0,8},{2,10},{4,12},{6,14},{8,0},{10,2},{12,4},{14,6},{16,24},{18,... | collective-permute-start | bytes 196616 | tf_op jit(solution)/shard_map/ppermute | solution.py:78
  53.3 2.1 %collective-permute-done.24 = f32[128,128]{1,0:T(8,128)S(1)} collective-permute-done((f32[128,128]{1,0:T(8,128)S(1)}, f32[128,128]{1,0:T(8,128)S(1)}, u32[]{:S(2)}, u32[]{:S(2)}) %collective-permute-start.24) | collective-permute-done | bytes 65568 | tf_op jit(solution)/shard_map/ppermute | solution.py:78
  55.4 1.9 %collective-permute-start.25 = (f32[128,128]{1,0:T(8,128)S(1)}, f32[128,128]{1,0:T(8,128)S(1)}, u32[]{:S(2)}, u32[]{:S(2)}) collective-permute-start(f32[128,128]{1,0:T(8,128)S(1)} %dynamic-slice_add_fusion.8), channel_id=1, source_target_pairs={{0,16},{2,18},{4,20},{6,22},{8,24},{10,26},{12,28},{14,30},{16,0},... | collective-permute-start | bytes 196616 | tf_op jit(solution)/shard_map/ppermute | solution.py:86
  57.4 1.5 %collective-permute-start.18 = (f32[128,128]{1,0:T(8,128)S(1)}, f32[128,128]{1,0:T(8,128)S(1)}, u32[]{:S(2)}, u32[]{:S(2)}) collective-permute-start(f32[128,128]{1,0:T(8,128)S(1)} %dynamic-slice_add_fusion.9), channel_id=1, source_target_pairs={{0,16},{2,18},{4,20},{6,22},{8,24},{10,26},{12,28},{14,30},{16,0},... | collective-permute-start | bytes 196616 | tf_op jit(solution)/shard_map/ppermute | solution.py:86
  58.8 3.3 %collective-permute-done.25 = f32[128,128]{1,0:T(8,128)S(1)} collective-permute-done((f32[128,128]{1,0:T(8,128)S(1)}, f32[128,128]{1,0:T(8,128)S(1)}, u32[]{:S(2)}, u32[]{:S(2)}) %collective-permute-start.25) | collective-permute-done | bytes 65568 | tf_op jit(solution)/shard_map/ppermute | solution.py:86
  64.0 2.6 %collective-permute-done.26 = f32[128,128]{1,0:T(8,128)S(1)} collective-permute-done((f32[128,128]{1,0:T(8,128)S(1)}, f32[128,128]{1,0:T(8,128)S(1)}, u32[]{:S(2)}, u32[]{:S(2)}) %collective-permute-start.26) | collective-permute-done | bytes 65568 | tf_op jit(solution)/shard_map/ppermute | solution.py:90
  66.6 1.1 %collective-permute-start.27 = (f32[256,128]{1,0:T(8,128)S(1)}, f32[256,128]{1,0:T(8,128)S(1)}, u32[]{:S(2)}, u32[]{:S(2)}) collective-permute-start(f32[256,128]{1,0:T(8,128)S(1)} %pad_maximum_fusion.8), channel_id=1, source_target_pairs={{0,4},{2,6},{4,0},{6,2},{8,12},{10,14},{12,8},{14,10},{16,20},{18,... | collective-permute-start | bytes 393224 | tf_op jit(solution)/shard_map/ppermute | solution.py:90
  67.7 1.1 %collective-permute-start.20 = (f32[256,128]{1,0:T(8,128)S(1)}, f32[256,128]{1,0:T(8,128)S(1)}, u32[]{:S(2)}, u32[]{:S(2)}) collective-permute-start(f32[256,128]{1,0:T(8,128)S(1)} %pad_maximum_fusion.7), channel_id=1, source_target_pairs={{0,8},{2,10},{4,12},{6,14},{8,0},{10,2},{12,4},{14,6},{16,24},{18,... | collective-permute-start | bytes 393224 | tf_op jit(solution)/shard_map/ppermute | solution.py:90
  68.8 2.8 %collective-permute-done.27 = f32[256,128]{1,0:T(8,128)S(1)} collective-permute-done((f32[256,128]{1,0:T(8,128)S(1)}, f32[256,128]{1,0:T(8,128)S(1)}, u32[]{:S(2)}, u32[]{:S(2)}) %collective-permute-start.27) | collective-permute-done | bytes 131104 | tf_op jit(solution)/shard_map/ppermute | solution.py:90
  71.7 1.0 %collective-permute-done.20 = f32[256,128]{1,0:T(8,128)S(1)} collective-permute-done((f32[256,128]{1,0:T(8,128)S(1)}, f32[256,128]{1,0:T(8,128)S(1)}, u32[]{:S(2)}, u32[]{:S(2)}) %collective-permute-start.20) | collective-permute-done | bytes 131104 | tf_op jit(solution)/shard_map/ppermute | solution.py:90
  (105 shorter events, 12.0 us)
Async XLA Ops:
  0.0 10.2 %collective-permute-start = (f32[1,1,2,64,512]{4,3,2,1,0:T(8,128)}, f32[1,1,2,64,512]{4,3,2,1,0:T(8,128)S(1)}, u32[]{:S(2)}, u32[]{:S(2)}) collective-permute-start(f32[1,1,2,64,512]{4,3,2,1,0:T(8,128)} %bitcast.51), channel_id=1, source_target_pairs={{0,1},{1,0},{2,3},{3,2},{4,5},{5,4},{6,7},{7,6},{8,9},{9,8},{10,11... | collective-permute-start | bytes 786440 | tf_op jit(solution)/shard_map/ppermute | solution.py:34
  4.6 5.5 %copy-start.2 = (f32[2,64,512]{2,1,0:T(8,128)S(1)}, f32[2,64,512]{2,1,0:T(8,128)}, u32[]{:S(2)}) copy-start(f32[2,64,512]{2,1,0:T(8,128)} %param.8) | copy-start | bytes 786436
  4.7 10.7 %slice-start = ((s8[8388608]{0:T(1024)(128)(4,1)}), s8[4194304]{0:T(1024)(128)(4,1)S(1)}, s32[]{:S(2)}) async-start(s8[8388608]{0:T(1024)(128)(4,1)} %bitcast.49), calls=%async_computation | async-start | bytes 8388608
  10.4 1.6 %collective-permute-start.1 = (f32[512,128]{1,0:T(8,128)S(1)}, f32[512,128]{1,0:T(8,128)S(1)}, u32[]{:S(2)}, u32[]{:S(2)}) collective-permute-start(f32[512,128]{1,0:T(8,128)S(1)} %constant_dynamic-slice_fusion.11), channel_id=1, source_target_pairs={{0,2},{2,0},{4,6},{6,4},{8,10},{10,8},{12,14},{14,12},{16,18},{18,... | collective-permute-start | bytes 786440 | tf_op jit(solution)/shard_map/ppermute | solution.py:78
  10.6 3.0 %collective-permute-start.8 = (f32[512,128]{1,0:T(8,128)S(1)}, f32[512,128]{1,0:T(8,128)S(1)}, u32[]{:S(2)}, u32[]{:S(2)}) collective-permute-start(f32[512,128]{1,0:T(8,128)S(1)} %constant_dynamic-slice_fusion.8), channel_id=1, source_target_pairs={{0,2},{2,0},{4,6},{6,4},{8,10},{10,8},{12,14},{14,12},{16,18},{18,... | collective-permute-start | bytes 786440 | tf_op jit(solution)/shard_map/ppermute | solution.py:78
  12.0 7.8 %collective-permute-start.2 = (f32[256,128]{1,0:T(8,128)S(1)}, f32[256,128]{1,0:T(8,128)S(1)}, u32[]{:S(2)}, u32[]{:S(2)}) collective-permute-start(f32[256,128]{1,0:T(8,128)S(1)} %constant_dynamic-slice_fusion.10), channel_id=1, source_target_pairs={{0,4},{2,6},{4,0},{6,2},{8,12},{10,14},{12,8},{14,10},{16,20},{18,... | collective-permute-start | bytes 393224 | tf_op jit(solution)/shard_map/ppermute | solution.py:78
  13.7 5.3 %collective-permute-start.9 = (f32[256,128]{1,0:T(8,128)S(1)}, f32[256,128]{1,0:T(8,128)S(1)}, u32[]{:S(2)}, u32[]{:S(2)}) collective-permute-start(f32[256,128]{1,0:T(8,128)S(1)} %constant_dynamic-slice_fusion.7), channel_id=1, source_target_pairs={{0,8},{2,10},{4,12},{6,14},{8,0},{10,2},{12,4},{14,6},{16,24},{18,... | collective-permute-start | bytes 393224 | tf_op jit(solution)/shard_map/ppermute | solution.py:78
  18.9 23.2 %copy-start.1 = (f32[1024,64]{0,1:T(8,128)S(1)}, f32[1024,64]{0,1:T(8,128)}, u32[]{:S(2)}) copy-start(f32[1024,64]{0,1:T(8,128)} %param.9) | copy-start | bytes 786436
  19.0 4.3 %collective-permute-start.10 = (f32[128,128]{1,0:T(8,128)S(1)}, f32[128,128]{1,0:T(8,128)S(1)}, u32[]{:S(2)}, u32[]{:S(2)}) collective-permute-start(f32[128,128]{1,0:T(8,128)S(1)} %constant_dynamic-slice_fusion.6), channel_id=1, source_target_pairs={{0,4},{2,6},{4,0},{6,2},{8,12},{10,14},{12,8},{14,10},{16,20},{18,... | collective-permute-start | bytes 196616 | tf_op jit(solution)/shard_map/ppermute | solution.py:78
  19.9 6.2 %collective-permute-start.3 = (f32[128,128]{1,0:T(8,128)S(1)}, f32[128,128]{1,0:T(8,128)S(1)}, u32[]{:S(2)}, u32[]{:S(2)}) collective-permute-start(f32[128,128]{1,0:T(8,128)S(1)} %constant_dynamic-slice_fusion.9), channel_id=1, source_target_pairs={{0,8},{2,10},{4,12},{6,14},{8,0},{10,2},{12,4},{14,6},{16,24},{18,... | collective-permute-start | bytes 196616 | tf_op jit(solution)/shard_map/ppermute | solution.py:78
  23.4 7.1 %collective-permute-start.11 = (f32[128,128]{1,0:T(8,128)S(1)}, f32[128,128]{1,0:T(8,128)S(1)}, u32[]{:S(2)}, u32[]{:S(2)}) collective-permute-start(f32[128,128]{1,0:T(8,128)S(1)} %dynamic-slice_add_fusion.10), channel_id=1, source_target_pairs={{0,16},{2,18},{4,20},{6,22},{8,24},{10,26},{12,28},{14,30},{16,0},... | collective-permute-start | bytes 196616 | tf_op jit(solution)/shard_map/ppermute | solution.py:86
  26.1 5.2 %collective-permute-start.4 = (f32[128,128]{1,0:T(8,128)S(1)}, f32[128,128]{1,0:T(8,128)S(1)}, u32[]{:S(2)}, u32[]{:S(2)}) collective-permute-start(f32[128,128]{1,0:T(8,128)S(1)} %dynamic-slice_add_fusion.11), channel_id=1, source_target_pairs={{0,16},{2,18},{4,20},{6,22},{8,24},{10,26},{12,28},{14,30},{16,0},... | collective-permute-start | bytes 196616 | tf_op jit(solution)/shard_map/ppermute | solution.py:86
  30.5 4.3 %collective-permute-start.12 = (f32[128,128]{1,0:T(8,128)S(1)}, f32[128,128]{1,0:T(8,128)S(1)}, u32[]{:S(2)}, u32[]{:S(2)}) collective-permute-start(f32[128,128]{1,0:T(8,128)S(1)} %add_subtract_fusion.2), channel_id=1, source_target_pairs={{0,4},{2,6},{4,0},{6,2},{8,12},{10,14},{12,8},{14,10},{16,20},{18,... | collective-permute-start | bytes 196616 | tf_op jit(solution)/shard_map/ppermute | solution.py:90
  31.3 4.5 %collective-permute-start.5 = (f32[128,128]{1,0:T(8,128)S(1)}, f32[128,128]{1,0:T(8,128)S(1)}, u32[]{:S(2)}, u32[]{:S(2)}) collective-permute-start(f32[128,128]{1,0:T(8,128)S(1)} %add_subtract_fusion.3), channel_id=1, source_target_pairs={{0,8},{2,10},{4,12},{6,14},{8,0},{10,2},{12,4},{14,6},{16,24},{18,... | collective-permute-start | bytes 196616 | tf_op jit(solution)/shard_map/ppermute | solution.py:90
  34.9 5.0 %collective-permute-start.13 = (f32[256,128]{1,0:T(8,128)S(1)}, f32[256,128]{1,0:T(8,128)S(1)}, u32[]{:S(2)}, u32[]{:S(2)}) collective-permute-start(f32[256,128]{1,0:T(8,128)S(1)} %pad_maximum_fusion.6), channel_id=1, source_target_pairs={{0,8},{2,10},{4,12},{6,14},{8,0},{10,2},{12,4},{14,6},{16,24},{18,... | collective-permute-start | bytes 393224 | tf_op jit(solution)/shard_map/ppermute | solution.py:90
  35.9 5.0 %collective-permute-start.6 = (f32[256,128]{1,0:T(8,128)S(1)}, f32[256,128]{1,0:T(8,128)S(1)}, u32[]{:S(2)}, u32[]{:S(2)}) collective-permute-start(f32[256,128]{1,0:T(8,128)S(1)} %pad_maximum_fusion.5), channel_id=1, source_target_pairs={{0,4},{2,6},{4,0},{6,2},{8,12},{10,14},{12,8},{14,10},{16,20},{18,... | collective-permute-start | bytes 393224 | tf_op jit(solution)/shard_map/ppermute | solution.py:90
  40.0 1.6 %collective-permute-start.14 = (f32[512,128]{1,0:T(8,128)S(1)}, f32[512,128]{1,0:T(8,128)S(1)}, u32[]{:S(2)}, u32[]{:S(2)}) collective-permute-start(f32[512,128]{1,0:T(8,128)S(1)} %pad_maximum_fusion.2), channel_id=1, source_target_pairs={{0,2},{2,0},{4,6},{6,4},{8,10},{10,8},{12,14},{14,12},{16,18},{18,... | collective-permute-start | bytes 786440 | tf_op jit(solution)/shard_map/ppermute | solution.py:90
  40.9 2.4 %collective-permute-start.7 = (f32[512,128]{1,0:T(8,128)S(1)}, f32[512,128]{1,0:T(8,128)S(1)}, u32[]{:S(2)}, u32[]{:S(2)}) collective-permute-start(f32[512,128]{1,0:T(8,128)S(1)} %pad_maximum_fusion.1), channel_id=1, source_target_pairs={{0,2},{2,0},{4,6},{6,4},{8,10},{10,8},{12,14},{14,12},{16,18},{18,... | collective-permute-start | bytes 786440 | tf_op jit(solution)/shard_map/ppermute | solution.py:90
  43.2 2.2 %collective-permute-start.22 = (f32[512,128]{1,0:T(8,128)S(1)}, f32[512,128]{1,0:T(8,128)S(1)}, u32[]{:S(2)}, u32[]{:S(2)}) collective-permute-start(f32[512,128]{1,0:T(8,128)S(1)} %constant_dynamic-slice_fusion.2), channel_id=1, source_target_pairs={{0,2},{2,0},{4,6},{6,4},{8,10},{10,8},{12,14},{14,12},{16,18},{18,... | collective-permute-start | bytes 786440 | tf_op jit(solution)/shard_map/ppermute | solution.py:78
  44.9 1.6 %collective-permute-start.15 = (f32[512,128]{1,0:T(8,128)S(1)}, f32[512,128]{1,0:T(8,128)S(1)}, u32[]{:S(2)}, u32[]{:S(2)}) collective-permute-start(f32[512,128]{1,0:T(8,128)S(1)} %constant_dynamic-slice_fusion.5), channel_id=1, source_target_pairs={{0,2},{2,0},{4,6},{6,4},{8,10},{10,8},{12,14},{14,12},{16,18},{18,... | collective-permute-start | bytes 786440 | tf_op jit(solution)/shard_map/ppermute | solution.py:78
  45.4 5.6 %collective-permute-start.23 = (f32[256,128]{1,0:T(8,128)S(1)}, f32[256,128]{1,0:T(8,128)S(1)}, u32[]{:S(2)}, u32[]{:S(2)}) collective-permute-start(f32[256,128]{1,0:T(8,128)S(1)} %constant_dynamic-slice_fusion.1), channel_id=1, source_target_pairs={{0,4},{2,6},{4,0},{6,2},{8,12},{10,14},{12,8},{14,10},{16,20},{18,... | collective-permute-start | bytes 393224 | tf_op jit(solution)/shard_map/ppermute | solution.py:78
  46.6 6.2 %collective-permute-start.16 = (f32[256,128]{1,0:T(8,128)S(1)}, f32[256,128]{1,0:T(8,128)S(1)}, u32[]{:S(2)}, u32[]{:S(2)}) collective-permute-start(f32[256,128]{1,0:T(8,128)S(1)} %constant_dynamic-slice_fusion.4), channel_id=1, source_target_pairs={{0,8},{2,10},{4,12},{6,14},{8,0},{10,2},{12,4},{14,6},{16,24},{18,... | collective-permute-start | bytes 393224 | tf_op jit(solution)/shard_map/ppermute | solution.py:78
  51.1 4.3 %collective-permute-start.24 = (f32[128,128]{1,0:T(8,128)S(1)}, f32[128,128]{1,0:T(8,128)S(1)}, u32[]{:S(2)}, u32[]{:S(2)}) collective-permute-start(f32[128,128]{1,0:T(8,128)S(1)} %constant_dynamic-slice_fusion), channel_id=1, source_target_pairs={{0,8},{2,10},{4,12},{6,14},{8,0},{10,2},{12,4},{14,6},{16,24},{18,... | collective-permute-start | bytes 196616 | tf_op jit(solution)/shard_map/ppermute | solution.py:78
  52.9 4.5 %collective-permute-start.17 = (f32[128,128]{1,0:T(8,128)S(1)}, f32[128,128]{1,0:T(8,128)S(1)}, u32[]{:S(2)}, u32[]{:S(2)}) collective-permute-start(f32[128,128]{1,0:T(8,128)S(1)} %constant_dynamic-slice_fusion.3), channel_id=1, source_target_pairs={{0,4},{2,6},{4,0},{6,2},{8,12},{10,14},{12,8},{14,10},{16,20},{18,... | collective-permute-start | bytes 196616 | tf_op jit(solution)/shard_map/ppermute | solution.py:78
  55.4 6.7 %collective-permute-start.25 = (f32[128,128]{1,0:T(8,128)S(1)}, f32[128,128]{1,0:T(8,128)S(1)}, u32[]{:S(2)}, u32[]{:S(2)}) collective-permute-start(f32[128,128]{1,0:T(8,128)S(1)} %dynamic-slice_add_fusion.8), channel_id=1, source_target_pairs={{0,16},{2,18},{4,20},{6,22},{8,24},{10,26},{12,28},{14,30},{16,0},... | collective-permute-start | bytes 196616 | tf_op jit(solution)/shard_map/ppermute | solution.py:86
  57.4 5.7 %collective-permute-start.18 = (f32[128,128]{1,0:T(8,128)S(1)}, f32[128,128]{1,0:T(8,128)S(1)}, u32[]{:S(2)}, u32[]{:S(2)}) collective-permute-start(f32[128,128]{1,0:T(8,128)S(1)} %dynamic-slice_add_fusion.9), channel_id=1, source_target_pairs={{0,16},{2,18},{4,20},{6,22},{8,24},{10,26},{12,28},{14,30},{16,0},... | collective-permute-start | bytes 196616 | tf_op jit(solution)/shard_map/ppermute | solution.py:86
  62.2 4.3 %collective-permute-start.26 = (f32[128,128]{1,0:T(8,128)S(1)}, f32[128,128]{1,0:T(8,128)S(1)}, u32[]{:S(2)}, u32[]{:S(2)}) collective-permute-start(f32[128,128]{1,0:T(8,128)S(1)} %add_subtract_fusion), channel_id=1, source_target_pairs={{0,8},{2,10},{4,12},{6,14},{8,0},{10,2},{12,4},{14,6},{16,24},{18,... | collective-permute-start | bytes 196616 | tf_op jit(solution)/shard_map/ppermute | solution.py:90
  63.1 4.5 %collective-permute-start.19 = (f32[128,128]{1,0:T(8,128)S(1)}, f32[128,128]{1,0:T(8,128)S(1)}, u32[]{:S(2)}, u32[]{:S(2)}) collective-permute-start(f32[128,128]{1,0:T(8,128)S(1)} %add_subtract_fusion.1), channel_id=1, source_target_pairs={{0,4},{2,6},{4,0},{6,2},{8,12},{10,14},{12,8},{14,10},{16,20},{18,... | collective-permute-start | bytes 196616 | tf_op jit(solution)/shard_map/ppermute | solution.py:90
  66.6 5.0 %collective-permute-start.27 = (f32[256,128]{1,0:T(8,128)S(1)}, f32[256,128]{1,0:T(8,128)S(1)}, u32[]{:S(2)}, u32[]{:S(2)}) collective-permute-start(f32[256,128]{1,0:T(8,128)S(1)} %pad_maximum_fusion.8), channel_id=1, source_target_pairs={{0,4},{2,6},{4,0},{6,2},{8,12},{10,14},{12,8},{14,10},{16,20},{18,... | collective-permute-start | bytes 393224 | tf_op jit(solution)/shard_map/ppermute | solution.py:90
  67.7 5.0 %collective-permute-start.20 = (f32[256,128]{1,0:T(8,128)S(1)}, f32[256,128]{1,0:T(8,128)S(1)}, u32[]{:S(2)}, u32[]{:S(2)}) collective-permute-start(f32[256,128]{1,0:T(8,128)S(1)} %pad_maximum_fusion.7), channel_id=1, source_target_pairs={{0,8},{2,10},{4,12},{6,14},{8,0},{10,2},{12,4},{14,6},{16,24},{18,... | collective-permute-start | bytes 393224 | tf_op jit(solution)/shard_map/ppermute | solution.py:90
  71.6 1.6 %collective-permute-start.28 = (f32[512,128]{1,0:T(8,128)S(1)}, f32[512,128]{1,0:T(8,128)S(1)}, u32[]{:S(2)}, u32[]{:S(2)}) collective-permute-start(f32[512,128]{1,0:T(8,128)S(1)} %pad_maximum_fusion.4), channel_id=1, source_target_pairs={{0,2},{2,0},{4,6},{6,4},{8,10},{10,8},{12,14},{14,12},{16,18},{18,... | collective-permute-start | bytes 786440 | tf_op jit(solution)/shard_map/ppermute | solution.py:90
  72.8 1.6 %collective-permute-start.21 = (f32[512,128]{1,0:T(8,128)S(1)}, f32[512,128]{1,0:T(8,128)S(1)}, u32[]{:S(2)}, u32[]{:S(2)}) collective-permute-start(f32[512,128]{1,0:T(8,128)S(1)} %pad_maximum_fusion.3), channel_id=1, source_target_pairs={{0,2},{2,0},{4,6},{6,4},{8,10},{10,8},{12,14},{14,12},{16,18},{18,... | collective-permute-start | bytes 786440 | tf_op jit(solution)/shard_map/ppermute | solution.py:90
  (2 other events, 9.8 us)

commit v24 on v23

--- a/solution.py
+++ b/solution.py
@@ -134,7 +134,7 @@
                 return tuple(matrix[:, cols] for cols in columns)
 
             first_blocks = []
-            for chain, (order, cols) in enumerate(zip(orders, columns)):
+            for chain, (order, cols) in enumerate(zip(orders, columns[::-1])):
                 remains, got_riders = ordered_reduce_then_gather(
                     first_sum[:, cols], right_side[0][:, cols], "blk", n, order,
                     inverse_pieces if chain == 0 else None,
@@ -144,7 +144,7 @@
                     panel_sum, inverse_pieces = got_riders
                 first_blocks.append(remains)
             inverse_full = jnp.concatenate(list(inverse_pieces), axis=2)
-            first_blocks = [product(inverse_full[0], remains) for remains in first_blocks]
+            first_blocks = [product(inverse_full[0], remains) for remains in first_blocks[::-1]]
             second_blocks = []
             for chain, (order, cols, block) in enumerate(zip(orders[::-1], columns, first_blocks)):
                 remains, _ = ordered_reduce_then_gather(

time: 75.7 us -> 77.4 us (1.022)
  starting transfers between devices: 29.5 us -> 30.9 us
    ppermute x12, waiting for transfers between devices: 14 us -> 12.9 us  [ordered_reduce_then_gather(): got = lax.ppermute(y, axis, [(i, i ^ 1 << j) for i in range(n)])]
    ppermute x12, starting transfers between devices: 7.65 us -> 8.76 us  [ordered_reduce_then_gather(): got = lax.ppermute(y, axis, [(i, i ^ 1 << j) for i in range(n)])]
  transfers between devices with their start and end apart: 29 -> 29, of which waited for: 19 -> 17; matrix products, arithmetic and copies ran while one was open for 20% -> 20% of each run, Pallas kernels for 0% -> 0%
where the time goes in v24:
time: 77.4 us; the launch traced here: 77.2 us
  starting transfers between devices  30.9 us (40%)
  waiting for transfers between devices  29.4 us (38%)
  matrix products  12.6 us (16%)
  local copies, waits for them, and re-layouts  2.26 us (3%)
  other arithmetic  1.56 us (2%)
    ppermute x12, waiting for transfers between devices, ordered_reduce_then_gather(): got = lax.ppermute(y, axis, [(i, i ^ 1 << j) for i in range(n)])  12.9 us
    dot_general x8, matrix products, product(): jnp.dot(left, right, precision=lax.Precision.HIGHEST, preferred_element_t...  12.6 us
    ppermute x12, starting transfers between devices, ordered_reduce_then_gather(): got = lax.ppermute(send, axis, [(i, i ^ 1 << j) for i in range(n)])  12 us
    ppermute x12, starting transfers between devices, ordered_reduce_then_gather(): got = lax.ppermute(y, axis, [(i, i ^ 1 << j) for i in range(n)])  8.76 us
    ppermute x12, waiting for transfers between devices, ordered_reduce_then_gather(): got = lax.ppermute(send, axis, [(i, i ^ 1 << j) for i in range(n)])  8.69 us
    ppermute x4, waiting for transfers between devices, ordered_reduce_then_gather(): y = y + lax.ppermute(y, axis, [(i, i ^ 1 << top) for i in range(n)])  7.84 us
    ppermute x4, starting transfers between devices, ordered_reduce_then_gather(): y = y + lax.ppermute(y, axis, [(i, i ^ 1 << top) for i in range(n)])  7.18 us
    ppermute x1, starting transfers between devices, doubling_gather(): got = lax.ppermute(y, axis, [(i, i ^ 1 << j) for i in range(n)])  2.94 us
  transfers between devices with their start and end apart: 29, of which 17 were waited for; matrix products, arithmetic and copies ran while one was open for 20% of the time, Pallas kernels for 0%

profile of v24, /device:TPU:0, one launch (start us, length us, event | category | flops | bytes accessed | tf_op | source)
XLA Modules:
  0.0 77.2 jit_solution(15906604073156809686)
XLA Ops:
  0.0 2.9 %collective-permute-start = (f32[1,1,2,64,512]{4,3,2,1,0:T(8,128)}, f32[1,1,2,64,512]{4,3,2,1,0:T(8,128)S(1)}, u32[]{:S(2)}, u32[]{:S(2)}) collective-permute-start(f32[1,1,2,64,512]{4,3,2,1,0:T(8,128)} %bitcast.51), channel_id=1, source_target_pairs={{0,1},{1,0},{2,3},{3,2},{4,5},{5,4},{6,7},{7,6},{8,9},{9,8},{10,11... | collective-permute-start | bytes 786440 | tf_op jit(solution)/shard_map/ppermute | solution.py:34
  2.9 1.7 %slice_bitcast_fusion = (f32[1024,256]{1,0:T(8,128)S(1)}, f32[1024,256]{1,0:T(8,128)S(1)}) fusion(f32[2,1024,256]{2,1,0:T(8,128)} %param.7), kind=kLoop, calls=%fused_computation.9 | loop fusion | bytes 4194304 | tf_op jit(solution)/shard_map/squeeze | solution.py:151
  4.7 5.4 %fusion.2 = f32[1024,256]{1,0:T(8,128)S(1)} fusion(f32[1024,256]{1,0:T(8,128)S(1)} %copy-done, f32[2,1024,1024]{2,1,0:T(8,128)} %param.5), kind=kOutput, calls=%fused_computation.2 | convolution fusion | flops 3221225472 | bytes 6291456 | tf_op jit(solution)/shard_map/dot_general | solution.py:8
  12.0 1.6 %collective-permute-start.2 = (f32[256,128]{1,0:T(8,128)S(1)}, f32[256,128]{1,0:T(8,128)S(1)}, u32[]{:S(2)}, u32[]{:S(2)}) collective-permute-start(f32[256,128]{1,0:T(8,128)S(1)} %constant_dynamic-slice_fusion.10), channel_id=1, source_target_pairs={{0,4},{2,6},{4,0},{6,2},{8,12},{10,14},{12,8},{14,10},{16,20},{18,... | collective-permute-start | bytes 393224 | tf_op jit(solution)/shard_map/ppermute | solution.py:78
  13.7 1.6 %collective-permute-start.4 = (f32[256,128]{1,0:T(8,128)S(1)}, f32[256,128]{1,0:T(8,128)S(1)}, u32[]{:S(2)}, u32[]{:S(2)}) collective-permute-start(f32[256,128]{1,0:T(8,128)S(1)} %constant_dynamic-slice_fusion.8), channel_id=1, source_target_pairs={{0,8},{2,10},{4,12},{6,14},{8,0},{10,2},{12,4},{14,6},{16,24},{18,... | collective-permute-start | bytes 393224 | tf_op jit(solution)/shard_map/ppermute | solution.py:78
  15.3 3.5 %fusion.6 = f32[1024,256]{1,0:T(8,128)S(1)} fusion(f32[1024,256]{1,0:T(8,128)S(1)} %copy-done, f32[2,1024,1024]{2,1,0:T(8,128)S(1)} %bitcast.50), kind=kOutput, calls=%fused_computation.6 | convolution fusion | flops 3221225472 | bytes 6291456 | tf_op jit(solution)/shard_map/dot_general | solution.py:8
  19.9 1.6 %collective-permute-start.10 = (f32[128,128]{1,0:T(8,128)S(1)}, f32[128,128]{1,0:T(8,128)S(1)}, u32[]{:S(2)}, u32[]{:S(2)}) collective-permute-start(f32[128,128]{1,0:T(8,128)S(1)} %constant_dynamic-slice_fusion.6), channel_id=1, source_target_pairs={{0,8},{2,10},{4,12},{6,14},{8,0},{10,2},{12,4},{14,6},{16,24},{18,... | collective-permute-start | bytes 196616 | tf_op jit(solution)/shard_map/ppermute | solution.py:78
  21.5 2.6 %collective-permute-done.10 = f32[128,128]{1,0:T(8,128)S(1)} collective-permute-done((f32[128,128]{1,0:T(8,128)S(1)}, f32[128,128]{1,0:T(8,128)S(1)}, u32[]{:S(2)}, u32[]{:S(2)}) %collective-permute-start.10) | collective-permute-done | bytes 65568 | tf_op jit(solution)/shard_map/ppermute | solution.py:78
  24.2 2.7 %collective-permute-start.11 = (f32[128,128]{1,0:T(8,128)S(1)}, f32[128,128]{1,0:T(8,128)S(1)}, u32[]{:S(2)}, u32[]{:S(2)}) collective-permute-start(f32[128,128]{1,0:T(8,128)S(1)} %dynamic-slice_add_fusion.10), channel_id=1, source_target_pairs={{0,16},{2,18},{4,20},{6,22},{8,24},{10,26},{12,28},{14,30},{16,0},... | collective-permute-start | bytes 196616 | tf_op jit(solution)/shard_map/ppermute | solution.py:86
  27.3 3.7 %collective-permute-done.11 = f32[128,128]{1,0:T(8,128)S(1)} collective-permute-done((f32[128,128]{1,0:T(8,128)S(1)}, f32[128,128]{1,0:T(8,128)S(1)}, u32[]{:S(2)}, u32[]{:S(2)}) %collective-permute-start.11) | collective-permute-done | bytes 65568 | tf_op jit(solution)/shard_map/ppermute | solution.py:86
  32.1 1.5 %collective-permute-start.7 = (f32[128,128]{1,0:T(8,128)S(1)}, f32[128,128]{1,0:T(8,128)S(1)}, u32[]{:S(2)}, u32[]{:S(2)}) collective-permute-start(f32[128,128]{1,0:T(8,128)S(1)} %add_subtract_fusion.3), channel_id=1, source_target_pairs={{0,4},{2,6},{4,0},{6,2},{8,12},{10,14},{12,8},{14,10},{16,20},{18,... | collective-permute-start | bytes 196616 | tf_op jit(solution)/shard_map/ppermute | solution.py:90
  33.6 1.8 %collective-permute-done.12 = f32[128,128]{1,0:T(8,128)S(1)} collective-permute-done((f32[128,128]{1,0:T(8,128)S(1)}, f32[128,128]{1,0:T(8,128)S(1)}, u32[]{:S(2)}, u32[]{:S(2)}) %collective-permute-start.12) | collective-permute-done | bytes 65568 | tf_op jit(solution)/shard_map/ppermute | solution.py:90
  35.4 1.8 %collective-permute-start.13 = (f32[256,128]{1,0:T(8,128)S(1)}, f32[256,128]{1,0:T(8,128)S(1)}, u32[]{:S(2)}, u32[]{:S(2)}) collective-permute-start(f32[256,128]{1,0:T(8,128)S(1)} %pad_maximum_fusion.6), channel_id=1, source_target_pairs={{0,4},{2,6},{4,0},{6,2},{8,12},{10,14},{12,8},{14,10},{16,20},{18,... | collective-permute-start | bytes 393224 | tf_op jit(solution)/shard_map/ppermute | solution.py:90
  37.2 1.2 %collective-permute-start.8 = (f32[256,128]{1,0:T(8,128)S(1)}, f32[256,128]{1,0:T(8,128)S(1)}, u32[]{:S(2)}, u32[]{:S(2)}) collective-permute-start(f32[256,128]{1,0:T(8,128)S(1)} %pad_maximum_fusion.5), channel_id=1, source_target_pairs={{0,8},{2,10},{4,12},{6,14},{8,0},{10,2},{12,4},{14,6},{16,24},{18,... | collective-permute-start | bytes 393224 | tf_op jit(solution)/shard_map/ppermute | solution.py:90
  38.4 2.0 %collective-permute-done.13 = f32[256,128]{1,0:T(8,128)S(1)} collective-permute-done((f32[256,128]{1,0:T(8,128)S(1)}, f32[256,128]{1,0:T(8,128)S(1)}, u32[]{:S(2)}, u32[]{:S(2)}) %collective-permute-start.13) | collective-permute-done | bytes 131104 | tf_op jit(solution)/shard_map/ppermute | solution.py:90
  40.6 1.7 %collective-permute-done.8 = f32[256,128]{1,0:T(8,128)S(1)} collective-permute-done((f32[256,128]{1,0:T(8,128)S(1)}, f32[256,128]{1,0:T(8,128)S(1)}, u32[]{:S(2)}, u32[]{:S(2)}) %collective-permute-start.8) | collective-permute-done | bytes 131104 | tf_op jit(solution)/shard_map/ppermute | solution.py:90
  42.9 1.0 %convolution_bitcast_fusion = f32[1024,128]{1,0:T(8,128)S(1)} fusion(f32[64,128]{1,0:T(8,128)S(1)} %fusion.13, f32[1024,64]{0,1:T(8,128)S(1)} %copy-done.1), kind=kOutput, calls=%fused_computation.7 | convolution fusion | flops 100663296 | bytes 819200 | tf_op jit(solution)/shard_map/dot_general | solution.py:8
  45.0 1.0 %convolution_bitcast_fusion.1 = f32[1024,128]{1,0:T(8,128)S(1)} fusion(f32[64,128]{1,0:T(8,128)S(1)} %fusion.9, f32[1024,64]{0,1:T(8,128)S(1)} %copy-done.1), kind=kOutput, calls=%fused_computation.8 | convolution fusion | flops 100663296 | bytes 819200 | tf_op jit(solution)/shard_map/dot_general | solution.py:8
  46.3 1.5 %collective-permute-start.23 = (f32[256,128]{1,0:T(8,128)S(1)}, f32[256,128]{1,0:T(8,128)S(1)}, u32[]{:S(2)}, u32[]{:S(2)}) collective-permute-start(f32[256,128]{1,0:T(8,128)S(1)} %constant_dynamic-slice_fusion.1), channel_id=1, source_target_pairs={{0,4},{2,6},{4,0},{6,2},{8,12},{10,14},{12,8},{14,10},{16,20},{18,... | collective-permute-start | bytes 393224 | tf_op jit(solution)/shard_map/ppermute | solution.py:78
  47.8 1.2 %collective-permute-start.16 = (f32[256,128]{1,0:T(8,128)S(1)}, f32[256,128]{1,0:T(8,128)S(1)}, u32[]{:S(2)}, u32[]{:S(2)}) collective-permute-start(f32[256,128]{1,0:T(8,128)S(1)} %constant_dynamic-slice_fusion.4), channel_id=1, source_target_pairs={{0,8},{2,10},{4,12},{6,14},{8,0},{10,2},{12,4},{14,6},{16,24},{18,... | collective-permute-start | bytes 393224 | tf_op jit(solution)/shard_map/ppermute | solution.py:78
  49.0 3.2 %collective-permute-done.23 = f32[256,128]{1,0:T(8,128)S(1)} collective-permute-done((f32[256,128]{1,0:T(8,128)S(1)}, f32[256,128]{1,0:T(8,128)S(1)}, u32[]{:S(2)}, u32[]{:S(2)}) %collective-permute-start.23) | collective-permute-done | bytes 131104 | tf_op jit(solution)/shard_map/ppermute | solution.py:78
  52.3 1.2 %collective-permute-start.24 = (f32[128,128]{1,0:T(8,128)S(1)}, f32[128,128]{1,0:T(8,128)S(1)}, u32[]{:S(2)}, u32[]{:S(2)}) collective-permute-start(f32[128,128]{1,0:T(8,128)S(1)} %constant_dynamic-slice_fusion), channel_id=1, source_target_pairs={{0,8},{2,10},{4,12},{6,14},{8,0},{10,2},{12,4},{14,6},{16,24},{18,... | collective-permute-start | bytes 196616 | tf_op jit(solution)/shard_map/ppermute | solution.py:78
  53.5 1.3 %collective-permute-start.17 = (f32[128,128]{1,0:T(8,128)S(1)}, f32[128,128]{1,0:T(8,128)S(1)}, u32[]{:S(2)}, u32[]{:S(2)}) collective-permute-start(f32[128,128]{1,0:T(8,128)S(1)} %constant_dynamic-slice_fusion.3), channel_id=1, source_target_pairs={{0,4},{2,6},{4,0},{6,2},{8,12},{10,14},{12,8},{14,10},{16,20},{18,... | collective-permute-start | bytes 196616 | tf_op jit(solution)/shard_map/ppermute | solution.py:78
  54.8 1.8 %collective-permute-done.24 = f32[128,128]{1,0:T(8,128)S(1)} collective-permute-done((f32[128,128]{1,0:T(8,128)S(1)}, f32[128,128]{1,0:T(8,128)S(1)}, u32[]{:S(2)}, u32[]{:S(2)}) %collective-permute-start.24) | collective-permute-done | bytes 65568 | tf_op jit(solution)/shard_map/ppermute | solution.py:78
  56.6 2.3 %collective-permute-start.25 = (f32[128,128]{1,0:T(8,128)S(1)}, f32[128,128]{1,0:T(8,128)S(1)}, u32[]{:S(2)}, u32[]{:S(2)}) collective-permute-start(f32[128,128]{1,0:T(8,128)S(1)} %dynamic-slice_add_fusion.8), channel_id=1, source_target_pairs={{0,16},{2,18},{4,20},{6,22},{8,24},{10,26},{12,28},{14,30},{16,0},... | collective-permute-start | bytes 196616 | tf_op jit(solution)/shard_map/ppermute | solution.py:86
  59.0 1.8 %collective-permute-start.18 = (f32[128,128]{1,0:T(8,128)S(1)}, f32[128,128]{1,0:T(8,128)S(1)}, u32[]{:S(2)}, u32[]{:S(2)}) collective-permute-start(f32[128,128]{1,0:T(8,128)S(1)} %dynamic-slice_add_fusion.9), channel_id=1, source_target_pairs={{0,16},{2,18},{4,20},{6,22},{8,24},{10,26},{12,28},{14,30},{16,0},... | collective-permute-start | bytes 196616 | tf_op jit(solution)/shard_map/ppermute | solution.py:86
  60.8 2.9 %collective-permute-done.25 = f32[128,128]{1,0:T(8,128)S(1)} collective-permute-done((f32[128,128]{1,0:T(8,128)S(1)}, f32[128,128]{1,0:T(8,128)S(1)}, u32[]{:S(2)}, u32[]{:S(2)}) %collective-permute-start.25) | collective-permute-done | bytes 65568 | tf_op jit(solution)/shard_map/ppermute | solution.py:86
  64.4 1.2 %collective-permute-start.19 = (f32[128,128]{1,0:T(8,128)S(1)}, f32[128,128]{1,0:T(8,128)S(1)}, u32[]{:S(2)}, u32[]{:S(2)}) collective-permute-start(f32[128,128]{1,0:T(8,128)S(1)} %add_subtract_fusion.1), channel_id=1, source_target_pairs={{0,4},{2,6},{4,0},{6,2},{8,12},{10,14},{12,8},{14,10},{16,20},{18,... | collective-permute-start | bytes 196616 | tf_op jit(solution)/shard_map/ppermute | solution.py:90
  65.7 2.4 %collective-permute-done.26 = f32[128,128]{1,0:T(8,128)S(1)} collective-permute-done((f32[128,128]{1,0:T(8,128)S(1)}, f32[128,128]{1,0:T(8,128)S(1)}, u32[]{:S(2)}, u32[]{:S(2)}) %collective-permute-start.26) | collective-permute-done | bytes 65568 | tf_op jit(solution)/shard_map/ppermute | solution.py:90
  68.1 1.3 %collective-permute-start.27 = (f32[256,128]{1,0:T(8,128)S(1)}, f32[256,128]{1,0:T(8,128)S(1)}, u32[]{:S(2)}, u32[]{:S(2)}) collective-permute-start(f32[256,128]{1,0:T(8,128)S(1)} %pad_maximum_fusion.8), channel_id=1, source_target_pairs={{0,4},{2,6},{4,0},{6,2},{8,12},{10,14},{12,8},{14,10},{16,20},{18,... | collective-permute-start | bytes 393224 | tf_op jit(solution)/shard_map/ppermute | solution.py:90
  70.4 2.8 %collective-permute-done.27 = f32[256,128]{1,0:T(8,128)S(1)} collective-permute-done((f32[256,128]{1,0:T(8,128)S(1)}, f32[256,128]{1,0:T(8,128)S(1)}, u32[]{:S(2)}, u32[]{:S(2)}) %collective-permute-start.27) | collective-permute-done | bytes 131104 | tf_op jit(solution)/shard_map/ppermute | solution.py:90
  73.3 1.2 %collective-permute-done.20 = f32[256,128]{1,0:T(8,128)S(1)} collective-permute-done((f32[256,128]{1,0:T(8,128)S(1)}, f32[256,128]{1,0:T(8,128)S(1)}, u32[]{:S(2)}, u32[]{:S(2)}) %collective-permute-start.20) | collective-permute-done | bytes 131104 | tf_op jit(solution)/shard_map/ppermute | solution.py:90
  (105 shorter events, 11.4 us)
Async XLA Ops:
  0.0 10.2 %collective-permute-start = (f32[1,1,2,64,512]{4,3,2,1,0:T(8,128)}, f32[1,1,2,64,512]{4,3,2,1,0:T(8,128)S(1)}, u32[]{:S(2)}, u32[]{:S(2)}) collective-permute-start(f32[1,1,2,64,512]{4,3,2,1,0:T(8,128)} %bitcast.51), channel_id=1, source_target_pairs={{0,1},{1,0},{2,3},{3,2},{4,5},{5,4},{6,7},{7,6},{8,9},{9,8},{10,11... | collective-permute-start | bytes 786440 | tf_op jit(solution)/shard_map/ppermute | solution.py:34
  4.6 5.5 %copy-start.2 = (f32[2,64,512]{2,1,0:T(8,128)S(1)}, f32[2,64,512]{2,1,0:T(8,128)}, u32[]{:S(2)}) copy-start(f32[2,64,512]{2,1,0:T(8,128)} %param.8) | copy-start | bytes 786436
  4.7 10.7 %slice-start = ((s8[8388608]{0:T(1024)(128)(4,1)}), s8[4194304]{0:T(1024)(128)(4,1)S(1)}, s32[]{:S(2)}) async-start(s8[8388608]{0:T(1024)(128)(4,1)} %bitcast.49), calls=%async_computation | async-start | bytes 8388608
  10.4 1.6 %collective-permute-start.1 = (f32[512,128]{1,0:T(8,128)S(1)}, f32[512,128]{1,0:T(8,128)S(1)}, u32[]{:S(2)}, u32[]{:S(2)}) collective-permute-start(f32[512,128]{1,0:T(8,128)S(1)} %constant_dynamic-slice_fusion.11), channel_id=1, source_target_pairs={{0,2},{2,0},{4,6},{6,4},{8,10},{10,8},{12,14},{14,12},{16,18},{18,... | collective-permute-start | bytes 786440 | tf_op jit(solution)/shard_map/ppermute | solution.py:78
  10.6 3.0 %collective-permute-start.3 = (f32[512,128]{1,0:T(8,128)S(1)}, f32[512,128]{1,0:T(8,128)S(1)}, u32[]{:S(2)}, u32[]{:S(2)}) collective-permute-start(f32[512,128]{1,0:T(8,128)S(1)} %constant_dynamic-slice_fusion.9), channel_id=1, source_target_pairs={{0,2},{2,0},{4,6},{6,4},{8,10},{10,8},{12,14},{14,12},{16,18},{18,... | collective-permute-start | bytes 786440 | tf_op jit(solution)/shard_map/ppermute | solution.py:78
  12.0 7.8 %collective-permute-start.2 = (f32[256,128]{1,0:T(8,128)S(1)}, f32[256,128]{1,0:T(8,128)S(1)}, u32[]{:S(2)}, u32[]{:S(2)}) collective-permute-start(f32[256,128]{1,0:T(8,128)S(1)} %constant_dynamic-slice_fusion.10), channel_id=1, source_target_pairs={{0,4},{2,6},{4,0},{6,2},{8,12},{10,14},{12,8},{14,10},{16,20},{18,... | collective-permute-start | bytes 393224 | tf_op jit(solution)/shard_map/ppermute | solution.py:78
  13.7 5.3 %collective-permute-start.4 = (f32[256,128]{1,0:T(8,128)S(1)}, f32[256,128]{1,0:T(8,128)S(1)}, u32[]{:S(2)}, u32[]{:S(2)}) collective-permute-start(f32[256,128]{1,0:T(8,128)S(1)} %constant_dynamic-slice_fusion.8), channel_id=1, source_target_pairs={{0,8},{2,10},{4,12},{6,14},{8,0},{10,2},{12,4},{14,6},{16,24},{18,... | collective-permute-start | bytes 393224 | tf_op jit(solution)/shard_map/ppermute | solution.py:78
  18.9 24.0 %copy-start.1 = (f32[1024,64]{0,1:T(8,128)S(1)}, f32[1024,64]{0,1:T(8,128)}, u32[]{:S(2)}) copy-start(f32[1024,64]{0,1:T(8,128)} %param.9) | copy-start | bytes 786436
  19.0 7.8 %collective-permute-start.5 = (f32[128,128]{1,0:T(8,128)S(1)}, f32[128,128]{1,0:T(8,128)S(1)}, u32[]{:S(2)}, u32[]{:S(2)}) collective-permute-start(f32[128,128]{1,0:T(8,128)S(1)} %constant_dynamic-slice_fusion.7), channel_id=1, source_target_pairs={{0,4},{2,6},{4,0},{6,2},{8,12},{10,14},{12,8},{14,10},{16,20},{18,... | collective-permute-start | bytes 196616 | tf_op jit(solution)/shard_map/ppermute | solution.py:78
  19.9 4.3 %collective-permute-start.10 = (f32[128,128]{1,0:T(8,128)S(1)}, f32[128,128]{1,0:T(8,128)S(1)}, u32[]{:S(2)}, u32[]{:S(2)}) collective-permute-start(f32[128,128]{1,0:T(8,128)S(1)} %constant_dynamic-slice_fusion.6), channel_id=1, source_target_pairs={{0,8},{2,10},{4,12},{6,14},{8,0},{10,2},{12,4},{14,6},{16,24},{18,... | collective-permute-start | bytes 196616 | tf_op jit(solution)/shard_map/ppermute | solution.py:78
  24.2 6.8 %collective-permute-start.11 = (f32[128,128]{1,0:T(8,128)S(1)}, f32[128,128]{1,0:T(8,128)S(1)}, u32[]{:S(2)}, u32[]{:S(2)}) collective-permute-start(f32[128,128]{1,0:T(8,128)S(1)} %dynamic-slice_add_fusion.10), channel_id=1, source_target_pairs={{0,16},{2,18},{4,20},{6,22},{8,24},{10,26},{12,28},{14,30},{16,0},... | collective-permute-start | bytes 196616 | tf_op jit(solution)/shard_map/ppermute | solution.py:86
  26.9 5.2 %collective-permute-start.6 = (f32[128,128]{1,0:T(8,128)S(1)}, f32[128,128]{1,0:T(8,128)S(1)}, u32[]{:S(2)}, u32[]{:S(2)}) collective-permute-start(f32[128,128]{1,0:T(8,128)S(1)} %dynamic-slice_add_fusion.11), channel_id=1, source_target_pairs={{0,16},{2,18},{4,20},{6,22},{8,24},{10,26},{12,28},{14,30},{16,0},... | collective-permute-start | bytes 196616 | tf_op jit(solution)/shard_map/ppermute | solution.py:86
  31.0 4.3 %collective-permute-start.12 = (f32[128,128]{1,0:T(8,128)S(1)}, f32[128,128]{1,0:T(8,128)S(1)}, u32[]{:S(2)}, u32[]{:S(2)}) collective-permute-start(f32[128,128]{1,0:T(8,128)S(1)} %add_subtract_fusion.2), channel_id=1, source_target_pairs={{0,8},{2,10},{4,12},{6,14},{8,0},{10,2},{12,4},{14,6},{16,24},{18,... | collective-permute-start | bytes 196616 | tf_op jit(solution)/shard_map/ppermute | solution.py:90
  32.1 5.1 %collective-permute-start.7 = (f32[128,128]{1,0:T(8,128)S(1)}, f32[128,128]{1,0:T(8,128)S(1)}, u32[]{:S(2)}, u32[]{:S(2)}) collective-permute-start(f32[128,128]{1,0:T(8,128)S(1)} %add_subtract_fusion.3), channel_id=1, source_target_pairs={{0,4},{2,6},{4,0},{6,2},{8,12},{10,14},{12,8},{14,10},{16,20},{18,... | collective-permute-start | bytes 196616 | tf_op jit(solution)/shard_map/ppermute | solution.py:90
  35.4 5.0 %collective-permute-start.13 = (f32[256,128]{1,0:T(8,128)S(1)}, f32[256,128]{1,0:T(8,128)S(1)}, u32[]{:S(2)}, u32[]{:S(2)}) collective-permute-start(f32[256,128]{1,0:T(8,128)S(1)} %pad_maximum_fusion.6), channel_id=1, source_target_pairs={{0,4},{2,6},{4,0},{6,2},{8,12},{10,14},{12,8},{14,10},{16,20},{18,... | collective-permute-start | bytes 393224 | tf_op jit(solution)/shard_map/ppermute | solution.py:90
  37.2 5.0 %collective-permute-start.8 = (f32[256,128]{1,0:T(8,128)S(1)}, f32[256,128]{1,0:T(8,128)S(1)}, u32[]{:S(2)}, u32[]{:S(2)}) collective-permute-start(f32[256,128]{1,0:T(8,128)S(1)} %pad_maximum_fusion.5), channel_id=1, source_target_pairs={{0,8},{2,10},{4,12},{6,14},{8,0},{10,2},{12,4},{14,6},{16,24},{18,... | collective-permute-start | bytes 393224 | tf_op jit(solution)/shard_map/ppermute | solution.py:90
  40.5 1.9 %collective-permute-start.14 = (f32[512,128]{1,0:T(8,128)S(1)}, f32[512,128]{1,0:T(8,128)S(1)}, u32[]{:S(2)}, u32[]{:S(2)}) collective-permute-start(f32[512,128]{1,0:T(8,128)S(1)} %pad_maximum_fusion.2), channel_id=1, source_target_pairs={{0,2},{2,0},{4,6},{6,4},{8,10},{10,8},{12,14},{14,12},{16,18},{18,... | collective-permute-start | bytes 786440 | tf_op jit(solution)/shard_map/ppermute | solution.py:90
  42.3 2.2 %collective-permute-start.9 = (f32[512,128]{1,0:T(8,128)S(1)}, f32[512,128]{1,0:T(8,128)S(1)}, u32[]{:S(2)}, u32[]{:S(2)}) collective-permute-start(f32[512,128]{1,0:T(8,128)S(1)} %pad_maximum_fusion.1), channel_id=1, source_target_pairs={{0,2},{2,0},{4,6},{6,4},{8,10},{10,8},{12,14},{14,12},{16,18},{18,... | collective-permute-start | bytes 786440 | tf_op jit(solution)/shard_map/ppermute | solution.py:90
  44.0 2.2 %collective-permute-start.22 = (f32[512,128]{1,0:T(8,128)S(1)}, f32[512,128]{1,0:T(8,128)S(1)}, u32[]{:S(2)}, u32[]{:S(2)}) collective-permute-start(f32[512,128]{1,0:T(8,128)S(1)} %constant_dynamic-slice_fusion.2), channel_id=1, source_target_pairs={{0,2},{2,0},{4,6},{6,4},{8,10},{10,8},{12,14},{14,12},{16,18},{18,... | collective-permute-start | bytes 786440 | tf_op jit(solution)/shard_map/ppermute | solution.py:78
  46.1 1.6 %collective-permute-start.15 = (f32[512,128]{1,0:T(8,128)S(1)}, f32[512,128]{1,0:T(8,128)S(1)}, u32[]{:S(2)}, u32[]{:S(2)}) collective-permute-start(f32[512,128]{1,0:T(8,128)S(1)} %constant_dynamic-slice_fusion.5), channel_id=1, source_target_pairs={{0,2},{2,0},{4,6},{6,4},{8,10},{10,8},{12,14},{14,12},{16,18},{18,... | collective-permute-start | bytes 786440 | tf_op jit(solution)/shard_map/ppermute | solution.py:78
  46.3 5.9 %collective-permute-start.23 = (f32[256,128]{1,0:T(8,128)S(1)}, f32[256,128]{1,0:T(8,128)S(1)}, u32[]{:S(2)}, u32[]{:S(2)}) collective-permute-start(f32[256,128]{1,0:T(8,128)S(1)} %constant_dynamic-slice_fusion.1), channel_id=1, source_target_pairs={{0,4},{2,6},{4,0},{6,2},{8,12},{10,14},{12,8},{14,10},{16,20},{18,... | collective-permute-start | bytes 393224 | tf_op jit(solution)/shard_map/ppermute | solution.py:78
  47.8 5.7 %collective-permute-start.16 = (f32[256,128]{1,0:T(8,128)S(1)}, f32[256,128]{1,0:T(8,128)S(1)}, u32[]{:S(2)}, u32[]{:S(2)}) collective-permute-start(f32[256,128]{1,0:T(8,128)S(1)} %constant_dynamic-slice_fusion.4), channel_id=1, source_target_pairs={{0,8},{2,10},{4,12},{6,14},{8,0},{10,2},{12,4},{14,6},{16,24},{18,... | collective-permute-start | bytes 393224 | tf_op jit(solution)/shard_map/ppermute | solution.py:78
  52.3 4.3 %collective-permute-start.24 = (f32[128,128]{1,0:T(8,128)S(1)}, f32[128,128]{1,0:T(8,128)S(1)}, u32[]{:S(2)}, u32[]{:S(2)}) collective-permute-start(f32[128,128]{1,0:T(8,128)S(1)} %constant_dynamic-slice_fusion), channel_id=1, source_target_pairs={{0,8},{2,10},{4,12},{6,14},{8,0},{10,2},{12,4},{14,6},{16,24},{18,... | collective-permute-start | bytes 196616 | tf_op jit(solution)/shard_map/ppermute | solution.py:78
  53.5 5.4 %collective-permute-start.17 = (f32[128,128]{1,0:T(8,128)S(1)}, f32[128,128]{1,0:T(8,128)S(1)}, u32[]{:S(2)}, u32[]{:S(2)}) collective-permute-start(f32[128,128]{1,0:T(8,128)S(1)} %constant_dynamic-slice_fusion.3), channel_id=1, source_target_pairs={{0,4},{2,6},{4,0},{6,2},{8,12},{10,14},{12,8},{14,10},{16,20},{18,... | collective-permute-start | bytes 196616 | tf_op jit(solution)/shard_map/ppermute | solution.py:78
  56.6 7.1 %collective-permute-start.25 = (f32[128,128]{1,0:T(8,128)S(1)}, f32[128,128]{1,0:T(8,128)S(1)}, u32[]{:S(2)}, u32[]{:S(2)}) collective-permute-start(f32[128,128]{1,0:T(8,128)S(1)} %dynamic-slice_add_fusion.8), channel_id=1, source_target_pairs={{0,16},{2,18},{4,20},{6,22},{8,24},{10,26},{12,28},{14,30},{16,0},... | collective-permute-start | bytes 196616 | tf_op jit(solution)/shard_map/ppermute | solution.py:86
  59.0 5.4 %collective-permute-start.18 = (f32[128,128]{1,0:T(8,128)S(1)}, f32[128,128]{1,0:T(8,128)S(1)}, u32[]{:S(2)}, u32[]{:S(2)}) collective-permute-start(f32[128,128]{1,0:T(8,128)S(1)} %dynamic-slice_add_fusion.9), channel_id=1, source_target_pairs={{0,16},{2,18},{4,20},{6,22},{8,24},{10,26},{12,28},{14,30},{16,0},... | collective-permute-start | bytes 196616 | tf_op jit(solution)/shard_map/ppermute | solution.py:86
  63.7 4.3 %collective-permute-start.26 = (f32[128,128]{1,0:T(8,128)S(1)}, f32[128,128]{1,0:T(8,128)S(1)}, u32[]{:S(2)}, u32[]{:S(2)}) collective-permute-start(f32[128,128]{1,0:T(8,128)S(1)} %add_subtract_fusion), channel_id=1, source_target_pairs={{0,8},{2,10},{4,12},{6,14},{8,0},{10,2},{12,4},{14,6},{16,24},{18,... | collective-permute-start | bytes 196616 | tf_op jit(solution)/shard_map/ppermute | solution.py:90
  64.4 4.9 %collective-permute-start.19 = (f32[128,128]{1,0:T(8,128)S(1)}, f32[128,128]{1,0:T(8,128)S(1)}, u32[]{:S(2)}, u32[]{:S(2)}) collective-permute-start(f32[128,128]{1,0:T(8,128)S(1)} %add_subtract_fusion.1), channel_id=1, source_target_pairs={{0,4},{2,6},{4,0},{6,2},{8,12},{10,14},{12,8},{14,10},{16,20},{18,... | collective-permute-start | bytes 196616 | tf_op jit(solution)/shard_map/ppermute | solution.py:90
  68.1 5.0 %collective-permute-start.27 = (f32[256,128]{1,0:T(8,128)S(1)}, f32[256,128]{1,0:T(8,128)S(1)}, u32[]{:S(2)}, u32[]{:S(2)}) collective-permute-start(f32[256,128]{1,0:T(8,128)S(1)} %pad_maximum_fusion.8), channel_id=1, source_target_pairs={{0,4},{2,6},{4,0},{6,2},{8,12},{10,14},{12,8},{14,10},{16,20},{18,... | collective-permute-start | bytes 393224 | tf_op jit(solution)/shard_map/ppermute | solution.py:90
  69.4 5.0 %collective-permute-start.20 = (f32[256,128]{1,0:T(8,128)S(1)}, f32[256,128]{1,0:T(8,128)S(1)}, u32[]{:S(2)}, u32[]{:S(2)}) collective-permute-start(f32[256,128]{1,0:T(8,128)S(1)} %pad_maximum_fusion.7), channel_id=1, source_target_pairs={{0,8},{2,10},{4,12},{6,14},{8,0},{10,2},{12,4},{14,6},{16,24},{18,... | collective-permute-start | bytes 393224 | tf_op jit(solution)/shard_map/ppermute | solution.py:90
  73.2 1.6 %collective-permute-start.28 = (f32[512,128]{1,0:T(8,128)S(1)}, f32[512,128]{1,0:T(8,128)S(1)}, u32[]{:S(2)}, u32[]{:S(2)}) collective-permute-start(f32[512,128]{1,0:T(8,128)S(1)} %pad_maximum_fusion.4), channel_id=1, source_target_pairs={{0,2},{2,0},{4,6},{6,4},{8,10},{10,8},{12,14},{14,12},{16,18},{18,... | collective-permute-start | bytes 786440 | tf_op jit(solution)/shard_map/ppermute | solution.py:90
  74.5 1.6 %collective-permute-start.21 = (f32[512,128]{1,0:T(8,128)S(1)}, f32[512,128]{1,0:T(8,128)S(1)}, u32[]{:S(2)}, u32[]{:S(2)}) collective-permute-start(f32[512,128]{1,0:T(8,128)S(1)} %pad_maximum_fusion.3), channel_id=1, source_target_pairs={{0,2},{2,0},{4,6},{6,4},{8,10},{10,8},{12,14},{14,12},{16,18},{18,... | collective-permute-start | bytes 786440 | tf_op jit(solution)/shard_map/ppermute | solution.py:90
  (2 other events, 9.8 us)

commit v25 on v22

--- a/solution.py
+++ b/solution.py
@@ -146,7 +146,7 @@
             inverse_full = jnp.concatenate(list(inverse_pieces), axis=2)
             first_blocks = [product(inverse_full[0], remains) for remains in first_blocks]
             second_blocks = []
-            for chain, (order, cols, block) in enumerate(zip(orders, columns, first_blocks)):
+            for chain, (order, cols, block) in enumerate(zip(orders[::-1], columns, first_blocks)):
                 remains, _ = ordered_reduce_then_gather(
                     panel_sum[chain] + product(coupling, block), right_side[1][:, cols], "blk", n, order
                 )

time: 75.9 us -> 75.7 us (level)
  waiting for transfers between devices: 30.6 us -> 29.2 us
  starting transfers between devices: 28.3 us -> 29.5 us
    ppermute x12, waiting for transfers between devices: 15.2 us -> 14 us  [ordered_reduce_then_gather(): got = lax.ppermute(y, axis, [(i, i ^ 1 << j) for i in range(n)])]
    ppermute x12, starting transfers between devices: 6.85 us -> 7.65 us  [ordered_reduce_then_gather(): got = lax.ppermute(y, axis, [(i, i ^ 1 << j) for i in range(n)])]
  transfers between devices with their start and end apart: 29 -> 29, of which waited for: 20 -> 19; matrix products, arithmetic and copies ran while one was open for 20% -> 20% of each run, Pallas kernels for 0% -> 0%
where the time goes in v25:
time: 75.7 us; the launch traced here: 75.6 us
  starting transfers between devices  29.5 us (39%)
  waiting for transfers between devices  29.2 us (39%)
  matrix products  12.6 us (17%)
  local copies, waits for them, and re-layouts  2.26 us (3%)
  other arithmetic  1.55 us (2%)
    ppermute x12, waiting for transfers between devices, ordered_reduce_then_gather(): got = lax.ppermute(y, axis, [(i, i ^ 1 << j) for i in range(n)])  14 us
    dot_general x8, matrix products, product(): jnp.dot(left, right, precision=lax.Precision.HIGHEST, preferred_element_t...  12.6 us
    ppermute x12, starting transfers between devices, ordered_reduce_then_gather(): got = lax.ppermute(send, axis, [(i, i ^ 1 << j) for i in range(n)])  11.5 us
    ppermute x12, waiting for transfers between devices, ordered_reduce_then_gather(): got = lax.ppermute(send, axis, [(i, i ^ 1 << j) for i in range(n)])  8 us
    ppermute x12, starting transfers between devices, ordered_reduce_then_gather(): got = lax.ppermute(y, axis, [(i, i ^ 1 << j) for i in range(n)])  7.65 us
    ppermute x4, starting transfers between devices, ordered_reduce_then_gather(): y = y + lax.ppermute(y, axis, [(i, i ^ 1 << top) for i in range(n)])  7.32 us
    ppermute x4, waiting for transfers between devices, ordered_reduce_then_gather(): y = y + lax.ppermute(y, axis, [(i, i ^ 1 << top) for i in range(n)])  7.18 us
    ppermute x1, starting transfers between devices, doubling_gather(): got = lax.ppermute(y, axis, [(i, i ^ 1 << j) for i in range(n)])  2.94 us
  transfers between devices with their start and end apart: 29, of which 19 were waited for; matrix products, arithmetic and copies ran while one was open for 20% of the time, Pallas kernels for 0%

profile of v25, /device:TPU:0, one launch (start us, length us, event | category | flops | bytes accessed | tf_op | source)
XLA Modules:
  0.0 75.6 jit_solution(7578197794108963143)
XLA Ops:
  0.0 2.9 %collective-permute-start = (f32[1,1,2,64,512]{4,3,2,1,0:T(8,128)}, f32[1,1,2,64,512]{4,3,2,1,0:T(8,128)S(1)}, u32[]{:S(2)}, u32[]{:S(2)}) collective-permute-start(f32[1,1,2,64,512]{4,3,2,1,0:T(8,128)} %bitcast.55), channel_id=1, source_target_pairs={{0,1},{1,0},{2,3},{3,2},{4,5},{5,4},{6,7},{7,6},{8,9},{9,8},{10,11... | collective-permute-start | bytes 786440 | tf_op jit(solution)/shard_map/ppermute | solution.py:34
  2.9 1.7 %slice_bitcast_fusion = (f32[1024,256]{1,0:T(8,128)S(1)}, f32[1024,256]{1,0:T(8,128)S(1)}) fusion(f32[2,1024,256]{2,1,0:T(8,128)} %param.7), kind=kLoop, calls=%fused_computation.11 | loop fusion | bytes 4194304 | tf_op jit(solution)/shard_map/squeeze | solution.py:151
  4.7 5.4 %fusion.2 = f32[1024,256]{1,0:T(8,128)S(1)} fusion(f32[1024,256]{1,0:T(8,128)S(1)} %copy-done, f32[2,1024,1024]{2,1,0:T(8,128)} %param.5), kind=kOutput, calls=%fused_computation.2 | convolution fusion | flops 3221225472 | bytes 6291456 | tf_op jit(solution)/shard_map/dot_general | solution.py:8
  11.1 0.9 %collective-permute-done.1 = f32[512,128]{1,0:T(8,128)S(1)} collective-permute-done((f32[512,128]{1,0:T(8,128)S(1)}, f32[512,128]{1,0:T(8,128)S(1)}, u32[]{:S(2)}, u32[]{:S(2)}) %collective-permute-start.1) | collective-permute-done | bytes 262176 | tf_op jit(solution)/shard_map/ppermute | solution.py:78
  12.0 1.6 %collective-permute-start.2 = (f32[256,128]{1,0:T(8,128)S(1)}, f32[256,128]{1,0:T(8,128)S(1)}, u32[]{:S(2)}, u32[]{:S(2)}) collective-permute-start(f32[256,128]{1,0:T(8,128)S(1)} %constant_dynamic-slice_fusion.10), channel_id=1, source_target_pairs={{0,4},{2,6},{4,0},{6,2},{8,12},{10,14},{12,8},{14,10},{16,20},{18,... | collective-permute-start | bytes 393224 | tf_op jit(solution)/shard_map/ppermute | solution.py:78
  13.7 1.6 %collective-permute-start.16 = (f32[256,128]{1,0:T(8,128)S(1)}, f32[256,128]{1,0:T(8,128)S(1)}, u32[]{:S(2)}, u32[]{:S(2)}) collective-permute-start(f32[256,128]{1,0:T(8,128)S(1)} %constant_dynamic-slice_fusion.4), channel_id=1, source_target_pairs={{0,8},{2,10},{4,12},{6,14},{8,0},{10,2},{12,4},{14,6},{16,24},{18,... | collective-permute-start | bytes 393224 | tf_op jit(solution)/shard_map/ppermute | solution.py:78
  15.3 3.5 %fusion.6 = f32[1024,256]{1,0:T(8,128)S(1)} fusion(f32[1024,256]{1,0:T(8,128)S(1)} %copy-done, f32[2,1024,1024]{2,1,0:T(8,128)S(1)} %bitcast.52), kind=kOutput, calls=%fused_computation.6 | convolution fusion | flops 3221225472 | bytes 6291456 | tf_op jit(solution)/shard_map/dot_general | solution.py:8
  19.9 1.6 %collective-permute-start.3 = (f32[128,128]{1,0:T(8,128)S(1)}, f32[128,128]{1,0:T(8,128)S(1)}, u32[]{:S(2)}, u32[]{:S(2)}) collective-permute-start(f32[128,128]{1,0:T(8,128)S(1)} %constant_dynamic-slice_fusion.9), channel_id=1, source_target_pairs={{0,8},{2,10},{4,12},{6,14},{8,0},{10,2},{12,4},{14,6},{16,24},{18,... | collective-permute-start | bytes 196616 | tf_op jit(solution)/shard_map/ppermute | solution.py:78
  21.6 1.8 %collective-permute-done.17 = f32[128,128]{1,0:T(8,128)S(1)} collective-permute-done((f32[128,128]{1,0:T(8,128)S(1)}, f32[128,128]{1,0:T(8,128)S(1)}, u32[]{:S(2)}, u32[]{:S(2)}) %collective-permute-start.17) | collective-permute-done | bytes 65568 | tf_op jit(solution)/shard_map/ppermute | solution.py:78
  23.4 2.7 %collective-permute-start.18 = (f32[128,128]{1,0:T(8,128)S(1)}, f32[128,128]{1,0:T(8,128)S(1)}, u32[]{:S(2)}, u32[]{:S(2)}) collective-permute-start(f32[128,128]{1,0:T(8,128)S(1)} %dynamic-slice_add_fusion.9), channel_id=1, source_target_pairs={{0,16},{2,18},{4,20},{6,22},{8,24},{10,26},{12,28},{14,30},{16,0},... | collective-permute-start | bytes 196616 | tf_op jit(solution)/shard_map/ppermute | solution.py:86
  26.1 1.3 %collective-permute-start.4 = (f32[128,128]{1,0:T(8,128)S(1)}, f32[128,128]{1,0:T(8,128)S(1)}, u32[]{:S(2)}, u32[]{:S(2)}) collective-permute-start(f32[128,128]{1,0:T(8,128)S(1)} %dynamic-slice_add_fusion.11), channel_id=1, source_target_pairs={{0,16},{2,18},{4,20},{6,22},{8,24},{10,26},{12,28},{14,30},{16,0},... | collective-permute-start | bytes 196616 | tf_op jit(solution)/shard_map/ppermute | solution.py:86
  27.4 3.1 %collective-permute-done.18 = f32[128,128]{1,0:T(8,128)S(1)} collective-permute-done((f32[128,128]{1,0:T(8,128)S(1)}, f32[128,128]{1,0:T(8,128)S(1)}, u32[]{:S(2)}, u32[]{:S(2)}) %collective-permute-start.18) | collective-permute-done | bytes 65568 | tf_op jit(solution)/shard_map/ppermute | solution.py:86
  31.3 2.1 %collective-permute-start.5 = (f32[128,128]{1,0:T(8,128)S(1)}, f32[128,128]{1,0:T(8,128)S(1)}, u32[]{:S(2)}, u32[]{:S(2)}) collective-permute-start(f32[128,128]{1,0:T(8,128)S(1)} %add_subtract_fusion.3), channel_id=1, source_target_pairs={{0,8},{2,10},{4,12},{6,14},{8,0},{10,2},{12,4},{14,6},{16,24},{18,... | collective-permute-start | bytes 196616 | tf_op jit(solution)/shard_map/ppermute | solution.py:90
  33.4 1.4 %collective-permute-done.19 = f32[128,128]{1,0:T(8,128)S(1)} collective-permute-done((f32[128,128]{1,0:T(8,128)S(1)}, f32[128,128]{1,0:T(8,128)S(1)}, u32[]{:S(2)}, u32[]{:S(2)}) %collective-permute-start.19) | collective-permute-done | bytes 65568 | tf_op jit(solution)/shard_map/ppermute | solution.py:90
  34.9 0.9 %collective-permute-done.5 = f32[128,128]{1,0:T(8,128)S(1)} collective-permute-done((f32[128,128]{1,0:T(8,128)S(1)}, f32[128,128]{1,0:T(8,128)S(1)}, u32[]{:S(2)}, u32[]{:S(2)}) %collective-permute-start.5) | collective-permute-done | bytes 65568 | tf_op jit(solution)/shard_map/ppermute | solution.py:90
  35.9 1.2 %collective-permute-start.6 = (f32[256,128]{1,0:T(8,128)S(1)}, f32[256,128]{1,0:T(8,128)S(1)}, u32[]{:S(2)}, u32[]{:S(2)}) collective-permute-start(f32[256,128]{1,0:T(8,128)S(1)} %pad_maximum_fusion.5), channel_id=1, source_target_pairs={{0,4},{2,6},{4,0},{6,2},{8,12},{10,14},{12,8},{14,10},{16,20},{18,... | collective-permute-start | bytes 393224 | tf_op jit(solution)/shard_map/ppermute | solution.py:90
  37.0 2.9 %collective-permute-done.20 = f32[256,128]{1,0:T(8,128)S(1)} collective-permute-done((f32[256,128]{1,0:T(8,128)S(1)}, f32[256,128]{1,0:T(8,128)S(1)}, u32[]{:S(2)}, u32[]{:S(2)}) %collective-permute-start.20) | collective-permute-done | bytes 131104 | tf_op jit(solution)/shard_map/ppermute | solution.py:90
  40.0 0.9 %collective-permute-done.6 = f32[256,128]{1,0:T(8,128)S(1)} collective-permute-done((f32[256,128]{1,0:T(8,128)S(1)}, f32[256,128]{1,0:T(8,128)S(1)}, u32[]{:S(2)}, u32[]{:S(2)}) %collective-permute-start.6) | collective-permute-done | bytes 131104 | tf_op jit(solution)/shard_map/ppermute | solution.py:90
  42.0 1.0 %convolution_bitcast_fusion = f32[1024,128]{1,0:T(8,128)S(1)} fusion(f32[64,128]{1,0:T(8,128)S(1)} %fusion.16, f32[1024,64]{0,1:T(8,128)S(1)} %copy-done.1), kind=kOutput, calls=%fused_computation.7 | convolution fusion | flops 100663296 | bytes 819200 | tf_op jit(solution)/shard_map/dot_general | solution.py:8
  43.8 1.0 %convolution_bitcast_fusion.1 = f32[1024,128]{1,0:T(8,128)S(1)} fusion(f32[64,128]{1,0:T(8,128)S(1)} %fusion.9, f32[1024,64]{0,1:T(8,128)S(1)} %copy-done.1), kind=kOutput, calls=%fused_computation.8 | convolution fusion | flops 100663296 | bytes 819200 | tf_op jit(solution)/shard_map/dot_general | solution.py:8
  46.6 1.7 %collective-permute-start.9 = (f32[256,128]{1,0:T(8,128)S(1)}, f32[256,128]{1,0:T(8,128)S(1)}, u32[]{:S(2)}, u32[]{:S(2)}) collective-permute-start(f32[256,128]{1,0:T(8,128)S(1)} %constant_dynamic-slice_fusion.7), channel_id=1, source_target_pairs={{0,8},{2,10},{4,12},{6,14},{8,0},{10,2},{12,4},{14,6},{16,24},{18,... | collective-permute-start | bytes 393224 | tf_op jit(solution)/shard_map/ppermute | solution.py:78
  48.3 2.7 %collective-permute-done.23 = f32[256,128]{1,0:T(8,128)S(1)} collective-permute-done((f32[256,128]{1,0:T(8,128)S(1)}, f32[256,128]{1,0:T(8,128)S(1)}, u32[]{:S(2)}, u32[]{:S(2)}) %collective-permute-start.23) | collective-permute-done | bytes 131104 | tf_op jit(solution)/shard_map/ppermute | solution.py:78
  51.1 1.7 %collective-permute-start.24 = (f32[128,128]{1,0:T(8,128)S(1)}, f32[128,128]{1,0:T(8,128)S(1)}, u32[]{:S(2)}, u32[]{:S(2)}) collective-permute-start(f32[128,128]{1,0:T(8,128)S(1)} %constant_dynamic-slice_fusion), channel_id=1, source_target_pairs={{0,8},{2,10},{4,12},{6,14},{8,0},{10,2},{12,4},{14,6},{16,24},{18,... | collective-permute-start | bytes 196616 | tf_op jit(solution)/shard_map/ppermute | solution.py:78
  53.3 2.1 %collective-permute-done.24 = f32[128,128]{1,0:T(8,128)S(1)} collective-permute-done((f32[128,128]{1,0:T(8,128)S(1)}, f32[128,128]{1,0:T(8,128)S(1)}, u32[]{:S(2)}, u32[]{:S(2)}) %collective-permute-start.24) | collective-permute-done | bytes 65568 | tf_op jit(solution)/shard_map/ppermute | solution.py:78
  55.4 1.9 %collective-permute-start.25 = (f32[128,128]{1,0:T(8,128)S(1)}, f32[128,128]{1,0:T(8,128)S(1)}, u32[]{:S(2)}, u32[]{:S(2)}) collective-permute-start(f32[128,128]{1,0:T(8,128)S(1)} %dynamic-slice_add_fusion.8), channel_id=1, source_target_pairs={{0,16},{2,18},{4,20},{6,22},{8,24},{10,26},{12,28},{14,30},{16,0},... | collective-permute-start | bytes 196616 | tf_op jit(solution)/shard_map/ppermute | solution.py:86
  57.4 1.5 %collective-permute-start.11 = (f32[128,128]{1,0:T(8,128)S(1)}, f32[128,128]{1,0:T(8,128)S(1)}, u32[]{:S(2)}, u32[]{:S(2)}) collective-permute-start(f32[128,128]{1,0:T(8,128)S(1)} %dynamic-slice_add_fusion.10), channel_id=1, source_target_pairs={{0,16},{2,18},{4,20},{6,22},{8,24},{10,26},{12,28},{14,30},{16,0},... | collective-permute-start | bytes 196616 | tf_op jit(solution)/shard_map/ppermute | solution.py:86
  58.8 3.3 %collective-permute-done.25 = f32[128,128]{1,0:T(8,128)S(1)} collective-permute-done((f32[128,128]{1,0:T(8,128)S(1)}, f32[128,128]{1,0:T(8,128)S(1)}, u32[]{:S(2)}, u32[]{:S(2)}) %collective-permute-start.25) | collective-permute-done | bytes 65568 | tf_op jit(solution)/shard_map/ppermute | solution.py:86
  64.0 2.6 %collective-permute-done.26 = f32[128,128]{1,0:T(8,128)S(1)} collective-permute-done((f32[128,128]{1,0:T(8,128)S(1)}, f32[128,128]{1,0:T(8,128)S(1)}, u32[]{:S(2)}, u32[]{:S(2)}) %collective-permute-start.26) | collective-permute-done | bytes 65568 | tf_op jit(solution)/shard_map/ppermute | solution.py:90
  66.6 1.1 %collective-permute-start.27 = (f32[256,128]{1,0:T(8,128)S(1)}, f32[256,128]{1,0:T(8,128)S(1)}, u32[]{:S(2)}, u32[]{:S(2)}) collective-permute-start(f32[256,128]{1,0:T(8,128)S(1)} %pad_maximum_fusion.8), channel_id=1, source_target_pairs={{0,4},{2,6},{4,0},{6,2},{8,12},{10,14},{12,8},{14,10},{16,20},{18,... | collective-permute-start | bytes 393224 | tf_op jit(solution)/shard_map/ppermute | solution.py:90
  67.7 1.1 %collective-permute-start.13 = (f32[256,128]{1,0:T(8,128)S(1)}, f32[256,128]{1,0:T(8,128)S(1)}, u32[]{:S(2)}, u32[]{:S(2)}) collective-permute-start(f32[256,128]{1,0:T(8,128)S(1)} %pad_maximum_fusion.6), channel_id=1, source_target_pairs={{0,8},{2,10},{4,12},{6,14},{8,0},{10,2},{12,4},{14,6},{16,24},{18,... | collective-permute-start | bytes 393224 | tf_op jit(solution)/shard_map/ppermute | solution.py:90
  68.8 2.8 %collective-permute-done.27 = f32[256,128]{1,0:T(8,128)S(1)} collective-permute-done((f32[256,128]{1,0:T(8,128)S(1)}, f32[256,128]{1,0:T(8,128)S(1)}, u32[]{:S(2)}, u32[]{:S(2)}) %collective-permute-start.27) | collective-permute-done | bytes 131104 | tf_op jit(solution)/shard_map/ppermute | solution.py:90
  71.7 1.0 %collective-permute-done.13 = f32[256,128]{1,0:T(8,128)S(1)} collective-permute-done((f32[256,128]{1,0:T(8,128)S(1)}, f32[256,128]{1,0:T(8,128)S(1)}, u32[]{:S(2)}, u32[]{:S(2)}) %collective-permute-start.13) | collective-permute-done | bytes 131104 | tf_op jit(solution)/shard_map/ppermute | solution.py:90
  (104 shorter events, 12.0 us)
Async XLA Ops:
  0.0 10.2 %collective-permute-start = (f32[1,1,2,64,512]{4,3,2,1,0:T(8,128)}, f32[1,1,2,64,512]{4,3,2,1,0:T(8,128)S(1)}, u32[]{:S(2)}, u32[]{:S(2)}) collective-permute-start(f32[1,1,2,64,512]{4,3,2,1,0:T(8,128)} %bitcast.55), channel_id=1, source_target_pairs={{0,1},{1,0},{2,3},{3,2},{4,5},{5,4},{6,7},{7,6},{8,9},{9,8},{10,11... | collective-permute-start | bytes 786440 | tf_op jit(solution)/shard_map/ppermute | solution.py:34
  4.6 5.5 %copy-start.2 = (f32[2,64,512]{2,1,0:T(8,128)S(1)}, f32[2,64,512]{2,1,0:T(8,128)}, u32[]{:S(2)}) copy-start(f32[2,64,512]{2,1,0:T(8,128)} %param.8) | copy-start | bytes 786436
  4.7 10.7 %slice-start = ((s8[8388608]{0:T(1024)(128)(4,1)}), s8[4194304]{0:T(1024)(128)(4,1)S(1)}, s32[]{:S(2)}) async-start(s8[8388608]{0:T(1024)(128)(4,1)} %bitcast.51), calls=%async_computation | async-start | bytes 8388608
  10.4 1.6 %collective-permute-start.1 = (f32[512,128]{1,0:T(8,128)S(1)}, f32[512,128]{1,0:T(8,128)S(1)}, u32[]{:S(2)}, u32[]{:S(2)}) collective-permute-start(f32[512,128]{1,0:T(8,128)S(1)} %constant_dynamic-slice_fusion.11), channel_id=1, source_target_pairs={{0,2},{2,0},{4,6},{6,4},{8,10},{10,8},{12,14},{14,12},{16,18},{18,... | collective-permute-start | bytes 786440 | tf_op jit(solution)/shard_map/ppermute | solution.py:78
  10.6 3.0 %collective-permute-start.15 = (f32[512,128]{1,0:T(8,128)S(1)}, f32[512,128]{1,0:T(8,128)S(1)}, u32[]{:S(2)}, u32[]{:S(2)}) collective-permute-start(f32[512,128]{1,0:T(8,128)S(1)} %constant_dynamic-slice_fusion.5), channel_id=1, source_target_pairs={{0,2},{2,0},{4,6},{6,4},{8,10},{10,8},{12,14},{14,12},{16,18},{18,... | collective-permute-start | bytes 786440 | tf_op jit(solution)/shard_map/ppermute | solution.py:78
  12.0 7.8 %collective-permute-start.2 = (f32[256,128]{1,0:T(8,128)S(1)}, f32[256,128]{1,0:T(8,128)S(1)}, u32[]{:S(2)}, u32[]{:S(2)}) collective-permute-start(f32[256,128]{1,0:T(8,128)S(1)} %constant_dynamic-slice_fusion.10), channel_id=1, source_target_pairs={{0,4},{2,6},{4,0},{6,2},{8,12},{10,14},{12,8},{14,10},{16,20},{18,... | collective-permute-start | bytes 393224 | tf_op jit(solution)/shard_map/ppermute | solution.py:78
  13.7 5.3 %collective-permute-start.16 = (f32[256,128]{1,0:T(8,128)S(1)}, f32[256,128]{1,0:T(8,128)S(1)}, u32[]{:S(2)}, u32[]{:S(2)}) collective-permute-start(f32[256,128]{1,0:T(8,128)S(1)} %constant_dynamic-slice_fusion.4), channel_id=1, source_target_pairs={{0,8},{2,10},{4,12},{6,14},{8,0},{10,2},{12,4},{14,6},{16,24},{18,... | collective-permute-start | bytes 393224 | tf_op jit(solution)/shard_map/ppermute | solution.py:78
  18.9 23.2 %copy-start.1 = (f32[1024,64]{0,1:T(8,128)S(1)}, f32[1024,64]{0,1:T(8,128)}, u32[]{:S(2)}) copy-start(f32[1024,64]{0,1:T(8,128)} %param.9) | copy-start | bytes 786436
  19.0 4.3 %collective-permute-start.17 = (f32[128,128]{1,0:T(8,128)S(1)}, f32[128,128]{1,0:T(8,128)S(1)}, u32[]{:S(2)}, u32[]{:S(2)}) collective-permute-start(f32[128,128]{1,0:T(8,128)S(1)} %constant_dynamic-slice_fusion.3), channel_id=1, source_target_pairs={{0,4},{2,6},{4,0},{6,2},{8,12},{10,14},{12,8},{14,10},{16,20},{18,... | collective-permute-start | bytes 196616 | tf_op jit(solution)/shard_map/ppermute | solution.py:78
  19.9 6.2 %collective-permute-start.3 = (f32[128,128]{1,0:T(8,128)S(1)}, f32[128,128]{1,0:T(8,128)S(1)}, u32[]{:S(2)}, u32[]{:S(2)}) collective-permute-start(f32[128,128]{1,0:T(8,128)S(1)} %constant_dynamic-slice_fusion.9), channel_id=1, source_target_pairs={{0,8},{2,10},{4,12},{6,14},{8,0},{10,2},{12,4},{14,6},{16,24},{18,... | collective-permute-start | bytes 196616 | tf_op jit(solution)/shard_map/ppermute | solution.py:78
  23.4 7.1 %collective-permute-start.18 = (f32[128,128]{1,0:T(8,128)S(1)}, f32[128,128]{1,0:T(8,128)S(1)}, u32[]{:S(2)}, u32[]{:S(2)}) collective-permute-start(f32[128,128]{1,0:T(8,128)S(1)} %dynamic-slice_add_fusion.9), channel_id=1, source_target_pairs={{0,16},{2,18},{4,20},{6,22},{8,24},{10,26},{12,28},{14,30},{16,0},... | collective-permute-start | bytes 196616 | tf_op jit(solution)/shard_map/ppermute | solution.py:86
  26.1 5.2 %collective-permute-start.4 = (f32[128,128]{1,0:T(8,128)S(1)}, f32[128,128]{1,0:T(8,128)S(1)}, u32[]{:S(2)}, u32[]{:S(2)}) collective-permute-start(f32[128,128]{1,0:T(8,128)S(1)} %dynamic-slice_add_fusion.11), channel_id=1, source_target_pairs={{0,16},{2,18},{4,20},{6,22},{8,24},{10,26},{12,28},{14,30},{16,0},... | collective-permute-start | bytes 196616 | tf_op jit(solution)/shard_map/ppermute | solution.py:86
  30.5 4.3 %collective-permute-start.19 = (f32[128,128]{1,0:T(8,128)S(1)}, f32[128,128]{1,0:T(8,128)S(1)}, u32[]{:S(2)}, u32[]{:S(2)}) collective-permute-start(f32[128,128]{1,0:T(8,128)S(1)} %add_subtract_fusion.1), channel_id=1, source_target_pairs={{0,4},{2,6},{4,0},{6,2},{8,12},{10,14},{12,8},{14,10},{16,20},{18,... | collective-permute-start | bytes 196616 | tf_op jit(solution)/shard_map/ppermute | solution.py:90
  31.3 4.5 %collective-permute-start.5 = (f32[128,128]{1,0:T(8,128)S(1)}, f32[128,128]{1,0:T(8,128)S(1)}, u32[]{:S(2)}, u32[]{:S(2)}) collective-permute-start(f32[128,128]{1,0:T(8,128)S(1)} %add_subtract_fusion.3), channel_id=1, source_target_pairs={{0,8},{2,10},{4,12},{6,14},{8,0},{10,2},{12,4},{14,6},{16,24},{18,... | collective-permute-start | bytes 196616 | tf_op jit(solution)/shard_map/ppermute | solution.py:90
  34.9 5.0 %collective-permute-start.20 = (f32[256,128]{1,0:T(8,128)S(1)}, f32[256,128]{1,0:T(8,128)S(1)}, u32[]{:S(2)}, u32[]{:S(2)}) collective-permute-start(f32[256,128]{1,0:T(8,128)S(1)} %pad_maximum_fusion.7), channel_id=1, source_target_pairs={{0,8},{2,10},{4,12},{6,14},{8,0},{10,2},{12,4},{14,6},{16,24},{18,... | collective-permute-start | bytes 393224 | tf_op jit(solution)/shard_map/ppermute | solution.py:90
  35.9 5.0 %collective-permute-start.6 = (f32[256,128]{1,0:T(8,128)S(1)}, f32[256,128]{1,0:T(8,128)S(1)}, u32[]{:S(2)}, u32[]{:S(2)}) collective-permute-start(f32[256,128]{1,0:T(8,128)S(1)} %pad_maximum_fusion.5), channel_id=1, source_target_pairs={{0,4},{2,6},{4,0},{6,2},{8,12},{10,14},{12,8},{14,10},{16,20},{18,... | collective-permute-start | bytes 393224 | tf_op jit(solution)/shard_map/ppermute | solution.py:90
  40.0 1.6 %collective-permute-start.21 = (f32[512,128]{1,0:T(8,128)S(1)}, f32[512,128]{1,0:T(8,128)S(1)}, u32[]{:S(2)}, u32[]{:S(2)}) collective-permute-start(f32[512,128]{1,0:T(8,128)S(1)} %pad_maximum_fusion.3), channel_id=1, source_target_pairs={{0,2},{2,0},{4,6},{6,4},{8,10},{10,8},{12,14},{14,12},{16,18},{18,... | collective-permute-start | bytes 786440 | tf_op jit(solution)/shard_map/ppermute | solution.py:90
  40.9 2.4 %collective-permute-start.7 = (f32[512,128]{1,0:T(8,128)S(1)}, f32[512,128]{1,0:T(8,128)S(1)}, u32[]{:S(2)}, u32[]{:S(2)}) collective-permute-start(f32[512,128]{1,0:T(8,128)S(1)} %pad_maximum_fusion.1), channel_id=1, source_target_pairs={{0,2},{2,0},{4,6},{6,4},{8,10},{10,8},{12,14},{14,12},{16,18},{18,... | collective-permute-start | bytes 786440 | tf_op jit(solution)/shard_map/ppermute | solution.py:90
  43.2 2.2 %collective-permute-start.22 = (f32[512,128]{1,0:T(8,128)S(1)}, f32[512,128]{1,0:T(8,128)S(1)}, u32[]{:S(2)}, u32[]{:S(2)}) collective-permute-start(f32[512,128]{1,0:T(8,128)S(1)} %constant_dynamic-slice_fusion.2), channel_id=1, source_target_pairs={{0,2},{2,0},{4,6},{6,4},{8,10},{10,8},{12,14},{14,12},{16,18},{18,... | collective-permute-start | bytes 786440 | tf_op jit(solution)/shard_map/ppermute | solution.py:78
  44.9 1.6 %collective-permute-start.8 = (f32[512,128]{1,0:T(8,128)S(1)}, f32[512,128]{1,0:T(8,128)S(1)}, u32[]{:S(2)}, u32[]{:S(2)}) collective-permute-start(f32[512,128]{1,0:T(8,128)S(1)} %constant_dynamic-slice_fusion.8), channel_id=1, source_target_pairs={{0,2},{2,0},{4,6},{6,4},{8,10},{10,8},{12,14},{14,12},{16,18},{18,... | collective-permute-start | bytes 786440 | tf_op jit(solution)/shard_map/ppermute | solution.py:78
  45.4 5.6 %collective-permute-start.23 = (f32[256,128]{1,0:T(8,128)S(1)}, f32[256,128]{1,0:T(8,128)S(1)}, u32[]{:S(2)}, u32[]{:S(2)}) collective-permute-start(f32[256,128]{1,0:T(8,128)S(1)} %constant_dynamic-slice_fusion.1), channel_id=1, source_target_pairs={{0,4},{2,6},{4,0},{6,2},{8,12},{10,14},{12,8},{14,10},{16,20},{18,... | collective-permute-start | bytes 393224 | tf_op jit(solution)/shard_map/ppermute | solution.py:78
  46.6 6.2 %collective-permute-start.9 = (f32[256,128]{1,0:T(8,128)S(1)}, f32[256,128]{1,0:T(8,128)S(1)}, u32[]{:S(2)}, u32[]{:S(2)}) collective-permute-start(f32[256,128]{1,0:T(8,128)S(1)} %constant_dynamic-slice_fusion.7), channel_id=1, source_target_pairs={{0,8},{2,10},{4,12},{6,14},{8,0},{10,2},{12,4},{14,6},{16,24},{18,... | collective-permute-start | bytes 393224 | tf_op jit(solution)/shard_map/ppermute | solution.py:78
  51.1 4.3 %collective-permute-start.24 = (f32[128,128]{1,0:T(8,128)S(1)}, f32[128,128]{1,0:T(8,128)S(1)}, u32[]{:S(2)}, u32[]{:S(2)}) collective-permute-start(f32[128,128]{1,0:T(8,128)S(1)} %constant_dynamic-slice_fusion), channel_id=1, source_target_pairs={{0,8},{2,10},{4,12},{6,14},{8,0},{10,2},{12,4},{14,6},{16,24},{18,... | collective-permute-start | bytes 196616 | tf_op jit(solution)/shard_map/ppermute | solution.py:78
  52.9 4.5 %collective-permute-start.10 = (f32[128,128]{1,0:T(8,128)S(1)}, f32[128,128]{1,0:T(8,128)S(1)}, u32[]{:S(2)}, u32[]{:S(2)}) collective-permute-start(f32[128,128]{1,0:T(8,128)S(1)} %constant_dynamic-slice_fusion.6), channel_id=1, source_target_pairs={{0,4},{2,6},{4,0},{6,2},{8,12},{10,14},{12,8},{14,10},{16,20},{18,... | collective-permute-start | bytes 196616 | tf_op jit(solution)/shard_map/ppermute | solution.py:78
  55.4 6.7 %collective-permute-start.25 = (f32[128,128]{1,0:T(8,128)S(1)}, f32[128,128]{1,0:T(8,128)S(1)}, u32[]{:S(2)}, u32[]{:S(2)}) collective-permute-start(f32[128,128]{1,0:T(8,128)S(1)} %dynamic-slice_add_fusion.8), channel_id=1, source_target_pairs={{0,16},{2,18},{4,20},{6,22},{8,24},{10,26},{12,28},{14,30},{16,0},... | collective-permute-start | bytes 196616 | tf_op jit(solution)/shard_map/ppermute | solution.py:86
  57.4 5.7 %collective-permute-start.11 = (f32[128,128]{1,0:T(8,128)S(1)}, f32[128,128]{1,0:T(8,128)S(1)}, u32[]{:S(2)}, u32[]{:S(2)}) collective-permute-start(f32[128,128]{1,0:T(8,128)S(1)} %dynamic-slice_add_fusion.10), channel_id=1, source_target_pairs={{0,16},{2,18},{4,20},{6,22},{8,24},{10,26},{12,28},{14,30},{16,0},... | collective-permute-start | bytes 196616 | tf_op jit(solution)/shard_map/ppermute | solution.py:86
  62.2 4.3 %collective-permute-start.26 = (f32[128,128]{1,0:T(8,128)S(1)}, f32[128,128]{1,0:T(8,128)S(1)}, u32[]{:S(2)}, u32[]{:S(2)}) collective-permute-start(f32[128,128]{1,0:T(8,128)S(1)} %add_subtract_fusion), channel_id=1, source_target_pairs={{0,8},{2,10},{4,12},{6,14},{8,0},{10,2},{12,4},{14,6},{16,24},{18,... | collective-permute-start | bytes 196616 | tf_op jit(solution)/shard_map/ppermute | solution.py:90
  63.1 4.5 %collective-permute-start.12 = (f32[128,128]{1,0:T(8,128)S(1)}, f32[128,128]{1,0:T(8,128)S(1)}, u32[]{:S(2)}, u32[]{:S(2)}) collective-permute-start(f32[128,128]{1,0:T(8,128)S(1)} %add_subtract_fusion.2), channel_id=1, source_target_pairs={{0,4},{2,6},{4,0},{6,2},{8,12},{10,14},{12,8},{14,10},{16,20},{18,... | collective-permute-start | bytes 196616 | tf_op jit(solution)/shard_map/ppermute | solution.py:90
  66.6 5.0 %collective-permute-start.27 = (f32[256,128]{1,0:T(8,128)S(1)}, f32[256,128]{1,0:T(8,128)S(1)}, u32[]{:S(2)}, u32[]{:S(2)}) collective-permute-start(f32[256,128]{1,0:T(8,128)S(1)} %pad_maximum_fusion.8), channel_id=1, source_target_pairs={{0,4},{2,6},{4,0},{6,2},{8,12},{10,14},{12,8},{14,10},{16,20},{18,... | collective-permute-start | bytes 393224 | tf_op jit(solution)/shard_map/ppermute | solution.py:90
  67.7 5.0 %collective-permute-start.13 = (f32[256,128]{1,0:T(8,128)S(1)}, f32[256,128]{1,0:T(8,128)S(1)}, u32[]{:S(2)}, u32[]{:S(2)}) collective-permute-start(f32[256,128]{1,0:T(8,128)S(1)} %pad_maximum_fusion.6), channel_id=1, source_target_pairs={{0,8},{2,10},{4,12},{6,14},{8,0},{10,2},{12,4},{14,6},{16,24},{18,... | collective-permute-start | bytes 393224 | tf_op jit(solution)/shard_map/ppermute | solution.py:90
  71.6 1.6 %collective-permute-start.28 = (f32[512,128]{1,0:T(8,128)S(1)}, f32[512,128]{1,0:T(8,128)S(1)}, u32[]{:S(2)}, u32[]{:S(2)}) collective-permute-start(f32[512,128]{1,0:T(8,128)S(1)} %pad_maximum_fusion.4), channel_id=1, source_target_pairs={{0,2},{2,0},{4,6},{6,4},{8,10},{10,8},{12,14},{14,12},{16,18},{18,... | collective-permute-start | bytes 786440 | tf_op jit(solution)/shard_map/ppermute | solution.py:90
  72.8 1.6 %collective-permute-start.14 = (f32[512,128]{1,0:T(8,128)S(1)}, f32[512,128]{1,0:T(8,128)S(1)}, u32[]{:S(2)}, u32[]{:S(2)}) collective-permute-start(f32[512,128]{1,0:T(8,128)S(1)} %pad_maximum_fusion.2), channel_id=1, source_target_pairs={{0,2},{2,0},{4,6},{6,4},{8,10},{10,8},{12,14},{14,12},{16,18},{18,... | collective-permute-start | bytes 786440 | tf_op jit(solution)/shard_map/ppermute | solution.py:90
  (2 other events, 9.8 us)
